TPU v7x, 32 devices: a whole 2x2x4 slice. The times are simulated.
32 devices in a mesh: rep: 2 (over x), span: 2 (over core), tp: 8 (over z, y).
Axes of the slice: x: 2, y: 2, z: 4, core: 2. Of those that a mesh axis runs over, the one named last changes fastest.
Arguments:
- hidden_in: bfloat16 [16, 128, 6144], P(('rep', 'span'), None, 'tp'), parts along dimension 0, may hold values from -6 to 6
- levels: int32 [16], P(('rep', 'span')), parts along dimension 0, may hold values from 0 to 3
- order: int32 [16], P('rep'), parts along dimension 0, may hold values from 0 to 7, each once
- cache_mask: int32 [16, 8], P('rep'), parts along dimension 0, may hold values 0 or 1
- finished: int32 [2], P('rep'), parts along dimension 0, may hold values from 0 to 7
- cache_kv: bfloat16 [16, 128, 2, 1024], P(('rep', 'span'), None, None, 'tp'), parts along dimension 0, may hold values from -300 to 300
- modulation: bfloat16 [4, 6, 6144], replicated, may hold values from 0.5 to 1.5
- w_qkv: bfloat16 [6144, 3, 1024], P(None, None, 'tp'), may hold values from -0.109375 to 0.109375
- w_out: bfloat16 [1024, 6144], P('tp'), may hold values from -0.375 to 0.375
- w_up: bfloat16 [6144, 4096], P(None, ('span', 'tp')), may hold values from -0.078125 to 0.078125
- w_down: bfloat16 [4096, 6144], P(('span', 'tp')), may hold values from -0.09375 to 0.09375
Outputs:
- layer_out: bfloat16 [16, 128, 6144], P(('rep', 'span'), None, 'tp'), parts along dimension 0
There are 2 independent parts, one for each index of `rep`. A program takes and returns all parts, laid end to end along the dimension named above; an argument that names none is the same for every part. Nothing has to cross between parts.
All inputs are finite; a program needn't handle non-finite values.
Results may differ from a plain program's by a relative error of at most 0.025.
The roundings to bfloat16 on the way count: a program that leaves them out, or rounds other values in their place, can miss the bound.
Values may be sent and summed in bfloat16 or wider, within the bound.
No kernel may reach another device: no remote copies, remote signals or barrier semaphores. Data moves between devices by JAX's collectives and lax.ppermute only.
A program may use at most 128 MiB of HBM per device.

v0:
```python
import math

import jax
import jax.numpy as jnp
from jax import lax
from jax.sharding import PartitionSpec as P

HEAD_DIM = 128


EPSILON = 1e-06
NEGATIVE = -1e30


def normalize(values):
    return values * lax.rsqrt(jnp.mean(values * values, axis=-1, keepdims=True) + EPSILON)


def select_row(source, target):
    matches = jnp.arange(source.shape[0], dtype=jnp.int32) == target
    return jnp.sum(jnp.where(matches.reshape((-1,) + (1,) * (source.ndim - 1)), source, 0), axis=0)


def attend(queries, cache_all, fresh_all, cache_seen, fresh_seen):
    row_count, head_count, head_size = queries.shape
    cache_keys = cache_all[:, :, 0].reshape(-1, head_count, head_size)
    cache_vals = cache_all[:, :, 1].reshape(-1, head_count, head_size)
    fresh_keys = fresh_all[:, :, 0].reshape(-1, head_count, head_size)
    fresh_vals = fresh_all[:, :, 1].reshape(-1, head_count, head_size)
    score_scale = 1.0 / math.sqrt(head_size)
    cache_scores = (
        jnp.einsum("qhd,khd->hqk", queries, cache_keys, preferred_element_type=jnp.float32)
        * score_scale
    )
    fresh_scores = (
        jnp.einsum("qhd,khd->hqk", queries, fresh_keys, preferred_element_type=jnp.float32)
        * score_scale
    )
    cache_scores = jnp.where(cache_seen[None, None, :], cache_scores, NEGATIVE)
    fresh_scores = jnp.where(fresh_seen[None, None, :], fresh_scores, NEGATIVE)
    scores = jnp.concatenate([cache_scores, fresh_scores], axis=2)
    row_max = jnp.max(scores, axis=2, keepdims=True)
    exp_terms = jnp.exp(scores - row_max)
    weights = (exp_terms / jnp.sum(exp_terms, axis=2, keepdims=True)).astype(jnp.bfloat16)
    split_at = cache_keys.shape[0]
    attended = jnp.einsum(
        "hqk,khd->qhd", weights[:, :, :split_at], cache_vals, preferred_element_type=jnp.float32
    )
    attended = attended + jnp.einsum(
        "hqk,khd->qhd", weights[:, :, split_at:], fresh_vals, preferred_element_type=jnp.float32
    )
    return attended.astype(jnp.bfloat16).reshape(row_count, head_count * head_size)


def local(
    hidden_in, levels, order, cache_mask, finished, cache_kv, modulation, w_qkv, w_out, w_up, w_down
):
    span_index = lax.axis_index("span")
    tp_rank = lax.axis_index("tp")
    model_width = modulation.shape[2]
    share_width = hidden_in.shape[2]
    local_count = hidden_in.shape[0]
    row_count = hidden_in.shape[1]
    up_full, down_full = (
        lax.all_gather(w_up, "span", axis=1, tiled=True),
        lax.all_gather(w_down, "span", axis=0, tiled=True),
    )
    mod_table = modulation.reshape(modulation.shape[0], -1)
    picker = (jnp.arange(mod_table.shape[0], dtype=jnp.int32)[None, :] == levels[:, None]).astype(
        jnp.bfloat16
    )
    mod_rows = jnp.dot(picker, mod_table, preferred_element_type=jnp.float32).reshape(
        local_count, 6, model_width
    )
    gathered = lax.all_gather(hidden_in, "tp", axis=2, tiled=True).astype(jnp.float32)
    attn_in = (normalize(gathered) * mod_rows[:, 1][:, None] + mod_rows[:, 0][:, None]).astype(
        jnp.bfloat16
    )
    per_device = w_qkv.shape[2]
    projected = jnp.dot(
        attn_in.reshape(local_count * row_count, model_width),
        w_qkv.reshape(model_width, -1),
        preferred_element_type=jnp.float32,
    )
    projected = projected.astype(jnp.bfloat16).reshape(local_count, row_count, 3, per_device)
    queries = projected[:, :, 0].reshape(local_count, row_count, -1, HEAD_DIM)
    fresh_kv = projected[:, :, 1:]
    cache_all, fresh_all = (
        lax.all_gather(cache_kv, "span", axis=0, tiled=True),
        lax.all_gather(fresh_kv, "span", axis=0, tiled=True),
    )
    positions = jnp.arange(cache_mask.shape[0], dtype=jnp.int32)
    my_spans = span_index * local_count + jnp.arange(local_count, dtype=jnp.int32)
    mask_rows = jax.vmap(lambda target: select_row(cache_mask, target))(my_spans)
    my_order = jax.vmap(lambda target: select_row(order, target))(my_spans)
    cache_seen = jnp.repeat(
        (mask_rows == 1) | (positions[None, :] == finished[0]), row_count, axis=1
    )
    fresh_seen = jnp.repeat(order[None, :] <= my_order[:, None], row_count, axis=1)
    attended = jax.vmap(
        lambda q_rows, c_seen, f_seen: attend(q_rows, cache_all, fresh_all, c_seen, f_seen)
    )(queries, cache_seen, fresh_seen)
    partial_value = jnp.dot(
        attended.reshape(local_count * row_count, -1), w_out, preferred_element_type=jnp.float32
    )
    partial_value = partial_value.reshape(local_count, row_count, model_width)
    mod_share = lax.dynamic_slice_in_dim(mod_rows, tp_rank * share_width, share_width, 2)
    attn_part = lax.psum_scatter(
        partial_value.astype(jnp.bfloat16), "tp", scatter_dimension=2, tiled=True
    ).astype(jnp.float32)
    residual = hidden_in.astype(jnp.float32) + mod_share[:, 2][:, None] * attn_part
    squares = lax.psum(jnp.sum(residual * residual, axis=2), "tp")
    scaled = residual * lax.rsqrt(squares / model_width + EPSILON)[:, :, None]
    mlp_part = (scaled * mod_share[:, 4][:, None] + mod_share[:, 3][:, None]).astype(jnp.bfloat16)
    pre_act = jnp.dot(
        lax.all_gather(mlp_part, "tp", axis=2, tiled=True),
        up_full,
        preferred_element_type=jnp.float32,
    )
    hidden_units = jax.nn.gelu(pre_act).astype(jnp.bfloat16)
    down_terms = jnp.dot(hidden_units, down_full, preferred_element_type=jnp.float32)
    mlp_out = lax.psum_scatter(
        down_terms.astype(jnp.bfloat16), "tp", scatter_dimension=2, tiled=True
    ).astype(jnp.float32)
    result = residual + mod_share[:, 5][:, None] * mlp_out
    return result.astype(jnp.bfloat16)


def solution(mesh):
    placed = (
        P(("rep", "span"), None, "tp"),
        P(("rep", "span")),
        P("rep"),
        P("rep", None),
        P("rep"),
        P(("rep", "span"), None, None, "tp"),
        P(),
        P(None, None, "tp"),
        P("tp", None),
        P(None, ("span", "tp")),
        P(("span", "tp"), None),
    )
    return jax.shard_map(
        local, mesh=mesh, in_specs=placed, out_specs=P(("rep", "span"), None, "tp"), check_vma=False
    )
```

profile of v0, /device:TPU:0, one launch (start us, length us, event | category | flops | bytes accessed | tf_op | source)
XLA Modules:
  0.0 528.1 jit_solution(8121966962387378399)
XLA Ops:
  7.4 0.7 all-gather.5.cloned.1.call-update
  8.1 0.0 reduce-scatter.3.cloned.1.call-start
  8.2 6.8 %copy.29 = bf16[6144,3,128]{0,2,1:T(8,128)(2,1)} copy(bf16[6144,3,128]{2,0,1:T(8,128)(2,1)} %param.18) | data formatting | bytes 9437184 | tf_op args[7]
  15.6 0.1 iota_compare_fusion
  15.7 0.1 select_reduce_fusion
  15.8 0.1 broadcast_bitcast_fusion.1
  15.9 0.2 select_reduce_fusion.1
  16.1 0.1 broadcast_compare_fusion
  16.2 0.1 broadcast_bitcast_fusion
  16.3 2.3 all_gather.19
  18.6 0.4 fusion.30
  19.0 93.2 %all-gather.5.cloned.1.call-done = bf16[4,128,6144]{2,1,0:T(8,128)(2,1)} async-done(((bf16[4,128,768]{2,1,0:T(8,128)(2,1)}), bf16[4,128,6144]{2,1,0:T(8,128)(2,1)}) %all-gather.5.cloned.1.call-update) | async-done | bytes 6291472 | tf_op jit(solution)/shard_map/all_gather | solution.py:75
  112.2 4.2 fusion
  116.4 0.3 copy-done.2
  116.8 2.7 fusion.3
  119.5 5.8 %convolution_convert_fusion.2 = bf16[512,384]{1,0:T(8,128)(2,1)S(1)} fusion(bf16[512,6144]{1,0:T(8,128)(2,1)S(1)} %bitcast.110, bf16[6144,384]{0,1:T(8,128)(2,1)} %bitcast.111), kind=kOutput, calls=%fused_computation.27 | convolution fusion | flops 2416115712 | bytes 11403264 | tf_op jit(solution)/shard_map/dot_general | solution.py:80
  125.3 0.2 copy.30
  125.5 0.1 reshape.192
  125.6 0.1 slice.60
  125.8 0.2 copy.33
  126.0 2.4 all_gather.20
  128.4 0.1 copy.39
  128.5 0.4 fusion.32
  129.0 0.8 fusion.9
  129.8 0.7 fusion.8
  130.5 0.9 divide_convert_fusion
  131.5 1.3 copy-done.5
  132.8 0.4 fusion.29
  133.2 5.4 %convolution_convert_fusion.1 = bf16[4,128,6144]{2,1,0:T(8,128)(2,1)} fusion(bf16[128,6144]{1,0:T(8,128)(2,1)S(1)} %copy-done, f32[128,4,128]{0,2,1:T(8,128)S(1)} %fusion.29, bf16[1024,128,1]{1,0,2:T(8,128)(2,1)S(1)} %bitcast.112, bf16[4,1,128,2048]{3,2,0,1:T(8,128)(2,1)} %copy-done.5), kind=kOutput, calls=%fused_computation.7 | convolution fusion | flops 942800896 | bytes 9437184 | tf_op jit(solution)/shard_map/dot_general | solution.py:103
  138.7 0.0 all-gather.9.cloned.1.call-start
  138.7 0.5 all-gather.9.cloned.1.call-update
  139.3 0.0 all-gather.7.cloned.1.call-start
  139.4 115.7 %reduce-scatter.3.cloned.1.call-done = bf16[4,128,768]{2,1,0:T(8,128)(2,1)} async-done(((bf16[4,128,6144]{2,1,0:T(8,128)(2,1)}), bf16[4,128,768]{2,1,0:T(8,128)(2,1)}) %reduce-scatter.3.cloned.1.call-update) | async-done | bytes 786448 | tf_op jit(solution)/shard_map/reduce_scatter | solution.py:108
  255.1 1.5 multiply_reduce_fusion
  256.6 19.6 %psum.7 = f32[4,128]{1,0:T(4,128)S(1)} all-reduce(f32[4,128]{1,0:T(4,128)S(1)} %multiply_reduce_fusion), channel_id=1, replica_groups=mesh['rep'=2,'span'=2,'tp'=8] {'tp'}, use_global_device_ids=true, to_apply=%region_8.9 | all-reduce | flops 512 | bytes 4096 | tf_op jit(solution)/shard_map/psum | solution.py:112
  276.2 2.4 add_convert_fusion.1
  278.6 0.0 all-gather.7.cloned.1.call-update
  278.6 0.0 all-gather.11.cloned.1.call-start
  278.7 0.5 all-gather.11.cloned.1.call-update
  279.2 0.0 reduce-scatter.5.cloned.1.call-start
  279.3 0.0 all-gather.9.cloned.1.call-done
  279.3 95.3 %all-gather.7.cloned.1.call-done = bf16[4,128,6144]{2,1,0:T(8,128)(2,1)} async-done(((bf16[4,128,768]{2,1,0:T(8,128)(2,1)}), bf16[4,128,6144]{2,1,0:T(8,128)(2,1)}) %all-gather.7.cloned.1.call-update) | async-done | bytes 6291472 | tf_op jit(solution)/shard_map/all_gather | solution.py:116
  374.6 8.2 %fusion.26 = bf16[4,128,512]{2,1,0:T(8,128)(2,1)S(1)} fusion(bf16[4,128,6144]{2,1,0:T(8,128)(2,1)} %all-gather.7.cloned.1.call-done, bf16[6144,512]{1,0:T(8,128)(2,1)} %all-gather.9.cloned.1.call-done), kind=kOutput, calls=%fused_computation.39 | convolution fusion | flops 3223584768 | bytes 13107200 | tf_op jit(solution)/shard_map/dot_general | solution.py:115
  382.8 8.3 %all-gather.11.cloned.1.call-done = bf16[512,6144]{1,0:T(8,128)(2,1)} async-done(((bf16[256,6144]{1,0:T(8,128)(2,1)}), bf16[512,6144]{1,0:T(8,128)(2,1)}) %all-gather.11.cloned.1.call-update) | async-done | bytes 6291472 | tf_op jit(solution)/shard_map/all_gather | solution.py:66
  391.1 8.1 %convolution_convert_fusion = bf16[4,128,6144]{2,1,0:T(8,128)(2,1)} fusion(bf16[4,128,512]{2,1,0:T(8,128)(2,1)S(1)} %fusion.26, bf16[512,6144]{1,0:T(8,128)(2,1)} %all-gather.11.cloned.1.call-done), kind=kOutput, calls=%fused_computation.6 | convolution fusion | flops 3224371200 | bytes 13107200 | tf_op jit(solution)/shard_map/dot_general | solution.py:121
  399.1 0.0 reduce-scatter.5.cloned.1.call-update
  399.2 118.9 %reduce-scatter.5.cloned.1.call-done = bf16[4,128,768]{2,1,0:T(8,128)(2,1)} async-done(((bf16[4,128,6144]{2,1,0:T(8,128)(2,1)}), bf16[4,128,768]{2,1,0:T(8,128)(2,1)}) %reduce-scatter.5.cloned.1.call-update) | async-done | bytes 786448 | tf_op jit(solution)/shard_map/reduce_scatter | solution.py:122
  518.1 2.4 add_convert_fusion
  (36 shorter events, 0.3 us)
Async XLA Ops:
  7.4 125.9 %copy-start = (bf16[128,6144]{1,0:T(8,128)(2,1)S(1)}, bf16[128,6144]{1,0:T(8,128)(2,1)}, u32[]{:S(2)}) copy-start(bf16[128,6144]{1,0:T(8,128)(2,1)} %param.19) | copy-start | bytes 4718596
  7.4 104.8 %all-gather.5.cloned.1.call-start = ((), (), s32[]{:S(2)}) async-start(), calls=%async_computation.2 | async-start | bytes 7077888 | tf_op jit(solution)/shard_map/all_gather | solution.py:75
  8.1 247.0 %reduce-scatter.3.cloned.1.call-start = ((), (), s32[]{:S(2)}) async-start(), calls=%async_computation.3 | async-start | bytes 7077888 | tf_op jit(solution)/shard_map/reduce_scatter | solution.py:108
  8.1 7.6 %copy-start.8 = (s32[8,8]{1,0:T(8,128)S(1)}, s32[8,8]{1,0:T(8,128)}, u32[]{:S(2)}) copy-start(s32[8,8]{1,0:T(8,128)} %param.14) | copy-start | bytes 772
  8.2 7.7 %copy-start.10 = (s32[8]{0:T(128)S(1)}, s32[8]{0:T(128)}, u32[]{:S(2)}) copy-start(s32[8]{0:T(128)} %param.13) | copy-start | bytes 100
  8.2 8.1 %copy-start.7 = (bf16[4,128,2,128]{3,2,1,0:T(2,128)(2,1)S(1)}, bf16[4,128,2,128]{3,2,1,0:T(2,128)(2,1)}, u32[]{:S(2)}) copy-start(bf16[4,128,2,128]{3,2,1,0:T(2,128)(2,1)} %param.16) | copy-start | bytes 786436
  8.2 10.4 %copy-start.6 = (bf16[4,6,6144]{2,0,1:T(4,128)(2,1)S(1)}, bf16[4,6,6144]{2,0,1:T(4,128)(2,1)}, u32[]{:S(2)}) copy-start(bf16[4,6,6144]{2,0,1:T(4,128)(2,1)} %param.17) | copy-start | bytes 884740
  8.2 10.4 %copy-start.9 = (s32[4]{0:T(128)S(1)}, s32[4]{0:T(128)}, u32[]{:S(2)}) copy-start(s32[4]{0:T(128)} %param.12) | copy-start | bytes 52
  112.2 4.6 copy-start.2
  131.4 1.3 copy-start.5
  138.7 116.4 %copy-start.3 = (bf16[4,128,768]{2,1,0:T(8,128)(2,1)S(1)}, bf16[4,128,768]{2,1,0:T(8,128)(2,1)}, u32[]{:S(2)}) copy-start(bf16[4,128,768]{2,1,0:T(8,128)(2,1)} %param.11) | copy-start | bytes 2359300
  138.7 140.6 %all-gather.9.cloned.1.call-start = ((), (), s32[]{:S(2)}) async-start(), calls=%async_computation.5 | async-start | bytes 9437184 | tf_op jit(solution)/shard_map/all_gather | solution.py:65
  139.3 235.3 %all-gather.7.cloned.1.call-start = ((), (), s32[]{:S(2)}) async-start(), calls=%async_computation.4 | async-start | bytes 7077888 | tf_op jit(solution)/shard_map/all_gather | solution.py:116
  278.6 112.4 %all-gather.11.cloned.1.call-start = ((), (), s32[]{:S(2)}) async-start(), calls=%async_computation.6 | async-start | bytes 9437184 | tf_op jit(solution)/shard_map/all_gather | solution.py:66
  279.2 238.9 %reduce-scatter.5.cloned.1.call-start = ((), (), s32[]{:S(2)}) async-start(), calls=%async_computation.7 | async-start | bytes 7077888 | tf_op jit(solution)/shard_map/reduce_scatter | solution.py:122
  399.1 119.0 %copy-start.4 = (bf16[4,128,768]{2,1,0:T(8,128)(2,1)S(1)}, bf16[4,128,768]{2,1,0:T(8,128)(2,1)}, u32[]{:S(2)}) copy-start(bf16[4,128,768]{2,1,0:T(8,128)(2,1)} %reduce-scatter.3.cloned.1.call-done) | copy-start | bytes 2359300
  399.2 121.3 %copy-start.1 = (bf16[128,6144]{1,0:T(8,128)(2,1)S(1)}, bf16[128,6144]{1,0:T(8,128)(2,1)}, u32[]{:S(2)}) copy-start(bf16[128,6144]{1,0:T(8,128)(2,1)} %param.19) | copy-start | bytes 4718596
Sparse Core Ops, SparseCore 0:
  10.4 101.7 all-gather.4
  138.8 116.2 reduce-scatter.2
Sparse Core Ops, SparseCore 1:
  140.7 13.8 all-gather.8
  278.7 95.8 all-gather.6
  376.0 15.0 all-gather.10
  399.2 118.8 reduce-scatter.4
where the time goes:
time: 529 us; the launch traced here: 528 us
  waiting for transfers between devices  433 us (82%)
  matrix products  29.6 us (6%)
  blocking collectives  24.2 us (5%)
  between operations  16 us (3%)
  other arithmetic  15.4 us (3%)
  local copies, waits for them, and re-layouts  9.57 us (2%)
    reduce_scatter x1, waiting for transfers between devices, local(): lax.psum_scatter(down_terms.astype(jnp.bfloat16), 'tp', scatter_dimension...  119 us
    reduce_scatter x1, waiting for transfers between devices, local(): lax.psum_scatter(partial_value.astype(jnp.bfloat16), 'tp', scatter_dimens...  116 us
    all_gather x1, waiting for transfers between devices, local(): lax.all_gather(mlp_part, 'tp', axis=2, tiled=True)  95.3 us
    all_gather x1, waiting for transfers between devices, local(): lax.all_gather(hidden_in, 'tp', axis=2, tiled=True).astype(jnp.float32)  93.2 us
    psum x1, blocking collectives, local(): squares = lax.psum(jnp.sum(residual * residual, axis=2), 'tp')  19.6 us
  transfers between devices with their start and end apart: 6, of which 5 were waited for; matrix products, arithmetic and copies ran while one was open for 4% of the time, Pallas kernels for 0%

commit v1 on v0

--- a/solution.py
+++ b/solution.py
@@ -10,6 +10,7 @@
 
 EPSILON = 1e-06
 NEGATIVE = -1e30
+WEIGHT_GATHER_BYTES = 24 * 2**20
 
 
 def normalize(values):
@@ -57,10 +58,21 @@
 ):
     span_index = lax.axis_index("span")
     tp_rank = lax.axis_index("tp")
+    span_count = lax.psum(1, "span")
+    tp_count = lax.psum(1, "tp")
     model_width = modulation.shape[2]
     share_width = hidden_in.shape[2]
     local_count = hidden_in.shape[0]
     row_count = hidden_in.shape[1]
+    token_count = local_count * row_count
+    gathered = lax.all_gather(hidden_in, "tp", axis=2, tiled=True).astype(jnp.float32)
+    gather_weights = tp_count * w_out.size * w_out.dtype.itemsize <= WEIGHT_GATHER_BYTES
+    if gather_weights:
+        column_part = model_width // span_count
+        w_out_part = lax.dynamic_slice_in_dim(w_out, span_index * column_part, column_part, 1)
+        w_out_full = lax.all_gather(
+            lax.all_gather(w_out_part, "tp", axis=0, tiled=True), "span", axis=1, tiled=True
+        )
     up_full, down_full = (
         lax.all_gather(w_up, "span", axis=1, tiled=True),
         lax.all_gather(w_down, "span", axis=0, tiled=True),
@@ -72,13 +84,12 @@
     mod_rows = jnp.dot(picker, mod_table, preferred_element_type=jnp.float32).reshape(
         local_count, 6, model_width
     )
-    gathered = lax.all_gather(hidden_in, "tp", axis=2, tiled=True).astype(jnp.float32)
     attn_in = (normalize(gathered) * mod_rows[:, 1][:, None] + mod_rows[:, 0][:, None]).astype(
         jnp.bfloat16
     )
     per_device = w_qkv.shape[2]
     projected = jnp.dot(
-        attn_in.reshape(local_count * row_count, model_width),
+        attn_in.reshape(token_count, model_width),
         w_qkv.reshape(model_width, -1),
         preferred_element_type=jnp.float32,
     )
@@ -100,28 +111,50 @@
     attended = jax.vmap(
         lambda q_rows, c_seen, f_seen: attend(q_rows, cache_all, fresh_all, c_seen, f_seen)
     )(queries, cache_seen, fresh_seen)
-    partial_value = jnp.dot(
-        attended.reshape(local_count * row_count, -1), w_out, preferred_element_type=jnp.float32
-    )
-    partial_value = partial_value.reshape(local_count, row_count, model_width)
-    mod_share = lax.dynamic_slice_in_dim(mod_rows, tp_rank * share_width, share_width, 2)
-    attn_part = lax.psum_scatter(
-        partial_value.astype(jnp.bfloat16), "tp", scatter_dimension=2, tiled=True
-    ).astype(jnp.float32)
-    residual = hidden_in.astype(jnp.float32) + mod_share[:, 2][:, None] * attn_part
-    squares = lax.psum(jnp.sum(residual * residual, axis=2), "tp")
-    scaled = residual * lax.rsqrt(squares / model_width + EPSILON)[:, :, None]
-    mlp_part = (scaled * mod_share[:, 4][:, None] + mod_share[:, 3][:, None]).astype(jnp.bfloat16)
-    pre_act = jnp.dot(
-        lax.all_gather(mlp_part, "tp", axis=2, tiled=True),
-        up_full,
-        preferred_element_type=jnp.float32,
-    )
+    if gather_weights:
+        attended_all = lax.all_gather(
+            attended.reshape(token_count, per_device), "tp", axis=1, tiled=True
+        )
+        def add_group(group, running):
+            term = jnp.dot(
+                lax.dynamic_slice_in_dim(attended_all, group * per_device, per_device, 1),
+                lax.dynamic_slice_in_dim(w_out_full, group * per_device, per_device, 0),
+                preferred_element_type=jnp.float32,
+            )
+            return running + term.astype(jnp.bfloat16).astype(jnp.float32)
+
+        attn_out = lax.fori_loop(
+            0, tp_count, add_group, jnp.zeros((token_count, model_width), jnp.float32)
+        )
+        attn_out = attn_out.reshape(local_count, row_count, model_width)
+        residual_full = gathered + mod_rows[:, 2][:, None] * attn_out
+        mlp_in = (
+            normalize(residual_full) * mod_rows[:, 4][:, None] + mod_rows[:, 3][:, None]
+        ).astype(jnp.bfloat16)
+    else:
+        partial_value = jnp.dot(
+            attended.reshape(token_count, -1), w_out, preferred_element_type=jnp.float32
+        ).reshape(local_count, row_count, model_width)
+        attn_part = lax.psum_scatter(
+            partial_value.astype(jnp.bfloat16), "tp", scatter_dimension=2, tiled=True
+        ).astype(jnp.float32)
+        mod_share = lax.dynamic_slice_in_dim(mod_rows, tp_rank * share_width, share_width, 2)
+        residual = hidden_in.astype(jnp.float32) + mod_share[:, 2][:, None] * attn_part
+        squares = lax.psum(jnp.sum(residual * residual, axis=2), "tp")
+        scaled = residual * lax.rsqrt(squares / model_width + EPSILON)[:, :, None]
+        mlp_part = (scaled * mod_share[:, 4][:, None] + mod_share[:, 3][:, None]).astype(
+            jnp.bfloat16
+        )
+        mlp_in = lax.all_gather(mlp_part, "tp", axis=2, tiled=True)
+    pre_act = jnp.dot(mlp_in, up_full, preferred_element_type=jnp.float32)
     hidden_units = jax.nn.gelu(pre_act).astype(jnp.bfloat16)
     down_terms = jnp.dot(hidden_units, down_full, preferred_element_type=jnp.float32)
     mlp_out = lax.psum_scatter(
         down_terms.astype(jnp.bfloat16), "tp", scatter_dimension=2, tiled=True
     ).astype(jnp.float32)
+    if gather_weights:
+        residual = lax.dynamic_slice_in_dim(residual_full, tp_rank * share_width, share_width, 2)
+        mod_share = lax.dynamic_slice_in_dim(mod_rows, tp_rank * share_width, share_width, 2)
     result = residual + mod_share[:, 5][:, None] * mlp_out
     return result.astype(jnp.bfloat16)
 

time: 529 us -> 529 us (level)
  matrix products: 29.6 us -> 119 us
  waiting for transfers between devices: 433 us -> 355 us
  blocking collectives: 24.2 us -> 4.44 us
  other arithmetic: 15.4 us -> 25.1 us
    reduce_scatter x1 -> x0, waiting for transfers between devices: 116 us -> none  [local(): lax.psum_scatter(partial_value.astype(jnp.bfloat16), 'tp', scatter_dimens...]
    dot_general x3 -> x11, matrix products: 19.4 us -> 109 us  [the longest x8 91.8 us: add_group(): jnp.dot(lax.dynamic_slice_in_dim(attended_all, group * per_device, per_de...]
    all_gather x1 -> x3, waiting for transfers between devices: 95.3 us -> 142 us  [the longest x1 78.4 us: local(): lax.all_gather(w_out_part, 'tp', axis=0, tiled=True)]
    psum x1 -> x0, blocking collectives: 19.6 us -> none  [local(): squares = lax.psum(jnp.sum(residual * residual, axis=2), 'tp')]
    reduce_sum x1 -> x2, other arithmetic: 4.24 us -> 17.6 us  [normalize(): jnp.mean(values * values, axis=-1, keepdims=True) + EPSILON]
    all_gather x1, waiting for transfers between devices: 8.31 us -> 0.02 us  [local(): lax.all_gather(w_down, 'span', axis=0, tiled=True)]
  transfers between devices with their start and end apart: 6 -> 7, of which waited for: 5 -> 5; matrix products, arithmetic and copies ran while one was open for 4% -> 27% of each run, Pallas kernels for 0% -> 0%
where the time goes in v1:
time: 529 us; the launch traced here: 528 us
  waiting for transfers between devices  355 us (67%)
  matrix products  119 us (22%)
  other arithmetic  25.1 us (5%)
  between operations  14.4 us (3%)
  local copies, waits for them, and re-layouts  9.76 us (2%)
    reduce_scatter x1, waiting for transfers between devices, local(): lax.psum_scatter(down_terms.astype(jnp.bfloat16), 'tp', scatter_dimension...  119 us
    dot_general x8, matrix products, add_group(): jnp.dot(lax.dynamic_slice_in_dim(attended_all, group * per_device, per_de...  91.8 us
    all_gather x1, waiting for transfers between devices, local(): lax.all_gather(hidden_in, 'tp', axis=2, tiled=True).astype(jnp.float32)  91.6 us
    all_gather x1, waiting for transfers between devices, local(): lax.all_gather(w_out_part, 'tp', axis=0, tiled=True)  78.4 us
    all_gather x1, waiting for transfers between devices, local(): lax.all_gather(attended.reshape(token_count, per_device), 'tp', axis=1, t...  38.4 us
    all_gather x1, waiting for transfers between devices, local(): lax.all_gather(lax.all_gather(w_out_part, 'tp', axis=0, tiled=True), 'spa...  25.2 us
    reduce_sum x2, other arithmetic, normalize(): jnp.mean(values * values, axis=-1, keepdims=True) + EPSILON  17.6 us
  transfers between devices with their start and end apart: 7, of which 5 were waited for; matrix products, arithmetic and copies ran while one was open for 27% of the time, Pallas kernels for 0%

profile of v1, /device:TPU:0, one launch (start us, length us, event | category | flops | bytes accessed | tf_op | source)
XLA Modules:
  0.0 528.1 jit_solution(3875462124296555248)
XLA Ops:
  6.6 0.7 all-gather.7.cloned.1.call-update
  7.3 0.6 copy-done
  7.9 0.9 constant_dynamic-slice_fusion
  9.0 6.7 %copy.26 = bf16[6144,3,128]{0,2,1:T(8,128)(2,1)} copy(bf16[6144,3,128]{2,0,1:T(8,128)(2,1)} %param.20) | data formatting | bytes 9437184 | tf_op args[7]
  16.4 0.1 select_reduce_fusion
  16.5 0.1 broadcast_bitcast_fusion.1
  16.6 0.2 select_reduce_fusion.1
  16.8 0.1 broadcast_compare_fusion
  16.9 0.1 broadcast_bitcast_fusion
  17.0 2.3 all_gather.25
  19.3 0.4 fusion.34
  19.8 91.6 %all-gather.7.cloned.1.call-done = bf16[4,128,6144]{2,1,0:T(8,128)(2,1)} async-done(((bf16[4,128,768]{2,1,0:T(8,128)(2,1)}), bf16[4,128,6144]{2,1,0:T(8,128)(2,1)}) %all-gather.7.cloned.1.call-update) | async-done | bytes 6291472 | tf_op jit(solution)/shard_map/all_gather | solution.py:68
  111.4 4.2 fusion.3
  115.6 0.3 copy-done.2
  116.0 2.7 fusion.6
  118.7 6.2 %convolution_convert_fusion.2 = bf16[512,384]{1,0:T(8,128)(2,1)S(1)} fusion(bf16[512,6144]{1,0:T(8,128)(2,1)S(1)} %bitcast.101, bf16[6144,384]{0,1:T(8,128)(2,1)} %bitcast.102), kind=kOutput, calls=%fused_computation.33 | convolution fusion | flops 2416115712 | bytes 11403264 | tf_op jit(solution)/shard_map/dot_general | solution.py:91
  124.9 0.2 copy.27
  125.1 0.1 reshape.201
  125.2 0.1 slice.61
  125.3 0.2 copy.30
  125.6 0.1 copy.33
  125.7 2.2 all_gather.26
  127.9 0.4 fusion.36
  128.4 0.8 fusion.15
  129.2 0.7 fusion.14
  129.9 0.9 divide_convert_fusion
  130.8 0.4 fusion.33
  131.3 1.1 fusion.20
  132.4 78.4 %all-gather.11.cloned.1.call-done = bf16[1024,3072]{1,0:T(8,128)(2,1)} async-done(((bf16[128,3072]{1,0:T(8,128)(2,1)}), bf16[1024,3072]{1,0:T(8,128)(2,1)}) %all-gather.11.cloned.1.call-update) | async-done | bytes 6291472 | tf_op jit(solution)/shard_map/all_gather | solution.py:74
  210.9 0.5 all-gather.15.cloned.1.call-update
  211.5 0.5 all-gather.17.cloned.1.call-update
  212.1 0.2 reduce-scatter.2.cloned.1.call-start
  212.3 38.4 %all-gather.9.cloned.1.call-done = bf16[512,1024]{1,0:T(8,128)(2,1)} async-done(((bf16[512,128]{1,0:T(8,128)(2,1)}), bf16[512,1024]{1,0:T(8,128)(2,1)}) %all-gather.9.cloned.1.call-update) | async-done | bytes 1048592 | tf_op jit(solution)/shard_map/all_gather | solution.py:115
  250.7 25.2 %all-gather.13.cloned.1.call-done = bf16[1024,6144]{1,0:T(8,128)(2,1)} async-done(((bf16[1024,3072]{1,0:T(8,128)(2,1)}), bf16[1024,6144]{1,0:T(8,128)(2,1)}) %all-gather.13.cloned.1.call-update) | async-done | bytes 12582928 | tf_op jit(solution)/shard_map/all_gather | solution.py:73
  275.9 91.8 %while.14 = (s32[]{:T(128)}, f32[512,6144]{1,0:T(8,128)}, bf16[512,1024]{1,0:T(8,128)(2,1)}, bf16[1024,6144]{1,0:T(8,128)(2,1)}, s32[]{:T(128)}, /*index=5*/s32[]{:T(128)}, s32[]{:T(128)}, s32[]{:T(128)}) while((s32[]{:T(128)}, f32[512,6144]{1,0:T(8,128)}, bf16[512,1024]{1,0:T(8,128)(2,1)}, bf16[1024,6144]{1,0:T(8,128)(2,1)}, ...), condition=%wide.region_7.8_spmd.clone, body=%wide.region_6.7_spmd.clone.sunk | while | flops 817889280 | bytes 26871436 | solution.py:126
  275.9 7.7 %select_add_fusion.2 = f32[512,6144]{1,0:T(8,128)} fusion(f32[512,6144]{1,0:T(8,128)} %get-tuple-element.159, pred[]{:T(512)S(6)} %compare.3, bf16[1024,6144]{1,0:T(8,128)(2,1)} %get-tuple-element.169, s32[]{:T(128)S(6)} %select_n.58, bf16[512,1024]{1,0:T(8,128)(2,1)} %get-tuple-element.168), kind=kOutput, calls=%fused_computation.clone.1 | convolution fusion | flops 817889280 | bytes 26871296 | tf_op jit(solution)/shard_map/while/body/eval_jaxpr/dot_general | solution.py:119
  283.6 13.8 %select_add_fusion.2 = f32[512,6144]{1,0:T(8,128)} fusion(f32[512,6144]{1,0:T(8,128)} %get-tuple-element.159, pred[]{:T(512)S(6)} %compare.3, bf16[1024,6144]{1,0:T(8,128)(2,1)} %get-tuple-element.169, s32[]{:T(128)S(6)} %select_n.58, bf16[512,1024]{1,0:T(8,128)(2,1)} %get-tuple-element.168), kind=kOutput, calls=%fused_computation.clone.1 | convolution fusion | flops 817889280 | bytes 26871296 | tf_op jit(solution)/shard_map/while/body/eval_jaxpr/dot_general | solution.py:119
  297.4 13.3 %select_add_fusion.2 = f32[512,6144]{1,0:T(8,128)} fusion(f32[512,6144]{1,0:T(8,128)} %get-tuple-element.159, pred[]{:T(512)S(6)} %compare.3, bf16[1024,6144]{1,0:T(8,128)(2,1)} %get-tuple-element.169, s32[]{:T(128)S(6)} %select_n.58, bf16[512,1024]{1,0:T(8,128)(2,1)} %get-tuple-element.168), kind=kOutput, calls=%fused_computation.clone.1 | convolution fusion | flops 817889280 | bytes 26871296 | tf_op jit(solution)/shard_map/while/body/eval_jaxpr/dot_general | solution.py:119
  310.7 11.4 %select_add_fusion.2 = f32[512,6144]{1,0:T(8,128)} fusion(f32[512,6144]{1,0:T(8,128)} %get-tuple-element.159, pred[]{:T(512)S(6)} %compare.3, bf16[1024,6144]{1,0:T(8,128)(2,1)} %get-tuple-element.169, s32[]{:T(128)S(6)} %select_n.58, bf16[512,1024]{1,0:T(8,128)(2,1)} %get-tuple-element.168), kind=kOutput, calls=%fused_computation.clone.1 | convolution fusion | flops 817889280 | bytes 26871296 | tf_op jit(solution)/shard_map/while/body/eval_jaxpr/dot_general | solution.py:119
  322.1 11.4 %select_add_fusion.2 = f32[512,6144]{1,0:T(8,128)} fusion(f32[512,6144]{1,0:T(8,128)} %get-tuple-element.159, pred[]{:T(512)S(6)} %compare.3, bf16[1024,6144]{1,0:T(8,128)(2,1)} %get-tuple-element.169, s32[]{:T(128)S(6)} %select_n.58, bf16[512,1024]{1,0:T(8,128)(2,1)} %get-tuple-element.168), kind=kOutput, calls=%fused_computation.clone.1 | convolution fusion | flops 817889280 | bytes 26871296 | tf_op jit(solution)/shard_map/while/body/eval_jaxpr/dot_general | solution.py:119
  333.5 11.4 %select_add_fusion.2 = f32[512,6144]{1,0:T(8,128)} fusion(f32[512,6144]{1,0:T(8,128)} %get-tuple-element.159, pred[]{:T(512)S(6)} %compare.3, bf16[1024,6144]{1,0:T(8,128)(2,1)} %get-tuple-element.169, s32[]{:T(128)S(6)} %select_n.58, bf16[512,1024]{1,0:T(8,128)(2,1)} %get-tuple-element.168), kind=kOutput, calls=%fused_computation.clone.1 | convolution fusion | flops 817889280 | bytes 26871296 | tf_op jit(solution)/shard_map/while/body/eval_jaxpr/dot_general | solution.py:119
  344.9 11.4 %select_add_fusion.2 = f32[512,6144]{1,0:T(8,128)} fusion(f32[512,6144]{1,0:T(8,128)} %get-tuple-element.159, pred[]{:T(512)S(6)} %compare.3, bf16[1024,6144]{1,0:T(8,128)(2,1)} %get-tuple-element.169, s32[]{:T(128)S(6)} %select_n.58, bf16[512,1024]{1,0:T(8,128)(2,1)} %get-tuple-element.168), kind=kOutput, calls=%fused_computation.clone.1 | convolution fusion | flops 817889280 | bytes 26871296 | tf_op jit(solution)/shard_map/while/body/eval_jaxpr/dot_general | solution.py:119
  356.3 11.4 %select_add_fusion.2 = f32[512,6144]{1,0:T(8,128)} fusion(f32[512,6144]{1,0:T(8,128)} %get-tuple-element.159, pred[]{:T(512)S(6)} %compare.3, bf16[1024,6144]{1,0:T(8,128)(2,1)} %get-tuple-element.169, s32[]{:T(128)S(6)} %select_n.58, bf16[512,1024]{1,0:T(8,128)(2,1)} %get-tuple-element.168), kind=kOutput, calls=%fused_computation.clone.1 | convolution fusion | flops 817889280 | bytes 26871296 | tf_op jit(solution)/shard_map/while/body/eval_jaxpr/dot_general | solution.py:119
  367.7 13.3 %multiply_reduce_fusion = (f32[4,128]{1,0:T(4,128)S(1)}, f32[4,128,6144]{2,1,0:T(8,128)}) fusion(f32[4,128,6144]{2,1,0:T(8,128)} %bitcast.100, f32[4,6144]{1,0:T(4,128)S(1)} %get-tuple-element.118, bf16[4,128,6144]{2,1,0:T(8,128)(2,1)} %all-gather.7.cloned.1.call-done), kind=kLoop, calls=%fused_computation.13 | loop fusion | flops 15728128 | bytes 31557632 | tf_op jit(solution)/shard_map/reduce_sum | solution.py:17
  381.0 10.0 %fusion.30 = bf16[4,128,512]{2,1,0:T(8,128)(2,1)S(1)} fusion(bf16[6144,512]{1,0:T(8,128)(2,1)} %all-gather.15.cloned.1.call-done, f32[4,128,6144]{2,1,0:T(8,128)} %get-tuple-element.109, f32[4,6144]{1,0:T(4,128)S(1)} %get-tuple-element.115, f32[4,6144]{1,0:T(4,128)S(1)} %get-tuple-element.114, f32[4,128]{1,0:T(4,128)S(1)} %add_rsqrt_fusion), kind=kOutput, calls=%fused_computation.44 | convolution fusion | flops 3236167680 | bytes 19597312 | tf_op jit(solution)/shard_map/dot_general | solution.py:149
  391.1 8.2 %convolution_convert_fusion.1 = bf16[4,128,6144]{2,1,0:T(8,128)(2,1)} fusion(bf16[4,128,512]{2,1,0:T(8,128)(2,1)S(1)} %fusion.30, bf16[512,6144]{1,0:T(8,128)(2,1)} %all-gather.17.cloned.1.call-done), kind=kOutput, calls=%fused_computation.14 | convolution fusion | flops 3224371200 | bytes 13107200 | tf_op jit(solution)/shard_map/dot_general | solution.py:151
  399.3 119.3 %reduce-scatter.2.cloned.1.call-done = bf16[4,128,768]{2,1,0:T(8,128)(2,1)} async-done(((bf16[4,128,6144]{2,1,0:T(8,128)(2,1)}), bf16[4,128,768]{2,1,0:T(8,128)(2,1)}) %reduce-scatter.2.cloned.1.call-update) | async-done | bytes 786448 | tf_op jit(solution)/shard_map/reduce_scatter | solution.py:152
  518.6 2.7 add_convert_fusion.2
  (42 shorter events, 0.7 us)
Async XLA Ops:
  6.5 1.4 copy-start
  6.5 104.8 %all-gather.7.cloned.1.call-start = ((), (), s32[]{:S(2)}) async-start(), calls=%async_computation.1 | async-start | bytes 7077888 | tf_op jit(solution)/shard_map/all_gather | solution.py:68
  6.5 9.9 %copy-start.5 = (s32[8,8]{1,0:T(8,128)S(1)}, s32[8,8]{1,0:T(8,128)}, u32[]{:S(2)}) copy-start(s32[8,8]{1,0:T(8,128)} %param.16) | copy-start | bytes 772
  6.5 10.1 %copy-start.7 = (s32[8]{0:T(128)S(1)}, s32[8]{0:T(128)}, u32[]{:S(2)}) copy-start(s32[8]{0:T(128)} %param.15) | copy-start | bytes 100
  6.5 10.4 %copy-start.4 = (bf16[4,128,2,128]{3,2,1,0:T(2,128)(2,1)S(1)}, bf16[4,128,2,128]{3,2,1,0:T(2,128)(2,1)}, u32[]{:S(2)}) copy-start(bf16[4,128,2,128]{3,2,1,0:T(2,128)(2,1)} %param.18) | copy-start | bytes 786436
  7.3 203.6 %all-gather.11.cloned.1.call-start = ((), (), s32[]{:S(2)}) async-start(), calls=%async_computation.3 | async-start | bytes 7077888 | tf_op jit(solution)/shard_map/all_gather | solution.py:74
  8.9 10.4 %copy-start.3 = (bf16[4,6,6144]{2,0,1:T(4,128)(2,1)S(1)}, bf16[4,6,6144]{2,0,1:T(4,128)(2,1)}, u32[]{:S(2)}) copy-start(bf16[4,6,6144]{2,0,1:T(4,128)(2,1)} %param.19) | copy-start | bytes 884740
  8.9 10.4 %copy-start.6 = (s32[4]{0:T(128)S(1)}, s32[4]{0:T(128)}, u32[]{:S(2)}) copy-start(s32[4]{0:T(128)} %param.14) | copy-start | bytes 52
  8.9 241.7 %all-gather.9.cloned.1.call-start = ((), (), s32[]{:S(2)}) async-start(), calls=%async_computation.2 | async-start | bytes 1179648 | tf_op jit(solution)/shard_map/all_gather | solution.py:115
  111.4 4.6 copy-start.2
  132.4 143.5 %all-gather.13.cloned.1.call-start = ((), (), s32[]{:S(2)}) async-start(), calls=%async_computation.4 | async-start | bytes 18874368 | tf_op jit(solution)/shard_map/all_gather | solution.py:73
  210.9 170.1 %all-gather.15.cloned.1.call-start = ((), (), s32[]{:S(2)}) async-start(), calls=%async_computation.5 | async-start | bytes 9437184 | tf_op jit(solution)/shard_map/all_gather | solution.py:77
  211.5 179.6 %all-gather.17.cloned.1.call-start = ((), (), s32[]{:S(2)}) async-start(), calls=%async_computation.6 | async-start | bytes 9437184 | tf_op jit(solution)/shard_map/all_gather | solution.py:78
  212.1 306.5 %reduce-scatter.2.cloned.1.call-start = ((), (), s32[]{:S(2)}) async-start(), calls=%async_computation.7 | async-start | bytes 7077888 | tf_op jit(solution)/shard_map/reduce_scatter | solution.py:152
  391.1 130.2 %copy-start.1 = (bf16[128,6144]{1,0:T(8,128)(2,1)S(1)}, bf16[128,6144]{1,0:T(8,128)(2,1)}, u32[]{:S(2)}) copy-start(bf16[128,6144]{1,0:T(8,128)(2,1)} %param.21) | copy-start | bytes 4718596
Sparse Core Ops, SparseCore 0:
  9.6 101.7 all-gather.6
  113.5 97.2 all-gather.10
  212.9 37.7 all-gather.8
  252.1 23.7 all-gather.12
  277.3 16.7 all-gather.14
  295.5 17.9 all-gather.16
  399.4 119.1 reduce-scatter.1

commit v2 on v1

--- a/solution.py
+++ b/solution.py
@@ -1,8 +1,11 @@
+import functools
 import math
 
 import jax
 import jax.numpy as jnp
 from jax import lax
+from jax.experimental import pallas as pl
+from jax.experimental.pallas import tpu as pltpu
 from jax.sharding import PartitionSpec as P
 
 HEAD_DIM = 128
@@ -15,6 +18,84 @@
 
 def normalize(values):
     return values * lax.rsqrt(jnp.mean(values * values, axis=-1, keepdims=True) + EPSILON)
+
+
+def snake_cycle(count):
+    return list(range(0, count, 2)) + list(range(count - 1, 0, -2)) if count % 2 == 0 else list(range(count))
+
+
+def ring_gather(block, axis_name, count):
+    cycle = snake_cycle(count)
+    ahead = [(cycle[p], cycle[(p + 1) % count]) for p in range(count)]
+    behind = [(cycle[p], cycle[(p - 1) % count]) for p in range(count)]
+    blocks = [block]
+    forward = block
+    for _ in range(count // 2):
+        forward = lax.ppermute(forward, axis_name, ahead)
+        blocks.append(forward)
+    backward = block
+    for _ in range((count - 1) // 2):
+        backward = lax.ppermute(backward, axis_name, behind)
+        blocks.append(backward)
+    return blocks
+
+
+def out_proj_kernel(group_count, tiles_per_half, span_ref, *refs):
+    att_refs = refs[:group_count]
+    mine_refs = refs[group_count:2 * group_count]
+    other_refs = refs[2 * group_count:3 * group_count]
+    out_ref = refs[3 * group_count]
+    tile = pl.program_id(0)
+
+    def accumulate(w_refs):
+        total = None
+        for group in range(group_count):
+            term = jnp.dot(att_refs[group][...], w_refs[group][...], preferred_element_type=jnp.float32)
+            term = term.astype(jnp.bfloat16).astype(jnp.float32)
+            total = term if total is None else total + term
+        out_ref[...] = total
+
+    @pl.when(tile < tiles_per_half)
+    def _():
+        accumulate(mine_refs)
+
+    @pl.when(tile >= tiles_per_half)
+    def _():
+        accumulate(other_refs)
+
+
+def grouped_out_proj(span_index, att_blocks, mine_blocks, other_blocks, tile_width=512):
+    group_count = len(att_blocks)
+    token_count, head_width = att_blocks[0].shape
+    half_width = mine_blocks[0].shape[1]
+    tile_width = min(tile_width, half_width)
+    tiles_per_half = half_width // tile_width
+    att_spec = pl.BlockSpec((token_count, head_width), lambda n, s: (0, 0))
+    mine_spec = pl.BlockSpec(
+        (head_width, tile_width), lambda n, s: (0, jnp.minimum(n, tiles_per_half - 1))
+    )
+    other_spec = pl.BlockSpec(
+        (head_width, tile_width), lambda n, s: (0, jnp.maximum(n - tiles_per_half, 0))
+    )
+    out_spec = pl.BlockSpec(
+        (token_count, tile_width),
+        lambda n, s: (0, ((n // tiles_per_half + s[0]) % 2) * tiles_per_half + n % tiles_per_half),
+    )
+    flops = 2 * token_count * head_width * group_count * half_width * 2
+    moved = 2 * (group_count * token_count * head_width + 2 * group_count * head_width * half_width)
+    return pl.pallas_call(
+        functools.partial(out_proj_kernel, group_count, tiles_per_half),
+        out_shape=jax.ShapeDtypeStruct((token_count, 2 * half_width), jnp.float32),
+        grid_spec=pltpu.PrefetchScalarGridSpec(
+            num_scalar_prefetch=1,
+            grid=(2 * tiles_per_half,),
+            in_specs=[att_spec] * group_count + [mine_spec] * group_count + [other_spec] * group_count,
+            out_specs=out_spec,
+        ),
+        cost_estimate=pl.CostEstimate(
+            flops=flops, bytes_accessed=moved + token_count * 2 * half_width * 4, transcendentals=0
+        ),
+    )(jnp.reshape(span_index, (1,)).astype(jnp.int32), *att_blocks, *mine_blocks, *other_blocks)
 
 
 def select_row(source, target):
@@ -66,13 +147,14 @@
     row_count = hidden_in.shape[1]
     token_count = local_count * row_count
     gathered = lax.all_gather(hidden_in, "tp", axis=2, tiled=True).astype(jnp.float32)
-    gather_weights = tp_count * w_out.size * w_out.dtype.itemsize <= WEIGHT_GATHER_BYTES
+    gather_weights = (
+        tp_count * w_out.size * w_out.dtype.itemsize <= WEIGHT_GATHER_BYTES and span_count == 2
+    )
     if gather_weights:
         column_part = model_width // span_count
         w_out_part = lax.dynamic_slice_in_dim(w_out, span_index * column_part, column_part, 1)
-        w_out_full = lax.all_gather(
-            lax.all_gather(w_out_part, "tp", axis=0, tiled=True), "span", axis=1, tiled=True
-        )
+        mine_blocks = ring_gather(w_out_part, "tp", tp_count)
+        other_blocks = [lax.ppermute(b, "span", [(0, 1), (1, 0)]) for b in mine_blocks]
     up_full, down_full = (
         lax.all_gather(w_up, "span", axis=1, tiled=True),
         lax.all_gather(w_down, "span", axis=0, tiled=True),
@@ -112,20 +194,8 @@
         lambda q_rows, c_seen, f_seen: attend(q_rows, cache_all, fresh_all, c_seen, f_seen)
     )(queries, cache_seen, fresh_seen)
     if gather_weights:
-        attended_all = lax.all_gather(
-            attended.reshape(token_count, per_device), "tp", axis=1, tiled=True
-        )
-        def add_group(group, running):
-            term = jnp.dot(
-                lax.dynamic_slice_in_dim(attended_all, group * per_device, per_device, 1),
-                lax.dynamic_slice_in_dim(w_out_full, group * per_device, per_device, 0),
-                preferred_element_type=jnp.float32,
-            )
-            return running + term.astype(jnp.bfloat16).astype(jnp.float32)
-
-        attn_out = lax.fori_loop(
-            0, tp_count, add_group, jnp.zeros((token_count, model_width), jnp.float32)
-        )
+        att_blocks = ring_gather(attended.reshape(token_count, per_device), "tp", tp_count)
+        attn_out = grouped_out_proj(span_index, att_blocks, mine_blocks, other_blocks)
         attn_out = attn_out.reshape(local_count, row_count, model_width)
         residual_full = gathered + mod_rows[:, 2][:, None] * attn_out
         mlp_in = (

time: 529 us -> 385 us (0.73)
  waiting for transfers between devices: 355 us -> 258 us
  matrix products: 119 us -> 26.9 us
  starting transfers between devices: 0.42 us -> 24.8 us
  Pallas kernels: 0 us -> 20.4 us
    all_gather x3 -> x0, waiting for transfers between devices: 142 us -> none  [the longest x1 78.4 us: local(): lax.all_gather(w_out_part, 'tp', axis=0, tiled=True)]
    dot_general x8 -> x0, matrix products: 91.8 us -> none  [add_group(): jnp.dot(lax.dynamic_slice_in_dim(attended_all, group * per_device, per_de...]
    ppermute x0 -> x22, waiting for transfers between devices: none -> 69.9 us  [the longest x8 53.5 us: ring_gather(): forward = lax.ppermute(forward, axis_name, ahead)]
    ppermute x0 -> x22, starting transfers between devices: none -> 24.7 us  [the longest x8 18.7 us: ring_gather(): forward = lax.ppermute(forward, axis_name, ahead)]
    all_gather x1, waiting for transfers between devices: 91.6 us -> 68.5 us  [local(): lax.all_gather(hidden_in, 'tp', axis=2, tiled=True).astype(jnp.float32)]
    pallas_call x0 -> x1, Pallas kernels: none -> 20.4 us  [grouped_out_proj(): pl.pallas_call(functools.partial(out_proj_kernel, group_count, tiles_per_...]
  transfers between devices with their start and end apart: 7 -> 26, of which waited for: 5 -> 10; matrix products, arithmetic and copies ran while one was open for 27% -> 13% of each run, Pallas kernels for 0% -> 5%
where the time goes in v2:
time: 385 us; the launch traced here: 384 us
  waiting for transfers between devices  258 us (67%)
  matrix products  26.9 us (7%)
  other arithmetic  25.2 us (7%)
  starting transfers between devices  24.8 us (6%)
  Pallas kernels  20.4 us (5%)
  between operations  14.2 us (4%)
  local copies, waits for them, and re-layouts  10.7 us (3%)
  blocking collectives  4.74 us (1%)
    reduce_scatter x1, waiting for transfers between devices, local(): lax.psum_scatter(down_terms.astype(jnp.bfloat16), 'tp', scatter_dimension...  118 us
    all_gather x1, waiting for transfers between devices, local(): lax.all_gather(hidden_in, 'tp', axis=2, tiled=True).astype(jnp.float32)  68.5 us
    ppermute x8, waiting for transfers between devices, ring_gather(): forward = lax.ppermute(forward, axis_name, ahead)  53.5 us
    pallas_call x1, Pallas kernels, grouped_out_proj(): pl.pallas_call(functools.partial(out_proj_kernel, group_count, tiles_per_...  20.4 us
    ppermute x8, starting transfers between devices, ring_gather(): forward = lax.ppermute(forward, axis_name, ahead)  18.7 us
    reduce_sum x2, other arithmetic, normalize(): jnp.mean(values * values, axis=-1, keepdims=True) + EPSILON  17.7 us
    ppermute x6, waiting for transfers between devices, ring_gather(): backward = lax.ppermute(backward, axis_name, behind)  16.4 us
    dot_general x1, matrix products, local(): pre_act = jnp.dot(mlp_in, up_full, preferred_element_type=jnp.float32)  10 us
  transfers between devices with their start and end apart: 26, of which 10 were waited for; matrix products, arithmetic and copies ran while one was open for 13% of the time, Pallas kernels for 5%

profile of v2, /device:TPU:0, one launch (start us, length us, event | category | flops | bytes accessed | tf_op | source)
XLA Modules:
  0.0 384.5 jit_solution(3099630063984866082)
XLA Ops:
  6.5 0.7 all-gather.4.cloned.1.call-update
  7.3 0.7 all-gather.6.cloned.1.call-update
  8.2 3.1 collective-permute-start.7
  11.4 6.7 %copy.26 = bf16[6144,3,128]{0,2,1:T(8,128)(2,1)} copy(bf16[6144,3,128]{2,0,1:T(8,128)(2,1)} %param.18) | data formatting | bytes 9437184 | tf_op args[7]
  19.3 0.4 fusion.31
  19.6 0.7 slice_bitcast_fusion.5
  20.3 15.3 %collective-permute-done.7.refs_9_ = bf16[128,3072]{1,0:T(8,128)(2,1)} collective-permute-done((bf16[128,3072]{1,0:T(8,128)(2,1)S(1)}, bf16[128,3072]{1,0:T(8,128)(2,1)}, u32[]{:S(2)}, u32[]{:S(2)}) %collective-permute-start.7) | collective-permute-done | bytes 786464 | tf_op jit(solution)/shard_map/ppermute | solution.py:34
  35.6 8.3 %collective-permute-start.8 = (bf16[128,3072]{1,0:T(8,128)(2,1)}, bf16[128,3072]{1,0:T(8,128)(2,1)}, u32[]{:S(2)}, u32[]{:S(2)}) collective-permute-start(bf16[128,3072]{1,0:T(8,128)(2,1)} %collective-permute-done.7.refs_9_), channel_id=1, source_target_pairs={{0,2},{2,4},{4,6},{6,7},{7,5},{5,3},{3,1},{1,0},{8,10},{10,12},{12... | collective-permute-start | bytes 2359304 | tf_op jit(solution)/shard_map/ppermute | solution.py:34
  44.1 2.2 all_gather.16
  46.5 0.4 collective-permute-start.19
  46.9 23.4 %collective-permute-done.8.refs_10_ = bf16[128,3072]{1,0:T(8,128)(2,1)} collective-permute-done((bf16[128,3072]{1,0:T(8,128)(2,1)}, bf16[128,3072]{1,0:T(8,128)(2,1)}, u32[]{:S(2)}, u32[]{:S(2)}) %collective-permute-start.8) | collective-permute-done | bytes 786464 | tf_op jit(solution)/shard_map/ppermute | solution.py:34
  70.3 2.5 collective-permute-start.9
  72.8 68.5 %all-gather.4.cloned.1.call-done = bf16[4,128,6144]{2,1,0:T(8,128)(2,1)} async-done(((bf16[4,128,768]{2,1,0:T(8,128)(2,1)}), bf16[4,128,6144]{2,1,0:T(8,128)(2,1)}) %all-gather.4.cloned.1.call-update) | async-done | bytes 6291472 | tf_op jit(solution)/shard_map/all_gather | solution.py:149
  141.3 4.2 %fusion = f32[4,128]{1,0:T(4,128)S(1)} fusion(bf16[4,128,6144]{2,1,0:T(8,128)(2,1)} %all-gather.4.cloned.1.call-done), kind=kLoop, calls=%fused_computation.3 | loop fusion | flops 9436672 | bytes 6293504 | tf_op jit(solution)/shard_map/reduce_sum | solution.py:20
  145.5 0.3 copy-done.2
  145.9 2.7 fusion.3
  148.6 6.3 %convolution_convert_fusion.1 = bf16[512,384]{1,0:T(8,128)(2,1)S(1)} fusion(bf16[512,6144]{1,0:T(8,128)(2,1)S(1)} %bitcast.102, bf16[6144,384]{0,1:T(8,128)(2,1)} %bitcast.103), kind=kOutput, calls=%fused_computation.28 | convolution fusion | flops 2416115712 | bytes 11403264 | tf_op jit(solution)/shard_map/dot_general | solution.py:173
  155.8 2.6 all_gather.17
  158.4 0.4 fusion.33
  158.8 0.8 fusion.12
  159.6 0.7 fusion.11
  160.5 0.7 collective-permute-start.13
  161.4 2.7 collective-permute-start.10
  164.1 0.9 divide_convert_fusion
  165.0 0.4 fusion.30
  165.5 16.4 %collective-permute-done.13.refs_15_ = bf16[128,3072]{1,0:T(8,128)(2,1)S(1)} collective-permute-done((bf16[128,3072]{1,0:T(8,128)(2,1)}, bf16[128,3072]{1,0:T(8,128)(2,1)S(1)}, u32[]{:S(2)}, u32[]{:S(2)}) %collective-permute-start.13) | collective-permute-done | bytes 786464 | tf_op jit(solution)/shard_map/ppermute | solution.py:38
  181.9 1.5 collective-permute-done.10.refs_12_
  183.4 0.4 fusion.17
  183.9 0.8 collective-permute-start
  184.7 1.3 collective-permute-start.4
  185.9 3.9 %collective-permute-done.refs_1_ = bf16[512,128]{1,0:T(8,128)(2,1)S(1)} collective-permute-done((bf16[512,128]{1,0:T(8,128)(2,1)S(1)}, bf16[512,128]{1,0:T(8,128)(2,1)S(1)}, u32[]{:S(2)}, u32[]{:S(2)}) %collective-permute-start) | collective-permute-done | bytes 131104 | tf_op jit(solution)/shard_map/ppermute | solution.py:34
  189.8 0.6 collective-permute-start.1
  190.4 1.5 collective-permute-start.5
  191.9 3.1 collective-permute-done.1.refs_2_
  195.0 0.4 collective-permute-start.2
  195.4 1.6 collective-permute-start.6
  197.0 2.9 collective-permute-done.2.refs_3_
  199.9 0.4 collective-permute-start.3
  200.4 0.9 copy-done.8
  201.2 0.2 copy-done.9
  201.5 3.4 collective-permute-done.3.refs_4_
  204.9 0.6 copy-done.20
  205.6 20.4 %shard_map.109 = f32[512,6144]{1,0:T(8,128)} custom-call(s32[1]{0:T(128)} %bitcast.5.span_ref, bf16[512,128]{1,0:T(8,128)(2,1)} %bitcast.110, bf16[512,128]{1,0:T(8,128)(2,1)} %copy-done.14, bf16[512,128]{1,0:T(8,128)(2,1)} %copy-done.16, bf16[512,128]{1,0:T(8,128)(2,1)} %copy-done.18, bf16[512,128]{1,0:T(8,128)(2,1)} %copy-done.20, ...), custom_call_target="tpu_custom_call" | custom-call | flops 6442450944 | bytes 26214400 | tf_op jit(solution)/shard_map/pallas_call | solution.py:86
  226.0 13.4 %multiply_reduce_fusion = (f32[4,128]{1,0:T(4,128)S(1)}, f32[4,128,6144]{2,1,0:T(8,128)}) fusion(f32[4,128,6144]{2,1,0:T(8,128)} %bitcast.101, f32[4,6144]{1,0:T(4,128)S(1)} %get-tuple-element.15, bf16[4,128,6144]{2,1,0:T(8,128)(2,1)} %all-gather.4.cloned.1.call-done), kind=kLoop, calls=%fused_computation.8 | loop fusion | flops 15728128 | bytes 31557632 | tf_op jit(solution)/shard_map/reduce_sum | solution.py:20
  239.5 10.0 %fusion.27 = bf16[4,128,512]{2,1,0:T(8,128)(2,1)S(1)} fusion(bf16[6144,512]{1,0:T(8,128)(2,1)} %all-gather.6.cloned.1.call-done, f32[4,128,6144]{2,1,0:T(8,128)} %get-tuple-element.6, f32[4,6144]{1,0:T(4,128)S(1)} %copy-done.21, f32[4,6144]{1,0:T(4,128)S(1)} %get-tuple-element.11, f32[4,128]{1,0:T(4,128)S(1)} %add_rsqrt_fusion), kind=kOutput, calls=%fused_computation.39 | convolution fusion | flops 3236167680 | bytes 19597312 | tf_op jit(solution)/shard_map/dot_general | solution.py:219
  249.5 8.1 %convolution_convert_fusion = bf16[4,128,6144]{2,1,0:T(8,128)(2,1)} fusion(bf16[4,128,512]{2,1,0:T(8,128)(2,1)S(1)} %fusion.27, bf16[512,6144]{1,0:T(8,128)(2,1)} %all-gather.8.cloned.1.call-done), kind=kOutput, calls=%fused_computation.9 | convolution fusion | flops 3224371200 | bytes 13107200 | tf_op jit(solution)/shard_map/dot_general | solution.py:221
  257.6 117.6 %reduce-scatter.2.cloned.1.call-done = bf16[4,128,768]{2,1,0:T(8,128)(2,1)} async-done(((bf16[4,128,6144]{2,1,0:T(8,128)(2,1)}), bf16[4,128,768]{2,1,0:T(8,128)(2,1)}) %reduce-scatter.2.cloned.1.call-update) | async-done | bytes 786448 | tf_op jit(solution)/shard_map/reduce_scatter | solution.py:222
  375.2 2.7 add_convert_fusion.2
  (102 shorter events, 2.5 us)
Async XLA Ops:
  6.5 1.5 copy-start
  6.5 134.8 %all-gather.4.cloned.1.call-start = ((), (), s32[]{:S(2)}) async-start(), calls=%async_computation.1 | async-start | bytes 7077888 | tf_op jit(solution)/shard_map/all_gather | solution.py:149
  7.3 232.2 %all-gather.6.cloned.1.call-start = ((), (), s32[]{:S(2)}) async-start(), calls=%async_computation.2 | async-start | bytes 9437184 | tf_op jit(solution)/shard_map/all_gather | solution.py:159
  8.0 241.5 %all-gather.8.cloned.1.call-start = ((), (), s32[]{:S(2)}) async-start(), calls=%async_computation.3 | async-start | bytes 9437184 | tf_op jit(solution)/shard_map/all_gather | solution.py:160
  8.1 10.0 %copy-start.3 = (bf16[128,3072]{1,0:T(8,128)(2,1)}, bf16[128,3072]{1,0:T(8,128)(2,1)S(1)}, u32[]{:S(2)}) copy-start(bf16[128,3072]{1,0:T(8,128)(2,1)S(1)} %constant_dynamic-slice_fusion.refs_8_) | copy-start | bytes 2359300
  8.2 27.4 %collective-permute-start.7 = (bf16[128,3072]{1,0:T(8,128)(2,1)S(1)}, bf16[128,3072]{1,0:T(8,128)(2,1)}, u32[]{:S(2)}, u32[]{:S(2)}) collective-permute-start(bf16[128,3072]{1,0:T(8,128)(2,1)S(1)} %constant_dynamic-slice_fusion.refs_8_), channel_id=1, source_target_pairs={{0,2},{2,4},{4,6},{6,7},{7,5},{5,3},{3,1},{1,0},{8,10},{10,12},{12... | collective-permute-start | bytes 2359304 | tf_op jit(solution)/shard_map/ppermute | solution.py:34
  11.2 35.3 %collective-permute-start.11 = (bf16[128,3072]{1,0:T(8,128)(2,1)S(1)}, bf16[128,3072]{1,0:T(8,128)(2,1)}, u32[]{:S(2)}, u32[]{:S(2)}) collective-permute-start(bf16[128,3072]{1,0:T(8,128)(2,1)S(1)} %constant_dynamic-slice_fusion.refs_8_), channel_id=1, source_target_pairs={{0,1},{2,0},{4,2},{6,4},{7,6},{5,7},{3,5},{1,3},{8,9},{10,8},{12,1... | collective-permute-start | bytes 2359304 | tf_op jit(solution)/shard_map/ppermute | solution.py:38
  11.2 149.1 %collective-permute-start.14 = (bf16[128,3072]{1,0:T(8,128)(2,1)S(1)}, bf16[128,3072]{1,0:T(8,128)(2,1)}, u32[]{:S(2)}, u32[]{:S(2)}) collective-permute-start(bf16[128,3072]{1,0:T(8,128)(2,1)S(1)} %constant_dynamic-slice_fusion.refs_8_), channel_id=1, source_target_pairs={{0,8},{8,0},{1,9},{9,1},{2,10},{10,2},{3,11},{11,3},{4,12},{12,4},... | collective-permute-start | bytes 2359304 | tf_op jit(solution)/shard_map/ppermute | solution.py:157
  11.3 7.6 %copy-start.22 = (s32[8,8]{1,0:T(8,128)S(1)}, s32[8,8]{1,0:T(8,128)}, u32[]{:S(2)}) copy-start(s32[8,8]{1,0:T(8,128)} %param.14) | copy-start | bytes 772
  11.3 7.8 %copy-start.24 = (s32[8]{0:T(128)S(1)}, s32[8]{0:T(128)}, u32[]{:S(2)}) copy-start(s32[8]{0:T(128)} %param.13) | copy-start | bytes 100
  11.3 8.0 %copy-start.11 = (bf16[4,6,6144]{2,0,1:T(4,128)(2,1)S(1)}, bf16[4,6,6144]{2,0,1:T(4,128)(2,1)}, u32[]{:S(2)}) copy-start(bf16[4,6,6144]{2,0,1:T(4,128)(2,1)} %param.17) | copy-start | bytes 884740
  11.3 8.0 %copy-start.23 = (s32[4]{0:T(128)S(1)}, s32[4]{0:T(128)}, u32[]{:S(2)}) copy-start(s32[4]{0:T(128)} %param.12) | copy-start | bytes 52
  11.3 32.7 %copy-start.12 = (bf16[4,128,2,128]{3,2,1,0:T(2,128)(2,1)S(1)}, bf16[4,128,2,128]{3,2,1,0:T(2,128)(2,1)}, u32[]{:S(2)}) copy-start(bf16[4,128,2,128]{3,2,1,0:T(2,128)(2,1)} %param.16) | copy-start | bytes 786436
  11.3 363.9 %reduce-scatter.2.cloned.1.call-start = ((), (), s32[]{:S(2)}) async-start(), calls=%async_computation.4 | async-start | bytes 7077888 | tf_op jit(solution)/shard_map/reduce_scatter | solution.py:222
  35.6 34.7 %collective-permute-start.8 = (bf16[128,3072]{1,0:T(8,128)(2,1)}, bf16[128,3072]{1,0:T(8,128)(2,1)}, u32[]{:S(2)}, u32[]{:S(2)}) collective-permute-start(bf16[128,3072]{1,0:T(8,128)(2,1)} %collective-permute-done.7.refs_9_), channel_id=1, source_target_pairs={{0,2},{2,4},{4,6},{6,7},{7,5},{5,3},{3,1},{1,0},{8,10},{10,12},{12... | collective-permute-start | bytes 2359304 | tf_op jit(solution)/shard_map/ppermute | solution.py:34
  46.3 115.0 %collective-permute-start.15 = (bf16[128,3072]{1,0:T(8,128)(2,1)}, bf16[128,3072]{1,0:T(8,128)(2,1)}, u32[]{:S(2)}, u32[]{:S(2)}) collective-permute-start(bf16[128,3072]{1,0:T(8,128)(2,1)} %collective-permute-done.7.refs_9_), channel_id=1, source_target_pairs={{0,8},{8,0},{1,9},{9,1},{2,10},{10,2},{3,11},{11,3},{4,12},{12,4},... | collective-permute-start | bytes 2359304 | tf_op jit(solution)/shard_map/ppermute | solution.py:157
  46.5 114.1 %collective-permute-start.12 = (bf16[128,3072]{1,0:T(8,128)(2,1)}, bf16[128,3072]{1,0:T(8,128)(2,1)}, u32[]{:S(2)}, u32[]{:S(2)}) collective-permute-start(bf16[128,3072]{1,0:T(8,128)(2,1)} %collective-permute-done.11.refs_13_), channel_id=1, source_target_pairs={{0,1},{2,0},{4,2},{6,4},{7,6},{5,7},{3,5},{1,3},{8,9},{10,8},{12,1... | collective-permute-start | bytes 2359304 | tf_op jit(solution)/shard_map/ppermute | solution.py:38
  46.5 118.9 %collective-permute-start.19 = (bf16[128,3072]{1,0:T(8,128)(2,1)}, bf16[128,3072]{1,0:T(8,128)(2,1)}, u32[]{:S(2)}, u32[]{:S(2)}) collective-permute-start(bf16[128,3072]{1,0:T(8,128)(2,1)} %collective-permute-done.11.refs_13_), channel_id=1, source_target_pairs={{0,8},{8,0},{1,9},{9,1},{2,10},{10,2},{3,11},{11,3},{4,12},{12,4},... | collective-permute-start | bytes 2359304 | tf_op jit(solution)/shard_map/ppermute | solution.py:157
  70.3 91.1 %collective-permute-start.9 = (bf16[128,3072]{1,0:T(8,128)(2,1)}, bf16[128,3072]{1,0:T(8,128)(2,1)}, u32[]{:S(2)}, u32[]{:S(2)}) collective-permute-start(bf16[128,3072]{1,0:T(8,128)(2,1)} %collective-permute-done.8.refs_10_), channel_id=1, source_target_pairs={{0,2},{2,4},{4,6},{6,7},{7,5},{5,3},{3,1},{1,0},{8,10},{10,12},{12... | collective-permute-start | bytes 2359304 | tf_op jit(solution)/shard_map/ppermute | solution.py:34
  141.3 4.6 %copy-start.2 = (bf16[4,128,6144]{2,1,0:T(8,128)(2,1)S(1)}, bf16[4,128,6144]{2,1,0:T(8,128)(2,1)}, u32[]{:S(2)}) copy-start(bf16[4,128,6144]{2,1,0:T(8,128)(2,1)} %all-gather.4.cloned.1.call-done) | copy-start | bytes 18874372
  160.3 23.5 %collective-permute-start.16 = (bf16[128,3072]{1,0:T(8,128)(2,1)}, bf16[128,3072]{1,0:T(8,128)(2,1)S(1)}, u32[]{:S(2)}, u32[]{:S(2)}) collective-permute-start(bf16[128,3072]{1,0:T(8,128)(2,1)} %collective-permute-done.8.refs_10_), channel_id=1, source_target_pairs={{0,8},{8,0},{1,9},{9,1},{2,10},{10,2},{3,11},{11,3},{4,12},{12,4},... | collective-permute-start | bytes 2359304 | tf_op jit(solution)/shard_map/ppermute | solution.py:157
  160.5 21.3 %collective-permute-start.13 = (bf16[128,3072]{1,0:T(8,128)(2,1)}, bf16[128,3072]{1,0:T(8,128)(2,1)S(1)}, u32[]{:S(2)}, u32[]{:S(2)}) collective-permute-start(bf16[128,3072]{1,0:T(8,128)(2,1)} %collective-permute-done.12.refs_14_), channel_id=1, source_target_pairs={{0,1},{2,0},{4,2},{6,4},{7,6},{5,7},{3,5},{1,3},{8,9},{10,8},{12,1... | collective-permute-start | bytes 2359304 | tf_op jit(solution)/shard_map/ppermute | solution.py:38
  161.3 23.4 %collective-permute-start.20 = (bf16[128,3072]{1,0:T(8,128)(2,1)}, bf16[128,3072]{1,0:T(8,128)(2,1)S(1)}, u32[]{:S(2)}, u32[]{:S(2)}) collective-permute-start(bf16[128,3072]{1,0:T(8,128)(2,1)} %collective-permute-done.12.refs_14_), channel_id=1, source_target_pairs={{0,8},{8,0},{1,9},{9,1},{2,10},{10,2},{3,11},{11,3},{4,12},{12,4},... | collective-permute-start | bytes 2359304 | tf_op jit(solution)/shard_map/ppermute | solution.py:157
  161.4 22.0 %collective-permute-start.10 = (bf16[128,3072]{1,0:T(8,128)(2,1)}, bf16[128,3072]{1,0:T(8,128)(2,1)S(1)}, u32[]{:S(2)}, u32[]{:S(2)}) collective-permute-start(bf16[128,3072]{1,0:T(8,128)(2,1)} %collective-permute-done.9.refs_11_), channel_id=1, source_target_pairs={{0,2},{2,4},{4,6},{6,7},{7,5},{5,3},{3,1},{1,0},{8,10},{10,12},{12... | collective-permute-start | bytes 2359304 | tf_op jit(solution)/shard_map/ppermute | solution.py:34
  165.4 34.9 %collective-permute-start.17 = (bf16[128,3072]{1,0:T(8,128)(2,1)}, bf16[128,3072]{1,0:T(8,128)(2,1)S(1)}, u32[]{:S(2)}, u32[]{:S(2)}) collective-permute-start(bf16[128,3072]{1,0:T(8,128)(2,1)} %collective-permute-done.9.refs_11_), channel_id=1, source_target_pairs={{0,8},{8,0},{1,9},{9,1},{2,10},{10,2},{3,11},{11,3},{4,12},{12,4},... | collective-permute-start | bytes 2359304 | tf_op jit(solution)/shard_map/ppermute | solution.py:157
  181.9 23.7 %copy-start.5 = (bf16[128,3072]{1,0:T(8,128)(2,1)}, bf16[128,3072]{1,0:T(8,128)(2,1)S(1)}, u32[]{:S(2)}) copy-start(bf16[128,3072]{1,0:T(8,128)(2,1)S(1)} %collective-permute-done.13.refs_15_) | copy-start | bytes 2359300
  181.9 18.5 %collective-permute-start.21 = (bf16[128,3072]{1,0:T(8,128)(2,1)S(1)}, bf16[128,3072]{1,0:T(8,128)(2,1)S(1)}, u32[]{:S(2)}, u32[]{:S(2)}) collective-permute-start(bf16[128,3072]{1,0:T(8,128)(2,1)S(1)} %collective-permute-done.13.refs_15_), channel_id=1, source_target_pairs={{0,8},{8,0},{1,9},{9,1},{2,10},{10,2},{3,11},{11,3},{4,12},{12,4},... | collective-permute-start | bytes 2359304 | tf_op jit(solution)/shard_map/ppermute | solution.py:157
  183.4 17.0 %copy-start.7 = (bf16[128,3072]{1,0:T(8,128)(2,1)}, bf16[128,3072]{1,0:T(8,128)(2,1)S(1)}, u32[]{:S(2)}) copy-start(bf16[128,3072]{1,0:T(8,128)(2,1)S(1)} %collective-permute-done.10.refs_12_) | copy-start | bytes 2359300
  183.4 17.0 %collective-permute-start.18 = (bf16[128,3072]{1,0:T(8,128)(2,1)S(1)}, bf16[128,3072]{1,0:T(8,128)(2,1)S(1)}, u32[]{:S(2)}, u32[]{:S(2)}) collective-permute-start(bf16[128,3072]{1,0:T(8,128)(2,1)S(1)} %collective-permute-done.10.refs_12_), channel_id=1, source_target_pairs={{0,8},{8,0},{1,9},{9,1},{2,10},{10,2},{3,11},{11,3},{4,12},{12,4},... | collective-permute-start | bytes 2359304 | tf_op jit(solution)/shard_map/ppermute | solution.py:157
  183.8 21.8 %copy-start.13 = (bf16[128,4,128]{0,2,1:T(8,128)(2,1)}, bf16[128,4,128]{0,2,1:T(8,128)(2,1)S(1)}, u32[]{:S(2)}) copy-start(bf16[128,4,128]{0,2,1:T(8,128)(2,1)S(1)} %fusion.17) | copy-start | bytes 393220
  183.9 21.7 %copy-start.4 = (bf16[128,3072]{1,0:T(8,128)(2,1)}, bf16[128,3072]{1,0:T(8,128)(2,1)S(1)}, u32[]{:S(2)}) copy-start(bf16[128,3072]{1,0:T(8,128)(2,1)S(1)} %collective-permute-done.16.refs_18_) | copy-start | bytes 2359300
  183.9 6.0 %collective-permute-start = (bf16[512,128]{1,0:T(8,128)(2,1)S(1)}, bf16[512,128]{1,0:T(8,128)(2,1)S(1)}, u32[]{:S(2)}, u32[]{:S(2)}) collective-permute-start(bf16[512,128]{1,0:T(8,128)(2,1)S(1)} %bitcast.108), channel_id=1, source_target_pairs={{0,2},{2,4},{4,6},{6,7},{7,5},{5,3},{3,1},{1,0},{8,10},{10,12},{12... | collective-permute-start | bytes 393224 | tf_op jit(solution)/shard_map/ppermute | solution.py:34
  184.7 20.9 %copy-start.6 = (bf16[128,3072]{1,0:T(8,128)(2,1)}, bf16[128,3072]{1,0:T(8,128)(2,1)S(1)}, u32[]{:S(2)}) copy-start(bf16[128,3072]{1,0:T(8,128)(2,1)S(1)} %collective-permute-done.20.refs_22_) | copy-start | bytes 2359300
  184.7 5.7 %collective-permute-start.4 = (bf16[512,128]{1,0:T(8,128)(2,1)S(1)}, bf16[512,128]{1,0:T(8,128)(2,1)S(1)}, u32[]{:S(2)}, u32[]{:S(2)}) collective-permute-start(bf16[512,128]{1,0:T(8,128)(2,1)S(1)} %bitcast.109), channel_id=1, source_target_pairs={{0,1},{2,0},{4,2},{6,4},{7,6},{5,7},{3,5},{1,3},{8,9},{10,8},{12,1... | collective-permute-start | bytes 393224 | tf_op jit(solution)/shard_map/ppermute | solution.py:38
  189.8 15.8 %copy-start.14 = (bf16[512,128]{1,0:T(8,128)(2,1)}, bf16[512,128]{1,0:T(8,128)(2,1)S(1)}, u32[]{:S(2)}) copy-start(bf16[512,128]{1,0:T(8,128)(2,1)S(1)} %collective-permute-done.refs_1_) | copy-start | bytes 393220
  189.8 5.1 %collective-permute-start.1 = (bf16[512,128]{1,0:T(8,128)(2,1)S(1)}, bf16[512,128]{1,0:T(8,128)(2,1)S(1)}, u32[]{:S(2)}, u32[]{:S(2)}) collective-permute-start(bf16[512,128]{1,0:T(8,128)(2,1)S(1)} %collective-permute-done.refs_1_), channel_id=1, source_target_pairs={{0,2},{2,4},{4,6},{6,7},{7,5},{5,3},{3,1},{1,0},{8,10},{10,12},{12... | collective-permute-start | bytes 393224 | tf_op jit(solution)/shard_map/ppermute | solution.py:34
  190.4 15.2 %copy-start.15 = (bf16[512,128]{1,0:T(8,128)(2,1)}, bf16[512,128]{1,0:T(8,128)(2,1)S(1)}, u32[]{:S(2)}) copy-start(bf16[512,128]{1,0:T(8,128)(2,1)S(1)} %collective-permute-done.4.refs_5_) | copy-start | bytes 393220
  190.4 5.0 %collective-permute-start.5 = (bf16[512,128]{1,0:T(8,128)(2,1)S(1)}, bf16[512,128]{1,0:T(8,128)(2,1)S(1)}, u32[]{:S(2)}, u32[]{:S(2)}) collective-permute-start(bf16[512,128]{1,0:T(8,128)(2,1)S(1)} %collective-permute-done.4.refs_5_), channel_id=1, source_target_pairs={{0,1},{2,0},{4,2},{6,4},{7,6},{5,7},{3,5},{1,3},{8,9},{10,8},{12,1... | collective-permute-start | bytes 393224 | tf_op jit(solution)/shard_map/ppermute | solution.py:38
  195.0 9.9 %copy-start.16 = (bf16[512,128]{1,0:T(8,128)(2,1)}, bf16[512,128]{1,0:T(8,128)(2,1)S(1)}, u32[]{:S(2)}) copy-start(bf16[512,128]{1,0:T(8,128)(2,1)S(1)} %collective-permute-done.1.refs_2_) | copy-start | bytes 393220
  195.0 5.0 %collective-permute-start.2 = (bf16[512,128]{1,0:T(8,128)(2,1)S(1)}, bf16[512,128]{1,0:T(8,128)(2,1)S(1)}, u32[]{:S(2)}, u32[]{:S(2)}) collective-permute-start(bf16[512,128]{1,0:T(8,128)(2,1)S(1)} %collective-permute-done.1.refs_2_), channel_id=1, source_target_pairs={{0,2},{2,4},{4,6},{6,7},{7,5},{5,3},{3,1},{1,0},{8,10},{10,12},{12... | collective-permute-start | bytes 393224 | tf_op jit(solution)/shard_map/ppermute | solution.py:34
  195.4 9.5 %copy-start.17 = (bf16[512,128]{1,0:T(8,128)(2,1)}, bf16[512,128]{1,0:T(8,128)(2,1)S(1)}, u32[]{:S(2)}) copy-start(bf16[512,128]{1,0:T(8,128)(2,1)S(1)} %collective-permute-done.5.refs_6_) | copy-start | bytes 393220
  195.4 5.9 %collective-permute-start.6 = (bf16[512,128]{1,0:T(8,128)(2,1)S(1)}, bf16[512,128]{1,0:T(8,128)(2,1)S(1)}, u32[]{:S(2)}, u32[]{:S(2)}) collective-permute-start(bf16[512,128]{1,0:T(8,128)(2,1)S(1)} %collective-permute-done.5.refs_6_), channel_id=1, source_target_pairs={{0,1},{2,0},{4,2},{6,4},{7,6},{5,7},{3,5},{1,3},{8,9},{10,8},{12,1... | collective-permute-start | bytes 393224 | tf_op jit(solution)/shard_map/ppermute | solution.py:38
  199.9 5.0 %copy-start.18 = (bf16[512,128]{1,0:T(8,128)(2,1)}, bf16[512,128]{1,0:T(8,128)(2,1)S(1)}, u32[]{:S(2)}) copy-start(bf16[512,128]{1,0:T(8,128)(2,1)S(1)} %collective-permute-done.2.refs_3_) | copy-start | bytes 393220
  199.9 5.0 %collective-permute-start.3 = (bf16[512,128]{1,0:T(8,128)(2,1)S(1)}, bf16[512,128]{1,0:T(8,128)(2,1)S(1)}, u32[]{:S(2)}, u32[]{:S(2)}) collective-permute-start(bf16[512,128]{1,0:T(8,128)(2,1)S(1)} %collective-permute-done.2.refs_3_), channel_id=1, source_target_pairs={{0,2},{2,4},{4,6},{6,7},{7,5},{5,3},{3,1},{1,0},{8,10},{10,12},{12... | collective-permute-start | bytes 393224 | tf_op jit(solution)/shard_map/ppermute | solution.py:34
  201.2 3.7 copy-start.10
  201.5 3.4 copy-start.19
  226.0 13.5 %copy-start.21 = (f32[4,6144]{1,0:T(4,128)S(1)}, f32[4,6144]{1,0:T(4,128)}, u32[]{:S(2)}) copy-start(f32[4,6144]{1,0:T(4,128)} %get-tuple-element.12) | copy-start | bytes 294916
  257.6 120.4 %copy-start.1 = (bf16[128,6144]{1,0:T(8,128)(2,1)S(1)}, bf16[128,6144]{1,0:T(8,128)(2,1)}, u32[]{:S(2)}) copy-start(bf16[128,6144]{1,0:T(8,128)(2,1)} %param.19) | copy-start | bytes 4718596
  (3 other events, 2.7 us)
Sparse Core Ops, SparseCore 0:
  9.6 131.6 all-gather.3
  142.8 17.3 all-gather.5
  161.8 18.3 all-gather.7
  257.7 117.4 reduce-scatter.1

commit v3 on v2

--- a/solution.py
+++ b/solution.py
@@ -40,11 +40,9 @@
     return blocks
 
 
-def out_proj_kernel(group_count, tiles_per_half, span_ref, *refs):
+def out_proj_kernel(group_count, set_count, tiles_per_set, place_ref, *refs):
     att_refs = refs[:group_count]
-    mine_refs = refs[group_count:2 * group_count]
-    other_refs = refs[2 * group_count:3 * group_count]
-    out_ref = refs[3 * group_count]
+    out_ref = refs[-1]
     tile = pl.program_id(0)
 
     def accumulate(w_refs):
@@ -55,47 +53,52 @@
             total = term if total is None else total + term
         out_ref[...] = total
 
-    @pl.when(tile < tiles_per_half)
-    def _():
-        accumulate(mine_refs)
-
-    @pl.when(tile >= tiles_per_half)
-    def _():
-        accumulate(other_refs)
-
-
-def grouped_out_proj(span_index, att_blocks, mine_blocks, other_blocks, tile_width=512):
+    for which in range(set_count):
+        w_refs = refs[group_count * (which + 1):group_count * (which + 2)]
+
+        @pl.when(tile // tiles_per_set == which)
+        def _():
+            accumulate(w_refs)
+
+
+def grouped_out_proj(placement, att_blocks, weight_sets, tile_width=512):
     group_count = len(att_blocks)
+    set_count = len(weight_sets)
     token_count, head_width = att_blocks[0].shape
-    half_width = mine_blocks[0].shape[1]
-    tile_width = min(tile_width, half_width)
-    tiles_per_half = half_width // tile_width
-    att_spec = pl.BlockSpec((token_count, head_width), lambda n, s: (0, 0))
-    mine_spec = pl.BlockSpec(
-        (head_width, tile_width), lambda n, s: (0, jnp.minimum(n, tiles_per_half - 1))
-    )
-    other_spec = pl.BlockSpec(
-        (head_width, tile_width), lambda n, s: (0, jnp.maximum(n - tiles_per_half, 0))
-    )
+    set_width = weight_sets[0][0].shape[1]
+    tile_width = min(tile_width, set_width)
+    tiles_per_set = set_width // tile_width
+    att_spec = pl.BlockSpec((token_count, head_width), lambda n, p: (0, 0))
+
+    def weight_spec(which):
+        return pl.BlockSpec(
+            (head_width, tile_width),
+            lambda n, p: (0, jnp.clip(n - which * tiles_per_set, 0, tiles_per_set - 1)),
+        )
+
     out_spec = pl.BlockSpec(
         (token_count, tile_width),
-        lambda n, s: (0, ((n // tiles_per_half + s[0]) % 2) * tiles_per_half + n % tiles_per_half),
-    )
-    flops = 2 * token_count * head_width * group_count * half_width * 2
-    moved = 2 * (group_count * token_count * head_width + 2 * group_count * head_width * half_width)
+        lambda n, p: (0, p[n // tiles_per_set] * tiles_per_set + n % tiles_per_set),
+    )
+    in_specs = [att_spec] * group_count
+    for which in range(set_count):
+        in_specs += [weight_spec(which)] * group_count
+    width = set_count * set_width
+    flops = 2 * token_count * head_width * group_count * width
+    moved = 2 * group_count * token_count * head_width + 2 * group_count * head_width * width
     return pl.pallas_call(
-        functools.partial(out_proj_kernel, group_count, tiles_per_half),
-        out_shape=jax.ShapeDtypeStruct((token_count, 2 * half_width), jnp.float32),
+        functools.partial(out_proj_kernel, group_count, set_count, tiles_per_set),
+        out_shape=jax.ShapeDtypeStruct((token_count, width), jnp.float32),
         grid_spec=pltpu.PrefetchScalarGridSpec(
             num_scalar_prefetch=1,
-            grid=(2 * tiles_per_half,),
-            in_specs=[att_spec] * group_count + [mine_spec] * group_count + [other_spec] * group_count,
+            grid=(set_count * tiles_per_set,),
+            in_specs=in_specs,
             out_specs=out_spec,
         ),
         cost_estimate=pl.CostEstimate(
-            flops=flops, bytes_accessed=moved + token_count * 2 * half_width * 4, transcendentals=0
+            flops=flops, bytes_accessed=moved + token_count * width * 4, transcendentals=0
         ),
-    )(jnp.reshape(span_index, (1,)).astype(jnp.int32), *att_blocks, *mine_blocks, *other_blocks)
+    )(placement, *att_blocks, *[b for blocks in weight_sets for b in blocks])
 
 
 def select_row(source, target):
@@ -140,6 +143,7 @@
     span_index = lax.axis_index("span")
     tp_rank = lax.axis_index("tp")
     span_count = lax.psum(1, "span")
+    rep_count = lax.psum(1, "rep")
     tp_count = lax.psum(1, "tp")
     model_width = modulation.shape[2]
     share_width = hidden_in.shape[2]
@@ -149,12 +153,29 @@
     gathered = lax.all_gather(hidden_in, "tp", axis=2, tiled=True).astype(jnp.float32)
     gather_weights = (
         tp_count * w_out.size * w_out.dtype.itemsize <= WEIGHT_GATHER_BYTES and span_count == 2
+        and rep_count == 2
     )
     if gather_weights:
-        column_part = model_width // span_count
-        w_out_part = lax.dynamic_slice_in_dim(w_out, span_index * column_part, column_part, 1)
+        rep_index = lax.axis_index("rep")
+        column_part = model_width // (rep_count * span_count)
+        slot = rep_index * span_count + span_index
+        w_out_part = lax.dynamic_slice_in_dim(w_out, slot * column_part, column_part, 1)
         mine_blocks = ring_gather(w_out_part, "tp", tp_count)
-        other_blocks = [lax.ppermute(b, "span", [(0, 1), (1, 0)]) for b in mine_blocks]
+        swap = [(0, 1), (1, 0)]
+        rep_blocks = [lax.ppermute(b, "rep", swap) for b in mine_blocks]
+        weight_sets = [
+            mine_blocks,
+            rep_blocks,
+            [lax.ppermute(b, "span", swap) for b in mine_blocks],
+            [lax.ppermute(b, "span", swap) for b in rep_blocks],
+        ]
+        placement = jnp.stack(
+            [
+                ((rep_index + dr) % 2) * span_count + (span_index + ds) % 2
+                for ds in (0, 1)
+                for dr in (0, 1)
+            ]
+        ).astype(jnp.int32)
     up_full, down_full = (
         lax.all_gather(w_up, "span", axis=1, tiled=True),
         lax.all_gather(w_down, "span", axis=0, tiled=True),
@@ -195,7 +216,7 @@
     )(queries, cache_seen, fresh_seen)
     if gather_weights:
         att_blocks = ring_gather(attended.reshape(token_count, per_device), "tp", tp_count)
-        attn_out = grouped_out_proj(span_index, att_blocks, mine_blocks, other_blocks)
+        attn_out = grouped_out_proj(placement, att_blocks, weight_sets)
         attn_out = attn_out.reshape(local_count, row_count, model_width)
         residual_full = gathered + mod_rows[:, 2][:, None] * attn_out
         mlp_in = (

time: 385 us -> 386 us (level)
    ppermute x8, waiting for transfers between devices: 53.5 us -> 13.5 us  [ring_gather(): forward = lax.ppermute(forward, axis_name, ahead)]
    ppermute x8 -> x24, waiting for transfers between devices: 0.02 us -> 23.9 us  [the longest x8 23.9 us: local(): rep_blocks = [lax.ppermute(b, 'rep', swap) for b in mine_blocks]]
    all_gather x1, waiting for transfers between devices: 68.5 us -> 91.2 us  [local(): lax.all_gather(hidden_in, 'tp', axis=2, tiled=True).astype(jnp.float32)]
    ppermute x8, starting transfers between devices: 18.7 us -> 9.11 us  [ring_gather(): forward = lax.ppermute(forward, axis_name, ahead)]
    ppermute x8 -> x24, starting transfers between devices: 0.93 us -> 10.3 us  [the longest x8 8.77 us: local(): rep_blocks = [lax.ppermute(b, 'rep', swap) for b in mine_blocks]]
    ppermute x6, waiting for transfers between devices: 16.4 us -> 9.41 us  [ring_gather(): backward = lax.ppermute(backward, axis_name, behind)]
    unnamed x57 -> x79, local copies, waits for them, and re-layouts: 9.28 us -> 7.55 us
  transfers between devices with their start and end apart: 26 -> 42, of which waited for: 10 -> 14; matrix products, arithmetic and copies ran while one was open for 13% -> 14% of each run, Pallas kernels for 5% -> 6%
where the time goes in v3:
time: 386 us
  waiting for transfers between devices  255 us (66%)
  matrix products  28.4 us (7%)
  other arithmetic  25.7 us (7%)
  starting transfers between devices  25.4 us (7%)
  Pallas kernels  22 us (6%)
  between operations  14.3 us (4%)
  local copies, waits for them, and re-layouts  10.4 us (3%)
  blocking collectives  4.58 us (1%)
    reduce_scatter x1, waiting for transfers between devices, local(): lax.psum_scatter(down_terms.astype(jnp.bfloat16), 'tp', scatter_dimension...  115 us
    all_gather x1, waiting for transfers between devices, local(): lax.all_gather(hidden_in, 'tp', axis=2, tiled=True).astype(jnp.float32)  91.2 us
    ppermute x8, waiting for transfers between devices, local(): rep_blocks = [lax.ppermute(b, 'rep', swap) for b in mine_blocks]  23.9 us
    pallas_call x1, Pallas kernels, grouped_out_proj(): pl.pallas_call(functools.partial(out_proj_kernel, group_count, set_count,...  22 us
    reduce_sum x2, other arithmetic, normalize(): jnp.mean(values * values, axis=-1, keepdims=True) + EPSILON  17.6 us
    ppermute x8, waiting for transfers between devices, ring_gather(): forward = lax.ppermute(forward, axis_name, ahead)  13.5 us
    dot_general x1, matrix products, local(): pre_act = jnp.dot(mlp_in, up_full, preferred_element_type=jnp.float32)  10 us
    ppermute x6, waiting for transfers between devices, ring_gather(): backward = lax.ppermute(backward, axis_name, behind)  9.41 us
  transfers between devices with their start and end apart: 42, of which 14 were waited for; matrix products, arithmetic and copies ran while one was open for 14% of the time, Pallas kernels for 6%

profile of v3, /device:TPU:0, one launch (start us, length us, event | category | flops | bytes accessed | tf_op | source)
XLA Modules:
  0.0 385.7 jit_solution(8692741801282053762)
XLA Ops:
  6.6 0.7 all-gather.4.cloned.1.call-update
  7.3 0.7 all-gather.6.cloned.1.call-update
  8.1 3.1 collective-permute-start.7
  11.2 1.9 collective-permute-start.14
  13.2 1.3 fusion.31
  14.6 0.7 slice_bitcast_fusion.5
  16.5 6.7 %copy.26 = bf16[6144,3,128]{0,2,1:T(8,128)(2,1)} copy(bf16[6144,3,128]{2,0,1:T(8,128)(2,1)} %param.18) | data formatting | bytes 9437184 | tf_op args[7]
  23.3 2.4 all_gather.16
  25.7 0.8 fusion.40
  26.5 1.5 collective-permute-start.8
  28.6 91.2 %all-gather.4.cloned.1.call-done = bf16[4,128,6144]{2,1,0:T(8,128)(2,1)} async-done(((bf16[4,128,768]{2,1,0:T(8,128)(2,1)}), bf16[4,128,6144]{2,1,0:T(8,128)(2,1)}) %all-gather.4.cloned.1.call-update) | async-done | bytes 6291472 | tf_op jit(solution)/shard_map/all_gather | solution.py:153
  119.8 4.2 %fusion = f32[4,128]{1,0:T(4,128)S(1)} fusion(bf16[4,128,6144]{2,1,0:T(8,128)(2,1)} %all-gather.4.cloned.1.call-done), kind=kLoop, calls=%fused_computation.3 | loop fusion | flops 9436672 | bytes 6293504 | tf_op jit(solution)/shard_map/reduce_sum | solution.py:20
  124.4 2.7 fusion.3
  127.1 1.5 collective-permute-start.19
  128.7 6.8 %convolution_convert_fusion.1 = bf16[512,384]{1,0:T(8,128)(2,1)S(1)} fusion(bf16[512,6144]{1,0:T(8,128)(2,1)S(1)} %bitcast.105, bf16[6144,384]{0,1:T(8,128)(2,1)} %bitcast.106), kind=kOutput, calls=%fused_computation.28 | convolution fusion | flops 2416115712 | bytes 11403264 | tf_op jit(solution)/shard_map/dot_general | solution.py:194
  136.1 2.2 all_gather.17
  139.0 0.6 collective-permute-start.9
  139.6 1.4 collective-permute-start.13
  141.0 0.7 fusion.41
  142.8 1.7 collective-permute-start.20
  144.5 6.2 %collective-permute-done.9.refs_11_ = bf16[128,1536]{1,0:T(8,128)(2,1)} collective-permute-done((bf16[128,1536]{1,0:T(8,128)(2,1)}, bf16[128,1536]{1,0:T(8,128)(2,1)}, u32[]{:S(2)}, u32[]{:S(2)}) %collective-permute-start.9) | collective-permute-done | bytes 393248 | tf_op jit(solution)/shard_map/ppermute | solution.py:34
  151.2 0.8 fusion.12
  152.0 0.7 fusion.11
  152.8 1.9 collective-permute-done.16.refs_18_
  154.7 7.2 %collective-permute-done.20.refs_22_ = bf16[128,1536]{1,0:T(8,128)(2,1)S(1)} collective-permute-done((bf16[128,1536]{1,0:T(8,128)(2,1)}, bf16[128,1536]{1,0:T(8,128)(2,1)S(1)}, u32[]{:S(2)}, u32[]{:S(2)}) %collective-permute-start.20) | collective-permute-done | bytes 393248 | tf_op jit(solution)/shard_map/ppermute | solution.py:165
  163.2 1.5 collective-permute-start.21
  164.7 0.9 divide_convert_fusion
  166.3 5.8 %collective-permute-done.10.refs_12_ = bf16[128,1536]{1,0:T(8,128)(2,1)S(1)} collective-permute-done((bf16[128,1536]{1,0:T(8,128)(2,1)}, bf16[128,1536]{1,0:T(8,128)(2,1)S(1)}, u32[]{:S(2)}, u32[]{:S(2)}) %collective-permute-start.10) | collective-permute-done | bytes 393248 | tf_op jit(solution)/shard_map/ppermute | solution.py:34
  172.1 2.8 collective-permute-done.17.refs_19_
  174.9 6.0 %collective-permute-done.21.refs_23_ = bf16[128,1536]{1,0:T(8,128)(2,1)} collective-permute-done((bf16[128,1536]{1,0:T(8,128)(2,1)}, bf16[128,1536]{1,0:T(8,128)(2,1)}, u32[]{:S(2)}, u32[]{:S(2)}) %collective-permute-start.21) | collective-permute-done | bytes 393248 | tf_op jit(solution)/shard_map/ppermute | solution.py:165
  182.1 1.4 collective-permute-start
  184.0 5.8 %collective-permute-done.18.refs_20_ = bf16[128,1536]{1,0:T(8,128)(2,1)} collective-permute-done((bf16[128,1536]{1,0:T(8,128)(2,1)S(1)}, bf16[128,1536]{1,0:T(8,128)(2,1)}, u32[]{:S(2)}, u32[]{:S(2)}) %collective-permute-start.18) | collective-permute-done | bytes 393248 | tf_op jit(solution)/shard_map/ppermute | solution.py:165
  189.8 1.5 collective-permute-start.4
  191.3 0.7 collective-permute-start.1
  192.0 3.8 collective-permute-done.4.refs_5_
  195.8 1.4 collective-permute-start.5
  197.2 0.7 collective-permute-start.2
  197.9 3.0 collective-permute-done.5.refs_6_
  200.9 1.4 collective-permute-start.6
  202.9 0.6 pad_add_fusion.place_ref
  203.6 2.3 collective-permute-done.6.refs_7_
  205.9 1.5 collective-permute-done.3.refs_4_
  207.5 22.0 %shard_map.109 = f32[512,6144]{1,0:T(8,128)} custom-call(s32[4]{0:T(128)} %pad_add_fusion.place_ref, bf16[512,128]{1,0:T(8,128)(2,1)} %bitcast.113, bf16[512,128]{1,0:T(8,128)(2,1)} %copy-done.26, bf16[512,128]{1,0:T(8,128)(2,1)} %copy-done.28, bf16[512,128]{1,0:T(8,128)(2,1)} %copy-done.30, bf16[512,128]{1,0:T(8,128)(2,1)} %collective-permute-done.3.refs_4_, ...), custom_call_target="tpu_custom_call" | custom-call | flops 6442450944 | bytes 26214400 | tf_op jit(solution)/shard_map/pallas_call | solution.py:89
  229.5 13.3 %multiply_reduce_fusion = (f32[4,128]{1,0:T(4,128)S(1)}, f32[4,128,6144]{2,1,0:T(8,128)}) fusion(f32[4,128,6144]{2,1,0:T(8,128)} %bitcast.104, f32[4,6144]{1,0:T(4,128)S(1)} %get-tuple-element.15, bf16[4,128,6144]{2,1,0:T(8,128)(2,1)} %all-gather.4.cloned.1.call-done), kind=kLoop, calls=%fused_computation.8 | loop fusion | flops 15728128 | bytes 31557632 | tf_op jit(solution)/shard_map/reduce_sum | solution.py:20
  242.8 10.0 %fusion.27 = bf16[4,128,512]{2,1,0:T(8,128)(2,1)S(1)} fusion(bf16[6144,512]{1,0:T(8,128)(2,1)} %all-gather.6.cloned.1.call-done, f32[4,128,6144]{2,1,0:T(8,128)} %get-tuple-element.6, f32[4,6144]{1,0:T(4,128)S(1)} %copy-done.32, f32[4,6144]{1,0:T(4,128)S(1)} %get-tuple-element.11, f32[4,128]{1,0:T(4,128)S(1)} %add_rsqrt_fusion), kind=kOutput, calls=%fused_computation.39 | convolution fusion | flops 3236167680 | bytes 19597312 | tf_op jit(solution)/shard_map/dot_general | solution.py:240
  252.9 8.1 %convolution_convert_fusion = bf16[4,128,6144]{2,1,0:T(8,128)(2,1)} fusion(bf16[4,128,512]{2,1,0:T(8,128)(2,1)S(1)} %fusion.27, bf16[512,6144]{1,0:T(8,128)(2,1)} %all-gather.8.cloned.1.call-done), kind=kOutput, calls=%fused_computation.9 | convolution fusion | flops 3224371200 | bytes 13107200 | tf_op jit(solution)/shard_map/dot_general | solution.py:242
  261.0 115.4 %reduce-scatter.2.cloned.1.call-done = bf16[4,128,768]{2,1,0:T(8,128)(2,1)} async-done(((bf16[4,128,6144]{2,1,0:T(8,128)(2,1)}), bf16[4,128,768]{2,1,0:T(8,128)(2,1)}) %reduce-scatter.2.cloned.1.call-update) | async-done | bytes 786448 | tf_op jit(solution)/shard_map/reduce_scatter | solution.py:243
  376.5 2.7 add_convert_fusion.2
  (157 shorter events, 8.8 us)
Async XLA Ops:
  6.5 113.3 %all-gather.4.cloned.1.call-start = ((), (), s32[]{:S(2)}) async-start(), calls=%async_computation.1 | async-start | bytes 7077888 | tf_op jit(solution)/shard_map/all_gather | solution.py:153
  7.3 235.6 %all-gather.6.cloned.1.call-start = ((), (), s32[]{:S(2)}) async-start(), calls=%async_computation.2 | async-start | bytes 9437184 | tf_op jit(solution)/shard_map/all_gather | solution.py:180
  8.0 244.9 %all-gather.8.cloned.1.call-start = ((), (), s32[]{:S(2)}) async-start(), calls=%async_computation.3 | async-start | bytes 9437184 | tf_op jit(solution)/shard_map/all_gather | solution.py:181
  8.1 18.3 %collective-permute-start.7 = (bf16[128,1536]{1,0:T(8,128)(2,1)S(1)}, bf16[128,1536]{1,0:T(8,128)(2,1)S(1)}, u32[]{:S(2)}, u32[]{:S(2)}) collective-permute-start(bf16[128,1536]{1,0:T(8,128)(2,1)S(1)} %constant_dynamic-slice_fusion.refs_8_), channel_id=1, source_target_pairs={{0,2},{2,4},{4,6},{6,7},{7,5},{5,3},{3,1},{1,0},{8,10},{10,12},{12... | collective-permute-start | bytes 1179656 | tf_op jit(solution)/shard_map/ppermute | solution.py:34
  11.2 17.3 %collective-permute-start.11 = (bf16[128,1536]{1,0:T(8,128)(2,1)S(1)}, bf16[128,1536]{1,0:T(8,128)(2,1)S(1)}, u32[]{:S(2)}, u32[]{:S(2)}) collective-permute-start(bf16[128,1536]{1,0:T(8,128)(2,1)S(1)} %constant_dynamic-slice_fusion.refs_8_), channel_id=1, source_target_pairs={{0,1},{2,0},{4,2},{6,4},{7,6},{5,7},{3,5},{1,3},{8,9},{10,8},{12,1... | collective-permute-start | bytes 1179656 | tf_op jit(solution)/shard_map/ppermute | solution.py:38
  11.2 115.9 %collective-permute-start.14 = (bf16[128,1536]{1,0:T(8,128)(2,1)S(1)}, bf16[128,1536]{1,0:T(8,128)(2,1)}, u32[]{:S(2)}, u32[]{:S(2)}) collective-permute-start(bf16[128,1536]{1,0:T(8,128)(2,1)S(1)} %constant_dynamic-slice_fusion.refs_8_), channel_id=1, source_target_pairs={{0,16},{16,0},{1,17},{17,1},{2,18},{18,2},{3,19},{19,3},{4,20},{20... | collective-permute-start | bytes 1179656 | tf_op jit(solution)/shard_map/ppermute | solution.py:165
  13.2 125.1 %collective-permute-start.22 = (bf16[128,1536]{1,0:T(8,128)(2,1)S(1)}, bf16[128,1536]{1,0:T(8,128)(2,1)}, u32[]{:S(2)}, u32[]{:S(2)}) collective-permute-start(bf16[128,1536]{1,0:T(8,128)(2,1)S(1)} %constant_dynamic-slice_fusion.refs_8_), channel_id=1, source_target_pairs={{0,8},{8,0},{1,9},{9,1},{2,10},{10,2},{3,11},{11,3},{4,12},{12,4},... | collective-permute-start | bytes 1179656 | tf_op jit(solution)/shard_map/ppermute | solution.py:169
  13.2 363.3 %reduce-scatter.2.cloned.1.call-start = ((), (), s32[]{:S(2)}) async-start(), calls=%async_computation.4 | async-start | bytes 7077888 | tf_op jit(solution)/shard_map/reduce_scatter | solution.py:243
  26.5 111.8 %copy-start.4 = (bf16[128,1536]{1,0:T(8,128)(2,1)}, bf16[128,1536]{1,0:T(8,128)(2,1)S(1)}, u32[]{:S(2)}) copy-start(bf16[128,1536]{1,0:T(8,128)(2,1)S(1)} %collective-permute-done.7.refs_9_) | copy-start | bytes 1179652
  26.5 112.0 %collective-permute-start.8 = (bf16[128,1536]{1,0:T(8,128)(2,1)S(1)}, bf16[128,1536]{1,0:T(8,128)(2,1)}, u32[]{:S(2)}, u32[]{:S(2)}) collective-permute-start(bf16[128,1536]{1,0:T(8,128)(2,1)S(1)} %collective-permute-done.7.refs_9_), channel_id=1, source_target_pairs={{0,2},{2,4},{4,6},{6,7},{7,5},{5,3},{3,1},{1,0},{8,10},{10,12},{12... | collective-permute-start | bytes 1179656 | tf_op jit(solution)/shard_map/ppermute | solution.py:34
  28.0 111.0 %collective-permute-start.15 = (bf16[128,1536]{1,0:T(8,128)(2,1)S(1)}, bf16[128,1536]{1,0:T(8,128)(2,1)}, u32[]{:S(2)}, u32[]{:S(2)}) collective-permute-start(bf16[128,1536]{1,0:T(8,128)(2,1)S(1)} %collective-permute-done.7.refs_9_), channel_id=1, source_target_pairs={{0,16},{16,0},{1,17},{17,1},{2,18},{18,2},{3,19},{19,3},{4,20},{20... | collective-permute-start | bytes 1179656 | tf_op jit(solution)/shard_map/ppermute | solution.py:165
  28.6 109.9 %copy-start.5 = (bf16[128,1536]{1,0:T(8,128)(2,1)}, bf16[128,1536]{1,0:T(8,128)(2,1)S(1)}, u32[]{:S(2)}) copy-start(bf16[128,1536]{1,0:T(8,128)(2,1)S(1)} %collective-permute-done.11.refs_13_) | copy-start | bytes 1179652
  28.6 110.3 %collective-permute-start.12 = (bf16[128,1536]{1,0:T(8,128)(2,1)S(1)}, bf16[128,1536]{1,0:T(8,128)(2,1)}, u32[]{:S(2)}, u32[]{:S(2)}) collective-permute-start(bf16[128,1536]{1,0:T(8,128)(2,1)S(1)} %collective-permute-done.11.refs_13_), channel_id=1, source_target_pairs={{0,1},{2,0},{4,2},{6,4},{7,6},{5,7},{3,5},{1,3},{8,9},{10,8},{12,1... | collective-permute-start | bytes 1179656 | tf_op jit(solution)/shard_map/ppermute | solution.py:38
  127.1 12.5 %collective-permute-start.19 = (bf16[128,1536]{1,0:T(8,128)(2,1)S(1)}, bf16[128,1536]{1,0:T(8,128)(2,1)}, u32[]{:S(2)}, u32[]{:S(2)}) collective-permute-start(bf16[128,1536]{1,0:T(8,128)(2,1)S(1)} %collective-permute-done.11.refs_13_), channel_id=1, source_target_pairs={{0,16},{16,0},{1,17},{17,1},{2,18},{18,2},{3,19},{19,3},{4,20},{20... | collective-permute-start | bytes 1179656 | tf_op jit(solution)/shard_map/ppermute | solution.py:165
  138.3 4.1 %collective-permute-start.23 = (bf16[128,1536]{1,0:T(8,128)(2,1)S(1)}, bf16[128,1536]{1,0:T(8,128)(2,1)S(1)}, u32[]{:S(2)}, u32[]{:S(2)}) collective-permute-start(bf16[128,1536]{1,0:T(8,128)(2,1)S(1)} %collective-permute-done.7.refs_9_), channel_id=1, source_target_pairs={{0,8},{8,0},{1,9},{9,1},{2,10},{10,2},{3,11},{11,3},{4,12},{12,4},... | collective-permute-start | bytes 1179656 | tf_op jit(solution)/shard_map/ppermute | solution.py:169
  138.5 4.4 %collective-permute-start.27 = (bf16[128,1536]{1,0:T(8,128)(2,1)S(1)}, bf16[128,1536]{1,0:T(8,128)(2,1)}, u32[]{:S(2)}, u32[]{:S(2)}) collective-permute-start(bf16[128,1536]{1,0:T(8,128)(2,1)S(1)} %collective-permute-done.11.refs_13_), channel_id=1, source_target_pairs={{0,8},{8,0},{1,9},{9,1},{2,10},{10,2},{3,11},{11,3},{4,12},{12,4},... | collective-permute-start | bytes 1179656 | tf_op jit(solution)/shard_map/ppermute | solution.py:169
  138.8 5.7 %collective-permute-start.30 = (bf16[128,1536]{1,0:T(8,128)(2,1)}, bf16[128,1536]{1,0:T(8,128)(2,1)}, u32[]{:S(2)}, u32[]{:S(2)}) collective-permute-start(bf16[128,1536]{1,0:T(8,128)(2,1)} %collective-permute-done.14.refs_16_), channel_id=1, source_target_pairs={{0,8},{8,0},{1,9},{9,1},{2,10},{10,2},{3,11},{11,3},{4,12},{12,4},... | collective-permute-start | bytes 1179656 | tf_op jit(solution)/shard_map/ppermute | solution.py:170
  139.0 11.7 %collective-permute-start.9 = (bf16[128,1536]{1,0:T(8,128)(2,1)}, bf16[128,1536]{1,0:T(8,128)(2,1)}, u32[]{:S(2)}, u32[]{:S(2)}) collective-permute-start(bf16[128,1536]{1,0:T(8,128)(2,1)} %collective-permute-done.8.refs_10_), channel_id=1, source_target_pairs={{0,2},{2,4},{4,6},{6,7},{7,5},{5,3},{3,1},{1,0},{8,10},{10,12},{12... | collective-permute-start | bytes 1179656 | tf_op jit(solution)/shard_map/ppermute | solution.py:34
  139.6 11.4 %collective-permute-start.13 = (bf16[128,1536]{1,0:T(8,128)(2,1)}, bf16[128,1536]{1,0:T(8,128)(2,1)}, u32[]{:S(2)}, u32[]{:S(2)}) collective-permute-start(bf16[128,1536]{1,0:T(8,128)(2,1)} %collective-permute-done.12.refs_14_), channel_id=1, source_target_pairs={{0,1},{2,0},{4,2},{6,4},{7,6},{5,7},{3,5},{1,3},{8,9},{10,8},{12,1... | collective-permute-start | bytes 1179656 | tf_op jit(solution)/shard_map/ppermute | solution.py:38
  142.4 12.3 %collective-permute-start.16 = (bf16[128,1536]{1,0:T(8,128)(2,1)}, bf16[128,1536]{1,0:T(8,128)(2,1)S(1)}, u32[]{:S(2)}, u32[]{:S(2)}) collective-permute-start(bf16[128,1536]{1,0:T(8,128)(2,1)} %collective-permute-done.8.refs_10_), channel_id=1, source_target_pairs={{0,16},{16,0},{1,17},{17,1},{2,18},{18,2},{3,19},{19,3},{4,20},{20... | collective-permute-start | bytes 1179656 | tf_op jit(solution)/shard_map/ppermute | solution.py:165
  142.8 19.1 %collective-permute-start.20 = (bf16[128,1536]{1,0:T(8,128)(2,1)}, bf16[128,1536]{1,0:T(8,128)(2,1)S(1)}, u32[]{:S(2)}, u32[]{:S(2)}) collective-permute-start(bf16[128,1536]{1,0:T(8,128)(2,1)} %collective-permute-done.12.refs_14_), channel_id=1, source_target_pairs={{0,16},{16,0},{1,17},{17,1},{2,18},{18,2},{3,19},{19,3},{4,20},{20... | collective-permute-start | bytes 1179656 | tf_op jit(solution)/shard_map/ppermute | solution.py:165
  144.5 18.0 %collective-permute-start.24 = (bf16[128,1536]{1,0:T(8,128)(2,1)}, bf16[128,1536]{1,0:T(8,128)(2,1)S(1)}, u32[]{:S(2)}, u32[]{:S(2)}) collective-permute-start(bf16[128,1536]{1,0:T(8,128)(2,1)} %collective-permute-done.8.refs_10_), channel_id=1, source_target_pairs={{0,8},{8,0},{1,9},{9,1},{2,10},{10,2},{3,11},{11,3},{4,12},{12,4},... | collective-permute-start | bytes 1179656 | tf_op jit(solution)/shard_map/ppermute | solution.py:169
  150.7 12.4 %collective-permute-start.28 = (bf16[128,1536]{1,0:T(8,128)(2,1)}, bf16[128,1536]{1,0:T(8,128)(2,1)S(1)}, u32[]{:S(2)}, u32[]{:S(2)}) collective-permute-start(bf16[128,1536]{1,0:T(8,128)(2,1)} %collective-permute-done.12.refs_14_), channel_id=1, source_target_pairs={{0,8},{8,0},{1,9},{9,1},{2,10},{10,2},{3,11},{11,3},{4,12},{12,4},... | collective-permute-start | bytes 1179656 | tf_op jit(solution)/shard_map/ppermute | solution.py:169
  151.0 12.1 %collective-permute-start.31 = (bf16[128,1536]{1,0:T(8,128)(2,1)}, bf16[128,1536]{1,0:T(8,128)(2,1)S(1)}, u32[]{:S(2)}, u32[]{:S(2)}) collective-permute-start(bf16[128,1536]{1,0:T(8,128)(2,1)} %collective-permute-done.15.refs_17_), channel_id=1, source_target_pairs={{0,8},{8,0},{1,9},{9,1},{2,10},{10,2},{3,11},{11,3},{4,12},{12,4},... | collective-permute-start | bytes 1179656 | tf_op jit(solution)/shard_map/ppermute | solution.py:170
  152.8 28.8 %copy-start.23 = (bf16[8,128,1,128]{3,1,0,2:T(8,128)(2,1)S(1)}, bf16[8,128,1,128]{3,1,0,2:T(8,128)(2,1)}, u32[]{:S(2)}) copy-start(bf16[8,128,1,128]{3,1,0,2:T(8,128)(2,1)} %get-tuple-element.16) | copy-start | bytes 786436
  154.7 10.9 %collective-permute-start.35 = (bf16[128,1536]{1,0:T(8,128)(2,1)}, bf16[128,1536]{1,0:T(8,128)(2,1)S(1)}, u32[]{:S(2)}, u32[]{:S(2)}) collective-permute-start(bf16[128,1536]{1,0:T(8,128)(2,1)} %collective-permute-done.19.refs_21_), channel_id=1, source_target_pairs={{0,8},{8,0},{1,9},{9,1},{2,10},{10,2},{3,11},{11,3},{4,12},{12,4},... | collective-permute-start | bytes 1179656 | tf_op jit(solution)/shard_map/ppermute | solution.py:170
  162.0 10.2 %collective-permute-start.10 = (bf16[128,1536]{1,0:T(8,128)(2,1)}, bf16[128,1536]{1,0:T(8,128)(2,1)S(1)}, u32[]{:S(2)}, u32[]{:S(2)}) collective-permute-start(bf16[128,1536]{1,0:T(8,128)(2,1)} %collective-permute-done.9.refs_11_), channel_id=1, source_target_pairs={{0,2},{2,4},{4,6},{6,7},{7,5},{5,3},{3,1},{1,0},{8,10},{10,12},{12... | collective-permute-start | bytes 1179656 | tf_op jit(solution)/shard_map/ppermute | solution.py:34
  162.6 12.4 %collective-permute-start.17 = (bf16[128,1536]{1,0:T(8,128)(2,1)}, bf16[128,1536]{1,0:T(8,128)(2,1)}, u32[]{:S(2)}, u32[]{:S(2)}) collective-permute-start(bf16[128,1536]{1,0:T(8,128)(2,1)} %collective-permute-done.9.refs_11_), channel_id=1, source_target_pairs={{0,16},{16,0},{1,17},{17,1},{2,18},{18,2},{3,19},{19,3},{4,20},{20... | collective-permute-start | bytes 1179656 | tf_op jit(solution)/shard_map/ppermute | solution.py:165
  163.1 18.4 %collective-permute-start.25 = (bf16[128,1536]{1,0:T(8,128)(2,1)}, bf16[128,1536]{1,0:T(8,128)(2,1)S(1)}, u32[]{:S(2)}, u32[]{:S(2)}) collective-permute-start(bf16[128,1536]{1,0:T(8,128)(2,1)} %collective-permute-done.9.refs_11_), channel_id=1, source_target_pairs={{0,8},{8,0},{1,9},{9,1},{2,10},{10,2},{3,11},{11,3},{4,12},{12,4},... | collective-permute-start | bytes 1179656 | tf_op jit(solution)/shard_map/ppermute | solution.py:169
  163.2 17.8 %collective-permute-start.21 = (bf16[128,1536]{1,0:T(8,128)(2,1)}, bf16[128,1536]{1,0:T(8,128)(2,1)}, u32[]{:S(2)}, u32[]{:S(2)}) collective-permute-start(bf16[128,1536]{1,0:T(8,128)(2,1)} %collective-permute-done.13.refs_15_), channel_id=1, source_target_pairs={{0,16},{16,0},{1,17},{17,1},{2,18},{18,2},{3,19},{19,3},{4,20},{20... | collective-permute-start | bytes 1179656 | tf_op jit(solution)/shard_map/ppermute | solution.py:165
  165.6 41.8 %copy-start.12 = (bf16[128,1536]{1,0:T(8,128)(2,1)}, bf16[128,1536]{1,0:T(8,128)(2,1)S(1)}, u32[]{:S(2)}) copy-start(bf16[128,1536]{1,0:T(8,128)(2,1)S(1)} %collective-permute-done.35.refs_37_) | copy-start | bytes 1179652
  165.6 16.5 %collective-permute-start.29 = (bf16[128,1536]{1,0:T(8,128)(2,1)}, bf16[128,1536]{1,0:T(8,128)(2,1)S(1)}, u32[]{:S(2)}, u32[]{:S(2)}) collective-permute-start(bf16[128,1536]{1,0:T(8,128)(2,1)} %collective-permute-done.13.refs_15_), channel_id=1, source_target_pairs={{0,8},{8,0},{1,9},{9,1},{2,10},{10,2},{3,11},{11,3},{4,12},{12,4},... | collective-permute-start | bytes 1179656 | tf_op jit(solution)/shard_map/ppermute | solution.py:169
  172.1 35.3 %copy-start.13 = (bf16[128,1536]{1,0:T(8,128)(2,1)}, bf16[128,1536]{1,0:T(8,128)(2,1)S(1)}, u32[]{:S(2)}) copy-start(bf16[128,1536]{1,0:T(8,128)(2,1)S(1)} %collective-permute-done.10.refs_12_) | copy-start | bytes 1179652
  172.1 11.3 %collective-permute-start.32 = (bf16[128,1536]{1,0:T(8,128)(2,1)S(1)}, bf16[128,1536]{1,0:T(8,128)(2,1)S(1)}, u32[]{:S(2)}, u32[]{:S(2)}) collective-permute-start(bf16[128,1536]{1,0:T(8,128)(2,1)S(1)} %collective-permute-done.16.refs_18_), channel_id=1, source_target_pairs={{0,8},{8,0},{1,9},{9,1},{2,10},{10,2},{3,11},{11,3},{4,12},{12,4},... | collective-permute-start | bytes 1179656 | tf_op jit(solution)/shard_map/ppermute | solution.py:170
  174.9 8.7 %collective-permute-start.36 = (bf16[128,1536]{1,0:T(8,128)(2,1)S(1)}, bf16[128,1536]{1,0:T(8,128)(2,1)S(1)}, u32[]{:S(2)}, u32[]{:S(2)}) collective-permute-start(bf16[128,1536]{1,0:T(8,128)(2,1)S(1)} %collective-permute-done.20.refs_22_), channel_id=1, source_target_pairs={{0,8},{8,0},{1,9},{9,1},{2,10},{10,2},{3,11},{11,3},{4,12},{12,4},... | collective-permute-start | bytes 1179656 | tf_op jit(solution)/shard_map/ppermute | solution.py:170
  181.0 8.8 %collective-permute-start.18 = (bf16[128,1536]{1,0:T(8,128)(2,1)S(1)}, bf16[128,1536]{1,0:T(8,128)(2,1)}, u32[]{:S(2)}, u32[]{:S(2)}) collective-permute-start(bf16[128,1536]{1,0:T(8,128)(2,1)S(1)} %collective-permute-done.10.refs_12_), channel_id=1, source_target_pairs={{0,16},{16,0},{1,17},{17,1},{2,18},{18,2},{3,19},{19,3},{4,20},{20... | collective-permute-start | bytes 1179656 | tf_op jit(solution)/shard_map/ppermute | solution.py:165
  181.6 8.3 %collective-permute-start.26 = (bf16[128,1536]{1,0:T(8,128)(2,1)S(1)}, bf16[128,1536]{1,0:T(8,128)(2,1)S(1)}, u32[]{:S(2)}, u32[]{:S(2)}) collective-permute-start(bf16[128,1536]{1,0:T(8,128)(2,1)S(1)} %collective-permute-done.10.refs_12_), channel_id=1, source_target_pairs={{0,8},{8,0},{1,9},{9,1},{2,10},{10,2},{3,11},{11,3},{4,12},{12,4},... | collective-permute-start | bytes 1179656 | tf_op jit(solution)/shard_map/ppermute | solution.py:169
  182.1 9.2 %collective-permute-start = (bf16[512,128]{1,0:T(8,128)(2,1)S(1)}, bf16[512,128]{1,0:T(8,128)(2,1)S(1)}, u32[]{:S(2)}, u32[]{:S(2)}) collective-permute-start(bf16[512,128]{1,0:T(8,128)(2,1)S(1)} %bitcast.111), channel_id=1, source_target_pairs={{0,2},{2,4},{4,6},{6,7},{7,5},{5,3},{3,1},{1,0},{8,10},{10,12},{12... | collective-permute-start | bytes 393224 | tf_op jit(solution)/shard_map/ppermute | solution.py:34
  183.5 20.1 %collective-permute-start.33 = (bf16[128,1536]{1,0:T(8,128)(2,1)}, bf16[128,1536]{1,0:T(8,128)(2,1)S(1)}, u32[]{:S(2)}, u32[]{:S(2)}) collective-permute-start(bf16[128,1536]{1,0:T(8,128)(2,1)} %collective-permute-done.17.refs_19_), channel_id=1, source_target_pairs={{0,8},{8,0},{1,9},{9,1},{2,10},{10,2},{3,11},{11,3},{4,12},{12,4},... | collective-permute-start | bytes 1179656 | tf_op jit(solution)/shard_map/ppermute | solution.py:170
  183.7 19.9 %collective-permute-start.37 = (bf16[128,1536]{1,0:T(8,128)(2,1)}, bf16[128,1536]{1,0:T(8,128)(2,1)S(1)}, u32[]{:S(2)}, u32[]{:S(2)}) collective-permute-start(bf16[128,1536]{1,0:T(8,128)(2,1)} %collective-permute-done.21.refs_23_), channel_id=1, source_target_pairs={{0,8},{8,0},{1,9},{9,1},{2,10},{10,2},{3,11},{11,3},{4,12},{12,4},... | collective-permute-start | bytes 1179656 | tf_op jit(solution)/shard_map/ppermute | solution.py:170
  189.8 13.8 %collective-permute-start.34 = (bf16[128,1536]{1,0:T(8,128)(2,1)}, bf16[128,1536]{1,0:T(8,128)(2,1)S(1)}, u32[]{:S(2)}, u32[]{:S(2)}) collective-permute-start(bf16[128,1536]{1,0:T(8,128)(2,1)} %collective-permute-done.18.refs_20_), channel_id=1, source_target_pairs={{0,8},{8,0},{1,9},{9,1},{2,10},{10,2},{3,11},{11,3},{4,12},{12,4},... | collective-permute-start | bytes 1179656 | tf_op jit(solution)/shard_map/ppermute | solution.py:170
  189.8 5.9 %collective-permute-start.4 = (bf16[512,128]{1,0:T(8,128)(2,1)S(1)}, bf16[512,128]{1,0:T(8,128)(2,1)S(1)}, u32[]{:S(2)}, u32[]{:S(2)}) collective-permute-start(bf16[512,128]{1,0:T(8,128)(2,1)S(1)} %bitcast.112), channel_id=1, source_target_pairs={{0,1},{2,0},{4,2},{6,4},{7,6},{5,7},{3,5},{1,3},{8,9},{10,8},{12,1... | collective-permute-start | bytes 393224 | tf_op jit(solution)/shard_map/ppermute | solution.py:38
  191.3 5.9 %collective-permute-start.1 = (bf16[512,128]{1,0:T(8,128)(2,1)S(1)}, bf16[512,128]{1,0:T(8,128)(2,1)S(1)}, u32[]{:S(2)}, u32[]{:S(2)}) collective-permute-start(bf16[512,128]{1,0:T(8,128)(2,1)S(1)} %collective-permute-done.refs_1_), channel_id=1, source_target_pairs={{0,2},{2,4},{4,6},{6,7},{7,5},{5,3},{3,1},{1,0},{8,10},{10,12},{12... | collective-permute-start | bytes 393224 | tf_op jit(solution)/shard_map/ppermute | solution.py:34
  195.8 5.1 %collective-permute-start.5 = (bf16[512,128]{1,0:T(8,128)(2,1)S(1)}, bf16[512,128]{1,0:T(8,128)(2,1)S(1)}, u32[]{:S(2)}, u32[]{:S(2)}) collective-permute-start(bf16[512,128]{1,0:T(8,128)(2,1)S(1)} %collective-permute-done.4.refs_5_), channel_id=1, source_target_pairs={{0,1},{2,0},{4,2},{6,4},{7,6},{5,7},{3,5},{1,3},{8,9},{10,8},{12,1... | collective-permute-start | bytes 393224 | tf_op jit(solution)/shard_map/ppermute | solution.py:38
  197.2 5.1 %collective-permute-start.2 = (bf16[512,128]{1,0:T(8,128)(2,1)S(1)}, bf16[512,128]{1,0:T(8,128)(2,1)S(1)}, u32[]{:S(2)}, u32[]{:S(2)}) collective-permute-start(bf16[512,128]{1,0:T(8,128)(2,1)S(1)} %collective-permute-done.1.refs_2_), channel_id=1, source_target_pairs={{0,2},{2,4},{4,6},{6,7},{7,5},{5,3},{3,1},{1,0},{8,10},{10,12},{12... | collective-permute-start | bytes 393224 | tf_op jit(solution)/shard_map/ppermute | solution.py:34
  200.9 5.0 %collective-permute-start.6 = (bf16[512,128]{1,0:T(8,128)(2,1)S(1)}, bf16[512,128]{1,0:T(8,128)(2,1)S(1)}, u32[]{:S(2)}, u32[]{:S(2)}) collective-permute-start(bf16[512,128]{1,0:T(8,128)(2,1)S(1)} %collective-permute-done.5.refs_6_), channel_id=1, source_target_pairs={{0,1},{2,0},{4,2},{6,4},{7,6},{5,7},{3,5},{1,3},{8,9},{10,8},{12,1... | collective-permute-start | bytes 393224 | tf_op jit(solution)/shard_map/ppermute | solution.py:38
  202.3 5.1 %collective-permute-start.3 = (bf16[512,128]{1,0:T(8,128)(2,1)S(1)}, bf16[512,128]{1,0:T(8,128)(2,1)}, u32[]{:S(2)}, u32[]{:S(2)}) collective-permute-start(bf16[512,128]{1,0:T(8,128)(2,1)S(1)} %collective-permute-done.2.refs_3_), channel_id=1, source_target_pairs={{0,2},{2,4},{4,6},{6,7},{7,5},{5,3},{3,1},{1,0},{8,10},{10,12},{12... | collective-permute-start | bytes 393224 | tf_op jit(solution)/shard_map/ppermute | solution.py:34
  261.0 118.2 %copy-start.1 = (bf16[128,6144]{1,0:T(8,128)(2,1)S(1)}, bf16[128,6144]{1,0:T(8,128)(2,1)}, u32[]{:S(2)}) copy-start(bf16[128,6144]{1,0:T(8,128)(2,1)} %param.19) | copy-start | bytes 4718596
  (30 other events, 313.6 us)
Sparse Core Ops, SparseCore 0:
  9.6 110.1 all-gather.3
  121.3 13.8 all-gather.5
  136.8 20.0 all-gather.7
  261.1 115.2 reduce-scatter.1

commit v4 on v3

--- a/solution.py
+++ b/solution.py
@@ -40,52 +40,61 @@
     return blocks
 
 
-def out_proj_kernel(group_count, set_count, tiles_per_set, place_ref, *refs):
+def direct_gather(block, axis_name, count):
+    cycle = snake_cycle(count)
+    shifts = list(range(1, count // 2 + 1)) + [-k for k in range(1, (count - 1) // 2 + 1)]
+    blocks = [block]
+    for shift in shifts:
+        pairs = [(cycle[(p - shift) % count], cycle[p]) for p in range(count)]
+        blocks.append(lax.ppermute(block, axis_name, pairs))
+    return blocks
+
+
+def out_proj_kernel(group_count, set_count, tiles_per_set, table_ref, *refs):
     att_refs = refs[:group_count]
     out_ref = refs[-1]
     tile = pl.program_id(0)
 
-    def accumulate(w_refs):
+    def accumulate(w_ref):
         total = None
         for group in range(group_count):
-            term = jnp.dot(att_refs[group][...], w_refs[group][...], preferred_element_type=jnp.float32)
+            term = jnp.dot(att_refs[group][...], w_ref[group], preferred_element_type=jnp.float32)
             term = term.astype(jnp.bfloat16).astype(jnp.float32)
             total = term if total is None else total + term
         out_ref[...] = total
 
     for which in range(set_count):
-        w_refs = refs[group_count * (which + 1):group_count * (which + 2)]
+        w_ref = refs[group_count + which]
 
         @pl.when(tile // tiles_per_set == which)
         def _():
-            accumulate(w_refs)
-
-
-def grouped_out_proj(placement, att_blocks, weight_sets, tile_width=512):
-    group_count = len(att_blocks)
+            accumulate(w_ref)
+
+
+def grouped_out_proj(table, att_all, weight_sets, tile_width=512):
     set_count = len(weight_sets)
-    token_count, head_width = att_blocks[0].shape
-    set_width = weight_sets[0][0].shape[1]
+    group_count, head_width, set_width = weight_sets[0].shape
+    token_count = att_all.shape[0]
     tile_width = min(tile_width, set_width)
     tiles_per_set = set_width // tile_width
-    att_spec = pl.BlockSpec((token_count, head_width), lambda n, p: (0, 0))
+
+    def att_spec(group):
+        return pl.BlockSpec((token_count, head_width), lambda n, p: (0, p[set_count + group]))
 
     def weight_spec(which):
         return pl.BlockSpec(
-            (head_width, tile_width),
-            lambda n, p: (0, jnp.clip(n - which * tiles_per_set, 0, tiles_per_set - 1)),
+            (group_count, head_width, tile_width),
+            lambda n, p: (0, 0, jnp.clip(n - which * tiles_per_set, 0, tiles_per_set - 1)),
         )
 
     out_spec = pl.BlockSpec(
         (token_count, tile_width),
         lambda n, p: (0, p[n // tiles_per_set] * tiles_per_set + n % tiles_per_set),
     )
-    in_specs = [att_spec] * group_count
-    for which in range(set_count):
-        in_specs += [weight_spec(which)] * group_count
+    in_specs = [att_spec(g) for g in range(group_count)] + [weight_spec(k) for k in range(set_count)]
     width = set_count * set_width
     flops = 2 * token_count * head_width * group_count * width
-    moved = 2 * group_count * token_count * head_width + 2 * group_count * head_width * width
+    moved = 2 * token_count * head_width * group_count + 2 * group_count * head_width * width
     return pl.pallas_call(
         functools.partial(out_proj_kernel, group_count, set_count, tiles_per_set),
         out_shape=jax.ShapeDtypeStruct((token_count, width), jnp.float32),
@@ -98,7 +107,7 @@
         cost_estimate=pl.CostEstimate(
             flops=flops, bytes_accessed=moved + token_count * width * 4, transcendentals=0
         ),
-    )(placement, *att_blocks, *[b for blocks in weight_sets for b in blocks])
+    )(table, *([att_all] * group_count), *weight_sets)
 
 
 def select_row(source, target):
@@ -160,22 +169,24 @@
         column_part = model_width // (rep_count * span_count)
         slot = rep_index * span_count + span_index
         w_out_part = lax.dynamic_slice_in_dim(w_out, slot * column_part, column_part, 1)
-        mine_blocks = ring_gather(w_out_part, "tp", tp_count)
+        mine = jnp.stack(ring_gather(w_out_part, "tp", tp_count))
         swap = [(0, 1), (1, 0)]
-        rep_blocks = [lax.ppermute(b, "rep", swap) for b in mine_blocks]
-        weight_sets = [
-            mine_blocks,
-            rep_blocks,
-            [lax.ppermute(b, "span", swap) for b in mine_blocks],
-            [lax.ppermute(b, "span", swap) for b in rep_blocks],
+        from_rep = lax.ppermute(mine, "rep", swap)
+        from_span = lax.ppermute(jnp.stack([mine, from_rep]), "span", swap)
+        weight_sets = [mine, from_rep, from_span[0], from_span[1]]
+        slots = [
+            ((rep_index + dr) % 2) * span_count + (span_index + ds) % 2
+            for ds in (0, 1)
+            for dr in (0, 1)
         ]
-        placement = jnp.stack(
-            [
-                ((rep_index + dr) % 2) * span_count + (span_index + ds) % 2
-                for ds in (0, 1)
-                for dr in (0, 1)
-            ]
-        ).astype(jnp.int32)
+        cycle = snake_cycle(tp_count)
+        position = [cycle.index(t) for t in range(tp_count)]
+        steps = list(range(tp_count // 2 + 1)) + [-k for k in range(1, (tp_count - 1) // 2 + 1)]
+        owners = jnp.array(
+            [[cycle[(position[t] - k) % tp_count] for k in steps] for t in range(tp_count)],
+            jnp.int32,
+        )[tp_rank]
+        table = jnp.concatenate([jnp.stack(slots).astype(jnp.int32), owners])
     up_full, down_full = (
         lax.all_gather(w_up, "span", axis=1, tiled=True),
         lax.all_gather(w_down, "span", axis=0, tiled=True),
@@ -215,8 +226,8 @@
         lambda q_rows, c_seen, f_seen: attend(q_rows, cache_all, fresh_all, c_seen, f_seen)
     )(queries, cache_seen, fresh_seen)
     if gather_weights:
-        att_blocks = ring_gather(attended.reshape(token_count, per_device), "tp", tp_count)
-        attn_out = grouped_out_proj(placement, att_blocks, weight_sets)
+        att_all = lax.all_gather(attended.reshape(token_count, per_device), "tp", axis=1, tiled=True)
+        attn_out = grouped_out_proj(table, att_all, weight_sets)
         attn_out = attn_out.reshape(local_count, row_count, model_width)
         residual_full = gathered + mod_rows[:, 2][:, None] * attn_out
         mlp_in = (

time: 386 us -> 438 us (1.13)
  local copies, waits for them, and re-layouts: 10.4 us -> 35.7 us
  waiting for transfers between devices: 255 us -> 276 us
  other arithmetic: 25.7 us -> 32.2 us
    all_gather x1, waiting for transfers between devices: 91.2 us -> 34.2 us  [local(): lax.all_gather(hidden_in, 'tp', axis=2, tiled=True).astype(jnp.float32)]
    ppermute x24 -> x2, waiting for transfers between devices: 23.9 us -> 77.8 us  [the longest x1 68.7 us: local(): from_rep = lax.ppermute(mine, 'rep', swap)]
    ppermute x8 -> x4, waiting for transfers between devices: 13.5 us -> 44.2 us  [ring_gather(): forward = lax.ppermute(forward, axis_name, ahead)]
    ppermute x8 -> x4, starting transfers between devices: 9.11 us -> 19.9 us  [ring_gather(): forward = lax.ppermute(forward, axis_name, ahead)]
    ppermute x6 -> x3, waiting for transfers between devices: 9.41 us -> 0.6 us  [ring_gather(): backward = lax.ppermute(backward, axis_name, behind)]
    ppermute x24 -> x2, starting transfers between devices: 10.3 us -> 1.54 us  [the longest x1 1.54 us: local(): from_rep = lax.ppermute(mine, 'rep', swap)]
    squeeze x0 -> x2, local copies, waits for them, and re-layouts: none -> 7.57 us  [the longest x1 6.87 us: local(): weight_sets = [mine, from_rep, from_span[0], from_span[1]]]
    unnamed x79 -> x36, local copies, waits for them, and re-layouts: 7.55 us -> 15.1 us
  transfers between devices with their start and end apart: 42 -> 14, of which waited for: 14 -> 8; matrix products, arithmetic and copies ran while one was open for 14% -> 20% of each run, Pallas kernels for 6% -> 5%
where the time goes in v4:
time: 438 us; the launch traced here: 437 us
  waiting for transfers between devices  276 us (63%)
  local copies, waits for them, and re-layouts  35.7 us (8%)
  other arithmetic  32.2 us (7%)
  matrix products  30.5 us (7%)
  starting transfers between devices  22.9 us (5%)
  Pallas kernels  21.4 us (5%)
  between operations  14.1 us (3%)
  blocking collectives  4.54 us (1%)
    reduce_scatter x1, waiting for transfers between devices, local(): lax.psum_scatter(down_terms.astype(jnp.bfloat16), 'tp', scatter_dimension...  118 us
    ppermute x1, waiting for transfers between devices, local(): from_rep = lax.ppermute(mine, 'rep', swap)  68.7 us
    ppermute x4, waiting for transfers between devices, ring_gather(): forward = lax.ppermute(forward, axis_name, ahead)  44.2 us
    all_gather x1, waiting for transfers between devices, local(): lax.all_gather(hidden_in, 'tp', axis=2, tiled=True).astype(jnp.float32)  34.2 us
    pallas_call x1, Pallas kernels, grouped_out_proj(): pl.pallas_call(functools.partial(out_proj_kernel, group_count, set_count,...  21.4 us
    ppermute x4, starting transfers between devices, ring_gather(): forward = lax.ppermute(forward, axis_name, ahead)  19.9 us
    reduce_sum x2, other arithmetic, normalize(): jnp.mean(values * values, axis=-1, keepdims=True) + EPSILON  17.6 us
    unnamed x36, local copies, waits for them, and re-layouts  15.1 us
  transfers between devices with their start and end apart: 14, of which 8 were waited for; matrix products, arithmetic and copies ran while one was open for 20% of the time, Pallas kernels for 5%

profile of v4, /device:TPU:0, one launch (start us, length us, event | category | flops | bytes accessed | tf_op | source)
XLA Modules:
  0.0 437.0 jit_solution(5177755955750531074)
XLA Ops:
  7.3 1.8 bitcast_dynamic-update-slice_fusion.7
  9.1 3.0 collective-permute-start
  12.8 0.8 select_reduce_fusion.1
  13.7 0.8 select_reduce_fusion
  15.3 1.0 fusion.31
  16.4 0.8 copy-done.4
  18.0 6.7 %copy.27 = bf16[6144,3,128]{0,2,1:T(8,128)(2,1)} copy(bf16[6144,3,128]{2,0,1:T(8,128)(2,1)} %param.19) | data formatting | bytes 9437184 | tf_op args[7]
  24.8 1.0 copy.30
  25.8 2.2 all_gather.19
  27.9 0.8 fusion.41
  28.8 2.0 collective-permute-start.1
  30.8 1.0 bitcast_dynamic-update-slice_fusion.6
  31.9 16.9 %collective-permute-done.1 = bf16[128,1536]{1,0:T(8,128)(2,1)S(1)} collective-permute-done((bf16[128,1536]{1,0:T(8,128)(2,1)}, bf16[128,1536]{1,0:T(8,128)(2,1)S(1)}, u32[]{:S(2)}, u32[]{:S(2)}) %collective-permute-start.1) | collective-permute-done | bytes 393248 | tf_op jit(solution)/shard_map/ppermute | solution.py:34
  48.8 8.1 %collective-permute-start.2 = (bf16[128,1536]{1,0:T(8,128)(2,1)S(1)}, bf16[128,1536]{1,0:T(8,128)(2,1)S(1)}, u32[]{:S(2)}, u32[]{:S(2)}) collective-permute-start(bf16[128,1536]{1,0:T(8,128)(2,1)S(1)} %collective-permute-done.1), channel_id=1, source_target_pairs={{0,2},{2,4},{4,6},{6,7},{7,5},{5,3},{3,1},{1,0},{8,10},{10,12},{12... | collective-permute-start | bytes 1179656 | tf_op jit(solution)/shard_map/ppermute | solution.py:34
  57.4 1.2 collective-permute-start.6
  58.7 11.9 %collective-permute-done.2 = bf16[128,1536]{1,0:T(8,128)(2,1)S(1)} collective-permute-done((bf16[128,1536]{1,0:T(8,128)(2,1)S(1)}, bf16[128,1536]{1,0:T(8,128)(2,1)S(1)}, u32[]{:S(2)}, u32[]{:S(2)}) %collective-permute-start.2) | collective-permute-done | bytes 393248 | tf_op jit(solution)/shard_map/ppermute | solution.py:34
  70.6 6.8 %collective-permute-start.3 = (bf16[128,1536]{1,0:T(8,128)(2,1)S(1)}, bf16[128,1536]{1,0:T(8,128)(2,1)S(1)}, u32[]{:S(2)}, u32[]{:S(2)}) collective-permute-start(bf16[128,1536]{1,0:T(8,128)(2,1)S(1)} %collective-permute-done.2), channel_id=1, source_target_pairs={{0,2},{2,4},{4,6},{6,7},{7,5},{5,3},{3,1},{1,0},{8,10},{10,12},{12... | collective-permute-start | bytes 1179656 | tf_op jit(solution)/shard_map/ppermute | solution.py:34
  77.5 15.4 %collective-permute-done.3 = bf16[128,1536]{1,0:T(8,128)(2,1)S(1)} collective-permute-done((bf16[128,1536]{1,0:T(8,128)(2,1)S(1)}, bf16[128,1536]{1,0:T(8,128)(2,1)S(1)}, u32[]{:S(2)}, u32[]{:S(2)}) %collective-permute-start.3) | collective-permute-done | bytes 393248 | tf_op jit(solution)/shard_map/ppermute | solution.py:34
  92.9 1.0 bitcast_dynamic-update-slice_fusion.2
  93.9 34.2 %all-gather.5.cloned.1.call-done = bf16[4,128,6144]{2,1,0:T(8,128)(2,1)} async-done(((bf16[4,128,768]{2,1,0:T(8,128)(2,1)}), bf16[4,128,6144]{2,1,0:T(8,128)(2,1)}) %all-gather.5.cloned.1.call-update) | async-done | bytes 6291472 | tf_op jit(solution)/shard_map/all_gather | solution.py:162
  128.1 4.2 fusion
  132.7 2.7 fusion.3
  135.4 6.6 %convolution_convert_fusion.1 = bf16[512,384]{1,0:T(8,128)(2,1)} fusion(bf16[512,6144]{1,0:T(8,128)(2,1)S(1)} %bitcast.130, bf16[6144,384]{0,1:T(8,128)(2,1)} %bitcast.131), kind=kOutput, calls=%fused_computation.31 | convolution fusion | flops 2416115712 | bytes 11403264 | tf_op jit(solution)/shard_map/dot_general | solution.py:205
  142.0 1.9 copy.28
  143.9 1.8 reshape.201
  145.7 1.7 slice.69
  147.4 1.6 slice.67
  149.1 1.1 copy.31
  150.2 2.4 all_gather.20
  152.6 0.8 fusion.42
  153.4 1.0 copy.34
  154.4 1.4 fusion.33
  155.8 1.8 fusion.12
  158.3 0.9 divide_convert_fusion
  159.7 1.1 fusion.17
  160.9 1.0 bitcast_dynamic-update-slice_fusion.1
  161.9 1.0 bitcast_dynamic-update-slice_fusion.refs_8_
  163.0 1.5 collective-permute-start.7
  164.6 68.7 %collective-permute-done.7.refs_9_ = bf16[8,128,1536]{2,1,0:T(8,128)(2,1)} collective-permute-done((bf16[8,128,1536]{2,1,0:T(8,128)(2,1)S(1)}, bf16[8,128,1536]{2,1,0:T(8,128)(2,1)}, u32[]{:S(2)}, u32[]{:S(2)}) %collective-permute-start.7) | collective-permute-done | bytes 3145760 | tf_op jit(solution)/shard_map/ppermute | solution.py:174
  233.3 5.1 %pad_maximum_fusion = bf16[2,8,128,1536]{3,2,1,0:T(8,128)(2,1)} fusion(bf16[1,8,128,1536]{3,2,1,0:T(8,128)(2,1)} %bitcast.41, bf16[1,8,128,1536]{3,2,1,0:T(8,128)(2,1)S(1)} %bitcast.129), kind=kLoop, calls=%fused_computation.11 | loop fusion | flops 3145728 | bytes 12582912 | tf_op jit(solution)/shard_map/stack | solution.py:175
  239.8 9.1 %collective-permute-done.8 = bf16[2,8,128,1536]{3,2,1,0:T(8,128)(2,1)} collective-permute-done((bf16[2,8,128,1536]{3,2,1,0:T(8,128)(2,1)}, bf16[2,8,128,1536]{3,2,1,0:T(8,128)(2,1)}, u32[]{:S(2)}, u32[]{:S(2)}) %collective-permute-start.8) | collective-permute-done | bytes 6291488 | tf_op jit(solution)/shard_map/ppermute | solution.py:175
  248.9 6.9 %slice_bitcast_fusion = (bf16[8,128,1536]{2,1,0:T(8,128)(2,1)}, bf16[8,128,1536]{2,1,0:T(8,128)(2,1)}) fusion(bf16[2,8,128,1536]{3,2,1,0:T(8,128)(2,1)} %collective-permute-done.8), kind=kLoop, calls=%fused_computation.20 | loop fusion | bytes 12582912 | tf_op jit(solution)/shard_map/squeeze | solution.py:176
  255.7 21.4 %shard_map.118 = f32[512,6144]{1,0:T(8,128)} custom-call(s32[12]{0:T(128)} %concatenate.22.table_ref, bf16[512,1024]{1,0:T(8,128)(2,1)} %all-gather.7.cloned.1.call-done.refs_0_.refs_1_.refs_2_.refs_3_.refs_4_.refs_5_.refs_6_.refs_7_, bf16[512,1024]{1,0:T(8,128)(2,1)} %all-gather.7.cloned.1.call-done.refs_0_.refs_1_.refs_2_.refs_3_.refs_4_.refs_5_.refs_6_.refs_7_, ...), custom_call_target="tpu_custom_call" | custom-call | flops 6442450944 | bytes 26214400 | tf_op jit(solution)/shard_map/pallas_call | solution.py:98
  277.1 13.4 %multiply_reduce_fusion = (f32[4,128]{1,0:T(4,128)S(1)}, f32[4,128,6144]{2,1,0:T(8,128)}) fusion(f32[4,128,6144]{2,1,0:T(8,128)} %bitcast.128, f32[4,6144]{1,0:T(4,128)S(1)} %get-tuple-element.19, bf16[4,128,6144]{2,1,0:T(8,128)(2,1)} %all-gather.5.cloned.1.call-done), kind=kLoop, calls=%fused_computation.8 | loop fusion | flops 15728128 | bytes 31557632 | tf_op jit(solution)/shard_map/reduce_sum | solution.py:20
  290.6 10.2 %fusion.27 = bf16[4,128,512]{2,1,0:T(8,128)(2,1)S(1)} fusion(bf16[6144,512]{1,0:T(8,128)(2,1)} %all-gather.9.cloned.1.call-done, f32[4,128,6144]{2,1,0:T(8,128)} %get-tuple-element.6, f32[4,6144]{1,0:T(4,128)S(1)} %copy-done.10, f32[4,6144]{1,0:T(4,128)S(1)} %copy-done.9, f32[4,128]{1,0:T(4,128)S(1)} %add_rsqrt_fusion), kind=kOutput, calls=%fused_computation.42 | convolution fusion | flops 3236167680 | bytes 19597312 | tf_op jit(solution)/shard_map/dot_general | solution.py:251
  300.8 8.1 %convolution_convert_fusion = bf16[4,128,6144]{2,1,0:T(8,128)(2,1)} fusion(bf16[4,128,512]{2,1,0:T(8,128)(2,1)S(1)} %fusion.27, bf16[512,6144]{1,0:T(8,128)(2,1)} %all-gather.11.cloned.1.call-done), kind=kOutput, calls=%fused_computation.9 | convolution fusion | flops 3224371200 | bytes 13107200 | tf_op jit(solution)/shard_map/dot_general | solution.py:253
  309.6 118.1 %reduce-scatter.2.cloned.1.call-done = bf16[4,128,768]{2,1,0:T(8,128)(2,1)} async-done(((bf16[4,128,6144]{2,1,0:T(8,128)(2,1)}), bf16[4,128,768]{2,1,0:T(8,128)(2,1)}) %reduce-scatter.2.cloned.1.call-update) | async-done | bytes 786448 | tf_op jit(solution)/shard_map/reduce_scatter | solution.py:254
  427.7 2.7 add_convert_fusion.2
  (62 shorter events, 7.0 us)
Async XLA Ops:
  6.5 8.8 %copy-start = (bf16[4,6,6144]{2,0,1:T(4,128)(2,1)S(1)}, bf16[4,6,6144]{2,0,1:T(4,128)(2,1)}, u32[]{:S(2)}) copy-start(bf16[4,6,6144]{2,0,1:T(4,128)(2,1)} %param.18) | copy-start | bytes 884740
  6.5 121.5 %all-gather.5.cloned.1.call-start = ((), (), s32[]{:S(2)}) async-start(), calls=%async_computation.1 | async-start | bytes 7077888 | tf_op jit(solution)/shard_map/all_gather | solution.py:162
  7.3 248.5 %all-gather.7.cloned.1.call-start = ((), (), s32[]{:S(2)}) async-start(), calls=%async_computation.2 | async-start | bytes 1179648 | tf_op jit(solution)/shard_map/all_gather | solution.py:229
  9.1 19.7 %collective-permute-start = (bf16[128,1536]{1,0:T(8,128)(2,1)}, bf16[128,1536]{1,0:T(8,128)(2,1)}, u32[]{:S(2)}, u32[]{:S(2)}) collective-permute-start(bf16[128,1536]{1,0:T(8,128)(2,1)} %get-tuple-element.8), channel_id=1, source_target_pairs={{0,2},{2,4},{4,6},{6,7},{7,5},{5,3},{3,1},{1,0},{8,10},{10,12},{12... | collective-permute-start | bytes 1179656 | tf_op jit(solution)/shard_map/ppermute | solution.py:34
  12.1 18.7 %collective-permute-start.4 = (bf16[128,1536]{1,0:T(8,128)(2,1)}, bf16[128,1536]{1,0:T(8,128)(2,1)}, u32[]{:S(2)}, u32[]{:S(2)}) collective-permute-start(bf16[128,1536]{1,0:T(8,128)(2,1)} %get-tuple-element.8), channel_id=1, source_target_pairs={{0,1},{2,0},{4,2},{6,4},{7,6},{5,7},{3,5},{1,3},{8,9},{10,8},{12,1... | collective-permute-start | bytes 1179656 | tf_op jit(solution)/shard_map/ppermute | solution.py:38
  16.4 0.8 copy-start.4
  28.8 20.0 %collective-permute-start.1 = (bf16[128,1536]{1,0:T(8,128)(2,1)}, bf16[128,1536]{1,0:T(8,128)(2,1)S(1)}, u32[]{:S(2)}, u32[]{:S(2)}) collective-permute-start(bf16[128,1536]{1,0:T(8,128)(2,1)} %collective-permute-done), channel_id=1, source_target_pairs={{0,2},{2,4},{4,6},{6,7},{7,5},{5,3},{3,1},{1,0},{8,10},{10,12},{12... | collective-permute-start | bytes 1179656 | tf_op jit(solution)/shard_map/ppermute | solution.py:34
  30.8 26.6 %collective-permute-start.5 = (bf16[128,1536]{1,0:T(8,128)(2,1)}, bf16[128,1536]{1,0:T(8,128)(2,1)}, u32[]{:S(2)}, u32[]{:S(2)}) collective-permute-start(bf16[128,1536]{1,0:T(8,128)(2,1)} %collective-permute-done.4), channel_id=1, source_target_pairs={{0,1},{2,0},{4,2},{6,4},{7,6},{5,7},{3,5},{1,3},{8,9},{10,8},{12,1... | collective-permute-start | bytes 1179656 | tf_op jit(solution)/shard_map/ppermute | solution.py:38
  48.8 21.9 %collective-permute-start.2 = (bf16[128,1536]{1,0:T(8,128)(2,1)S(1)}, bf16[128,1536]{1,0:T(8,128)(2,1)S(1)}, u32[]{:S(2)}, u32[]{:S(2)}) collective-permute-start(bf16[128,1536]{1,0:T(8,128)(2,1)S(1)} %collective-permute-done.1), channel_id=1, source_target_pairs={{0,2},{2,4},{4,6},{6,7},{7,5},{5,3},{3,1},{1,0},{8,10},{10,12},{12... | collective-permute-start | bytes 1179656 | tf_op jit(solution)/shard_map/ppermute | solution.py:34
  57.4 104.5 %collective-permute-start.6 = (bf16[128,1536]{1,0:T(8,128)(2,1)}, bf16[128,1536]{1,0:T(8,128)(2,1)}, u32[]{:S(2)}, u32[]{:S(2)}) collective-permute-start(bf16[128,1536]{1,0:T(8,128)(2,1)} %collective-permute-done.5), channel_id=1, source_target_pairs={{0,1},{2,0},{4,2},{6,4},{7,6},{5,7},{3,5},{1,3},{8,9},{10,8},{12,1... | collective-permute-start | bytes 1179656 | tf_op jit(solution)/shard_map/ppermute | solution.py:38
  58.7 73.7 %copy-start.5 = (f32[4,6144]{1,0:T(4,128)S(1)}, f32[4,6144]{1,0:T(4,128)}, u32[]{:S(2)}) copy-start(f32[4,6144]{1,0:T(4,128)} %get-tuple-element.17) | copy-start | bytes 294916
  58.7 73.7 %copy-start.6 = (f32[4,6144]{1,0:T(4,128)S(1)}, f32[4,6144]{1,0:T(4,128)}, u32[]{:S(2)}) copy-start(f32[4,6144]{1,0:T(4,128)} %get-tuple-element.18) | copy-start | bytes 294916
  70.6 22.2 %collective-permute-start.3 = (bf16[128,1536]{1,0:T(8,128)(2,1)S(1)}, bf16[128,1536]{1,0:T(8,128)(2,1)S(1)}, u32[]{:S(2)}, u32[]{:S(2)}) collective-permute-start(bf16[128,1536]{1,0:T(8,128)(2,1)S(1)} %collective-permute-done.2), channel_id=1, source_target_pairs={{0,2},{2,4},{4,6},{6,7},{7,5},{5,3},{3,1},{1,0},{8,10},{10,12},{12... | collective-permute-start | bytes 1179656 | tf_op jit(solution)/shard_map/ppermute | solution.py:34
  128.1 4.6 %copy-start.2 = (bf16[4,128,6144]{2,1,0:T(8,128)(2,1)S(1)}, bf16[4,128,6144]{2,1,0:T(8,128)(2,1)}, u32[]{:S(2)}) copy-start(bf16[4,128,6144]{2,1,0:T(8,128)(2,1)} %all-gather.5.cloned.1.call-done) | copy-start | bytes 18874372
  158.3 1.0 copy-start.8
  158.3 1.4 copy-start.7
  160.8 129.7 %all-gather.9.cloned.1.call-start = ((), (), s32[]{:S(2)}) async-start(), calls=%async_computation.3 | async-start | bytes 9437184 | tf_op jit(solution)/shard_map/all_gather | solution.py:191
  163.0 75.4 %copy-start.3 = (bf16[8,128,1536]{2,1,0:T(8,128)(2,1)}, bf16[8,128,1536]{2,1,0:T(8,128)(2,1)S(1)}, u32[]{:S(2)}) copy-start(bf16[8,128,1536]{2,1,0:T(8,128)(2,1)S(1)} %bitcast_dynamic-update-slice_fusion.refs_8_) | copy-start | bytes 9437188
  163.0 70.3 %collective-permute-start.7 = (bf16[8,128,1536]{2,1,0:T(8,128)(2,1)S(1)}, bf16[8,128,1536]{2,1,0:T(8,128)(2,1)}, u32[]{:S(2)}, u32[]{:S(2)}) collective-permute-start(bf16[8,128,1536]{2,1,0:T(8,128)(2,1)S(1)} %bitcast_dynamic-update-slice_fusion.refs_8_), channel_id=1, source_target_pairs={{0,16},{16,0},{1,17},{17,1},{2,18},{18,2},{3,19},{19,3},{4,20},{20... | collective-permute-start | bytes 9437192 | tf_op jit(solution)/shard_map/ppermute | solution.py:174
  164.5 136.3 %all-gather.11.cloned.1.call-start = ((), (), s32[]{:S(2)}) async-start(), calls=%async_computation.4 | async-start | bytes 9437184 | tf_op jit(solution)/shard_map/all_gather | solution.py:192
  238.4 10.5 %collective-permute-start.8 = (bf16[2,8,128,1536]{3,2,1,0:T(8,128)(2,1)}, bf16[2,8,128,1536]{3,2,1,0:T(8,128)(2,1)}, u32[]{:S(2)}, u32[]{:S(2)}) collective-permute-start(bf16[2,8,128,1536]{3,2,1,0:T(8,128)(2,1)} %pad_maximum_fusion), channel_id=1, source_target_pairs={{0,8},{8,0},{1,9},{9,1},{2,10},{10,2},{3,11},{11,3},{4,12},{12,4},... | collective-permute-start | bytes 18874376 | tf_op jit(solution)/shard_map/ppermute | solution.py:175
  238.4 189.3 %reduce-scatter.2.cloned.1.call-start = ((), (), s32[]{:S(2)}) async-start(), calls=%async_computation.5 | async-start | bytes 7077888 | tf_op jit(solution)/shard_map/reduce_scatter | solution.py:254
  277.1 13.4 %copy-start.9 = (f32[4,6144]{1,0:T(4,128)S(1)}, f32[4,6144]{1,0:T(4,128)}, u32[]{:S(2)}) copy-start(f32[4,6144]{1,0:T(4,128)} %get-tuple-element.15) | copy-start | bytes 294916
  277.1 13.5 %copy-start.10 = (f32[4,6144]{1,0:T(4,128)S(1)}, f32[4,6144]{1,0:T(4,128)}, u32[]{:S(2)}) copy-start(f32[4,6144]{1,0:T(4,128)} %get-tuple-element.16) | copy-start | bytes 294916
  308.9 121.6 %copy-start.1 = (bf16[4,6,6144]{2,0,1:T(4,128)(2,1)S(1)}, bf16[4,6,6144]{2,0,1:T(4,128)(2,1)}, u32[]{:S(2)}) copy-start(bf16[4,6,6144]{2,0,1:T(4,128)(2,1)} %param.18) | copy-start | bytes 884740
Sparse Core Ops, SparseCore 0:
  9.6 118.4 all-gather.4
  161.0 40.1 all-gather.6
  202.7 14.5 all-gather.8
  238.5 17.5 all-gather.10
  309.0 118.6 reduce-scatter.1

commit v5 on v4

--- a/solution.py
+++ b/solution.py
@@ -40,40 +40,31 @@
     return blocks
 
 
-def direct_gather(block, axis_name, count):
-    cycle = snake_cycle(count)
-    shifts = list(range(1, count // 2 + 1)) + [-k for k in range(1, (count - 1) // 2 + 1)]
-    blocks = [block]
-    for shift in shifts:
-        pairs = [(cycle[(p - shift) % count], cycle[p]) for p in range(count)]
-        blocks.append(lax.ppermute(block, axis_name, pairs))
-    return blocks
-
-
 def out_proj_kernel(group_count, set_count, tiles_per_set, table_ref, *refs):
     att_refs = refs[:group_count]
     out_ref = refs[-1]
     tile = pl.program_id(0)
 
-    def accumulate(w_ref):
+    def accumulate(w_refs):
         total = None
         for group in range(group_count):
-            term = jnp.dot(att_refs[group][...], w_ref[group], preferred_element_type=jnp.float32)
+            term = jnp.dot(att_refs[group][...], w_refs[group][...], preferred_element_type=jnp.float32)
             term = term.astype(jnp.bfloat16).astype(jnp.float32)
             total = term if total is None else total + term
         out_ref[...] = total
 
     for which in range(set_count):
-        w_ref = refs[group_count + which]
+        w_refs = refs[group_count * (which + 1):group_count * (which + 2)]
 
         @pl.when(tile // tiles_per_set == which)
         def _():
-            accumulate(w_ref)
+            accumulate(w_refs)
 
 
 def grouped_out_proj(table, att_all, weight_sets, tile_width=512):
     set_count = len(weight_sets)
-    group_count, head_width, set_width = weight_sets[0].shape
+    group_count = len(weight_sets[0])
+    head_width, set_width = weight_sets[0][0].shape
     token_count = att_all.shape[0]
     tile_width = min(tile_width, set_width)
     tiles_per_set = set_width // tile_width
@@ -83,15 +74,17 @@
 
     def weight_spec(which):
         return pl.BlockSpec(
-            (group_count, head_width, tile_width),
-            lambda n, p: (0, 0, jnp.clip(n - which * tiles_per_set, 0, tiles_per_set - 1)),
+            (head_width, tile_width),
+            lambda n, p: (0, jnp.clip(n - which * tiles_per_set, 0, tiles_per_set - 1)),
         )
 
     out_spec = pl.BlockSpec(
         (token_count, tile_width),
         lambda n, p: (0, p[n // tiles_per_set] * tiles_per_set + n % tiles_per_set),
     )
-    in_specs = [att_spec(g) for g in range(group_count)] + [weight_spec(k) for k in range(set_count)]
+    in_specs = [att_spec(g) for g in range(group_count)]
+    for which in range(set_count):
+        in_specs += [weight_spec(which)] * group_count
     width = set_count * set_width
     flops = 2 * token_count * head_width * group_count * width
     moved = 2 * token_count * head_width * group_count + 2 * group_count * head_width * width
@@ -107,7 +100,7 @@
         cost_estimate=pl.CostEstimate(
             flops=flops, bytes_accessed=moved + token_count * width * 4, transcendentals=0
         ),
-    )(table, *([att_all] * group_count), *weight_sets)
+    )(table, *([att_all] * group_count), *[b for blocks in weight_sets for b in blocks])
 
 
 def select_row(source, target):
@@ -169,11 +162,15 @@
         column_part = model_width // (rep_count * span_count)
         slot = rep_index * span_count + span_index
         w_out_part = lax.dynamic_slice_in_dim(w_out, slot * column_part, column_part, 1)
-        mine = jnp.stack(ring_gather(w_out_part, "tp", tp_count))
+        mine_blocks = ring_gather(w_out_part, "tp", tp_count)
         swap = [(0, 1), (1, 0)]
-        from_rep = lax.ppermute(mine, "rep", swap)
-        from_span = lax.ppermute(jnp.stack([mine, from_rep]), "span", swap)
-        weight_sets = [mine, from_rep, from_span[0], from_span[1]]
+        rep_blocks = [lax.ppermute(b, "rep", swap) for b in mine_blocks]
+        weight_sets = [
+            mine_blocks,
+            rep_blocks,
+            [lax.ppermute(b, "span", swap) for b in mine_blocks],
+            [lax.ppermute(b, "span", swap) for b in rep_blocks],
+        ]
         slots = [
             ((rep_index + dr) % 2) * span_count + (span_index + ds) % 2
             for ds in (0, 1)

time: 438 us -> 393 us (0.90)
  local copies, waits for them, and re-layouts: 35.7 us -> 11 us
  other arithmetic: 32.2 us -> 25.1 us
  waiting for transfers between devices: 276 us -> 269 us
    all_gather x1, waiting for transfers between devices: 34.2 us -> 91.8 us  [local(): lax.all_gather(hidden_in, 'tp', axis=2, tiled=True).astype(jnp.float32)]
    ppermute x2 -> x24, waiting for transfers between devices: 77.8 us -> 27.8 us  [the longest x8 26.5 us: local(): rep_blocks = [lax.ppermute(b, 'rep', swap) for b in mine_blocks]]
    ppermute x4, waiting for transfers between devices: 44.2 us -> 24.4 us  [ring_gather(): forward = lax.ppermute(forward, axis_name, ahead)]
    ppermute x4, starting transfers between devices: 19.9 us -> 4.24 us  [ring_gather(): forward = lax.ppermute(forward, axis_name, ahead)]
    ppermute x2 -> x24, starting transfers between devices: 1.54 us -> 11.5 us  [the longest x8 9.08 us: local(): rep_blocks = [lax.ppermute(b, 'rep', swap) for b in mine_blocks]]
    unnamed x36 -> x71, local copies, waits for them, and re-layouts: 15.1 us -> 7.56 us
    squeeze x1 -> x0, local copies, waits for them, and re-layouts: 6.87 us -> none  [local(): weight_sets = [mine, from_rep, from_span[0], from_span[1]]]
    ppermute x3, waiting for transfers between devices: 0.6 us -> 6.85 us  [ring_gather(): backward = lax.ppermute(backward, axis_name, behind)]
  transfers between devices with their start and end apart: 14 -> 36, of which waited for: 8 -> 15; matrix products, arithmetic and copies ran while one was open for 20% -> 9% of each run, Pallas kernels for 5% -> 6%
where the time goes in v5:
time: 393 us
  waiting for transfers between devices  269 us (68%)
  matrix products  27.1 us (7%)
  other arithmetic  25.1 us (6%)
  Pallas kernels  22.4 us (6%)
  starting transfers between devices  18.8 us (5%)
  between operations  14.3 us (4%)
  local copies, waits for them, and re-layouts  11 us (3%)
  blocking collectives  4.44 us (1%)
    reduce_scatter x1, waiting for transfers between devices, local(): lax.psum_scatter(down_terms.astype(jnp.bfloat16), 'tp', scatter_dimension...  116 us
    all_gather x1, waiting for transfers between devices, local(): lax.all_gather(hidden_in, 'tp', axis=2, tiled=True).astype(jnp.float32)  91.8 us
    ppermute x8, waiting for transfers between devices, local(): rep_blocks = [lax.ppermute(b, 'rep', swap) for b in mine_blocks]  26.5 us
    ppermute x4, waiting for transfers between devices, ring_gather(): forward = lax.ppermute(forward, axis_name, ahead)  24.4 us
    pallas_call x1, Pallas kernels, grouped_out_proj(): pl.pallas_call(functools.partial(out_proj_kernel, group_count, set_count,...  22.4 us
    reduce_sum x2, other arithmetic, normalize(): jnp.mean(values * values, axis=-1, keepdims=True) + EPSILON  17.6 us
    dot_general x1, matrix products, local(): pre_act = jnp.dot(mlp_in, up_full, preferred_element_type=jnp.float32)  10 us
    ppermute x8, starting transfers between devices, local(): rep_blocks = [lax.ppermute(b, 'rep', swap) for b in mine_blocks]  9.08 us
  transfers between devices with their start and end apart: 36, of which 15 were waited for; matrix products, arithmetic and copies ran while one was open for 9% of the time, Pallas kernels for 6%

profile of v5, /device:TPU:0, one launch (start us, length us, event | category | flops | bytes accessed | tf_op | source)
XLA Modules:
  0.0 392.5 jit_solution(3206226855251728643)
XLA Ops:
  6.5 0.7 all-gather.5.cloned.1.call-update
  7.4 6.7 %copy.27 = bf16[6144,3,128]{0,2,1:T(8,128)(2,1)} copy(bf16[6144,3,128]{2,0,1:T(8,128)(2,1)} %param.19) | data formatting | bytes 9437184 | tf_op args[7]
  15.5 2.3 all_gather.19
  17.7 0.7 fusion.41
  18.8 0.7 slice_bitcast_fusion.5
  19.5 91.8 %all-gather.5.cloned.1.call-done = bf16[4,128,6144]{2,1,0:T(8,128)(2,1)} async-done(((bf16[4,128,768]{2,1,0:T(8,128)(2,1)}), bf16[4,128,6144]{2,1,0:T(8,128)(2,1)}) %all-gather.5.cloned.1.call-update) | async-done | bytes 6291472 | tf_op jit(solution)/shard_map/all_gather | solution.py:155
  111.4 4.2 %fusion = f32[4,128]{1,0:T(4,128)S(1)} fusion(bf16[4,128,6144]{2,1,0:T(8,128)(2,1)} %all-gather.5.cloned.1.call-done), kind=kLoop, calls=%fused_computation.3 | loop fusion | flops 9436672 | bytes 6293504 | tf_op jit(solution)/shard_map/reduce_sum | solution.py:20
  116.0 2.7 fusion.3
  118.7 5.8 %convolution_convert_fusion.1 = bf16[512,384]{1,0:T(8,128)(2,1)S(1)} fusion(bf16[512,6144]{1,0:T(8,128)(2,1)S(1)} %bitcast.107, bf16[6144,384]{0,1:T(8,128)(2,1)} %bitcast.108), kind=kOutput, calls=%fused_computation.28 | convolution fusion | flops 2416115712 | bytes 11403264 | tf_op jit(solution)/shard_map/dot_general | solution.py:202
  125.2 2.2 all_gather.20
  128.0 0.8 fusion.12
  128.8 0.7 fusion.11
  129.5 0.9 divide_convert_fusion
  130.9 1.1 fusion.17
  132.1 0.7 all-gather.9.cloned.1.call-update
  133.5 0.9 collective-permute-start
  134.4 1.2 collective-permute-start.4
  135.5 1.5 collective-permute-start.7
  137.0 9.1 %collective-permute-done.refs_9_ = bf16[128,1536]{1,0:T(8,128)(2,1)S(1)} collective-permute-done((bf16[128,1536]{1,0:T(8,128)(2,1)S(1)}, bf16[128,1536]{1,0:T(8,128)(2,1)S(1)}, u32[]{:S(2)}, u32[]{:S(2)}) %collective-permute-start) | collective-permute-done | bytes 393248 | tf_op jit(solution)/shard_map/ppermute | solution.py:34
  146.1 0.8 collective-permute-start.1
  146.9 1.2 collective-permute-start.5
  148.1 1.5 collective-permute-start.8
  150.2 6.3 %collective-permute-done.1.refs_10_ = bf16[128,1536]{1,0:T(8,128)(2,1)S(1)} collective-permute-done((bf16[128,1536]{1,0:T(8,128)(2,1)S(1)}, bf16[128,1536]{1,0:T(8,128)(2,1)S(1)}, u32[]{:S(2)}, u32[]{:S(2)}) %collective-permute-start.1) | collective-permute-done | bytes 393248 | tf_op jit(solution)/shard_map/ppermute | solution.py:34
  156.4 2.3 collective-permute-done.5.refs_14_
  158.7 1.5 collective-permute-done.8.refs_17_
  160.2 0.8 collective-permute-start.2
  161.0 5.3 %collective-permute-done.12.refs_21_ = bf16[128,1536]{1,0:T(8,128)(2,1)S(1)} collective-permute-done((bf16[128,1536]{1,0:T(8,128)(2,1)S(1)}, bf16[128,1536]{1,0:T(8,128)(2,1)S(1)}, u32[]{:S(2)}, u32[]{:S(2)}) %collective-permute-start.12) | collective-permute-done | bytes 393248 | tf_op jit(solution)/shard_map/ppermute | solution.py:167
  166.9 1.5 collective-permute-start.9
  168.9 5.6 %collective-permute-done.2.refs_11_ = bf16[128,1536]{1,0:T(8,128)(2,1)S(1)} collective-permute-done((bf16[128,1536]{1,0:T(8,128)(2,1)S(1)}, bf16[128,1536]{1,0:T(8,128)(2,1)S(1)}, u32[]{:S(2)}, u32[]{:S(2)}) %collective-permute-start.2) | collective-permute-done | bytes 393248 | tf_op jit(solution)/shard_map/ppermute | solution.py:34
  174.5 4.6 %collective-permute-done.6.refs_15_ = bf16[128,1536]{1,0:T(8,128)(2,1)S(1)} collective-permute-done((bf16[128,1536]{1,0:T(8,128)(2,1)S(1)}, bf16[128,1536]{1,0:T(8,128)(2,1)S(1)}, u32[]{:S(2)}, u32[]{:S(2)}) %collective-permute-start.6) | collective-permute-done | bytes 393248 | tf_op jit(solution)/shard_map/ppermute | solution.py:38
  179.6 4.3 %collective-permute-done.13.refs_22_ = bf16[128,1536]{1,0:T(8,128)(2,1)} collective-permute-done((bf16[128,1536]{1,0:T(8,128)(2,1)S(1)}, bf16[128,1536]{1,0:T(8,128)(2,1)}, u32[]{:S(2)}, u32[]{:S(2)}) %collective-permute-start.13) | collective-permute-done | bytes 393248 | tf_op jit(solution)/shard_map/ppermute | solution.py:167
  183.9 1.7 collective-permute-start.3
  185.6 1.5 collective-permute-start.10
  187.0 0.6 collective-permute-start.14
  188.3 3.5 collective-permute-done.3.refs_12_
  191.8 5.9 %collective-permute-done.10.refs_19_ = bf16[128,1536]{1,0:T(8,128)(2,1)} collective-permute-done((bf16[128,1536]{1,0:T(8,128)(2,1)S(1)}, bf16[128,1536]{1,0:T(8,128)(2,1)}, u32[]{:S(2)}, u32[]{:S(2)}) %collective-permute-start.10) | collective-permute-done | bytes 393248 | tf_op jit(solution)/shard_map/ppermute | solution.py:167
  197.7 1.5 collective-permute-start.11
  199.2 6.6 %collective-permute-done.14.refs_23_ = bf16[128,1536]{1,0:T(8,128)(2,1)} collective-permute-done((bf16[128,1536]{1,0:T(8,128)(2,1)S(1)}, bf16[128,1536]{1,0:T(8,128)(2,1)}, u32[]{:S(2)}, u32[]{:S(2)}) %collective-permute-start.14) | collective-permute-done | bytes 393248 | tf_op jit(solution)/shard_map/ppermute | solution.py:167
  207.0 3.0 collective-permute-done.11.refs_20_
  210.1 0.7 fusion.40
  210.8 0.7 concatenate.22.table_ref
  211.5 1.2 collective-permute-done.27.refs_36_
  212.8 22.4 %shard_map.118 = f32[512,6144]{1,0:T(8,128)} custom-call(s32[12]{0:T(128)} %concatenate.22.table_ref, bf16[512,1024]{1,0:T(8,128)(2,1)} %all-gather.7.cloned.1.call-done.refs_0_.refs_1_.refs_2_.refs_3_.refs_4_.refs_5_.refs_6_.refs_7_, bf16[512,1024]{1,0:T(8,128)(2,1)} %all-gather.7.cloned.1.call-done.refs_0_.refs_1_.refs_2_.refs_3_.refs_4_.refs_5_.refs_6_.refs_7_, ...), custom_call_target="tpu_custom_call" | custom-call | flops 6442450944 | bytes 26214400 | tf_op jit(solution)/shard_map/pallas_call | solution.py:91
  235.2 13.4 %multiply_reduce_fusion = (f32[4,128]{1,0:T(4,128)S(1)}, f32[4,128,6144]{2,1,0:T(8,128)}) fusion(f32[4,128,6144]{2,1,0:T(8,128)} %bitcast.106, f32[4,6144]{1,0:T(4,128)S(1)} %get-tuple-element.15, bf16[4,128,6144]{2,1,0:T(8,128)(2,1)} %all-gather.5.cloned.1.call-done), kind=kLoop, calls=%fused_computation.8 | loop fusion | flops 15728128 | bytes 31557632 | tf_op jit(solution)/shard_map/reduce_sum | solution.py:20
  248.6 10.0 %fusion.27 = bf16[4,128,512]{2,1,0:T(8,128)(2,1)S(1)} fusion(bf16[6144,512]{1,0:T(8,128)(2,1)} %all-gather.9.cloned.1.call-done, f32[4,128,6144]{2,1,0:T(8,128)} %get-tuple-element.6, f32[4,6144]{1,0:T(4,128)S(1)} %copy-done.28, f32[4,6144]{1,0:T(4,128)S(1)} %get-tuple-element.11, f32[4,128]{1,0:T(4,128)S(1)} %add_rsqrt_fusion), kind=kOutput, calls=%fused_computation.39 | convolution fusion | flops 3236167680 | bytes 19597312 | tf_op jit(solution)/shard_map/dot_general | solution.py:248
  258.7 8.1 %convolution_convert_fusion = bf16[4,128,6144]{2,1,0:T(8,128)(2,1)} fusion(bf16[4,128,512]{2,1,0:T(8,128)(2,1)S(1)} %fusion.27, bf16[512,6144]{1,0:T(8,128)(2,1)} %all-gather.11.cloned.1.call-done), kind=kOutput, calls=%fused_computation.9 | convolution fusion | flops 3224371200 | bytes 13107200 | tf_op jit(solution)/shard_map/dot_general | solution.py:250
  266.8 116.4 %reduce-scatter.2.cloned.1.call-done = bf16[4,128,768]{2,1,0:T(8,128)(2,1)} async-done(((bf16[4,128,6144]{2,1,0:T(8,128)(2,1)}), bf16[4,128,768]{2,1,0:T(8,128)(2,1)}) %reduce-scatter.2.cloned.1.call-update) | async-done | bytes 786448 | tf_op jit(solution)/shard_map/reduce_scatter | solution.py:251
  383.3 2.7 add_convert_fusion.2
  (139 shorter events, 8.1 us)
Async XLA Ops:
  6.5 126.9 %copy-start = (bf16[128,6144]{1,0:T(8,128)(2,1)S(1)}, bf16[128,6144]{1,0:T(8,128)(2,1)}, u32[]{:S(2)}) copy-start(bf16[128,6144]{1,0:T(8,128)(2,1)} %param.20) | copy-start | bytes 4718596
  6.5 104.8 %all-gather.5.cloned.1.call-start = ((), (), s32[]{:S(2)}) async-start(), calls=%async_computation.1 | async-start | bytes 7077888 | tf_op jit(solution)/shard_map/all_gather | solution.py:155
  7.3 205.4 %all-gather.7.cloned.1.call-start = ((), (), s32[]{:S(2)}) async-start(), calls=%async_computation.2 | async-start | bytes 1179648 | tf_op jit(solution)/shard_map/all_gather | solution.py:226
  132.0 116.6 %all-gather.9.cloned.1.call-start = ((), (), s32[]{:S(2)}) async-start(), calls=%async_computation.3 | async-start | bytes 9437184 | tf_op jit(solution)/shard_map/all_gather | solution.py:188
  132.8 125.9 %all-gather.11.cloned.1.call-start = ((), (), s32[]{:S(2)}) async-start(), calls=%async_computation.4 | async-start | bytes 9437184 | tf_op jit(solution)/shard_map/all_gather | solution.py:189
  133.3 249.9 %reduce-scatter.2.cloned.1.call-start = ((), (), s32[]{:S(2)}) async-start(), calls=%async_computation.5 | async-start | bytes 7077888 | tf_op jit(solution)/shard_map/reduce_scatter | solution.py:251
  133.4 79.3 %copy-start.3 = (bf16[128,1536]{1,0:T(8,128)(2,1)}, bf16[128,1536]{1,0:T(8,128)(2,1)S(1)}, u32[]{:S(2)}) copy-start(bf16[128,1536]{1,0:T(8,128)(2,1)S(1)} %constant_dynamic-slice_fusion.refs_8_) | copy-start | bytes 1179652
  133.5 12.6 %collective-permute-start = (bf16[128,1536]{1,0:T(8,128)(2,1)S(1)}, bf16[128,1536]{1,0:T(8,128)(2,1)S(1)}, u32[]{:S(2)}, u32[]{:S(2)}) collective-permute-start(bf16[128,1536]{1,0:T(8,128)(2,1)S(1)} %constant_dynamic-slice_fusion.refs_8_), channel_id=1, source_target_pairs={{0,2},{2,4},{4,6},{6,7},{7,5},{5,3},{3,1},{1,0},{8,10},{10,12},{12... | collective-permute-start | bytes 1179656 | tf_op jit(solution)/shard_map/ppermute | solution.py:34
  134.4 12.6 %collective-permute-start.4 = (bf16[128,1536]{1,0:T(8,128)(2,1)S(1)}, bf16[128,1536]{1,0:T(8,128)(2,1)S(1)}, u32[]{:S(2)}, u32[]{:S(2)}) collective-permute-start(bf16[128,1536]{1,0:T(8,128)(2,1)S(1)} %constant_dynamic-slice_fusion.refs_8_), channel_id=1, source_target_pairs={{0,1},{2,0},{4,2},{6,4},{7,6},{5,7},{3,5},{1,3},{8,9},{10,8},{12,1... | collective-permute-start | bytes 1179656 | tf_op jit(solution)/shard_map/ppermute | solution.py:38
  135.5 14.1 %collective-permute-start.7 = (bf16[128,1536]{1,0:T(8,128)(2,1)S(1)}, bf16[128,1536]{1,0:T(8,128)(2,1)S(1)}, u32[]{:S(2)}, u32[]{:S(2)}) collective-permute-start(bf16[128,1536]{1,0:T(8,128)(2,1)S(1)} %constant_dynamic-slice_fusion.refs_8_), channel_id=1, source_target_pairs={{0,16},{16,0},{1,17},{17,1},{2,18},{18,2},{3,19},{19,3},{4,20},{20... | collective-permute-start | bytes 1179656 | tf_op jit(solution)/shard_map/ppermute | solution.py:167
  137.0 13.1 %collective-permute-start.15 = (bf16[128,1536]{1,0:T(8,128)(2,1)S(1)}, bf16[128,1536]{1,0:T(8,128)(2,1)S(1)}, u32[]{:S(2)}, u32[]{:S(2)}) collective-permute-start(bf16[128,1536]{1,0:T(8,128)(2,1)S(1)} %constant_dynamic-slice_fusion.refs_8_), channel_id=1, source_target_pairs={{0,8},{8,0},{1,9},{9,1},{2,10},{10,2},{3,11},{11,3},{4,12},{12,4},... | collective-permute-start | bytes 1179656 | tf_op jit(solution)/shard_map/ppermute | solution.py:171
  146.1 66.6 %copy-start.4 = (bf16[128,1536]{1,0:T(8,128)(2,1)}, bf16[128,1536]{1,0:T(8,128)(2,1)S(1)}, u32[]{:S(2)}) copy-start(bf16[128,1536]{1,0:T(8,128)(2,1)S(1)} %collective-permute-done.refs_9_) | copy-start | bytes 1179652
  146.1 10.3 %collective-permute-start.1 = (bf16[128,1536]{1,0:T(8,128)(2,1)S(1)}, bf16[128,1536]{1,0:T(8,128)(2,1)S(1)}, u32[]{:S(2)}, u32[]{:S(2)}) collective-permute-start(bf16[128,1536]{1,0:T(8,128)(2,1)S(1)} %collective-permute-done.refs_9_), channel_id=1, source_target_pairs={{0,2},{2,4},{4,6},{6,7},{7,5},{5,3},{3,1},{1,0},{8,10},{10,12},{12... | collective-permute-start | bytes 1179656 | tf_op jit(solution)/shard_map/ppermute | solution.py:34
  146.9 65.8 %copy-start.5 = (bf16[128,1536]{1,0:T(8,128)(2,1)}, bf16[128,1536]{1,0:T(8,128)(2,1)S(1)}, u32[]{:S(2)}) copy-start(bf16[128,1536]{1,0:T(8,128)(2,1)S(1)} %collective-permute-done.4.refs_13_) | copy-start | bytes 1179652
  146.9 11.8 %collective-permute-start.5 = (bf16[128,1536]{1,0:T(8,128)(2,1)S(1)}, bf16[128,1536]{1,0:T(8,128)(2,1)S(1)}, u32[]{:S(2)}, u32[]{:S(2)}) collective-permute-start(bf16[128,1536]{1,0:T(8,128)(2,1)S(1)} %collective-permute-done.4.refs_13_), channel_id=1, source_target_pairs={{0,1},{2,0},{4,2},{6,4},{7,6},{5,7},{3,5},{1,3},{8,9},{10,8},{12,1... | collective-permute-start | bytes 1179656 | tf_op jit(solution)/shard_map/ppermute | solution.py:38
  148.1 12.1 %collective-permute-start.8 = (bf16[128,1536]{1,0:T(8,128)(2,1)S(1)}, bf16[128,1536]{1,0:T(8,128)(2,1)S(1)}, u32[]{:S(2)}, u32[]{:S(2)}) collective-permute-start(bf16[128,1536]{1,0:T(8,128)(2,1)S(1)} %collective-permute-done.refs_9_), channel_id=1, source_target_pairs={{0,16},{16,0},{1,17},{17,1},{2,18},{18,2},{3,19},{19,3},{4,20},{20... | collective-permute-start | bytes 1179656 | tf_op jit(solution)/shard_map/ppermute | solution.py:167
  149.6 63.1 %copy-start.6 = (bf16[128,1536]{1,0:T(8,128)(2,1)}, bf16[128,1536]{1,0:T(8,128)(2,1)S(1)}, u32[]{:S(2)}) copy-start(bf16[128,1536]{1,0:T(8,128)(2,1)S(1)} %collective-permute-done.7.refs_16_) | copy-start | bytes 1179652
  149.6 16.7 %collective-permute-start.12 = (bf16[128,1536]{1,0:T(8,128)(2,1)S(1)}, bf16[128,1536]{1,0:T(8,128)(2,1)S(1)}, u32[]{:S(2)}, u32[]{:S(2)}) collective-permute-start(bf16[128,1536]{1,0:T(8,128)(2,1)S(1)} %collective-permute-done.4.refs_13_), channel_id=1, source_target_pairs={{0,16},{16,0},{1,17},{17,1},{2,18},{18,2},{3,19},{19,3},{4,20},{20... | collective-permute-start | bytes 1179656 | tf_op jit(solution)/shard_map/ppermute | solution.py:167
  150.1 62.6 %copy-start.7 = (bf16[128,1536]{1,0:T(8,128)(2,1)}, bf16[128,1536]{1,0:T(8,128)(2,1)S(1)}, u32[]{:S(2)}) copy-start(bf16[128,1536]{1,0:T(8,128)(2,1)S(1)} %collective-permute-done.15.refs_24_) | copy-start | bytes 1179652
  150.1 16.7 %collective-permute-start.16 = (bf16[128,1536]{1,0:T(8,128)(2,1)S(1)}, bf16[128,1536]{1,0:T(8,128)(2,1)S(1)}, u32[]{:S(2)}, u32[]{:S(2)}) collective-permute-start(bf16[128,1536]{1,0:T(8,128)(2,1)S(1)} %collective-permute-done.refs_9_), channel_id=1, source_target_pairs={{0,8},{8,0},{1,9},{9,1},{2,10},{10,2},{3,11},{11,3},{4,12},{12,4},... | collective-permute-start | bytes 1179656 | tf_op jit(solution)/shard_map/ppermute | solution.py:171
  156.4 56.3 %copy-start.8 = (bf16[128,1536]{1,0:T(8,128)(2,1)}, bf16[128,1536]{1,0:T(8,128)(2,1)S(1)}, u32[]{:S(2)}) copy-start(bf16[128,1536]{1,0:T(8,128)(2,1)S(1)} %collective-permute-done.1.refs_10_) | copy-start | bytes 1179652
  156.4 11.9 %collective-permute-start.20 = (bf16[128,1536]{1,0:T(8,128)(2,1)S(1)}, bf16[128,1536]{1,0:T(8,128)(2,1)S(1)}, u32[]{:S(2)}, u32[]{:S(2)}) collective-permute-start(bf16[128,1536]{1,0:T(8,128)(2,1)S(1)} %collective-permute-done.4.refs_13_), channel_id=1, source_target_pairs={{0,8},{8,0},{1,9},{9,1},{2,10},{10,2},{3,11},{11,3},{4,12},{12,4},... | collective-permute-start | bytes 1179656 | tf_op jit(solution)/shard_map/ppermute | solution.py:171
  158.7 54.1 %copy-start.9 = (bf16[128,1536]{1,0:T(8,128)(2,1)}, bf16[128,1536]{1,0:T(8,128)(2,1)S(1)}, u32[]{:S(2)}) copy-start(bf16[128,1536]{1,0:T(8,128)(2,1)S(1)} %collective-permute-done.5.refs_14_) | copy-start | bytes 1179652
  158.7 10.2 %collective-permute-start.23 = (bf16[128,1536]{1,0:T(8,128)(2,1)S(1)}, bf16[128,1536]{1,0:T(8,128)(2,1)S(1)}, u32[]{:S(2)}, u32[]{:S(2)}) collective-permute-start(bf16[128,1536]{1,0:T(8,128)(2,1)S(1)} %collective-permute-done.7.refs_16_), channel_id=1, source_target_pairs={{0,8},{8,0},{1,9},{9,1},{2,10},{10,2},{3,11},{11,3},{4,12},{12,4},... | collective-permute-start | bytes 1179656 | tf_op jit(solution)/shard_map/ppermute | solution.py:172
  160.2 26.9 %copy-start.10 = (bf16[128,1536]{1,0:T(8,128)(2,1)}, bf16[128,1536]{1,0:T(8,128)(2,1)S(1)}, u32[]{:S(2)}) copy-start(bf16[128,1536]{1,0:T(8,128)(2,1)S(1)} %collective-permute-done.8.refs_17_) | copy-start | bytes 1179652
  160.2 14.4 %collective-permute-start.2 = (bf16[128,1536]{1,0:T(8,128)(2,1)S(1)}, bf16[128,1536]{1,0:T(8,128)(2,1)S(1)}, u32[]{:S(2)}, u32[]{:S(2)}) collective-permute-start(bf16[128,1536]{1,0:T(8,128)(2,1)S(1)} %collective-permute-done.1.refs_10_), channel_id=1, source_target_pairs={{0,2},{2,4},{4,6},{6,7},{7,5},{5,3},{3,1},{1,0},{8,10},{10,12},{12... | collective-permute-start | bytes 1179656 | tf_op jit(solution)/shard_map/ppermute | solution.py:34
  166.3 12.8 %collective-permute-start.6 = (bf16[128,1536]{1,0:T(8,128)(2,1)S(1)}, bf16[128,1536]{1,0:T(8,128)(2,1)S(1)}, u32[]{:S(2)}, u32[]{:S(2)}) collective-permute-start(bf16[128,1536]{1,0:T(8,128)(2,1)S(1)} %collective-permute-done.5.refs_14_), channel_id=1, source_target_pairs={{0,1},{2,0},{4,2},{6,4},{7,6},{5,7},{3,5},{1,3},{8,9},{10,8},{12,1... | collective-permute-start | bytes 1179656 | tf_op jit(solution)/shard_map/ppermute | solution.py:38
  166.9 12.2 %collective-permute-start.9 = (bf16[128,1536]{1,0:T(8,128)(2,1)S(1)}, bf16[128,1536]{1,0:T(8,128)(2,1)S(1)}, u32[]{:S(2)}, u32[]{:S(2)}) collective-permute-start(bf16[128,1536]{1,0:T(8,128)(2,1)S(1)} %collective-permute-done.1.refs_10_), channel_id=1, source_target_pairs={{0,16},{16,0},{1,17},{17,1},{2,18},{18,2},{3,19},{19,3},{4,20},{20... | collective-permute-start | bytes 1179656 | tf_op jit(solution)/shard_map/ppermute | solution.py:167
  168.3 15.5 %collective-permute-start.13 = (bf16[128,1536]{1,0:T(8,128)(2,1)S(1)}, bf16[128,1536]{1,0:T(8,128)(2,1)}, u32[]{:S(2)}, u32[]{:S(2)}) collective-permute-start(bf16[128,1536]{1,0:T(8,128)(2,1)S(1)} %collective-permute-done.5.refs_14_), channel_id=1, source_target_pairs={{0,16},{16,0},{1,17},{17,1},{2,18},{18,2},{3,19},{19,3},{4,20},{20... | collective-permute-start | bytes 1179656 | tf_op jit(solution)/shard_map/ppermute | solution.py:167
  168.9 16.6 %collective-permute-start.17 = (bf16[128,1536]{1,0:T(8,128)(2,1)S(1)}, bf16[128,1536]{1,0:T(8,128)(2,1)S(1)}, u32[]{:S(2)}, u32[]{:S(2)}) collective-permute-start(bf16[128,1536]{1,0:T(8,128)(2,1)S(1)} %collective-permute-done.1.refs_10_), channel_id=1, source_target_pairs={{0,8},{8,0},{1,9},{9,1},{2,10},{10,2},{3,11},{11,3},{4,12},{12,4},... | collective-permute-start | bytes 1179656 | tf_op jit(solution)/shard_map/ppermute | solution.py:171
  174.5 12.5 %collective-permute-start.21 = (bf16[128,1536]{1,0:T(8,128)(2,1)S(1)}, bf16[128,1536]{1,0:T(8,128)(2,1)S(1)}, u32[]{:S(2)}, u32[]{:S(2)}) collective-permute-start(bf16[128,1536]{1,0:T(8,128)(2,1)S(1)} %collective-permute-done.5.refs_14_), channel_id=1, source_target_pairs={{0,8},{8,0},{1,9},{9,1},{2,10},{10,2},{3,11},{11,3},{4,12},{12,4},... | collective-permute-start | bytes 1179656 | tf_op jit(solution)/shard_map/ppermute | solution.py:171
  179.1 26.7 %copy-start.16 = (bf16[128,1536]{1,0:T(8,128)(2,1)}, bf16[128,1536]{1,0:T(8,128)(2,1)S(1)}, u32[]{:S(2)}) copy-start(bf16[128,1536]{1,0:T(8,128)(2,1)S(1)} %collective-permute-done.6.refs_15_) | copy-start | bytes 1179652
  179.1 8.5 %collective-permute-start.24 = (bf16[128,1536]{1,0:T(8,128)(2,1)S(1)}, bf16[128,1536]{1,0:T(8,128)(2,1)S(1)}, u32[]{:S(2)}, u32[]{:S(2)}) collective-permute-start(bf16[128,1536]{1,0:T(8,128)(2,1)S(1)} %collective-permute-done.8.refs_17_), channel_id=1, source_target_pairs={{0,8},{8,0},{1,9},{9,1},{2,10},{10,2},{3,11},{11,3},{4,12},{12,4},... | collective-permute-start | bytes 1179656 | tf_op jit(solution)/shard_map/ppermute | solution.py:172
  179.1 27.2 %copy-start.17 = (bf16[128,1536]{1,0:T(8,128)(2,1)}, bf16[128,1536]{1,0:T(8,128)(2,1)S(1)}, u32[]{:S(2)}) copy-start(bf16[128,1536]{1,0:T(8,128)(2,1)S(1)} %collective-permute-done.9.refs_18_) | copy-start | bytes 1179652
  179.1 8.6 %collective-permute-start.28 = (bf16[128,1536]{1,0:T(8,128)(2,1)S(1)}, bf16[128,1536]{1,0:T(8,128)(2,1)S(1)}, u32[]{:S(2)}, u32[]{:S(2)}) collective-permute-start(bf16[128,1536]{1,0:T(8,128)(2,1)S(1)} %collective-permute-done.12.refs_21_), channel_id=1, source_target_pairs={{0,8},{8,0},{1,9},{9,1},{2,10},{10,2},{3,11},{11,3},{4,12},{12,4},... | collective-permute-start | bytes 1179656 | tf_op jit(solution)/shard_map/ppermute | solution.py:172
  183.9 7.9 %collective-permute-start.3 = (bf16[128,1536]{1,0:T(8,128)(2,1)S(1)}, bf16[128,1536]{1,0:T(8,128)(2,1)}, u32[]{:S(2)}, u32[]{:S(2)}) collective-permute-start(bf16[128,1536]{1,0:T(8,128)(2,1)S(1)} %collective-permute-done.2.refs_11_), channel_id=1, source_target_pairs={{0,2},{2,4},{4,6},{6,7},{7,5},{5,3},{3,1},{1,0},{8,10},{10,12},{12... | collective-permute-start | bytes 1179656 | tf_op jit(solution)/shard_map/ppermute | solution.py:34
  185.6 12.2 %collective-permute-start.10 = (bf16[128,1536]{1,0:T(8,128)(2,1)S(1)}, bf16[128,1536]{1,0:T(8,128)(2,1)}, u32[]{:S(2)}, u32[]{:S(2)}) collective-permute-start(bf16[128,1536]{1,0:T(8,128)(2,1)S(1)} %collective-permute-done.2.refs_11_), channel_id=1, source_target_pairs={{0,16},{16,0},{1,17},{17,1},{2,18},{18,2},{3,19},{19,3},{4,20},{20... | collective-permute-start | bytes 1179656 | tf_op jit(solution)/shard_map/ppermute | solution.py:167
  187.0 18.7 %collective-permute-start.14 = (bf16[128,1536]{1,0:T(8,128)(2,1)S(1)}, bf16[128,1536]{1,0:T(8,128)(2,1)}, u32[]{:S(2)}, u32[]{:S(2)}) collective-permute-start(bf16[128,1536]{1,0:T(8,128)(2,1)S(1)} %collective-permute-done.6.refs_15_), channel_id=1, source_target_pairs={{0,16},{16,0},{1,17},{17,1},{2,18},{18,2},{3,19},{19,3},{4,20},{20... | collective-permute-start | bytes 1179656 | tf_op jit(solution)/shard_map/ppermute | solution.py:167
  187.7 18.1 %collective-permute-start.18 = (bf16[128,1536]{1,0:T(8,128)(2,1)S(1)}, bf16[128,1536]{1,0:T(8,128)(2,1)S(1)}, u32[]{:S(2)}, u32[]{:S(2)}) collective-permute-start(bf16[128,1536]{1,0:T(8,128)(2,1)S(1)} %collective-permute-done.2.refs_11_), channel_id=1, source_target_pairs={{0,8},{8,0},{1,9},{9,1},{2,10},{10,2},{3,11},{11,3},{4,12},{12,4},... | collective-permute-start | bytes 1179656 | tf_op jit(solution)/shard_map/ppermute | solution.py:171
  187.8 18.6 %collective-permute-start.22 = (bf16[128,1536]{1,0:T(8,128)(2,1)S(1)}, bf16[128,1536]{1,0:T(8,128)(2,1)S(1)}, u32[]{:S(2)}, u32[]{:S(2)}) collective-permute-start(bf16[128,1536]{1,0:T(8,128)(2,1)S(1)} %collective-permute-done.6.refs_15_), channel_id=1, source_target_pairs={{0,8},{8,0},{1,9},{9,1},{2,10},{10,2},{3,11},{11,3},{4,12},{12,4},... | collective-permute-start | bytes 1179656 | tf_op jit(solution)/shard_map/ppermute | solution.py:171
  191.8 14.7 %collective-permute-start.25 = (bf16[128,1536]{1,0:T(8,128)(2,1)S(1)}, bf16[128,1536]{1,0:T(8,128)(2,1)S(1)}, u32[]{:S(2)}, u32[]{:S(2)}) collective-permute-start(bf16[128,1536]{1,0:T(8,128)(2,1)S(1)} %collective-permute-done.9.refs_18_), channel_id=1, source_target_pairs={{0,8},{8,0},{1,9},{9,1},{2,10},{10,2},{3,11},{11,3},{4,12},{12,4},... | collective-permute-start | bytes 1179656 | tf_op jit(solution)/shard_map/ppermute | solution.py:172
  197.7 12.3 %collective-permute-start.11 = (bf16[128,1536]{1,0:T(8,128)(2,1)}, bf16[128,1536]{1,0:T(8,128)(2,1)}, u32[]{:S(2)}, u32[]{:S(2)}) collective-permute-start(bf16[128,1536]{1,0:T(8,128)(2,1)} %collective-permute-done.3.refs_12_), channel_id=1, source_target_pairs={{0,16},{16,0},{1,17},{17,1},{2,18},{18,2},{3,19},{19,3},{4,20},{20... | collective-permute-start | bytes 1179656 | tf_op jit(solution)/shard_map/ppermute | solution.py:167
  205.8 5.7 %collective-permute-start.29 = (bf16[128,1536]{1,0:T(8,128)(2,1)}, bf16[128,1536]{1,0:T(8,128)(2,1)}, u32[]{:S(2)}, u32[]{:S(2)}) collective-permute-start(bf16[128,1536]{1,0:T(8,128)(2,1)} %collective-permute-done.13.refs_22_), channel_id=1, source_target_pairs={{0,8},{8,0},{1,9},{9,1},{2,10},{10,2},{3,11},{11,3},{4,12},{12,4},... | collective-permute-start | bytes 1179656 | tf_op jit(solution)/shard_map/ppermute | solution.py:172
  205.8 5.7 %collective-permute-start.19 = (bf16[128,1536]{1,0:T(8,128)(2,1)}, bf16[128,1536]{1,0:T(8,128)(2,1)}, u32[]{:S(2)}, u32[]{:S(2)}) collective-permute-start(bf16[128,1536]{1,0:T(8,128)(2,1)} %collective-permute-done.3.refs_12_), channel_id=1, source_target_pairs={{0,8},{8,0},{1,9},{9,1},{2,10},{10,2},{3,11},{11,3},{4,12},{12,4},... | collective-permute-start | bytes 1179656 | tf_op jit(solution)/shard_map/ppermute | solution.py:171
  206.4 5.1 %collective-permute-start.26 = (bf16[128,1536]{1,0:T(8,128)(2,1)}, bf16[128,1536]{1,0:T(8,128)(2,1)}, u32[]{:S(2)}, u32[]{:S(2)}) collective-permute-start(bf16[128,1536]{1,0:T(8,128)(2,1)} %collective-permute-done.10.refs_19_), channel_id=1, source_target_pairs={{0,8},{8,0},{1,9},{9,1},{2,10},{10,2},{3,11},{11,3},{4,12},{12,4},... | collective-permute-start | bytes 1179656 | tf_op jit(solution)/shard_map/ppermute | solution.py:172
  206.5 5.0 %collective-permute-start.30 = (bf16[128,1536]{1,0:T(8,128)(2,1)}, bf16[128,1536]{1,0:T(8,128)(2,1)}, u32[]{:S(2)}, u32[]{:S(2)}) collective-permute-start(bf16[128,1536]{1,0:T(8,128)(2,1)} %collective-permute-done.14.refs_23_), channel_id=1, source_target_pairs={{0,8},{8,0},{1,9},{9,1},{2,10},{10,2},{3,11},{11,3},{4,12},{12,4},... | collective-permute-start | bytes 1179656 | tf_op jit(solution)/shard_map/ppermute | solution.py:172
  210.0 2.7 collective-permute-start.27
  266.8 119.2 %copy-start.1 = (bf16[128,6144]{1,0:T(8,128)(2,1)S(1)}, bf16[128,6144]{1,0:T(8,128)(2,1)}, u32[]{:S(2)}) copy-start(bf16[128,6144]{1,0:T(8,128)(2,1)} %param.20) | copy-start | bytes 4718596
  (20 other events, 264.0 us)
Sparse Core Ops, SparseCore 0:
  9.6 101.7 all-gather.4
  132.1 44.3 all-gather.6
  178.1 17.0 all-gather.8
  196.6 18.1 all-gather.10
  266.9 116.2 reduce-scatter.1

commit v6 on v2

--- a/solution.py
+++ b/solution.py
@@ -38,6 +38,31 @@
         backward = lax.ppermute(backward, axis_name, behind)
         blocks.append(backward)
     return blocks
+
+
+def ring_reduce_scatter(terms, axis_name, count):
+    token_count, width = terms.shape
+    block = width // count
+    half = block // 2
+    cycle = snake_cycle(count)
+    position = jnp.array([cycle.index(t) for t in range(count)], jnp.int32)[lax.axis_index(axis_name)]
+    owners = jnp.array(cycle, jnp.int32)
+    rounded = terms.astype(jnp.bfloat16)
+
+    def own_part(slot, side):
+        start = owners[slot % count] * block + side * half
+        return lax.dynamic_slice_in_dim(rounded, start, half, 1).astype(jnp.float32)
+
+    ahead = [(cycle[p], cycle[(p + 1) % count]) for p in range(count)]
+    behind = [(cycle[p], cycle[(p - 1) % count]) for p in range(count)]
+    forward = own_part(position - 1 + count, 0)
+    backward = own_part(position + 1, 1)
+    for step in range(count - 1):
+        forward = lax.ppermute(forward.astype(jnp.bfloat16), axis_name, ahead).astype(jnp.float32)
+        forward = forward + own_part(position - 2 - step + 2 * count, 0)
+        backward = lax.ppermute(backward.astype(jnp.bfloat16), axis_name, behind).astype(jnp.float32)
+        backward = backward + own_part(position + 2 + step, 1)
+    return jnp.concatenate([forward, backward], axis=1)
 
 
 def out_proj_kernel(group_count, tiles_per_half, span_ref, *refs):
@@ -219,9 +244,14 @@
     pre_act = jnp.dot(mlp_in, up_full, preferred_element_type=jnp.float32)
     hidden_units = jax.nn.gelu(pre_act).astype(jnp.bfloat16)
     down_terms = jnp.dot(hidden_units, down_full, preferred_element_type=jnp.float32)
-    mlp_out = lax.psum_scatter(
-        down_terms.astype(jnp.bfloat16), "tp", scatter_dimension=2, tiled=True
-    ).astype(jnp.float32)
+    if gather_weights:
+        mlp_out = ring_reduce_scatter(
+            down_terms.reshape(token_count, model_width), "tp", tp_count
+        ).reshape(local_count, row_count, share_width)
+    else:
+        mlp_out = lax.psum_scatter(
+            down_terms.astype(jnp.bfloat16), "tp", scatter_dimension=2, tiled=True
+        ).astype(jnp.float32)
     if gather_weights:
         residual = lax.dynamic_slice_in_dim(residual_full, tp_rank * share_width, share_width, 2)
         mod_share = lax.dynamic_slice_in_dim(mod_rows, tp_rank * share_width, share_width, 2)

time: 385 us -> 360 us (0.935)
  waiting for transfers between devices: 258 us -> 188 us
  starting transfers between devices: 24.8 us -> 41.6 us
  between operations: 14.2 us -> 30.8 us
  other arithmetic: 25.2 us -> 34.6 us
    reduce_scatter x1 -> x0, waiting for transfers between devices: 118 us -> none  [local(): lax.psum_scatter(down_terms.astype(jnp.bfloat16), 'tp', scatter_dimension...]
    ppermute x0 -> x14, waiting for transfers between devices: none -> 52.2 us  [the longest x7 43.6 us: ring_reduce_scatter(): lax.ppermute(forward.astype(jnp.bfloat16), axis_name, ahead)]
    ppermute x0 -> x14, starting transfers between devices: none -> 16.3 us  [the longest x7 9.93 us: ring_reduce_scatter(): lax.ppermute(forward.astype(jnp.bfloat16), axis_name, ahead)]
    convert_element_type x0 -> x6, other arithmetic: none -> 8.02 us  [ring_reduce_scatter(): forward.astype(jnp.bfloat16)]
    unnamed x57 -> x47, local copies, waits for them, and re-layouts: 9.28 us -> 10.3 us
  transfers between devices with their start and end apart: 26 -> 39, of which waited for: 10 -> 20; matrix products, arithmetic and copies ran while one was open for 13% -> 14% of each run, Pallas kernels for 5% -> 6%
where the time goes in v6:
time: 360 us; the launch traced here: 359 us
  waiting for transfers between devices  188 us (52%)
  starting transfers between devices  41.6 us (12%)
  other arithmetic  34.6 us (10%)
  between operations  30.8 us (9%)
  matrix products  25.3 us (7%)
  Pallas kernels  20.4 us (6%)
  local copies, waits for them, and re-layouts  13.1 us (4%)
  blocking collectives  4.74 us (1%)
    all_gather x1, waiting for transfers between devices, local(): lax.all_gather(hidden_in, 'tp', axis=2, tiled=True).astype(jnp.float32)  68.5 us
    ppermute x8, waiting for transfers between devices, ring_gather(): forward = lax.ppermute(forward, axis_name, ahead)  49.9 us
    ppermute x7, waiting for transfers between devices, ring_reduce_scatter(): lax.ppermute(forward.astype(jnp.bfloat16), axis_name, ahead)  43.6 us
    pallas_call x1, Pallas kernels, grouped_out_proj(): pl.pallas_call(functools.partial(out_proj_kernel, group_count, tiles_per_...  20.4 us
    ppermute x8, starting transfers between devices, ring_gather(): forward = lax.ppermute(forward, axis_name, ahead)  18.8 us
    reduce_sum x2, other arithmetic, normalize(): jnp.mean(values * values, axis=-1, keepdims=True) + EPSILON  17.7 us
    ppermute x6, waiting for transfers between devices, ring_gather(): backward = lax.ppermute(backward, axis_name, behind)  16.4 us
    unnamed x47, local copies, waits for them, and re-layouts  10.3 us
  transfers between devices with their start and end apart: 39, of which 20 were waited for; matrix products, arithmetic and copies ran while one was open for 14% of the time, Pallas kernels for 6%

profile of v6, /device:TPU:0, one launch (start us, length us, event | category | flops | bytes accessed | tf_op | source)
XLA Modules:
  0.0 359.0 jit_solution(14339275770087881244)
XLA Ops:
  8.2 3.1 collective-permute-start.7
  11.3 6.7 %copy.28 = bf16[6144,3,128]{0,2,1:T(8,128)(2,1)} copy(bf16[6144,3,128]{2,0,1:T(8,128)(2,1)} %param.20) | data formatting | bytes 9437184 | tf_op args[7]
  20.3 15.5 %collective-permute-done.7.refs_9_ = bf16[128,3072]{1,0:T(8,128)(2,1)} collective-permute-done((bf16[128,3072]{1,0:T(8,128)(2,1)S(1)}, bf16[128,3072]{1,0:T(8,128)(2,1)}, u32[]{:S(2)}, u32[]{:S(2)}) %collective-permute-start.7) | collective-permute-done | bytes 786464 | tf_op jit(solution)/shard_map/ppermute | solution.py:34
  35.7 8.5 %collective-permute-start.8 = (bf16[128,3072]{1,0:T(8,128)(2,1)}, bf16[128,3072]{1,0:T(8,128)(2,1)}, u32[]{:S(2)}, u32[]{:S(2)}) collective-permute-start(bf16[128,3072]{1,0:T(8,128)(2,1)} %collective-permute-done.7.refs_9_), channel_id=1, source_target_pairs={{0,2},{2,4},{4,6},{6,7},{7,5},{5,3},{3,1},{1,0},{8,10},{10,12},{12... | collective-permute-start | bytes 2359304 | tf_op jit(solution)/shard_map/ppermute | solution.py:34
  44.5 2.2 all_gather.16
  47.3 23.1 %collective-permute-done.8.refs_10_ = bf16[128,3072]{1,0:T(8,128)(2,1)} collective-permute-done((bf16[128,3072]{1,0:T(8,128)(2,1)}, bf16[128,3072]{1,0:T(8,128)(2,1)}, u32[]{:S(2)}, u32[]{:S(2)}) %collective-permute-start.8) | collective-permute-done | bytes 786464 | tf_op jit(solution)/shard_map/ppermute | solution.py:34
  70.4 2.5 collective-permute-start.9
  72.8 68.5 %all-gather.4.cloned.1.call-done = bf16[4,128,6144]{2,1,0:T(8,128)(2,1)} async-done(((bf16[4,128,768]{2,1,0:T(8,128)(2,1)}), bf16[4,128,6144]{2,1,0:T(8,128)(2,1)}) %all-gather.4.cloned.1.call-update) | async-done | bytes 6291472 | tf_op jit(solution)/shard_map/all_gather | solution.py:174
  141.3 4.2 %fusion = f32[4,128]{1,0:T(4,128)S(1)} fusion(bf16[4,128,6144]{2,1,0:T(8,128)(2,1)} %all-gather.4.cloned.1.call-done), kind=kLoop, calls=%fused_computation.3 | loop fusion | flops 9436672 | bytes 6293504 | tf_op jit(solution)/shard_map/reduce_sum | solution.py:20
  145.9 2.7 fusion.3
  148.6 6.3 %convolution_convert_fusion.1 = bf16[512,384]{1,0:T(8,128)(2,1)S(1)} fusion(bf16[512,6144]{1,0:T(8,128)(2,1)S(1)} %bitcast.147, bf16[6144,384]{0,1:T(8,128)(2,1)} %bitcast.148), kind=kOutput, calls=%fused_computation.29 | convolution fusion | flops 2416115712 | bytes 11403264 | tf_op jit(solution)/shard_map/dot_general | solution.py:198
  155.7 2.6 all_gather.17
  161.4 2.7 collective-permute-start.10
  165.5 16.4 %collective-permute-done.13.refs_15_ = bf16[128,3072]{1,0:T(8,128)(2,1)S(1)} collective-permute-done((bf16[128,3072]{1,0:T(8,128)(2,1)}, bf16[128,3072]{1,0:T(8,128)(2,1)S(1)}, u32[]{:S(2)}, u32[]{:S(2)}) %collective-permute-start.13) | collective-permute-done | bytes 786464 | tf_op jit(solution)/shard_map/ppermute | solution.py:38
  181.9 1.7 collective-permute-done.10.refs_12_
  184.7 1.4 collective-permute-start.4
  186.2 3.9 %collective-permute-done.refs_1_ = bf16[512,128]{1,0:T(8,128)(2,1)S(1)} collective-permute-done((bf16[512,128]{1,0:T(8,128)(2,1)S(1)}, bf16[512,128]{1,0:T(8,128)(2,1)S(1)}, u32[]{:S(2)}, u32[]{:S(2)}) %collective-permute-start) | collective-permute-done | bytes 131104 | tf_op jit(solution)/shard_map/ppermute | solution.py:34
  190.6 1.5 collective-permute-start.5
  192.1 3.1 collective-permute-done.1.refs_2_
  195.8 1.7 collective-permute-start.6
  197.5 2.7 collective-permute-done.2.refs_3_
  211.2 20.4 %shard_map.127 = f32[512,6144]{1,0:T(8,128)} custom-call(s32[1]{0:T(128)} %bitcast.5.span_ref, bf16[512,128]{1,0:T(8,128)(2,1)} %bitcast.155, bf16[512,128]{1,0:T(8,128)(2,1)} %copy-done.11, bf16[512,128]{1,0:T(8,128)(2,1)} %copy-done.13, bf16[512,128]{1,0:T(8,128)(2,1)} %collective-permute-done.2.refs_3_, bf16[512,128]{1,0:T(8,128)(2,1)} %collective-permute-done.3.refs_4_, ...), custom_call_target="tpu_custom_call" | custom-call | flops 6442450944 | bytes 26214400 | tf_op jit(solution)/shard_map/pallas_call | solution.py:111
  231.5 13.4 %multiply_reduce_fusion = (f32[4,128]{1,0:T(4,128)S(1)}, f32[4,128,6144]{2,1,0:T(8,128)}) fusion(f32[4,128,6144]{2,1,0:T(8,128)} %bitcast.137, f32[4,6144]{1,0:T(4,128)S(1)} %get-tuple-element.31, bf16[4,128,6144]{2,1,0:T(8,128)(2,1)} %all-gather.4.cloned.1.call-done), kind=kLoop, calls=%fused_computation.8 | loop fusion | flops 15728128 | bytes 31557632 | tf_op jit(solution)/shard_map/reduce_sum | solution.py:20
  245.0 10.0 %fusion.27 = bf16[4,128,512]{2,1,0:T(8,128)(2,1)S(1)} fusion(bf16[6144,512]{1,0:T(8,128)(2,1)} %all-gather.6.cloned.1.call-done, f32[4,128,6144]{2,1,0:T(8,128)} %get-tuple-element.6, f32[4,6144]{1,0:T(4,128)S(1)} %copy-done.15, f32[4,6144]{1,0:T(4,128)S(1)} %get-tuple-element.27, f32[4,128]{1,0:T(4,128)S(1)} %add_rsqrt_fusion), kind=kOutput, calls=%fused_computation.40 | convolution fusion | flops 3236167680 | bytes 19597312 | tf_op jit(solution)/shard_map/dot_general | solution.py:244
  255.1 6.4 %convolution_convert_fusion = bf16[4,128,6144]{2,1,0:T(8,128)(2,1)S(1)} fusion(bf16[4,128,512]{2,1,0:T(8,128)(2,1)S(1)} %fusion.27, bf16[512,6144]{1,0:T(8,128)(2,1)} %all-gather.8.cloned.1.call-done), kind=kOutput, calls=%fused_computation.9 | convolution fusion | flops 3224371200 | bytes 13107200 | tf_op jit(solution)/shard_map/dot_general | solution.py:246
  261.5 2.6 copy-done.3
  264.2 1.9 collective-permute-start.22
  267.7 5.0 %collective-permute-done.22 = bf16[512,384]{1,0:T(8,128)(2,1)S(1)} collective-permute-done((bf16[512,384]{1,0:T(8,128)(2,1)S(1)}, bf16[512,384]{1,0:T(8,128)(2,1)S(1)}, u32[]{:S(2)}, u32[]{:S(2)}) %collective-permute-start.22) | collective-permute-done | bytes 393248 | tf_op jit(solution)/shard_map/ppermute | solution.py:61
  272.7 1.7 collective-permute-done.29
  276.3 1.7 collective-permute-start.30
  279.2 5.1 %collective-permute-done.23 = bf16[512,384]{1,0:T(8,128)(2,1)S(1)} collective-permute-done((bf16[512,384]{1,0:T(8,128)(2,1)S(1)}, bf16[512,384]{1,0:T(8,128)(2,1)S(1)}, u32[]{:S(2)}, u32[]{:S(2)}) %collective-permute-start.23) | collective-permute-done | bytes 393248 | tf_op jit(solution)/shard_map/ppermute | solution.py:61
  284.3 1.3 add_convert_fusion.17
  286.4 1.6 collective-permute-start.31
  289.1 6.0 %collective-permute-done.24 = bf16[512,384]{1,0:T(8,128)(2,1)S(1)} collective-permute-done((bf16[512,384]{1,0:T(8,128)(2,1)S(1)}, bf16[512,384]{1,0:T(8,128)(2,1)S(1)}, u32[]{:S(2)}, u32[]{:S(2)}) %collective-permute-start.24) | collective-permute-done | bytes 393248 | tf_op jit(solution)/shard_map/ppermute | solution.py:61
  296.4 3.0 collective-permute-start.25
  300.8 6.5 %collective-permute-done.25 = bf16[512,384]{1,0:T(8,128)(2,1)S(1)} collective-permute-done((bf16[512,384]{1,0:T(8,128)(2,1)S(1)}, bf16[512,384]{1,0:T(8,128)(2,1)S(1)}, u32[]{:S(2)}, u32[]{:S(2)}) %collective-permute-start.25) | collective-permute-done | bytes 393248 | tf_op jit(solution)/shard_map/ppermute | solution.py:61
  307.3 4.1 %collective-permute-done.32 = bf16[512,384]{1,0:T(8,128)(2,1)S(1)} collective-permute-done((bf16[512,384]{1,0:T(8,128)(2,1)S(1)}, bf16[512,384]{1,0:T(8,128)(2,1)S(1)}, u32[]{:S(2)}, u32[]{:S(2)}) %collective-permute-start.32) | collective-permute-done | bytes 393248 | tf_op jit(solution)/shard_map/ppermute | solution.py:63
  312.7 2.4 collective-permute-start.26
  316.3 8.2 %collective-permute-done.26 = bf16[512,384]{1,0:T(8,128)(2,1)S(1)} collective-permute-done((bf16[512,384]{1,0:T(8,128)(2,1)S(1)}, bf16[512,384]{1,0:T(8,128)(2,1)S(1)}, u32[]{:S(2)}, u32[]{:S(2)}) %collective-permute-start.26) | collective-permute-done | bytes 393248 | tf_op jit(solution)/shard_map/ppermute | solution.py:61
  324.5 1.7 collective-permute-done.33
  326.2 1.3 add_convert_fusion.14
  328.1 1.5 collective-permute-start.34
  330.3 7.7 %collective-permute-done.27 = bf16[512,384]{1,0:T(8,128)(2,1)S(1)} collective-permute-done((bf16[512,384]{1,0:T(8,128)(2,1)S(1)}, bf16[512,384]{1,0:T(8,128)(2,1)S(1)}, u32[]{:S(2)}, u32[]{:S(2)}) %collective-permute-start.27) | collective-permute-done | bytes 393248 | tf_op jit(solution)/shard_map/ppermute | solution.py:61
  338.4 1.4 add_convert_fusion.13
  340.4 1.5 collective-permute-start.35
  342.5 5.2 %collective-permute-done.28 = bf16[512,384]{1,0:T(8,128)(2,1)S(1)} collective-permute-done((bf16[512,384]{1,0:T(8,128)(2,1)S(1)}, bf16[512,384]{1,0:T(8,128)(2,1)S(1)}, u32[]{:S(2)}, u32[]{:S(2)}) %collective-permute-start.28) | collective-permute-done | bytes 393248 | tf_op jit(solution)/shard_map/ppermute | solution.py:61
  348.3 1.4 convert_add_fusion.2
  349.8 2.6 add_convert_fusion.2
  (128 shorter events, 21.5 us)
Async XLA Ops:
  6.5 134.8 %all-gather.4.cloned.1.call-start = ((), (), s32[]{:S(2)}) async-start(), calls=%async_computation | async-start | bytes 7077888 | tf_op jit(solution)/shard_map/all_gather | solution.py:174
  7.3 237.7 %all-gather.6.cloned.1.call-start = ((), (), s32[]{:S(2)}) async-start(), calls=%async_computation.1 | async-start | bytes 9437184 | tf_op jit(solution)/shard_map/all_gather | solution.py:184
  8.0 247.1 %all-gather.8.cloned.1.call-start = ((), (), s32[]{:S(2)}) async-start(), calls=%async_computation.2 | async-start | bytes 9437184 | tf_op jit(solution)/shard_map/all_gather | solution.py:185
  8.2 27.5 %collective-permute-start.7 = (bf16[128,3072]{1,0:T(8,128)(2,1)S(1)}, bf16[128,3072]{1,0:T(8,128)(2,1)}, u32[]{:S(2)}, u32[]{:S(2)}) collective-permute-start(bf16[128,3072]{1,0:T(8,128)(2,1)S(1)} %constant_dynamic-slice_fusion.2.refs_8_), channel_id=1, source_target_pairs={{0,2},{2,4},{4,6},{6,7},{7,5},{5,3},{3,1},{1,0},{8,10},{10,12},{12... | collective-permute-start | bytes 2359304 | tf_op jit(solution)/shard_map/ppermute | solution.py:34
  11.3 35.6 %collective-permute-start.11 = (bf16[128,3072]{1,0:T(8,128)(2,1)S(1)}, bf16[128,3072]{1,0:T(8,128)(2,1)}, u32[]{:S(2)}, u32[]{:S(2)}) collective-permute-start(bf16[128,3072]{1,0:T(8,128)(2,1)S(1)} %constant_dynamic-slice_fusion.2.refs_8_), channel_id=1, source_target_pairs={{0,1},{2,0},{4,2},{6,4},{7,6},{5,7},{3,5},{1,3},{8,9},{10,8},{12,1... | collective-permute-start | bytes 2359304 | tf_op jit(solution)/shard_map/ppermute | solution.py:38
  11.3 149.1 %collective-permute-start.14 = (bf16[128,3072]{1,0:T(8,128)(2,1)S(1)}, bf16[128,3072]{1,0:T(8,128)(2,1)}, u32[]{:S(2)}, u32[]{:S(2)}) collective-permute-start(bf16[128,3072]{1,0:T(8,128)(2,1)S(1)} %constant_dynamic-slice_fusion.2.refs_8_), channel_id=1, source_target_pairs={{0,8},{8,0},{1,9},{9,1},{2,10},{10,2},{3,11},{11,3},{4,12},{12,4},... | collective-permute-start | bytes 2359304 | tf_op jit(solution)/shard_map/ppermute | solution.py:182
  11.3 33.1 %copy-start.9 = (bf16[4,128,2,128]{3,2,1,0:T(2,128)(2,1)S(1)}, bf16[4,128,2,128]{3,2,1,0:T(2,128)(2,1)}, u32[]{:S(2)}) copy-start(bf16[4,128,2,128]{3,2,1,0:T(2,128)(2,1)} %param.18) | copy-start | bytes 786436
  35.7 34.6 %collective-permute-start.8 = (bf16[128,3072]{1,0:T(8,128)(2,1)}, bf16[128,3072]{1,0:T(8,128)(2,1)}, u32[]{:S(2)}, u32[]{:S(2)}) collective-permute-start(bf16[128,3072]{1,0:T(8,128)(2,1)} %collective-permute-done.7.refs_9_), channel_id=1, source_target_pairs={{0,2},{2,4},{4,6},{6,7},{7,5},{5,3},{3,1},{1,0},{8,10},{10,12},{12... | collective-permute-start | bytes 2359304 | tf_op jit(solution)/shard_map/ppermute | solution.py:34
  46.7 114.6 %collective-permute-start.15 = (bf16[128,3072]{1,0:T(8,128)(2,1)}, bf16[128,3072]{1,0:T(8,128)(2,1)}, u32[]{:S(2)}, u32[]{:S(2)}) collective-permute-start(bf16[128,3072]{1,0:T(8,128)(2,1)} %collective-permute-done.7.refs_9_), channel_id=1, source_target_pairs={{0,8},{8,0},{1,9},{9,1},{2,10},{10,2},{3,11},{11,3},{4,12},{12,4},... | collective-permute-start | bytes 2359304 | tf_op jit(solution)/shard_map/ppermute | solution.py:182
  46.9 113.7 %collective-permute-start.12 = (bf16[128,3072]{1,0:T(8,128)(2,1)}, bf16[128,3072]{1,0:T(8,128)(2,1)}, u32[]{:S(2)}, u32[]{:S(2)}) collective-permute-start(bf16[128,3072]{1,0:T(8,128)(2,1)} %collective-permute-done.11.refs_13_), channel_id=1, source_target_pairs={{0,1},{2,0},{4,2},{6,4},{7,6},{5,7},{3,5},{1,3},{8,9},{10,8},{12,1... | collective-permute-start | bytes 2359304 | tf_op jit(solution)/shard_map/ppermute | solution.py:38
  46.9 118.5 %collective-permute-start.19 = (bf16[128,3072]{1,0:T(8,128)(2,1)}, bf16[128,3072]{1,0:T(8,128)(2,1)}, u32[]{:S(2)}, u32[]{:S(2)}) collective-permute-start(bf16[128,3072]{1,0:T(8,128)(2,1)} %collective-permute-done.11.refs_13_), channel_id=1, source_target_pairs={{0,8},{8,0},{1,9},{9,1},{2,10},{10,2},{3,11},{11,3},{4,12},{12,4},... | collective-permute-start | bytes 2359304 | tf_op jit(solution)/shard_map/ppermute | solution.py:182
  70.4 91.0 %collective-permute-start.9 = (bf16[128,3072]{1,0:T(8,128)(2,1)}, bf16[128,3072]{1,0:T(8,128)(2,1)}, u32[]{:S(2)}, u32[]{:S(2)}) collective-permute-start(bf16[128,3072]{1,0:T(8,128)(2,1)} %collective-permute-done.8.refs_10_), channel_id=1, source_target_pairs={{0,2},{2,4},{4,6},{6,7},{7,5},{5,3},{3,1},{1,0},{8,10},{10,12},{12... | collective-permute-start | bytes 2359304 | tf_op jit(solution)/shard_map/ppermute | solution.py:34
  159.6 41.1 %copy-start.19 = (s32[8]{0:T(128)S(1)}, s32[8]{0:T(128)}, u32[]{:S(2)}) copy-start(s32[8]{0:T(128)} %constant.221.clone) | copy-start | bytes 100
  159.6 49.6 %copy-start.14 = (s32[8]{0:T(128)S(1)}, s32[8]{0:T(128)}, u32[]{:S(2)}) copy-start(s32[8]{0:T(128)} %constant.222.clone) | copy-start | bytes 100
  160.4 23.7 %collective-permute-start.16 = (bf16[128,3072]{1,0:T(8,128)(2,1)}, bf16[128,3072]{1,0:T(8,128)(2,1)S(1)}, u32[]{:S(2)}, u32[]{:S(2)}) collective-permute-start(bf16[128,3072]{1,0:T(8,128)(2,1)} %collective-permute-done.8.refs_10_), channel_id=1, source_target_pairs={{0,8},{8,0},{1,9},{9,1},{2,10},{10,2},{3,11},{11,3},{4,12},{12,4},... | collective-permute-start | bytes 2359304 | tf_op jit(solution)/shard_map/ppermute | solution.py:182
  160.6 21.4 %collective-permute-start.13 = (bf16[128,3072]{1,0:T(8,128)(2,1)}, bf16[128,3072]{1,0:T(8,128)(2,1)S(1)}, u32[]{:S(2)}, u32[]{:S(2)}) collective-permute-start(bf16[128,3072]{1,0:T(8,128)(2,1)} %collective-permute-done.12.refs_14_), channel_id=1, source_target_pairs={{0,1},{2,0},{4,2},{6,4},{7,6},{5,7},{3,5},{1,3},{8,9},{10,8},{12,1... | collective-permute-start | bytes 2359304 | tf_op jit(solution)/shard_map/ppermute | solution.py:38
  161.3 23.4 %collective-permute-start.20 = (bf16[128,3072]{1,0:T(8,128)(2,1)}, bf16[128,3072]{1,0:T(8,128)(2,1)S(1)}, u32[]{:S(2)}, u32[]{:S(2)}) collective-permute-start(bf16[128,3072]{1,0:T(8,128)(2,1)} %collective-permute-done.12.refs_14_), channel_id=1, source_target_pairs={{0,8},{8,0},{1,9},{9,1},{2,10},{10,2},{3,11},{11,3},{4,12},{12,4},... | collective-permute-start | bytes 2359304 | tf_op jit(solution)/shard_map/ppermute | solution.py:182
  161.4 22.2 %collective-permute-start.10 = (bf16[128,3072]{1,0:T(8,128)(2,1)}, bf16[128,3072]{1,0:T(8,128)(2,1)}, u32[]{:S(2)}, u32[]{:S(2)}) collective-permute-start(bf16[128,3072]{1,0:T(8,128)(2,1)} %collective-permute-done.9.refs_11_), channel_id=1, source_target_pairs={{0,2},{2,4},{4,6},{6,7},{7,5},{5,3},{3,1},{1,0},{8,10},{10,12},{12... | collective-permute-start | bytes 2359304 | tf_op jit(solution)/shard_map/ppermute | solution.py:34
  165.4 45.6 %collective-permute-start.17 = (bf16[128,3072]{1,0:T(8,128)(2,1)}, bf16[128,3072]{1,0:T(8,128)(2,1)}, u32[]{:S(2)}, u32[]{:S(2)}) collective-permute-start(bf16[128,3072]{1,0:T(8,128)(2,1)} %collective-permute-done.9.refs_11_), channel_id=1, source_target_pairs={{0,8},{8,0},{1,9},{9,1},{2,10},{10,2},{3,11},{11,3},{4,12},{12,4},... | collective-permute-start | bytes 2359304 | tf_op jit(solution)/shard_map/ppermute | solution.py:182
  181.9 29.2 %copy-start.6 = (bf16[128,3072]{1,0:T(8,128)(2,1)}, bf16[128,3072]{1,0:T(8,128)(2,1)S(1)}, u32[]{:S(2)}) copy-start(bf16[128,3072]{1,0:T(8,128)(2,1)S(1)} %collective-permute-done.13.refs_15_) | copy-start | bytes 2359300
  181.9 29.2 %collective-permute-start.21 = (bf16[128,3072]{1,0:T(8,128)(2,1)S(1)}, bf16[128,3072]{1,0:T(8,128)(2,1)}, u32[]{:S(2)}, u32[]{:S(2)}) collective-permute-start(bf16[128,3072]{1,0:T(8,128)(2,1)S(1)} %collective-permute-done.13.refs_15_), channel_id=1, source_target_pairs={{0,8},{8,0},{1,9},{9,1},{2,10},{10,2},{3,11},{11,3},{4,12},{12,4},... | collective-permute-start | bytes 2359304 | tf_op jit(solution)/shard_map/ppermute | solution.py:182
  183.6 27.5 %collective-permute-start.18 = (bf16[128,3072]{1,0:T(8,128)(2,1)}, bf16[128,3072]{1,0:T(8,128)(2,1)}, u32[]{:S(2)}, u32[]{:S(2)}) collective-permute-start(bf16[128,3072]{1,0:T(8,128)(2,1)} %collective-permute-done.10.refs_12_), channel_id=1, source_target_pairs={{0,8},{8,0},{1,9},{9,1},{2,10},{10,2},{3,11},{11,3},{4,12},{12,4},... | collective-permute-start | bytes 2359304 | tf_op jit(solution)/shard_map/ppermute | solution.py:182
  184.0 27.1 %copy-start.10 = (bf16[128,4,128]{0,2,1:T(8,128)(2,1)}, bf16[128,4,128]{0,2,1:T(8,128)(2,1)S(1)}, u32[]{:S(2)}) copy-start(bf16[128,4,128]{0,2,1:T(8,128)(2,1)S(1)} %fusion.17) | copy-start | bytes 393220
  184.1 27.1 %copy-start.5 = (bf16[128,3072]{1,0:T(8,128)(2,1)}, bf16[128,3072]{1,0:T(8,128)(2,1)S(1)}, u32[]{:S(2)}) copy-start(bf16[128,3072]{1,0:T(8,128)(2,1)S(1)} %collective-permute-done.16.refs_18_) | copy-start | bytes 2359300
  184.1 6.0 %collective-permute-start = (bf16[512,128]{1,0:T(8,128)(2,1)S(1)}, bf16[512,128]{1,0:T(8,128)(2,1)S(1)}, u32[]{:S(2)}, u32[]{:S(2)}) collective-permute-start(bf16[512,128]{1,0:T(8,128)(2,1)S(1)} %bitcast.153), channel_id=1, source_target_pairs={{0,2},{2,4},{4,6},{6,7},{7,5},{5,3},{3,1},{1,0},{8,10},{10,12},{12... | collective-permute-start | bytes 393224 | tf_op jit(solution)/shard_map/ppermute | solution.py:34
  184.7 26.4 %copy-start.7 = (bf16[128,3072]{1,0:T(8,128)(2,1)}, bf16[128,3072]{1,0:T(8,128)(2,1)S(1)}, u32[]{:S(2)}) copy-start(bf16[128,3072]{1,0:T(8,128)(2,1)S(1)} %collective-permute-done.20.refs_22_) | copy-start | bytes 2359300
  184.7 5.8 %collective-permute-start.4 = (bf16[512,128]{1,0:T(8,128)(2,1)S(1)}, bf16[512,128]{1,0:T(8,128)(2,1)S(1)}, u32[]{:S(2)}, u32[]{:S(2)}) collective-permute-start(bf16[512,128]{1,0:T(8,128)(2,1)S(1)} %bitcast.154), channel_id=1, source_target_pairs={{0,1},{2,0},{4,2},{6,4},{7,6},{5,7},{3,5},{1,3},{8,9},{10,8},{12,1... | collective-permute-start | bytes 393224 | tf_op jit(solution)/shard_map/ppermute | solution.py:38
  190.0 21.1 %copy-start.11 = (bf16[512,128]{1,0:T(8,128)(2,1)}, bf16[512,128]{1,0:T(8,128)(2,1)S(1)}, u32[]{:S(2)}) copy-start(bf16[512,128]{1,0:T(8,128)(2,1)S(1)} %collective-permute-done.refs_1_) | copy-start | bytes 393220
  190.0 5.1 %collective-permute-start.1 = (bf16[512,128]{1,0:T(8,128)(2,1)S(1)}, bf16[512,128]{1,0:T(8,128)(2,1)S(1)}, u32[]{:S(2)}, u32[]{:S(2)}) collective-permute-start(bf16[512,128]{1,0:T(8,128)(2,1)S(1)} %collective-permute-done.refs_1_), channel_id=1, source_target_pairs={{0,2},{2,4},{4,6},{6,7},{7,5},{5,3},{3,1},{1,0},{8,10},{10,12},{12... | collective-permute-start | bytes 393224 | tf_op jit(solution)/shard_map/ppermute | solution.py:34
  190.6 5.1 %collective-permute-start.5 = (bf16[512,128]{1,0:T(8,128)(2,1)S(1)}, bf16[512,128]{1,0:T(8,128)(2,1)}, u32[]{:S(2)}, u32[]{:S(2)}) collective-permute-start(bf16[512,128]{1,0:T(8,128)(2,1)S(1)} %collective-permute-done.4.refs_5_), channel_id=1, source_target_pairs={{0,1},{2,0},{4,2},{6,4},{7,6},{5,7},{3,5},{1,3},{8,9},{10,8},{12,1... | collective-permute-start | bytes 393224 | tf_op jit(solution)/shard_map/ppermute | solution.py:38
  195.2 5.1 %collective-permute-start.2 = (bf16[512,128]{1,0:T(8,128)(2,1)S(1)}, bf16[512,128]{1,0:T(8,128)(2,1)}, u32[]{:S(2)}, u32[]{:S(2)}) collective-permute-start(bf16[512,128]{1,0:T(8,128)(2,1)S(1)} %collective-permute-done.1.refs_2_), channel_id=1, source_target_pairs={{0,2},{2,4},{4,6},{6,7},{7,5},{5,3},{3,1},{1,0},{8,10},{10,12},{12... | collective-permute-start | bytes 393224 | tf_op jit(solution)/shard_map/ppermute | solution.py:34
  195.8 15.3 %collective-permute-start.6 = (bf16[512,128]{1,0:T(8,128)(2,1)}, bf16[512,128]{1,0:T(8,128)(2,1)}, u32[]{:S(2)}, u32[]{:S(2)}) collective-permute-start(bf16[512,128]{1,0:T(8,128)(2,1)} %collective-permute-done.5.refs_6_), channel_id=1, source_target_pairs={{0,1},{2,0},{4,2},{6,4},{7,6},{5,7},{3,5},{1,3},{8,9},{10,8},{12,1... | collective-permute-start | bytes 393224 | tf_op jit(solution)/shard_map/ppermute | solution.py:38
  200.2 10.9 %collective-permute-start.3 = (bf16[512,128]{1,0:T(8,128)(2,1)}, bf16[512,128]{1,0:T(8,128)(2,1)}, u32[]{:S(2)}, u32[]{:S(2)}) collective-permute-start(bf16[512,128]{1,0:T(8,128)(2,1)} %collective-permute-done.2.refs_3_), channel_id=1, source_target_pairs={{0,2},{2,4},{4,6},{6,7},{7,5},{5,3},{3,1},{1,0},{8,10},{10,12},{12... | collective-permute-start | bytes 393224 | tf_op jit(solution)/shard_map/ppermute | solution.py:34
  264.2 8.4 %collective-permute-start.22 = (bf16[512,384]{1,0:T(8,128)(2,1)S(1)}, bf16[512,384]{1,0:T(8,128)(2,1)S(1)}, u32[]{:S(2)}, u32[]{:S(2)}) collective-permute-start(bf16[512,384]{1,0:T(8,128)(2,1)S(1)} %get-tuple-element.21), channel_id=1, source_target_pairs={{0,2},{2,4},{4,6},{6,7},{7,5},{5,3},{3,1},{1,0},{8,10},{10,12},{12... | collective-permute-start | bytes 1179656 | tf_op jit(solution)/shard_map/ppermute | solution.py:61
  266.2 8.2 %collective-permute-start.29 = (bf16[512,384]{1,0:T(8,128)(2,1)S(1)}, bf16[512,384]{1,0:T(8,128)(2,1)S(1)}, u32[]{:S(2)}, u32[]{:S(2)}) collective-permute-start(bf16[512,384]{1,0:T(8,128)(2,1)S(1)} %get-tuple-element.22), channel_id=1, source_target_pairs={{0,1},{2,0},{4,2},{6,4},{7,6},{5,7},{3,5},{1,3},{8,9},{10,8},{12,1... | collective-permute-start | bytes 1179656 | tf_op jit(solution)/shard_map/ppermute | solution.py:63
  275.7 8.6 %collective-permute-start.23 = (bf16[512,384]{1,0:T(8,128)(2,1)S(1)}, bf16[512,384]{1,0:T(8,128)(2,1)S(1)}, u32[]{:S(2)}, u32[]{:S(2)}) collective-permute-start(bf16[512,384]{1,0:T(8,128)(2,1)S(1)} %get-tuple-element.19), channel_id=1, source_target_pairs={{0,2},{2,4},{4,6},{6,7},{7,5},{5,3},{3,1},{1,0},{8,10},{10,12},{12... | collective-permute-start | bytes 1179656 | tf_op jit(solution)/shard_map/ppermute | solution.py:61
  276.3 8.0 %collective-permute-start.30 = (bf16[512,384]{1,0:T(8,128)(2,1)S(1)}, bf16[512,384]{1,0:T(8,128)(2,1)S(1)}, u32[]{:S(2)}, u32[]{:S(2)}) collective-permute-start(bf16[512,384]{1,0:T(8,128)(2,1)S(1)} %get-tuple-element.20), channel_id=1, source_target_pairs={{0,1},{2,0},{4,2},{6,4},{7,6},{5,7},{3,5},{1,3},{8,9},{10,8},{12,1... | collective-permute-start | bytes 1179656 | tf_op jit(solution)/shard_map/ppermute | solution.py:63
  285.6 9.5 %collective-permute-start.24 = (bf16[512,384]{1,0:T(8,128)(2,1)S(1)}, bf16[512,384]{1,0:T(8,128)(2,1)S(1)}, u32[]{:S(2)}, u32[]{:S(2)}) collective-permute-start(bf16[512,384]{1,0:T(8,128)(2,1)S(1)} %get-tuple-element.17), channel_id=1, source_target_pairs={{0,2},{2,4},{4,6},{6,7},{7,5},{5,3},{3,1},{1,0},{8,10},{10,12},{12... | collective-permute-start | bytes 1179656 | tf_op jit(solution)/shard_map/ppermute | solution.py:61
  286.4 8.8 %collective-permute-start.31 = (bf16[512,384]{1,0:T(8,128)(2,1)S(1)}, bf16[512,384]{1,0:T(8,128)(2,1)S(1)}, u32[]{:S(2)}, u32[]{:S(2)}) collective-permute-start(bf16[512,384]{1,0:T(8,128)(2,1)S(1)} %get-tuple-element.18), channel_id=1, source_target_pairs={{0,1},{2,0},{4,2},{6,4},{7,6},{5,7},{3,5},{1,3},{8,9},{10,8},{12,1... | collective-permute-start | bytes 1179656 | tf_op jit(solution)/shard_map/ppermute | solution.py:63
  296.4 10.8 %collective-permute-start.25 = (bf16[512,384]{1,0:T(8,128)(2,1)S(1)}, bf16[512,384]{1,0:T(8,128)(2,1)S(1)}, u32[]{:S(2)}, u32[]{:S(2)}) collective-permute-start(bf16[512,384]{1,0:T(8,128)(2,1)S(1)} %get-tuple-element.15), channel_id=1, source_target_pairs={{0,2},{2,4},{4,6},{6,7},{7,5},{5,3},{3,1},{1,0},{8,10},{10,12},{12... | collective-permute-start | bytes 1179656 | tf_op jit(solution)/shard_map/ppermute | solution.py:61
  299.4 11.9 %collective-permute-start.32 = (bf16[512,384]{1,0:T(8,128)(2,1)S(1)}, bf16[512,384]{1,0:T(8,128)(2,1)S(1)}, u32[]{:S(2)}, u32[]{:S(2)}) collective-permute-start(bf16[512,384]{1,0:T(8,128)(2,1)S(1)} %get-tuple-element.16), channel_id=1, source_target_pairs={{0,1},{2,0},{4,2},{6,4},{7,6},{5,7},{3,5},{1,3},{8,9},{10,8},{12,1... | collective-permute-start | bytes 1179656 | tf_op jit(solution)/shard_map/ppermute | solution.py:63
  312.7 11.8 %collective-permute-start.26 = (bf16[512,384]{1,0:T(8,128)(2,1)S(1)}, bf16[512,384]{1,0:T(8,128)(2,1)S(1)}, u32[]{:S(2)}, u32[]{:S(2)}) collective-permute-start(bf16[512,384]{1,0:T(8,128)(2,1)S(1)} %get-tuple-element.13), channel_id=1, source_target_pairs={{0,2},{2,4},{4,6},{6,7},{7,5},{5,3},{3,1},{1,0},{8,10},{10,12},{12... | collective-permute-start | bytes 1179656 | tf_op jit(solution)/shard_map/ppermute | solution.py:61
  315.1 11.1 %collective-permute-start.33 = (bf16[512,384]{1,0:T(8,128)(2,1)S(1)}, bf16[512,384]{1,0:T(8,128)(2,1)S(1)}, u32[]{:S(2)}, u32[]{:S(2)}) collective-permute-start(bf16[512,384]{1,0:T(8,128)(2,1)S(1)} %get-tuple-element.14), channel_id=1, source_target_pairs={{0,1},{2,0},{4,2},{6,4},{7,6},{5,7},{3,5},{1,3},{8,9},{10,8},{12,1... | collective-permute-start | bytes 1179656 | tf_op jit(solution)/shard_map/ppermute | solution.py:63
  327.5 10.4 %collective-permute-start.27 = (bf16[512,384]{1,0:T(8,128)(2,1)S(1)}, bf16[512,384]{1,0:T(8,128)(2,1)S(1)}, u32[]{:S(2)}, u32[]{:S(2)}) collective-permute-start(bf16[512,384]{1,0:T(8,128)(2,1)S(1)} %get-tuple-element.11), channel_id=1, source_target_pairs={{0,2},{2,4},{4,6},{6,7},{7,5},{5,3},{3,1},{1,0},{8,10},{10,12},{12... | collective-permute-start | bytes 1179656 | tf_op jit(solution)/shard_map/ppermute | solution.py:61
  328.1 10.2 %collective-permute-start.34 = (bf16[512,384]{1,0:T(8,128)(2,1)S(1)}, bf16[512,384]{1,0:T(8,128)(2,1)}, u32[]{:S(2)}, u32[]{:S(2)}) collective-permute-start(bf16[512,384]{1,0:T(8,128)(2,1)S(1)} %get-tuple-element.12), channel_id=1, source_target_pairs={{0,1},{2,0},{4,2},{6,4},{7,6},{5,7},{3,5},{1,3},{8,9},{10,8},{12,1... | collective-permute-start | bytes 1179656 | tf_op jit(solution)/shard_map/ppermute | solution.py:63
  330.2 22.2 %copy-start.1 = (bf16[128,6144]{1,0:T(8,128)(2,1)S(1)}, bf16[128,6144]{1,0:T(8,128)(2,1)}, u32[]{:S(2)}) copy-start(bf16[128,6144]{1,0:T(8,128)(2,1)} %param.21) | copy-start | bytes 4718596
  339.8 7.8 %collective-permute-start.28 = (bf16[512,384]{1,0:T(8,128)(2,1)S(1)}, bf16[512,384]{1,0:T(8,128)(2,1)S(1)}, u32[]{:S(2)}, u32[]{:S(2)}) collective-permute-start(bf16[512,384]{1,0:T(8,128)(2,1)S(1)} %get-tuple-element.9), channel_id=1, source_target_pairs={{0,2},{2,4},{4,6},{6,7},{7,5},{5,3},{3,1},{1,0},{8,10},{10,12},{12... | collective-permute-start | bytes 1179656 | tf_op jit(solution)/shard_map/ppermute | solution.py:61
  340.4 7.9 %collective-permute-start.35 = (bf16[512,384]{1,0:T(8,128)(2,1)S(1)}, bf16[512,384]{1,0:T(8,128)(2,1)}, u32[]{:S(2)}, u32[]{:S(2)}) collective-permute-start(bf16[512,384]{1,0:T(8,128)(2,1)S(1)} %get-tuple-element.10), channel_id=1, source_target_pairs={{0,1},{2,0},{4,2},{6,4},{7,6},{5,7},{3,5},{1,3},{8,9},{10,8},{12,1... | collective-permute-start | bytes 1179656 | tf_op jit(solution)/shard_map/ppermute | solution.py:63
  (11 other events, 96.8 us)
Sparse Core Ops, SparseCore 0:
  9.6 131.6 all-gather.3
  142.8 17.3 all-gather.5
  161.8 18.3 all-gather.7

commit v7 on v6

--- a/solution.py
+++ b/solution.py
@@ -171,10 +171,21 @@
     local_count = hidden_in.shape[0]
     row_count = hidden_in.shape[1]
     token_count = local_count * row_count
-    gathered = lax.all_gather(hidden_in, "tp", axis=2, tiled=True).astype(jnp.float32)
     gather_weights = (
         tp_count * w_out.size * w_out.dtype.itemsize <= WEIGHT_GATHER_BYTES and span_count == 2
     )
+    if gather_weights:
+        cycle = snake_cycle(tp_count)
+        position = jnp.array([cycle.index(t) for t in range(tp_count)], jnp.int32)[tp_rank]
+        steps = list(range(tp_count // 2 + 1)) + [-k for k in range(1, (tp_count - 1) // 2 + 1)]
+        owners = jnp.array(cycle, jnp.int32)
+        gathered = jnp.zeros(hidden_in.shape[:2] + (model_width,), hidden_in.dtype)
+        for step, piece in zip(steps, ring_gather(hidden_in, "tp", tp_count)):
+            owner = owners[(position - step + tp_count) % tp_count]
+            gathered = lax.dynamic_update_slice_in_dim(gathered, piece, owner * share_width, 2)
+        gathered = gathered.astype(jnp.float32)
+    else:
+        gathered = lax.all_gather(hidden_in, "tp", axis=2, tiled=True).astype(jnp.float32)
     if gather_weights:
         column_part = model_width // span_count
         w_out_part = lax.dynamic_slice_in_dim(w_out, span_index * column_part, column_part, 1)

time: 360 us -> 334 us (0.928)
  waiting for transfers between devices: 188 us -> 158 us
  local copies, waits for them, and re-layouts: 13.1 us -> 21.7 us
    all_gather x1 -> x0, waiting for transfers between devices: 68.5 us -> none  [local(): lax.all_gather(hidden_in, 'tp', axis=2, tiled=True).astype(jnp.float32)]
    ppermute x8 -> x12, waiting for transfers between devices: 49.9 us -> 79.3 us  [ring_gather(): forward = lax.ppermute(forward, axis_name, ahead)]
    ppermute x7, waiting for transfers between devices: 43.6 us -> 51.2 us  [ring_reduce_scatter(): lax.ppermute(forward.astype(jnp.bfloat16), axis_name, ahead)]
    dynamic_update_slice x0 -> x8, local copies, waits for them, and re-layouts: none -> 7.58 us  [local(): lax.dynamic_update_slice_in_dim(gathered, piece, owner * share_width, 2)]
    ppermute x6 -> x9, waiting for transfers between devices: 16.4 us -> 21.1 us  [ring_gather(): backward = lax.ppermute(backward, axis_name, behind)]
    ppermute x7, starting transfers between devices: 9.93 us -> 6.26 us  [ring_reduce_scatter(): lax.ppermute(forward.astype(jnp.bfloat16), axis_name, ahead)]
    ppermute x8 -> x12, starting transfers between devices: 18.8 us -> 21.6 us  [ring_gather(): forward = lax.ppermute(forward, axis_name, ahead)]
    unnamed x47 -> x55, local copies, waits for them, and re-layouts: 10.3 us -> 10.5 us
  transfers between devices with their start and end apart: 39 -> 45, of which waited for: 20 -> 24; matrix products, arithmetic and copies ran while one was open for 14% -> 17% of each run, Pallas kernels for 6% -> 6%
where the time goes in v7:
time: 334 us; the launch traced here: 333 us
  waiting for transfers between devices  158 us (47%)
  starting transfers between devices  40 us (12%)
  other arithmetic  31.7 us (9%)
  between operations  31.3 us (9%)
  matrix products  24.8 us (7%)
  local copies, waits for them, and re-layouts  21.7 us (6%)
  Pallas kernels  20.4 us (6%)
  blocking collectives  4.54 us (1%)
    ppermute x12, waiting for transfers between devices, ring_gather(): forward = lax.ppermute(forward, axis_name, ahead)  79.3 us
    ppermute x7, waiting for transfers between devices, ring_reduce_scatter(): lax.ppermute(forward.astype(jnp.bfloat16), axis_name, ahead)  51.2 us
    ppermute x12, starting transfers between devices, ring_gather(): forward = lax.ppermute(forward, axis_name, ahead)  21.6 us
    ppermute x9, waiting for transfers between devices, ring_gather(): backward = lax.ppermute(backward, axis_name, behind)  21.1 us
    pallas_call x1, Pallas kernels, grouped_out_proj(): pl.pallas_call(functools.partial(out_proj_kernel, group_count, tiles_per_...  20.4 us
    reduce_sum x2, other arithmetic, normalize(): jnp.mean(values * values, axis=-1, keepdims=True) + EPSILON  14.7 us
    unnamed x55, local copies, waits for them, and re-layouts  10.5 us
    dot_general x1, matrix products, local(): pre_act = jnp.dot(mlp_in, up_full, preferred_element_type=jnp.float32)  10 us
  transfers between devices with their start and end apart: 45, of which 24 were waited for; matrix products, arithmetic and copies ran while one was open for 17% of the time, Pallas kernels for 6%

profile of v7, /device:TPU:0, one launch (start us, length us, event | category | flops | bytes accessed | tf_op | source)
XLA Modules:
  0.0 332.9 jit_solution(15674647549351645318)
XLA Ops:
  7.4 3.1 collective-permute-start
  10.5 2.1 collective-permute-start.14
  14.4 14.7 %collective-permute-done = bf16[4,128,768]{2,1,0:T(8,128)(2,1)} collective-permute-done((bf16[4,128,768]{2,1,0:T(8,128)(2,1)}, bf16[4,128,768]{2,1,0:T(8,128)(2,1)}, u32[]{:S(2)}, u32[]{:S(2)}) %collective-permute-start) | collective-permute-done | bytes 786464 | tf_op jit(solution)/shard_map/ppermute | solution.py:34
  29.1 2.1 collective-permute-start.1
  31.5 30.3 %collective-permute-done.1 = bf16[4,128,768]{2,1,0:T(8,128)(2,1)S(1)} collective-permute-done((bf16[4,128,768]{2,1,0:T(8,128)(2,1)}, bf16[4,128,768]{2,1,0:T(8,128)(2,1)S(1)}, u32[]{:S(2)}, u32[]{:S(2)}) %collective-permute-start.1) | collective-permute-done | bytes 786464 | tf_op jit(solution)/shard_map/ppermute | solution.py:34
  61.8 1.8 collective-permute-start.2
  65.2 2.2 all_gather.12
  67.5 13.2 %collective-permute-done.2 = bf16[4,128,768]{2,1,0:T(8,128)(2,1)} collective-permute-done((bf16[4,128,768]{2,1,0:T(8,128)(2,1)S(1)}, bf16[4,128,768]{2,1,0:T(8,128)(2,1)}, u32[]{:S(2)}, u32[]{:S(2)}) %collective-permute-start.2) | collective-permute-done | bytes 786464 | tf_op jit(solution)/shard_map/ppermute | solution.py:34
  80.7 1.5 collective-permute-start.3
  95.2 6.8 %copy.30 = bf16[6144,3,128]{0,2,1:T(8,128)(2,1)} copy(bf16[6144,3,128]{2,0,1:T(8,128)(2,1)} %param.22) | data formatting | bytes 9437184 | tf_op args[7]
  103.0 1.6 collective-permute-start.15
  113.2 7.4 %collective-permute-done.15.refs_10_ = bf16[128,3072]{1,0:T(8,128)(2,1)} collective-permute-done((bf16[128,3072]{1,0:T(8,128)(2,1)}, bf16[128,3072]{1,0:T(8,128)(2,1)}, u32[]{:S(2)}, u32[]{:S(2)}) %collective-permute-start.15) | collective-permute-done | bytes 786464 | tf_op jit(solution)/shard_map/ppermute | solution.py:34
  120.6 4.7 %collective-permute-done.6 = bf16[4,128,768]{2,1,0:T(8,128)(2,1)S(1)} collective-permute-done((bf16[4,128,768]{2,1,0:T(8,128)(2,1)}, bf16[4,128,768]{2,1,0:T(8,128)(2,1)S(1)}, u32[]{:S(2)}, u32[]{:S(2)}) %collective-permute-start.6) | collective-permute-done | bytes 786464 | tf_op jit(solution)/shard_map/ppermute | solution.py:38
  125.3 1.6 collective-permute-start.16
  128.3 2.7 fusion.3
  131.1 5.8 %convolution_convert_fusion.1 = bf16[512,384]{1,0:T(8,128)(2,1)S(1)} fusion(bf16[512,6144]{1,0:T(8,128)(2,1)S(1)} %bitcast.150, bf16[6144,384]{0,1:T(8,128)(2,1)} %bitcast.151), kind=kOutput, calls=%fused_computation.29 | convolution fusion | flops 2416115712 | bytes 11403264 | tf_op jit(solution)/shard_map/dot_general | solution.py:209
  137.7 2.4 all_gather.13
  142.9 1.6 collective-permute-start.17
  146.0 16.3 %collective-permute-done.20.refs_15_ = bf16[128,3072]{1,0:T(8,128)(2,1)S(1)} collective-permute-done((bf16[128,3072]{1,0:T(8,128)(2,1)}, bf16[128,3072]{1,0:T(8,128)(2,1)S(1)}, u32[]{:S(2)}, u32[]{:S(2)}) %collective-permute-start.20) | collective-permute-done | bytes 786464 | tf_op jit(solution)/shard_map/ppermute | solution.py:38
  163.5 1.6 collective-permute-start.7
  165.6 3.9 %collective-permute-done.7.refs_1_ = bf16[512,128]{1,0:T(8,128)(2,1)S(1)} collective-permute-done((bf16[512,128]{1,0:T(8,128)(2,1)S(1)}, bf16[512,128]{1,0:T(8,128)(2,1)S(1)}, u32[]{:S(2)}, u32[]{:S(2)}) %collective-permute-start.7) | collective-permute-done | bytes 131104 | tf_op jit(solution)/shard_map/ppermute | solution.py:34
  169.5 1.6 collective-permute-start.8
  171.5 3.1 collective-permute-done.8.refs_2_
  174.7 1.6 collective-permute-start.9
  176.7 3.0 collective-permute-done.9.refs_3_
  179.7 1.6 collective-permute-start.10
  182.0 3.1 collective-permute-done.10.refs_4_
  185.1 20.4 %shard_map.145 = f32[512,6144]{1,0:T(8,128)} custom-call(s32[1]{0:T(128)} %bitcast.21.span_ref, bf16[512,128]{1,0:T(8,128)(2,1)} %bitcast.158, bf16[512,128]{1,0:T(8,128)(2,1)} %copy-done.14, bf16[512,128]{1,0:T(8,128)(2,1)} %copy-done.16, bf16[512,128]{1,0:T(8,128)(2,1)} %collective-permute-done.9.refs_3_, ...), custom_call_target="tpu_custom_call" | custom-call | flops 6442450944 | bytes 26214400 | tf_op jit(solution)/shard_map/pallas_call | solution.py:111
  205.4 13.4 %multiply_reduce_fusion = (f32[4,128]{1,0:T(4,128)S(1)}, f32[4,128,6144]{2,1,0:T(8,128)}) fusion(f32[4,128,6144]{2,1,0:T(8,128)} %bitcast.140, f32[4,6144]{1,0:T(4,128)S(1)} %get-tuple-element.31, bf16[4,128,6144]{2,1,0:T(8,128)(2,1)} %copy-done.2), kind=kLoop, calls=%fused_computation.8 | loop fusion | flops 15728128 | bytes 31557632 | tf_op jit(solution)/shard_map/reduce_sum | solution.py:20
  218.9 10.0 %fusion.27 = bf16[4,128,512]{2,1,0:T(8,128)(2,1)S(1)} fusion(bf16[6144,512]{1,0:T(8,128)(2,1)} %all-gather.3.cloned.1.call-done, f32[4,128,6144]{2,1,0:T(8,128)} %get-tuple-element.6, f32[4,6144]{1,0:T(4,128)S(1)} %copy-done.19, f32[4,6144]{1,0:T(4,128)S(1)} %copy-done.18, f32[4,128]{1,0:T(4,128)S(1)} %add_rsqrt_fusion), kind=kOutput, calls=%fused_computation.40 | convolution fusion | flops 3236167680 | bytes 19597312 | tf_op jit(solution)/shard_map/dot_general | solution.py:255
  228.9 6.4 %convolution_convert_fusion = bf16[4,128,6144]{2,1,0:T(8,128)(2,1)S(1)} fusion(bf16[4,128,512]{2,1,0:T(8,128)(2,1)S(1)} %fusion.27, bf16[512,6144]{1,0:T(8,128)(2,1)} %all-gather.5.cloned.1.call-done), kind=kOutput, calls=%fused_computation.9 | convolution fusion | flops 3224371200 | bytes 13107200 | tf_op jit(solution)/shard_map/dot_general | solution.py:257
  235.4 2.6 copy-done.3
  238.1 1.6 collective-permute-start.29
  241.4 4.5 %collective-permute-done.29 = bf16[512,384]{1,0:T(8,128)(2,1)S(1)} collective-permute-done((bf16[512,384]{1,0:T(8,128)(2,1)S(1)}, bf16[512,384]{1,0:T(8,128)(2,1)S(1)}, u32[]{:S(2)}, u32[]{:S(2)}) %collective-permute-start.29) | collective-permute-done | bytes 393248 | tf_op jit(solution)/shard_map/ppermute | solution.py:61
  245.9 1.5 collective-permute-done.36
  248.8 2.0 collective-permute-start.30
  252.1 5.5 %collective-permute-done.30 = bf16[512,384]{1,0:T(8,128)(2,1)S(1)} collective-permute-done((bf16[512,384]{1,0:T(8,128)(2,1)S(1)}, bf16[512,384]{1,0:T(8,128)(2,1)S(1)}, u32[]{:S(2)}, u32[]{:S(2)}) %collective-permute-start.30) | collective-permute-done | bytes 393248 | tf_op jit(solution)/shard_map/ppermute | solution.py:61
  257.6 2.8 collective-permute-done.37
  262.0 1.8 collective-permute-start.38
  264.4 8.0 %collective-permute-done.31 = bf16[512,384]{1,0:T(8,128)(2,1)S(1)} collective-permute-done((bf16[512,384]{1,0:T(8,128)(2,1)S(1)}, bf16[512,384]{1,0:T(8,128)(2,1)S(1)}, u32[]{:S(2)}, u32[]{:S(2)}) %collective-permute-start.31) | collective-permute-done | bytes 393248 | tf_op jit(solution)/shard_map/ppermute | solution.py:61
  276.2 9.9 %collective-permute-done.32 = bf16[512,384]{1,0:T(8,128)(2,1)S(1)} collective-permute-done((bf16[512,384]{1,0:T(8,128)(2,1)S(1)}, bf16[512,384]{1,0:T(8,128)(2,1)S(1)}, u32[]{:S(2)}, u32[]{:S(2)}) %collective-permute-start.32) | collective-permute-done | bytes 393248 | tf_op jit(solution)/shard_map/ppermute | solution.py:61
  288.3 1.7 collective-permute-start.40
  290.0 8.7 %collective-permute-done.33 = bf16[512,384]{1,0:T(8,128)(2,1)S(1)} collective-permute-done((bf16[512,384]{1,0:T(8,128)(2,1)S(1)}, bf16[512,384]{1,0:T(8,128)(2,1)S(1)}, u32[]{:S(2)}, u32[]{:S(2)}) %collective-permute-start.33) | collective-permute-done | bytes 393248 | tf_op jit(solution)/shard_map/ppermute | solution.py:61
  300.7 1.7 collective-permute-start.41
  302.4 8.7 %collective-permute-done.34 = bf16[512,384]{1,0:T(8,128)(2,1)S(1)} collective-permute-done((bf16[512,384]{1,0:T(8,128)(2,1)S(1)}, bf16[512,384]{1,0:T(8,128)(2,1)S(1)}, u32[]{:S(2)}, u32[]{:S(2)}) %collective-permute-start.34) | collective-permute-done | bytes 393248 | tf_op jit(solution)/shard_map/ppermute | solution.py:61
  311.8 1.6 add_convert_fusion.13
  315.5 5.7 %collective-permute-done.35 = bf16[512,384]{1,0:T(8,128)(2,1)S(1)} collective-permute-done((bf16[512,384]{1,0:T(8,128)(2,1)S(1)}, bf16[512,384]{1,0:T(8,128)(2,1)S(1)}, u32[]{:S(2)}, u32[]{:S(2)}) %collective-permute-start.35) | collective-permute-done | bytes 393248 | tf_op jit(solution)/shard_map/ppermute | solution.py:61
  323.5 2.6 add_convert_fusion.2
  (156 shorter events, 39.3 us)
Async XLA Ops:
  6.5 83.0 %copy-start.17 = (s32[8]{0:T(128)S(1)}, s32[8]{0:T(128)}, u32[]{:S(2)}) copy-start(s32[8]{0:T(128)} %constant.289.clone) | copy-start | bytes 100
  6.6 58.6 %copy-start.12 = (bf16[4,128,2,128]{3,2,1,0:T(2,128)(2,1)S(1)}, bf16[4,128,2,128]{3,2,1,0:T(2,128)(2,1)}, u32[]{:S(2)}) copy-start(bf16[4,128,2,128]{3,2,1,0:T(2,128)(2,1)} %param.20) | copy-start | bytes 786436
  6.6 212.3 %all-gather.3.cloned.1.call-start = ((), (), s32[]{:S(2)}) async-start(), calls=%async_computation | async-start | bytes 9437184 | tf_op jit(solution)/shard_map/all_gather | solution.py:195
  7.3 221.6 %all-gather.5.cloned.1.call-start = ((), (), s32[]{:S(2)}) async-start(), calls=%async_computation.1 | async-start | bytes 9437184 | tf_op jit(solution)/shard_map/all_gather | solution.py:196
  7.4 21.7 %collective-permute-start = (bf16[4,128,768]{2,1,0:T(8,128)(2,1)}, bf16[4,128,768]{2,1,0:T(8,128)(2,1)}, u32[]{:S(2)}, u32[]{:S(2)}) collective-permute-start(bf16[4,128,768]{2,1,0:T(8,128)(2,1)} %param.15), channel_id=1, source_target_pairs={{0,2},{2,4},{4,6},{6,7},{7,5},{5,3},{3,1},{1,0},{8,10},{10,12},{12... | collective-permute-start | bytes 2359304 | tf_op jit(solution)/shard_map/ppermute | solution.py:34
  10.4 53.3 %collective-permute-start.4 = (bf16[4,128,768]{2,1,0:T(8,128)(2,1)}, bf16[4,128,768]{2,1,0:T(8,128)(2,1)}, u32[]{:S(2)}, u32[]{:S(2)}) collective-permute-start(bf16[4,128,768]{2,1,0:T(8,128)(2,1)} %param.15), channel_id=1, source_target_pairs={{0,1},{2,0},{4,2},{6,4},{7,6},{5,7},{3,5},{1,3},{8,9},{10,8},{12,1... | collective-permute-start | bytes 2359304 | tf_op jit(solution)/shard_map/ppermute | solution.py:38
  10.5 91.5 %copy-start.4 = (bf16[128,3072]{1,0:T(8,128)(2,1)}, bf16[128,3072]{1,0:T(8,128)(2,1)S(1)}, u32[]{:S(2)}) copy-start(bf16[128,3072]{1,0:T(8,128)(2,1)S(1)} %constant_dynamic-slice_fusion.2.refs_8_) | copy-start | bytes 2359300
  10.5 92.5 %collective-permute-start.14 = (bf16[128,3072]{1,0:T(8,128)(2,1)S(1)}, bf16[128,3072]{1,0:T(8,128)(2,1)}, u32[]{:S(2)}, u32[]{:S(2)}) collective-permute-start(bf16[128,3072]{1,0:T(8,128)(2,1)S(1)} %constant_dynamic-slice_fusion.2.refs_8_), channel_id=1, source_target_pairs={{0,2},{2,4},{4,6},{6,7},{7,5},{5,3},{3,1},{1,0},{8,10},{10,12},{12... | collective-permute-start | bytes 2359304 | tf_op jit(solution)/shard_map/ppermute | solution.py:34
  12.6 96.2 %collective-permute-start.18 = (bf16[128,3072]{1,0:T(8,128)(2,1)S(1)}, bf16[128,3072]{1,0:T(8,128)(2,1)}, u32[]{:S(2)}, u32[]{:S(2)}) collective-permute-start(bf16[128,3072]{1,0:T(8,128)(2,1)S(1)} %constant_dynamic-slice_fusion.2.refs_8_), channel_id=1, source_target_pairs={{0,1},{2,0},{4,2},{6,4},{7,6},{5,7},{3,5},{1,3},{8,9},{10,8},{12,1... | collective-permute-start | bytes 2359304 | tf_op jit(solution)/shard_map/ppermute | solution.py:38
  12.6 129.5 %collective-permute-start.21 = (bf16[128,3072]{1,0:T(8,128)(2,1)S(1)}, bf16[128,3072]{1,0:T(8,128)(2,1)}, u32[]{:S(2)}, u32[]{:S(2)}) collective-permute-start(bf16[128,3072]{1,0:T(8,128)(2,1)S(1)} %constant_dynamic-slice_fusion.2.refs_8_), channel_id=1, source_target_pairs={{0,8},{8,0},{1,9},{9,1},{2,10},{10,2},{3,11},{11,3},{4,12},{12,4},... | collective-permute-start | bytes 2359304 | tf_op jit(solution)/shard_map/ppermute | solution.py:193
  29.1 32.8 %collective-permute-start.1 = (bf16[4,128,768]{2,1,0:T(8,128)(2,1)}, bf16[4,128,768]{2,1,0:T(8,128)(2,1)S(1)}, u32[]{:S(2)}, u32[]{:S(2)}) collective-permute-start(bf16[4,128,768]{2,1,0:T(8,128)(2,1)} %collective-permute-done), channel_id=1, source_target_pairs={{0,2},{2,4},{4,6},{6,7},{7,5},{5,3},{3,1},{1,0},{8,10},{10,12},{12... | collective-permute-start | bytes 2359304 | tf_op jit(solution)/shard_map/ppermute | solution.py:34
  61.8 18.8 %collective-permute-start.2 = (bf16[4,128,768]{2,1,0:T(8,128)(2,1)S(1)}, bf16[4,128,768]{2,1,0:T(8,128)(2,1)}, u32[]{:S(2)}, u32[]{:S(2)}) collective-permute-start(bf16[4,128,768]{2,1,0:T(8,128)(2,1)S(1)} %collective-permute-done.1), channel_id=1, source_target_pairs={{0,2},{2,4},{4,6},{6,7},{7,5},{5,3},{3,1},{1,0},{8,10},{10,12},{12... | collective-permute-start | bytes 2359304 | tf_op jit(solution)/shard_map/ppermute | solution.py:34
  63.7 40.9 %collective-permute-start.5 = (bf16[4,128,768]{2,1,0:T(8,128)(2,1)}, bf16[4,128,768]{2,1,0:T(8,128)(2,1)}, u32[]{:S(2)}, u32[]{:S(2)}) collective-permute-start(bf16[4,128,768]{2,1,0:T(8,128)(2,1)} %collective-permute-done.4), channel_id=1, source_target_pairs={{0,1},{2,0},{4,2},{6,4},{7,6},{5,7},{3,5},{1,3},{8,9},{10,8},{12,1... | collective-permute-start | bytes 2359304 | tf_op jit(solution)/shard_map/ppermute | solution.py:38
  80.7 28.2 %collective-permute-start.3 = (bf16[4,128,768]{2,1,0:T(8,128)(2,1)}, bf16[4,128,768]{2,1,0:T(8,128)(2,1)}, u32[]{:S(2)}, u32[]{:S(2)}) collective-permute-start(bf16[4,128,768]{2,1,0:T(8,128)(2,1)} %collective-permute-done.2), channel_id=1, source_target_pairs={{0,2},{2,4},{4,6},{6,7},{7,5},{5,3},{3,1},{1,0},{8,10},{10,12},{12... | collective-permute-start | bytes 2359304 | tf_op jit(solution)/shard_map/ppermute | solution.py:34
  103.0 17.6 %collective-permute-start.15 = (bf16[128,3072]{1,0:T(8,128)(2,1)}, bf16[128,3072]{1,0:T(8,128)(2,1)}, u32[]{:S(2)}, u32[]{:S(2)}) collective-permute-start(bf16[128,3072]{1,0:T(8,128)(2,1)} %collective-permute-done.14.refs_9_), channel_id=1, source_target_pairs={{0,2},{2,4},{4,6},{6,7},{7,5},{5,3},{3,1},{1,0},{8,10},{10,12},{12... | collective-permute-start | bytes 2359304 | tf_op jit(solution)/shard_map/ppermute | solution.py:34
  104.6 20.7 %collective-permute-start.6 = (bf16[4,128,768]{2,1,0:T(8,128)(2,1)}, bf16[4,128,768]{2,1,0:T(8,128)(2,1)S(1)}, u32[]{:S(2)}, u32[]{:S(2)}) collective-permute-start(bf16[4,128,768]{2,1,0:T(8,128)(2,1)} %collective-permute-done.5), channel_id=1, source_target_pairs={{0,1},{2,0},{4,2},{6,4},{7,6},{5,7},{3,5},{1,3},{8,9},{10,8},{12,1... | collective-permute-start | bytes 2359304 | tf_op jit(solution)/shard_map/ppermute | solution.py:38
  108.8 34.0 %collective-permute-start.22 = (bf16[128,3072]{1,0:T(8,128)(2,1)}, bf16[128,3072]{1,0:T(8,128)(2,1)}, u32[]{:S(2)}, u32[]{:S(2)}) collective-permute-start(bf16[128,3072]{1,0:T(8,128)(2,1)} %collective-permute-done.14.refs_9_), channel_id=1, source_target_pairs={{0,8},{8,0},{1,9},{9,1},{2,10},{10,2},{3,11},{11,3},{4,12},{12,4},... | collective-permute-start | bytes 2359304 | tf_op jit(solution)/shard_map/ppermute | solution.py:193
  108.9 33.4 %collective-permute-start.19 = (bf16[128,3072]{1,0:T(8,128)(2,1)}, bf16[128,3072]{1,0:T(8,128)(2,1)}, u32[]{:S(2)}, u32[]{:S(2)}) collective-permute-start(bf16[128,3072]{1,0:T(8,128)(2,1)} %collective-permute-done.18.refs_13_), channel_id=1, source_target_pairs={{0,1},{2,0},{4,2},{6,4},{7,6},{5,7},{3,5},{1,3},{8,9},{10,8},{12,1... | collective-permute-start | bytes 2359304 | tf_op jit(solution)/shard_map/ppermute | solution.py:38
  120.6 25.2 %collective-permute-start.26 = (bf16[128,3072]{1,0:T(8,128)(2,1)}, bf16[128,3072]{1,0:T(8,128)(2,1)}, u32[]{:S(2)}, u32[]{:S(2)}) collective-permute-start(bf16[128,3072]{1,0:T(8,128)(2,1)} %collective-permute-done.18.refs_13_), channel_id=1, source_target_pairs={{0,8},{8,0},{1,9},{9,1},{2,10},{10,2},{3,11},{11,3},{4,12},{12,4},... | collective-permute-start | bytes 2359304 | tf_op jit(solution)/shard_map/ppermute | solution.py:193
  125.3 17.5 %collective-permute-start.16 = (bf16[128,3072]{1,0:T(8,128)(2,1)}, bf16[128,3072]{1,0:T(8,128)(2,1)}, u32[]{:S(2)}, u32[]{:S(2)}) collective-permute-start(bf16[128,3072]{1,0:T(8,128)(2,1)} %collective-permute-done.15.refs_10_), channel_id=1, source_target_pairs={{0,2},{2,4},{4,6},{6,7},{7,5},{5,3},{3,1},{1,0},{8,10},{10,12},{12... | collective-permute-start | bytes 2359304 | tf_op jit(solution)/shard_map/ppermute | solution.py:34
  142.1 21.4 %collective-permute-start.23 = (bf16[128,3072]{1,0:T(8,128)(2,1)}, bf16[128,3072]{1,0:T(8,128)(2,1)S(1)}, u32[]{:S(2)}, u32[]{:S(2)}) collective-permute-start(bf16[128,3072]{1,0:T(8,128)(2,1)} %collective-permute-done.15.refs_10_), channel_id=1, source_target_pairs={{0,8},{8,0},{1,9},{9,1},{2,10},{10,2},{3,11},{11,3},{4,12},{12,4},... | collective-permute-start | bytes 2359304 | tf_op jit(solution)/shard_map/ppermute | solution.py:193
  142.3 20.0 %collective-permute-start.20 = (bf16[128,3072]{1,0:T(8,128)(2,1)}, bf16[128,3072]{1,0:T(8,128)(2,1)S(1)}, u32[]{:S(2)}, u32[]{:S(2)}) collective-permute-start(bf16[128,3072]{1,0:T(8,128)(2,1)} %collective-permute-done.19.refs_14_), channel_id=1, source_target_pairs={{0,1},{2,0},{4,2},{6,4},{7,6},{5,7},{3,5},{1,3},{8,9},{10,8},{12,1... | collective-permute-start | bytes 2359304 | tf_op jit(solution)/shard_map/ppermute | solution.py:38
  142.8 22.4 %collective-permute-start.27 = (bf16[128,3072]{1,0:T(8,128)(2,1)}, bf16[128,3072]{1,0:T(8,128)(2,1)S(1)}, u32[]{:S(2)}, u32[]{:S(2)}) collective-permute-start(bf16[128,3072]{1,0:T(8,128)(2,1)} %collective-permute-done.19.refs_14_), channel_id=1, source_target_pairs={{0,8},{8,0},{1,9},{9,1},{2,10},{10,2},{3,11},{11,3},{4,12},{12,4},... | collective-permute-start | bytes 2359304 | tf_op jit(solution)/shard_map/ppermute | solution.py:193
  142.9 20.2 %collective-permute-start.17 = (bf16[128,3072]{1,0:T(8,128)(2,1)}, bf16[128,3072]{1,0:T(8,128)(2,1)}, u32[]{:S(2)}, u32[]{:S(2)}) collective-permute-start(bf16[128,3072]{1,0:T(8,128)(2,1)} %collective-permute-done.16.refs_11_), channel_id=1, source_target_pairs={{0,2},{2,4},{4,6},{6,7},{7,5},{5,3},{3,1},{1,0},{8,10},{10,12},{12... | collective-permute-start | bytes 2359304 | tf_op jit(solution)/shard_map/ppermute | solution.py:34
  145.8 36.1 %collective-permute-start.24 = (bf16[128,3072]{1,0:T(8,128)(2,1)}, bf16[128,3072]{1,0:T(8,128)(2,1)}, u32[]{:S(2)}, u32[]{:S(2)}) collective-permute-start(bf16[128,3072]{1,0:T(8,128)(2,1)} %collective-permute-done.16.refs_11_), channel_id=1, source_target_pairs={{0,8},{8,0},{1,9},{9,1},{2,10},{10,2},{3,11},{11,3},{4,12},{12,4},... | collective-permute-start | bytes 2359304 | tf_op jit(solution)/shard_map/ppermute | solution.py:193
  162.3 19.6 %collective-permute-start.28 = (bf16[128,3072]{1,0:T(8,128)(2,1)S(1)}, bf16[128,3072]{1,0:T(8,128)(2,1)}, u32[]{:S(2)}, u32[]{:S(2)}) collective-permute-start(bf16[128,3072]{1,0:T(8,128)(2,1)S(1)} %collective-permute-done.20.refs_15_), channel_id=1, source_target_pairs={{0,8},{8,0},{1,9},{9,1},{2,10},{10,2},{3,11},{11,3},{4,12},{12,4},... | collective-permute-start | bytes 2359304 | tf_op jit(solution)/shard_map/ppermute | solution.py:193
  163.1 21.9 %collective-permute-start.25 = (bf16[128,3072]{1,0:T(8,128)(2,1)}, bf16[128,3072]{1,0:T(8,128)(2,1)}, u32[]{:S(2)}, u32[]{:S(2)}) collective-permute-start(bf16[128,3072]{1,0:T(8,128)(2,1)} %collective-permute-done.17.refs_12_), channel_id=1, source_target_pairs={{0,8},{8,0},{1,9},{9,1},{2,10},{10,2},{3,11},{11,3},{4,12},{12,4},... | collective-permute-start | bytes 2359304 | tf_op jit(solution)/shard_map/ppermute | solution.py:193
  163.5 6.0 %collective-permute-start.7 = (bf16[512,128]{1,0:T(8,128)(2,1)S(1)}, bf16[512,128]{1,0:T(8,128)(2,1)S(1)}, u32[]{:S(2)}, u32[]{:S(2)}) collective-permute-start(bf16[512,128]{1,0:T(8,128)(2,1)S(1)} %bitcast.156), channel_id=1, source_target_pairs={{0,2},{2,4},{4,6},{6,7},{7,5},{5,3},{3,1},{1,0},{8,10},{10,12},{12... | collective-permute-start | bytes 393224 | tf_op jit(solution)/shard_map/ppermute | solution.py:34
  165.2 5.9 %collective-permute-start.11 = (bf16[512,128]{1,0:T(8,128)(2,1)S(1)}, bf16[512,128]{1,0:T(8,128)(2,1)S(1)}, u32[]{:S(2)}, u32[]{:S(2)}) collective-permute-start(bf16[512,128]{1,0:T(8,128)(2,1)S(1)} %bitcast.157), channel_id=1, source_target_pairs={{0,1},{2,0},{4,2},{6,4},{7,6},{5,7},{3,5},{1,3},{8,9},{10,8},{12,1... | collective-permute-start | bytes 393224 | tf_op jit(solution)/shard_map/ppermute | solution.py:38
  169.5 5.1 %collective-permute-start.8 = (bf16[512,128]{1,0:T(8,128)(2,1)S(1)}, bf16[512,128]{1,0:T(8,128)(2,1)S(1)}, u32[]{:S(2)}, u32[]{:S(2)}) collective-permute-start(bf16[512,128]{1,0:T(8,128)(2,1)S(1)} %collective-permute-done.7.refs_1_), channel_id=1, source_target_pairs={{0,2},{2,4},{4,6},{6,7},{7,5},{5,3},{3,1},{1,0},{8,10},{10,12},{12... | collective-permute-start | bytes 393224 | tf_op jit(solution)/shard_map/ppermute | solution.py:34
  171.1 5.1 %collective-permute-start.12 = (bf16[512,128]{1,0:T(8,128)(2,1)S(1)}, bf16[512,128]{1,0:T(8,128)(2,1)}, u32[]{:S(2)}, u32[]{:S(2)}) collective-permute-start(bf16[512,128]{1,0:T(8,128)(2,1)S(1)} %collective-permute-done.11.refs_5_), channel_id=1, source_target_pairs={{0,1},{2,0},{4,2},{6,4},{7,6},{5,7},{3,5},{1,3},{8,9},{10,8},{12,1... | collective-permute-start | bytes 393224 | tf_op jit(solution)/shard_map/ppermute | solution.py:38
  174.7 5.1 %collective-permute-start.9 = (bf16[512,128]{1,0:T(8,128)(2,1)S(1)}, bf16[512,128]{1,0:T(8,128)(2,1)}, u32[]{:S(2)}, u32[]{:S(2)}) collective-permute-start(bf16[512,128]{1,0:T(8,128)(2,1)S(1)} %collective-permute-done.8.refs_2_), channel_id=1, source_target_pairs={{0,2},{2,4},{4,6},{6,7},{7,5},{5,3},{3,1},{1,0},{8,10},{10,12},{12... | collective-permute-start | bytes 393224 | tf_op jit(solution)/shard_map/ppermute | solution.py:34
  176.2 5.7 %collective-permute-start.13 = (bf16[512,128]{1,0:T(8,128)(2,1)}, bf16[512,128]{1,0:T(8,128)(2,1)}, u32[]{:S(2)}, u32[]{:S(2)}) collective-permute-start(bf16[512,128]{1,0:T(8,128)(2,1)} %collective-permute-done.12.refs_6_), channel_id=1, source_target_pairs={{0,1},{2,0},{4,2},{6,4},{7,6},{5,7},{3,5},{1,3},{8,9},{10,8},{12,1... | collective-permute-start | bytes 393224 | tf_op jit(solution)/shard_map/ppermute | solution.py:38
  179.7 5.3 %collective-permute-start.10 = (bf16[512,128]{1,0:T(8,128)(2,1)}, bf16[512,128]{1,0:T(8,128)(2,1)}, u32[]{:S(2)}, u32[]{:S(2)}) collective-permute-start(bf16[512,128]{1,0:T(8,128)(2,1)} %collective-permute-done.9.refs_3_), channel_id=1, source_target_pairs={{0,2},{2,4},{4,6},{6,7},{7,5},{5,3},{3,1},{1,0},{8,10},{10,12},{12... | collective-permute-start | bytes 393224 | tf_op jit(solution)/shard_map/ppermute | solution.py:34
  238.1 7.8 %collective-permute-start.29 = (bf16[512,384]{1,0:T(8,128)(2,1)S(1)}, bf16[512,384]{1,0:T(8,128)(2,1)S(1)}, u32[]{:S(2)}, u32[]{:S(2)}) collective-permute-start(bf16[512,384]{1,0:T(8,128)(2,1)S(1)} %get-tuple-element.21), channel_id=1, source_target_pairs={{0,2},{2,4},{4,6},{6,7},{7,5},{5,3},{3,1},{1,0},{8,10},{10,12},{12... | collective-permute-start | bytes 1179656 | tf_op jit(solution)/shard_map/ppermute | solution.py:61
  239.7 7.8 %collective-permute-start.36 = (bf16[512,384]{1,0:T(8,128)(2,1)S(1)}, bf16[512,384]{1,0:T(8,128)(2,1)S(1)}, u32[]{:S(2)}, u32[]{:S(2)}) collective-permute-start(bf16[512,384]{1,0:T(8,128)(2,1)S(1)} %get-tuple-element.22), channel_id=1, source_target_pairs={{0,1},{2,0},{4,2},{6,4},{7,6},{5,7},{3,5},{1,3},{8,9},{10,8},{12,1... | collective-permute-start | bytes 1179656 | tf_op jit(solution)/shard_map/ppermute | solution.py:63
  248.8 8.9 %collective-permute-start.30 = (bf16[512,384]{1,0:T(8,128)(2,1)S(1)}, bf16[512,384]{1,0:T(8,128)(2,1)S(1)}, u32[]{:S(2)}, u32[]{:S(2)}) collective-permute-start(bf16[512,384]{1,0:T(8,128)(2,1)S(1)} %get-tuple-element.19), channel_id=1, source_target_pairs={{0,2},{2,4},{4,6},{6,7},{7,5},{5,3},{3,1},{1,0},{8,10},{10,12},{12... | collective-permute-start | bytes 1179656 | tf_op jit(solution)/shard_map/ppermute | solution.py:61
  250.8 9.6 %collective-permute-start.37 = (bf16[512,384]{1,0:T(8,128)(2,1)S(1)}, bf16[512,384]{1,0:T(8,128)(2,1)S(1)}, u32[]{:S(2)}, u32[]{:S(2)}) collective-permute-start(bf16[512,384]{1,0:T(8,128)(2,1)S(1)} %get-tuple-element.20), channel_id=1, source_target_pairs={{0,1},{2,0},{4,2},{6,4},{7,6},{5,7},{3,5},{1,3},{8,9},{10,8},{12,1... | collective-permute-start | bytes 1179656 | tf_op jit(solution)/shard_map/ppermute | solution.py:63
  261.7 10.8 %collective-permute-start.31 = (bf16[512,384]{1,0:T(8,128)(2,1)S(1)}, bf16[512,384]{1,0:T(8,128)(2,1)S(1)}, u32[]{:S(2)}, u32[]{:S(2)}) collective-permute-start(bf16[512,384]{1,0:T(8,128)(2,1)S(1)} %get-tuple-element.17), channel_id=1, source_target_pairs={{0,2},{2,4},{4,6},{6,7},{7,5},{5,3},{3,1},{1,0},{8,10},{10,12},{12... | collective-permute-start | bytes 1179656 | tf_op jit(solution)/shard_map/ppermute | solution.py:61
  262.0 10.9 %collective-permute-start.38 = (bf16[512,384]{1,0:T(8,128)(2,1)S(1)}, bf16[512,384]{1,0:T(8,128)(2,1)S(1)}, u32[]{:S(2)}, u32[]{:S(2)}) collective-permute-start(bf16[512,384]{1,0:T(8,128)(2,1)S(1)} %get-tuple-element.18), channel_id=1, source_target_pairs={{0,1},{2,0},{4,2},{6,4},{7,6},{5,7},{3,5},{1,3},{8,9},{10,8},{12,1... | collective-permute-start | bytes 1179656 | tf_op jit(solution)/shard_map/ppermute | solution.py:63
  274.1 12.0 %collective-permute-start.32 = (bf16[512,384]{1,0:T(8,128)(2,1)S(1)}, bf16[512,384]{1,0:T(8,128)(2,1)S(1)}, u32[]{:S(2)}, u32[]{:S(2)}) collective-permute-start(bf16[512,384]{1,0:T(8,128)(2,1)S(1)} %get-tuple-element.15), channel_id=1, source_target_pairs={{0,2},{2,4},{4,6},{6,7},{7,5},{5,3},{3,1},{1,0},{8,10},{10,12},{12... | collective-permute-start | bytes 1179656 | tf_op jit(solution)/shard_map/ppermute | solution.py:61
  275.1 11.5 %collective-permute-start.39 = (bf16[512,384]{1,0:T(8,128)(2,1)S(1)}, bf16[512,384]{1,0:T(8,128)(2,1)S(1)}, u32[]{:S(2)}, u32[]{:S(2)}) collective-permute-start(bf16[512,384]{1,0:T(8,128)(2,1)S(1)} %get-tuple-element.16), channel_id=1, source_target_pairs={{0,1},{2,0},{4,2},{6,4},{7,6},{5,7},{3,5},{1,3},{8,9},{10,8},{12,1... | collective-permute-start | bytes 1179656 | tf_op jit(solution)/shard_map/ppermute | solution.py:63
  287.9 10.8 %collective-permute-start.33 = (bf16[512,384]{1,0:T(8,128)(2,1)S(1)}, bf16[512,384]{1,0:T(8,128)(2,1)S(1)}, u32[]{:S(2)}, u32[]{:S(2)}) collective-permute-start(bf16[512,384]{1,0:T(8,128)(2,1)S(1)} %get-tuple-element.13), channel_id=1, source_target_pairs={{0,2},{2,4},{4,6},{6,7},{7,5},{5,3},{3,1},{1,0},{8,10},{10,12},{12... | collective-permute-start | bytes 1179656 | tf_op jit(solution)/shard_map/ppermute | solution.py:61
  288.3 10.7 %collective-permute-start.40 = (bf16[512,384]{1,0:T(8,128)(2,1)S(1)}, bf16[512,384]{1,0:T(8,128)(2,1)S(1)}, u32[]{:S(2)}, u32[]{:S(2)}) collective-permute-start(bf16[512,384]{1,0:T(8,128)(2,1)S(1)} %get-tuple-element.14), channel_id=1, source_target_pairs={{0,1},{2,0},{4,2},{6,4},{7,6},{5,7},{3,5},{1,3},{8,9},{10,8},{12,1... | collective-permute-start | bytes 1179656 | tf_op jit(solution)/shard_map/ppermute | solution.py:63
  300.3 10.8 %collective-permute-start.34 = (bf16[512,384]{1,0:T(8,128)(2,1)S(1)}, bf16[512,384]{1,0:T(8,128)(2,1)S(1)}, u32[]{:S(2)}, u32[]{:S(2)}) collective-permute-start(bf16[512,384]{1,0:T(8,128)(2,1)S(1)} %get-tuple-element.11), channel_id=1, source_target_pairs={{0,2},{2,4},{4,6},{6,7},{7,5},{5,3},{3,1},{1,0},{8,10},{10,12},{12... | collective-permute-start | bytes 1179656 | tf_op jit(solution)/shard_map/ppermute | solution.py:61
  300.7 11.2 %collective-permute-start.41 = (bf16[512,384]{1,0:T(8,128)(2,1)S(1)}, bf16[512,384]{1,0:T(8,128)(2,1)}, u32[]{:S(2)}, u32[]{:S(2)}) collective-permute-start(bf16[512,384]{1,0:T(8,128)(2,1)S(1)} %get-tuple-element.12), channel_id=1, source_target_pairs={{0,1},{2,0},{4,2},{6,4},{7,6},{5,7},{3,5},{1,3},{8,9},{10,8},{12,1... | collective-permute-start | bytes 1179656 | tf_op jit(solution)/shard_map/ppermute | solution.py:63
  313.4 7.8 %collective-permute-start.35 = (bf16[512,384]{1,0:T(8,128)(2,1)S(1)}, bf16[512,384]{1,0:T(8,128)(2,1)S(1)}, u32[]{:S(2)}, u32[]{:S(2)}) collective-permute-start(bf16[512,384]{1,0:T(8,128)(2,1)S(1)} %get-tuple-element.9), channel_id=1, source_target_pairs={{0,2},{2,4},{4,6},{6,7},{7,5},{5,3},{3,1},{1,0},{8,10},{10,12},{12... | collective-permute-start | bytes 1179656 | tf_op jit(solution)/shard_map/ppermute | solution.py:61
  314.1 7.9 %collective-permute-start.42 = (bf16[512,384]{1,0:T(8,128)(2,1)S(1)}, bf16[512,384]{1,0:T(8,128)(2,1)}, u32[]{:S(2)}, u32[]{:S(2)}) collective-permute-start(bf16[512,384]{1,0:T(8,128)(2,1)S(1)} %get-tuple-element.10), channel_id=1, source_target_pairs={{0,1},{2,0},{4,2},{6,4},{7,6},{5,7},{3,5},{1,3},{8,9},{10,8},{12,1... | collective-permute-start | bytes 1179656 | tf_op jit(solution)/shard_map/ppermute | solution.py:63
  (21 other events, 340.0 us)
Sparse Core Ops, SparseCore 0:
  8.9 18.3 all-gather.2
  28.9 17.9 all-gather.4

commit v8 on v3

--- a/solution.py
+++ b/solution.py
@@ -38,6 +38,31 @@
         backward = lax.ppermute(backward, axis_name, behind)
         blocks.append(backward)
     return blocks
+
+
+def ring_reduce_scatter(terms, axis_name, count):
+    token_count, width = terms.shape
+    block = width // count
+    half = block // 2
+    cycle = snake_cycle(count)
+    position = jnp.array([cycle.index(t) for t in range(count)], jnp.int32)[lax.axis_index(axis_name)]
+    owners = jnp.array(cycle, jnp.int32)
+    rounded = terms.astype(jnp.bfloat16)
+
+    def own_part(slot, side):
+        start = owners[slot % count] * block + side * half
+        return lax.dynamic_slice_in_dim(rounded, start, half, 1).astype(jnp.float32)
+
+    ahead = [(cycle[p], cycle[(p + 1) % count]) for p in range(count)]
+    behind = [(cycle[p], cycle[(p - 1) % count]) for p in range(count)]
+    forward = own_part(position - 1 + count, 0)
+    backward = own_part(position + 1, 1)
+    for step in range(count - 1):
+        forward = lax.ppermute(forward.astype(jnp.bfloat16), axis_name, ahead).astype(jnp.float32)
+        forward = forward + own_part(position - 2 - step + 2 * count, 0)
+        backward = lax.ppermute(backward.astype(jnp.bfloat16), axis_name, behind).astype(jnp.float32)
+        backward = backward + own_part(position + 2 + step, 1)
+    return jnp.concatenate([forward, backward], axis=1)
 
 
 def out_proj_kernel(group_count, set_count, tiles_per_set, place_ref, *refs):
@@ -150,11 +175,22 @@
     local_count = hidden_in.shape[0]
     row_count = hidden_in.shape[1]
     token_count = local_count * row_count
-    gathered = lax.all_gather(hidden_in, "tp", axis=2, tiled=True).astype(jnp.float32)
     gather_weights = (
         tp_count * w_out.size * w_out.dtype.itemsize <= WEIGHT_GATHER_BYTES and span_count == 2
         and rep_count == 2
     )
+    if gather_weights:
+        cycle = snake_cycle(tp_count)
+        position = jnp.array([cycle.index(t) for t in range(tp_count)], jnp.int32)[tp_rank]
+        steps = list(range(tp_count // 2 + 1)) + [-k for k in range(1, (tp_count - 1) // 2 + 1)]
+        owners = jnp.array(cycle, jnp.int32)
+        gathered = jnp.zeros(hidden_in.shape[:2] + (model_width,), hidden_in.dtype)
+        for step, piece in zip(steps, ring_gather(hidden_in, "tp", tp_count)):
+            owner = owners[(position - step + tp_count) % tp_count]
+            gathered = lax.dynamic_update_slice_in_dim(gathered, piece, owner * share_width, 2)
+        gathered = gathered.astype(jnp.float32)
+    else:
+        gathered = lax.all_gather(hidden_in, "tp", axis=2, tiled=True).astype(jnp.float32)
     if gather_weights:
         rep_index = lax.axis_index("rep")
         column_part = model_width // (rep_count * span_count)
@@ -240,9 +276,14 @@
     pre_act = jnp.dot(mlp_in, up_full, preferred_element_type=jnp.float32)
     hidden_units = jax.nn.gelu(pre_act).astype(jnp.bfloat16)
     down_terms = jnp.dot(hidden_units, down_full, preferred_element_type=jnp.float32)
-    mlp_out = lax.psum_scatter(
-        down_terms.astype(jnp.bfloat16), "tp", scatter_dimension=2, tiled=True
-    ).astype(jnp.float32)
+    if gather_weights:
+        mlp_out = ring_reduce_scatter(
+            down_terms.reshape(token_count, model_width), "tp", tp_count
+        ).reshape(local_count, row_count, share_width)
+    else:
+        mlp_out = lax.psum_scatter(
+            down_terms.astype(jnp.bfloat16), "tp", scatter_dimension=2, tiled=True
+        ).astype(jnp.float32)
     if gather_weights:
         residual = lax.dynamic_slice_in_dim(residual_full, tp_rank * share_width, share_width, 2)
         mod_share = lax.dynamic_slice_in_dim(mod_rows, tp_rank * share_width, share_width, 2)

time: 386 us -> 349 us (0.904)
  waiting for transfers between devices: 255 us -> 158 us
  starting transfers between devices: 25.4 us -> 50.9 us
  between operations: 14.3 us -> 31.9 us
  local copies, waits for them, and re-layouts: 10.4 us -> 22.7 us
  other arithmetic: 25.7 us -> 32.4 us
    reduce_scatter x1 -> x0, waiting for transfers between devices: 115 us -> none  [local(): lax.psum_scatter(down_terms.astype(jnp.bfloat16), 'tp', scatter_dimension...]
    all_gather x1 -> x0, waiting for transfers between devices: 91.2 us -> none  [local(): lax.all_gather(hidden_in, 'tp', axis=2, tiled=True).astype(jnp.float32)]
    ppermute x0 -> x14, waiting for transfers between devices: none -> 57.8 us  [the longest x7 48.2 us: ring_reduce_scatter(): lax.ppermute(forward.astype(jnp.bfloat16), axis_name, ahead)]
    ppermute x8 -> x12, waiting for transfers between devices: 13.5 us -> 57.3 us  [ring_gather(): forward = lax.ppermute(forward, axis_name, ahead)]
    ppermute x0 -> x14, starting transfers between devices: none -> 14.6 us  [the longest x7 9.37 us: ring_reduce_scatter(): lax.ppermute(forward.astype(jnp.bfloat16), axis_name, ahead)]
    ppermute x8 -> x12, starting transfers between devices: 9.11 us -> 21.6 us  [ring_gather(): forward = lax.ppermute(forward, axis_name, ahead)]
    ppermute x6 -> x9, waiting for transfers between devices: 9.41 us -> 18 us  [ring_gather(): backward = lax.ppermute(backward, axis_name, behind)]
    convert_element_type x0 -> x6, other arithmetic: none -> 8.11 us  [ring_reduce_scatter(): forward.astype(jnp.bfloat16)]
  transfers between devices with their start and end apart: 42 -> 61, of which waited for: 14 -> 32; matrix products, arithmetic and copies ran while one was open for 14% -> 17% of each run, Pallas kernels for 6% -> 6%
where the time goes in v8:
time: 349 us; the launch traced here: 348 us
  waiting for transfers between devices  158 us (45%)
  starting transfers between devices  50.9 us (15%)
  other arithmetic  32.4 us (9%)
  between operations  31.9 us (9%)
  matrix products  25.9 us (7%)
  local copies, waits for them, and re-layouts  22.7 us (7%)
  Pallas kernels  22 us (6%)
  blocking collectives  4.36 us (1%)
    ppermute x12, waiting for transfers between devices, ring_gather(): forward = lax.ppermute(forward, axis_name, ahead)  57.3 us
    ppermute x7, waiting for transfers between devices, ring_reduce_scatter(): lax.ppermute(forward.astype(jnp.bfloat16), axis_name, ahead)  48.2 us
    ppermute x8, waiting for transfers between devices, local(): rep_blocks = [lax.ppermute(b, 'rep', swap) for b in mine_blocks]  23.9 us
    pallas_call x1, Pallas kernels, grouped_out_proj(): pl.pallas_call(functools.partial(out_proj_kernel, group_count, set_count,...  22 us
    ppermute x12, starting transfers between devices, ring_gather(): forward = lax.ppermute(forward, axis_name, ahead)  21.6 us
    ppermute x9, waiting for transfers between devices, ring_gather(): backward = lax.ppermute(backward, axis_name, behind)  18 us
    reduce_sum x2, other arithmetic, normalize(): jnp.mean(values * values, axis=-1, keepdims=True) + EPSILON  14.8 us
    unnamed x83, local copies, waits for them, and re-layouts  11.7 us
  transfers between devices with their start and end apart: 61, of which 32 were waited for; matrix products, arithmetic and copies ran while one was open for 17% of the time, Pallas kernels for 6%

profile of v8, /device:TPU:0, one launch (start us, length us, event | category | flops | bytes accessed | tf_op | source)
XLA Modules:
  0.0 348.0 jit_solution(5801472633865068838)
XLA Ops:
  7.3 3.1 collective-permute-start
  10.5 2.1 collective-permute-start.14
  12.6 1.9 collective-permute-start.21
  17.2 11.8 %collective-permute-done = bf16[4,128,768]{2,1,0:T(8,128)(2,1)} collective-permute-done((bf16[4,128,768]{2,1,0:T(8,128)(2,1)}, bf16[4,128,768]{2,1,0:T(8,128)(2,1)}, u32[]{:S(2)}, u32[]{:S(2)}) %collective-permute-start) | collective-permute-done | bytes 786464 | tf_op jit(solution)/shard_map/ppermute | solution.py:34
  29.0 2.1 collective-permute-start.1
  31.5 21.9 %collective-permute-done.1 = bf16[4,128,768]{2,1,0:T(8,128)(2,1)S(1)} collective-permute-done((bf16[4,128,768]{2,1,0:T(8,128)(2,1)}, bf16[4,128,768]{2,1,0:T(8,128)(2,1)S(1)}, u32[]{:S(2)}, u32[]{:S(2)}) %collective-permute-start.1) | collective-permute-done | bytes 786464 | tf_op jit(solution)/shard_map/ppermute | solution.py:34
  53.4 1.8 collective-permute-start.2
  58.4 2.2 all_gather.12
  60.7 11.6 %collective-permute-done.2 = bf16[4,128,768]{2,1,0:T(8,128)(2,1)} collective-permute-done((bf16[4,128,768]{2,1,0:T(8,128)(2,1)S(1)}, bf16[4,128,768]{2,1,0:T(8,128)(2,1)}, u32[]{:S(2)}, u32[]{:S(2)}) %collective-permute-start.2) | collective-permute-done | bytes 786464 | tf_op jit(solution)/shard_map/ppermute | solution.py:34
  86.9 6.8 %copy.30 = bf16[6144,3,128]{0,2,1:T(8,128)(2,1)} copy(bf16[6144,3,128]{2,0,1:T(8,128)(2,1)} %param.22) | data formatting | bytes 9437184 | tf_op args[7]
  104.4 8.7 %collective-permute-done.6 = bf16[4,128,768]{2,1,0:T(8,128)(2,1)S(1)} collective-permute-done((bf16[4,128,768]{2,1,0:T(8,128)(2,1)}, bf16[4,128,768]{2,1,0:T(8,128)(2,1)S(1)}, u32[]{:S(2)}, u32[]{:S(2)}) %collective-permute-start.6) | collective-permute-done | bytes 786464 | tf_op jit(solution)/shard_map/ppermute | solution.py:38
  115.2 2.7 fusion.3
  119.2 5.8 %convolution_convert_fusion.1 = bf16[512,384]{1,0:T(8,128)(2,1)S(1)} fusion(bf16[512,6144]{1,0:T(8,128)(2,1)S(1)} %bitcast.153, bf16[6144,384]{0,1:T(8,128)(2,1)} %bitcast.154), kind=kOutput, calls=%fused_computation.29 | convolution fusion | flops 2416115712 | bytes 11403264 | tf_op jit(solution)/shard_map/dot_general | solution.py:230
  125.6 2.2 all_gather.13
  128.5 1.6 collective-permute-start.16
  134.0 6.2 %collective-permute-done.16.refs_11_ = bf16[128,1536]{1,0:T(8,128)(2,1)} collective-permute-done((bf16[128,1536]{1,0:T(8,128)(2,1)}, bf16[128,1536]{1,0:T(8,128)(2,1)}, u32[]{:S(2)}, u32[]{:S(2)}) %collective-permute-start.16) | collective-permute-done | bytes 393248 | tf_op jit(solution)/shard_map/ppermute | solution.py:34
  144.2 7.3 %collective-permute-done.27.refs_22_ = bf16[128,1536]{1,0:T(8,128)(2,1)S(1)} collective-permute-done((bf16[128,1536]{1,0:T(8,128)(2,1)S(1)}, bf16[128,1536]{1,0:T(8,128)(2,1)S(1)}, u32[]{:S(2)}, u32[]{:S(2)}) %collective-permute-start.27) | collective-permute-done | bytes 393248 | tf_op jit(solution)/shard_map/ppermute | solution.py:201
  156.8 4.9 %collective-permute-done.17.refs_12_ = bf16[128,1536]{1,0:T(8,128)(2,1)S(1)} collective-permute-done((bf16[128,1536]{1,0:T(8,128)(2,1)}, bf16[128,1536]{1,0:T(8,128)(2,1)S(1)}, u32[]{:S(2)}, u32[]{:S(2)}) %collective-permute-start.17) | collective-permute-done | bytes 393248 | tf_op jit(solution)/shard_map/ppermute | solution.py:34
  161.7 3.7 %collective-permute-done.24.refs_19_ = bf16[128,1536]{1,0:T(8,128)(2,1)} collective-permute-done((bf16[128,1536]{1,0:T(8,128)(2,1)}, bf16[128,1536]{1,0:T(8,128)(2,1)}, u32[]{:S(2)}, u32[]{:S(2)}) %collective-permute-start.24) | collective-permute-done | bytes 393248 | tf_op jit(solution)/shard_map/ppermute | solution.py:201
  165.4 5.9 %collective-permute-done.28.refs_23_ = bf16[128,1536]{1,0:T(8,128)(2,1)S(1)} collective-permute-done((bf16[128,1536]{1,0:T(8,128)(2,1)}, bf16[128,1536]{1,0:T(8,128)(2,1)S(1)}, u32[]{:S(2)}, u32[]{:S(2)}) %collective-permute-start.28) | collective-permute-done | bytes 393248 | tf_op jit(solution)/shard_map/ppermute | solution.py:201
  172.4 1.6 collective-permute-start.7
  174.6 5.6 %collective-permute-done.25.refs_20_ = bf16[128,1536]{1,0:T(8,128)(2,1)} collective-permute-done((bf16[128,1536]{1,0:T(8,128)(2,1)S(1)}, bf16[128,1536]{1,0:T(8,128)(2,1)}, u32[]{:S(2)}, u32[]{:S(2)}) %collective-permute-start.25) | collective-permute-done | bytes 393248 | tf_op jit(solution)/shard_map/ppermute | solution.py:201
  181.0 1.6 collective-permute-start.8
  182.6 3.6 %collective-permute-done.11.refs_5_ = bf16[512,128]{1,0:T(8,128)(2,1)S(1)} collective-permute-done((bf16[512,128]{1,0:T(8,128)(2,1)S(1)}, bf16[512,128]{1,0:T(8,128)(2,1)S(1)}, u32[]{:S(2)}, u32[]{:S(2)}) %collective-permute-start.11) | collective-permute-done | bytes 131104 | tf_op jit(solution)/shard_map/ppermute | solution.py:38
  186.9 1.6 collective-permute-start.9
  188.5 2.9 collective-permute-done.12.refs_6_
  192.1 1.6 collective-permute-start.10
  195.0 1.7 collective-permute-done.13.refs_7_
  197.5 22.0 %shard_map.145 = f32[512,6144]{1,0:T(8,128)} custom-call(s32[4]{0:T(128)} %pad_add_fusion.place_ref, bf16[512,128]{1,0:T(8,128)(2,1)} %bitcast.161, bf16[512,128]{1,0:T(8,128)(2,1)} %copy-done.29, bf16[512,128]{1,0:T(8,128)(2,1)} %copy-done.31, bf16[512,128]{1,0:T(8,128)(2,1)} %collective-permute-done.9.refs_3_, ...), custom_call_target="tpu_custom_call" | custom-call | flops 6442450944 | bytes 26214400 | tf_op jit(solution)/shard_map/pallas_call | solution.py:114
  219.5 13.5 %multiply_reduce_fusion = (f32[4,128]{1,0:T(4,128)S(1)}, f32[4,128,6144]{2,1,0:T(8,128)}) fusion(f32[4,128,6144]{2,1,0:T(8,128)} %bitcast.143, f32[4,6144]{1,0:T(4,128)S(1)} %get-tuple-element.31, bf16[4,128,6144]{2,1,0:T(8,128)(2,1)} %copy-done.2), kind=kLoop, calls=%fused_computation.8 | loop fusion | flops 15728128 | bytes 31557632 | tf_op jit(solution)/shard_map/reduce_sum | solution.py:20
  233.0 10.0 %fusion.27 = bf16[4,128,512]{2,1,0:T(8,128)(2,1)S(1)} fusion(bf16[6144,512]{1,0:T(8,128)(2,1)} %all-gather.3.cloned.1.call-done, f32[4,128,6144]{2,1,0:T(8,128)} %get-tuple-element.6, f32[4,6144]{1,0:T(4,128)S(1)} %copy-done.34, f32[4,6144]{1,0:T(4,128)S(1)} %copy-done.33, f32[4,128]{1,0:T(4,128)S(1)} %add_rsqrt_fusion), kind=kOutput, calls=%fused_computation.40 | convolution fusion | flops 3236167680 | bytes 19597312 | tf_op jit(solution)/shard_map/dot_general | solution.py:276
  243.0 6.6 %convolution_convert_fusion = bf16[4,128,6144]{2,1,0:T(8,128)(2,1)S(1)} fusion(bf16[4,128,512]{2,1,0:T(8,128)(2,1)S(1)} %fusion.27, bf16[512,6144]{1,0:T(8,128)(2,1)} %all-gather.5.cloned.1.call-done), kind=kOutput, calls=%fused_computation.9 | convolution fusion | flops 3224371200 | bytes 13107200 | tf_op jit(solution)/shard_map/dot_general | solution.py:278
  249.7 2.6 copy-done.3
  252.4 1.6 collective-permute-start.45
  255.8 5.3 %collective-permute-done.45 = bf16[512,384]{1,0:T(8,128)(2,1)S(1)} collective-permute-done((bf16[512,384]{1,0:T(8,128)(2,1)S(1)}, bf16[512,384]{1,0:T(8,128)(2,1)S(1)}, u32[]{:S(2)}, u32[]{:S(2)}) %collective-permute-start.45) | collective-permute-done | bytes 393248 | tf_op jit(solution)/shard_map/ppermute | solution.py:61
  263.7 1.7 collective-permute-start.46
  267.1 4.5 %collective-permute-done.46 = bf16[512,384]{1,0:T(8,128)(2,1)S(1)} collective-permute-done((bf16[512,384]{1,0:T(8,128)(2,1)S(1)}, bf16[512,384]{1,0:T(8,128)(2,1)S(1)}, u32[]{:S(2)}, u32[]{:S(2)}) %collective-permute-start.46) | collective-permute-done | bytes 393248 | tf_op jit(solution)/shard_map/ppermute | solution.py:61
  271.6 1.6 collective-permute-done.53
  277.3 5.6 %collective-permute-done.47 = bf16[512,384]{1,0:T(8,128)(2,1)S(1)} collective-permute-done((bf16[512,384]{1,0:T(8,128)(2,1)S(1)}, bf16[512,384]{1,0:T(8,128)(2,1)S(1)}, u32[]{:S(2)}, u32[]{:S(2)}) %collective-permute-start.47) | collective-permute-done | bytes 393248 | tf_op jit(solution)/shard_map/ppermute | solution.py:61
  282.9 1.9 collective-permute-done.54
  286.1 2.2 collective-permute-start.48
  288.3 7.9 %collective-permute-done.48 = bf16[512,384]{1,0:T(8,128)(2,1)S(1)} collective-permute-done((bf16[512,384]{1,0:T(8,128)(2,1)S(1)}, bf16[512,384]{1,0:T(8,128)(2,1)S(1)}, u32[]{:S(2)}, u32[]{:S(2)}) %collective-permute-start.48) | collective-permute-done | bytes 393248 | tf_op jit(solution)/shard_map/ppermute | solution.py:61
  296.2 2.8 collective-permute-done.55
  302.4 9.8 %collective-permute-done.49 = bf16[512,384]{1,0:T(8,128)(2,1)S(1)} collective-permute-done((bf16[512,384]{1,0:T(8,128)(2,1)S(1)}, bf16[512,384]{1,0:T(8,128)(2,1)S(1)}, u32[]{:S(2)}, u32[]{:S(2)}) %collective-permute-start.49) | collective-permute-done | bytes 393248 | tf_op jit(solution)/shard_map/ppermute | solution.py:61
  314.8 1.7 collective-permute-start.57
  316.5 9.3 %collective-permute-done.50 = bf16[512,384]{1,0:T(8,128)(2,1)S(1)} collective-permute-done((bf16[512,384]{1,0:T(8,128)(2,1)S(1)}, bf16[512,384]{1,0:T(8,128)(2,1)S(1)}, u32[]{:S(2)}, u32[]{:S(2)}) %collective-permute-start.50) | collective-permute-done | bytes 393248 | tf_op jit(solution)/shard_map/ppermute | solution.py:61
  330.3 5.7 %collective-permute-done.51 = bf16[512,384]{1,0:T(8,128)(2,1)S(1)} collective-permute-done((bf16[512,384]{1,0:T(8,128)(2,1)S(1)}, bf16[512,384]{1,0:T(8,128)(2,1)S(1)}, u32[]{:S(2)}, u32[]{:S(2)}) %collective-permute-start.51) | collective-permute-done | bytes 393248 | tf_op jit(solution)/shard_map/ppermute | solution.py:61
  338.5 2.6 add_convert_fusion.2
  (217 shorter events, 62.8 us)
Async XLA Ops:
  6.5 226.4 %all-gather.3.cloned.1.call-start = ((), (), s32[]{:S(2)}) async-start(), calls=%async_computation | async-start | bytes 9437184 | tf_op jit(solution)/shard_map/all_gather | solution.py:216
  7.3 235.8 %all-gather.5.cloned.1.call-start = ((), (), s32[]{:S(2)}) async-start(), calls=%async_computation.1 | async-start | bytes 9437184 | tf_op jit(solution)/shard_map/all_gather | solution.py:217
  7.3 21.7 %collective-permute-start = (bf16[4,128,768]{2,1,0:T(8,128)(2,1)}, bf16[4,128,768]{2,1,0:T(8,128)(2,1)}, u32[]{:S(2)}, u32[]{:S(2)}) collective-permute-start(bf16[4,128,768]{2,1,0:T(8,128)(2,1)} %param.15), channel_id=1, source_target_pairs={{0,2},{2,4},{4,6},{6,7},{7,5},{5,3},{3,1},{1,0},{8,10},{10,12},{12... | collective-permute-start | bytes 2359304 | tf_op jit(solution)/shard_map/ppermute | solution.py:34
  10.4 44.9 %collective-permute-start.4 = (bf16[4,128,768]{2,1,0:T(8,128)(2,1)}, bf16[4,128,768]{2,1,0:T(8,128)(2,1)S(1)}, u32[]{:S(2)}, u32[]{:S(2)}) collective-permute-start(bf16[4,128,768]{2,1,0:T(8,128)(2,1)} %param.15), channel_id=1, source_target_pairs={{0,1},{2,0},{4,2},{6,4},{7,6},{5,7},{3,5},{1,3},{8,9},{10,8},{12,1... | collective-permute-start | bytes 2359304 | tf_op jit(solution)/shard_map/ppermute | solution.py:38
  10.5 88.1 %collective-permute-start.14 = (bf16[128,1536]{1,0:T(8,128)(2,1)S(1)}, bf16[128,1536]{1,0:T(8,128)(2,1)}, u32[]{:S(2)}, u32[]{:S(2)}) collective-permute-start(bf16[128,1536]{1,0:T(8,128)(2,1)S(1)} %constant_dynamic-slice_fusion.2.refs_8_), channel_id=1, source_target_pairs={{0,2},{2,4},{4,6},{6,7},{7,5},{5,3},{3,1},{1,0},{8,10},{10,12},{12... | collective-permute-start | bytes 1179656 | tf_op jit(solution)/shard_map/ppermute | solution.py:34
  12.6 90.2 %collective-permute-start.18 = (bf16[128,1536]{1,0:T(8,128)(2,1)S(1)}, bf16[128,1536]{1,0:T(8,128)(2,1)}, u32[]{:S(2)}, u32[]{:S(2)}) collective-permute-start(bf16[128,1536]{1,0:T(8,128)(2,1)S(1)} %constant_dynamic-slice_fusion.2.refs_8_), channel_id=1, source_target_pairs={{0,1},{2,0},{4,2},{6,4},{7,6},{5,7},{3,5},{1,3},{8,9},{10,8},{12,1... | collective-permute-start | bytes 1179656 | tf_op jit(solution)/shard_map/ppermute | solution.py:38
  12.6 105.3 %collective-permute-start.21 = (bf16[128,1536]{1,0:T(8,128)(2,1)S(1)}, bf16[128,1536]{1,0:T(8,128)(2,1)}, u32[]{:S(2)}, u32[]{:S(2)}) collective-permute-start(bf16[128,1536]{1,0:T(8,128)(2,1)S(1)} %constant_dynamic-slice_fusion.2.refs_8_), channel_id=1, source_target_pairs={{0,16},{16,0},{1,17},{17,1},{2,18},{18,2},{3,19},{19,3},{4,20},{20... | collective-permute-start | bytes 1179656 | tf_op jit(solution)/shard_map/ppermute | solution.py:201
  29.0 24.3 %collective-permute-start.1 = (bf16[4,128,768]{2,1,0:T(8,128)(2,1)}, bf16[4,128,768]{2,1,0:T(8,128)(2,1)S(1)}, u32[]{:S(2)}, u32[]{:S(2)}) collective-permute-start(bf16[4,128,768]{2,1,0:T(8,128)(2,1)} %collective-permute-done), channel_id=1, source_target_pairs={{0,2},{2,4},{4,6},{6,7},{7,5},{5,3},{3,1},{1,0},{8,10},{10,12},{12... | collective-permute-start | bytes 2359304 | tf_op jit(solution)/shard_map/ppermute | solution.py:34
  53.4 18.8 %collective-permute-start.2 = (bf16[4,128,768]{2,1,0:T(8,128)(2,1)S(1)}, bf16[4,128,768]{2,1,0:T(8,128)(2,1)}, u32[]{:S(2)}, u32[]{:S(2)}) collective-permute-start(bf16[4,128,768]{2,1,0:T(8,128)(2,1)S(1)} %collective-permute-done.1), channel_id=1, source_target_pairs={{0,2},{2,4},{4,6},{6,7},{7,5},{5,3},{3,1},{1,0},{8,10},{10,12},{12... | collective-permute-start | bytes 2359304 | tf_op jit(solution)/shard_map/ppermute | solution.py:34
  55.3 40.2 %collective-permute-start.5 = (bf16[4,128,768]{2,1,0:T(8,128)(2,1)S(1)}, bf16[4,128,768]{2,1,0:T(8,128)(2,1)}, u32[]{:S(2)}, u32[]{:S(2)}) collective-permute-start(bf16[4,128,768]{2,1,0:T(8,128)(2,1)S(1)} %collective-permute-done.4), channel_id=1, source_target_pairs={{0,1},{2,0},{4,2},{6,4},{7,6},{5,7},{3,5},{1,3},{8,9},{10,8},{12,1... | collective-permute-start | bytes 2359304 | tf_op jit(solution)/shard_map/ppermute | solution.py:38
  72.2 26.5 %collective-permute-start.3 = (bf16[4,128,768]{2,1,0:T(8,128)(2,1)}, bf16[4,128,768]{2,1,0:T(8,128)(2,1)}, u32[]{:S(2)}, u32[]{:S(2)}) collective-permute-start(bf16[4,128,768]{2,1,0:T(8,128)(2,1)} %collective-permute-done.2), channel_id=1, source_target_pairs={{0,2},{2,4},{4,6},{6,7},{7,5},{5,3},{3,1},{1,0},{8,10},{10,12},{12... | collective-permute-start | bytes 2359304 | tf_op jit(solution)/shard_map/ppermute | solution.py:34
  95.4 17.6 %collective-permute-start.6 = (bf16[4,128,768]{2,1,0:T(8,128)(2,1)}, bf16[4,128,768]{2,1,0:T(8,128)(2,1)S(1)}, u32[]{:S(2)}, u32[]{:S(2)}) collective-permute-start(bf16[4,128,768]{2,1,0:T(8,128)(2,1)} %collective-permute-done.5), channel_id=1, source_target_pairs={{0,1},{2,0},{4,2},{6,4},{7,6},{5,7},{3,5},{1,3},{8,9},{10,8},{12,1... | collective-permute-start | bytes 2359304 | tf_op jit(solution)/shard_map/ppermute | solution.py:38
  98.6 29.2 %collective-permute-start.29 = (bf16[128,1536]{1,0:T(8,128)(2,1)S(1)}, bf16[128,1536]{1,0:T(8,128)(2,1)}, u32[]{:S(2)}, u32[]{:S(2)}) collective-permute-start(bf16[128,1536]{1,0:T(8,128)(2,1)S(1)} %constant_dynamic-slice_fusion.2.refs_8_), channel_id=1, source_target_pairs={{0,8},{8,0},{1,9},{9,1},{2,10},{10,2},{3,11},{11,3},{4,12},{12,4},... | collective-permute-start | bytes 1179656 | tf_op jit(solution)/shard_map/ppermute | solution.py:205
  98.7 29.3 %collective-permute-start.15 = (bf16[128,1536]{1,0:T(8,128)(2,1)}, bf16[128,1536]{1,0:T(8,128)(2,1)}, u32[]{:S(2)}, u32[]{:S(2)}) collective-permute-start(bf16[128,1536]{1,0:T(8,128)(2,1)} %collective-permute-done.14.refs_9_), channel_id=1, source_target_pairs={{0,2},{2,4},{4,6},{6,7},{7,5},{5,3},{3,1},{1,0},{8,10},{10,12},{12... | collective-permute-start | bytes 1179656 | tf_op jit(solution)/shard_map/ppermute | solution.py:34
  102.8 25.7 %collective-permute-start.22 = (bf16[128,1536]{1,0:T(8,128)(2,1)}, bf16[128,1536]{1,0:T(8,128)(2,1)S(1)}, u32[]{:S(2)}, u32[]{:S(2)}) collective-permute-start(bf16[128,1536]{1,0:T(8,128)(2,1)} %collective-permute-done.14.refs_9_), channel_id=1, source_target_pairs={{0,16},{16,0},{1,17},{17,1},{2,18},{18,2},{3,19},{19,3},{4,20},{20... | collective-permute-start | bytes 1179656 | tf_op jit(solution)/shard_map/ppermute | solution.py:201
  113.0 15.3 %collective-permute-start.19 = (bf16[128,1536]{1,0:T(8,128)(2,1)}, bf16[128,1536]{1,0:T(8,128)(2,1)S(1)}, u32[]{:S(2)}, u32[]{:S(2)}) collective-permute-start(bf16[128,1536]{1,0:T(8,128)(2,1)} %collective-permute-done.18.refs_13_), channel_id=1, source_target_pairs={{0,1},{2,0},{4,2},{6,4},{7,6},{5,7},{3,5},{1,3},{8,9},{10,8},{12,1... | collective-permute-start | bytes 1179656 | tf_op jit(solution)/shard_map/ppermute | solution.py:38
  117.9 12.2 %collective-permute-start.26 = (bf16[128,1536]{1,0:T(8,128)(2,1)}, bf16[128,1536]{1,0:T(8,128)(2,1)}, u32[]{:S(2)}, u32[]{:S(2)}) collective-permute-start(bf16[128,1536]{1,0:T(8,128)(2,1)} %collective-permute-done.18.refs_13_), channel_id=1, source_target_pairs={{0,16},{16,0},{1,17},{17,1},{2,18},{18,2},{3,19},{19,3},{4,20},{20... | collective-permute-start | bytes 1179656 | tf_op jit(solution)/shard_map/ppermute | solution.py:201
  128.5 11.7 %collective-permute-start.16 = (bf16[128,1536]{1,0:T(8,128)(2,1)}, bf16[128,1536]{1,0:T(8,128)(2,1)}, u32[]{:S(2)}, u32[]{:S(2)}) collective-permute-start(bf16[128,1536]{1,0:T(8,128)(2,1)} %collective-permute-done.15.refs_10_), channel_id=1, source_target_pairs={{0,2},{2,4},{4,6},{6,7},{7,5},{5,3},{3,1},{1,0},{8,10},{10,12},{12... | collective-permute-start | bytes 1179656 | tf_op jit(solution)/shard_map/ppermute | solution.py:34
  130.1 11.2 %collective-permute-start.20 = (bf16[128,1536]{1,0:T(8,128)(2,1)S(1)}, bf16[128,1536]{1,0:T(8,128)(2,1)}, u32[]{:S(2)}, u32[]{:S(2)}) collective-permute-start(bf16[128,1536]{1,0:T(8,128)(2,1)S(1)} %collective-permute-done.19.refs_14_), channel_id=1, source_target_pairs={{0,1},{2,0},{4,2},{6,4},{7,6},{5,7},{3,5},{1,3},{8,9},{10,8},{12,1... | collective-permute-start | bytes 1179656 | tf_op jit(solution)/shard_map/ppermute | solution.py:38
  131.9 12.3 %collective-permute-start.23 = (bf16[128,1536]{1,0:T(8,128)(2,1)}, bf16[128,1536]{1,0:T(8,128)(2,1)S(1)}, u32[]{:S(2)}, u32[]{:S(2)}) collective-permute-start(bf16[128,1536]{1,0:T(8,128)(2,1)} %collective-permute-done.15.refs_10_), channel_id=1, source_target_pairs={{0,16},{16,0},{1,17},{17,1},{2,18},{18,2},{3,19},{19,3},{4,20},{20... | collective-permute-start | bytes 1179656 | tf_op jit(solution)/shard_map/ppermute | solution.py:201
  132.8 18.7 %collective-permute-start.27 = (bf16[128,1536]{1,0:T(8,128)(2,1)S(1)}, bf16[128,1536]{1,0:T(8,128)(2,1)S(1)}, u32[]{:S(2)}, u32[]{:S(2)}) collective-permute-start(bf16[128,1536]{1,0:T(8,128)(2,1)S(1)} %collective-permute-done.19.refs_14_), channel_id=1, source_target_pairs={{0,16},{16,0},{1,17},{17,1},{2,18},{18,2},{3,19},{19,3},{4,20},{20... | collective-permute-start | bytes 1179656 | tf_op jit(solution)/shard_map/ppermute | solution.py:201
  134.0 19.0 %collective-permute-start.31 = (bf16[128,1536]{1,0:T(8,128)(2,1)}, bf16[128,1536]{1,0:T(8,128)(2,1)S(1)}, u32[]{:S(2)}, u32[]{:S(2)}) collective-permute-start(bf16[128,1536]{1,0:T(8,128)(2,1)} %collective-permute-done.15.refs_10_), channel_id=1, source_target_pairs={{0,8},{8,0},{1,9},{9,1},{2,10},{10,2},{3,11},{11,3},{4,12},{12,4},... | collective-permute-start | bytes 1179656 | tf_op jit(solution)/shard_map/ppermute | solution.py:205
  140.2 13.4 %collective-permute-start.35 = (bf16[128,1536]{1,0:T(8,128)(2,1)S(1)}, bf16[128,1536]{1,0:T(8,128)(2,1)S(1)}, u32[]{:S(2)}, u32[]{:S(2)}) collective-permute-start(bf16[128,1536]{1,0:T(8,128)(2,1)S(1)} %collective-permute-done.19.refs_14_), channel_id=1, source_target_pairs={{0,8},{8,0},{1,9},{9,1},{2,10},{10,2},{3,11},{11,3},{4,12},{12,4},... | collective-permute-start | bytes 1179656 | tf_op jit(solution)/shard_map/ppermute | solution.py:205
  141.3 12.3 %collective-permute-start.38 = (bf16[128,1536]{1,0:T(8,128)(2,1)S(1)}, bf16[128,1536]{1,0:T(8,128)(2,1)S(1)}, u32[]{:S(2)}, u32[]{:S(2)}) collective-permute-start(bf16[128,1536]{1,0:T(8,128)(2,1)S(1)} %collective-permute-done.22.refs_17_), channel_id=1, source_target_pairs={{0,8},{8,0},{1,9},{9,1},{2,10},{10,2},{3,11},{11,3},{4,12},{12,4},... | collective-permute-start | bytes 1179656 | tf_op jit(solution)/shard_map/ppermute | solution.py:206
  144.2 11.9 %collective-permute-start.42 = (bf16[128,1536]{1,0:T(8,128)(2,1)}, bf16[128,1536]{1,0:T(8,128)(2,1)S(1)}, u32[]{:S(2)}, u32[]{:S(2)}) collective-permute-start(bf16[128,1536]{1,0:T(8,128)(2,1)} %collective-permute-done.26.refs_21_), channel_id=1, source_target_pairs={{0,8},{8,0},{1,9},{9,1},{2,10},{10,2},{3,11},{11,3},{4,12},{12,4},... | collective-permute-start | bytes 1179656 | tf_op jit(solution)/shard_map/ppermute | solution.py:206
  151.5 10.2 %collective-permute-start.17 = (bf16[128,1536]{1,0:T(8,128)(2,1)}, bf16[128,1536]{1,0:T(8,128)(2,1)S(1)}, u32[]{:S(2)}, u32[]{:S(2)}) collective-permute-start(bf16[128,1536]{1,0:T(8,128)(2,1)} %collective-permute-done.16.refs_11_), channel_id=1, source_target_pairs={{0,2},{2,4},{4,6},{6,7},{7,5},{5,3},{3,1},{1,0},{8,10},{10,12},{12... | collective-permute-start | bytes 1179656 | tf_op jit(solution)/shard_map/ppermute | solution.py:34
  153.1 12.4 %collective-permute-start.24 = (bf16[128,1536]{1,0:T(8,128)(2,1)}, bf16[128,1536]{1,0:T(8,128)(2,1)}, u32[]{:S(2)}, u32[]{:S(2)}) collective-permute-start(bf16[128,1536]{1,0:T(8,128)(2,1)} %collective-permute-done.16.refs_11_), channel_id=1, source_target_pairs={{0,16},{16,0},{1,17},{17,1},{2,18},{18,2},{3,19},{19,3},{4,20},{20... | collective-permute-start | bytes 1179656 | tf_op jit(solution)/shard_map/ppermute | solution.py:201
  153.6 18.3 %collective-permute-start.32 = (bf16[128,1536]{1,0:T(8,128)(2,1)}, bf16[128,1536]{1,0:T(8,128)(2,1)S(1)}, u32[]{:S(2)}, u32[]{:S(2)}) collective-permute-start(bf16[128,1536]{1,0:T(8,128)(2,1)} %collective-permute-done.16.refs_11_), channel_id=1, source_target_pairs={{0,8},{8,0},{1,9},{9,1},{2,10},{10,2},{3,11},{11,3},{4,12},{12,4},... | collective-permute-start | bytes 1179656 | tf_op jit(solution)/shard_map/ppermute | solution.py:205
  153.6 17.7 %collective-permute-start.28 = (bf16[128,1536]{1,0:T(8,128)(2,1)}, bf16[128,1536]{1,0:T(8,128)(2,1)S(1)}, u32[]{:S(2)}, u32[]{:S(2)}) collective-permute-start(bf16[128,1536]{1,0:T(8,128)(2,1)} %collective-permute-done.20.refs_15_), channel_id=1, source_target_pairs={{0,16},{16,0},{1,17},{17,1},{2,18},{18,2},{3,19},{19,3},{4,20},{20... | collective-permute-start | bytes 1179656 | tf_op jit(solution)/shard_map/ppermute | solution.py:201
  156.1 16.3 %collective-permute-start.36 = (bf16[128,1536]{1,0:T(8,128)(2,1)}, bf16[128,1536]{1,0:T(8,128)(2,1)S(1)}, u32[]{:S(2)}, u32[]{:S(2)}) collective-permute-start(bf16[128,1536]{1,0:T(8,128)(2,1)} %collective-permute-done.20.refs_15_), channel_id=1, source_target_pairs={{0,8},{8,0},{1,9},{9,1},{2,10},{10,2},{3,11},{11,3},{4,12},{12,4},... | collective-permute-start | bytes 1179656 | tf_op jit(solution)/shard_map/ppermute | solution.py:205
  161.7 12.3 %collective-permute-start.39 = (bf16[128,1536]{1,0:T(8,128)(2,1)S(1)}, bf16[128,1536]{1,0:T(8,128)(2,1)S(1)}, u32[]{:S(2)}, u32[]{:S(2)}) collective-permute-start(bf16[128,1536]{1,0:T(8,128)(2,1)S(1)} %collective-permute-done.23.refs_18_), channel_id=1, source_target_pairs={{0,8},{8,0},{1,9},{9,1},{2,10},{10,2},{3,11},{11,3},{4,12},{12,4},... | collective-permute-start | bytes 1179656 | tf_op jit(solution)/shard_map/ppermute | solution.py:206
  165.4 8.8 %collective-permute-start.43 = (bf16[128,1536]{1,0:T(8,128)(2,1)S(1)}, bf16[128,1536]{1,0:T(8,128)(2,1)S(1)}, u32[]{:S(2)}, u32[]{:S(2)}) collective-permute-start(bf16[128,1536]{1,0:T(8,128)(2,1)S(1)} %collective-permute-done.27.refs_22_), channel_id=1, source_target_pairs={{0,8},{8,0},{1,9},{9,1},{2,10},{10,2},{3,11},{11,3},{4,12},{12,4},... | collective-permute-start | bytes 1179656 | tf_op jit(solution)/shard_map/ppermute | solution.py:206
  171.3 8.8 %collective-permute-start.25 = (bf16[128,1536]{1,0:T(8,128)(2,1)S(1)}, bf16[128,1536]{1,0:T(8,128)(2,1)}, u32[]{:S(2)}, u32[]{:S(2)}) collective-permute-start(bf16[128,1536]{1,0:T(8,128)(2,1)S(1)} %collective-permute-done.17.refs_12_), channel_id=1, source_target_pairs={{0,16},{16,0},{1,17},{17,1},{2,18},{18,2},{3,19},{19,3},{4,20},{20... | collective-permute-start | bytes 1179656 | tf_op jit(solution)/shard_map/ppermute | solution.py:201
  171.9 8.3 %collective-permute-start.33 = (bf16[128,1536]{1,0:T(8,128)(2,1)S(1)}, bf16[128,1536]{1,0:T(8,128)(2,1)S(1)}, u32[]{:S(2)}, u32[]{:S(2)}) collective-permute-start(bf16[128,1536]{1,0:T(8,128)(2,1)S(1)} %collective-permute-done.17.refs_12_), channel_id=1, source_target_pairs={{0,8},{8,0},{1,9},{9,1},{2,10},{10,2},{3,11},{11,3},{4,12},{12,4},... | collective-permute-start | bytes 1179656 | tf_op jit(solution)/shard_map/ppermute | solution.py:205
  172.4 8.4 %collective-permute-start.7 = (bf16[512,128]{1,0:T(8,128)(2,1)S(1)}, bf16[512,128]{1,0:T(8,128)(2,1)S(1)}, u32[]{:S(2)}, u32[]{:S(2)}) collective-permute-start(bf16[512,128]{1,0:T(8,128)(2,1)S(1)} %bitcast.159), channel_id=1, source_target_pairs={{0,2},{2,4},{4,6},{6,7},{7,5},{5,3},{3,1},{1,0},{8,10},{10,12},{12... | collective-permute-start | bytes 393224 | tf_op jit(solution)/shard_map/ppermute | solution.py:34
  174.0 20.9 %collective-permute-start.40 = (bf16[128,1536]{1,0:T(8,128)(2,1)}, bf16[128,1536]{1,0:T(8,128)(2,1)}, u32[]{:S(2)}, u32[]{:S(2)}) collective-permute-start(bf16[128,1536]{1,0:T(8,128)(2,1)} %collective-permute-done.24.refs_19_), channel_id=1, source_target_pairs={{0,8},{8,0},{1,9},{9,1},{2,10},{10,2},{3,11},{11,3},{4,12},{12,4},... | collective-permute-start | bytes 1179656 | tf_op jit(solution)/shard_map/ppermute | solution.py:206
  174.2 20.7 %collective-permute-start.44 = (bf16[128,1536]{1,0:T(8,128)(2,1)S(1)}, bf16[128,1536]{1,0:T(8,128)(2,1)}, u32[]{:S(2)}, u32[]{:S(2)}) collective-permute-start(bf16[128,1536]{1,0:T(8,128)(2,1)S(1)} %collective-permute-done.28.refs_23_), channel_id=1, source_target_pairs={{0,8},{8,0},{1,9},{9,1},{2,10},{10,2},{3,11},{11,3},{4,12},{12,4},... | collective-permute-start | bytes 1179656 | tf_op jit(solution)/shard_map/ppermute | solution.py:206
  180.2 14.8 %collective-permute-start.41 = (bf16[128,1536]{1,0:T(8,128)(2,1)}, bf16[128,1536]{1,0:T(8,128)(2,1)}, u32[]{:S(2)}, u32[]{:S(2)}) collective-permute-start(bf16[128,1536]{1,0:T(8,128)(2,1)} %collective-permute-done.25.refs_20_), channel_id=1, source_target_pairs={{0,8},{8,0},{1,9},{9,1},{2,10},{10,2},{3,11},{11,3},{4,12},{12,4},... | collective-permute-start | bytes 1179656 | tf_op jit(solution)/shard_map/ppermute | solution.py:206
  252.4 8.8 %collective-permute-start.45 = (bf16[512,384]{1,0:T(8,128)(2,1)S(1)}, bf16[512,384]{1,0:T(8,128)(2,1)S(1)}, u32[]{:S(2)}, u32[]{:S(2)}) collective-permute-start(bf16[512,384]{1,0:T(8,128)(2,1)S(1)} %get-tuple-element.21), channel_id=1, source_target_pairs={{0,2},{2,4},{4,6},{6,7},{7,5},{5,3},{3,1},{1,0},{8,10},{10,12},{12... | collective-permute-start | bytes 1179656 | tf_op jit(solution)/shard_map/ppermute | solution.py:61
  254.0 8.4 %collective-permute-start.52 = (bf16[512,384]{1,0:T(8,128)(2,1)S(1)}, bf16[512,384]{1,0:T(8,128)(2,1)S(1)}, u32[]{:S(2)}, u32[]{:S(2)}) collective-permute-start(bf16[512,384]{1,0:T(8,128)(2,1)S(1)} %get-tuple-element.22), channel_id=1, source_target_pairs={{0,1},{2,0},{4,2},{6,4},{7,6},{5,7},{3,5},{1,3},{8,9},{10,8},{12,1... | collective-permute-start | bytes 1179656 | tf_op jit(solution)/shard_map/ppermute | solution.py:63
  274.5 8.4 %collective-permute-start.47 = (bf16[512,384]{1,0:T(8,128)(2,1)S(1)}, bf16[512,384]{1,0:T(8,128)(2,1)S(1)}, u32[]{:S(2)}, u32[]{:S(2)}) collective-permute-start(bf16[512,384]{1,0:T(8,128)(2,1)S(1)} %get-tuple-element.17), channel_id=1, source_target_pairs={{0,2},{2,4},{4,6},{6,7},{7,5},{5,3},{3,1},{1,0},{8,10},{10,12},{12... | collective-permute-start | bytes 1179656 | tf_op jit(solution)/shard_map/ppermute | solution.py:61
  276.0 8.7 %collective-permute-start.54 = (bf16[512,384]{1,0:T(8,128)(2,1)S(1)}, bf16[512,384]{1,0:T(8,128)(2,1)S(1)}, u32[]{:S(2)}, u32[]{:S(2)}) collective-permute-start(bf16[512,384]{1,0:T(8,128)(2,1)S(1)} %get-tuple-element.18), channel_id=1, source_target_pairs={{0,1},{2,0},{4,2},{6,4},{7,6},{5,7},{3,5},{1,3},{8,9},{10,8},{12,1... | collective-permute-start | bytes 1179656 | tf_op jit(solution)/shard_map/ppermute | solution.py:63
  286.1 10.1 %collective-permute-start.48 = (bf16[512,384]{1,0:T(8,128)(2,1)S(1)}, bf16[512,384]{1,0:T(8,128)(2,1)S(1)}, u32[]{:S(2)}, u32[]{:S(2)}) collective-permute-start(bf16[512,384]{1,0:T(8,128)(2,1)S(1)} %get-tuple-element.15), channel_id=1, source_target_pairs={{0,2},{2,4},{4,6},{6,7},{7,5},{5,3},{3,1},{1,0},{8,10},{10,12},{12... | collective-permute-start | bytes 1179656 | tf_op jit(solution)/shard_map/ppermute | solution.py:61
  288.2 10.7 %collective-permute-start.55 = (bf16[512,384]{1,0:T(8,128)(2,1)S(1)}, bf16[512,384]{1,0:T(8,128)(2,1)S(1)}, u32[]{:S(2)}, u32[]{:S(2)}) collective-permute-start(bf16[512,384]{1,0:T(8,128)(2,1)S(1)} %get-tuple-element.16), channel_id=1, source_target_pairs={{0,1},{2,0},{4,2},{6,4},{7,6},{5,7},{3,5},{1,3},{8,9},{10,8},{12,1... | collective-permute-start | bytes 1179656 | tf_op jit(solution)/shard_map/ppermute | solution.py:63
  300.3 11.9 %collective-permute-start.49 = (bf16[512,384]{1,0:T(8,128)(2,1)S(1)}, bf16[512,384]{1,0:T(8,128)(2,1)S(1)}, u32[]{:S(2)}, u32[]{:S(2)}) collective-permute-start(bf16[512,384]{1,0:T(8,128)(2,1)S(1)} %get-tuple-element.13), channel_id=1, source_target_pairs={{0,2},{2,4},{4,6},{6,7},{7,5},{5,3},{3,1},{1,0},{8,10},{10,12},{12... | collective-permute-start | bytes 1179656 | tf_op jit(solution)/shard_map/ppermute | solution.py:61
  301.4 11.7 %collective-permute-start.56 = (bf16[512,384]{1,0:T(8,128)(2,1)S(1)}, bf16[512,384]{1,0:T(8,128)(2,1)S(1)}, u32[]{:S(2)}, u32[]{:S(2)}) collective-permute-start(bf16[512,384]{1,0:T(8,128)(2,1)S(1)} %get-tuple-element.14), channel_id=1, source_target_pairs={{0,1},{2,0},{4,2},{6,4},{7,6},{5,7},{3,5},{1,3},{8,9},{10,8},{12,1... | collective-permute-start | bytes 1179656 | tf_op jit(solution)/shard_map/ppermute | solution.py:63
  314.4 11.4 %collective-permute-start.50 = (bf16[512,384]{1,0:T(8,128)(2,1)S(1)}, bf16[512,384]{1,0:T(8,128)(2,1)S(1)}, u32[]{:S(2)}, u32[]{:S(2)}) collective-permute-start(bf16[512,384]{1,0:T(8,128)(2,1)S(1)} %get-tuple-element.11), channel_id=1, source_target_pairs={{0,2},{2,4},{4,6},{6,7},{7,5},{5,3},{3,1},{1,0},{8,10},{10,12},{12... | collective-permute-start | bytes 1179656 | tf_op jit(solution)/shard_map/ppermute | solution.py:61
  314.8 11.9 %collective-permute-start.57 = (bf16[512,384]{1,0:T(8,128)(2,1)S(1)}, bf16[512,384]{1,0:T(8,128)(2,1)}, u32[]{:S(2)}, u32[]{:S(2)}) collective-permute-start(bf16[512,384]{1,0:T(8,128)(2,1)S(1)} %get-tuple-element.12), channel_id=1, source_target_pairs={{0,1},{2,0},{4,2},{6,4},{7,6},{5,7},{3,5},{1,3},{8,9},{10,8},{12,1... | collective-permute-start | bytes 1179656 | tf_op jit(solution)/shard_map/ppermute | solution.py:63
  (51 other events, 896.2 us)
Sparse Core Ops, SparseCore 0:
  8.9 18.3 all-gather.2
  28.8 17.9 all-gather.4

commit v9 on v7

--- a/solution.py
+++ b/solution.py
@@ -63,6 +63,16 @@
         backward = lax.ppermute(backward.astype(jnp.bfloat16), axis_name, behind).astype(jnp.float32)
         backward = backward + own_part(position + 2 + step, 1)
     return jnp.concatenate([forward, backward], axis=1)
+
+
+def direct_gather(block, axis_name, count):
+    cycle = snake_cycle(count)
+    shifts = list(range(1, count // 2 + 1)) + [-k for k in range(1, (count - 1) // 2 + 1)]
+    blocks = [block]
+    for shift in shifts:
+        pairs = [(cycle[(p - shift) % count], cycle[p]) for p in range(count)]
+        blocks.append(lax.ppermute(block, axis_name, pairs))
+    return blocks
 
 
 def out_proj_kernel(group_count, tiles_per_half, span_ref, *refs):
@@ -230,7 +240,7 @@
         lambda q_rows, c_seen, f_seen: attend(q_rows, cache_all, fresh_all, c_seen, f_seen)
     )(queries, cache_seen, fresh_seen)
     if gather_weights:
-        att_blocks = ring_gather(attended.reshape(token_count, per_device), "tp", tp_count)
+        att_blocks = direct_gather(attended.reshape(token_count, per_device), "tp", tp_count)
         attn_out = grouped_out_proj(span_index, att_blocks, mine_blocks, other_blocks)
         attn_out = attn_out.reshape(local_count, row_count, model_width)
         residual_full = gathered + mod_rows[:, 2][:, None] * attn_out

time: 334 us -> 337 us (level)
  starting transfers between devices: 40 us -> 53 us
  waiting for transfers between devices: 158 us -> 146 us
    ppermute x0 -> x7, starting transfers between devices: none -> 19.3 us  [direct_gather(): blocks.append(lax.ppermute(block, axis_name, pairs))]
    ppermute x12 -> x8, waiting for transfers between devices: 79.3 us -> 62.1 us  [ring_gather(): forward = lax.ppermute(forward, axis_name, ahead)]
    ppermute x0 -> x7, waiting for transfers between devices: none -> 10.6 us  [direct_gather(): blocks.append(lax.ppermute(block, axis_name, pairs))]
    ppermute x12 -> x8, starting transfers between devices: 21.6 us -> 14.7 us  [ring_gather(): forward = lax.ppermute(forward, axis_name, ahead)]
    ppermute x7, waiting for transfers between devices: 51.2 us -> 46.6 us  [ring_reduce_scatter(): lax.ppermute(forward.astype(jnp.bfloat16), axis_name, ahead)]
    ppermute x9 -> x6, waiting for transfers between devices: 21.1 us -> 20.8 us  [ring_gather(): backward = lax.ppermute(backward, axis_name, behind)]
  transfers between devices with their start and end apart: 45 -> 45, of which waited for: 24 -> 23; matrix products, arithmetic and copies ran while one was open for 17% -> 17% of each run, Pallas kernels for 6% -> 6%
where the time goes in v9:
time: 337 us; the launch traced here: 335 us
  waiting for transfers between devices  146 us (43%)
  starting transfers between devices  53 us (16%)
  between operations  32.5 us (10%)
  other arithmetic  31.7 us (9%)
  matrix products  24.8 us (7%)
  local copies, waits for them, and re-layouts  22.4 us (7%)
  Pallas kernels  20.4 us (6%)
  blocking collectives  4.54 us (1%)
    ppermute x8, waiting for transfers between devices, ring_gather(): forward = lax.ppermute(forward, axis_name, ahead)  62.1 us
    ppermute x7, waiting for transfers between devices, ring_reduce_scatter(): lax.ppermute(forward.astype(jnp.bfloat16), axis_name, ahead)  46.6 us
    ppermute x6, waiting for transfers between devices, ring_gather(): backward = lax.ppermute(backward, axis_name, behind)  20.8 us
    pallas_call x1, Pallas kernels, grouped_out_proj(): pl.pallas_call(functools.partial(out_proj_kernel, group_count, tiles_per_...  20.4 us
    ppermute x7, starting transfers between devices, direct_gather(): blocks.append(lax.ppermute(block, axis_name, pairs))  19.3 us
    ppermute x8, starting transfers between devices, ring_gather(): forward = lax.ppermute(forward, axis_name, ahead)  14.7 us
    reduce_sum x2, other arithmetic, normalize(): jnp.mean(values * values, axis=-1, keepdims=True) + EPSILON  14.7 us
    unnamed x55, local copies, waits for them, and re-layouts  11.2 us
  transfers between devices with their start and end apart: 45, of which 23 were waited for; matrix products, arithmetic and copies ran while one was open for 17% of the time, Pallas kernels for 6%

profile of v9, /device:TPU:0, one launch (start us, length us, event | category | flops | bytes accessed | tf_op | source)
XLA Modules:
  0.0 335.4 jit_solution(494618404042830548)
XLA Ops:
  7.4 3.1 collective-permute-start
  10.5 2.1 collective-permute-start.14
  14.4 14.7 %collective-permute-done = bf16[4,128,768]{2,1,0:T(8,128)(2,1)} collective-permute-done((bf16[4,128,768]{2,1,0:T(8,128)(2,1)}, bf16[4,128,768]{2,1,0:T(8,128)(2,1)}, u32[]{:S(2)}, u32[]{:S(2)}) %collective-permute-start) | collective-permute-done | bytes 786464 | tf_op jit(solution)/shard_map/ppermute | solution.py:34
  29.1 2.1 collective-permute-start.1
  31.5 30.3 %collective-permute-done.1 = bf16[4,128,768]{2,1,0:T(8,128)(2,1)S(1)} collective-permute-done((bf16[4,128,768]{2,1,0:T(8,128)(2,1)}, bf16[4,128,768]{2,1,0:T(8,128)(2,1)S(1)}, u32[]{:S(2)}, u32[]{:S(2)}) %collective-permute-start.1) | collective-permute-done | bytes 786464 | tf_op jit(solution)/shard_map/ppermute | solution.py:34
  61.8 1.8 collective-permute-start.2
  64.0 1.8 collective-permute-start.15
  67.1 2.2 all_gather.12
  69.4 13.0 %collective-permute-done.2 = bf16[4,128,768]{2,1,0:T(8,128)(2,1)} collective-permute-done((bf16[4,128,768]{2,1,0:T(8,128)(2,1)S(1)}, bf16[4,128,768]{2,1,0:T(8,128)(2,1)}, u32[]{:S(2)}, u32[]{:S(2)}) %collective-permute-start.2) | collective-permute-done | bytes 786464 | tf_op jit(solution)/shard_map/ppermute | solution.py:34
  82.4 1.8 collective-permute-start.3
  98.3 6.8 %copy.30 = bf16[6144,3,128]{0,2,1:T(8,128)(2,1)} copy(bf16[6144,3,128]{2,0,1:T(8,128)(2,1)} %param.22) | data formatting | bytes 9437184 | tf_op args[7]
  106.3 1.7 collective-permute-start.6
  112.1 4.1 %collective-permute-done.3 = bf16[4,128,768]{2,1,0:T(8,128)(2,1)} collective-permute-done((bf16[4,128,768]{2,1,0:T(8,128)(2,1)}, bf16[4,128,768]{2,1,0:T(8,128)(2,1)}, u32[]{:S(2)}, u32[]{:S(2)}) %collective-permute-start.3) | collective-permute-done | bytes 786464 | tf_op jit(solution)/shard_map/ppermute | solution.py:34
  119.9 7.0 %collective-permute-done.19.refs_14_ = bf16[128,3072]{1,0:T(8,128)(2,1)} collective-permute-done((bf16[128,3072]{1,0:T(8,128)(2,1)}, bf16[128,3072]{1,0:T(8,128)(2,1)}, u32[]{:S(2)}, u32[]{:S(2)}) %collective-permute-start.19) | collective-permute-done | bytes 786464 | tf_op jit(solution)/shard_map/ppermute | solution.py:38
  126.9 13.8 %collective-permute-done.6 = bf16[4,128,768]{2,1,0:T(8,128)(2,1)S(1)} collective-permute-done((bf16[4,128,768]{2,1,0:T(8,128)(2,1)}, bf16[4,128,768]{2,1,0:T(8,128)(2,1)S(1)}, u32[]{:S(2)}, u32[]{:S(2)}) %collective-permute-start.6) | collective-permute-done | bytes 786464 | tf_op jit(solution)/shard_map/ppermute | solution.py:38
  140.9 1.8 collective-permute-start.17
  144.1 2.7 fusion.3
  146.8 5.8 %convolution_convert_fusion.1 = bf16[512,384]{1,0:T(8,128)(2,1)S(1)} fusion(bf16[512,6144]{1,0:T(8,128)(2,1)S(1)} %bitcast.150, bf16[6144,384]{0,1:T(8,128)(2,1)} %bitcast.151), kind=kOutput, calls=%fused_computation.29 | convolution fusion | flops 2416115712 | bytes 11403264 | tf_op jit(solution)/shard_map/dot_general | solution.py:219
  153.5 2.4 all_gather.13
  161.0 3.5 %collective-permute-start.10 = (bf16[512,128]{1,0:T(8,128)(2,1)S(1)}, bf16[512,128]{1,0:T(8,128)(2,1)S(1)}, u32[]{:S(2)}, u32[]{:S(2)}) collective-permute-start(bf16[512,128]{1,0:T(8,128)(2,1)S(1)} %bitcast.156), channel_id=1, source_target_pairs={{7,0},{5,2},{3,4},{1,6},{0,7},{2,5},{4,3},{6,1},{15,8},{13,10},{11... | collective-permute-start | bytes 393224 | tf_op jit(solution)/shard_map/ppermute | solution.py:74
  164.5 1.6 collective-permute-start.11
  166.4 3.6 %collective-permute-start.13 = (bf16[512,128]{1,0:T(8,128)(2,1)S(1)}, bf16[512,128]{1,0:T(8,128)(2,1)}, u32[]{:S(2)}, u32[]{:S(2)}) collective-permute-start(bf16[512,128]{1,0:T(8,128)(2,1)S(1)} %bitcast.159), channel_id=1, source_target_pairs={{6,0},{7,2},{5,4},{3,6},{1,7},{0,5},{2,3},{4,1},{14,8},{15,10},{13... | collective-permute-start | bytes 393224 | tf_op jit(solution)/shard_map/ppermute | solution.py:74
  170.0 2.2 collective-permute-start.7
  172.1 6.9 %collective-permute-start.8 = (bf16[512,128]{1,0:T(8,128)(2,1)S(1)}, bf16[512,128]{1,0:T(8,128)(2,1)}, u32[]{:S(2)}, u32[]{:S(2)}) collective-permute-start(bf16[512,128]{1,0:T(8,128)(2,1)S(1)} %bitcast.161), channel_id=1, source_target_pairs={{3,0},{1,2},{0,4},{2,6},{4,7},{6,5},{7,3},{5,1},{11,8},{9,10},{8,1... | collective-permute-start | bytes 393224 | tf_op jit(solution)/shard_map/ppermute | solution.py:74
  179.0 3.3 collective-permute-done.12.refs_6_
  185.2 7.0 %collective-permute-done.9.refs_3_ = bf16[512,128]{1,0:T(8,128)(2,1)} collective-permute-done((bf16[512,128]{1,0:T(8,128)(2,1)S(1)}, bf16[512,128]{1,0:T(8,128)(2,1)}, u32[]{:S(2)}, u32[]{:S(2)}) %collective-permute-start.9) | collective-permute-done | bytes 131104 | tf_op jit(solution)/shard_map/ppermute | solution.py:74
  192.3 20.4 %shard_map.145 = f32[512,6144]{1,0:T(8,128)} custom-call(s32[1]{0:T(128)} %bitcast.21.span_ref, bf16[512,128]{1,0:T(8,128)(2,1)} %bitcast.163, bf16[512,128]{1,0:T(8,128)(2,1)} %collective-permute-done.7.refs_1_, bf16[512,128]{1,0:T(8,128)(2,1)} %collective-permute-done.8.refs_2_, bf16[512,128]{1,0:T(8,128)(2,1)} %collective-permute-done.9.refs_3_, ...), custom_call_target="tpu_custom_call" | custom-call | flops 6442450944 | bytes 26214400 | tf_op jit(solution)/shard_map/pallas_call | solution.py:121
  212.6 13.4 %multiply_reduce_fusion = (f32[4,128]{1,0:T(4,128)S(1)}, f32[4,128,6144]{2,1,0:T(8,128)}) fusion(f32[4,128,6144]{2,1,0:T(8,128)} %bitcast.140, f32[4,6144]{1,0:T(4,128)S(1)} %get-tuple-element.31, bf16[4,128,6144]{2,1,0:T(8,128)(2,1)} %copy-done.2), kind=kLoop, calls=%fused_computation.8 | loop fusion | flops 15728128 | bytes 31557632 | tf_op jit(solution)/shard_map/reduce_sum | solution.py:20
  226.1 10.0 %fusion.27 = bf16[4,128,512]{2,1,0:T(8,128)(2,1)S(1)} fusion(bf16[6144,512]{1,0:T(8,128)(2,1)} %all-gather.3.cloned.1.call-done, f32[4,128,6144]{2,1,0:T(8,128)} %get-tuple-element.6, f32[4,6144]{1,0:T(4,128)S(1)} %copy-done.19, f32[4,6144]{1,0:T(4,128)S(1)} %copy-done.18, f32[4,128]{1,0:T(4,128)S(1)} %add_rsqrt_fusion), kind=kOutput, calls=%fused_computation.40 | convolution fusion | flops 3236167680 | bytes 19597312 | tf_op jit(solution)/shard_map/dot_general | solution.py:265
  236.1 6.4 %convolution_convert_fusion = bf16[4,128,6144]{2,1,0:T(8,128)(2,1)S(1)} fusion(bf16[4,128,512]{2,1,0:T(8,128)(2,1)S(1)} %fusion.27, bf16[512,6144]{1,0:T(8,128)(2,1)} %all-gather.5.cloned.1.call-done), kind=kOutput, calls=%fused_computation.9 | convolution fusion | flops 3224371200 | bytes 13107200 | tf_op jit(solution)/shard_map/dot_general | solution.py:267
  242.6 2.6 copy-done.3
  245.4 2.0 collective-permute-start.36
  248.6 7.8 %collective-permute-done.29 = bf16[512,384]{1,0:T(8,128)(2,1)S(1)} collective-permute-done((bf16[512,384]{1,0:T(8,128)(2,1)S(1)}, bf16[512,384]{1,0:T(8,128)(2,1)S(1)}, u32[]{:S(2)}, u32[]{:S(2)}) %collective-permute-start.29) | collective-permute-done | bytes 393248 | tf_op jit(solution)/shard_map/ppermute | solution.py:61
  258.0 1.8 collective-permute-start.37
  261.2 6.8 %collective-permute-done.30 = bf16[512,384]{1,0:T(8,128)(2,1)S(1)} collective-permute-done((bf16[512,384]{1,0:T(8,128)(2,1)S(1)}, bf16[512,384]{1,0:T(8,128)(2,1)S(1)}, u32[]{:S(2)}, u32[]{:S(2)}) %collective-permute-start.30) | collective-permute-done | bytes 393248 | tf_op jit(solution)/shard_map/ppermute | solution.py:61
  268.3 1.3 add_convert_fusion.17
  272.3 6.6 %collective-permute-done.31 = bf16[512,384]{1,0:T(8,128)(2,1)S(1)} collective-permute-done((bf16[512,384]{1,0:T(8,128)(2,1)S(1)}, bf16[512,384]{1,0:T(8,128)(2,1)S(1)}, u32[]{:S(2)}, u32[]{:S(2)}) %collective-permute-start.31) | collective-permute-done | bytes 393248 | tf_op jit(solution)/shard_map/ppermute | solution.py:61
  282.6 6.1 %collective-permute-done.32 = bf16[512,384]{1,0:T(8,128)(2,1)S(1)} collective-permute-done((bf16[512,384]{1,0:T(8,128)(2,1)S(1)}, bf16[512,384]{1,0:T(8,128)(2,1)S(1)}, u32[]{:S(2)}, u32[]{:S(2)}) %collective-permute-start.32) | collective-permute-done | bytes 393248 | tf_op jit(solution)/shard_map/ppermute | solution.py:61
  292.7 6.8 %collective-permute-done.33 = bf16[512,384]{1,0:T(8,128)(2,1)S(1)} collective-permute-done((bf16[512,384]{1,0:T(8,128)(2,1)S(1)}, bf16[512,384]{1,0:T(8,128)(2,1)S(1)}, u32[]{:S(2)}, u32[]{:S(2)}) %collective-permute-start.33) | collective-permute-done | bytes 393248 | tf_op jit(solution)/shard_map/ppermute | solution.py:61
  300.1 1.3 add_convert_fusion.14
  302.2 1.3 collective-permute-start.41
  303.5 7.2 %collective-permute-done.34 = bf16[512,384]{1,0:T(8,128)(2,1)S(1)} collective-permute-done((bf16[512,384]{1,0:T(8,128)(2,1)S(1)}, bf16[512,384]{1,0:T(8,128)(2,1)S(1)}, u32[]{:S(2)}, u32[]{:S(2)}) %collective-permute-start.34) | collective-permute-done | bytes 393248 | tf_op jit(solution)/shard_map/ppermute | solution.py:61
  312.4 1.6 add_convert_fusion.13
  314.0 2.6 collective-permute-start.35
  316.5 5.3 %collective-permute-done.35 = bf16[512,384]{1,0:T(8,128)(2,1)S(1)} collective-permute-done((bf16[512,384]{1,0:T(8,128)(2,1)S(1)}, bf16[512,384]{1,0:T(8,128)(2,1)S(1)}, u32[]{:S(2)}, u32[]{:S(2)}) %collective-permute-start.35) | collective-permute-done | bytes 393248 | tf_op jit(solution)/shard_map/ppermute | solution.py:61
  321.8 2.6 collective-permute-done.42
  324.4 1.4 convert_add_fusion.2
  325.9 2.6 add_convert_fusion.2
  (156 shorter events, 38.2 us)
Async XLA Ops:
  6.5 85.9 %copy-start.17 = (s32[8]{0:T(128)S(1)}, s32[8]{0:T(128)}, u32[]{:S(2)}) copy-start(s32[8]{0:T(128)} %constant.289.clone) | copy-start | bytes 100
  6.6 60.5 %copy-start.12 = (bf16[4,128,2,128]{3,2,1,0:T(2,128)(2,1)S(1)}, bf16[4,128,2,128]{3,2,1,0:T(2,128)(2,1)}, u32[]{:S(2)}) copy-start(bf16[4,128,2,128]{3,2,1,0:T(2,128)(2,1)} %param.20) | copy-start | bytes 786436
  6.6 219.5 %all-gather.3.cloned.1.call-start = ((), (), s32[]{:S(2)}) async-start(), calls=%async_computation | async-start | bytes 9437184 | tf_op jit(solution)/shard_map/all_gather | solution.py:205
  7.3 228.8 %all-gather.5.cloned.1.call-start = ((), (), s32[]{:S(2)}) async-start(), calls=%async_computation.1 | async-start | bytes 9437184 | tf_op jit(solution)/shard_map/all_gather | solution.py:206
  7.4 21.7 %collective-permute-start = (bf16[4,128,768]{2,1,0:T(8,128)(2,1)}, bf16[4,128,768]{2,1,0:T(8,128)(2,1)}, u32[]{:S(2)}, u32[]{:S(2)}) collective-permute-start(bf16[4,128,768]{2,1,0:T(8,128)(2,1)} %param.15), channel_id=1, source_target_pairs={{0,2},{2,4},{4,6},{6,7},{7,5},{5,3},{3,1},{1,0},{8,10},{10,12},{12... | collective-permute-start | bytes 2359304 | tf_op jit(solution)/shard_map/ppermute | solution.py:34
  10.4 53.3 %collective-permute-start.4 = (bf16[4,128,768]{2,1,0:T(8,128)(2,1)}, bf16[4,128,768]{2,1,0:T(8,128)(2,1)}, u32[]{:S(2)}, u32[]{:S(2)}) collective-permute-start(bf16[4,128,768]{2,1,0:T(8,128)(2,1)} %param.15), channel_id=1, source_target_pairs={{0,1},{2,0},{4,2},{6,4},{7,6},{5,7},{3,5},{1,3},{8,9},{10,8},{12,1... | collective-permute-start | bytes 2359304 | tf_op jit(solution)/shard_map/ppermute | solution.py:38
  10.5 94.5 %copy-start.4 = (bf16[128,3072]{1,0:T(8,128)(2,1)}, bf16[128,3072]{1,0:T(8,128)(2,1)S(1)}, u32[]{:S(2)}) copy-start(bf16[128,3072]{1,0:T(8,128)(2,1)S(1)} %constant_dynamic-slice_fusion.2.refs_8_) | copy-start | bytes 2359300
  10.5 53.4 %collective-permute-start.14 = (bf16[128,3072]{1,0:T(8,128)(2,1)S(1)}, bf16[128,3072]{1,0:T(8,128)(2,1)}, u32[]{:S(2)}, u32[]{:S(2)}) collective-permute-start(bf16[128,3072]{1,0:T(8,128)(2,1)S(1)} %constant_dynamic-slice_fusion.2.refs_8_), channel_id=1, source_target_pairs={{0,2},{2,4},{4,6},{6,7},{7,5},{5,3},{3,1},{1,0},{8,10},{10,12},{12... | collective-permute-start | bytes 2359304 | tf_op jit(solution)/shard_map/ppermute | solution.py:34
  12.6 93.4 %collective-permute-start.18 = (bf16[128,3072]{1,0:T(8,128)(2,1)S(1)}, bf16[128,3072]{1,0:T(8,128)(2,1)}, u32[]{:S(2)}, u32[]{:S(2)}) collective-permute-start(bf16[128,3072]{1,0:T(8,128)(2,1)S(1)} %constant_dynamic-slice_fusion.2.refs_8_), channel_id=1, source_target_pairs={{0,1},{2,0},{4,2},{6,4},{7,6},{5,7},{3,5},{1,3},{8,9},{10,8},{12,1... | collective-permute-start | bytes 2359304 | tf_op jit(solution)/shard_map/ppermute | solution.py:38
  12.6 145.3 %collective-permute-start.21 = (bf16[128,3072]{1,0:T(8,128)(2,1)S(1)}, bf16[128,3072]{1,0:T(8,128)(2,1)}, u32[]{:S(2)}, u32[]{:S(2)}) collective-permute-start(bf16[128,3072]{1,0:T(8,128)(2,1)S(1)} %constant_dynamic-slice_fusion.2.refs_8_), channel_id=1, source_target_pairs={{0,8},{8,0},{1,9},{9,1},{2,10},{10,2},{3,11},{11,3},{4,12},{12,4},... | collective-permute-start | bytes 2359304 | tf_op jit(solution)/shard_map/ppermute | solution.py:203
  29.1 32.8 %collective-permute-start.1 = (bf16[4,128,768]{2,1,0:T(8,128)(2,1)}, bf16[4,128,768]{2,1,0:T(8,128)(2,1)S(1)}, u32[]{:S(2)}, u32[]{:S(2)}) collective-permute-start(bf16[4,128,768]{2,1,0:T(8,128)(2,1)} %collective-permute-done), channel_id=1, source_target_pairs={{0,2},{2,4},{4,6},{6,7},{7,5},{5,3},{3,1},{1,0},{8,10},{10,12},{12... | collective-permute-start | bytes 2359304 | tf_op jit(solution)/shard_map/ppermute | solution.py:34
  61.8 20.6 %collective-permute-start.2 = (bf16[4,128,768]{2,1,0:T(8,128)(2,1)S(1)}, bf16[4,128,768]{2,1,0:T(8,128)(2,1)}, u32[]{:S(2)}, u32[]{:S(2)}) collective-permute-start(bf16[4,128,768]{2,1,0:T(8,128)(2,1)S(1)} %collective-permute-done.1), channel_id=1, source_target_pairs={{0,2},{2,4},{4,6},{6,7},{7,5},{5,3},{3,1},{1,0},{8,10},{10,12},{12... | collective-permute-start | bytes 2359304 | tf_op jit(solution)/shard_map/ppermute | solution.py:34
  63.7 42.6 %collective-permute-start.5 = (bf16[4,128,768]{2,1,0:T(8,128)(2,1)}, bf16[4,128,768]{2,1,0:T(8,128)(2,1)}, u32[]{:S(2)}, u32[]{:S(2)}) collective-permute-start(bf16[4,128,768]{2,1,0:T(8,128)(2,1)} %collective-permute-done.4), channel_id=1, source_target_pairs={{0,1},{2,0},{4,2},{6,4},{7,6},{5,7},{3,5},{1,3},{8,9},{10,8},{12,1... | collective-permute-start | bytes 2359304 | tf_op jit(solution)/shard_map/ppermute | solution.py:38
  64.0 44.1 %collective-permute-start.15 = (bf16[128,3072]{1,0:T(8,128)(2,1)}, bf16[128,3072]{1,0:T(8,128)(2,1)}, u32[]{:S(2)}, u32[]{:S(2)}) collective-permute-start(bf16[128,3072]{1,0:T(8,128)(2,1)} %collective-permute-done.14.refs_9_), channel_id=1, source_target_pairs={{0,2},{2,4},{4,6},{6,7},{7,5},{5,3},{3,1},{1,0},{8,10},{10,12},{12... | collective-permute-start | bytes 2359304 | tf_op jit(solution)/shard_map/ppermute | solution.py:34
  82.4 33.7 %collective-permute-start.3 = (bf16[4,128,768]{2,1,0:T(8,128)(2,1)}, bf16[4,128,768]{2,1,0:T(8,128)(2,1)}, u32[]{:S(2)}, u32[]{:S(2)}) collective-permute-start(bf16[4,128,768]{2,1,0:T(8,128)(2,1)} %collective-permute-done.2), channel_id=1, source_target_pairs={{0,2},{2,4},{4,6},{6,7},{7,5},{5,3},{3,1},{1,0},{8,10},{10,12},{12... | collective-permute-start | bytes 2359304 | tf_op jit(solution)/shard_map/ppermute | solution.py:34
  106.0 20.8 %collective-permute-start.19 = (bf16[128,3072]{1,0:T(8,128)(2,1)}, bf16[128,3072]{1,0:T(8,128)(2,1)}, u32[]{:S(2)}, u32[]{:S(2)}) collective-permute-start(bf16[128,3072]{1,0:T(8,128)(2,1)} %collective-permute-done.18.refs_13_), channel_id=1, source_target_pairs={{0,1},{2,0},{4,2},{6,4},{7,6},{5,7},{3,5},{1,3},{8,9},{10,8},{12,1... | collective-permute-start | bytes 2359304 | tf_op jit(solution)/shard_map/ppermute | solution.py:38
  106.3 34.3 %collective-permute-start.6 = (bf16[4,128,768]{2,1,0:T(8,128)(2,1)}, bf16[4,128,768]{2,1,0:T(8,128)(2,1)S(1)}, u32[]{:S(2)}, u32[]{:S(2)}) collective-permute-start(bf16[4,128,768]{2,1,0:T(8,128)(2,1)} %collective-permute-done.5), channel_id=1, source_target_pairs={{0,1},{2,0},{4,2},{6,4},{7,6},{5,7},{3,5},{1,3},{8,9},{10,8},{12,1... | collective-permute-start | bytes 2359304 | tf_op jit(solution)/shard_map/ppermute | solution.py:38
  108.1 32.8 %collective-permute-start.16 = (bf16[128,3072]{1,0:T(8,128)(2,1)}, bf16[128,3072]{1,0:T(8,128)(2,1)}, u32[]{:S(2)}, u32[]{:S(2)}) collective-permute-start(bf16[128,3072]{1,0:T(8,128)(2,1)} %collective-permute-done.15.refs_10_), channel_id=1, source_target_pairs={{0,2},{2,4},{4,6},{6,7},{7,5},{5,3},{3,1},{1,0},{8,10},{10,12},{12... | collective-permute-start | bytes 2359304 | tf_op jit(solution)/shard_map/ppermute | solution.py:34
  116.1 41.9 %collective-permute-start.22 = (bf16[128,3072]{1,0:T(8,128)(2,1)}, bf16[128,3072]{1,0:T(8,128)(2,1)}, u32[]{:S(2)}, u32[]{:S(2)}) collective-permute-start(bf16[128,3072]{1,0:T(8,128)(2,1)} %collective-permute-done.14.refs_9_), channel_id=1, source_target_pairs={{0,8},{8,0},{1,9},{9,1},{2,10},{10,2},{3,11},{11,3},{4,12},{12,4},... | collective-permute-start | bytes 2359304 | tf_op jit(solution)/shard_map/ppermute | solution.py:203
  126.9 31.6 %collective-permute-start.26 = (bf16[128,3072]{1,0:T(8,128)(2,1)}, bf16[128,3072]{1,0:T(8,128)(2,1)}, u32[]{:S(2)}, u32[]{:S(2)}) collective-permute-start(bf16[128,3072]{1,0:T(8,128)(2,1)} %collective-permute-done.18.refs_13_), channel_id=1, source_target_pairs={{0,8},{8,0},{1,9},{9,1},{2,10},{10,2},{3,11},{11,3},{4,12},{12,4},... | collective-permute-start | bytes 2359304 | tf_op jit(solution)/shard_map/ppermute | solution.py:203
  140.6 18.0 %collective-permute-start.20 = (bf16[128,3072]{1,0:T(8,128)(2,1)}, bf16[128,3072]{1,0:T(8,128)(2,1)}, u32[]{:S(2)}, u32[]{:S(2)}) collective-permute-start(bf16[128,3072]{1,0:T(8,128)(2,1)} %collective-permute-done.19.refs_14_), channel_id=1, source_target_pairs={{0,1},{2,0},{4,2},{6,4},{7,6},{5,7},{3,5},{1,3},{8,9},{10,8},{12,1... | collective-permute-start | bytes 2359304 | tf_op jit(solution)/shard_map/ppermute | solution.py:38
  140.9 19.0 %collective-permute-start.17 = (bf16[128,3072]{1,0:T(8,128)(2,1)}, bf16[128,3072]{1,0:T(8,128)(2,1)}, u32[]{:S(2)}, u32[]{:S(2)}) collective-permute-start(bf16[128,3072]{1,0:T(8,128)(2,1)} %collective-permute-done.16.refs_11_), channel_id=1, source_target_pairs={{0,2},{2,4},{4,6},{6,7},{7,5},{5,3},{3,1},{1,0},{8,10},{10,12},{12... | collective-permute-start | bytes 2359304 | tf_op jit(solution)/shard_map/ppermute | solution.py:34
  157.9 3.1 collective-permute-start.23
  158.1 6.5 %collective-permute-start.27 = (bf16[128,3072]{1,0:T(8,128)(2,1)}, bf16[128,3072]{1,0:T(8,128)(2,1)S(1)}, u32[]{:S(2)}, u32[]{:S(2)}) collective-permute-start(bf16[128,3072]{1,0:T(8,128)(2,1)} %collective-permute-done.19.refs_14_), channel_id=1, source_target_pairs={{0,8},{8,0},{1,9},{9,1},{2,10},{10,2},{3,11},{11,3},{4,12},{12,4},... | collective-permute-start | bytes 2359304 | tf_op jit(solution)/shard_map/ppermute | solution.py:203
  158.5 7.7 %collective-permute-start.24 = (bf16[128,3072]{1,0:T(8,128)(2,1)}, bf16[128,3072]{1,0:T(8,128)(2,1)S(1)}, u32[]{:S(2)}, u32[]{:S(2)}) collective-permute-start(bf16[128,3072]{1,0:T(8,128)(2,1)} %collective-permute-done.16.refs_11_), channel_id=1, source_target_pairs={{0,8},{8,0},{1,9},{9,1},{2,10},{10,2},{3,11},{11,3},{4,12},{12,4},... | collective-permute-start | bytes 2359304 | tf_op jit(solution)/shard_map/ppermute | solution.py:203
  158.6 7.8 %collective-permute-start.28 = (bf16[128,3072]{1,0:T(8,128)(2,1)}, bf16[128,3072]{1,0:T(8,128)(2,1)}, u32[]{:S(2)}, u32[]{:S(2)}) collective-permute-start(bf16[128,3072]{1,0:T(8,128)(2,1)} %collective-permute-done.20.refs_15_), channel_id=1, source_target_pairs={{0,8},{8,0},{1,9},{9,1},{2,10},{10,2},{3,11},{11,3},{4,12},{12,4},... | collective-permute-start | bytes 2359304 | tf_op jit(solution)/shard_map/ppermute | solution.py:203
  159.9 32.3 %collective-permute-start.25 = (bf16[128,3072]{1,0:T(8,128)(2,1)}, bf16[128,3072]{1,0:T(8,128)(2,1)}, u32[]{:S(2)}, u32[]{:S(2)}) collective-permute-start(bf16[128,3072]{1,0:T(8,128)(2,1)} %collective-permute-done.17.refs_12_), channel_id=1, source_target_pairs={{0,8},{8,0},{1,9},{9,1},{2,10},{10,2},{3,11},{11,3},{4,12},{12,4},... | collective-permute-start | bytes 2359304 | tf_op jit(solution)/shard_map/ppermute | solution.py:203
  161.0 8.9 %collective-permute-start.10 = (bf16[512,128]{1,0:T(8,128)(2,1)S(1)}, bf16[512,128]{1,0:T(8,128)(2,1)S(1)}, u32[]{:S(2)}, u32[]{:S(2)}) collective-permute-start(bf16[512,128]{1,0:T(8,128)(2,1)S(1)} %bitcast.156), channel_id=1, source_target_pairs={{7,0},{5,2},{3,4},{1,6},{0,7},{2,5},{4,3},{6,1},{15,8},{13,10},{11... | collective-permute-start | bytes 393224 | tf_op jit(solution)/shard_map/ppermute | solution.py:74
  164.5 7.6 %collective-permute-start.11 = (bf16[512,128]{1,0:T(8,128)(2,1)S(1)}, bf16[512,128]{1,0:T(8,128)(2,1)S(1)}, u32[]{:S(2)}, u32[]{:S(2)}) collective-permute-start(bf16[512,128]{1,0:T(8,128)(2,1)S(1)} %bitcast.157), channel_id=1, source_target_pairs={{2,0},{4,2},{6,4},{7,6},{5,7},{3,5},{1,3},{0,1},{10,8},{12,10},{14... | collective-permute-start | bytes 393224 | tf_op jit(solution)/shard_map/ppermute | solution.py:74
  166.1 16.2 %collective-permute-start.12 = (bf16[512,128]{1,0:T(8,128)(2,1)S(1)}, bf16[512,128]{1,0:T(8,128)(2,1)S(1)}, u32[]{:S(2)}, u32[]{:S(2)}) collective-permute-start(bf16[512,128]{1,0:T(8,128)(2,1)S(1)} %bitcast.158), channel_id=1, source_target_pairs={{4,0},{6,2},{7,4},{5,6},{3,7},{1,5},{0,3},{2,1},{12,8},{14,10},{15... | collective-permute-start | bytes 393224 | tf_op jit(solution)/shard_map/ppermute | solution.py:74
  166.4 18.5 %collective-permute-start.13 = (bf16[512,128]{1,0:T(8,128)(2,1)S(1)}, bf16[512,128]{1,0:T(8,128)(2,1)}, u32[]{:S(2)}, u32[]{:S(2)}) collective-permute-start(bf16[512,128]{1,0:T(8,128)(2,1)S(1)} %bitcast.159), channel_id=1, source_target_pairs={{6,0},{7,2},{5,4},{3,6},{1,7},{0,5},{2,3},{4,1},{14,8},{15,10},{13... | collective-permute-start | bytes 393224 | tf_op jit(solution)/shard_map/ppermute | solution.py:74
  170.0 14.9 %collective-permute-start.7 = (bf16[512,128]{1,0:T(8,128)(2,1)S(1)}, bf16[512,128]{1,0:T(8,128)(2,1)}, u32[]{:S(2)}, u32[]{:S(2)}) collective-permute-start(bf16[512,128]{1,0:T(8,128)(2,1)S(1)} %bitcast.160), channel_id=1, source_target_pairs={{1,0},{0,2},{2,4},{4,6},{6,7},{7,5},{5,3},{3,1},{9,8},{8,10},{10,1... | collective-permute-start | bytes 393224 | tf_op jit(solution)/shard_map/ppermute | solution.py:74
  172.1 13.1 %collective-permute-start.8 = (bf16[512,128]{1,0:T(8,128)(2,1)S(1)}, bf16[512,128]{1,0:T(8,128)(2,1)}, u32[]{:S(2)}, u32[]{:S(2)}) collective-permute-start(bf16[512,128]{1,0:T(8,128)(2,1)S(1)} %bitcast.161), channel_id=1, source_target_pairs={{3,0},{1,2},{0,4},{2,6},{4,7},{6,5},{7,3},{5,1},{11,8},{9,10},{8,1... | collective-permute-start | bytes 393224 | tf_op jit(solution)/shard_map/ppermute | solution.py:74
  182.9 9.3 %collective-permute-start.9 = (bf16[512,128]{1,0:T(8,128)(2,1)S(1)}, bf16[512,128]{1,0:T(8,128)(2,1)}, u32[]{:S(2)}, u32[]{:S(2)}) collective-permute-start(bf16[512,128]{1,0:T(8,128)(2,1)S(1)} %bitcast.162), channel_id=1, source_target_pairs={{5,0},{3,2},{1,4},{0,6},{2,7},{4,5},{6,3},{7,1},{13,8},{11,10},{9,... | collective-permute-start | bytes 393224 | tf_op jit(solution)/shard_map/ppermute | solution.py:74
  245.3 11.1 %collective-permute-start.29 = (bf16[512,384]{1,0:T(8,128)(2,1)S(1)}, bf16[512,384]{1,0:T(8,128)(2,1)S(1)}, u32[]{:S(2)}, u32[]{:S(2)}) collective-permute-start(bf16[512,384]{1,0:T(8,128)(2,1)S(1)} %get-tuple-element.21), channel_id=1, source_target_pairs={{0,2},{2,4},{4,6},{6,7},{7,5},{5,3},{3,1},{1,0},{8,10},{10,12},{12... | collective-permute-start | bytes 1179656 | tf_op jit(solution)/shard_map/ppermute | solution.py:61
  245.4 11.1 %collective-permute-start.36 = (bf16[512,384]{1,0:T(8,128)(2,1)S(1)}, bf16[512,384]{1,0:T(8,128)(2,1)S(1)}, u32[]{:S(2)}, u32[]{:S(2)}) collective-permute-start(bf16[512,384]{1,0:T(8,128)(2,1)S(1)} %get-tuple-element.22), channel_id=1, source_target_pairs={{0,1},{2,0},{4,2},{6,4},{7,6},{5,7},{3,5},{1,3},{8,9},{10,8},{12,1... | collective-permute-start | bytes 1179656 | tf_op jit(solution)/shard_map/ppermute | solution.py:63
  257.8 10.2 %collective-permute-start.30 = (bf16[512,384]{1,0:T(8,128)(2,1)S(1)}, bf16[512,384]{1,0:T(8,128)(2,1)S(1)}, u32[]{:S(2)}, u32[]{:S(2)}) collective-permute-start(bf16[512,384]{1,0:T(8,128)(2,1)S(1)} %get-tuple-element.19), channel_id=1, source_target_pairs={{0,2},{2,4},{4,6},{6,7},{7,5},{5,3},{3,1},{1,0},{8,10},{10,12},{12... | collective-permute-start | bytes 1179656 | tf_op jit(solution)/shard_map/ppermute | solution.py:61
  258.0 10.2 %collective-permute-start.37 = (bf16[512,384]{1,0:T(8,128)(2,1)S(1)}, bf16[512,384]{1,0:T(8,128)(2,1)S(1)}, u32[]{:S(2)}, u32[]{:S(2)}) collective-permute-start(bf16[512,384]{1,0:T(8,128)(2,1)S(1)} %get-tuple-element.20), channel_id=1, source_target_pairs={{0,1},{2,0},{4,2},{6,4},{7,6},{5,7},{3,5},{1,3},{8,9},{10,8},{12,1... | collective-permute-start | bytes 1179656 | tf_op jit(solution)/shard_map/ppermute | solution.py:63
  269.6 9.4 %collective-permute-start.31 = (bf16[512,384]{1,0:T(8,128)(2,1)S(1)}, bf16[512,384]{1,0:T(8,128)(2,1)S(1)}, u32[]{:S(2)}, u32[]{:S(2)}) collective-permute-start(bf16[512,384]{1,0:T(8,128)(2,1)S(1)} %get-tuple-element.17), channel_id=1, source_target_pairs={{0,2},{2,4},{4,6},{6,7},{7,5},{5,3},{3,1},{1,0},{8,10},{10,12},{12... | collective-permute-start | bytes 1179656 | tf_op jit(solution)/shard_map/ppermute | solution.py:61
  270.6 8.6 %collective-permute-start.38 = (bf16[512,384]{1,0:T(8,128)(2,1)S(1)}, bf16[512,384]{1,0:T(8,128)(2,1)S(1)}, u32[]{:S(2)}, u32[]{:S(2)}) collective-permute-start(bf16[512,384]{1,0:T(8,128)(2,1)S(1)} %get-tuple-element.18), channel_id=1, source_target_pairs={{0,1},{2,0},{4,2},{6,4},{7,6},{5,7},{3,5},{1,3},{8,9},{10,8},{12,1... | collective-permute-start | bytes 1179656 | tf_op jit(solution)/shard_map/ppermute | solution.py:63
  280.5 8.2 %collective-permute-start.32 = (bf16[512,384]{1,0:T(8,128)(2,1)S(1)}, bf16[512,384]{1,0:T(8,128)(2,1)S(1)}, u32[]{:S(2)}, u32[]{:S(2)}) collective-permute-start(bf16[512,384]{1,0:T(8,128)(2,1)S(1)} %get-tuple-element.15), channel_id=1, source_target_pairs={{0,2},{2,4},{4,6},{6,7},{7,5},{5,3},{3,1},{1,0},{8,10},{10,12},{12... | collective-permute-start | bytes 1179656 | tf_op jit(solution)/shard_map/ppermute | solution.py:61
  281.5 7.8 %collective-permute-start.39 = (bf16[512,384]{1,0:T(8,128)(2,1)S(1)}, bf16[512,384]{1,0:T(8,128)(2,1)S(1)}, u32[]{:S(2)}, u32[]{:S(2)}) collective-permute-start(bf16[512,384]{1,0:T(8,128)(2,1)S(1)} %get-tuple-element.16), channel_id=1, source_target_pairs={{0,1},{2,0},{4,2},{6,4},{7,6},{5,7},{3,5},{1,3},{8,9},{10,8},{12,1... | collective-permute-start | bytes 1179656 | tf_op jit(solution)/shard_map/ppermute | solution.py:63
  290.6 8.9 %collective-permute-start.33 = (bf16[512,384]{1,0:T(8,128)(2,1)S(1)}, bf16[512,384]{1,0:T(8,128)(2,1)S(1)}, u32[]{:S(2)}, u32[]{:S(2)}) collective-permute-start(bf16[512,384]{1,0:T(8,128)(2,1)S(1)} %get-tuple-element.13), channel_id=1, source_target_pairs={{0,2},{2,4},{4,6},{6,7},{7,5},{5,3},{3,1},{1,0},{8,10},{10,12},{12... | collective-permute-start | bytes 1179656 | tf_op jit(solution)/shard_map/ppermute | solution.py:61
  291.6 8.5 %collective-permute-start.40 = (bf16[512,384]{1,0:T(8,128)(2,1)S(1)}, bf16[512,384]{1,0:T(8,128)(2,1)S(1)}, u32[]{:S(2)}, u32[]{:S(2)}) collective-permute-start(bf16[512,384]{1,0:T(8,128)(2,1)S(1)} %get-tuple-element.14), channel_id=1, source_target_pairs={{0,1},{2,0},{4,2},{6,4},{7,6},{5,7},{3,5},{1,3},{8,9},{10,8},{12,1... | collective-permute-start | bytes 1179656 | tf_op jit(solution)/shard_map/ppermute | solution.py:63
  301.4 9.2 %collective-permute-start.34 = (bf16[512,384]{1,0:T(8,128)(2,1)S(1)}, bf16[512,384]{1,0:T(8,128)(2,1)S(1)}, u32[]{:S(2)}, u32[]{:S(2)}) collective-permute-start(bf16[512,384]{1,0:T(8,128)(2,1)S(1)} %get-tuple-element.11), channel_id=1, source_target_pairs={{0,2},{2,4},{4,6},{6,7},{7,5},{5,3},{3,1},{1,0},{8,10},{10,12},{12... | collective-permute-start | bytes 1179656 | tf_op jit(solution)/shard_map/ppermute | solution.py:61
  302.2 10.2 %collective-permute-start.41 = (bf16[512,384]{1,0:T(8,128)(2,1)S(1)}, bf16[512,384]{1,0:T(8,128)(2,1)}, u32[]{:S(2)}, u32[]{:S(2)}) collective-permute-start(bf16[512,384]{1,0:T(8,128)(2,1)S(1)} %get-tuple-element.12), channel_id=1, source_target_pairs={{0,1},{2,0},{4,2},{6,4},{7,6},{5,7},{3,5},{1,3},{8,9},{10,8},{12,1... | collective-permute-start | bytes 1179656 | tf_op jit(solution)/shard_map/ppermute | solution.py:63
  314.0 7.9 %collective-permute-start.35 = (bf16[512,384]{1,0:T(8,128)(2,1)S(1)}, bf16[512,384]{1,0:T(8,128)(2,1)S(1)}, u32[]{:S(2)}, u32[]{:S(2)}) collective-permute-start(bf16[512,384]{1,0:T(8,128)(2,1)S(1)} %get-tuple-element.9), channel_id=1, source_target_pairs={{0,2},{2,4},{4,6},{6,7},{7,5},{5,3},{3,1},{1,0},{8,10},{10,12},{12... | collective-permute-start | bytes 1179656 | tf_op jit(solution)/shard_map/ppermute | solution.py:61
  316.5 7.9 %collective-permute-start.42 = (bf16[512,384]{1,0:T(8,128)(2,1)S(1)}, bf16[512,384]{1,0:T(8,128)(2,1)}, u32[]{:S(2)}, u32[]{:S(2)}) collective-permute-start(bf16[512,384]{1,0:T(8,128)(2,1)S(1)} %get-tuple-element.10), channel_id=1, source_target_pairs={{0,1},{2,0},{4,2},{6,4},{7,6},{5,7},{3,5},{1,3},{8,9},{10,8},{12,1... | collective-permute-start | bytes 1179656 | tf_op jit(solution)/shard_map/ppermute | solution.py:63
  (21 other events, 388.9 us)
Sparse Core Ops, SparseCore 0:
  8.9 18.3 all-gather.2
  28.9 17.9 all-gather.4

commit v10 on v7

--- a/solution.py
+++ b/solution.py
@@ -65,11 +65,11 @@
     return jnp.concatenate([forward, backward], axis=1)
 
 
-def out_proj_kernel(group_count, tiles_per_half, span_ref, *refs):
+def out_proj_kernel(group_count, tiles_per_half, row_count, span_ref, *refs):
     att_refs = refs[:group_count]
     mine_refs = refs[group_count:2 * group_count]
     other_refs = refs[2 * group_count:3 * group_count]
-    out_ref = refs[3 * group_count]
+    hidden_ref, scale_ref, out_ref, squares_ref = refs[3 * group_count:]
     tile = pl.program_id(0)
 
     def accumulate(w_refs):
@@ -78,7 +78,15 @@
             term = jnp.dot(att_refs[group][...], w_refs[group][...], preferred_element_type=jnp.float32)
             term = term.astype(jnp.bfloat16).astype(jnp.float32)
             total = term if total is None else total + term
-        out_ref[...] = total
+        for span in range(scale_ref.shape[0]):
+            rows = slice(span * row_count, (span + 1) * row_count)
+            out_ref[rows, :] = (
+                hidden_ref[rows, :].astype(jnp.float32) + scale_ref[span:span + 1, :] * total[rows, :]
+            )
+        result = out_ref[...]
+        squares_ref[...] = jnp.broadcast_to(
+            jnp.sum(result * result, axis=1, keepdims=True), squares_ref.shape
+        )
 
     @pl.when(tile < tiles_per_half)
     def _():
@@ -89,10 +97,13 @@
         accumulate(other_refs)
 
 
-def grouped_out_proj(span_index, att_blocks, mine_blocks, other_blocks, tile_width=512):
+def grouped_out_proj(
+    span_index, att_blocks, mine_blocks, other_blocks, hidden, scale, tile_width=512
+):
     group_count = len(att_blocks)
     token_count, head_width = att_blocks[0].shape
     half_width = mine_blocks[0].shape[1]
+    span_rows = scale.shape[0]
     tile_width = min(tile_width, half_width)
     tiles_per_half = half_width // tile_width
     att_spec = pl.BlockSpec((token_count, head_width), lambda n, s: (0, 0))
@@ -102,25 +113,41 @@
     other_spec = pl.BlockSpec(
         (head_width, tile_width), lambda n, s: (0, jnp.maximum(n - tiles_per_half, 0))
     )
-    out_spec = pl.BlockSpec(
-        (token_count, tile_width),
-        lambda n, s: (0, ((n // tiles_per_half + s[0]) % 2) * tiles_per_half + n % tiles_per_half),
-    )
+
+    def column(n, s):
+        return ((n // tiles_per_half + s[0]) % 2) * tiles_per_half + n % tiles_per_half
+
+    out_spec = pl.BlockSpec((token_count, tile_width), lambda n, s: (0, column(n, s)))
+    hidden_spec = pl.BlockSpec((token_count, tile_width), lambda n, s: (0, column(n, s)))
+    scale_spec = pl.BlockSpec((span_rows, tile_width), lambda n, s: (0, column(n, s)))
+    squares_spec = pl.BlockSpec((token_count, 128), lambda n, s: (0, n))
+    tile_count = 2 * tiles_per_half
     flops = 2 * token_count * head_width * group_count * half_width * 2
     moved = 2 * (group_count * token_count * head_width + 2 * group_count * head_width * half_width)
-    return pl.pallas_call(
-        functools.partial(out_proj_kernel, group_count, tiles_per_half),
-        out_shape=jax.ShapeDtypeStruct((token_count, 2 * half_width), jnp.float32),
+    moved += token_count * 2 * half_width * (4 + 2)
+    residual, squares = pl.pallas_call(
+        functools.partial(out_proj_kernel, group_count, tiles_per_half, token_count // span_rows),
+        out_shape=(
+            jax.ShapeDtypeStruct((token_count, 2 * half_width), jnp.float32),
+            jax.ShapeDtypeStruct((token_count, tile_count * 128), jnp.float32),
+        ),
         grid_spec=pltpu.PrefetchScalarGridSpec(
             num_scalar_prefetch=1,
-            grid=(2 * tiles_per_half,),
-            in_specs=[att_spec] * group_count + [mine_spec] * group_count + [other_spec] * group_count,
-            out_specs=out_spec,
+            grid=(tile_count,),
+            in_specs=[att_spec] * group_count + [mine_spec] * group_count + [other_spec] * group_count
+            + [hidden_spec, scale_spec],
+            out_specs=[out_spec, squares_spec],
         ),
-        cost_estimate=pl.CostEstimate(
-            flops=flops, bytes_accessed=moved + token_count * 2 * half_width * 4, transcendentals=0
-        ),
-    )(jnp.reshape(span_index, (1,)).astype(jnp.int32), *att_blocks, *mine_blocks, *other_blocks)
+        cost_estimate=pl.CostEstimate(flops=flops, bytes_accessed=moved, transcendentals=0),
+    )(
+        jnp.reshape(span_index, (1,)).astype(jnp.int32),
+        *att_blocks,
+        *mine_blocks,
+        *other_blocks,
+        hidden,
+        scale,
+    )
+    return residual, squares.reshape(token_count, tile_count, 128)[:, :, 0].sum(axis=1)
 
 
 def select_row(source, target):
@@ -183,6 +210,7 @@
         for step, piece in zip(steps, ring_gather(hidden_in, "tp", tp_count)):
             owner = owners[(position - step + tp_count) % tp_count]
             gathered = lax.dynamic_update_slice_in_dim(gathered, piece, owner * share_width, 2)
+        gathered_narrow = gathered
         gathered = gathered.astype(jnp.float32)
     else:
         gathered = lax.all_gather(hidden_in, "tp", axis=2, tiled=True).astype(jnp.float32)
@@ -231,11 +259,18 @@
     )(queries, cache_seen, fresh_seen)
     if gather_weights:
         att_blocks = ring_gather(attended.reshape(token_count, per_device), "tp", tp_count)
-        attn_out = grouped_out_proj(span_index, att_blocks, mine_blocks, other_blocks)
-        attn_out = attn_out.reshape(local_count, row_count, model_width)
-        residual_full = gathered + mod_rows[:, 2][:, None] * attn_out
+        residual_rows, square_sums = grouped_out_proj(
+            span_index,
+            att_blocks,
+            mine_blocks,
+            other_blocks,
+            gathered_narrow.reshape(token_count, model_width),
+            mod_rows[:, 2],
+        )
+        residual_full = residual_rows.reshape(local_count, row_count, model_width)
+        inverse = lax.rsqrt(square_sums.reshape(local_count, row_count, 1) / model_width + EPSILON)
         mlp_in = (
-            normalize(residual_full) * mod_rows[:, 4][:, None] + mod_rows[:, 3][:, None]
+            residual_full * inverse * mod_rows[:, 4][:, None] + mod_rows[:, 3][:, None]
         ).astype(jnp.bfloat16)
     else:
         partial_value = jnp.dot(

time: 334 us -> 330 us (0.988)
  other arithmetic: 31.7 us -> 19.3 us
  local copies, waits for them, and re-layouts: 21.7 us -> 25.9 us
    reduce_sum x2 -> x1, other arithmetic: 14.7 us -> 1.31 us  [normalize(): jnp.mean(values * values, axis=-1, keepdims=True) + EPSILON]
    pallas_call x0 -> x1, local copies, waits for them, and re-layouts: none -> 3.55 us  [grouped_out_proj(): pl.pallas_call(functools.partial(out_proj_kernel, group_count, tiles_per_...]
    unnamed x55 -> x59, local copies, waits for them, and re-layouts: 10.5 us -> 11 us
  transfers between devices with their start and end apart: 45 -> 45, of which waited for: 24 -> 24; matrix products, arithmetic and copies ran while one was open for 17% -> 14% of each run, Pallas kernels for 6% -> 7%
where the time goes in v10:
time: 330 us; the launch traced here: 328 us
  waiting for transfers between devices  158 us (48%)
  starting transfers between devices  40 us (12%)
  between operations  33.1 us (10%)
  local copies, waits for them, and re-layouts  25.9 us (8%)
  matrix products  24.8 us (8%)
  Pallas kernels  23.1 us (7%)
  other arithmetic  19.3 us (6%)
  blocking collectives  4.54 us (1%)
    ppermute x12, waiting for transfers between devices, ring_gather(): forward = lax.ppermute(forward, axis_name, ahead)  78.7 us
    ppermute x7, waiting for transfers between devices, ring_reduce_scatter(): lax.ppermute(forward.astype(jnp.bfloat16), axis_name, ahead)  50.2 us
    pallas_call x1, Pallas kernels, grouped_out_proj(): pl.pallas_call(functools.partial(out_proj_kernel, group_count, tiles_per_...  23.1 us
    ppermute x12, starting transfers between devices, ring_gather(): forward = lax.ppermute(forward, axis_name, ahead)  21.6 us
    ppermute x9, waiting for transfers between devices, ring_gather(): backward = lax.ppermute(backward, axis_name, behind)  21.1 us
    unnamed x59, local copies, waits for them, and re-layouts  11 us
    dot_general x1, matrix products, local(): pre_act = jnp.dot(mlp_in, up_full, preferred_element_type=jnp.float32)  10 us
    convert_element_type x6, other arithmetic, ring_reduce_scatter(): forward.astype(jnp.bfloat16)  8.11 us
  transfers between devices with their start and end apart: 45, of which 24 were waited for; matrix products, arithmetic and copies ran while one was open for 14% of the time, Pallas kernels for 7%

profile of v10, /device:TPU:0, one launch (start us, length us, event | category | flops | bytes accessed | tf_op | source)
XLA Modules:
  0.0 328.5 jit_solution(14034017248574326956)
XLA Ops:
  7.4 3.1 collective-permute-start
  10.5 2.1 collective-permute-start.14
  14.4 14.7 %collective-permute-done = bf16[4,128,768]{2,1,0:T(8,128)(2,1)} collective-permute-done((bf16[4,128,768]{2,1,0:T(8,128)(2,1)}, bf16[4,128,768]{2,1,0:T(8,128)(2,1)}, u32[]{:S(2)}, u32[]{:S(2)}) %collective-permute-start) | collective-permute-done | bytes 786464 | tf_op jit(solution)/shard_map/ppermute | solution.py:34
  29.1 2.1 collective-permute-start.1
  31.5 30.3 %collective-permute-done.1 = bf16[4,128,768]{2,1,0:T(8,128)(2,1)S(1)} collective-permute-done((bf16[4,128,768]{2,1,0:T(8,128)(2,1)}, bf16[4,128,768]{2,1,0:T(8,128)(2,1)S(1)}, u32[]{:S(2)}, u32[]{:S(2)}) %collective-permute-start.1) | collective-permute-done | bytes 786464 | tf_op jit(solution)/shard_map/ppermute | solution.py:34
  61.8 1.8 collective-permute-start.2
  65.4 2.2 all_gather.12
  67.7 13.0 %collective-permute-done.2 = bf16[4,128,768]{2,1,0:T(8,128)(2,1)} collective-permute-done((bf16[4,128,768]{2,1,0:T(8,128)(2,1)S(1)}, bf16[4,128,768]{2,1,0:T(8,128)(2,1)}, u32[]{:S(2)}, u32[]{:S(2)}) %collective-permute-start.2) | collective-permute-done | bytes 786464 | tf_op jit(solution)/shard_map/ppermute | solution.py:34
  80.7 1.5 collective-permute-start.3
  96.8 6.7 %copy.32 = bf16[6144,3,128]{0,2,1:T(8,128)(2,1)} copy(bf16[6144,3,128]{2,0,1:T(8,128)(2,1)} %param.22) | data formatting | bytes 9437184 | tf_op args[7]
  104.5 1.6 collective-permute-start.15
  114.7 7.4 %collective-permute-done.15.refs_10_ = bf16[128,3072]{1,0:T(8,128)(2,1)} collective-permute-done((bf16[128,3072]{1,0:T(8,128)(2,1)}, bf16[128,3072]{1,0:T(8,128)(2,1)}, u32[]{:S(2)}, u32[]{:S(2)}) %collective-permute-start.15) | collective-permute-done | bytes 786464 | tf_op jit(solution)/shard_map/ppermute | solution.py:34
  122.1 4.7 %collective-permute-done.6 = bf16[4,128,768]{2,1,0:T(8,128)(2,1)S(1)} collective-permute-done((bf16[4,128,768]{2,1,0:T(8,128)(2,1)}, bf16[4,128,768]{2,1,0:T(8,128)(2,1)S(1)}, u32[]{:S(2)}, u32[]{:S(2)}) %collective-permute-start.6) | collective-permute-done | bytes 786464 | tf_op jit(solution)/shard_map/ppermute | solution.py:38
  126.9 1.6 collective-permute-start.16
  129.9 2.7 fusion.3
  132.6 5.8 %convolution_convert_fusion.1 = bf16[512,384]{1,0:T(8,128)(2,1)S(1)} fusion(bf16[512,6144]{1,0:T(8,128)(2,1)S(1)} %bitcast.154, bf16[6144,384]{0,1:T(8,128)(2,1)} %bitcast.155), kind=kOutput, calls=%fused_computation.27 | convolution fusion | flops 2416115712 | bytes 11403264 | tf_op jit(solution)/shard_map/dot_general | solution.py:237
  139.2 2.4 all_gather.13
  144.4 1.6 collective-permute-start.17
  147.5 16.3 %collective-permute-done.20.refs_15_ = bf16[128,3072]{1,0:T(8,128)(2,1)S(1)} collective-permute-done((bf16[128,3072]{1,0:T(8,128)(2,1)}, bf16[128,3072]{1,0:T(8,128)(2,1)S(1)}, u32[]{:S(2)}, u32[]{:S(2)}) %collective-permute-start.20) | collective-permute-done | bytes 786464 | tf_op jit(solution)/shard_map/ppermute | solution.py:38
  165.1 1.6 collective-permute-start.7
  167.2 3.9 %collective-permute-done.7.refs_1_ = bf16[512,128]{1,0:T(8,128)(2,1)S(1)} collective-permute-done((bf16[512,128]{1,0:T(8,128)(2,1)S(1)}, bf16[512,128]{1,0:T(8,128)(2,1)S(1)}, u32[]{:S(2)}, u32[]{:S(2)}) %collective-permute-start.7) | collective-permute-done | bytes 131104 | tf_op jit(solution)/shard_map/ppermute | solution.py:34
  171.0 1.6 collective-permute-start.8
  173.1 3.1 collective-permute-done.8.refs_2_
  176.2 1.6 collective-permute-start.9
  178.2 2.9 collective-permute-done.9.refs_3_
  181.2 1.6 collective-permute-start.10
  183.3 2.8 collective-permute-done.10.refs_4_
  186.8 23.1 %shard_map.145 = (f32[512,6144]{1,0:T(8,128)}, f32[512,1536]{1,0:T(8,128)}) custom-call(s32[1]{0:T(128)} %bitcast.span_ref, bf16[512,128]{1,0:T(8,128)(2,1)} %bitcast.167, bf16[512,128]{1,0:T(8,128)(2,1)} %copy-done.17, bf16[512,128]{1,0:T(8,128)(2,1)} %copy-done.19, bf16[512,128]{1,0:T(8,128)(2,1)} %copy-done.21, bf16[512,128]{1,0:T(8,128)(2,1)} %copy-done.23, ...), custom_call_target="tpu_custom_call" | custom-call | flops 6442450944 | bytes 32505856 | tf_op jit(solution)/shard_map/pallas_call | solution.py:128
  209.9 3.5 %copy.39 = f32[512,1536]{0,1:T(8,128)} copy(f32[512,1536]{1,0:T(8,128)} %get-tuple-element.8) | data formatting | bytes 6291456 | tf_op jit(solution)/shard_map/pallas_call | solution.py:128
  214.4 10.0 %fusion.27 = bf16[4,128,512]{2,1,0:T(8,128)(2,1)S(1)} fusion(bf16[6144,512]{1,0:T(8,128)(2,1)} %all-gather.3.cloned.1.call-done, f32[4,128,6144]{2,1,0:T(8,128)} %bitcast.161, f32[4,6144]{1,0:T(4,128)S(1)} %copy-done.11, f32[4,6144]{1,0:T(4,128)S(1)} %get-tuple-element.29, f32[4,128]{1,0:T(4,128)S(1)} %rsqrt_bitcast_fusion), kind=kOutput, calls=%fused_computation.38 | convolution fusion | flops 3236167680 | bytes 19597312 | tf_op jit(solution)/shard_map/dot_general | solution.py:290
  224.5 6.4 %convolution_convert_fusion = bf16[4,128,6144]{2,1,0:T(8,128)(2,1)S(1)} fusion(bf16[4,128,512]{2,1,0:T(8,128)(2,1)S(1)} %fusion.27, bf16[512,6144]{1,0:T(8,128)(2,1)} %all-gather.5.cloned.1.call-done), kind=kOutput, calls=%fused_computation.7 | convolution fusion | flops 3224371200 | bytes 13107200 | tf_op jit(solution)/shard_map/dot_general | solution.py:292
  230.9 2.6 copy-done.3
  233.6 1.6 collective-permute-start.29
  237.0 4.5 %collective-permute-done.29 = bf16[512,384]{1,0:T(8,128)(2,1)S(1)} collective-permute-done((bf16[512,384]{1,0:T(8,128)(2,1)S(1)}, bf16[512,384]{1,0:T(8,128)(2,1)S(1)}, u32[]{:S(2)}, u32[]{:S(2)}) %collective-permute-start.29) | collective-permute-done | bytes 393248 | tf_op jit(solution)/shard_map/ppermute | solution.py:61
  241.4 1.5 collective-permute-done.36
  244.3 2.1 collective-permute-start.30
  247.7 5.6 %collective-permute-done.30 = bf16[512,384]{1,0:T(8,128)(2,1)S(1)} collective-permute-done((bf16[512,384]{1,0:T(8,128)(2,1)S(1)}, bf16[512,384]{1,0:T(8,128)(2,1)S(1)}, u32[]{:S(2)}, u32[]{:S(2)}) %collective-permute-start.30) | collective-permute-done | bytes 393248 | tf_op jit(solution)/shard_map/ppermute | solution.py:61
  253.3 2.8 collective-permute-done.37
  260.1 8.1 %collective-permute-done.31 = bf16[512,384]{1,0:T(8,128)(2,1)S(1)} collective-permute-done((bf16[512,384]{1,0:T(8,128)(2,1)S(1)}, bf16[512,384]{1,0:T(8,128)(2,1)S(1)}, u32[]{:S(2)}, u32[]{:S(2)}) %collective-permute-start.31) | collective-permute-done | bytes 393248 | tf_op jit(solution)/shard_map/ppermute | solution.py:61
  271.5 1.4 collective-permute-start.39
  272.9 9.5 %collective-permute-done.32 = bf16[512,384]{1,0:T(8,128)(2,1)S(1)} collective-permute-done((bf16[512,384]{1,0:T(8,128)(2,1)S(1)}, bf16[512,384]{1,0:T(8,128)(2,1)S(1)}, u32[]{:S(2)}, u32[]{:S(2)}) %collective-permute-start.32) | collective-permute-done | bytes 393248 | tf_op jit(solution)/shard_map/ppermute | solution.py:61
  284.4 1.7 collective-permute-start.40
  286.1 8.5 %collective-permute-done.33 = bf16[512,384]{1,0:T(8,128)(2,1)S(1)} collective-permute-done((bf16[512,384]{1,0:T(8,128)(2,1)S(1)}, bf16[512,384]{1,0:T(8,128)(2,1)S(1)}, u32[]{:S(2)}, u32[]{:S(2)}) %collective-permute-start.33) | collective-permute-done | bytes 393248 | tf_op jit(solution)/shard_map/ppermute | solution.py:61
  296.6 1.6 collective-permute-start.41
  298.2 8.2 %collective-permute-done.34 = bf16[512,384]{1,0:T(8,128)(2,1)S(1)} collective-permute-done((bf16[512,384]{1,0:T(8,128)(2,1)S(1)}, bf16[512,384]{1,0:T(8,128)(2,1)S(1)}, u32[]{:S(2)}, u32[]{:S(2)}) %collective-permute-start.34) | collective-permute-done | bytes 393248 | tf_op jit(solution)/shard_map/ppermute | solution.py:61
  307.2 1.6 add_convert_fusion.13
  310.8 5.7 %collective-permute-done.35 = bf16[512,384]{1,0:T(8,128)(2,1)S(1)} collective-permute-done((bf16[512,384]{1,0:T(8,128)(2,1)S(1)}, bf16[512,384]{1,0:T(8,128)(2,1)S(1)}, u32[]{:S(2)}, u32[]{:S(2)}) %collective-permute-start.35) | collective-permute-done | bytes 393248 | tf_op jit(solution)/shard_map/ppermute | solution.py:61
  319.0 2.6 add_convert_fusion.2
  (161 shorter events, 42.2 us)
Async XLA Ops:
  6.5 84.6 %copy-start.10 = (s32[8]{0:T(128)S(1)}, s32[8]{0:T(128)}, u32[]{:S(2)}) copy-start(s32[8]{0:T(128)} %constant.289.clone) | copy-start | bytes 100
  6.6 58.8 %copy-start.9 = (bf16[4,128,2,128]{3,2,1,0:T(2,128)(2,1)S(1)}, bf16[4,128,2,128]{3,2,1,0:T(2,128)(2,1)}, u32[]{:S(2)}) copy-start(bf16[4,128,2,128]{3,2,1,0:T(2,128)(2,1)} %param.20) | copy-start | bytes 786436
  6.6 207.8 %all-gather.3.cloned.1.call-start = ((), (), s32[]{:S(2)}) async-start(), calls=%async_computation | async-start | bytes 9437184 | tf_op jit(solution)/shard_map/all_gather | solution.py:223
  7.3 217.1 %all-gather.5.cloned.1.call-start = ((), (), s32[]{:S(2)}) async-start(), calls=%async_computation.1 | async-start | bytes 9437184 | tf_op jit(solution)/shard_map/all_gather | solution.py:224
  7.4 21.7 %collective-permute-start = (bf16[4,128,768]{2,1,0:T(8,128)(2,1)}, bf16[4,128,768]{2,1,0:T(8,128)(2,1)}, u32[]{:S(2)}, u32[]{:S(2)}) collective-permute-start(bf16[4,128,768]{2,1,0:T(8,128)(2,1)} %param.15), channel_id=1, source_target_pairs={{0,2},{2,4},{4,6},{6,7},{7,5},{5,3},{3,1},{1,0},{8,10},{10,12},{12... | collective-permute-start | bytes 2359304 | tf_op jit(solution)/shard_map/ppermute | solution.py:34
  10.4 53.3 %collective-permute-start.4 = (bf16[4,128,768]{2,1,0:T(8,128)(2,1)}, bf16[4,128,768]{2,1,0:T(8,128)(2,1)}, u32[]{:S(2)}, u32[]{:S(2)}) collective-permute-start(bf16[4,128,768]{2,1,0:T(8,128)(2,1)} %param.15), channel_id=1, source_target_pairs={{0,1},{2,0},{4,2},{6,4},{7,6},{5,7},{3,5},{1,3},{8,9},{10,8},{12,1... | collective-permute-start | bytes 2359304 | tf_op jit(solution)/shard_map/ppermute | solution.py:38
  10.5 93.0 %copy-start.5 = (bf16[128,3072]{1,0:T(8,128)(2,1)}, bf16[128,3072]{1,0:T(8,128)(2,1)S(1)}, u32[]{:S(2)}) copy-start(bf16[128,3072]{1,0:T(8,128)(2,1)S(1)} %constant_dynamic-slice_fusion.2.refs_8_) | copy-start | bytes 2359300
  10.5 94.0 %collective-permute-start.14 = (bf16[128,3072]{1,0:T(8,128)(2,1)S(1)}, bf16[128,3072]{1,0:T(8,128)(2,1)}, u32[]{:S(2)}, u32[]{:S(2)}) collective-permute-start(bf16[128,3072]{1,0:T(8,128)(2,1)S(1)} %constant_dynamic-slice_fusion.2.refs_8_), channel_id=1, source_target_pairs={{0,2},{2,4},{4,6},{6,7},{7,5},{5,3},{3,1},{1,0},{8,10},{10,12},{12... | collective-permute-start | bytes 2359304 | tf_op jit(solution)/shard_map/ppermute | solution.py:34
  12.6 97.7 %collective-permute-start.18 = (bf16[128,3072]{1,0:T(8,128)(2,1)S(1)}, bf16[128,3072]{1,0:T(8,128)(2,1)}, u32[]{:S(2)}, u32[]{:S(2)}) collective-permute-start(bf16[128,3072]{1,0:T(8,128)(2,1)S(1)} %constant_dynamic-slice_fusion.2.refs_8_), channel_id=1, source_target_pairs={{0,1},{2,0},{4,2},{6,4},{7,6},{5,7},{3,5},{1,3},{8,9},{10,8},{12,1... | collective-permute-start | bytes 2359304 | tf_op jit(solution)/shard_map/ppermute | solution.py:38
  12.6 131.0 %collective-permute-start.21 = (bf16[128,3072]{1,0:T(8,128)(2,1)S(1)}, bf16[128,3072]{1,0:T(8,128)(2,1)}, u32[]{:S(2)}, u32[]{:S(2)}) collective-permute-start(bf16[128,3072]{1,0:T(8,128)(2,1)S(1)} %constant_dynamic-slice_fusion.2.refs_8_), channel_id=1, source_target_pairs={{0,8},{8,0},{1,9},{9,1},{2,10},{10,2},{3,11},{11,3},{4,12},{12,4},... | collective-permute-start | bytes 2359304 | tf_op jit(solution)/shard_map/ppermute | solution.py:221
  29.1 32.8 %collective-permute-start.1 = (bf16[4,128,768]{2,1,0:T(8,128)(2,1)}, bf16[4,128,768]{2,1,0:T(8,128)(2,1)S(1)}, u32[]{:S(2)}, u32[]{:S(2)}) collective-permute-start(bf16[4,128,768]{2,1,0:T(8,128)(2,1)} %collective-permute-done), channel_id=1, source_target_pairs={{0,2},{2,4},{4,6},{6,7},{7,5},{5,3},{3,1},{1,0},{8,10},{10,12},{12... | collective-permute-start | bytes 2359304 | tf_op jit(solution)/shard_map/ppermute | solution.py:34
  61.8 18.8 %collective-permute-start.2 = (bf16[4,128,768]{2,1,0:T(8,128)(2,1)S(1)}, bf16[4,128,768]{2,1,0:T(8,128)(2,1)}, u32[]{:S(2)}, u32[]{:S(2)}) collective-permute-start(bf16[4,128,768]{2,1,0:T(8,128)(2,1)S(1)} %collective-permute-done.1), channel_id=1, source_target_pairs={{0,2},{2,4},{4,6},{6,7},{7,5},{5,3},{3,1},{1,0},{8,10},{10,12},{12... | collective-permute-start | bytes 2359304 | tf_op jit(solution)/shard_map/ppermute | solution.py:34
  63.7 42.4 %collective-permute-start.5 = (bf16[4,128,768]{2,1,0:T(8,128)(2,1)}, bf16[4,128,768]{2,1,0:T(8,128)(2,1)}, u32[]{:S(2)}, u32[]{:S(2)}) collective-permute-start(bf16[4,128,768]{2,1,0:T(8,128)(2,1)} %collective-permute-done.4), channel_id=1, source_target_pairs={{0,1},{2,0},{4,2},{6,4},{7,6},{5,7},{3,5},{1,3},{8,9},{10,8},{12,1... | collective-permute-start | bytes 2359304 | tf_op jit(solution)/shard_map/ppermute | solution.py:38
  80.7 29.7 %collective-permute-start.3 = (bf16[4,128,768]{2,1,0:T(8,128)(2,1)}, bf16[4,128,768]{2,1,0:T(8,128)(2,1)}, u32[]{:S(2)}, u32[]{:S(2)}) collective-permute-start(bf16[4,128,768]{2,1,0:T(8,128)(2,1)} %collective-permute-done.2), channel_id=1, source_target_pairs={{0,2},{2,4},{4,6},{6,7},{7,5},{5,3},{3,1},{1,0},{8,10},{10,12},{12... | collective-permute-start | bytes 2359304 | tf_op jit(solution)/shard_map/ppermute | solution.py:34
  104.5 17.6 %collective-permute-start.15 = (bf16[128,3072]{1,0:T(8,128)(2,1)}, bf16[128,3072]{1,0:T(8,128)(2,1)}, u32[]{:S(2)}, u32[]{:S(2)}) collective-permute-start(bf16[128,3072]{1,0:T(8,128)(2,1)} %collective-permute-done.14.refs_9_), channel_id=1, source_target_pairs={{0,2},{2,4},{4,6},{6,7},{7,5},{5,3},{3,1},{1,0},{8,10},{10,12},{12... | collective-permute-start | bytes 2359304 | tf_op jit(solution)/shard_map/ppermute | solution.py:34
  106.2 20.7 %collective-permute-start.6 = (bf16[4,128,768]{2,1,0:T(8,128)(2,1)}, bf16[4,128,768]{2,1,0:T(8,128)(2,1)S(1)}, u32[]{:S(2)}, u32[]{:S(2)}) collective-permute-start(bf16[4,128,768]{2,1,0:T(8,128)(2,1)} %collective-permute-done.5), channel_id=1, source_target_pairs={{0,1},{2,0},{4,2},{6,4},{7,6},{5,7},{3,5},{1,3},{8,9},{10,8},{12,1... | collective-permute-start | bytes 2359304 | tf_op jit(solution)/shard_map/ppermute | solution.py:38
  110.3 34.0 %collective-permute-start.22 = (bf16[128,3072]{1,0:T(8,128)(2,1)}, bf16[128,3072]{1,0:T(8,128)(2,1)}, u32[]{:S(2)}, u32[]{:S(2)}) collective-permute-start(bf16[128,3072]{1,0:T(8,128)(2,1)} %collective-permute-done.14.refs_9_), channel_id=1, source_target_pairs={{0,8},{8,0},{1,9},{9,1},{2,10},{10,2},{3,11},{11,3},{4,12},{12,4},... | collective-permute-start | bytes 2359304 | tf_op jit(solution)/shard_map/ppermute | solution.py:221
  110.4 33.4 %collective-permute-start.19 = (bf16[128,3072]{1,0:T(8,128)(2,1)}, bf16[128,3072]{1,0:T(8,128)(2,1)}, u32[]{:S(2)}, u32[]{:S(2)}) collective-permute-start(bf16[128,3072]{1,0:T(8,128)(2,1)} %collective-permute-done.18.refs_13_), channel_id=1, source_target_pairs={{0,1},{2,0},{4,2},{6,4},{7,6},{5,7},{3,5},{1,3},{8,9},{10,8},{12,1... | collective-permute-start | bytes 2359304 | tf_op jit(solution)/shard_map/ppermute | solution.py:38
  122.1 25.2 %collective-permute-start.26 = (bf16[128,3072]{1,0:T(8,128)(2,1)}, bf16[128,3072]{1,0:T(8,128)(2,1)}, u32[]{:S(2)}, u32[]{:S(2)}) collective-permute-start(bf16[128,3072]{1,0:T(8,128)(2,1)} %collective-permute-done.18.refs_13_), channel_id=1, source_target_pairs={{0,8},{8,0},{1,9},{9,1},{2,10},{10,2},{3,11},{11,3},{4,12},{12,4},... | collective-permute-start | bytes 2359304 | tf_op jit(solution)/shard_map/ppermute | solution.py:221
  126.9 17.5 %collective-permute-start.16 = (bf16[128,3072]{1,0:T(8,128)(2,1)}, bf16[128,3072]{1,0:T(8,128)(2,1)}, u32[]{:S(2)}, u32[]{:S(2)}) collective-permute-start(bf16[128,3072]{1,0:T(8,128)(2,1)} %collective-permute-done.15.refs_10_), channel_id=1, source_target_pairs={{0,2},{2,4},{4,6},{6,7},{7,5},{5,3},{3,1},{1,0},{8,10},{10,12},{12... | collective-permute-start | bytes 2359304 | tf_op jit(solution)/shard_map/ppermute | solution.py:34
  143.6 21.4 %collective-permute-start.23 = (bf16[128,3072]{1,0:T(8,128)(2,1)}, bf16[128,3072]{1,0:T(8,128)(2,1)S(1)}, u32[]{:S(2)}, u32[]{:S(2)}) collective-permute-start(bf16[128,3072]{1,0:T(8,128)(2,1)} %collective-permute-done.15.refs_10_), channel_id=1, source_target_pairs={{0,8},{8,0},{1,9},{9,1},{2,10},{10,2},{3,11},{11,3},{4,12},{12,4},... | collective-permute-start | bytes 2359304 | tf_op jit(solution)/shard_map/ppermute | solution.py:221
  143.8 20.0 %collective-permute-start.20 = (bf16[128,3072]{1,0:T(8,128)(2,1)}, bf16[128,3072]{1,0:T(8,128)(2,1)S(1)}, u32[]{:S(2)}, u32[]{:S(2)}) collective-permute-start(bf16[128,3072]{1,0:T(8,128)(2,1)} %collective-permute-done.19.refs_14_), channel_id=1, source_target_pairs={{0,1},{2,0},{4,2},{6,4},{7,6},{5,7},{3,5},{1,3},{8,9},{10,8},{12,1... | collective-permute-start | bytes 2359304 | tf_op jit(solution)/shard_map/ppermute | solution.py:38
  144.3 22.4 %collective-permute-start.27 = (bf16[128,3072]{1,0:T(8,128)(2,1)}, bf16[128,3072]{1,0:T(8,128)(2,1)}, u32[]{:S(2)}, u32[]{:S(2)}) collective-permute-start(bf16[128,3072]{1,0:T(8,128)(2,1)} %collective-permute-done.19.refs_14_), channel_id=1, source_target_pairs={{0,8},{8,0},{1,9},{9,1},{2,10},{10,2},{3,11},{11,3},{4,12},{12,4},... | collective-permute-start | bytes 2359304 | tf_op jit(solution)/shard_map/ppermute | solution.py:221
  144.4 20.2 %collective-permute-start.17 = (bf16[128,3072]{1,0:T(8,128)(2,1)}, bf16[128,3072]{1,0:T(8,128)(2,1)}, u32[]{:S(2)}, u32[]{:S(2)}) collective-permute-start(bf16[128,3072]{1,0:T(8,128)(2,1)} %collective-permute-done.16.refs_11_), channel_id=1, source_target_pairs={{0,2},{2,4},{4,6},{6,7},{7,5},{5,3},{3,1},{1,0},{8,10},{10,12},{12... | collective-permute-start | bytes 2359304 | tf_op jit(solution)/shard_map/ppermute | solution.py:34
  147.3 36.0 %collective-permute-start.24 = (bf16[128,3072]{1,0:T(8,128)(2,1)}, bf16[128,3072]{1,0:T(8,128)(2,1)}, u32[]{:S(2)}, u32[]{:S(2)}) collective-permute-start(bf16[128,3072]{1,0:T(8,128)(2,1)} %collective-permute-done.16.refs_11_), channel_id=1, source_target_pairs={{0,8},{8,0},{1,9},{9,1},{2,10},{10,2},{3,11},{11,3},{4,12},{12,4},... | collective-permute-start | bytes 2359304 | tf_op jit(solution)/shard_map/ppermute | solution.py:221
  163.9 19.4 %collective-permute-start.28 = (bf16[128,3072]{1,0:T(8,128)(2,1)S(1)}, bf16[128,3072]{1,0:T(8,128)(2,1)}, u32[]{:S(2)}, u32[]{:S(2)}) collective-permute-start(bf16[128,3072]{1,0:T(8,128)(2,1)S(1)} %collective-permute-done.20.refs_15_), channel_id=1, source_target_pairs={{0,8},{8,0},{1,9},{9,1},{2,10},{10,2},{3,11},{11,3},{4,12},{12,4},... | collective-permute-start | bytes 2359304 | tf_op jit(solution)/shard_map/ppermute | solution.py:221
  164.6 21.5 %collective-permute-start.25 = (bf16[128,3072]{1,0:T(8,128)(2,1)}, bf16[128,3072]{1,0:T(8,128)(2,1)}, u32[]{:S(2)}, u32[]{:S(2)}) collective-permute-start(bf16[128,3072]{1,0:T(8,128)(2,1)} %collective-permute-done.17.refs_12_), channel_id=1, source_target_pairs={{0,8},{8,0},{1,9},{9,1},{2,10},{10,2},{3,11},{11,3},{4,12},{12,4},... | collective-permute-start | bytes 2359304 | tf_op jit(solution)/shard_map/ppermute | solution.py:221
  165.1 6.0 %collective-permute-start.7 = (bf16[512,128]{1,0:T(8,128)(2,1)S(1)}, bf16[512,128]{1,0:T(8,128)(2,1)S(1)}, u32[]{:S(2)}, u32[]{:S(2)}) collective-permute-start(bf16[512,128]{1,0:T(8,128)(2,1)S(1)} %bitcast.165), channel_id=1, source_target_pairs={{0,2},{2,4},{4,6},{6,7},{7,5},{5,3},{3,1},{1,0},{8,10},{10,12},{12... | collective-permute-start | bytes 393224 | tf_op jit(solution)/shard_map/ppermute | solution.py:34
  166.7 5.9 %collective-permute-start.11 = (bf16[512,128]{1,0:T(8,128)(2,1)S(1)}, bf16[512,128]{1,0:T(8,128)(2,1)S(1)}, u32[]{:S(2)}, u32[]{:S(2)}) collective-permute-start(bf16[512,128]{1,0:T(8,128)(2,1)S(1)} %bitcast.166), channel_id=1, source_target_pairs={{0,1},{2,0},{4,2},{6,4},{7,6},{5,7},{3,5},{1,3},{8,9},{10,8},{12,1... | collective-permute-start | bytes 393224 | tf_op jit(solution)/shard_map/ppermute | solution.py:38
  171.0 5.1 %collective-permute-start.8 = (bf16[512,128]{1,0:T(8,128)(2,1)S(1)}, bf16[512,128]{1,0:T(8,128)(2,1)S(1)}, u32[]{:S(2)}, u32[]{:S(2)}) collective-permute-start(bf16[512,128]{1,0:T(8,128)(2,1)S(1)} %collective-permute-done.7.refs_1_), channel_id=1, source_target_pairs={{0,2},{2,4},{4,6},{6,7},{7,5},{5,3},{3,1},{1,0},{8,10},{10,12},{12... | collective-permute-start | bytes 393224 | tf_op jit(solution)/shard_map/ppermute | solution.py:34
  172.6 5.1 %collective-permute-start.12 = (bf16[512,128]{1,0:T(8,128)(2,1)S(1)}, bf16[512,128]{1,0:T(8,128)(2,1)S(1)}, u32[]{:S(2)}, u32[]{:S(2)}) collective-permute-start(bf16[512,128]{1,0:T(8,128)(2,1)S(1)} %collective-permute-done.11.refs_5_), channel_id=1, source_target_pairs={{0,1},{2,0},{4,2},{6,4},{7,6},{5,7},{3,5},{1,3},{8,9},{10,8},{12,1... | collective-permute-start | bytes 393224 | tf_op jit(solution)/shard_map/ppermute | solution.py:38
  176.2 5.0 %collective-permute-start.9 = (bf16[512,128]{1,0:T(8,128)(2,1)S(1)}, bf16[512,128]{1,0:T(8,128)(2,1)S(1)}, u32[]{:S(2)}, u32[]{:S(2)}) collective-permute-start(bf16[512,128]{1,0:T(8,128)(2,1)S(1)} %collective-permute-done.8.refs_2_), channel_id=1, source_target_pairs={{0,2},{2,4},{4,6},{6,7},{7,5},{5,3},{3,1},{1,0},{8,10},{10,12},{12... | collective-permute-start | bytes 393224 | tf_op jit(solution)/shard_map/ppermute | solution.py:34
  177.8 5.6 %collective-permute-start.13 = (bf16[512,128]{1,0:T(8,128)(2,1)S(1)}, bf16[512,128]{1,0:T(8,128)(2,1)S(1)}, u32[]{:S(2)}, u32[]{:S(2)}) collective-permute-start(bf16[512,128]{1,0:T(8,128)(2,1)S(1)} %collective-permute-done.12.refs_6_), channel_id=1, source_target_pairs={{0,1},{2,0},{4,2},{6,4},{7,6},{5,7},{3,5},{1,3},{8,9},{10,8},{12,1... | collective-permute-start | bytes 393224 | tf_op jit(solution)/shard_map/ppermute | solution.py:38
  181.2 5.0 %collective-permute-start.10 = (bf16[512,128]{1,0:T(8,128)(2,1)S(1)}, bf16[512,128]{1,0:T(8,128)(2,1)S(1)}, u32[]{:S(2)}, u32[]{:S(2)}) collective-permute-start(bf16[512,128]{1,0:T(8,128)(2,1)S(1)} %collective-permute-done.9.refs_3_), channel_id=1, source_target_pairs={{0,2},{2,4},{4,6},{6,7},{7,5},{5,3},{3,1},{1,0},{8,10},{10,12},{12... | collective-permute-start | bytes 393224 | tf_op jit(solution)/shard_map/ppermute | solution.py:34
  233.6 7.8 %collective-permute-start.29 = (bf16[512,384]{1,0:T(8,128)(2,1)S(1)}, bf16[512,384]{1,0:T(8,128)(2,1)S(1)}, u32[]{:S(2)}, u32[]{:S(2)}) collective-permute-start(bf16[512,384]{1,0:T(8,128)(2,1)S(1)} %get-tuple-element.23), channel_id=1, source_target_pairs={{0,2},{2,4},{4,6},{6,7},{7,5},{5,3},{3,1},{1,0},{8,10},{10,12},{12... | collective-permute-start | bytes 1179656 | tf_op jit(solution)/shard_map/ppermute | solution.py:61
  235.2 7.8 %collective-permute-start.36 = (bf16[512,384]{1,0:T(8,128)(2,1)S(1)}, bf16[512,384]{1,0:T(8,128)(2,1)S(1)}, u32[]{:S(2)}, u32[]{:S(2)}) collective-permute-start(bf16[512,384]{1,0:T(8,128)(2,1)S(1)} %get-tuple-element.24), channel_id=1, source_target_pairs={{0,1},{2,0},{4,2},{6,4},{7,6},{5,7},{3,5},{1,3},{8,9},{10,8},{12,1... | collective-permute-start | bytes 1179656 | tf_op jit(solution)/shard_map/ppermute | solution.py:63
  244.3 9.0 %collective-permute-start.30 = (bf16[512,384]{1,0:T(8,128)(2,1)S(1)}, bf16[512,384]{1,0:T(8,128)(2,1)S(1)}, u32[]{:S(2)}, u32[]{:S(2)}) collective-permute-start(bf16[512,384]{1,0:T(8,128)(2,1)S(1)} %get-tuple-element.21), channel_id=1, source_target_pairs={{0,2},{2,4},{4,6},{6,7},{7,5},{5,3},{3,1},{1,0},{8,10},{10,12},{12... | collective-permute-start | bytes 1179656 | tf_op jit(solution)/shard_map/ppermute | solution.py:61
  246.4 9.7 %collective-permute-start.37 = (bf16[512,384]{1,0:T(8,128)(2,1)S(1)}, bf16[512,384]{1,0:T(8,128)(2,1)S(1)}, u32[]{:S(2)}, u32[]{:S(2)}) collective-permute-start(bf16[512,384]{1,0:T(8,128)(2,1)S(1)} %get-tuple-element.22), channel_id=1, source_target_pairs={{0,1},{2,0},{4,2},{6,4},{7,6},{5,7},{3,5},{1,3},{8,9},{10,8},{12,1... | collective-permute-start | bytes 1179656 | tf_op jit(solution)/shard_map/ppermute | solution.py:63
  257.4 10.8 %collective-permute-start.31 = (bf16[512,384]{1,0:T(8,128)(2,1)S(1)}, bf16[512,384]{1,0:T(8,128)(2,1)S(1)}, u32[]{:S(2)}, u32[]{:S(2)}) collective-permute-start(bf16[512,384]{1,0:T(8,128)(2,1)S(1)} %get-tuple-element.19), channel_id=1, source_target_pairs={{0,2},{2,4},{4,6},{6,7},{7,5},{5,3},{3,1},{1,0},{8,10},{10,12},{12... | collective-permute-start | bytes 1179656 | tf_op jit(solution)/shard_map/ppermute | solution.py:61
  258.2 11.3 %collective-permute-start.38 = (bf16[512,384]{1,0:T(8,128)(2,1)S(1)}, bf16[512,384]{1,0:T(8,128)(2,1)S(1)}, u32[]{:S(2)}, u32[]{:S(2)}) collective-permute-start(bf16[512,384]{1,0:T(8,128)(2,1)S(1)} %get-tuple-element.20), channel_id=1, source_target_pairs={{0,1},{2,0},{4,2},{6,4},{7,6},{5,7},{3,5},{1,3},{8,9},{10,8},{12,1... | collective-permute-start | bytes 1179656 | tf_op jit(solution)/shard_map/ppermute | solution.py:63
  270.8 11.6 %collective-permute-start.32 = (bf16[512,384]{1,0:T(8,128)(2,1)S(1)}, bf16[512,384]{1,0:T(8,128)(2,1)S(1)}, u32[]{:S(2)}, u32[]{:S(2)}) collective-permute-start(bf16[512,384]{1,0:T(8,128)(2,1)S(1)} %get-tuple-element.17), channel_id=1, source_target_pairs={{0,2},{2,4},{4,6},{6,7},{7,5},{5,3},{3,1},{1,0},{8,10},{10,12},{12... | collective-permute-start | bytes 1179656 | tf_op jit(solution)/shard_map/ppermute | solution.py:61
  271.5 11.2 %collective-permute-start.39 = (bf16[512,384]{1,0:T(8,128)(2,1)S(1)}, bf16[512,384]{1,0:T(8,128)(2,1)S(1)}, u32[]{:S(2)}, u32[]{:S(2)}) collective-permute-start(bf16[512,384]{1,0:T(8,128)(2,1)S(1)} %get-tuple-element.18), channel_id=1, source_target_pairs={{0,1},{2,0},{4,2},{6,4},{7,6},{5,7},{3,5},{1,3},{8,9},{10,8},{12,1... | collective-permute-start | bytes 1179656 | tf_op jit(solution)/shard_map/ppermute | solution.py:63
  284.0 10.5 %collective-permute-start.33 = (bf16[512,384]{1,0:T(8,128)(2,1)S(1)}, bf16[512,384]{1,0:T(8,128)(2,1)S(1)}, u32[]{:S(2)}, u32[]{:S(2)}) collective-permute-start(bf16[512,384]{1,0:T(8,128)(2,1)S(1)} %get-tuple-element.15), channel_id=1, source_target_pairs={{0,2},{2,4},{4,6},{6,7},{7,5},{5,3},{3,1},{1,0},{8,10},{10,12},{12... | collective-permute-start | bytes 1179656 | tf_op jit(solution)/shard_map/ppermute | solution.py:61
  284.4 10.4 %collective-permute-start.40 = (bf16[512,384]{1,0:T(8,128)(2,1)S(1)}, bf16[512,384]{1,0:T(8,128)(2,1)S(1)}, u32[]{:S(2)}, u32[]{:S(2)}) collective-permute-start(bf16[512,384]{1,0:T(8,128)(2,1)S(1)} %get-tuple-element.16), channel_id=1, source_target_pairs={{0,1},{2,0},{4,2},{6,4},{7,6},{5,7},{3,5},{1,3},{8,9},{10,8},{12,1... | collective-permute-start | bytes 1179656 | tf_op jit(solution)/shard_map/ppermute | solution.py:63
  296.1 10.3 %collective-permute-start.34 = (bf16[512,384]{1,0:T(8,128)(2,1)S(1)}, bf16[512,384]{1,0:T(8,128)(2,1)S(1)}, u32[]{:S(2)}, u32[]{:S(2)}) collective-permute-start(bf16[512,384]{1,0:T(8,128)(2,1)S(1)} %get-tuple-element.13), channel_id=1, source_target_pairs={{0,2},{2,4},{4,6},{6,7},{7,5},{5,3},{3,1},{1,0},{8,10},{10,12},{12... | collective-permute-start | bytes 1179656 | tf_op jit(solution)/shard_map/ppermute | solution.py:61
  296.6 10.6 %collective-permute-start.41 = (bf16[512,384]{1,0:T(8,128)(2,1)S(1)}, bf16[512,384]{1,0:T(8,128)(2,1)}, u32[]{:S(2)}, u32[]{:S(2)}) collective-permute-start(bf16[512,384]{1,0:T(8,128)(2,1)S(1)} %get-tuple-element.14), channel_id=1, source_target_pairs={{0,1},{2,0},{4,2},{6,4},{7,6},{5,7},{3,5},{1,3},{8,9},{10,8},{12,1... | collective-permute-start | bytes 1179656 | tf_op jit(solution)/shard_map/ppermute | solution.py:63
  308.8 7.8 %collective-permute-start.35 = (bf16[512,384]{1,0:T(8,128)(2,1)S(1)}, bf16[512,384]{1,0:T(8,128)(2,1)S(1)}, u32[]{:S(2)}, u32[]{:S(2)}) collective-permute-start(bf16[512,384]{1,0:T(8,128)(2,1)S(1)} %get-tuple-element.11), channel_id=1, source_target_pairs={{0,2},{2,4},{4,6},{6,7},{7,5},{5,3},{3,1},{1,0},{8,10},{10,12},{12... | collective-permute-start | bytes 1179656 | tf_op jit(solution)/shard_map/ppermute | solution.py:61
  309.6 7.9 %collective-permute-start.42 = (bf16[512,384]{1,0:T(8,128)(2,1)S(1)}, bf16[512,384]{1,0:T(8,128)(2,1)}, u32[]{:S(2)}, u32[]{:S(2)}) collective-permute-start(bf16[512,384]{1,0:T(8,128)(2,1)S(1)} %get-tuple-element.12), channel_id=1, source_target_pairs={{0,1},{2,0},{4,2},{6,4},{7,6},{5,7},{3,5},{1,3},{8,9},{10,8},{12,1... | collective-permute-start | bytes 1179656 | tf_op jit(solution)/shard_map/ppermute | solution.py:63
  (23 other events, 322.4 us)
Sparse Core Ops, SparseCore 0:
  8.9 18.3 all-gather.2
  28.9 17.9 all-gather.4

commit v11 on v10

--- a/solution.py
+++ b/solution.py
@@ -24,8 +24,8 @@
     return list(range(0, count, 2)) + list(range(count - 1, 0, -2)) if count % 2 == 0 else list(range(count))
 
 
-def ring_gather(block, axis_name, count):
-    cycle = snake_cycle(count)
+def ring_gather(block, axis_name, count, reverse=False):
+    cycle = snake_cycle(count)[::-1] if reverse else snake_cycle(count)
     ahead = [(cycle[p], cycle[(p + 1) % count]) for p in range(count)]
     behind = [(cycle[p], cycle[(p - 1) % count]) for p in range(count)]
     blocks = [block]
@@ -217,7 +217,7 @@
     if gather_weights:
         column_part = model_width // span_count
         w_out_part = lax.dynamic_slice_in_dim(w_out, span_index * column_part, column_part, 1)
-        mine_blocks = ring_gather(w_out_part, "tp", tp_count)
+        mine_blocks = ring_gather(w_out_part, "tp", tp_count, reverse=True)
         other_blocks = [lax.ppermute(b, "span", [(0, 1), (1, 0)]) for b in mine_blocks]
     up_full, down_full = (
         lax.all_gather(w_up, "span", axis=1, tiled=True),
@@ -258,7 +258,9 @@
         lambda q_rows, c_seen, f_seen: attend(q_rows, cache_all, fresh_all, c_seen, f_seen)
     )(queries, cache_seen, fresh_seen)
     if gather_weights:
-        att_blocks = ring_gather(attended.reshape(token_count, per_device), "tp", tp_count)
+        att_blocks = ring_gather(
+            attended.reshape(token_count, per_device), "tp", tp_count, reverse=True
+        )
         residual_rows, square_sums = grouped_out_proj(
             span_index,
             att_blocks,

time: 330 us -> 343 us (1.039)
  waiting for transfers between devices: 158 us -> 172 us
    ppermute x9, waiting for transfers between devices: 21.1 us -> 30.1 us  [ring_gather(): backward = lax.ppermute(backward, axis_name, behind)]
    ppermute x12, starting transfers between devices: 21.6 us -> 14.7 us  [ring_gather(): forward = lax.ppermute(forward, axis_name, ahead)]
    ppermute x12, waiting for transfers between devices: 78.7 us -> 83.9 us  [ring_gather(): forward = lax.ppermute(forward, axis_name, ahead)]
    ppermute x9, starting transfers between devices: 3.17 us -> 8.23 us  [ring_gather(): backward = lax.ppermute(backward, axis_name, behind)]
where the time goes in v11:
time: 343 us; the launch traced here: 342 us
  waiting for transfers between devices  172 us (50%)
  starting transfers between devices  38.6 us (11%)
  between operations  33.1 us (10%)
  local copies, waits for them, and re-layouts  25.9 us (8%)
  matrix products  24.8 us (7%)
  Pallas kernels  23.1 us (7%)
  other arithmetic  19.3 us (6%)
  blocking collectives  4.54 us (1%)
    ppermute x12, waiting for transfers between devices, ring_gather(): forward = lax.ppermute(forward, axis_name, ahead)  83.9 us
    ppermute x7, waiting for transfers between devices, ring_reduce_scatter(): lax.ppermute(forward.astype(jnp.bfloat16), axis_name, ahead)  50 us
    ppermute x9, waiting for transfers between devices, ring_gather(): backward = lax.ppermute(backward, axis_name, behind)  30.1 us
    pallas_call x1, Pallas kernels, grouped_out_proj(): pl.pallas_call(functools.partial(out_proj_kernel, group_count, tiles_per_...  23.1 us
    ppermute x12, starting transfers between devices, ring_gather(): forward = lax.ppermute(forward, axis_name, ahead)  14.7 us
    unnamed x59, local copies, waits for them, and re-layouts  11 us
    dot_general x1, matrix products, local(): pre_act = jnp.dot(mlp_in, up_full, preferred_element_type=jnp.float32)  10 us
    ppermute x9, starting transfers between devices, ring_gather(): backward = lax.ppermute(backward, axis_name, behind)  8.23 us
  transfers between devices with their start and end apart: 45, of which 24 were waited for; matrix products, arithmetic and copies ran while one was open for 14% of the time, Pallas kernels for 7%

profile of v11, /device:TPU:0, one launch (start us, length us, event | category | flops | bytes accessed | tf_op | source)
XLA Modules:
  0.0 341.6 jit_solution(7954026760571014488)
XLA Ops:
  7.4 3.1 collective-permute-start
  10.5 2.0 collective-permute-start.14
  14.5 14.6 %collective-permute-done = bf16[4,128,768]{2,1,0:T(8,128)(2,1)} collective-permute-done((bf16[4,128,768]{2,1,0:T(8,128)(2,1)}, bf16[4,128,768]{2,1,0:T(8,128)(2,1)}, u32[]{:S(2)}, u32[]{:S(2)}) %collective-permute-start) | collective-permute-done | bytes 786464 | tf_op jit(solution)/shard_map/ppermute | solution.py:34
  29.1 2.1 collective-permute-start.1
  31.5 30.3 %collective-permute-done.1 = bf16[4,128,768]{2,1,0:T(8,128)(2,1)S(1)} collective-permute-done((bf16[4,128,768]{2,1,0:T(8,128)(2,1)}, bf16[4,128,768]{2,1,0:T(8,128)(2,1)S(1)}, u32[]{:S(2)}, u32[]{:S(2)}) %collective-permute-start.1) | collective-permute-done | bytes 786464 | tf_op jit(solution)/shard_map/ppermute | solution.py:34
  61.8 1.8 collective-permute-start.2
  65.4 2.2 all_gather.12
  67.7 13.0 %collective-permute-done.2 = bf16[4,128,768]{2,1,0:T(8,128)(2,1)} collective-permute-done((bf16[4,128,768]{2,1,0:T(8,128)(2,1)S(1)}, bf16[4,128,768]{2,1,0:T(8,128)(2,1)}, u32[]{:S(2)}, u32[]{:S(2)}) %collective-permute-start.2) | collective-permute-done | bytes 786464 | tf_op jit(solution)/shard_map/ppermute | solution.py:34
  80.7 1.5 collective-permute-start.3
  96.8 6.7 %copy.32 = bf16[6144,3,128]{0,2,1:T(8,128)(2,1)} copy(bf16[6144,3,128]{2,0,1:T(8,128)(2,1)} %param.22) | data formatting | bytes 9437184 | tf_op args[7]
  114.8 10.6 %collective-permute-done.15.refs_10_ = bf16[128,3072]{1,0:T(8,128)(2,1)} collective-permute-done((bf16[128,3072]{1,0:T(8,128)(2,1)}, bf16[128,3072]{1,0:T(8,128)(2,1)}, u32[]{:S(2)}, u32[]{:S(2)}) %collective-permute-start.15) | collective-permute-done | bytes 786464 | tf_op jit(solution)/shard_map/ppermute | solution.py:34
  125.4 13.8 %collective-permute-done.6 = bf16[4,128,768]{2,1,0:T(8,128)(2,1)S(1)} collective-permute-done((bf16[4,128,768]{2,1,0:T(8,128)(2,1)}, bf16[4,128,768]{2,1,0:T(8,128)(2,1)S(1)}, u32[]{:S(2)}, u32[]{:S(2)}) %collective-permute-start.6) | collective-permute-done | bytes 786464 | tf_op jit(solution)/shard_map/ppermute | solution.py:38
  141.1 2.7 fusion.3
  143.9 5.8 %convolution_convert_fusion.1 = bf16[512,384]{1,0:T(8,128)(2,1)S(1)} fusion(bf16[512,6144]{1,0:T(8,128)(2,1)S(1)} %bitcast.154, bf16[6144,384]{0,1:T(8,128)(2,1)} %bitcast.155), kind=kOutput, calls=%fused_computation.27 | convolution fusion | flops 2416115712 | bytes 11403264 | tf_op jit(solution)/shard_map/dot_general | solution.py:237
  150.5 2.4 all_gather.13
  155.1 1.5 collective-permute-start.20
  158.8 16.3 %collective-permute-done.20.refs_15_ = bf16[128,3072]{1,0:T(8,128)(2,1)S(1)} collective-permute-done((bf16[128,3072]{1,0:T(8,128)(2,1)}, bf16[128,3072]{1,0:T(8,128)(2,1)S(1)}, u32[]{:S(2)}, u32[]{:S(2)}) %collective-permute-start.20) | collective-permute-done | bytes 786464 | tf_op jit(solution)/shard_map/ppermute | solution.py:38
  175.2 1.7 collective-permute-done.17.refs_12_
  178.0 1.4 collective-permute-start.11
  179.4 3.9 %collective-permute-done.7.refs_1_ = bf16[512,128]{1,0:T(8,128)(2,1)S(1)} collective-permute-done((bf16[512,128]{1,0:T(8,128)(2,1)S(1)}, bf16[512,128]{1,0:T(8,128)(2,1)S(1)}, u32[]{:S(2)}, u32[]{:S(2)}) %collective-permute-start.7) | collective-permute-done | bytes 131104 | tf_op jit(solution)/shard_map/ppermute | solution.py:34
  183.9 1.4 collective-permute-start.12
  185.3 3.1 collective-permute-done.8.refs_2_
  190.5 2.9 collective-permute-done.9.refs_3_
  194.6 3.7 %collective-permute-done.10.refs_4_ = bf16[512,128]{1,0:T(8,128)(2,1)S(1)} collective-permute-done((bf16[512,128]{1,0:T(8,128)(2,1)S(1)}, bf16[512,128]{1,0:T(8,128)(2,1)S(1)}, u32[]{:S(2)}, u32[]{:S(2)}) %collective-permute-start.10) | collective-permute-done | bytes 131104 | tf_op jit(solution)/shard_map/ppermute | solution.py:34
  199.0 23.1 %shard_map.145 = (f32[512,6144]{1,0:T(8,128)}, f32[512,1536]{1,0:T(8,128)}) custom-call(s32[1]{0:T(128)} %bitcast.span_ref, bf16[512,128]{1,0:T(8,128)(2,1)} %bitcast.167, bf16[512,128]{1,0:T(8,128)(2,1)} %copy-done.17, bf16[512,128]{1,0:T(8,128)(2,1)} %copy-done.19, bf16[512,128]{1,0:T(8,128)(2,1)} %copy-done.21, bf16[512,128]{1,0:T(8,128)(2,1)} %copy-done.23, ...), custom_call_target="tpu_custom_call" | custom-call | flops 6442450944 | bytes 32505856 | tf_op jit(solution)/shard_map/pallas_call | solution.py:128
  222.1 3.5 %copy.39 = f32[512,1536]{0,1:T(8,128)} copy(f32[512,1536]{1,0:T(8,128)} %get-tuple-element.8) | data formatting | bytes 6291456 | tf_op jit(solution)/shard_map/pallas_call | solution.py:128
  226.7 10.0 %fusion.27 = bf16[4,128,512]{2,1,0:T(8,128)(2,1)S(1)} fusion(bf16[6144,512]{1,0:T(8,128)(2,1)} %all-gather.3.cloned.1.call-done, f32[4,128,6144]{2,1,0:T(8,128)} %bitcast.161, f32[4,6144]{1,0:T(4,128)S(1)} %copy-done.11, f32[4,6144]{1,0:T(4,128)S(1)} %get-tuple-element.29, f32[4,128]{1,0:T(4,128)S(1)} %rsqrt_bitcast_fusion), kind=kOutput, calls=%fused_computation.38 | convolution fusion | flops 3236167680 | bytes 19597312 | tf_op jit(solution)/shard_map/dot_general | solution.py:292
  236.7 6.4 %convolution_convert_fusion = bf16[4,128,6144]{2,1,0:T(8,128)(2,1)S(1)} fusion(bf16[4,128,512]{2,1,0:T(8,128)(2,1)S(1)} %fusion.27, bf16[512,6144]{1,0:T(8,128)(2,1)} %all-gather.5.cloned.1.call-done), kind=kOutput, calls=%fused_computation.7 | convolution fusion | flops 3224371200 | bytes 13107200 | tf_op jit(solution)/shard_map/dot_general | solution.py:294
  243.2 2.6 copy-done.3
  245.9 1.6 collective-permute-start.29
  249.2 4.5 %collective-permute-done.29 = bf16[512,384]{1,0:T(8,128)(2,1)S(1)} collective-permute-done((bf16[512,384]{1,0:T(8,128)(2,1)S(1)}, bf16[512,384]{1,0:T(8,128)(2,1)S(1)}, u32[]{:S(2)}, u32[]{:S(2)}) %collective-permute-start.29) | collective-permute-done | bytes 393248 | tf_op jit(solution)/shard_map/ppermute | solution.py:61
  253.7 1.6 collective-permute-done.36
  256.6 1.6 collective-permute-start.30
  260.0 4.9 %collective-permute-done.30 = bf16[512,384]{1,0:T(8,128)(2,1)S(1)} collective-permute-done((bf16[512,384]{1,0:T(8,128)(2,1)S(1)}, bf16[512,384]{1,0:T(8,128)(2,1)S(1)}, u32[]{:S(2)}, u32[]{:S(2)}) %collective-permute-start.30) | collective-permute-done | bytes 393248 | tf_op jit(solution)/shard_map/ppermute | solution.py:61
  264.9 2.0 collective-permute-done.37
  268.1 2.6 collective-permute-start.31
  271.3 7.3 %collective-permute-done.31 = bf16[512,384]{1,0:T(8,128)(2,1)S(1)} collective-permute-done((bf16[512,384]{1,0:T(8,128)(2,1)S(1)}, bf16[512,384]{1,0:T(8,128)(2,1)S(1)}, u32[]{:S(2)}, u32[]{:S(2)}) %collective-permute-start.31) | collective-permute-done | bytes 393248 | tf_op jit(solution)/shard_map/ppermute | solution.py:61
  278.7 2.8 collective-permute-done.38
  283.3 1.6 collective-permute-start.39
  284.9 9.9 %collective-permute-done.32 = bf16[512,384]{1,0:T(8,128)(2,1)S(1)} collective-permute-done((bf16[512,384]{1,0:T(8,128)(2,1)S(1)}, bf16[512,384]{1,0:T(8,128)(2,1)S(1)}, u32[]{:S(2)}, u32[]{:S(2)}) %collective-permute-start.32) | collective-permute-done | bytes 393248 | tf_op jit(solution)/shard_map/ppermute | solution.py:61
  296.9 1.6 collective-permute-start.40
  298.5 8.9 %collective-permute-done.33 = bf16[512,384]{1,0:T(8,128)(2,1)S(1)} collective-permute-done((bf16[512,384]{1,0:T(8,128)(2,1)S(1)}, bf16[512,384]{1,0:T(8,128)(2,1)S(1)}, u32[]{:S(2)}, u32[]{:S(2)}) %collective-permute-start.33) | collective-permute-done | bytes 393248 | tf_op jit(solution)/shard_map/ppermute | solution.py:61
  309.3 1.7 collective-permute-start.41
  311.0 8.8 %collective-permute-done.34 = bf16[512,384]{1,0:T(8,128)(2,1)S(1)} collective-permute-done((bf16[512,384]{1,0:T(8,128)(2,1)S(1)}, bf16[512,384]{1,0:T(8,128)(2,1)S(1)}, u32[]{:S(2)}, u32[]{:S(2)}) %collective-permute-start.34) | collective-permute-done | bytes 393248 | tf_op jit(solution)/shard_map/ppermute | solution.py:61
  320.5 1.6 add_convert_fusion.13
  322.7 1.5 collective-permute-start.42
  324.2 5.7 %collective-permute-done.35 = bf16[512,384]{1,0:T(8,128)(2,1)S(1)} collective-permute-done((bf16[512,384]{1,0:T(8,128)(2,1)S(1)}, bf16[512,384]{1,0:T(8,128)(2,1)S(1)}, u32[]{:S(2)}, u32[]{:S(2)}) %collective-permute-start.35) | collective-permute-done | bytes 393248 | tf_op jit(solution)/shard_map/ppermute | solution.py:61
  332.1 2.6 add_convert_fusion.2
  (161 shorter events, 41.6 us)
Async XLA Ops:
  6.5 84.6 %copy-start.10 = (s32[8]{0:T(128)S(1)}, s32[8]{0:T(128)}, u32[]{:S(2)}) copy-start(s32[8]{0:T(128)} %constant.289.clone) | copy-start | bytes 100
  6.6 58.8 %copy-start.9 = (bf16[4,128,2,128]{3,2,1,0:T(2,128)(2,1)S(1)}, bf16[4,128,2,128]{3,2,1,0:T(2,128)(2,1)}, u32[]{:S(2)}) copy-start(bf16[4,128,2,128]{3,2,1,0:T(2,128)(2,1)} %param.20) | copy-start | bytes 786436
  6.6 220.1 %all-gather.3.cloned.1.call-start = ((), (), s32[]{:S(2)}) async-start(), calls=%async_computation | async-start | bytes 9437184 | tf_op jit(solution)/shard_map/all_gather | solution.py:223
  7.3 229.4 %all-gather.5.cloned.1.call-start = ((), (), s32[]{:S(2)}) async-start(), calls=%async_computation.1 | async-start | bytes 9437184 | tf_op jit(solution)/shard_map/all_gather | solution.py:224
  7.4 21.7 %collective-permute-start = (bf16[4,128,768]{2,1,0:T(8,128)(2,1)}, bf16[4,128,768]{2,1,0:T(8,128)(2,1)}, u32[]{:S(2)}, u32[]{:S(2)}) collective-permute-start(bf16[4,128,768]{2,1,0:T(8,128)(2,1)} %param.15), channel_id=1, source_target_pairs={{0,2},{2,4},{4,6},{6,7},{7,5},{5,3},{3,1},{1,0},{8,10},{10,12},{12... | collective-permute-start | bytes 2359304 | tf_op jit(solution)/shard_map/ppermute | solution.py:34
  10.4 53.3 %collective-permute-start.4 = (bf16[4,128,768]{2,1,0:T(8,128)(2,1)}, bf16[4,128,768]{2,1,0:T(8,128)(2,1)}, u32[]{:S(2)}, u32[]{:S(2)}) collective-permute-start(bf16[4,128,768]{2,1,0:T(8,128)(2,1)} %param.15), channel_id=1, source_target_pairs={{0,1},{2,0},{4,2},{6,4},{7,6},{5,7},{3,5},{1,3},{8,9},{10,8},{12,1... | collective-permute-start | bytes 2359304 | tf_op jit(solution)/shard_map/ppermute | solution.py:38
  10.5 93.0 %copy-start.5 = (bf16[128,3072]{1,0:T(8,128)(2,1)}, bf16[128,3072]{1,0:T(8,128)(2,1)S(1)}, u32[]{:S(2)}) copy-start(bf16[128,3072]{1,0:T(8,128)(2,1)S(1)} %constant_dynamic-slice_fusion.2.refs_8_) | copy-start | bytes 2359300
  10.5 94.0 %collective-permute-start.14 = (bf16[128,3072]{1,0:T(8,128)(2,1)S(1)}, bf16[128,3072]{1,0:T(8,128)(2,1)}, u32[]{:S(2)}, u32[]{:S(2)}) collective-permute-start(bf16[128,3072]{1,0:T(8,128)(2,1)S(1)} %constant_dynamic-slice_fusion.2.refs_8_), channel_id=1, source_target_pairs={{1,3},{3,5},{5,7},{7,6},{6,4},{4,2},{2,0},{0,1},{9,11},{11,13},{13... | collective-permute-start | bytes 2359304 | tf_op jit(solution)/shard_map/ppermute | solution.py:34
  12.5 97.7 %collective-permute-start.18 = (bf16[128,3072]{1,0:T(8,128)(2,1)S(1)}, bf16[128,3072]{1,0:T(8,128)(2,1)}, u32[]{:S(2)}, u32[]{:S(2)}) collective-permute-start(bf16[128,3072]{1,0:T(8,128)(2,1)S(1)} %constant_dynamic-slice_fusion.2.refs_8_), channel_id=1, source_target_pairs={{1,0},{3,1},{5,3},{7,5},{6,7},{4,6},{2,4},{0,2},{9,8},{11,9},{13,1... | collective-permute-start | bytes 2359304 | tf_op jit(solution)/shard_map/ppermute | solution.py:38
  12.7 142.3 %collective-permute-start.21 = (bf16[128,3072]{1,0:T(8,128)(2,1)S(1)}, bf16[128,3072]{1,0:T(8,128)(2,1)}, u32[]{:S(2)}, u32[]{:S(2)}) collective-permute-start(bf16[128,3072]{1,0:T(8,128)(2,1)S(1)} %constant_dynamic-slice_fusion.2.refs_8_), channel_id=1, source_target_pairs={{0,8},{8,0},{1,9},{9,1},{2,10},{10,2},{3,11},{11,3},{4,12},{12,4},... | collective-permute-start | bytes 2359304 | tf_op jit(solution)/shard_map/ppermute | solution.py:221
  29.1 32.8 %collective-permute-start.1 = (bf16[4,128,768]{2,1,0:T(8,128)(2,1)}, bf16[4,128,768]{2,1,0:T(8,128)(2,1)S(1)}, u32[]{:S(2)}, u32[]{:S(2)}) collective-permute-start(bf16[4,128,768]{2,1,0:T(8,128)(2,1)} %collective-permute-done), channel_id=1, source_target_pairs={{0,2},{2,4},{4,6},{6,7},{7,5},{5,3},{3,1},{1,0},{8,10},{10,12},{12... | collective-permute-start | bytes 2359304 | tf_op jit(solution)/shard_map/ppermute | solution.py:34
  61.8 18.8 %collective-permute-start.2 = (bf16[4,128,768]{2,1,0:T(8,128)(2,1)S(1)}, bf16[4,128,768]{2,1,0:T(8,128)(2,1)}, u32[]{:S(2)}, u32[]{:S(2)}) collective-permute-start(bf16[4,128,768]{2,1,0:T(8,128)(2,1)S(1)} %collective-permute-done.1), channel_id=1, source_target_pairs={{0,2},{2,4},{4,6},{6,7},{7,5},{5,3},{3,1},{1,0},{8,10},{10,12},{12... | collective-permute-start | bytes 2359304 | tf_op jit(solution)/shard_map/ppermute | solution.py:34
  63.7 41.4 %collective-permute-start.5 = (bf16[4,128,768]{2,1,0:T(8,128)(2,1)}, bf16[4,128,768]{2,1,0:T(8,128)(2,1)}, u32[]{:S(2)}, u32[]{:S(2)}) collective-permute-start(bf16[4,128,768]{2,1,0:T(8,128)(2,1)} %collective-permute-done.4), channel_id=1, source_target_pairs={{0,1},{2,0},{4,2},{6,4},{7,6},{5,7},{3,5},{1,3},{8,9},{10,8},{12,1... | collective-permute-start | bytes 2359304 | tf_op jit(solution)/shard_map/ppermute | solution.py:38
  80.7 29.7 %collective-permute-start.3 = (bf16[4,128,768]{2,1,0:T(8,128)(2,1)}, bf16[4,128,768]{2,1,0:T(8,128)(2,1)}, u32[]{:S(2)}, u32[]{:S(2)}) collective-permute-start(bf16[4,128,768]{2,1,0:T(8,128)(2,1)} %collective-permute-done.2), channel_id=1, source_target_pairs={{0,2},{2,4},{4,6},{6,7},{7,5},{5,3},{3,1},{1,0},{8,10},{10,12},{12... | collective-permute-start | bytes 2359304 | tf_op jit(solution)/shard_map/ppermute | solution.py:34
  104.5 20.8 %collective-permute-start.15 = (bf16[128,3072]{1,0:T(8,128)(2,1)}, bf16[128,3072]{1,0:T(8,128)(2,1)}, u32[]{:S(2)}, u32[]{:S(2)}) collective-permute-start(bf16[128,3072]{1,0:T(8,128)(2,1)} %collective-permute-done.14.refs_9_), channel_id=1, source_target_pairs={{1,3},{3,5},{5,7},{7,6},{6,4},{4,2},{2,0},{0,1},{9,11},{11,13},{13... | collective-permute-start | bytes 2359304 | tf_op jit(solution)/shard_map/ppermute | solution.py:34
  105.1 34.0 %collective-permute-start.6 = (bf16[4,128,768]{2,1,0:T(8,128)(2,1)}, bf16[4,128,768]{2,1,0:T(8,128)(2,1)S(1)}, u32[]{:S(2)}, u32[]{:S(2)}) collective-permute-start(bf16[4,128,768]{2,1,0:T(8,128)(2,1)} %collective-permute-done.5), channel_id=1, source_target_pairs={{0,1},{2,0},{4,2},{6,4},{7,6},{5,7},{3,5},{1,3},{8,9},{10,8},{12,1... | collective-permute-start | bytes 2359304 | tf_op jit(solution)/shard_map/ppermute | solution.py:38
  110.3 46.3 %collective-permute-start.22 = (bf16[128,3072]{1,0:T(8,128)(2,1)}, bf16[128,3072]{1,0:T(8,128)(2,1)}, u32[]{:S(2)}, u32[]{:S(2)}) collective-permute-start(bf16[128,3072]{1,0:T(8,128)(2,1)} %collective-permute-done.14.refs_9_), channel_id=1, source_target_pairs={{0,8},{8,0},{1,9},{9,1},{2,10},{10,2},{3,11},{11,3},{4,12},{12,4},... | collective-permute-start | bytes 2359304 | tf_op jit(solution)/shard_map/ppermute | solution.py:221
  110.4 44.8 %collective-permute-start.19 = (bf16[128,3072]{1,0:T(8,128)(2,1)}, bf16[128,3072]{1,0:T(8,128)(2,1)}, u32[]{:S(2)}, u32[]{:S(2)}) collective-permute-start(bf16[128,3072]{1,0:T(8,128)(2,1)} %collective-permute-done.18.refs_13_), channel_id=1, source_target_pairs={{1,0},{3,1},{5,3},{7,5},{6,7},{4,6},{2,4},{0,2},{9,8},{11,9},{13,1... | collective-permute-start | bytes 2359304 | tf_op jit(solution)/shard_map/ppermute | solution.py:38
  125.4 33.2 %collective-permute-start.26 = (bf16[128,3072]{1,0:T(8,128)(2,1)}, bf16[128,3072]{1,0:T(8,128)(2,1)}, u32[]{:S(2)}, u32[]{:S(2)}) collective-permute-start(bf16[128,3072]{1,0:T(8,128)(2,1)} %collective-permute-done.18.refs_13_), channel_id=1, source_target_pairs={{0,8},{8,0},{1,9},{9,1},{2,10},{10,2},{3,11},{11,3},{4,12},{12,4},... | collective-permute-start | bytes 2359304 | tf_op jit(solution)/shard_map/ppermute | solution.py:221
  139.1 17.5 %collective-permute-start.16 = (bf16[128,3072]{1,0:T(8,128)(2,1)}, bf16[128,3072]{1,0:T(8,128)(2,1)}, u32[]{:S(2)}, u32[]{:S(2)}) collective-permute-start(bf16[128,3072]{1,0:T(8,128)(2,1)} %collective-permute-done.15.refs_10_), channel_id=1, source_target_pairs={{1,3},{3,5},{5,7},{7,6},{6,4},{4,2},{2,0},{0,1},{9,11},{11,13},{13... | collective-permute-start | bytes 2359304 | tf_op jit(solution)/shard_map/ppermute | solution.py:34
  154.9 22.4 %collective-permute-start.23 = (bf16[128,3072]{1,0:T(8,128)(2,1)}, bf16[128,3072]{1,0:T(8,128)(2,1)S(1)}, u32[]{:S(2)}, u32[]{:S(2)}) collective-permute-start(bf16[128,3072]{1,0:T(8,128)(2,1)} %collective-permute-done.15.refs_10_), channel_id=1, source_target_pairs={{0,8},{8,0},{1,9},{9,1},{2,10},{10,2},{3,11},{11,3},{4,12},{12,4},... | collective-permute-start | bytes 2359304 | tf_op jit(solution)/shard_map/ppermute | solution.py:221
  155.1 20.0 %collective-permute-start.20 = (bf16[128,3072]{1,0:T(8,128)(2,1)}, bf16[128,3072]{1,0:T(8,128)(2,1)S(1)}, u32[]{:S(2)}, u32[]{:S(2)}) collective-permute-start(bf16[128,3072]{1,0:T(8,128)(2,1)} %collective-permute-done.19.refs_14_), channel_id=1, source_target_pairs={{1,0},{3,1},{5,3},{7,5},{6,7},{4,6},{2,4},{0,2},{9,8},{11,9},{13,1... | collective-permute-start | bytes 2359304 | tf_op jit(solution)/shard_map/ppermute | solution.py:38
  156.6 21.4 %collective-permute-start.27 = (bf16[128,3072]{1,0:T(8,128)(2,1)}, bf16[128,3072]{1,0:T(8,128)(2,1)}, u32[]{:S(2)}, u32[]{:S(2)}) collective-permute-start(bf16[128,3072]{1,0:T(8,128)(2,1)} %collective-permute-done.19.refs_14_), channel_id=1, source_target_pairs={{0,8},{8,0},{1,9},{9,1},{2,10},{10,2},{3,11},{11,3},{4,12},{12,4},... | collective-permute-start | bytes 2359304 | tf_op jit(solution)/shard_map/ppermute | solution.py:221
  156.7 20.2 %collective-permute-start.17 = (bf16[128,3072]{1,0:T(8,128)(2,1)}, bf16[128,3072]{1,0:T(8,128)(2,1)}, u32[]{:S(2)}, u32[]{:S(2)}) collective-permute-start(bf16[128,3072]{1,0:T(8,128)(2,1)} %collective-permute-done.16.refs_11_), channel_id=1, source_target_pairs={{1,3},{3,5},{5,7},{7,6},{6,4},{4,2},{2,0},{0,1},{9,11},{11,13},{13... | collective-permute-start | bytes 2359304 | tf_op jit(solution)/shard_map/ppermute | solution.py:34
  158.6 36.0 %collective-permute-start.24 = (bf16[128,3072]{1,0:T(8,128)(2,1)}, bf16[128,3072]{1,0:T(8,128)(2,1)}, u32[]{:S(2)}, u32[]{:S(2)}) collective-permute-start(bf16[128,3072]{1,0:T(8,128)(2,1)} %collective-permute-done.16.refs_11_), channel_id=1, source_target_pairs={{0,8},{8,0},{1,9},{9,1},{2,10},{10,2},{3,11},{11,3},{4,12},{12,4},... | collective-permute-start | bytes 2359304 | tf_op jit(solution)/shard_map/ppermute | solution.py:221
  175.2 19.5 %collective-permute-start.28 = (bf16[128,3072]{1,0:T(8,128)(2,1)S(1)}, bf16[128,3072]{1,0:T(8,128)(2,1)}, u32[]{:S(2)}, u32[]{:S(2)}) collective-permute-start(bf16[128,3072]{1,0:T(8,128)(2,1)S(1)} %collective-permute-done.20.refs_15_), channel_id=1, source_target_pairs={{0,8},{8,0},{1,9},{9,1},{2,10},{10,2},{3,11},{11,3},{4,12},{12,4},... | collective-permute-start | bytes 2359304 | tf_op jit(solution)/shard_map/ppermute | solution.py:221
  176.9 21.5 %collective-permute-start.25 = (bf16[128,3072]{1,0:T(8,128)(2,1)}, bf16[128,3072]{1,0:T(8,128)(2,1)}, u32[]{:S(2)}, u32[]{:S(2)}) collective-permute-start(bf16[128,3072]{1,0:T(8,128)(2,1)} %collective-permute-done.17.refs_12_), channel_id=1, source_target_pairs={{0,8},{8,0},{1,9},{9,1},{2,10},{10,2},{3,11},{11,3},{4,12},{12,4},... | collective-permute-start | bytes 2359304 | tf_op jit(solution)/shard_map/ppermute | solution.py:221
  177.4 6.0 %collective-permute-start.7 = (bf16[512,128]{1,0:T(8,128)(2,1)S(1)}, bf16[512,128]{1,0:T(8,128)(2,1)S(1)}, u32[]{:S(2)}, u32[]{:S(2)}) collective-permute-start(bf16[512,128]{1,0:T(8,128)(2,1)S(1)} %bitcast.165), channel_id=1, source_target_pairs={{1,3},{3,5},{5,7},{7,6},{6,4},{4,2},{2,0},{0,1},{9,11},{11,13},{13... | collective-permute-start | bytes 393224 | tf_op jit(solution)/shard_map/ppermute | solution.py:34
  178.0 5.9 %collective-permute-start.11 = (bf16[512,128]{1,0:T(8,128)(2,1)S(1)}, bf16[512,128]{1,0:T(8,128)(2,1)S(1)}, u32[]{:S(2)}, u32[]{:S(2)}) collective-permute-start(bf16[512,128]{1,0:T(8,128)(2,1)S(1)} %bitcast.166), channel_id=1, source_target_pairs={{1,0},{3,1},{5,3},{7,5},{6,7},{4,6},{2,4},{0,2},{9,8},{11,9},{13,1... | collective-permute-start | bytes 393224 | tf_op jit(solution)/shard_map/ppermute | solution.py:38
  183.3 5.1 %collective-permute-start.8 = (bf16[512,128]{1,0:T(8,128)(2,1)S(1)}, bf16[512,128]{1,0:T(8,128)(2,1)S(1)}, u32[]{:S(2)}, u32[]{:S(2)}) collective-permute-start(bf16[512,128]{1,0:T(8,128)(2,1)S(1)} %collective-permute-done.7.refs_1_), channel_id=1, source_target_pairs={{1,3},{3,5},{5,7},{7,6},{6,4},{4,2},{2,0},{0,1},{9,11},{11,13},{13... | collective-permute-start | bytes 393224 | tf_op jit(solution)/shard_map/ppermute | solution.py:34
  183.9 5.1 %collective-permute-start.12 = (bf16[512,128]{1,0:T(8,128)(2,1)S(1)}, bf16[512,128]{1,0:T(8,128)(2,1)S(1)}, u32[]{:S(2)}, u32[]{:S(2)}) collective-permute-start(bf16[512,128]{1,0:T(8,128)(2,1)S(1)} %collective-permute-done.11.refs_5_), channel_id=1, source_target_pairs={{1,0},{3,1},{5,3},{7,5},{6,7},{4,6},{2,4},{0,2},{9,8},{11,9},{13,1... | collective-permute-start | bytes 393224 | tf_op jit(solution)/shard_map/ppermute | solution.py:38
  188.4 5.0 %collective-permute-start.9 = (bf16[512,128]{1,0:T(8,128)(2,1)S(1)}, bf16[512,128]{1,0:T(8,128)(2,1)S(1)}, u32[]{:S(2)}, u32[]{:S(2)}) collective-permute-start(bf16[512,128]{1,0:T(8,128)(2,1)S(1)} %collective-permute-done.8.refs_2_), channel_id=1, source_target_pairs={{1,3},{3,5},{5,7},{7,6},{6,4},{4,2},{2,0},{0,1},{9,11},{11,13},{13... | collective-permute-start | bytes 393224 | tf_op jit(solution)/shard_map/ppermute | solution.py:34
  189.0 5.6 %collective-permute-start.13 = (bf16[512,128]{1,0:T(8,128)(2,1)S(1)}, bf16[512,128]{1,0:T(8,128)(2,1)S(1)}, u32[]{:S(2)}, u32[]{:S(2)}) collective-permute-start(bf16[512,128]{1,0:T(8,128)(2,1)S(1)} %collective-permute-done.12.refs_6_), channel_id=1, source_target_pairs={{1,0},{3,1},{5,3},{7,5},{6,7},{4,6},{2,4},{0,2},{9,8},{11,9},{13,1... | collective-permute-start | bytes 393224 | tf_op jit(solution)/shard_map/ppermute | solution.py:38
  193.4 5.0 %collective-permute-start.10 = (bf16[512,128]{1,0:T(8,128)(2,1)S(1)}, bf16[512,128]{1,0:T(8,128)(2,1)S(1)}, u32[]{:S(2)}, u32[]{:S(2)}) collective-permute-start(bf16[512,128]{1,0:T(8,128)(2,1)S(1)} %collective-permute-done.9.refs_3_), channel_id=1, source_target_pairs={{1,3},{3,5},{5,7},{7,6},{6,4},{4,2},{2,0},{0,1},{9,11},{11,13},{13... | collective-permute-start | bytes 393224 | tf_op jit(solution)/shard_map/ppermute | solution.py:34
  245.9 7.8 %collective-permute-start.29 = (bf16[512,384]{1,0:T(8,128)(2,1)S(1)}, bf16[512,384]{1,0:T(8,128)(2,1)S(1)}, u32[]{:S(2)}, u32[]{:S(2)}) collective-permute-start(bf16[512,384]{1,0:T(8,128)(2,1)S(1)} %get-tuple-element.23), channel_id=1, source_target_pairs={{0,2},{2,4},{4,6},{6,7},{7,5},{5,3},{3,1},{1,0},{8,10},{10,12},{12... | collective-permute-start | bytes 1179656 | tf_op jit(solution)/shard_map/ppermute | solution.py:61
  247.5 7.8 %collective-permute-start.36 = (bf16[512,384]{1,0:T(8,128)(2,1)S(1)}, bf16[512,384]{1,0:T(8,128)(2,1)S(1)}, u32[]{:S(2)}, u32[]{:S(2)}) collective-permute-start(bf16[512,384]{1,0:T(8,128)(2,1)S(1)} %get-tuple-element.24), channel_id=1, source_target_pairs={{0,1},{2,0},{4,2},{6,4},{7,6},{5,7},{3,5},{1,3},{8,9},{10,8},{12,1... | collective-permute-start | bytes 1179656 | tf_op jit(solution)/shard_map/ppermute | solution.py:63
  256.6 8.3 %collective-permute-start.30 = (bf16[512,384]{1,0:T(8,128)(2,1)S(1)}, bf16[512,384]{1,0:T(8,128)(2,1)S(1)}, u32[]{:S(2)}, u32[]{:S(2)}) collective-permute-start(bf16[512,384]{1,0:T(8,128)(2,1)S(1)} %get-tuple-element.21), channel_id=1, source_target_pairs={{0,2},{2,4},{4,6},{6,7},{7,5},{5,3},{3,1},{1,0},{8,10},{10,12},{12... | collective-permute-start | bytes 1179656 | tf_op jit(solution)/shard_map/ppermute | solution.py:61
  258.2 8.6 %collective-permute-start.37 = (bf16[512,384]{1,0:T(8,128)(2,1)S(1)}, bf16[512,384]{1,0:T(8,128)(2,1)S(1)}, u32[]{:S(2)}, u32[]{:S(2)}) collective-permute-start(bf16[512,384]{1,0:T(8,128)(2,1)S(1)} %get-tuple-element.22), channel_id=1, source_target_pairs={{0,1},{2,0},{4,2},{6,4},{7,6},{5,7},{3,5},{1,3},{8,9},{10,8},{12,1... | collective-permute-start | bytes 1179656 | tf_op jit(solution)/shard_map/ppermute | solution.py:63
  268.1 10.5 %collective-permute-start.31 = (bf16[512,384]{1,0:T(8,128)(2,1)S(1)}, bf16[512,384]{1,0:T(8,128)(2,1)S(1)}, u32[]{:S(2)}, u32[]{:S(2)}) collective-permute-start(bf16[512,384]{1,0:T(8,128)(2,1)S(1)} %get-tuple-element.19), channel_id=1, source_target_pairs={{0,2},{2,4},{4,6},{6,7},{7,5},{5,3},{3,1},{1,0},{8,10},{10,12},{12... | collective-permute-start | bytes 1179656 | tf_op jit(solution)/shard_map/ppermute | solution.py:61
  270.7 10.8 %collective-permute-start.38 = (bf16[512,384]{1,0:T(8,128)(2,1)S(1)}, bf16[512,384]{1,0:T(8,128)(2,1)S(1)}, u32[]{:S(2)}, u32[]{:S(2)}) collective-permute-start(bf16[512,384]{1,0:T(8,128)(2,1)S(1)} %get-tuple-element.20), channel_id=1, source_target_pairs={{0,1},{2,0},{4,2},{6,4},{7,6},{5,7},{3,5},{1,3},{8,9},{10,8},{12,1... | collective-permute-start | bytes 1179656 | tf_op jit(solution)/shard_map/ppermute | solution.py:63
  282.8 12.0 %collective-permute-start.32 = (bf16[512,384]{1,0:T(8,128)(2,1)S(1)}, bf16[512,384]{1,0:T(8,128)(2,1)S(1)}, u32[]{:S(2)}, u32[]{:S(2)}) collective-permute-start(bf16[512,384]{1,0:T(8,128)(2,1)S(1)} %get-tuple-element.17), channel_id=1, source_target_pairs={{0,2},{2,4},{4,6},{6,7},{7,5},{5,3},{3,1},{1,0},{8,10},{10,12},{12... | collective-permute-start | bytes 1179656 | tf_op jit(solution)/shard_map/ppermute | solution.py:61
  283.3 11.8 %collective-permute-start.39 = (bf16[512,384]{1,0:T(8,128)(2,1)S(1)}, bf16[512,384]{1,0:T(8,128)(2,1)S(1)}, u32[]{:S(2)}, u32[]{:S(2)}) collective-permute-start(bf16[512,384]{1,0:T(8,128)(2,1)S(1)} %get-tuple-element.18), channel_id=1, source_target_pairs={{0,1},{2,0},{4,2},{6,4},{7,6},{5,7},{3,5},{1,3},{8,9},{10,8},{12,1... | collective-permute-start | bytes 1179656 | tf_op jit(solution)/shard_map/ppermute | solution.py:63
  296.4 11.0 %collective-permute-start.33 = (bf16[512,384]{1,0:T(8,128)(2,1)S(1)}, bf16[512,384]{1,0:T(8,128)(2,1)S(1)}, u32[]{:S(2)}, u32[]{:S(2)}) collective-permute-start(bf16[512,384]{1,0:T(8,128)(2,1)S(1)} %get-tuple-element.15), channel_id=1, source_target_pairs={{0,2},{2,4},{4,6},{6,7},{7,5},{5,3},{3,1},{1,0},{8,10},{10,12},{12... | collective-permute-start | bytes 1179656 | tf_op jit(solution)/shard_map/ppermute | solution.py:61
  296.9 10.7 %collective-permute-start.40 = (bf16[512,384]{1,0:T(8,128)(2,1)S(1)}, bf16[512,384]{1,0:T(8,128)(2,1)S(1)}, u32[]{:S(2)}, u32[]{:S(2)}) collective-permute-start(bf16[512,384]{1,0:T(8,128)(2,1)S(1)} %get-tuple-element.16), channel_id=1, source_target_pairs={{0,1},{2,0},{4,2},{6,4},{7,6},{5,7},{3,5},{1,3},{8,9},{10,8},{12,1... | collective-permute-start | bytes 1179656 | tf_op jit(solution)/shard_map/ppermute | solution.py:63
  308.9 10.9 %collective-permute-start.34 = (bf16[512,384]{1,0:T(8,128)(2,1)S(1)}, bf16[512,384]{1,0:T(8,128)(2,1)S(1)}, u32[]{:S(2)}, u32[]{:S(2)}) collective-permute-start(bf16[512,384]{1,0:T(8,128)(2,1)S(1)} %get-tuple-element.13), channel_id=1, source_target_pairs={{0,2},{2,4},{4,6},{6,7},{7,5},{5,3},{3,1},{1,0},{8,10},{10,12},{12... | collective-permute-start | bytes 1179656 | tf_op jit(solution)/shard_map/ppermute | solution.py:61
  309.3 11.2 %collective-permute-start.41 = (bf16[512,384]{1,0:T(8,128)(2,1)S(1)}, bf16[512,384]{1,0:T(8,128)(2,1)}, u32[]{:S(2)}, u32[]{:S(2)}) collective-permute-start(bf16[512,384]{1,0:T(8,128)(2,1)S(1)} %get-tuple-element.14), channel_id=1, source_target_pairs={{0,1},{2,0},{4,2},{6,4},{7,6},{5,7},{3,5},{1,3},{8,9},{10,8},{12,1... | collective-permute-start | bytes 1179656 | tf_op jit(solution)/shard_map/ppermute | solution.py:63
  322.1 7.8 %collective-permute-start.35 = (bf16[512,384]{1,0:T(8,128)(2,1)S(1)}, bf16[512,384]{1,0:T(8,128)(2,1)S(1)}, u32[]{:S(2)}, u32[]{:S(2)}) collective-permute-start(bf16[512,384]{1,0:T(8,128)(2,1)S(1)} %get-tuple-element.11), channel_id=1, source_target_pairs={{0,2},{2,4},{4,6},{6,7},{7,5},{5,3},{3,1},{1,0},{8,10},{10,12},{12... | collective-permute-start | bytes 1179656 | tf_op jit(solution)/shard_map/ppermute | solution.py:61
  322.7 7.9 %collective-permute-start.42 = (bf16[512,384]{1,0:T(8,128)(2,1)S(1)}, bf16[512,384]{1,0:T(8,128)(2,1)}, u32[]{:S(2)}, u32[]{:S(2)}) collective-permute-start(bf16[512,384]{1,0:T(8,128)(2,1)S(1)} %get-tuple-element.12), channel_id=1, source_target_pairs={{0,1},{2,0},{4,2},{6,4},{7,6},{5,7},{3,5},{1,3},{8,9},{10,8},{12,1... | collective-permute-start | bytes 1179656 | tf_op jit(solution)/shard_map/ppermute | solution.py:63
  (23 other events, 326.6 us)
Sparse Core Ops, SparseCore 0:
  8.9 18.3 all-gather.2
  28.9 17.9 all-gather.4

commit v12 on v10

--- a/solution.py
+++ b/solution.py
@@ -211,14 +211,16 @@
             owner = owners[(position - step + tp_count) % tp_count]
             gathered = lax.dynamic_update_slice_in_dim(gathered, piece, owner * share_width, 2)
         gathered_narrow = gathered
-        gathered = gathered.astype(jnp.float32)
     else:
         gathered = lax.all_gather(hidden_in, "tp", axis=2, tiled=True).astype(jnp.float32)
     if gather_weights:
         column_part = model_width // span_count
         w_out_part = lax.dynamic_slice_in_dim(w_out, span_index * column_part, column_part, 1)
+        gathered_narrow, w_out_part = lax.optimization_barrier((gathered_narrow, w_out_part))
         mine_blocks = ring_gather(w_out_part, "tp", tp_count)
         other_blocks = [lax.ppermute(b, "span", [(0, 1), (1, 0)]) for b in mine_blocks]
+    if gather_weights:
+        gathered = gathered_narrow.astype(jnp.float32)
     up_full, down_full = (
         lax.all_gather(w_up, "span", axis=1, tiled=True),
         lax.all_gather(w_down, "span", axis=0, tiled=True),

time: 330 us -> 348 us (1.055)
  local copies, waits for them, and re-layouts: 25.9 us -> 38.2 us
  other arithmetic: 19.3 us -> 25 us
    dynamic_update_slice x8, local copies, waits for them, and re-layouts: 7.58 us -> 15.9 us  [local(): lax.dynamic_update_slice_in_dim(gathered, piece, owner * share_width, 2)]
    ppermute x12, waiting for transfers between devices: 78.7 us -> 83.3 us  [ring_gather(): forward = lax.ppermute(forward, axis_name, ahead)]
    unnamed x59 -> x65, local copies, waits for them, and re-layouts: 11 us -> 11.3 us
  transfers between devices with their start and end apart: 45 -> 45, of which waited for: 24 -> 27; matrix products, arithmetic and copies ran while one was open for 14% -> 18% of each run, Pallas kernels for 7% -> 7%
where the time goes in v12:
time: 348 us; the launch traced here: 346 us
  waiting for transfers between devices  160 us (46%)
  starting transfers between devices  40.4 us (12%)
  local copies, waits for them, and re-layouts  38.2 us (11%)
  between operations  32.5 us (9%)
  other arithmetic  25 us (7%)
  Pallas kernels  23.1 us (7%)
  matrix products  22.4 us (6%)
  blocking collectives  4.53 us (1%)
    ppermute x12, waiting for transfers between devices, ring_gather(): forward = lax.ppermute(forward, axis_name, ahead)  83.3 us
    ppermute x7, waiting for transfers between devices, ring_reduce_scatter(): lax.ppermute(forward.astype(jnp.bfloat16), axis_name, ahead)  46.7 us
    pallas_call x1, Pallas kernels, grouped_out_proj(): pl.pallas_call(functools.partial(out_proj_kernel, group_count, tiles_per_...  23.1 us
    ppermute x9, waiting for transfers between devices, ring_gather(): backward = lax.ppermute(backward, axis_name, behind)  20.9 us
    ppermute x12, starting transfers between devices, ring_gather(): forward = lax.ppermute(forward, axis_name, ahead)  20.2 us
    dynamic_update_slice x8, local copies, waits for them, and re-layouts, local(): lax.dynamic_update_slice_in_dim(gathered, piece, owner * share_width, 2)  15.9 us
    unnamed x65, local copies, waits for them, and re-layouts  11.3 us
    dot_general x1, matrix products, local(): pre_act = jnp.dot(mlp_in, up_full, preferred_element_type=jnp.float32)  10 us
  transfers between devices with their start and end apart: 45, of which 27 were waited for; matrix products, arithmetic and copies ran while one was open for 18% of the time, Pallas kernels for 7%

profile of v12, /device:TPU:0, one launch (start us, length us, event | category | flops | bytes accessed | tf_op | source)
XLA Modules:
  0.0 346.1 jit_solution(11230485237411114177)
XLA Ops:
  7.3 3.1 collective-permute-start
  12.4 15.7 %collective-permute-done = bf16[4,128,768]{2,1,0:T(8,128)(2,1)S(1)} collective-permute-done((bf16[4,128,768]{2,1,0:T(8,128)(2,1)}, bf16[4,128,768]{2,1,0:T(8,128)(2,1)S(1)}, u32[]{:S(2)}, u32[]{:S(2)}) %collective-permute-start) | collective-permute-done | bytes 786464 | tf_op jit(solution)/shard_map/ppermute | solution.py:34
  28.1 1.8 collective-permute-start.1
  31.3 15.8 %collective-permute-done.1 = bf16[4,128,768]{2,1,0:T(8,128)(2,1)} collective-permute-done((bf16[4,128,768]{2,1,0:T(8,128)(2,1)S(1)}, bf16[4,128,768]{2,1,0:T(8,128)(2,1)}, u32[]{:S(2)}, u32[]{:S(2)}) %collective-permute-start.1) | collective-permute-done | bytes 786464 | tf_op jit(solution)/shard_map/ppermute | solution.py:34
  49.3 2.2 all_gather.12
  62.5 2.8 collective-permute-done.2
  66.4 3.4 broadcast_in_dim.71
  69.9 2.1 constant_dynamic-update-slice_fusion.7
  76.3 6.6 %copy.32 = bf16[6144,3,128]{0,2,1:T(8,128)(2,1)} copy(bf16[6144,3,128]{2,0,1:T(8,128)(2,1)} %param.22) | data formatting | bytes 9437184 | tf_op args[7]
  84.8 2.1 constant_dynamic-update-slice_fusion.6
  86.9 2.1 constant_dynamic-update-slice_fusion.5
  89.0 2.1 constant_dynamic-update-slice_fusion.4
  91.1 2.1 constant_dynamic-update-slice_fusion.3
  93.3 2.2 constant_dynamic-update-slice_fusion.2
  95.5 2.1 constant_dynamic-update-slice_fusion.1
  97.6 3.4 collective-permute-done.6
  102.0 4.2 %fusion = f32[4,128]{1,0:T(4,128)S(1)} fusion(bf16[4,128,6144]{2,1,0:T(8,128)(2,1)} %constant_dynamic-update-slice_fusion), kind=kLoop, calls=%fused_computation.2 | loop fusion | flops 9436672 | bytes 6293504 | tf_op jit(solution)/shard_map/reduce_sum | solution.py:20
  106.3 5.5 %fusion.3 = bf16[4,128,6144]{2,1,0:T(8,128)(2,1)S(1)} fusion(bf16[4,128,6144]{2,1,0:T(8,128)(2,1)} %constant_dynamic-update-slice_fusion, f32[4,6144]{1,0:T(4,128)S(1)} %copy-done.5, f32[4,6144]{1,0:T(4,128)S(1)} %copy-done.6, f32[4,128]{1,0:T(4,128)S(1)} %add_rsqrt_fusion), kind=kLoop, calls=%fused_computation.5 | loop fusion | flops 15728640 | bytes 12781568 | tf_op jit(solution)/shard_map/convert_element_type | solution.py:235
  111.8 3.4 convolution_convert_fusion.1
  115.7 1.7 collective-permute-start.14
  118.0 2.4 all_gather.13
  122.5 10.7 %collective-permute-done.14.refs_9_ = bf16[128,3072]{1,0:T(8,128)(2,1)} collective-permute-done((bf16[128,3072]{1,0:T(8,128)(2,1)S(1)}, bf16[128,3072]{1,0:T(8,128)(2,1)}, u32[]{:S(2)}, u32[]{:S(2)}) %collective-permute-start.14) | collective-permute-done | bytes 786464 | tf_op jit(solution)/shard_map/ppermute | solution.py:34
  133.2 1.6 collective-permute-start.15
  136.7 14.3 %collective-permute-done.15.refs_10_ = bf16[128,3072]{1,0:T(8,128)(2,1)} collective-permute-done((bf16[128,3072]{1,0:T(8,128)(2,1)}, bf16[128,3072]{1,0:T(8,128)(2,1)}, u32[]{:S(2)}, u32[]{:S(2)}) %collective-permute-start.15) | collective-permute-done | bytes 786464 | tf_op jit(solution)/shard_map/ppermute | solution.py:34
  150.9 1.6 collective-permute-start.16
  153.0 1.6 collective-permute-start.7
  155.1 14.5 %collective-permute-done.7.refs_1_ = bf16[512,128]{1,0:T(8,128)(2,1)S(1)} collective-permute-done((bf16[512,128]{1,0:T(8,128)(2,1)S(1)}, bf16[512,128]{1,0:T(8,128)(2,1)S(1)}, u32[]{:S(2)}, u32[]{:S(2)}) %collective-permute-start.7) | collective-permute-done | bytes 131104 | tf_op jit(solution)/shard_map/ppermute | solution.py:34
  171.6 3.2 collective-permute-done.8.refs_2_
  174.9 1.6 collective-permute-start.9
  176.9 2.9 collective-permute-done.9.refs_3_
  182.0 2.8 collective-permute-done.10.refs_4_
  187.7 17.4 %collective-permute-done.20.refs_15_ = bf16[128,3072]{1,0:T(8,128)(2,1)} collective-permute-done((bf16[128,3072]{1,0:T(8,128)(2,1)}, bf16[128,3072]{1,0:T(8,128)(2,1)}, u32[]{:S(2)}, u32[]{:S(2)}) %collective-permute-start.20) | collective-permute-done | bytes 786464 | tf_op jit(solution)/shard_map/ppermute | solution.py:38
  208.9 23.1 %shard_map.145 = (f32[512,6144]{1,0:T(8,128)}, f32[512,1536]{1,0:T(8,128)}) custom-call(s32[1]{0:T(128)} %bitcast.span_ref, bf16[512,128]{1,0:T(8,128)(2,1)} %bitcast.168, bf16[512,128]{1,0:T(8,128)(2,1)} %copy-done.18, bf16[512,128]{1,0:T(8,128)(2,1)} %copy-done.20, bf16[512,128]{1,0:T(8,128)(2,1)} %copy-done.22, bf16[512,128]{1,0:T(8,128)(2,1)} %copy-done.24, ...), custom_call_target="tpu_custom_call" | custom-call | flops 6442450944 | bytes 32505856 | tf_op jit(solution)/shard_map/pallas_call | solution.py:128
  232.0 3.6 %copy.39 = f32[512,1536]{0,1:T(8,128)} copy(f32[512,1536]{1,0:T(8,128)} %get-tuple-element.12) | data formatting | bytes 6291456 | tf_op jit(solution)/shard_map/pallas_call | solution.py:128
  236.6 10.0 %fusion.27 = bf16[4,128,512]{2,1,0:T(8,128)(2,1)S(1)} fusion(bf16[6144,512]{1,0:T(8,128)(2,1)} %all-gather.3.cloned.1.call-done, f32[4,128,6144]{2,1,0:T(8,128)} %bitcast.162, f32[4,6144]{1,0:T(4,128)S(1)} %copy-done.11, f32[4,6144]{1,0:T(4,128)S(1)} %copy-done.10, f32[4,128]{1,0:T(4,128)S(1)} %rsqrt_bitcast_fusion), kind=kOutput, calls=%fused_computation.38 | convolution fusion | flops 3236167680 | bytes 19597312 | tf_op jit(solution)/shard_map/dot_general | solution.py:292
  246.6 6.4 %convolution_convert_fusion = bf16[4,128,6144]{2,1,0:T(8,128)(2,1)S(1)} fusion(bf16[4,128,512]{2,1,0:T(8,128)(2,1)S(1)} %fusion.27, bf16[512,6144]{1,0:T(8,128)(2,1)} %all-gather.5.cloned.1.call-done), kind=kOutput, calls=%fused_computation.7 | convolution fusion | flops 3224371200 | bytes 13107200 | tf_op jit(solution)/shard_map/dot_general | solution.py:294
  253.1 2.6 copy-done.2
  255.7 1.7 collective-permute-start.29
  259.1 7.9 %collective-permute-done.29 = bf16[512,384]{1,0:T(8,128)(2,1)S(1)} collective-permute-done((bf16[512,384]{1,0:T(8,128)(2,1)S(1)}, bf16[512,384]{1,0:T(8,128)(2,1)S(1)}, u32[]{:S(2)}, u32[]{:S(2)}) %collective-permute-start.29) | collective-permute-done | bytes 393248 | tf_op jit(solution)/shard_map/ppermute | solution.py:61
  269.6 1.6 collective-permute-start.30
  273.0 6.7 %collective-permute-done.30 = bf16[512,384]{1,0:T(8,128)(2,1)S(1)} collective-permute-done((bf16[512,384]{1,0:T(8,128)(2,1)S(1)}, bf16[512,384]{1,0:T(8,128)(2,1)S(1)}, u32[]{:S(2)}, u32[]{:S(2)}) %collective-permute-start.30) | collective-permute-done | bytes 393248 | tf_op jit(solution)/shard_map/ppermute | solution.py:61
  285.1 6.2 %collective-permute-done.31 = bf16[512,384]{1,0:T(8,128)(2,1)S(1)} collective-permute-done((bf16[512,384]{1,0:T(8,128)(2,1)S(1)}, bf16[512,384]{1,0:T(8,128)(2,1)S(1)}, u32[]{:S(2)}, u32[]{:S(2)}) %collective-permute-start.31) | collective-permute-done | bytes 393248 | tf_op jit(solution)/shard_map/ppermute | solution.py:61
  295.9 5.8 %collective-permute-done.32 = bf16[512,384]{1,0:T(8,128)(2,1)S(1)} collective-permute-done((bf16[512,384]{1,0:T(8,128)(2,1)S(1)}, bf16[512,384]{1,0:T(8,128)(2,1)S(1)}, u32[]{:S(2)}, u32[]{:S(2)}) %collective-permute-start.32) | collective-permute-done | bytes 393248 | tf_op jit(solution)/shard_map/ppermute | solution.py:61
  305.7 6.6 %collective-permute-done.33 = bf16[512,384]{1,0:T(8,128)(2,1)S(1)} collective-permute-done((bf16[512,384]{1,0:T(8,128)(2,1)S(1)}, bf16[512,384]{1,0:T(8,128)(2,1)S(1)}, u32[]{:S(2)}, u32[]{:S(2)}) %collective-permute-start.33) | collective-permute-done | bytes 393248 | tf_op jit(solution)/shard_map/ppermute | solution.py:61
  316.9 7.7 %collective-permute-done.34 = bf16[512,384]{1,0:T(8,128)(2,1)S(1)} collective-permute-done((bf16[512,384]{1,0:T(8,128)(2,1)S(1)}, bf16[512,384]{1,0:T(8,128)(2,1)S(1)}, u32[]{:S(2)}, u32[]{:S(2)}) %collective-permute-start.34) | collective-permute-done | bytes 393248 | tf_op jit(solution)/shard_map/ppermute | solution.py:61
  327.2 1.8 collective-permute-start.42
  329.0 5.7 %collective-permute-done.35 = bf16[512,384]{1,0:T(8,128)(2,1)S(1)} collective-permute-done((bf16[512,384]{1,0:T(8,128)(2,1)S(1)}, bf16[512,384]{1,0:T(8,128)(2,1)S(1)}, u32[]{:S(2)}, u32[]{:S(2)}) %collective-permute-start.35) | collective-permute-done | bytes 393248 | tf_op jit(solution)/shard_map/ppermute | solution.py:61
  336.7 2.6 add_convert_fusion.2
  (168 shorter events, 54.3 us)
Async XLA Ops:
  6.5 76.5 %copy-start = (bf16[128,6144]{1,0:T(8,128)(2,1)S(1)}, bf16[128,6144]{1,0:T(8,128)(2,1)}, u32[]{:S(2)}) copy-start(bf16[128,6144]{1,0:T(8,128)(2,1)} %param.23) | copy-start | bytes 4718596
  6.5 54.5 %copy-start.9 = (s32[8]{0:T(128)S(1)}, s32[8]{0:T(128)}, u32[]{:S(2)}) copy-start(s32[8]{0:T(128)} %constant.289.clone) | copy-start | bytes 100
  6.6 230.0 %all-gather.3.cloned.1.call-start = ((), (), s32[]{:S(2)}) async-start(), calls=%async_computation | async-start | bytes 9437184 | tf_op jit(solution)/shard_map/all_gather | solution.py:225
  7.3 239.3 %all-gather.5.cloned.1.call-start = ((), (), s32[]{:S(2)}) async-start(), calls=%async_computation.1 | async-start | bytes 9437184 | tf_op jit(solution)/shard_map/all_gather | solution.py:226
  7.3 20.8 %collective-permute-start = (bf16[4,128,768]{2,1,0:T(8,128)(2,1)}, bf16[4,128,768]{2,1,0:T(8,128)(2,1)S(1)}, u32[]{:S(2)}, u32[]{:S(2)}) collective-permute-start(bf16[4,128,768]{2,1,0:T(8,128)(2,1)} %param.15), channel_id=1, source_target_pairs={{0,2},{2,4},{4,6},{6,7},{7,5},{5,3},{3,1},{1,0},{8,10},{10,12},{12... | collective-permute-start | bytes 2359304 | tf_op jit(solution)/shard_map/ppermute | solution.py:34
  10.4 38.3 %collective-permute-start.4 = (bf16[4,128,768]{2,1,0:T(8,128)(2,1)}, bf16[4,128,768]{2,1,0:T(8,128)(2,1)}, u32[]{:S(2)}, u32[]{:S(2)}) collective-permute-start(bf16[4,128,768]{2,1,0:T(8,128)(2,1)} %param.15), channel_id=1, source_target_pairs={{0,1},{2,0},{4,2},{6,4},{7,6},{5,7},{3,5},{1,3},{8,9},{10,8},{12,1... | collective-permute-start | bytes 2359304 | tf_op jit(solution)/shard_map/ppermute | solution.py:38
  28.1 18.9 %collective-permute-start.1 = (bf16[4,128,768]{2,1,0:T(8,128)(2,1)S(1)}, bf16[4,128,768]{2,1,0:T(8,128)(2,1)}, u32[]{:S(2)}, u32[]{:S(2)}) collective-permute-start(bf16[4,128,768]{2,1,0:T(8,128)(2,1)S(1)} %collective-permute-done), channel_id=1, source_target_pairs={{0,2},{2,4},{4,6},{6,7},{7,5},{5,3},{3,1},{1,0},{8,10},{10,12},{12... | collective-permute-start | bytes 2359304 | tf_op jit(solution)/shard_map/ppermute | solution.py:34
  47.1 18.2 %collective-permute-start.2 = (bf16[4,128,768]{2,1,0:T(8,128)(2,1)}, bf16[4,128,768]{2,1,0:T(8,128)(2,1)}, u32[]{:S(2)}, u32[]{:S(2)}) collective-permute-start(bf16[4,128,768]{2,1,0:T(8,128)(2,1)} %collective-permute-done.1), channel_id=1, source_target_pairs={{0,2},{2,4},{4,6},{6,7},{7,5},{5,3},{3,1},{1,0},{8,10},{10,12},{12... | collective-permute-start | bytes 2359304 | tf_op jit(solution)/shard_map/ppermute | solution.py:34
  48.7 35.3 %collective-permute-start.5 = (bf16[4,128,768]{2,1,0:T(8,128)(2,1)}, bf16[4,128,768]{2,1,0:T(8,128)(2,1)}, u32[]{:S(2)}, u32[]{:S(2)}) collective-permute-start(bf16[4,128,768]{2,1,0:T(8,128)(2,1)} %collective-permute-done.4), channel_id=1, source_target_pairs={{0,1},{2,0},{4,2},{6,4},{7,6},{5,7},{3,5},{1,3},{8,9},{10,8},{12,1... | collective-permute-start | bytes 2359304 | tf_op jit(solution)/shard_map/ppermute | solution.py:38
  65.3 25.9 %collective-permute-start.3 = (bf16[4,128,768]{2,1,0:T(8,128)(2,1)}, bf16[4,128,768]{2,1,0:T(8,128)(2,1)}, u32[]{:S(2)}, u32[]{:S(2)}) collective-permute-start(bf16[4,128,768]{2,1,0:T(8,128)(2,1)} %collective-permute-done.2), channel_id=1, source_target_pairs={{0,2},{2,4},{4,6},{6,7},{7,5},{5,3},{3,1},{1,0},{8,10},{10,12},{12... | collective-permute-start | bytes 2359304 | tf_op jit(solution)/shard_map/ppermute | solution.py:34
  84.0 17.1 %collective-permute-start.6 = (bf16[4,128,768]{2,1,0:T(8,128)(2,1)}, bf16[4,128,768]{2,1,0:T(8,128)(2,1)S(1)}, u32[]{:S(2)}, u32[]{:S(2)}) collective-permute-start(bf16[4,128,768]{2,1,0:T(8,128)(2,1)} %collective-permute-done.5), channel_id=1, source_target_pairs={{0,1},{2,0},{4,2},{6,4},{7,6},{5,7},{3,5},{1,3},{8,9},{10,8},{12,1... | collective-permute-start | bytes 2359304 | tf_op jit(solution)/shard_map/ppermute | solution.py:38
  115.7 17.5 %collective-permute-start.14 = (bf16[128,3072]{1,0:T(8,128)(2,1)S(1)}, bf16[128,3072]{1,0:T(8,128)(2,1)}, u32[]{:S(2)}, u32[]{:S(2)}) collective-permute-start(bf16[128,3072]{1,0:T(8,128)(2,1)S(1)} %copy-done.4), channel_id=1, source_target_pairs={{0,2},{2,4},{4,6},{6,7},{7,5},{5,3},{3,1},{1,0},{8,10},{10,12},{12... | collective-permute-start | bytes 2359304 | tf_op jit(solution)/shard_map/ppermute | solution.py:34
  117.4 18.8 %collective-permute-start.18 = (bf16[128,3072]{1,0:T(8,128)(2,1)S(1)}, bf16[128,3072]{1,0:T(8,128)(2,1)}, u32[]{:S(2)}, u32[]{:S(2)}) collective-permute-start(bf16[128,3072]{1,0:T(8,128)(2,1)S(1)} %copy-done.4), channel_id=1, source_target_pairs={{0,1},{2,0},{4,2},{6,4},{7,6},{5,7},{3,5},{1,3},{8,9},{10,8},{12,1... | collective-permute-start | bytes 2359304 | tf_op jit(solution)/shard_map/ppermute | solution.py:38
  133.2 17.7 %collective-permute-start.15 = (bf16[128,3072]{1,0:T(8,128)(2,1)}, bf16[128,3072]{1,0:T(8,128)(2,1)}, u32[]{:S(2)}, u32[]{:S(2)}) collective-permute-start(bf16[128,3072]{1,0:T(8,128)(2,1)} %collective-permute-done.14.refs_9_), channel_id=1, source_target_pairs={{0,2},{2,4},{4,6},{6,7},{7,5},{5,3},{3,1},{1,0},{8,10},{10,12},{12... | collective-permute-start | bytes 2359304 | tf_op jit(solution)/shard_map/ppermute | solution.py:34
  136.2 48.6 %collective-permute-start.19 = (bf16[128,3072]{1,0:T(8,128)(2,1)}, bf16[128,3072]{1,0:T(8,128)(2,1)}, u32[]{:S(2)}, u32[]{:S(2)}) collective-permute-start(bf16[128,3072]{1,0:T(8,128)(2,1)} %collective-permute-done.18.refs_13_), channel_id=1, source_target_pairs={{0,1},{2,0},{4,2},{6,4},{7,6},{5,7},{3,5},{1,3},{8,9},{10,8},{12,1... | collective-permute-start | bytes 2359304 | tf_op jit(solution)/shard_map/ppermute | solution.py:38
  150.9 34.7 %collective-permute-start.16 = (bf16[128,3072]{1,0:T(8,128)(2,1)}, bf16[128,3072]{1,0:T(8,128)(2,1)}, u32[]{:S(2)}, u32[]{:S(2)}) collective-permute-start(bf16[128,3072]{1,0:T(8,128)(2,1)} %collective-permute-done.15.refs_10_), channel_id=1, source_target_pairs={{0,2},{2,4},{4,6},{6,7},{7,5},{5,3},{3,1},{1,0},{8,10},{10,12},{12... | collective-permute-start | bytes 2359304 | tf_op jit(solution)/shard_map/ppermute | solution.py:34
  153.0 55.8 %copy-start.17 = (bf16[128,4,128]{0,2,1:T(8,128)(2,1)}, bf16[128,4,128]{0,2,1:T(8,128)(2,1)S(1)}, u32[]{:S(2)}) copy-start(bf16[128,4,128]{0,2,1:T(8,128)(2,1)S(1)} %fusion.17) | copy-start | bytes 393220
  153.0 16.6 %collective-permute-start.7 = (bf16[512,128]{1,0:T(8,128)(2,1)S(1)}, bf16[512,128]{1,0:T(8,128)(2,1)S(1)}, u32[]{:S(2)}, u32[]{:S(2)}) collective-permute-start(bf16[512,128]{1,0:T(8,128)(2,1)S(1)} %bitcast.166), channel_id=1, source_target_pairs={{0,2},{2,4},{4,6},{6,7},{7,5},{5,3},{3,1},{1,0},{8,10},{10,12},{12... | collective-permute-start | bytes 393224 | tf_op jit(solution)/shard_map/ppermute | solution.py:34
  154.7 16.6 %collective-permute-start.11 = (bf16[512,128]{1,0:T(8,128)(2,1)S(1)}, bf16[512,128]{1,0:T(8,128)(2,1)S(1)}, u32[]{:S(2)}, u32[]{:S(2)}) collective-permute-start(bf16[512,128]{1,0:T(8,128)(2,1)S(1)} %bitcast.167), channel_id=1, source_target_pairs={{0,1},{2,0},{4,2},{6,4},{7,6},{5,7},{3,5},{1,3},{8,9},{10,8},{12,1... | collective-permute-start | bytes 393224 | tf_op jit(solution)/shard_map/ppermute | solution.py:38
  169.6 5.3 %collective-permute-start.8 = (bf16[512,128]{1,0:T(8,128)(2,1)S(1)}, bf16[512,128]{1,0:T(8,128)(2,1)S(1)}, u32[]{:S(2)}, u32[]{:S(2)}) collective-permute-start(bf16[512,128]{1,0:T(8,128)(2,1)S(1)} %collective-permute-done.7.refs_1_), channel_id=1, source_target_pairs={{0,2},{2,4},{4,6},{6,7},{7,5},{5,3},{3,1},{1,0},{8,10},{10,12},{12... | collective-permute-start | bytes 393224 | tf_op jit(solution)/shard_map/ppermute | solution.py:34
  171.2 5.3 %collective-permute-start.12 = (bf16[512,128]{1,0:T(8,128)(2,1)S(1)}, bf16[512,128]{1,0:T(8,128)(2,1)S(1)}, u32[]{:S(2)}, u32[]{:S(2)}) collective-permute-start(bf16[512,128]{1,0:T(8,128)(2,1)S(1)} %collective-permute-done.11.refs_5_), channel_id=1, source_target_pairs={{0,1},{2,0},{4,2},{6,4},{7,6},{5,7},{3,5},{1,3},{8,9},{10,8},{12,1... | collective-permute-start | bytes 393224 | tf_op jit(solution)/shard_map/ppermute | solution.py:38
  174.9 5.0 %collective-permute-start.9 = (bf16[512,128]{1,0:T(8,128)(2,1)S(1)}, bf16[512,128]{1,0:T(8,128)(2,1)S(1)}, u32[]{:S(2)}, u32[]{:S(2)}) collective-permute-start(bf16[512,128]{1,0:T(8,128)(2,1)S(1)} %collective-permute-done.8.refs_2_), channel_id=1, source_target_pairs={{0,2},{2,4},{4,6},{6,7},{7,5},{5,3},{3,1},{1,0},{8,10},{10,12},{12... | collective-permute-start | bytes 393224 | tf_op jit(solution)/shard_map/ppermute | solution.py:34
  176.5 5.0 %collective-permute-start.13 = (bf16[512,128]{1,0:T(8,128)(2,1)S(1)}, bf16[512,128]{1,0:T(8,128)(2,1)S(1)}, u32[]{:S(2)}, u32[]{:S(2)}) collective-permute-start(bf16[512,128]{1,0:T(8,128)(2,1)S(1)} %collective-permute-done.12.refs_6_), channel_id=1, source_target_pairs={{0,1},{2,0},{4,2},{6,4},{7,6},{5,7},{3,5},{1,3},{8,9},{10,8},{12,1... | collective-permute-start | bytes 393224 | tf_op jit(solution)/shard_map/ppermute | solution.py:38
  179.8 5.0 %collective-permute-start.10 = (bf16[512,128]{1,0:T(8,128)(2,1)S(1)}, bf16[512,128]{1,0:T(8,128)(2,1)S(1)}, u32[]{:S(2)}, u32[]{:S(2)}) collective-permute-start(bf16[512,128]{1,0:T(8,128)(2,1)S(1)} %collective-permute-done.9.refs_3_), channel_id=1, source_target_pairs={{0,2},{2,4},{4,6},{6,7},{7,5},{5,3},{3,1},{1,0},{8,10},{10,12},{12... | collective-permute-start | bytes 393224 | tf_op jit(solution)/shard_map/ppermute | solution.py:34
  181.5 5.5 %collective-permute-start.21 = (bf16[128,3072]{1,0:T(8,128)(2,1)S(1)}, bf16[128,3072]{1,0:T(8,128)(2,1)S(1)}, u32[]{:S(2)}, u32[]{:S(2)}) collective-permute-start(bf16[128,3072]{1,0:T(8,128)(2,1)S(1)} %copy-done.4), channel_id=1, source_target_pairs={{0,8},{8,0},{1,9},{9,1},{2,10},{10,2},{3,11},{11,3},{4,12},{12,4},... | collective-permute-start | bytes 2359304 | tf_op jit(solution)/shard_map/ppermute | solution.py:221
  181.5 5.6 %collective-permute-start.22 = (bf16[128,3072]{1,0:T(8,128)(2,1)}, bf16[128,3072]{1,0:T(8,128)(2,1)}, u32[]{:S(2)}, u32[]{:S(2)}) collective-permute-start(bf16[128,3072]{1,0:T(8,128)(2,1)} %collective-permute-done.14.refs_9_), channel_id=1, source_target_pairs={{0,8},{8,0},{1,9},{9,1},{2,10},{10,2},{3,11},{11,3},{4,12},{12,4},... | collective-permute-start | bytes 2359304 | tf_op jit(solution)/shard_map/ppermute | solution.py:221
  184.8 2.8 collective-permute-start.26
  184.8 20.3 %collective-permute-start.20 = (bf16[128,3072]{1,0:T(8,128)(2,1)}, bf16[128,3072]{1,0:T(8,128)(2,1)}, u32[]{:S(2)}, u32[]{:S(2)}) collective-permute-start(bf16[128,3072]{1,0:T(8,128)(2,1)} %collective-permute-done.19.refs_14_), channel_id=1, source_target_pairs={{0,1},{2,0},{4,2},{6,4},{7,6},{5,7},{3,5},{1,3},{8,9},{10,8},{12,1... | collective-permute-start | bytes 2359304 | tf_op jit(solution)/shard_map/ppermute | solution.py:38
  185.6 19.9 %collective-permute-start.17 = (bf16[128,3072]{1,0:T(8,128)(2,1)}, bf16[128,3072]{1,0:T(8,128)(2,1)}, u32[]{:S(2)}, u32[]{:S(2)}) collective-permute-start(bf16[128,3072]{1,0:T(8,128)(2,1)} %collective-permute-done.16.refs_11_), channel_id=1, source_target_pairs={{0,2},{2,4},{4,6},{6,7},{7,5},{5,3},{3,1},{1,0},{8,10},{10,12},{12... | collective-permute-start | bytes 2359304 | tf_op jit(solution)/shard_map/ppermute | solution.py:34
  186.9 19.4 %collective-permute-start.23 = (bf16[128,3072]{1,0:T(8,128)(2,1)}, bf16[128,3072]{1,0:T(8,128)(2,1)S(1)}, u32[]{:S(2)}, u32[]{:S(2)}) collective-permute-start(bf16[128,3072]{1,0:T(8,128)(2,1)} %collective-permute-done.15.refs_10_), channel_id=1, source_target_pairs={{0,8},{8,0},{1,9},{9,1},{2,10},{10,2},{3,11},{11,3},{4,12},{12,4},... | collective-permute-start | bytes 2359304 | tf_op jit(solution)/shard_map/ppermute | solution.py:221
  187.0 19.3 %collective-permute-start.27 = (bf16[128,3072]{1,0:T(8,128)(2,1)}, bf16[128,3072]{1,0:T(8,128)(2,1)S(1)}, u32[]{:S(2)}, u32[]{:S(2)}) collective-permute-start(bf16[128,3072]{1,0:T(8,128)(2,1)} %collective-permute-done.19.refs_14_), channel_id=1, source_target_pairs={{0,8},{8,0},{1,9},{9,1},{2,10},{10,2},{3,11},{11,3},{4,12},{12,4},... | collective-permute-start | bytes 2359304 | tf_op jit(solution)/shard_map/ppermute | solution.py:221
  187.6 18.8 %collective-permute-start.24 = (bf16[128,3072]{1,0:T(8,128)(2,1)}, bf16[128,3072]{1,0:T(8,128)(2,1)}, u32[]{:S(2)}, u32[]{:S(2)}) collective-permute-start(bf16[128,3072]{1,0:T(8,128)(2,1)} %collective-permute-done.16.refs_11_), channel_id=1, source_target_pairs={{0,8},{8,0},{1,9},{9,1},{2,10},{10,2},{3,11},{11,3},{4,12},{12,4},... | collective-permute-start | bytes 2359304 | tf_op jit(solution)/shard_map/ppermute | solution.py:221
  205.1 2.6 collective-permute-start.28
  205.5 3.3 collective-permute-start.25
  255.7 11.3 %collective-permute-start.29 = (bf16[512,384]{1,0:T(8,128)(2,1)S(1)}, bf16[512,384]{1,0:T(8,128)(2,1)S(1)}, u32[]{:S(2)}, u32[]{:S(2)}) collective-permute-start(bf16[512,384]{1,0:T(8,128)(2,1)S(1)} %get-tuple-element.27), channel_id=1, source_target_pairs={{0,2},{2,4},{4,6},{6,7},{7,5},{5,3},{3,1},{1,0},{8,10},{10,12},{12... | collective-permute-start | bytes 1179656 | tf_op jit(solution)/shard_map/ppermute | solution.py:61
  257.4 10.9 %collective-permute-start.36 = (bf16[512,384]{1,0:T(8,128)(2,1)S(1)}, bf16[512,384]{1,0:T(8,128)(2,1)S(1)}, u32[]{:S(2)}, u32[]{:S(2)}) collective-permute-start(bf16[512,384]{1,0:T(8,128)(2,1)S(1)} %get-tuple-element.28), channel_id=1, source_target_pairs={{0,1},{2,0},{4,2},{6,4},{7,6},{5,7},{3,5},{1,3},{8,9},{10,8},{12,1... | collective-permute-start | bytes 1179656 | tf_op jit(solution)/shard_map/ppermute | solution.py:63
  269.6 10.1 %collective-permute-start.30 = (bf16[512,384]{1,0:T(8,128)(2,1)S(1)}, bf16[512,384]{1,0:T(8,128)(2,1)S(1)}, u32[]{:S(2)}, u32[]{:S(2)}) collective-permute-start(bf16[512,384]{1,0:T(8,128)(2,1)S(1)} %get-tuple-element.25), channel_id=1, source_target_pairs={{0,2},{2,4},{4,6},{6,7},{7,5},{5,3},{3,1},{1,0},{8,10},{10,12},{12... | collective-permute-start | bytes 1179656 | tf_op jit(solution)/shard_map/ppermute | solution.py:61
  271.3 9.8 %collective-permute-start.37 = (bf16[512,384]{1,0:T(8,128)(2,1)S(1)}, bf16[512,384]{1,0:T(8,128)(2,1)S(1)}, u32[]{:S(2)}, u32[]{:S(2)}) collective-permute-start(bf16[512,384]{1,0:T(8,128)(2,1)S(1)} %get-tuple-element.26), channel_id=1, source_target_pairs={{0,1},{2,0},{4,2},{6,4},{7,6},{5,7},{3,5},{1,3},{8,9},{10,8},{12,1... | collective-permute-start | bytes 1179656 | tf_op jit(solution)/shard_map/ppermute | solution.py:63
  282.4 8.9 %collective-permute-start.31 = (bf16[512,384]{1,0:T(8,128)(2,1)S(1)}, bf16[512,384]{1,0:T(8,128)(2,1)S(1)}, u32[]{:S(2)}, u32[]{:S(2)}) collective-permute-start(bf16[512,384]{1,0:T(8,128)(2,1)S(1)} %get-tuple-element.23), channel_id=1, source_target_pairs={{0,2},{2,4},{4,6},{6,7},{7,5},{5,3},{3,1},{1,0},{8,10},{10,12},{12... | collective-permute-start | bytes 1179656 | tf_op jit(solution)/shard_map/ppermute | solution.py:61
  284.0 8.6 %collective-permute-start.38 = (bf16[512,384]{1,0:T(8,128)(2,1)S(1)}, bf16[512,384]{1,0:T(8,128)(2,1)S(1)}, u32[]{:S(2)}, u32[]{:S(2)}) collective-permute-start(bf16[512,384]{1,0:T(8,128)(2,1)S(1)} %get-tuple-element.24), channel_id=1, source_target_pairs={{0,1},{2,0},{4,2},{6,4},{7,6},{5,7},{3,5},{1,3},{8,9},{10,8},{12,1... | collective-permute-start | bytes 1179656 | tf_op jit(solution)/shard_map/ppermute | solution.py:63
  293.9 7.8 %collective-permute-start.32 = (bf16[512,384]{1,0:T(8,128)(2,1)S(1)}, bf16[512,384]{1,0:T(8,128)(2,1)S(1)}, u32[]{:S(2)}, u32[]{:S(2)}) collective-permute-start(bf16[512,384]{1,0:T(8,128)(2,1)S(1)} %get-tuple-element.21), channel_id=1, source_target_pairs={{0,2},{2,4},{4,6},{6,7},{7,5},{5,3},{3,1},{1,0},{8,10},{10,12},{12... | collective-permute-start | bytes 1179656 | tf_op jit(solution)/shard_map/ppermute | solution.py:61
  294.5 7.8 %collective-permute-start.39 = (bf16[512,384]{1,0:T(8,128)(2,1)S(1)}, bf16[512,384]{1,0:T(8,128)(2,1)S(1)}, u32[]{:S(2)}, u32[]{:S(2)}) collective-permute-start(bf16[512,384]{1,0:T(8,128)(2,1)S(1)} %get-tuple-element.22), channel_id=1, source_target_pairs={{0,1},{2,0},{4,2},{6,4},{7,6},{5,7},{3,5},{1,3},{8,9},{10,8},{12,1... | collective-permute-start | bytes 1179656 | tf_op jit(solution)/shard_map/ppermute | solution.py:63
  303.6 8.7 %collective-permute-start.33 = (bf16[512,384]{1,0:T(8,128)(2,1)S(1)}, bf16[512,384]{1,0:T(8,128)(2,1)S(1)}, u32[]{:S(2)}, u32[]{:S(2)}) collective-permute-start(bf16[512,384]{1,0:T(8,128)(2,1)S(1)} %get-tuple-element.19), channel_id=1, source_target_pairs={{0,2},{2,4},{4,6},{6,7},{7,5},{5,3},{3,1},{1,0},{8,10},{10,12},{12... | collective-permute-start | bytes 1179656 | tf_op jit(solution)/shard_map/ppermute | solution.py:61
  304.4 9.0 %collective-permute-start.40 = (bf16[512,384]{1,0:T(8,128)(2,1)S(1)}, bf16[512,384]{1,0:T(8,128)(2,1)S(1)}, u32[]{:S(2)}, u32[]{:S(2)}) collective-permute-start(bf16[512,384]{1,0:T(8,128)(2,1)S(1)} %get-tuple-element.20), channel_id=1, source_target_pairs={{0,1},{2,0},{4,2},{6,4},{7,6},{5,7},{3,5},{1,3},{8,9},{10,8},{12,1... | collective-permute-start | bytes 1179656 | tf_op jit(solution)/shard_map/ppermute | solution.py:63
  314.8 9.8 %collective-permute-start.34 = (bf16[512,384]{1,0:T(8,128)(2,1)S(1)}, bf16[512,384]{1,0:T(8,128)(2,1)S(1)}, u32[]{:S(2)}, u32[]{:S(2)}) collective-permute-start(bf16[512,384]{1,0:T(8,128)(2,1)S(1)} %get-tuple-element.17), channel_id=1, source_target_pairs={{0,2},{2,4},{4,6},{6,7},{7,5},{5,3},{3,1},{1,0},{8,10},{10,12},{12... | collective-permute-start | bytes 1179656 | tf_op jit(solution)/shard_map/ppermute | solution.py:61
  315.3 10.1 %collective-permute-start.41 = (bf16[512,384]{1,0:T(8,128)(2,1)S(1)}, bf16[512,384]{1,0:T(8,128)(2,1)}, u32[]{:S(2)}, u32[]{:S(2)}) collective-permute-start(bf16[512,384]{1,0:T(8,128)(2,1)S(1)} %get-tuple-element.18), channel_id=1, source_target_pairs={{0,1},{2,0},{4,2},{6,4},{7,6},{5,7},{3,5},{1,3},{8,9},{10,8},{12,1... | collective-permute-start | bytes 1179656 | tf_op jit(solution)/shard_map/ppermute | solution.py:63
  326.9 7.8 %collective-permute-start.35 = (bf16[512,384]{1,0:T(8,128)(2,1)S(1)}, bf16[512,384]{1,0:T(8,128)(2,1)S(1)}, u32[]{:S(2)}, u32[]{:S(2)}) collective-permute-start(bf16[512,384]{1,0:T(8,128)(2,1)S(1)} %get-tuple-element.15), channel_id=1, source_target_pairs={{0,2},{2,4},{4,6},{6,7},{7,5},{5,3},{3,1},{1,0},{8,10},{10,12},{12... | collective-permute-start | bytes 1179656 | tf_op jit(solution)/shard_map/ppermute | solution.py:61
  327.2 7.9 %collective-permute-start.42 = (bf16[512,384]{1,0:T(8,128)(2,1)S(1)}, bf16[512,384]{1,0:T(8,128)(2,1)}, u32[]{:S(2)}, u32[]{:S(2)}) collective-permute-start(bf16[512,384]{1,0:T(8,128)(2,1)S(1)} %get-tuple-element.16), channel_id=1, source_target_pairs={{0,1},{2,0},{4,2},{6,4},{7,6},{5,7},{3,5},{1,3},{8,9},{10,8},{12,1... | collective-permute-start | bytes 1179656 | tf_op jit(solution)/shard_map/ppermute | solution.py:63
  (26 other events, 382.3 us)
Sparse Core Ops, SparseCore 0:
  8.9 18.3 all-gather.2
  28.8 17.9 all-gather.4

commit v13 on v10

--- a/solution.py
+++ b/solution.py
@@ -259,19 +259,37 @@
     )(queries, cache_seen, fresh_seen)
     if gather_weights:
         att_blocks = ring_gather(attended.reshape(token_count, per_device), "tp", tp_count)
-        residual_rows, square_sums = grouped_out_proj(
-            span_index,
-            att_blocks,
-            mine_blocks,
-            other_blocks,
-            gathered_narrow.reshape(token_count, model_width),
-            mod_rows[:, 2],
-        )
-        residual_full = residual_rows.reshape(local_count, row_count, model_width)
-        inverse = lax.rsqrt(square_sums.reshape(local_count, row_count, 1) / model_width + EPSILON)
-        mlp_in = (
-            residual_full * inverse * mod_rows[:, 4][:, None] + mod_rows[:, 3][:, None]
-        ).astype(jnp.bfloat16)
+        halves = 2 if local_count % 2 == 0 else 1
+        per_half = local_count // halves
+        half_tokens = per_half * row_count
+        hidden_rows = gathered_narrow.reshape(token_count, model_width)
+        outputs = []
+        for half in range(halves):
+            rows = slice(half * half_tokens, (half + 1) * half_tokens)
+            mod_half = mod_rows[half * per_half:(half + 1) * per_half]
+            residual_rows, square_sums = grouped_out_proj(
+                span_index,
+                [b[rows] for b in att_blocks],
+                mine_blocks,
+                other_blocks,
+                hidden_rows[rows],
+                mod_half[:, 2],
+            )
+            residual_full = residual_rows.reshape(per_half, row_count, model_width)
+            inverse = lax.rsqrt(square_sums.reshape(per_half, row_count, 1) / model_width + EPSILON)
+            mlp_in = (
+                residual_full * inverse * mod_half[:, 4][:, None] + mod_half[:, 3][:, None]
+            ).astype(jnp.bfloat16)
+            pre_act = jnp.dot(mlp_in, up_full, preferred_element_type=jnp.float32)
+            hidden_units = jax.nn.gelu(pre_act).astype(jnp.bfloat16)
+            down_terms = jnp.dot(hidden_units, down_full, preferred_element_type=jnp.float32)
+            mlp_out = ring_reduce_scatter(
+                down_terms.reshape(half_tokens, model_width), "tp", tp_count
+            ).reshape(per_half, row_count, share_width)
+            residual = lax.dynamic_slice_in_dim(residual_full, tp_rank * share_width, share_width, 2)
+            mod_share = lax.dynamic_slice_in_dim(mod_half, tp_rank * share_width, share_width, 2)
+            outputs.append((residual + mod_share[:, 5][:, None] * mlp_out).astype(jnp.bfloat16))
+        return jnp.concatenate(outputs, axis=0)
     else:
         partial_value = jnp.dot(
             attended.reshape(token_count, -1), w_out, preferred_element_type=jnp.float32
@@ -290,17 +308,9 @@
     pre_act = jnp.dot(mlp_in, up_full, preferred_element_type=jnp.float32)
     hidden_units = jax.nn.gelu(pre_act).astype(jnp.bfloat16)
     down_terms = jnp.dot(hidden_units, down_full, preferred_element_type=jnp.float32)
-    if gather_weights:
-        mlp_out = ring_reduce_scatter(
-            down_terms.reshape(token_count, model_width), "tp", tp_count
-        ).reshape(local_count, row_count, share_width)
-    else:
-        mlp_out = lax.psum_scatter(
-            down_terms.astype(jnp.bfloat16), "tp", scatter_dimension=2, tiled=True
-        ).astype(jnp.float32)
-    if gather_weights:
-        residual = lax.dynamic_slice_in_dim(residual_full, tp_rank * share_width, share_width, 2)
-        mod_share = lax.dynamic_slice_in_dim(mod_rows, tp_rank * share_width, share_width, 2)
+    mlp_out = lax.psum_scatter(
+        down_terms.astype(jnp.bfloat16), "tp", scatter_dimension=2, tiled=True
+    ).astype(jnp.float32)
     result = residual + mod_share[:, 5][:, None] * mlp_out
     return result.astype(jnp.bfloat16)
 

time: 330 us -> 328 us (level)
  waiting for transfers between devices: 158 us -> 118 us
  local copies, waits for them, and re-layouts: 25.9 us -> 43.2 us
  starting transfers between devices: 40 us -> 55.4 us
  Pallas kernels: 23.1 us -> 33.5 us
  other arithmetic: 19.3 us -> 12.5 us
    ppermute x7 -> x14, waiting for transfers between devices: 50.2 us -> 13.6 us  [ring_reduce_scatter(): lax.ppermute(forward.astype(jnp.bfloat16), axis_name, ahead)]
    ppermute x12, waiting for transfers between devices: 78.7 us -> 55.5 us  [ring_gather(): forward = lax.ppermute(forward, axis_name, ahead)]
    slice x0 -> x11, local copies, waits for them, and re-layouts: none -> 11.1 us  [the longest x8 5.35 us: local(): b[rows]]
    pallas_call x1 -> x2, Pallas kernels: 23.1 us -> 33.5 us  [grouped_out_proj(): pl.pallas_call(functools.partial(out_proj_kernel, group_count, tiles_per_...]
    ppermute x7 -> x14, starting transfers between devices: 7.64 us -> 17.7 us  [ring_reduce_scatter(): lax.ppermute(backward.astype(jnp.bfloat16), axis_name, behind)]
    ppermute x9, waiting for transfers between devices: 21.1 us -> 30.5 us  [ring_gather(): backward = lax.ppermute(backward, axis_name, behind)]
    ppermute x7 -> x14, waiting for transfers between devices: 7.07 us -> 16.4 us  [ring_reduce_scatter(): lax.ppermute(backward.astype(jnp.bfloat16), axis_name, behind)]
    convert_element_type x6 -> x12, other arithmetic: 8.11 us -> 1.39 us  [ring_reduce_scatter(): forward.astype(jnp.bfloat16)]
  transfers between devices with their start and end apart: 45 -> 59, of which waited for: 24 -> 35; matrix products, arithmetic and copies ran while one was open for 14% -> 21% of each run, Pallas kernels for 7% -> 10%
where the time goes in v13:
time: 328 us; the launch traced here: 326 us
  waiting for transfers between devices  118 us (36%)
  starting transfers between devices  55.4 us (17%)
  local copies, waits for them, and re-layouts  43.2 us (13%)
  Pallas kernels  33.5 us (10%)
  between operations  32.7 us (10%)
  matrix products  26.4 us (8%)
  other arithmetic  12.5 us (4%)
  blocking collectives  4.36 us (1%)
    ppermute x12, waiting for transfers between devices, ring_gather(): forward = lax.ppermute(forward, axis_name, ahead)  55.5 us
    pallas_call x2, Pallas kernels, grouped_out_proj(): pl.pallas_call(functools.partial(out_proj_kernel, group_count, tiles_per_...  33.5 us
    ppermute x9, waiting for transfers between devices, ring_gather(): backward = lax.ppermute(backward, axis_name, behind)  30.5 us
    ppermute x12, starting transfers between devices, ring_gather(): forward = lax.ppermute(forward, axis_name, ahead)  21 us
    ppermute x14, starting transfers between devices, ring_reduce_scatter(): lax.ppermute(backward.astype(jnp.bfloat16), axis_name, behind)  17.7 us
    ppermute x14, waiting for transfers between devices, ring_reduce_scatter(): lax.ppermute(backward.astype(jnp.bfloat16), axis_name, behind)  16.4 us
    unnamed x83, local copies, waits for them, and re-layouts  13.7 us
    ppermute x14, waiting for transfers between devices, ring_reduce_scatter(): lax.ppermute(forward.astype(jnp.bfloat16), axis_name, ahead)  13.6 us
  transfers between devices with their start and end apart: 59, of which 35 were waited for; matrix products, arithmetic and copies ran while one was open for 21% of the time, Pallas kernels for 10%

profile of v13, /device:TPU:0, one launch (start us, length us, event | category | flops | bytes accessed | tf_op | source)
XLA Modules:
  0.0 326.4 jit_solution(1593369620849244355)
XLA Ops:
  7.3 3.1 collective-permute-start
  10.5 2.1 collective-permute-start.14
  14.6 2.4 fusion.58
  19.0 10.1 %collective-permute-done = bf16[4,128,768]{2,1,0:T(8,128)(2,1)} collective-permute-done((bf16[4,128,768]{2,1,0:T(8,128)(2,1)}, bf16[4,128,768]{2,1,0:T(8,128)(2,1)}, u32[]{:S(2)}, u32[]{:S(2)}) %collective-permute-start) | collective-permute-done | bytes 786464 | tf_op jit(solution)/shard_map/ppermute | solution.py:34
  29.0 2.1 collective-permute-start.1
  31.6 30.3 %collective-permute-done.1 = bf16[4,128,768]{2,1,0:T(8,128)(2,1)} collective-permute-done((bf16[4,128,768]{2,1,0:T(8,128)(2,1)}, bf16[4,128,768]{2,1,0:T(8,128)(2,1)}, u32[]{:S(2)}, u32[]{:S(2)}) %collective-permute-start.1) | collective-permute-done | bytes 786464 | tf_op jit(solution)/shard_map/ppermute | solution.py:34
  61.9 1.8 collective-permute-start.2
  69.4 2.2 all_gather.12
  71.7 1.8 collective-permute-start.15
  73.5 9.2 %collective-permute-done.2 = bf16[4,128,768]{2,1,0:T(8,128)(2,1)} collective-permute-done((bf16[4,128,768]{2,1,0:T(8,128)(2,1)}, bf16[4,128,768]{2,1,0:T(8,128)(2,1)}, u32[]{:S(2)}, u32[]{:S(2)}) %collective-permute-start.2) | collective-permute-done | bytes 786464 | tf_op jit(solution)/shard_map/ppermute | solution.py:34
  82.7 1.8 collective-permute-start.3
  99.2 1.6 copy.56
  100.7 1.6 copy.57
  102.3 6.7 %copy.36 = bf16[6144,3,128]{0,2,1:T(8,128)(2,1)} copy(bf16[6144,3,128]{2,0,1:T(8,128)(2,1)} %param.24) | data formatting | bytes 9437184 | tf_op args[7]
  115.2 1.8 collective-permute-start.19
  121.1 10.7 %collective-permute-done.6 = bf16[4,128,768]{2,1,0:T(8,128)(2,1)S(1)} collective-permute-done((bf16[4,128,768]{2,1,0:T(8,128)(2,1)}, bf16[4,128,768]{2,1,0:T(8,128)(2,1)S(1)}, u32[]{:S(2)}, u32[]{:S(2)}) %collective-permute-start.6) | collective-permute-done | bytes 786464 | tf_op jit(solution)/shard_map/ppermute | solution.py:38
  133.3 2.7 fusion.3
  136.0 5.8 %convolution_convert_fusion.2 = bf16[512,384]{1,0:T(8,128)(2,1)S(1)} fusion(bf16[512,6144]{1,0:T(8,128)(2,1)S(1)} %bitcast.172, bf16[6144,384]{0,1:T(8,128)(2,1)} %bitcast.173), kind=kOutput, calls=%fused_computation.32 | convolution fusion | flops 2416115712 | bytes 11403264 | tf_op jit(solution)/shard_map/dot_general | solution.py:237
  142.5 2.2 all_gather.13
  148.5 1.6 collective-permute-start.7
  150.1 3.1 fusion.57
  153.7 1.6 collective-permute-start.17
  156.4 19.8 %collective-permute-done.11 = bf16[512,128]{1,0:T(8,128)(2,1)S(1)} collective-permute-done((bf16[512,128]{1,0:T(8,128)(2,1)S(1)}, bf16[512,128]{1,0:T(8,128)(2,1)S(1)}, u32[]{:S(2)}, u32[]{:S(2)}) %collective-permute-start.11) | collective-permute-done | bytes 131104 | tf_op jit(solution)/shard_map/ppermute | solution.py:38
  176.2 1.6 collective-permute-start.8
  178.9 2.4 collective-permute-done.8
  181.3 1.6 collective-permute-start.9
  184.0 2.3 collective-permute-done.9
  186.2 1.6 collective-permute-start.10
  197.4 16.7 %shard_map.163 = (f32[256,6144]{1,0:T(8,128)}, f32[256,1536]{1,0:T(8,128)}) custom-call(s32[1]{0:T(128)} %bitcast.span_ref, bf16[256,128]{1,0:T(8,128)(2,1)} %bitcast.204, bf16[256,128]{1,0:T(8,128)(2,1)} %get-tuple-element.77.refs_1_, bf16[256,128]{1,0:T(8,128)(2,1)} %get-tuple-element.75.refs_2_, bf16[256,128]{1,0:T(8,128)(2,1)} %get-tuple-element.73.refs_3_, ...), custom_call_target="tpu_custom_call" | custom-call | flops 3221225472 | bytes 22544384 | tf_op jit(solution)/shard_map/pallas_call | solution.py:128
  214.1 1.9 copy.43
  216.0 16.7 %shard_map.164 = (f32[256,6144]{1,0:T(8,128)}, f32[256,1536]{1,0:T(8,128)}) custom-call(s32[1]{0:T(128)} %bitcast.span_ref, bf16[256,128]{1,0:T(8,128)(2,1)} %bitcast.203, bf16[256,128]{1,0:T(8,128)(2,1)} %get-tuple-element.78.refs_1_, bf16[256,128]{1,0:T(8,128)(2,1)} %get-tuple-element.76.refs_2_, bf16[256,128]{1,0:T(8,128)(2,1)} %get-tuple-element.74.refs_3_, ...), custom_call_target="tpu_custom_call" | custom-call | flops 3221225472 | bytes 22544384 | tf_op jit(solution)/shard_map/pallas_call | solution.py:128
  232.7 1.9 copy.44
  234.7 6.6 %fusion.34 = bf16[2,128,512]{2,1,0:T(8,128)(2,1)S(1)} fusion(bf16[6144,512]{1,0:T(8,128)(2,1)} %all-gather.3.cloned.1.call-done, f32[2,128,6144]{2,1,0:T(8,128)} %bitcast.210, f32[2,6144]{1,0:T(2,128)S(1)} %copy-done.28, f32[2,6144]{1,0:T(2,128)S(1)} %copy-done.27, f32[2,128]{1,0:T(2,128)S(1)} %rsqrt_bitcast_fusion.1), kind=kOutput, calls=%fused_computation.53 | convolution fusion | flops 1618083840 | bytes 12944384 | tf_op jit(solution)/shard_map/dot_general | solution.py:283
  241.4 4.8 %convolution_convert_fusion.1 = bf16[2,128,6144]{2,1,0:T(8,128)(2,1)S(1)} fusion(bf16[2,128,512]{2,1,0:T(8,128)(2,1)S(1)} %fusion.34, bf16[512,6144]{1,0:T(8,128)(2,1)} %all-gather.5.cloned.1.call-done), kind=kOutput, calls=%fused_computation.7 | convolution fusion | flops 1612185600 | bytes 9699328 | tf_op jit(solution)/shard_map/dot_general | solution.py:285
  248.4 5.1 %fusion.46 = bf16[2,128,512]{2,1,0:T(8,128)(2,1)S(1)} fusion(bf16[6144,512]{1,0:T(8,128)(2,1)} %all-gather.3.cloned.1.call-done, f32[2,128,6144]{2,1,0:T(8,128)S(1)} %bitcast.213, f32[2,6144]{1,0:T(2,128)S(1)} %copy-done.26, f32[2,6144]{1,0:T(2,128)S(1)} %copy-done.25, f32[2,128]{1,0:T(2,128)S(1)} %rsqrt_bitcast_fusion), kind=kOutput, calls=%fused_computation.61 | convolution fusion | flops 1618083840 | bytes 12944384 | tf_op jit(solution)/shard_map/dot_general | solution.py:283
  253.5 1.8 convolution_convert_fusion
  257.6 1.6 collective-permute-start.30
  259.7 3.5 %collective-permute-done.43 = bf16[256,384]{1,0:T(8,128)(2,1)S(1)} collective-permute-done((bf16[256,384]{1,0:T(8,128)(2,1)S(1)}, bf16[256,384]{1,0:T(8,128)(2,1)S(1)}, u32[]{:S(2)}, u32[]{:S(2)}) %collective-permute-start.43) | collective-permute-done | bytes 196640 | tf_op jit(solution)/shard_map/ppermute | solution.py:61
  265.2 1.7 collective-permute-start.51
  269.4 1.8 collective-permute-start.38
  273.6 1.8 collective-permute-start.52
  277.8 1.7 collective-permute-start.39
  282.0 1.7 collective-permute-start.53
  286.2 1.7 collective-permute-start.40
  290.4 1.7 collective-permute-start.54
  294.7 1.7 collective-permute-start.41
  302.8 1.8 collective-permute-start.35
  305.7 1.6 collective-permute-done.55
  (244 shorter events, 80.5 us)
Async XLA Ops:
  6.5 228.2 %all-gather.3.cloned.1.call-start = ((), (), s32[]{:S(2)}) async-start(), calls=%async_computation | async-start | bytes 9437184 | tf_op jit(solution)/shard_map/all_gather | solution.py:223
  7.3 234.0 %all-gather.5.cloned.1.call-start = ((), (), s32[]{:S(2)}) async-start(), calls=%async_computation.1 | async-start | bytes 9437184 | tf_op jit(solution)/shard_map/all_gather | solution.py:224
  7.3 21.7 %collective-permute-start = (bf16[4,128,768]{2,1,0:T(8,128)(2,1)}, bf16[4,128,768]{2,1,0:T(8,128)(2,1)}, u32[]{:S(2)}, u32[]{:S(2)}) collective-permute-start(bf16[4,128,768]{2,1,0:T(8,128)(2,1)} %param.17), channel_id=1, source_target_pairs={{0,2},{2,4},{4,6},{6,7},{7,5},{5,3},{3,1},{1,0},{8,10},{10,12},{12... | collective-permute-start | bytes 2359304 | tf_op jit(solution)/shard_map/ppermute | solution.py:34
  10.4 53.4 %collective-permute-start.4 = (bf16[4,128,768]{2,1,0:T(8,128)(2,1)}, bf16[4,128,768]{2,1,0:T(8,128)(2,1)}, u32[]{:S(2)}, u32[]{:S(2)}) collective-permute-start(bf16[4,128,768]{2,1,0:T(8,128)(2,1)} %param.17), channel_id=1, source_target_pairs={{0,1},{2,0},{4,2},{6,4},{7,6},{5,7},{3,5},{1,3},{8,9},{10,8},{12,1... | collective-permute-start | bytes 2359304 | tf_op jit(solution)/shard_map/ppermute | solution.py:38
  10.5 61.2 %collective-permute-start.14 = (bf16[128,3072]{1,0:T(8,128)(2,1)S(1)}, bf16[128,3072]{1,0:T(8,128)(2,1)S(1)}, u32[]{:S(2)}, u32[]{:S(2)}) collective-permute-start(bf16[128,3072]{1,0:T(8,128)(2,1)S(1)} %constant_dynamic-slice_fusion.6.refs_8_), channel_id=1, source_target_pairs={{0,2},{2,4},{4,6},{6,7},{7,5},{5,3},{3,1},{1,0},{8,10},{10,12},{12... | collective-permute-start | bytes 2359304 | tf_op jit(solution)/shard_map/ppermute | solution.py:34
  12.6 102.5 %collective-permute-start.18 = (bf16[128,3072]{1,0:T(8,128)(2,1)S(1)}, bf16[128,3072]{1,0:T(8,128)(2,1)S(1)}, u32[]{:S(2)}, u32[]{:S(2)}) collective-permute-start(bf16[128,3072]{1,0:T(8,128)(2,1)S(1)} %constant_dynamic-slice_fusion.6.refs_8_), channel_id=1, source_target_pairs={{0,1},{2,0},{4,2},{6,4},{7,6},{5,7},{3,5},{1,3},{8,9},{10,8},{12,1... | collective-permute-start | bytes 2359304 | tf_op jit(solution)/shard_map/ppermute | solution.py:38
  12.6 140.6 %collective-permute-start.21 = (bf16[128,3072]{1,0:T(8,128)(2,1)S(1)}, bf16[128,3072]{1,0:T(8,128)(2,1)}, u32[]{:S(2)}, u32[]{:S(2)}) collective-permute-start(bf16[128,3072]{1,0:T(8,128)(2,1)S(1)} %constant_dynamic-slice_fusion.6.refs_8_), channel_id=1, source_target_pairs={{0,8},{8,0},{1,9},{9,1},{2,10},{10,2},{3,11},{11,3},{4,12},{12,4},... | collective-permute-start | bytes 2359304 | tf_op jit(solution)/shard_map/ppermute | solution.py:221
  29.0 32.9 %collective-permute-start.1 = (bf16[4,128,768]{2,1,0:T(8,128)(2,1)}, bf16[4,128,768]{2,1,0:T(8,128)(2,1)}, u32[]{:S(2)}, u32[]{:S(2)}) collective-permute-start(bf16[4,128,768]{2,1,0:T(8,128)(2,1)} %collective-permute-done), channel_id=1, source_target_pairs={{0,2},{2,4},{4,6},{6,7},{7,5},{5,3},{3,1},{1,0},{8,10},{10,12},{12... | collective-permute-start | bytes 2359304 | tf_op jit(solution)/shard_map/ppermute | solution.py:34
  61.9 20.8 %collective-permute-start.2 = (bf16[4,128,768]{2,1,0:T(8,128)(2,1)}, bf16[4,128,768]{2,1,0:T(8,128)(2,1)}, u32[]{:S(2)}, u32[]{:S(2)}) collective-permute-start(bf16[4,128,768]{2,1,0:T(8,128)(2,1)} %collective-permute-done.1), channel_id=1, source_target_pairs={{0,2},{2,4},{4,6},{6,7},{7,5},{5,3},{3,1},{1,0},{8,10},{10,12},{12... | collective-permute-start | bytes 2359304 | tf_op jit(solution)/shard_map/ppermute | solution.py:34
  63.8 47.3 %collective-permute-start.5 = (bf16[4,128,768]{2,1,0:T(8,128)(2,1)}, bf16[4,128,768]{2,1,0:T(8,128)(2,1)}, u32[]{:S(2)}, u32[]{:S(2)}) collective-permute-start(bf16[4,128,768]{2,1,0:T(8,128)(2,1)} %collective-permute-done.4), channel_id=1, source_target_pairs={{0,1},{2,0},{4,2},{6,4},{7,6},{5,7},{3,5},{1,3},{8,9},{10,8},{12,1... | collective-permute-start | bytes 2359304 | tf_op jit(solution)/shard_map/ppermute | solution.py:38
  71.7 43.5 %collective-permute-start.15 = (bf16[128,3072]{1,0:T(8,128)(2,1)S(1)}, bf16[128,3072]{1,0:T(8,128)(2,1)}, u32[]{:S(2)}, u32[]{:S(2)}) collective-permute-start(bf16[128,3072]{1,0:T(8,128)(2,1)S(1)} %collective-permute-done.14.refs_9_), channel_id=1, source_target_pairs={{0,2},{2,4},{4,6},{6,7},{7,5},{5,3},{3,1},{1,0},{8,10},{10,12},{12... | collective-permute-start | bytes 2359304 | tf_op jit(solution)/shard_map/ppermute | solution.py:34
  82.7 34.3 %collective-permute-start.3 = (bf16[4,128,768]{2,1,0:T(8,128)(2,1)}, bf16[4,128,768]{2,1,0:T(8,128)(2,1)}, u32[]{:S(2)}, u32[]{:S(2)}) collective-permute-start(bf16[4,128,768]{2,1,0:T(8,128)(2,1)} %collective-permute-done.2), channel_id=1, source_target_pairs={{0,2},{2,4},{4,6},{6,7},{7,5},{5,3},{3,1},{1,0},{8,10},{10,12},{12... | collective-permute-start | bytes 2359304 | tf_op jit(solution)/shard_map/ppermute | solution.py:34
  111.1 20.7 %collective-permute-start.6 = (bf16[4,128,768]{2,1,0:T(8,128)(2,1)}, bf16[4,128,768]{2,1,0:T(8,128)(2,1)S(1)}, u32[]{:S(2)}, u32[]{:S(2)}) collective-permute-start(bf16[4,128,768]{2,1,0:T(8,128)(2,1)} %collective-permute-done.5), channel_id=1, source_target_pairs={{0,1},{2,0},{4,2},{6,4},{7,6},{5,7},{3,5},{1,3},{8,9},{10,8},{12,1... | collective-permute-start | bytes 2359304 | tf_op jit(solution)/shard_map/ppermute | solution.py:38
  115.1 63.3 %collective-permute-start.22 = (bf16[128,3072]{1,0:T(8,128)(2,1)S(1)}, bf16[128,3072]{1,0:T(8,128)(2,1)}, u32[]{:S(2)}, u32[]{:S(2)}) collective-permute-start(bf16[128,3072]{1,0:T(8,128)(2,1)S(1)} %collective-permute-done.14.refs_9_), channel_id=1, source_target_pairs={{0,8},{8,0},{1,9},{9,1},{2,10},{10,2},{3,11},{11,3},{4,12},{12,4},... | collective-permute-start | bytes 2359304 | tf_op jit(solution)/shard_map/ppermute | solution.py:221
  115.2 38.0 %collective-permute-start.19 = (bf16[128,3072]{1,0:T(8,128)(2,1)S(1)}, bf16[128,3072]{1,0:T(8,128)(2,1)}, u32[]{:S(2)}, u32[]{:S(2)}) collective-permute-start(bf16[128,3072]{1,0:T(8,128)(2,1)S(1)} %collective-permute-done.18.refs_13_), channel_id=1, source_target_pairs={{0,1},{2,0},{4,2},{6,4},{7,6},{5,7},{3,5},{1,3},{8,9},{10,8},{12,1... | collective-permute-start | bytes 2359304 | tf_op jit(solution)/shard_map/ppermute | solution.py:38
  117.0 36.8 %collective-permute-start.16 = (bf16[128,3072]{1,0:T(8,128)(2,1)}, bf16[128,3072]{1,0:T(8,128)(2,1)}, u32[]{:S(2)}, u32[]{:S(2)}) collective-permute-start(bf16[128,3072]{1,0:T(8,128)(2,1)} %collective-permute-done.15.refs_10_), channel_id=1, source_target_pairs={{0,2},{2,4},{4,6},{6,7},{7,5},{5,3},{3,1},{1,0},{8,10},{10,12},{12... | collective-permute-start | bytes 2359304 | tf_op jit(solution)/shard_map/ppermute | solution.py:34
  148.5 6.8 %collective-permute-start.7 = (bf16[512,128]{1,0:T(8,128)(2,1)S(1)}, bf16[512,128]{1,0:T(8,128)(2,1)S(1)}, u32[]{:S(2)}, u32[]{:S(2)}) collective-permute-start(bf16[512,128]{1,0:T(8,128)(2,1)S(1)} %bitcast.207), channel_id=1, source_target_pairs={{0,2},{2,4},{4,6},{6,7},{7,5},{5,3},{3,1},{1,0},{8,10},{10,12},{12... | collective-permute-start | bytes 393224 | tf_op jit(solution)/shard_map/ppermute | solution.py:34
  153.2 35.3 %collective-permute-start.26 = (bf16[128,3072]{1,0:T(8,128)(2,1)S(1)}, bf16[128,3072]{1,0:T(8,128)(2,1)S(1)}, u32[]{:S(2)}, u32[]{:S(2)}) collective-permute-start(bf16[128,3072]{1,0:T(8,128)(2,1)S(1)} %collective-permute-done.18.refs_13_), channel_id=1, source_target_pairs={{0,8},{8,0},{1,9},{9,1},{2,10},{10,2},{3,11},{11,3},{4,12},{12,4},... | collective-permute-start | bytes 2359304 | tf_op jit(solution)/shard_map/ppermute | solution.py:221
  153.2 35.2 %collective-permute-start.20 = (bf16[128,3072]{1,0:T(8,128)(2,1)}, bf16[128,3072]{1,0:T(8,128)(2,1)S(1)}, u32[]{:S(2)}, u32[]{:S(2)}) collective-permute-start(bf16[128,3072]{1,0:T(8,128)(2,1)} %collective-permute-done.19.refs_14_), channel_id=1, source_target_pairs={{0,1},{2,0},{4,2},{6,4},{7,6},{5,7},{3,5},{1,3},{8,9},{10,8},{12,1... | collective-permute-start | bytes 2359304 | tf_op jit(solution)/shard_map/ppermute | solution.py:38
  153.7 35.3 %collective-permute-start.17 = (bf16[128,3072]{1,0:T(8,128)(2,1)}, bf16[128,3072]{1,0:T(8,128)(2,1)S(1)}, u32[]{:S(2)}, u32[]{:S(2)}) collective-permute-start(bf16[128,3072]{1,0:T(8,128)(2,1)} %collective-permute-done.16.refs_11_), channel_id=1, source_target_pairs={{0,2},{2,4},{4,6},{6,7},{7,5},{5,3},{3,1},{1,0},{8,10},{10,12},{12... | collective-permute-start | bytes 2359304 | tf_op jit(solution)/shard_map/ppermute | solution.py:34
  155.3 20.9 %collective-permute-start.11 = (bf16[512,128]{1,0:T(8,128)(2,1)S(1)}, bf16[512,128]{1,0:T(8,128)(2,1)S(1)}, u32[]{:S(2)}, u32[]{:S(2)}) collective-permute-start(bf16[512,128]{1,0:T(8,128)(2,1)S(1)} %bitcast.208), channel_id=1, source_target_pairs={{0,1},{2,0},{4,2},{6,4},{7,6},{5,7},{3,5},{1,3},{8,9},{10,8},{12,1... | collective-permute-start | bytes 393224 | tf_op jit(solution)/shard_map/ppermute | solution.py:38
  189.0 6.5 %collective-permute-start.24 = (bf16[128,3072]{1,0:T(8,128)(2,1)}, bf16[128,3072]{1,0:T(8,128)(2,1)S(1)}, u32[]{:S(2)}, u32[]{:S(2)}) collective-permute-start(bf16[128,3072]{1,0:T(8,128)(2,1)} %collective-permute-done.16.refs_11_), channel_id=1, source_target_pairs={{0,8},{8,0},{1,9},{9,1},{2,10},{10,2},{3,11},{11,3},{4,12},{12,4},... | collective-permute-start | bytes 2359304 | tf_op jit(solution)/shard_map/ppermute | solution.py:221
  246.3 11.2 %collective-permute-start.29 = (bf16[256,384]{1,0:T(8,128)(2,1)S(1)}, bf16[256,384]{1,0:T(8,128)(2,1)S(1)}, u32[]{:S(2)}, u32[]{:S(2)}) collective-permute-start(bf16[256,384]{1,0:T(8,128)(2,1)S(1)} %get-tuple-element.29), channel_id=1, source_target_pairs={{0,2},{2,4},{4,6},{6,7},{7,5},{5,3},{3,1},{1,0},{8,10},{10,12},{12... | collective-permute-start | bytes 589832 | tf_op jit(solution)/shard_map/ppermute | solution.py:61
  247.8 9.6 %collective-permute-start.36 = (bf16[256,384]{1,0:T(8,128)(2,1)S(1)}, bf16[256,384]{1,0:T(8,128)(2,1)S(1)}, u32[]{:S(2)}, u32[]{:S(2)}) collective-permute-start(bf16[256,384]{1,0:T(8,128)(2,1)S(1)} %get-tuple-element.30), channel_id=1, source_target_pairs={{0,1},{2,0},{4,2},{6,4},{7,6},{5,7},{3,5},{1,3},{8,9},{10,8},{12,1... | collective-permute-start | bytes 589832 | tf_op jit(solution)/shard_map/ppermute | solution.py:63
  255.4 7.8 %collective-permute-start.43 = (bf16[256,384]{1,0:T(8,128)(2,1)S(1)}, bf16[256,384]{1,0:T(8,128)(2,1)S(1)}, u32[]{:S(2)}, u32[]{:S(2)}) collective-permute-start(bf16[256,384]{1,0:T(8,128)(2,1)S(1)} %get-tuple-element.45), channel_id=1, source_target_pairs={{0,2},{2,4},{4,6},{6,7},{7,5},{5,3},{3,1},{1,0},{8,10},{10,12},{12... | collective-permute-start | bytes 589832 | tf_op jit(solution)/shard_map/ppermute | solution.py:61
  256.9 7.8 %collective-permute-start.50 = (bf16[256,384]{1,0:T(8,128)(2,1)S(1)}, bf16[256,384]{1,0:T(8,128)(2,1)S(1)}, u32[]{:S(2)}, u32[]{:S(2)}) collective-permute-start(bf16[256,384]{1,0:T(8,128)(2,1)S(1)} %get-tuple-element.46), channel_id=1, source_target_pairs={{0,1},{2,0},{4,2},{6,4},{7,6},{5,7},{3,5},{1,3},{8,9},{10,8},{12,1... | collective-permute-start | bytes 589832 | tf_op jit(solution)/shard_map/ppermute | solution.py:63
  257.6 9.8 %collective-permute-start.30 = (bf16[256,384]{1,0:T(8,128)(2,1)S(1)}, bf16[256,384]{1,0:T(8,128)(2,1)S(1)}, u32[]{:S(2)}, u32[]{:S(2)}) collective-permute-start(bf16[256,384]{1,0:T(8,128)(2,1)S(1)} %get-tuple-element.27), channel_id=1, source_target_pairs={{0,2},{2,4},{4,6},{6,7},{7,5},{5,3},{3,1},{1,0},{8,10},{10,12},{12... | collective-permute-start | bytes 589832 | tf_op jit(solution)/shard_map/ppermute | solution.py:61
  259.1 9.8 %collective-permute-start.37 = (bf16[256,384]{1,0:T(8,128)(2,1)S(1)}, bf16[256,384]{1,0:T(8,128)(2,1)S(1)}, u32[]{:S(2)}, u32[]{:S(2)}) collective-permute-start(bf16[256,384]{1,0:T(8,128)(2,1)S(1)} %get-tuple-element.28), channel_id=1, source_target_pairs={{0,1},{2,0},{4,2},{6,4},{7,6},{5,7},{3,5},{1,3},{8,9},{10,8},{12,1... | collective-permute-start | bytes 589832 | tf_op jit(solution)/shard_map/ppermute | solution.py:63
  264.8 7.2 %collective-permute-start.44 = (bf16[256,384]{1,0:T(8,128)(2,1)S(1)}, bf16[256,384]{1,0:T(8,128)(2,1)S(1)}, u32[]{:S(2)}, u32[]{:S(2)}) collective-permute-start(bf16[256,384]{1,0:T(8,128)(2,1)S(1)} %get-tuple-element.43), channel_id=1, source_target_pairs={{0,2},{2,4},{4,6},{6,7},{7,5},{5,3},{3,1},{1,0},{8,10},{10,12},{12... | collective-permute-start | bytes 589832 | tf_op jit(solution)/shard_map/ppermute | solution.py:61
  265.2 8.0 %collective-permute-start.51 = (bf16[256,384]{1,0:T(8,128)(2,1)S(1)}, bf16[256,384]{1,0:T(8,128)(2,1)S(1)}, u32[]{:S(2)}, u32[]{:S(2)}) collective-permute-start(bf16[256,384]{1,0:T(8,128)(2,1)S(1)} %get-tuple-element.44), channel_id=1, source_target_pairs={{0,1},{2,0},{4,2},{6,4},{7,6},{5,7},{3,5},{1,3},{8,9},{10,8},{12,1... | collective-permute-start | bytes 589832 | tf_op jit(solution)/shard_map/ppermute | solution.py:63
  269.0 7.2 %collective-permute-start.31 = (bf16[256,384]{1,0:T(8,128)(2,1)S(1)}, bf16[256,384]{1,0:T(8,128)(2,1)S(1)}, u32[]{:S(2)}, u32[]{:S(2)}) collective-permute-start(bf16[256,384]{1,0:T(8,128)(2,1)S(1)} %get-tuple-element.25), channel_id=1, source_target_pairs={{0,2},{2,4},{4,6},{6,7},{7,5},{5,3},{3,1},{1,0},{8,10},{10,12},{12... | collective-permute-start | bytes 589832 | tf_op jit(solution)/shard_map/ppermute | solution.py:61
  269.4 8.0 %collective-permute-start.38 = (bf16[256,384]{1,0:T(8,128)(2,1)S(1)}, bf16[256,384]{1,0:T(8,128)(2,1)S(1)}, u32[]{:S(2)}, u32[]{:S(2)}) collective-permute-start(bf16[256,384]{1,0:T(8,128)(2,1)S(1)} %get-tuple-element.26), channel_id=1, source_target_pairs={{0,1},{2,0},{4,2},{6,4},{7,6},{5,7},{3,5},{1,3},{8,9},{10,8},{12,1... | collective-permute-start | bytes 589832 | tf_op jit(solution)/shard_map/ppermute | solution.py:63
  273.3 7.2 %collective-permute-start.45 = (bf16[256,384]{1,0:T(8,128)(2,1)S(1)}, bf16[256,384]{1,0:T(8,128)(2,1)S(1)}, u32[]{:S(2)}, u32[]{:S(2)}) collective-permute-start(bf16[256,384]{1,0:T(8,128)(2,1)S(1)} %get-tuple-element.41), channel_id=1, source_target_pairs={{0,2},{2,4},{4,6},{6,7},{7,5},{5,3},{3,1},{1,0},{8,10},{10,12},{12... | collective-permute-start | bytes 589832 | tf_op jit(solution)/shard_map/ppermute | solution.py:61
  273.6 8.0 %collective-permute-start.52 = (bf16[256,384]{1,0:T(8,128)(2,1)S(1)}, bf16[256,384]{1,0:T(8,128)(2,1)S(1)}, u32[]{:S(2)}, u32[]{:S(2)}) collective-permute-start(bf16[256,384]{1,0:T(8,128)(2,1)S(1)} %get-tuple-element.42), channel_id=1, source_target_pairs={{0,1},{2,0},{4,2},{6,4},{7,6},{5,7},{3,5},{1,3},{8,9},{10,8},{12,1... | collective-permute-start | bytes 589832 | tf_op jit(solution)/shard_map/ppermute | solution.py:63
  277.5 7.2 %collective-permute-start.32 = (bf16[256,384]{1,0:T(8,128)(2,1)S(1)}, bf16[256,384]{1,0:T(8,128)(2,1)S(1)}, u32[]{:S(2)}, u32[]{:S(2)}) collective-permute-start(bf16[256,384]{1,0:T(8,128)(2,1)S(1)} %get-tuple-element.23), channel_id=1, source_target_pairs={{0,2},{2,4},{4,6},{6,7},{7,5},{5,3},{3,1},{1,0},{8,10},{10,12},{12... | collective-permute-start | bytes 589832 | tf_op jit(solution)/shard_map/ppermute | solution.py:61
  277.8 8.0 %collective-permute-start.39 = (bf16[256,384]{1,0:T(8,128)(2,1)S(1)}, bf16[256,384]{1,0:T(8,128)(2,1)S(1)}, u32[]{:S(2)}, u32[]{:S(2)}) collective-permute-start(bf16[256,384]{1,0:T(8,128)(2,1)S(1)} %get-tuple-element.24), channel_id=1, source_target_pairs={{0,1},{2,0},{4,2},{6,4},{7,6},{5,7},{3,5},{1,3},{8,9},{10,8},{12,1... | collective-permute-start | bytes 589832 | tf_op jit(solution)/shard_map/ppermute | solution.py:63
  281.7 7.2 %collective-permute-start.46 = (bf16[256,384]{1,0:T(8,128)(2,1)S(1)}, bf16[256,384]{1,0:T(8,128)(2,1)S(1)}, u32[]{:S(2)}, u32[]{:S(2)}) collective-permute-start(bf16[256,384]{1,0:T(8,128)(2,1)S(1)} %get-tuple-element.39), channel_id=1, source_target_pairs={{0,2},{2,4},{4,6},{6,7},{7,5},{5,3},{3,1},{1,0},{8,10},{10,12},{12... | collective-permute-start | bytes 589832 | tf_op jit(solution)/shard_map/ppermute | solution.py:61
  282.0 8.0 %collective-permute-start.53 = (bf16[256,384]{1,0:T(8,128)(2,1)S(1)}, bf16[256,384]{1,0:T(8,128)(2,1)S(1)}, u32[]{:S(2)}, u32[]{:S(2)}) collective-permute-start(bf16[256,384]{1,0:T(8,128)(2,1)S(1)} %get-tuple-element.40), channel_id=1, source_target_pairs={{0,1},{2,0},{4,2},{6,4},{7,6},{5,7},{3,5},{1,3},{8,9},{10,8},{12,1... | collective-permute-start | bytes 589832 | tf_op jit(solution)/shard_map/ppermute | solution.py:63
  285.9 7.2 %collective-permute-start.33 = (bf16[256,384]{1,0:T(8,128)(2,1)S(1)}, bf16[256,384]{1,0:T(8,128)(2,1)S(1)}, u32[]{:S(2)}, u32[]{:S(2)}) collective-permute-start(bf16[256,384]{1,0:T(8,128)(2,1)S(1)} %get-tuple-element.21), channel_id=1, source_target_pairs={{0,2},{2,4},{4,6},{6,7},{7,5},{5,3},{3,1},{1,0},{8,10},{10,12},{12... | collective-permute-start | bytes 589832 | tf_op jit(solution)/shard_map/ppermute | solution.py:61
  286.2 8.0 %collective-permute-start.40 = (bf16[256,384]{1,0:T(8,128)(2,1)S(1)}, bf16[256,384]{1,0:T(8,128)(2,1)S(1)}, u32[]{:S(2)}, u32[]{:S(2)}) collective-permute-start(bf16[256,384]{1,0:T(8,128)(2,1)S(1)} %get-tuple-element.22), channel_id=1, source_target_pairs={{0,1},{2,0},{4,2},{6,4},{7,6},{5,7},{3,5},{1,3},{8,9},{10,8},{12,1... | collective-permute-start | bytes 589832 | tf_op jit(solution)/shard_map/ppermute | solution.py:63
  290.1 7.2 %collective-permute-start.47 = (bf16[256,384]{1,0:T(8,128)(2,1)S(1)}, bf16[256,384]{1,0:T(8,128)(2,1)S(1)}, u32[]{:S(2)}, u32[]{:S(2)}) collective-permute-start(bf16[256,384]{1,0:T(8,128)(2,1)S(1)} %get-tuple-element.37), channel_id=1, source_target_pairs={{0,2},{2,4},{4,6},{6,7},{7,5},{5,3},{3,1},{1,0},{8,10},{10,12},{12... | collective-permute-start | bytes 589832 | tf_op jit(solution)/shard_map/ppermute | solution.py:61
  290.4 8.0 %collective-permute-start.54 = (bf16[256,384]{1,0:T(8,128)(2,1)S(1)}, bf16[256,384]{1,0:T(8,128)(2,1)S(1)}, u32[]{:S(2)}, u32[]{:S(2)}) collective-permute-start(bf16[256,384]{1,0:T(8,128)(2,1)S(1)} %get-tuple-element.38), channel_id=1, source_target_pairs={{0,1},{2,0},{4,2},{6,4},{7,6},{5,7},{3,5},{1,3},{8,9},{10,8},{12,1... | collective-permute-start | bytes 589832 | tf_op jit(solution)/shard_map/ppermute | solution.py:63
  294.3 7.2 %collective-permute-start.34 = (bf16[256,384]{1,0:T(8,128)(2,1)S(1)}, bf16[256,384]{1,0:T(8,128)(2,1)S(1)}, u32[]{:S(2)}, u32[]{:S(2)}) collective-permute-start(bf16[256,384]{1,0:T(8,128)(2,1)S(1)} %get-tuple-element.19), channel_id=1, source_target_pairs={{0,2},{2,4},{4,6},{6,7},{7,5},{5,3},{3,1},{1,0},{8,10},{10,12},{12... | collective-permute-start | bytes 589832 | tf_op jit(solution)/shard_map/ppermute | solution.py:61
  294.7 8.0 %collective-permute-start.41 = (bf16[256,384]{1,0:T(8,128)(2,1)S(1)}, bf16[256,384]{1,0:T(8,128)(2,1)S(1)}, u32[]{:S(2)}, u32[]{:S(2)}) collective-permute-start(bf16[256,384]{1,0:T(8,128)(2,1)S(1)} %get-tuple-element.20), channel_id=1, source_target_pairs={{0,1},{2,0},{4,2},{6,4},{7,6},{5,7},{3,5},{1,3},{8,9},{10,8},{12,1... | collective-permute-start | bytes 589832 | tf_op jit(solution)/shard_map/ppermute | solution.py:63
  298.5 7.2 %collective-permute-start.48 = (bf16[256,384]{1,0:T(8,128)(2,1)S(1)}, bf16[256,384]{1,0:T(8,128)(2,1)S(1)}, u32[]{:S(2)}, u32[]{:S(2)}) collective-permute-start(bf16[256,384]{1,0:T(8,128)(2,1)S(1)} %get-tuple-element.35), channel_id=1, source_target_pairs={{0,2},{2,4},{4,6},{6,7},{7,5},{5,3},{3,1},{1,0},{8,10},{10,12},{12... | collective-permute-start | bytes 589832 | tf_op jit(solution)/shard_map/ppermute | solution.py:61
  299.5 7.8 %collective-permute-start.55 = (bf16[256,384]{1,0:T(8,128)(2,1)S(1)}, bf16[256,384]{1,0:T(8,128)(2,1)S(1)}, u32[]{:S(2)}, u32[]{:S(2)}) collective-permute-start(bf16[256,384]{1,0:T(8,128)(2,1)S(1)} %get-tuple-element.36), channel_id=1, source_target_pairs={{0,1},{2,0},{4,2},{6,4},{7,6},{5,7},{3,5},{1,3},{8,9},{10,8},{12,1... | collective-permute-start | bytes 589832 | tf_op jit(solution)/shard_map/ppermute | solution.py:63
  302.8 7.8 %collective-permute-start.35 = (bf16[256,384]{1,0:T(8,128)(2,1)S(1)}, bf16[256,384]{1,0:T(8,128)(2,1)S(1)}, u32[]{:S(2)}, u32[]{:S(2)}) collective-permute-start(bf16[256,384]{1,0:T(8,128)(2,1)S(1)} %get-tuple-element.17), channel_id=1, source_target_pairs={{0,2},{2,4},{4,6},{6,7},{7,5},{5,3},{3,1},{1,0},{8,10},{10,12},{12... | collective-permute-start | bytes 589832 | tf_op jit(solution)/shard_map/ppermute | solution.py:61
  304.5 7.5 %collective-permute-start.42 = (bf16[256,384]{1,0:T(8,128)(2,1)S(1)}, bf16[256,384]{1,0:T(8,128)(2,1)S(1)}, u32[]{:S(2)}, u32[]{:S(2)}) collective-permute-start(bf16[256,384]{1,0:T(8,128)(2,1)S(1)} %get-tuple-element.18), channel_id=1, source_target_pairs={{0,1},{2,0},{4,2},{6,4},{7,6},{5,7},{3,5},{1,3},{8,9},{10,8},{12,1... | collective-permute-start | bytes 589832 | tf_op jit(solution)/shard_map/ppermute | solution.py:63
  (48 other events, 863.7 us)
Sparse Core Ops, SparseCore 0:
  8.9 18.3 all-gather.2
  28.8 17.9 all-gather.4

commit v14 on v10

--- a/solution.py
+++ b/solution.py
@@ -84,9 +84,15 @@
                 hidden_ref[rows, :].astype(jnp.float32) + scale_ref[span:span + 1, :] * total[rows, :]
             )
         result = out_ref[...]
-        squares_ref[...] = jnp.broadcast_to(
-            jnp.sum(result * result, axis=1, keepdims=True), squares_ref.shape
-        )
+        partial = jnp.broadcast_to(jnp.sum(result * result, axis=1, keepdims=True), squares_ref.shape)
+
+        @pl.when(tile == 0)
+        def _():
+            squares_ref[...] = partial
+
+        @pl.when(tile > 0)
+        def _():
+            squares_ref[...] += partial
 
     @pl.when(tile < tiles_per_half)
     def _():
@@ -120,7 +126,7 @@
     out_spec = pl.BlockSpec((token_count, tile_width), lambda n, s: (0, column(n, s)))
     hidden_spec = pl.BlockSpec((token_count, tile_width), lambda n, s: (0, column(n, s)))
     scale_spec = pl.BlockSpec((span_rows, tile_width), lambda n, s: (0, column(n, s)))
-    squares_spec = pl.BlockSpec((token_count, 128), lambda n, s: (0, n))
+    squares_spec = pl.BlockSpec((token_count, 128), lambda n, s: (0, 0))
     tile_count = 2 * tiles_per_half
     flops = 2 * token_count * head_width * group_count * half_width * 2
     moved = 2 * (group_count * token_count * head_width + 2 * group_count * head_width * half_width)
@@ -129,7 +135,7 @@
         functools.partial(out_proj_kernel, group_count, tiles_per_half, token_count // span_rows),
         out_shape=(
             jax.ShapeDtypeStruct((token_count, 2 * half_width), jnp.float32),
-            jax.ShapeDtypeStruct((token_count, tile_count * 128), jnp.float32),
+            jax.ShapeDtypeStruct((token_count, 128), jnp.float32),
         ),
         grid_spec=pltpu.PrefetchScalarGridSpec(
             num_scalar_prefetch=1,
@@ -147,7 +153,7 @@
         hidden,
         scale,
     )
-    return residual, squares.reshape(token_count, tile_count, 128)[:, :, 0].sum(axis=1)
+    return residual, squares[:, 0]
 
 
 def select_row(source, target):

time: 330 us -> 327 us (level)
  local copies, waits for them, and re-layouts: 25.9 us -> 21.6 us
    pallas_call x1 -> x0, local copies, waits for them, and re-layouts: 3.55 us -> none  [grouped_out_proj(): pl.pallas_call(functools.partial(out_proj_kernel, group_count, tiles_per_...]
  transfers between devices with their start and end apart: 45 -> 45, of which waited for: 24 -> 25; matrix products, arithmetic and copies ran while one was open for 14% -> 13% of each run, Pallas kernels for 7% -> 7%
where the time goes in v14:
time: 327 us; the launch traced here: 326 us
  waiting for transfers between devices  159 us (49%)
  starting transfers between devices  39.9 us (12%)
  between operations  32.8 us (10%)
  matrix products  24.9 us (8%)
  Pallas kernels  22.9 us (7%)
  local copies, waits for them, and re-layouts  21.6 us (7%)
  other arithmetic  20 us (6%)
  blocking collectives  4.54 us (1%)
    ppermute x12, waiting for transfers between devices, ring_gather(): forward = lax.ppermute(forward, axis_name, ahead)  78.7 us
    ppermute x7, waiting for transfers between devices, ring_reduce_scatter(): lax.ppermute(forward.astype(jnp.bfloat16), axis_name, ahead)  50.8 us
    pallas_call x1, Pallas kernels, grouped_out_proj(): pl.pallas_call(functools.partial(out_proj_kernel, group_count, tiles_per_...  22.9 us
    ppermute x12, starting transfers between devices, ring_gather(): forward = lax.ppermute(forward, axis_name, ahead)  21.6 us
    ppermute x9, waiting for transfers between devices, ring_gather(): backward = lax.ppermute(backward, axis_name, behind)  21.1 us
    unnamed x59, local copies, waits for them, and re-layouts  10.3 us
    dot_general x1, matrix products, local(): pre_act = jnp.dot(mlp_in, up_full, preferred_element_type=jnp.float32)  10 us
    convert_element_type x6, other arithmetic, ring_reduce_scatter(): forward.astype(jnp.bfloat16)  8.73 us
  transfers between devices with their start and end apart: 45, of which 25 were waited for; matrix products, arithmetic and copies ran while one was open for 13% of the time, Pallas kernels for 7%

profile of v14, /device:TPU:0, one launch (start us, length us, event | category | flops | bytes accessed | tf_op | source)
XLA Modules:
  0.0 325.6 jit_solution(1826809258907958879)
XLA Ops:
  7.4 3.1 collective-permute-start
  10.5 2.1 collective-permute-start.14
  14.4 14.6 %collective-permute-done = bf16[4,128,768]{2,1,0:T(8,128)(2,1)} collective-permute-done((bf16[4,128,768]{2,1,0:T(8,128)(2,1)}, bf16[4,128,768]{2,1,0:T(8,128)(2,1)}, u32[]{:S(2)}, u32[]{:S(2)}) %collective-permute-start) | collective-permute-done | bytes 786464 | tf_op jit(solution)/shard_map/ppermute | solution.py:34
  29.1 2.1 collective-permute-start.1
  31.5 30.3 %collective-permute-done.1 = bf16[4,128,768]{2,1,0:T(8,128)(2,1)S(1)} collective-permute-done((bf16[4,128,768]{2,1,0:T(8,128)(2,1)}, bf16[4,128,768]{2,1,0:T(8,128)(2,1)S(1)}, u32[]{:S(2)}, u32[]{:S(2)}) %collective-permute-start.1) | collective-permute-done | bytes 786464 | tf_op jit(solution)/shard_map/ppermute | solution.py:34
  61.8 1.8 collective-permute-start.2
  65.4 2.2 all_gather.12
  67.6 13.1 %collective-permute-done.2 = bf16[4,128,768]{2,1,0:T(8,128)(2,1)} collective-permute-done((bf16[4,128,768]{2,1,0:T(8,128)(2,1)S(1)}, bf16[4,128,768]{2,1,0:T(8,128)(2,1)}, u32[]{:S(2)}, u32[]{:S(2)}) %collective-permute-start.2) | collective-permute-done | bytes 786464 | tf_op jit(solution)/shard_map/ppermute | solution.py:34
  80.7 1.5 collective-permute-start.3
  96.5 6.7 %copy.30 = bf16[6144,3,128]{0,2,1:T(8,128)(2,1)} copy(bf16[6144,3,128]{2,0,1:T(8,128)(2,1)} %param.22) | data formatting | bytes 9437184 | tf_op args[7]
  104.2 1.6 collective-permute-start.15
  114.4 7.4 %collective-permute-done.15.refs_10_ = bf16[128,3072]{1,0:T(8,128)(2,1)} collective-permute-done((bf16[128,3072]{1,0:T(8,128)(2,1)}, bf16[128,3072]{1,0:T(8,128)(2,1)}, u32[]{:S(2)}, u32[]{:S(2)}) %collective-permute-start.15) | collective-permute-done | bytes 786464 | tf_op jit(solution)/shard_map/ppermute | solution.py:34
  121.8 4.7 %collective-permute-done.6 = bf16[4,128,768]{2,1,0:T(8,128)(2,1)S(1)} collective-permute-done((bf16[4,128,768]{2,1,0:T(8,128)(2,1)}, bf16[4,128,768]{2,1,0:T(8,128)(2,1)S(1)}, u32[]{:S(2)}, u32[]{:S(2)}) %collective-permute-start.6) | collective-permute-done | bytes 786464 | tf_op jit(solution)/shard_map/ppermute | solution.py:38
  126.5 1.6 collective-permute-start.16
  129.5 2.7 fusion.3
  132.3 5.8 %convolution_convert_fusion.1 = bf16[512,384]{1,0:T(8,128)(2,1)S(1)} fusion(bf16[512,6144]{1,0:T(8,128)(2,1)S(1)} %bitcast.152, bf16[6144,384]{0,1:T(8,128)(2,1)} %bitcast.153), kind=kOutput, calls=%fused_computation.27 | convolution fusion | flops 2416115712 | bytes 11403264 | tf_op jit(solution)/shard_map/dot_general | solution.py:243
  138.9 2.4 all_gather.13
  144.1 1.6 collective-permute-start.17
  147.2 16.3 %collective-permute-done.20.refs_15_ = bf16[128,3072]{1,0:T(8,128)(2,1)S(1)} collective-permute-done((bf16[128,3072]{1,0:T(8,128)(2,1)}, bf16[128,3072]{1,0:T(8,128)(2,1)S(1)}, u32[]{:S(2)}, u32[]{:S(2)}) %collective-permute-start.20) | collective-permute-done | bytes 786464 | tf_op jit(solution)/shard_map/ppermute | solution.py:38
  164.8 1.6 collective-permute-start.7
  166.9 3.9 %collective-permute-done.7.refs_1_ = bf16[512,128]{1,0:T(8,128)(2,1)S(1)} collective-permute-done((bf16[512,128]{1,0:T(8,128)(2,1)S(1)}, bf16[512,128]{1,0:T(8,128)(2,1)S(1)}, u32[]{:S(2)}, u32[]{:S(2)}) %collective-permute-start.7) | collective-permute-done | bytes 131104 | tf_op jit(solution)/shard_map/ppermute | solution.py:34
  170.7 1.6 collective-permute-start.8
  172.8 3.1 collective-permute-done.8.refs_2_
  175.9 1.5 collective-permute-start.9
  177.9 2.9 collective-permute-done.9.refs_3_
  180.8 1.5 collective-permute-start.10
  183.1 2.7 collective-permute-done.10.refs_4_
  186.5 22.9 %shard_map.145 = (f32[512,6144]{1,0:T(8,128)}, f32[512,128]{1,0:T(8,128)}) custom-call(s32[1]{0:T(128)} %bitcast.span_ref, bf16[512,128]{1,0:T(8,128)(2,1)} %bitcast.165, bf16[512,128]{1,0:T(8,128)(2,1)} %copy-done.17, bf16[512,128]{1,0:T(8,128)(2,1)} %copy-done.19, bf16[512,128]{1,0:T(8,128)(2,1)} %copy-done.21, bf16[512,128]{1,0:T(8,128)(2,1)} %copy-done.23, ...), custom_call_target="tpu_custom_call" | custom-call | flops 6442450944 | bytes 32505856 | tf_op jit(solution)/shard_map/pallas_call | solution.py:134
  210.5 10.0 %fusion.27 = bf16[4,128,512]{2,1,0:T(8,128)(2,1)S(1)} fusion(bf16[6144,512]{1,0:T(8,128)(2,1)} %all-gather.3.cloned.1.call-done, f32[4,128,6144]{2,1,0:T(8,128)} %bitcast.158, f32[4,6144]{1,0:T(4,128)S(1)} %copy-done.11, f32[4,6144]{1,0:T(4,128)S(1)} %copy-done.10, f32[4,128]{1,0:T(4,128)S(1)} %bitcast.162), kind=kOutput, calls=%fused_computation.38 | convolution fusion | flops 3236167680 | bytes 19597312 | tf_op jit(solution)/shard_map/dot_general | solution.py:296
  220.6 6.6 %convolution_convert_fusion = bf16[4,128,6144]{2,1,0:T(8,128)(2,1)S(1)} fusion(bf16[4,128,512]{2,1,0:T(8,128)(2,1)S(1)} %fusion.27, bf16[512,6144]{1,0:T(8,128)(2,1)} %all-gather.5.cloned.1.call-done), kind=kOutput, calls=%fused_computation.7 | convolution fusion | flops 3224371200 | bytes 13107200 | tf_op jit(solution)/shard_map/dot_general | solution.py:298
  227.2 2.6 copy-done.3
  229.9 1.6 collective-permute-start.29
  233.2 4.6 %collective-permute-done.29 = bf16[512,384]{1,0:T(8,128)(2,1)S(1)} collective-permute-done((bf16[512,384]{1,0:T(8,128)(2,1)S(1)}, bf16[512,384]{1,0:T(8,128)(2,1)S(1)}, u32[]{:S(2)}, u32[]{:S(2)}) %collective-permute-start.29) | collective-permute-done | bytes 393248 | tf_op jit(solution)/shard_map/ppermute | solution.py:61
  237.7 1.5 collective-permute-done.36
  240.6 2.1 collective-permute-start.30
  244.0 5.5 %collective-permute-done.30 = bf16[512,384]{1,0:T(8,128)(2,1)S(1)} collective-permute-done((bf16[512,384]{1,0:T(8,128)(2,1)S(1)}, bf16[512,384]{1,0:T(8,128)(2,1)S(1)}, u32[]{:S(2)}, u32[]{:S(2)}) %collective-permute-start.30) | collective-permute-done | bytes 393248 | tf_op jit(solution)/shard_map/ppermute | solution.py:61
  249.5 2.8 collective-permute-done.37
  256.3 8.2 %collective-permute-done.31 = bf16[512,384]{1,0:T(8,128)(2,1)S(1)} collective-permute-done((bf16[512,384]{1,0:T(8,128)(2,1)S(1)}, bf16[512,384]{1,0:T(8,128)(2,1)S(1)}, u32[]{:S(2)}, u32[]{:S(2)}) %collective-permute-start.31) | collective-permute-done | bytes 393248 | tf_op jit(solution)/shard_map/ppermute | solution.py:61
  267.6 1.6 collective-permute-start.39
  269.2 9.5 %collective-permute-done.32 = bf16[512,384]{1,0:T(8,128)(2,1)S(1)} collective-permute-done((bf16[512,384]{1,0:T(8,128)(2,1)S(1)}, bf16[512,384]{1,0:T(8,128)(2,1)S(1)}, u32[]{:S(2)}, u32[]{:S(2)}) %collective-permute-start.32) | collective-permute-done | bytes 393248 | tf_op jit(solution)/shard_map/ppermute | solution.py:61
  280.6 1.7 collective-permute-start.40
  282.2 8.6 %collective-permute-done.33 = bf16[512,384]{1,0:T(8,128)(2,1)S(1)} collective-permute-done((bf16[512,384]{1,0:T(8,128)(2,1)S(1)}, bf16[512,384]{1,0:T(8,128)(2,1)S(1)}, u32[]{:S(2)}, u32[]{:S(2)}) %collective-permute-start.33) | collective-permute-done | bytes 393248 | tf_op jit(solution)/shard_map/ppermute | solution.py:61
  292.8 1.6 collective-permute-start.41
  294.4 8.5 %collective-permute-done.34 = bf16[512,384]{1,0:T(8,128)(2,1)S(1)} collective-permute-done((bf16[512,384]{1,0:T(8,128)(2,1)S(1)}, bf16[512,384]{1,0:T(8,128)(2,1)S(1)}, u32[]{:S(2)}, u32[]{:S(2)}) %collective-permute-start.34) | collective-permute-done | bytes 393248 | tf_op jit(solution)/shard_map/ppermute | solution.py:61
  303.2 2.2 add_convert_fusion.13
  307.5 6.0 %collective-permute-done.35 = bf16[512,384]{1,0:T(8,128)(2,1)S(1)} collective-permute-done((bf16[512,384]{1,0:T(8,128)(2,1)}, bf16[512,384]{1,0:T(8,128)(2,1)S(1)}, u32[]{:S(2)}, u32[]{:S(2)}) %collective-permute-start.35) | collective-permute-done | bytes 393248 | tf_op jit(solution)/shard_map/ppermute | solution.py:61
  314.6 1.4 convert_add_fusion.1
  316.1 2.6 add_convert_fusion.2
  (159 shorter events, 40.5 us)
Async XLA Ops:
  6.5 84.1 %copy-start.9 = (s32[8]{0:T(128)S(1)}, s32[8]{0:T(128)}, u32[]{:S(2)}) copy-start(s32[8]{0:T(128)} %constant.289.clone) | copy-start | bytes 100
  6.6 58.7 %copy-start.8 = (bf16[4,128,2,128]{3,2,1,0:T(2,128)(2,1)S(1)}, bf16[4,128,2,128]{3,2,1,0:T(2,128)(2,1)}, u32[]{:S(2)}) copy-start(bf16[4,128,2,128]{3,2,1,0:T(2,128)(2,1)} %param.20) | copy-start | bytes 786436
  6.6 203.9 %all-gather.3.cloned.1.call-start = ((), (), s32[]{:S(2)}) async-start(), calls=%async_computation | async-start | bytes 9437184 | tf_op jit(solution)/shard_map/all_gather | solution.py:229
  7.3 213.3 %all-gather.5.cloned.1.call-start = ((), (), s32[]{:S(2)}) async-start(), calls=%async_computation.1 | async-start | bytes 9437184 | tf_op jit(solution)/shard_map/all_gather | solution.py:230
  7.4 21.7 %collective-permute-start = (bf16[4,128,768]{2,1,0:T(8,128)(2,1)}, bf16[4,128,768]{2,1,0:T(8,128)(2,1)}, u32[]{:S(2)}, u32[]{:S(2)}) collective-permute-start(bf16[4,128,768]{2,1,0:T(8,128)(2,1)} %param.15), channel_id=1, source_target_pairs={{0,2},{2,4},{4,6},{6,7},{7,5},{5,3},{3,1},{1,0},{8,10},{10,12},{12... | collective-permute-start | bytes 2359304 | tf_op jit(solution)/shard_map/ppermute | solution.py:34
  10.4 53.3 %collective-permute-start.4 = (bf16[4,128,768]{2,1,0:T(8,128)(2,1)}, bf16[4,128,768]{2,1,0:T(8,128)(2,1)}, u32[]{:S(2)}, u32[]{:S(2)}) collective-permute-start(bf16[4,128,768]{2,1,0:T(8,128)(2,1)} %param.15), channel_id=1, source_target_pairs={{0,1},{2,0},{4,2},{6,4},{7,6},{5,7},{3,5},{1,3},{8,9},{10,8},{12,1... | collective-permute-start | bytes 2359304 | tf_op jit(solution)/shard_map/ppermute | solution.py:38
  10.5 92.7 %copy-start.5 = (bf16[128,3072]{1,0:T(8,128)(2,1)}, bf16[128,3072]{1,0:T(8,128)(2,1)S(1)}, u32[]{:S(2)}) copy-start(bf16[128,3072]{1,0:T(8,128)(2,1)S(1)} %constant_dynamic-slice_fusion.2.refs_8_) | copy-start | bytes 2359300
  10.5 93.7 %collective-permute-start.14 = (bf16[128,3072]{1,0:T(8,128)(2,1)S(1)}, bf16[128,3072]{1,0:T(8,128)(2,1)}, u32[]{:S(2)}, u32[]{:S(2)}) collective-permute-start(bf16[128,3072]{1,0:T(8,128)(2,1)S(1)} %constant_dynamic-slice_fusion.2.refs_8_), channel_id=1, source_target_pairs={{0,2},{2,4},{4,6},{6,7},{7,5},{5,3},{3,1},{1,0},{8,10},{10,12},{12... | collective-permute-start | bytes 2359304 | tf_op jit(solution)/shard_map/ppermute | solution.py:34
  12.6 97.4 %collective-permute-start.18 = (bf16[128,3072]{1,0:T(8,128)(2,1)S(1)}, bf16[128,3072]{1,0:T(8,128)(2,1)}, u32[]{:S(2)}, u32[]{:S(2)}) collective-permute-start(bf16[128,3072]{1,0:T(8,128)(2,1)S(1)} %constant_dynamic-slice_fusion.2.refs_8_), channel_id=1, source_target_pairs={{0,1},{2,0},{4,2},{6,4},{7,6},{5,7},{3,5},{1,3},{8,9},{10,8},{12,1... | collective-permute-start | bytes 2359304 | tf_op jit(solution)/shard_map/ppermute | solution.py:38
  12.6 130.7 %collective-permute-start.21 = (bf16[128,3072]{1,0:T(8,128)(2,1)S(1)}, bf16[128,3072]{1,0:T(8,128)(2,1)}, u32[]{:S(2)}, u32[]{:S(2)}) collective-permute-start(bf16[128,3072]{1,0:T(8,128)(2,1)S(1)} %constant_dynamic-slice_fusion.2.refs_8_), channel_id=1, source_target_pairs={{0,8},{8,0},{1,9},{9,1},{2,10},{10,2},{3,11},{11,3},{4,12},{12,4},... | collective-permute-start | bytes 2359304 | tf_op jit(solution)/shard_map/ppermute | solution.py:227
  29.1 32.8 %collective-permute-start.1 = (bf16[4,128,768]{2,1,0:T(8,128)(2,1)}, bf16[4,128,768]{2,1,0:T(8,128)(2,1)S(1)}, u32[]{:S(2)}, u32[]{:S(2)}) collective-permute-start(bf16[4,128,768]{2,1,0:T(8,128)(2,1)} %collective-permute-done), channel_id=1, source_target_pairs={{0,2},{2,4},{4,6},{6,7},{7,5},{5,3},{3,1},{1,0},{8,10},{10,12},{12... | collective-permute-start | bytes 2359304 | tf_op jit(solution)/shard_map/ppermute | solution.py:34
  61.8 18.8 %collective-permute-start.2 = (bf16[4,128,768]{2,1,0:T(8,128)(2,1)S(1)}, bf16[4,128,768]{2,1,0:T(8,128)(2,1)}, u32[]{:S(2)}, u32[]{:S(2)}) collective-permute-start(bf16[4,128,768]{2,1,0:T(8,128)(2,1)S(1)} %collective-permute-done.1), channel_id=1, source_target_pairs={{0,2},{2,4},{4,6},{6,7},{7,5},{5,3},{3,1},{1,0},{8,10},{10,12},{12... | collective-permute-start | bytes 2359304 | tf_op jit(solution)/shard_map/ppermute | solution.py:34
  63.7 42.1 %collective-permute-start.5 = (bf16[4,128,768]{2,1,0:T(8,128)(2,1)}, bf16[4,128,768]{2,1,0:T(8,128)(2,1)}, u32[]{:S(2)}, u32[]{:S(2)}) collective-permute-start(bf16[4,128,768]{2,1,0:T(8,128)(2,1)} %collective-permute-done.4), channel_id=1, source_target_pairs={{0,1},{2,0},{4,2},{6,4},{7,6},{5,7},{3,5},{1,3},{8,9},{10,8},{12,1... | collective-permute-start | bytes 2359304 | tf_op jit(solution)/shard_map/ppermute | solution.py:38
  80.7 29.4 %collective-permute-start.3 = (bf16[4,128,768]{2,1,0:T(8,128)(2,1)}, bf16[4,128,768]{2,1,0:T(8,128)(2,1)}, u32[]{:S(2)}, u32[]{:S(2)}) collective-permute-start(bf16[4,128,768]{2,1,0:T(8,128)(2,1)} %collective-permute-done.2), channel_id=1, source_target_pairs={{0,2},{2,4},{4,6},{6,7},{7,5},{5,3},{3,1},{1,0},{8,10},{10,12},{12... | collective-permute-start | bytes 2359304 | tf_op jit(solution)/shard_map/ppermute | solution.py:34
  104.2 17.6 %collective-permute-start.15 = (bf16[128,3072]{1,0:T(8,128)(2,1)}, bf16[128,3072]{1,0:T(8,128)(2,1)}, u32[]{:S(2)}, u32[]{:S(2)}) collective-permute-start(bf16[128,3072]{1,0:T(8,128)(2,1)} %collective-permute-done.14.refs_9_), channel_id=1, source_target_pairs={{0,2},{2,4},{4,6},{6,7},{7,5},{5,3},{3,1},{1,0},{8,10},{10,12},{12... | collective-permute-start | bytes 2359304 | tf_op jit(solution)/shard_map/ppermute | solution.py:34
  105.9 20.7 %collective-permute-start.6 = (bf16[4,128,768]{2,1,0:T(8,128)(2,1)}, bf16[4,128,768]{2,1,0:T(8,128)(2,1)S(1)}, u32[]{:S(2)}, u32[]{:S(2)}) collective-permute-start(bf16[4,128,768]{2,1,0:T(8,128)(2,1)} %collective-permute-done.5), channel_id=1, source_target_pairs={{0,1},{2,0},{4,2},{6,4},{7,6},{5,7},{3,5},{1,3},{8,9},{10,8},{12,1... | collective-permute-start | bytes 2359304 | tf_op jit(solution)/shard_map/ppermute | solution.py:38
  110.0 34.0 %collective-permute-start.22 = (bf16[128,3072]{1,0:T(8,128)(2,1)}, bf16[128,3072]{1,0:T(8,128)(2,1)}, u32[]{:S(2)}, u32[]{:S(2)}) collective-permute-start(bf16[128,3072]{1,0:T(8,128)(2,1)} %collective-permute-done.14.refs_9_), channel_id=1, source_target_pairs={{0,8},{8,0},{1,9},{9,1},{2,10},{10,2},{3,11},{11,3},{4,12},{12,4},... | collective-permute-start | bytes 2359304 | tf_op jit(solution)/shard_map/ppermute | solution.py:227
  110.1 33.4 %collective-permute-start.19 = (bf16[128,3072]{1,0:T(8,128)(2,1)}, bf16[128,3072]{1,0:T(8,128)(2,1)}, u32[]{:S(2)}, u32[]{:S(2)}) collective-permute-start(bf16[128,3072]{1,0:T(8,128)(2,1)} %collective-permute-done.18.refs_13_), channel_id=1, source_target_pairs={{0,1},{2,0},{4,2},{6,4},{7,6},{5,7},{3,5},{1,3},{8,9},{10,8},{12,1... | collective-permute-start | bytes 2359304 | tf_op jit(solution)/shard_map/ppermute | solution.py:38
  121.8 25.2 %collective-permute-start.26 = (bf16[128,3072]{1,0:T(8,128)(2,1)}, bf16[128,3072]{1,0:T(8,128)(2,1)}, u32[]{:S(2)}, u32[]{:S(2)}) collective-permute-start(bf16[128,3072]{1,0:T(8,128)(2,1)} %collective-permute-done.18.refs_13_), channel_id=1, source_target_pairs={{0,8},{8,0},{1,9},{9,1},{2,10},{10,2},{3,11},{11,3},{4,12},{12,4},... | collective-permute-start | bytes 2359304 | tf_op jit(solution)/shard_map/ppermute | solution.py:227
  126.5 17.5 %collective-permute-start.16 = (bf16[128,3072]{1,0:T(8,128)(2,1)}, bf16[128,3072]{1,0:T(8,128)(2,1)}, u32[]{:S(2)}, u32[]{:S(2)}) collective-permute-start(bf16[128,3072]{1,0:T(8,128)(2,1)} %collective-permute-done.15.refs_10_), channel_id=1, source_target_pairs={{0,2},{2,4},{4,6},{6,7},{7,5},{5,3},{3,1},{1,0},{8,10},{10,12},{12... | collective-permute-start | bytes 2359304 | tf_op jit(solution)/shard_map/ppermute | solution.py:34
  143.3 21.4 %collective-permute-start.23 = (bf16[128,3072]{1,0:T(8,128)(2,1)}, bf16[128,3072]{1,0:T(8,128)(2,1)S(1)}, u32[]{:S(2)}, u32[]{:S(2)}) collective-permute-start(bf16[128,3072]{1,0:T(8,128)(2,1)} %collective-permute-done.15.refs_10_), channel_id=1, source_target_pairs={{0,8},{8,0},{1,9},{9,1},{2,10},{10,2},{3,11},{11,3},{4,12},{12,4},... | collective-permute-start | bytes 2359304 | tf_op jit(solution)/shard_map/ppermute | solution.py:227
  143.5 20.0 %collective-permute-start.20 = (bf16[128,3072]{1,0:T(8,128)(2,1)}, bf16[128,3072]{1,0:T(8,128)(2,1)S(1)}, u32[]{:S(2)}, u32[]{:S(2)}) collective-permute-start(bf16[128,3072]{1,0:T(8,128)(2,1)} %collective-permute-done.19.refs_14_), channel_id=1, source_target_pairs={{0,1},{2,0},{4,2},{6,4},{7,6},{5,7},{3,5},{1,3},{8,9},{10,8},{12,1... | collective-permute-start | bytes 2359304 | tf_op jit(solution)/shard_map/ppermute | solution.py:38
  144.0 22.4 %collective-permute-start.27 = (bf16[128,3072]{1,0:T(8,128)(2,1)}, bf16[128,3072]{1,0:T(8,128)(2,1)}, u32[]{:S(2)}, u32[]{:S(2)}) collective-permute-start(bf16[128,3072]{1,0:T(8,128)(2,1)} %collective-permute-done.19.refs_14_), channel_id=1, source_target_pairs={{0,8},{8,0},{1,9},{9,1},{2,10},{10,2},{3,11},{11,3},{4,12},{12,4},... | collective-permute-start | bytes 2359304 | tf_op jit(solution)/shard_map/ppermute | solution.py:227
  144.1 20.2 %collective-permute-start.17 = (bf16[128,3072]{1,0:T(8,128)(2,1)}, bf16[128,3072]{1,0:T(8,128)(2,1)}, u32[]{:S(2)}, u32[]{:S(2)}) collective-permute-start(bf16[128,3072]{1,0:T(8,128)(2,1)} %collective-permute-done.16.refs_11_), channel_id=1, source_target_pairs={{0,2},{2,4},{4,6},{6,7},{7,5},{5,3},{3,1},{1,0},{8,10},{10,12},{12... | collective-permute-start | bytes 2359304 | tf_op jit(solution)/shard_map/ppermute | solution.py:34
  147.0 36.1 %collective-permute-start.24 = (bf16[128,3072]{1,0:T(8,128)(2,1)}, bf16[128,3072]{1,0:T(8,128)(2,1)}, u32[]{:S(2)}, u32[]{:S(2)}) collective-permute-start(bf16[128,3072]{1,0:T(8,128)(2,1)} %collective-permute-done.16.refs_11_), channel_id=1, source_target_pairs={{0,8},{8,0},{1,9},{9,1},{2,10},{10,2},{3,11},{11,3},{4,12},{12,4},... | collective-permute-start | bytes 2359304 | tf_op jit(solution)/shard_map/ppermute | solution.py:227
  163.6 19.5 %collective-permute-start.28 = (bf16[128,3072]{1,0:T(8,128)(2,1)S(1)}, bf16[128,3072]{1,0:T(8,128)(2,1)}, u32[]{:S(2)}, u32[]{:S(2)}) collective-permute-start(bf16[128,3072]{1,0:T(8,128)(2,1)S(1)} %collective-permute-done.20.refs_15_), channel_id=1, source_target_pairs={{0,8},{8,0},{1,9},{9,1},{2,10},{10,2},{3,11},{11,3},{4,12},{12,4},... | collective-permute-start | bytes 2359304 | tf_op jit(solution)/shard_map/ppermute | solution.py:227
  164.3 21.5 %collective-permute-start.25 = (bf16[128,3072]{1,0:T(8,128)(2,1)}, bf16[128,3072]{1,0:T(8,128)(2,1)}, u32[]{:S(2)}, u32[]{:S(2)}) collective-permute-start(bf16[128,3072]{1,0:T(8,128)(2,1)} %collective-permute-done.17.refs_12_), channel_id=1, source_target_pairs={{0,8},{8,0},{1,9},{9,1},{2,10},{10,2},{3,11},{11,3},{4,12},{12,4},... | collective-permute-start | bytes 2359304 | tf_op jit(solution)/shard_map/ppermute | solution.py:227
  164.8 6.0 %collective-permute-start.7 = (bf16[512,128]{1,0:T(8,128)(2,1)S(1)}, bf16[512,128]{1,0:T(8,128)(2,1)S(1)}, u32[]{:S(2)}, u32[]{:S(2)}) collective-permute-start(bf16[512,128]{1,0:T(8,128)(2,1)S(1)} %bitcast.163), channel_id=1, source_target_pairs={{0,2},{2,4},{4,6},{6,7},{7,5},{5,3},{3,1},{1,0},{8,10},{10,12},{12... | collective-permute-start | bytes 393224 | tf_op jit(solution)/shard_map/ppermute | solution.py:34
  166.4 5.9 %collective-permute-start.11 = (bf16[512,128]{1,0:T(8,128)(2,1)S(1)}, bf16[512,128]{1,0:T(8,128)(2,1)S(1)}, u32[]{:S(2)}, u32[]{:S(2)}) collective-permute-start(bf16[512,128]{1,0:T(8,128)(2,1)S(1)} %bitcast.164), channel_id=1, source_target_pairs={{0,1},{2,0},{4,2},{6,4},{7,6},{5,7},{3,5},{1,3},{8,9},{10,8},{12,1... | collective-permute-start | bytes 393224 | tf_op jit(solution)/shard_map/ppermute | solution.py:38
  170.7 5.1 %collective-permute-start.8 = (bf16[512,128]{1,0:T(8,128)(2,1)S(1)}, bf16[512,128]{1,0:T(8,128)(2,1)S(1)}, u32[]{:S(2)}, u32[]{:S(2)}) collective-permute-start(bf16[512,128]{1,0:T(8,128)(2,1)S(1)} %collective-permute-done.7.refs_1_), channel_id=1, source_target_pairs={{0,2},{2,4},{4,6},{6,7},{7,5},{5,3},{3,1},{1,0},{8,10},{10,12},{12... | collective-permute-start | bytes 393224 | tf_op jit(solution)/shard_map/ppermute | solution.py:34
  172.3 5.1 %collective-permute-start.12 = (bf16[512,128]{1,0:T(8,128)(2,1)S(1)}, bf16[512,128]{1,0:T(8,128)(2,1)S(1)}, u32[]{:S(2)}, u32[]{:S(2)}) collective-permute-start(bf16[512,128]{1,0:T(8,128)(2,1)S(1)} %collective-permute-done.11.refs_5_), channel_id=1, source_target_pairs={{0,1},{2,0},{4,2},{6,4},{7,6},{5,7},{3,5},{1,3},{8,9},{10,8},{12,1... | collective-permute-start | bytes 393224 | tf_op jit(solution)/shard_map/ppermute | solution.py:38
  175.9 5.0 %collective-permute-start.9 = (bf16[512,128]{1,0:T(8,128)(2,1)S(1)}, bf16[512,128]{1,0:T(8,128)(2,1)S(1)}, u32[]{:S(2)}, u32[]{:S(2)}) collective-permute-start(bf16[512,128]{1,0:T(8,128)(2,1)S(1)} %collective-permute-done.8.refs_2_), channel_id=1, source_target_pairs={{0,2},{2,4},{4,6},{6,7},{7,5},{5,3},{3,1},{1,0},{8,10},{10,12},{12... | collective-permute-start | bytes 393224 | tf_op jit(solution)/shard_map/ppermute | solution.py:34
  177.4 5.7 %collective-permute-start.13 = (bf16[512,128]{1,0:T(8,128)(2,1)S(1)}, bf16[512,128]{1,0:T(8,128)(2,1)S(1)}, u32[]{:S(2)}, u32[]{:S(2)}) collective-permute-start(bf16[512,128]{1,0:T(8,128)(2,1)S(1)} %collective-permute-done.12.refs_6_), channel_id=1, source_target_pairs={{0,1},{2,0},{4,2},{6,4},{7,6},{5,7},{3,5},{1,3},{8,9},{10,8},{12,1... | collective-permute-start | bytes 393224 | tf_op jit(solution)/shard_map/ppermute | solution.py:38
  180.8 5.0 %collective-permute-start.10 = (bf16[512,128]{1,0:T(8,128)(2,1)S(1)}, bf16[512,128]{1,0:T(8,128)(2,1)S(1)}, u32[]{:S(2)}, u32[]{:S(2)}) collective-permute-start(bf16[512,128]{1,0:T(8,128)(2,1)S(1)} %collective-permute-done.9.refs_3_), channel_id=1, source_target_pairs={{0,2},{2,4},{4,6},{6,7},{7,5},{5,3},{3,1},{1,0},{8,10},{10,12},{12... | collective-permute-start | bytes 393224 | tf_op jit(solution)/shard_map/ppermute | solution.py:34
  229.9 7.8 %collective-permute-start.29 = (bf16[512,384]{1,0:T(8,128)(2,1)S(1)}, bf16[512,384]{1,0:T(8,128)(2,1)S(1)}, u32[]{:S(2)}, u32[]{:S(2)}) collective-permute-start(bf16[512,384]{1,0:T(8,128)(2,1)S(1)} %get-tuple-element.23), channel_id=1, source_target_pairs={{0,2},{2,4},{4,6},{6,7},{7,5},{5,3},{3,1},{1,0},{8,10},{10,12},{12... | collective-permute-start | bytes 1179656 | tf_op jit(solution)/shard_map/ppermute | solution.py:61
  231.5 7.8 %collective-permute-start.36 = (bf16[512,384]{1,0:T(8,128)(2,1)S(1)}, bf16[512,384]{1,0:T(8,128)(2,1)S(1)}, u32[]{:S(2)}, u32[]{:S(2)}) collective-permute-start(bf16[512,384]{1,0:T(8,128)(2,1)S(1)} %get-tuple-element.24), channel_id=1, source_target_pairs={{0,1},{2,0},{4,2},{6,4},{7,6},{5,7},{3,5},{1,3},{8,9},{10,8},{12,1... | collective-permute-start | bytes 1179656 | tf_op jit(solution)/shard_map/ppermute | solution.py:63
  240.6 9.0 %collective-permute-start.30 = (bf16[512,384]{1,0:T(8,128)(2,1)S(1)}, bf16[512,384]{1,0:T(8,128)(2,1)S(1)}, u32[]{:S(2)}, u32[]{:S(2)}) collective-permute-start(bf16[512,384]{1,0:T(8,128)(2,1)S(1)} %get-tuple-element.21), channel_id=1, source_target_pairs={{0,2},{2,4},{4,6},{6,7},{7,5},{5,3},{3,1},{1,0},{8,10},{10,12},{12... | collective-permute-start | bytes 1179656 | tf_op jit(solution)/shard_map/ppermute | solution.py:61
  242.6 9.6 %collective-permute-start.37 = (bf16[512,384]{1,0:T(8,128)(2,1)S(1)}, bf16[512,384]{1,0:T(8,128)(2,1)S(1)}, u32[]{:S(2)}, u32[]{:S(2)}) collective-permute-start(bf16[512,384]{1,0:T(8,128)(2,1)S(1)} %get-tuple-element.22), channel_id=1, source_target_pairs={{0,1},{2,0},{4,2},{6,4},{7,6},{5,7},{3,5},{1,3},{8,9},{10,8},{12,1... | collective-permute-start | bytes 1179656 | tf_op jit(solution)/shard_map/ppermute | solution.py:63
  253.6 10.8 %collective-permute-start.31 = (bf16[512,384]{1,0:T(8,128)(2,1)S(1)}, bf16[512,384]{1,0:T(8,128)(2,1)S(1)}, u32[]{:S(2)}, u32[]{:S(2)}) collective-permute-start(bf16[512,384]{1,0:T(8,128)(2,1)S(1)} %get-tuple-element.19), channel_id=1, source_target_pairs={{0,2},{2,4},{4,6},{6,7},{7,5},{5,3},{3,1},{1,0},{8,10},{10,12},{12... | collective-permute-start | bytes 1179656 | tf_op jit(solution)/shard_map/ppermute | solution.py:61
  254.5 11.3 %collective-permute-start.38 = (bf16[512,384]{1,0:T(8,128)(2,1)S(1)}, bf16[512,384]{1,0:T(8,128)(2,1)S(1)}, u32[]{:S(2)}, u32[]{:S(2)}) collective-permute-start(bf16[512,384]{1,0:T(8,128)(2,1)S(1)} %get-tuple-element.20), channel_id=1, source_target_pairs={{0,1},{2,0},{4,2},{6,4},{7,6},{5,7},{3,5},{1,3},{8,9},{10,8},{12,1... | collective-permute-start | bytes 1179656 | tf_op jit(solution)/shard_map/ppermute | solution.py:63
  267.1 11.6 %collective-permute-start.32 = (bf16[512,384]{1,0:T(8,128)(2,1)S(1)}, bf16[512,384]{1,0:T(8,128)(2,1)S(1)}, u32[]{:S(2)}, u32[]{:S(2)}) collective-permute-start(bf16[512,384]{1,0:T(8,128)(2,1)S(1)} %get-tuple-element.17), channel_id=1, source_target_pairs={{0,2},{2,4},{4,6},{6,7},{7,5},{5,3},{3,1},{1,0},{8,10},{10,12},{12... | collective-permute-start | bytes 1179656 | tf_op jit(solution)/shard_map/ppermute | solution.py:61
  267.6 11.3 %collective-permute-start.39 = (bf16[512,384]{1,0:T(8,128)(2,1)S(1)}, bf16[512,384]{1,0:T(8,128)(2,1)S(1)}, u32[]{:S(2)}, u32[]{:S(2)}) collective-permute-start(bf16[512,384]{1,0:T(8,128)(2,1)S(1)} %get-tuple-element.18), channel_id=1, source_target_pairs={{0,1},{2,0},{4,2},{6,4},{7,6},{5,7},{3,5},{1,3},{8,9},{10,8},{12,1... | collective-permute-start | bytes 1179656 | tf_op jit(solution)/shard_map/ppermute | solution.py:63
  280.2 10.6 %collective-permute-start.33 = (bf16[512,384]{1,0:T(8,128)(2,1)S(1)}, bf16[512,384]{1,0:T(8,128)(2,1)S(1)}, u32[]{:S(2)}, u32[]{:S(2)}) collective-permute-start(bf16[512,384]{1,0:T(8,128)(2,1)S(1)} %get-tuple-element.15), channel_id=1, source_target_pairs={{0,2},{2,4},{4,6},{6,7},{7,5},{5,3},{3,1},{1,0},{8,10},{10,12},{12... | collective-permute-start | bytes 1179656 | tf_op jit(solution)/shard_map/ppermute | solution.py:61
  280.6 10.5 %collective-permute-start.40 = (bf16[512,384]{1,0:T(8,128)(2,1)S(1)}, bf16[512,384]{1,0:T(8,128)(2,1)S(1)}, u32[]{:S(2)}, u32[]{:S(2)}) collective-permute-start(bf16[512,384]{1,0:T(8,128)(2,1)S(1)} %get-tuple-element.16), channel_id=1, source_target_pairs={{0,1},{2,0},{4,2},{6,4},{7,6},{5,7},{3,5},{1,3},{8,9},{10,8},{12,1... | collective-permute-start | bytes 1179656 | tf_op jit(solution)/shard_map/ppermute | solution.py:63
  292.4 10.6 %collective-permute-start.34 = (bf16[512,384]{1,0:T(8,128)(2,1)S(1)}, bf16[512,384]{1,0:T(8,128)(2,1)S(1)}, u32[]{:S(2)}, u32[]{:S(2)}) collective-permute-start(bf16[512,384]{1,0:T(8,128)(2,1)S(1)} %get-tuple-element.13), channel_id=1, source_target_pairs={{0,2},{2,4},{4,6},{6,7},{7,5},{5,3},{3,1},{1,0},{8,10},{10,12},{12... | collective-permute-start | bytes 1179656 | tf_op jit(solution)/shard_map/ppermute | solution.py:61
  292.8 10.4 %collective-permute-start.41 = (bf16[512,384]{1,0:T(8,128)(2,1)S(1)}, bf16[512,384]{1,0:T(8,128)(2,1)}, u32[]{:S(2)}, u32[]{:S(2)}) collective-permute-start(bf16[512,384]{1,0:T(8,128)(2,1)S(1)} %get-tuple-element.14), channel_id=1, source_target_pairs={{0,1},{2,0},{4,2},{6,4},{7,6},{5,7},{3,5},{1,3},{8,9},{10,8},{12,1... | collective-permute-start | bytes 1179656 | tf_op jit(solution)/shard_map/ppermute | solution.py:63
  305.4 8.0 %collective-permute-start.35 = (bf16[512,384]{1,0:T(8,128)(2,1)}, bf16[512,384]{1,0:T(8,128)(2,1)S(1)}, u32[]{:S(2)}, u32[]{:S(2)}) collective-permute-start(bf16[512,384]{1,0:T(8,128)(2,1)} %get-tuple-element.11), channel_id=1, source_target_pairs={{0,2},{2,4},{4,6},{6,7},{7,5},{5,3},{3,1},{1,0},{8,10},{10,12},{12... | collective-permute-start | bytes 1179656 | tf_op jit(solution)/shard_map/ppermute | solution.py:61
  306.7 7.9 %collective-permute-start.42 = (bf16[512,384]{1,0:T(8,128)(2,1)S(1)}, bf16[512,384]{1,0:T(8,128)(2,1)}, u32[]{:S(2)}, u32[]{:S(2)}) collective-permute-start(bf16[512,384]{1,0:T(8,128)(2,1)S(1)} %get-tuple-element.12), channel_id=1, source_target_pairs={{0,1},{2,0},{4,2},{6,4},{7,6},{5,7},{3,5},{1,3},{8,9},{10,8},{12,1... | collective-permute-start | bytes 1179656 | tf_op jit(solution)/shard_map/ppermute | solution.py:63
  (23 other events, 365.7 us)
Sparse Core Ops, SparseCore 0:
  8.9 18.3 all-gather.2
  28.9 17.9 all-gather.4

commit v15 on v14

--- a/solution.py
+++ b/solution.py
@@ -104,7 +104,7 @@
 
 
 def grouped_out_proj(
-    span_index, att_blocks, mine_blocks, other_blocks, hidden, scale, tile_width=512
+    span_index, att_blocks, mine_blocks, other_blocks, hidden, scale, tile_width=1024
 ):
     group_count = len(att_blocks)
     token_count, head_width = att_blocks[0].shape

time: 327 us -> 326 us (level)
  no operation moved by 1% of the time
where the time goes in v15:
time: 326 us; the launch traced here: 325 us
  waiting for transfers between devices  159 us (49%)
  starting transfers between devices  40 us (12%)
  between operations  32.8 us (10%)
  matrix products  24.9 us (8%)
  local copies, waits for them, and re-layouts  21.6 us (7%)
  Pallas kernels  21.6 us (7%)
  other arithmetic  20 us (6%)
  blocking collectives  4.54 us (1%)
    ppermute x12, waiting for transfers between devices, ring_gather(): forward = lax.ppermute(forward, axis_name, ahead)  78.7 us
    ppermute x7, waiting for transfers between devices, ring_reduce_scatter(): lax.ppermute(forward.astype(jnp.bfloat16), axis_name, ahead)  51.2 us
    pallas_call x1, Pallas kernels, grouped_out_proj(): pl.pallas_call(functools.partial(out_proj_kernel, group_count, tiles_per_...  21.6 us
    ppermute x12, starting transfers between devices, ring_gather(): forward = lax.ppermute(forward, axis_name, ahead)  21.6 us
    ppermute x9, waiting for transfers between devices, ring_gather(): backward = lax.ppermute(backward, axis_name, behind)  21.1 us
    unnamed x59, local copies, waits for them, and re-layouts  10.3 us
    dot_general x1, matrix products, local(): pre_act = jnp.dot(mlp_in, up_full, preferred_element_type=jnp.float32)  10 us
    convert_element_type x6, other arithmetic, ring_reduce_scatter(): forward.astype(jnp.bfloat16)  8.73 us
  transfers between devices with their start and end apart: 45, of which 25 were waited for; matrix products, arithmetic and copies ran while one was open for 13% of the time, Pallas kernels for 7%

profile of v15, /device:TPU:0, one launch (start us, length us, event | category | flops | bytes accessed | tf_op | source)
XLA Modules:
  0.0 324.5 jit_solution(3013180674996683208)
XLA Ops:
  7.4 3.1 collective-permute-start
  10.5 2.1 collective-permute-start.14
  14.4 14.6 %collective-permute-done = bf16[4,128,768]{2,1,0:T(8,128)(2,1)} collective-permute-done((bf16[4,128,768]{2,1,0:T(8,128)(2,1)}, bf16[4,128,768]{2,1,0:T(8,128)(2,1)}, u32[]{:S(2)}, u32[]{:S(2)}) %collective-permute-start) | collective-permute-done | bytes 786464 | tf_op jit(solution)/shard_map/ppermute | solution.py:34
  29.1 2.1 collective-permute-start.1
  31.5 30.3 %collective-permute-done.1 = bf16[4,128,768]{2,1,0:T(8,128)(2,1)S(1)} collective-permute-done((bf16[4,128,768]{2,1,0:T(8,128)(2,1)}, bf16[4,128,768]{2,1,0:T(8,128)(2,1)S(1)}, u32[]{:S(2)}, u32[]{:S(2)}) %collective-permute-start.1) | collective-permute-done | bytes 786464 | tf_op jit(solution)/shard_map/ppermute | solution.py:34
  61.8 1.8 collective-permute-start.2
  65.4 2.2 all_gather.12
  67.6 13.1 %collective-permute-done.2 = bf16[4,128,768]{2,1,0:T(8,128)(2,1)} collective-permute-done((bf16[4,128,768]{2,1,0:T(8,128)(2,1)S(1)}, bf16[4,128,768]{2,1,0:T(8,128)(2,1)}, u32[]{:S(2)}, u32[]{:S(2)}) %collective-permute-start.2) | collective-permute-done | bytes 786464 | tf_op jit(solution)/shard_map/ppermute | solution.py:34
  80.7 1.5 collective-permute-start.3
  96.5 6.7 %copy.30 = bf16[6144,3,128]{0,2,1:T(8,128)(2,1)} copy(bf16[6144,3,128]{2,0,1:T(8,128)(2,1)} %param.22) | data formatting | bytes 9437184 | tf_op args[7]
  104.2 1.6 collective-permute-start.15
  114.4 7.4 %collective-permute-done.15.refs_10_ = bf16[128,3072]{1,0:T(8,128)(2,1)} collective-permute-done((bf16[128,3072]{1,0:T(8,128)(2,1)}, bf16[128,3072]{1,0:T(8,128)(2,1)}, u32[]{:S(2)}, u32[]{:S(2)}) %collective-permute-start.15) | collective-permute-done | bytes 786464 | tf_op jit(solution)/shard_map/ppermute | solution.py:34
  121.8 4.7 %collective-permute-done.6 = bf16[4,128,768]{2,1,0:T(8,128)(2,1)S(1)} collective-permute-done((bf16[4,128,768]{2,1,0:T(8,128)(2,1)}, bf16[4,128,768]{2,1,0:T(8,128)(2,1)S(1)}, u32[]{:S(2)}, u32[]{:S(2)}) %collective-permute-start.6) | collective-permute-done | bytes 786464 | tf_op jit(solution)/shard_map/ppermute | solution.py:38
  126.5 1.6 collective-permute-start.16
  129.5 2.7 fusion.3
  132.3 5.8 %convolution_convert_fusion.1 = bf16[512,384]{1,0:T(8,128)(2,1)S(1)} fusion(bf16[512,6144]{1,0:T(8,128)(2,1)S(1)} %bitcast.152, bf16[6144,384]{0,1:T(8,128)(2,1)} %bitcast.153), kind=kOutput, calls=%fused_computation.27 | convolution fusion | flops 2416115712 | bytes 11403264 | tf_op jit(solution)/shard_map/dot_general | solution.py:243
  138.9 2.4 all_gather.13
  144.1 1.6 collective-permute-start.17
  147.2 16.3 %collective-permute-done.20.refs_15_ = bf16[128,3072]{1,0:T(8,128)(2,1)S(1)} collective-permute-done((bf16[128,3072]{1,0:T(8,128)(2,1)}, bf16[128,3072]{1,0:T(8,128)(2,1)S(1)}, u32[]{:S(2)}, u32[]{:S(2)}) %collective-permute-start.20) | collective-permute-done | bytes 786464 | tf_op jit(solution)/shard_map/ppermute | solution.py:38
  164.8 1.6 collective-permute-start.7
  166.9 3.9 %collective-permute-done.7.refs_1_ = bf16[512,128]{1,0:T(8,128)(2,1)S(1)} collective-permute-done((bf16[512,128]{1,0:T(8,128)(2,1)S(1)}, bf16[512,128]{1,0:T(8,128)(2,1)S(1)}, u32[]{:S(2)}, u32[]{:S(2)}) %collective-permute-start.7) | collective-permute-done | bytes 131104 | tf_op jit(solution)/shard_map/ppermute | solution.py:34
  170.7 1.6 collective-permute-start.8
  172.8 3.1 collective-permute-done.8.refs_2_
  175.9 1.5 collective-permute-start.9
  177.9 2.9 collective-permute-done.9.refs_3_
  180.8 1.5 collective-permute-start.10
  183.1 2.7 collective-permute-done.10.refs_4_
  186.5 21.6 %shard_map.145 = (f32[512,6144]{1,0:T(8,128)}, f32[512,128]{1,0:T(8,128)}) custom-call(s32[1]{0:T(128)} %bitcast.span_ref, bf16[512,128]{1,0:T(8,128)(2,1)} %bitcast.165, bf16[512,128]{1,0:T(8,128)(2,1)} %copy-done.17, bf16[512,128]{1,0:T(8,128)(2,1)} %copy-done.19, bf16[512,128]{1,0:T(8,128)(2,1)} %copy-done.21, bf16[512,128]{1,0:T(8,128)(2,1)} %copy-done.23, ...), custom_call_target="tpu_custom_call" | custom-call | flops 6442450944 | bytes 32505856 | tf_op jit(solution)/shard_map/pallas_call | solution.py:134
  209.3 10.0 %fusion.27 = bf16[4,128,512]{2,1,0:T(8,128)(2,1)S(1)} fusion(bf16[6144,512]{1,0:T(8,128)(2,1)} %all-gather.3.cloned.1.call-done, f32[4,128,6144]{2,1,0:T(8,128)} %bitcast.158, f32[4,6144]{1,0:T(4,128)S(1)} %copy-done.11, f32[4,6144]{1,0:T(4,128)S(1)} %copy-done.10, f32[4,128]{1,0:T(4,128)S(1)} %bitcast.162), kind=kOutput, calls=%fused_computation.38 | convolution fusion | flops 3236167680 | bytes 19597312 | tf_op jit(solution)/shard_map/dot_general | solution.py:296
  219.3 6.6 %convolution_convert_fusion = bf16[4,128,6144]{2,1,0:T(8,128)(2,1)S(1)} fusion(bf16[4,128,512]{2,1,0:T(8,128)(2,1)S(1)} %fusion.27, bf16[512,6144]{1,0:T(8,128)(2,1)} %all-gather.5.cloned.1.call-done), kind=kOutput, calls=%fused_computation.7 | convolution fusion | flops 3224371200 | bytes 13107200 | tf_op jit(solution)/shard_map/dot_general | solution.py:298
  225.9 2.6 copy-done.3
  228.6 1.6 collective-permute-start.29
  231.9 4.6 %collective-permute-done.29 = bf16[512,384]{1,0:T(8,128)(2,1)S(1)} collective-permute-done((bf16[512,384]{1,0:T(8,128)(2,1)S(1)}, bf16[512,384]{1,0:T(8,128)(2,1)S(1)}, u32[]{:S(2)}, u32[]{:S(2)}) %collective-permute-start.29) | collective-permute-done | bytes 393248 | tf_op jit(solution)/shard_map/ppermute | solution.py:61
  236.5 1.5 collective-permute-done.36
  239.3 2.1 collective-permute-start.30
  242.8 5.6 %collective-permute-done.30 = bf16[512,384]{1,0:T(8,128)(2,1)S(1)} collective-permute-done((bf16[512,384]{1,0:T(8,128)(2,1)S(1)}, bf16[512,384]{1,0:T(8,128)(2,1)S(1)}, u32[]{:S(2)}, u32[]{:S(2)}) %collective-permute-start.30) | collective-permute-done | bytes 393248 | tf_op jit(solution)/shard_map/ppermute | solution.py:61
  248.4 2.8 collective-permute-done.37
  255.1 8.2 %collective-permute-done.31 = bf16[512,384]{1,0:T(8,128)(2,1)S(1)} collective-permute-done((bf16[512,384]{1,0:T(8,128)(2,1)S(1)}, bf16[512,384]{1,0:T(8,128)(2,1)S(1)}, u32[]{:S(2)}, u32[]{:S(2)}) %collective-permute-start.31) | collective-permute-done | bytes 393248 | tf_op jit(solution)/shard_map/ppermute | solution.py:61
  266.2 1.6 collective-permute-start.39
  267.8 9.6 %collective-permute-done.32 = bf16[512,384]{1,0:T(8,128)(2,1)S(1)} collective-permute-done((bf16[512,384]{1,0:T(8,128)(2,1)S(1)}, bf16[512,384]{1,0:T(8,128)(2,1)S(1)}, u32[]{:S(2)}, u32[]{:S(2)}) %collective-permute-start.32) | collective-permute-done | bytes 393248 | tf_op jit(solution)/shard_map/ppermute | solution.py:61
  279.3 1.7 collective-permute-start.40
  281.0 8.7 %collective-permute-done.33 = bf16[512,384]{1,0:T(8,128)(2,1)S(1)} collective-permute-done((bf16[512,384]{1,0:T(8,128)(2,1)S(1)}, bf16[512,384]{1,0:T(8,128)(2,1)S(1)}, u32[]{:S(2)}, u32[]{:S(2)}) %collective-permute-start.33) | collective-permute-done | bytes 393248 | tf_op jit(solution)/shard_map/ppermute | solution.py:61
  291.5 1.7 collective-permute-start.41
  293.2 8.6 %collective-permute-done.34 = bf16[512,384]{1,0:T(8,128)(2,1)S(1)} collective-permute-done((bf16[512,384]{1,0:T(8,128)(2,1)S(1)}, bf16[512,384]{1,0:T(8,128)(2,1)S(1)}, u32[]{:S(2)}, u32[]{:S(2)}) %collective-permute-start.34) | collective-permute-done | bytes 393248 | tf_op jit(solution)/shard_map/ppermute | solution.py:61
  302.0 2.2 add_convert_fusion.13
  304.2 1.5 collective-permute-start.35
  306.2 6.0 %collective-permute-done.35 = bf16[512,384]{1,0:T(8,128)(2,1)S(1)} collective-permute-done((bf16[512,384]{1,0:T(8,128)(2,1)}, bf16[512,384]{1,0:T(8,128)(2,1)S(1)}, u32[]{:S(2)}, u32[]{:S(2)}) %collective-permute-start.35) | collective-permute-done | bytes 393248 | tf_op jit(solution)/shard_map/ppermute | solution.py:61
  315.1 2.6 add_convert_fusion.2
  (159 shorter events, 40.1 us)
Async XLA Ops:
  6.5 84.1 %copy-start.9 = (s32[8]{0:T(128)S(1)}, s32[8]{0:T(128)}, u32[]{:S(2)}) copy-start(s32[8]{0:T(128)} %constant.289.clone) | copy-start | bytes 100
  6.6 58.7 %copy-start.8 = (bf16[4,128,2,128]{3,2,1,0:T(2,128)(2,1)S(1)}, bf16[4,128,2,128]{3,2,1,0:T(2,128)(2,1)}, u32[]{:S(2)}) copy-start(bf16[4,128,2,128]{3,2,1,0:T(2,128)(2,1)} %param.20) | copy-start | bytes 786436
  6.6 202.7 %all-gather.3.cloned.1.call-start = ((), (), s32[]{:S(2)}) async-start(), calls=%async_computation | async-start | bytes 9437184 | tf_op jit(solution)/shard_map/all_gather | solution.py:229
  7.3 212.0 %all-gather.5.cloned.1.call-start = ((), (), s32[]{:S(2)}) async-start(), calls=%async_computation.1 | async-start | bytes 9437184 | tf_op jit(solution)/shard_map/all_gather | solution.py:230
  7.4 21.7 %collective-permute-start = (bf16[4,128,768]{2,1,0:T(8,128)(2,1)}, bf16[4,128,768]{2,1,0:T(8,128)(2,1)}, u32[]{:S(2)}, u32[]{:S(2)}) collective-permute-start(bf16[4,128,768]{2,1,0:T(8,128)(2,1)} %param.15), channel_id=1, source_target_pairs={{0,2},{2,4},{4,6},{6,7},{7,5},{5,3},{3,1},{1,0},{8,10},{10,12},{12... | collective-permute-start | bytes 2359304 | tf_op jit(solution)/shard_map/ppermute | solution.py:34
  10.4 53.3 %collective-permute-start.4 = (bf16[4,128,768]{2,1,0:T(8,128)(2,1)}, bf16[4,128,768]{2,1,0:T(8,128)(2,1)}, u32[]{:S(2)}, u32[]{:S(2)}) collective-permute-start(bf16[4,128,768]{2,1,0:T(8,128)(2,1)} %param.15), channel_id=1, source_target_pairs={{0,1},{2,0},{4,2},{6,4},{7,6},{5,7},{3,5},{1,3},{8,9},{10,8},{12,1... | collective-permute-start | bytes 2359304 | tf_op jit(solution)/shard_map/ppermute | solution.py:38
  10.5 92.7 %copy-start.5 = (bf16[128,3072]{1,0:T(8,128)(2,1)}, bf16[128,3072]{1,0:T(8,128)(2,1)S(1)}, u32[]{:S(2)}) copy-start(bf16[128,3072]{1,0:T(8,128)(2,1)S(1)} %constant_dynamic-slice_fusion.2.refs_8_) | copy-start | bytes 2359300
  10.5 93.7 %collective-permute-start.14 = (bf16[128,3072]{1,0:T(8,128)(2,1)S(1)}, bf16[128,3072]{1,0:T(8,128)(2,1)}, u32[]{:S(2)}, u32[]{:S(2)}) collective-permute-start(bf16[128,3072]{1,0:T(8,128)(2,1)S(1)} %constant_dynamic-slice_fusion.2.refs_8_), channel_id=1, source_target_pairs={{0,2},{2,4},{4,6},{6,7},{7,5},{5,3},{3,1},{1,0},{8,10},{10,12},{12... | collective-permute-start | bytes 2359304 | tf_op jit(solution)/shard_map/ppermute | solution.py:34
  12.6 97.4 %collective-permute-start.18 = (bf16[128,3072]{1,0:T(8,128)(2,1)S(1)}, bf16[128,3072]{1,0:T(8,128)(2,1)}, u32[]{:S(2)}, u32[]{:S(2)}) collective-permute-start(bf16[128,3072]{1,0:T(8,128)(2,1)S(1)} %constant_dynamic-slice_fusion.2.refs_8_), channel_id=1, source_target_pairs={{0,1},{2,0},{4,2},{6,4},{7,6},{5,7},{3,5},{1,3},{8,9},{10,8},{12,1... | collective-permute-start | bytes 2359304 | tf_op jit(solution)/shard_map/ppermute | solution.py:38
  12.6 130.7 %collective-permute-start.21 = (bf16[128,3072]{1,0:T(8,128)(2,1)S(1)}, bf16[128,3072]{1,0:T(8,128)(2,1)}, u32[]{:S(2)}, u32[]{:S(2)}) collective-permute-start(bf16[128,3072]{1,0:T(8,128)(2,1)S(1)} %constant_dynamic-slice_fusion.2.refs_8_), channel_id=1, source_target_pairs={{0,8},{8,0},{1,9},{9,1},{2,10},{10,2},{3,11},{11,3},{4,12},{12,4},... | collective-permute-start | bytes 2359304 | tf_op jit(solution)/shard_map/ppermute | solution.py:227
  29.1 32.8 %collective-permute-start.1 = (bf16[4,128,768]{2,1,0:T(8,128)(2,1)}, bf16[4,128,768]{2,1,0:T(8,128)(2,1)S(1)}, u32[]{:S(2)}, u32[]{:S(2)}) collective-permute-start(bf16[4,128,768]{2,1,0:T(8,128)(2,1)} %collective-permute-done), channel_id=1, source_target_pairs={{0,2},{2,4},{4,6},{6,7},{7,5},{5,3},{3,1},{1,0},{8,10},{10,12},{12... | collective-permute-start | bytes 2359304 | tf_op jit(solution)/shard_map/ppermute | solution.py:34
  61.8 18.8 %collective-permute-start.2 = (bf16[4,128,768]{2,1,0:T(8,128)(2,1)S(1)}, bf16[4,128,768]{2,1,0:T(8,128)(2,1)}, u32[]{:S(2)}, u32[]{:S(2)}) collective-permute-start(bf16[4,128,768]{2,1,0:T(8,128)(2,1)S(1)} %collective-permute-done.1), channel_id=1, source_target_pairs={{0,2},{2,4},{4,6},{6,7},{7,5},{5,3},{3,1},{1,0},{8,10},{10,12},{12... | collective-permute-start | bytes 2359304 | tf_op jit(solution)/shard_map/ppermute | solution.py:34
  63.7 42.1 %collective-permute-start.5 = (bf16[4,128,768]{2,1,0:T(8,128)(2,1)}, bf16[4,128,768]{2,1,0:T(8,128)(2,1)}, u32[]{:S(2)}, u32[]{:S(2)}) collective-permute-start(bf16[4,128,768]{2,1,0:T(8,128)(2,1)} %collective-permute-done.4), channel_id=1, source_target_pairs={{0,1},{2,0},{4,2},{6,4},{7,6},{5,7},{3,5},{1,3},{8,9},{10,8},{12,1... | collective-permute-start | bytes 2359304 | tf_op jit(solution)/shard_map/ppermute | solution.py:38
  80.7 29.4 %collective-permute-start.3 = (bf16[4,128,768]{2,1,0:T(8,128)(2,1)}, bf16[4,128,768]{2,1,0:T(8,128)(2,1)}, u32[]{:S(2)}, u32[]{:S(2)}) collective-permute-start(bf16[4,128,768]{2,1,0:T(8,128)(2,1)} %collective-permute-done.2), channel_id=1, source_target_pairs={{0,2},{2,4},{4,6},{6,7},{7,5},{5,3},{3,1},{1,0},{8,10},{10,12},{12... | collective-permute-start | bytes 2359304 | tf_op jit(solution)/shard_map/ppermute | solution.py:34
  104.2 17.6 %collective-permute-start.15 = (bf16[128,3072]{1,0:T(8,128)(2,1)}, bf16[128,3072]{1,0:T(8,128)(2,1)}, u32[]{:S(2)}, u32[]{:S(2)}) collective-permute-start(bf16[128,3072]{1,0:T(8,128)(2,1)} %collective-permute-done.14.refs_9_), channel_id=1, source_target_pairs={{0,2},{2,4},{4,6},{6,7},{7,5},{5,3},{3,1},{1,0},{8,10},{10,12},{12... | collective-permute-start | bytes 2359304 | tf_op jit(solution)/shard_map/ppermute | solution.py:34
  105.9 20.7 %collective-permute-start.6 = (bf16[4,128,768]{2,1,0:T(8,128)(2,1)}, bf16[4,128,768]{2,1,0:T(8,128)(2,1)S(1)}, u32[]{:S(2)}, u32[]{:S(2)}) collective-permute-start(bf16[4,128,768]{2,1,0:T(8,128)(2,1)} %collective-permute-done.5), channel_id=1, source_target_pairs={{0,1},{2,0},{4,2},{6,4},{7,6},{5,7},{3,5},{1,3},{8,9},{10,8},{12,1... | collective-permute-start | bytes 2359304 | tf_op jit(solution)/shard_map/ppermute | solution.py:38
  110.0 34.0 %collective-permute-start.22 = (bf16[128,3072]{1,0:T(8,128)(2,1)}, bf16[128,3072]{1,0:T(8,128)(2,1)}, u32[]{:S(2)}, u32[]{:S(2)}) collective-permute-start(bf16[128,3072]{1,0:T(8,128)(2,1)} %collective-permute-done.14.refs_9_), channel_id=1, source_target_pairs={{0,8},{8,0},{1,9},{9,1},{2,10},{10,2},{3,11},{11,3},{4,12},{12,4},... | collective-permute-start | bytes 2359304 | tf_op jit(solution)/shard_map/ppermute | solution.py:227
  110.1 33.4 %collective-permute-start.19 = (bf16[128,3072]{1,0:T(8,128)(2,1)}, bf16[128,3072]{1,0:T(8,128)(2,1)}, u32[]{:S(2)}, u32[]{:S(2)}) collective-permute-start(bf16[128,3072]{1,0:T(8,128)(2,1)} %collective-permute-done.18.refs_13_), channel_id=1, source_target_pairs={{0,1},{2,0},{4,2},{6,4},{7,6},{5,7},{3,5},{1,3},{8,9},{10,8},{12,1... | collective-permute-start | bytes 2359304 | tf_op jit(solution)/shard_map/ppermute | solution.py:38
  121.8 25.2 %collective-permute-start.26 = (bf16[128,3072]{1,0:T(8,128)(2,1)}, bf16[128,3072]{1,0:T(8,128)(2,1)}, u32[]{:S(2)}, u32[]{:S(2)}) collective-permute-start(bf16[128,3072]{1,0:T(8,128)(2,1)} %collective-permute-done.18.refs_13_), channel_id=1, source_target_pairs={{0,8},{8,0},{1,9},{9,1},{2,10},{10,2},{3,11},{11,3},{4,12},{12,4},... | collective-permute-start | bytes 2359304 | tf_op jit(solution)/shard_map/ppermute | solution.py:227
  126.5 17.5 %collective-permute-start.16 = (bf16[128,3072]{1,0:T(8,128)(2,1)}, bf16[128,3072]{1,0:T(8,128)(2,1)}, u32[]{:S(2)}, u32[]{:S(2)}) collective-permute-start(bf16[128,3072]{1,0:T(8,128)(2,1)} %collective-permute-done.15.refs_10_), channel_id=1, source_target_pairs={{0,2},{2,4},{4,6},{6,7},{7,5},{5,3},{3,1},{1,0},{8,10},{10,12},{12... | collective-permute-start | bytes 2359304 | tf_op jit(solution)/shard_map/ppermute | solution.py:34
  143.3 21.4 %collective-permute-start.23 = (bf16[128,3072]{1,0:T(8,128)(2,1)}, bf16[128,3072]{1,0:T(8,128)(2,1)S(1)}, u32[]{:S(2)}, u32[]{:S(2)}) collective-permute-start(bf16[128,3072]{1,0:T(8,128)(2,1)} %collective-permute-done.15.refs_10_), channel_id=1, source_target_pairs={{0,8},{8,0},{1,9},{9,1},{2,10},{10,2},{3,11},{11,3},{4,12},{12,4},... | collective-permute-start | bytes 2359304 | tf_op jit(solution)/shard_map/ppermute | solution.py:227
  143.5 20.0 %collective-permute-start.20 = (bf16[128,3072]{1,0:T(8,128)(2,1)}, bf16[128,3072]{1,0:T(8,128)(2,1)S(1)}, u32[]{:S(2)}, u32[]{:S(2)}) collective-permute-start(bf16[128,3072]{1,0:T(8,128)(2,1)} %collective-permute-done.19.refs_14_), channel_id=1, source_target_pairs={{0,1},{2,0},{4,2},{6,4},{7,6},{5,7},{3,5},{1,3},{8,9},{10,8},{12,1... | collective-permute-start | bytes 2359304 | tf_op jit(solution)/shard_map/ppermute | solution.py:38
  144.0 22.4 %collective-permute-start.27 = (bf16[128,3072]{1,0:T(8,128)(2,1)}, bf16[128,3072]{1,0:T(8,128)(2,1)}, u32[]{:S(2)}, u32[]{:S(2)}) collective-permute-start(bf16[128,3072]{1,0:T(8,128)(2,1)} %collective-permute-done.19.refs_14_), channel_id=1, source_target_pairs={{0,8},{8,0},{1,9},{9,1},{2,10},{10,2},{3,11},{11,3},{4,12},{12,4},... | collective-permute-start | bytes 2359304 | tf_op jit(solution)/shard_map/ppermute | solution.py:227
  144.1 20.2 %collective-permute-start.17 = (bf16[128,3072]{1,0:T(8,128)(2,1)}, bf16[128,3072]{1,0:T(8,128)(2,1)}, u32[]{:S(2)}, u32[]{:S(2)}) collective-permute-start(bf16[128,3072]{1,0:T(8,128)(2,1)} %collective-permute-done.16.refs_11_), channel_id=1, source_target_pairs={{0,2},{2,4},{4,6},{6,7},{7,5},{5,3},{3,1},{1,0},{8,10},{10,12},{12... | collective-permute-start | bytes 2359304 | tf_op jit(solution)/shard_map/ppermute | solution.py:34
  147.0 36.1 %collective-permute-start.24 = (bf16[128,3072]{1,0:T(8,128)(2,1)}, bf16[128,3072]{1,0:T(8,128)(2,1)}, u32[]{:S(2)}, u32[]{:S(2)}) collective-permute-start(bf16[128,3072]{1,0:T(8,128)(2,1)} %collective-permute-done.16.refs_11_), channel_id=1, source_target_pairs={{0,8},{8,0},{1,9},{9,1},{2,10},{10,2},{3,11},{11,3},{4,12},{12,4},... | collective-permute-start | bytes 2359304 | tf_op jit(solution)/shard_map/ppermute | solution.py:227
  163.6 19.5 %collective-permute-start.28 = (bf16[128,3072]{1,0:T(8,128)(2,1)S(1)}, bf16[128,3072]{1,0:T(8,128)(2,1)}, u32[]{:S(2)}, u32[]{:S(2)}) collective-permute-start(bf16[128,3072]{1,0:T(8,128)(2,1)S(1)} %collective-permute-done.20.refs_15_), channel_id=1, source_target_pairs={{0,8},{8,0},{1,9},{9,1},{2,10},{10,2},{3,11},{11,3},{4,12},{12,4},... | collective-permute-start | bytes 2359304 | tf_op jit(solution)/shard_map/ppermute | solution.py:227
  164.3 21.5 %collective-permute-start.25 = (bf16[128,3072]{1,0:T(8,128)(2,1)}, bf16[128,3072]{1,0:T(8,128)(2,1)}, u32[]{:S(2)}, u32[]{:S(2)}) collective-permute-start(bf16[128,3072]{1,0:T(8,128)(2,1)} %collective-permute-done.17.refs_12_), channel_id=1, source_target_pairs={{0,8},{8,0},{1,9},{9,1},{2,10},{10,2},{3,11},{11,3},{4,12},{12,4},... | collective-permute-start | bytes 2359304 | tf_op jit(solution)/shard_map/ppermute | solution.py:227
  164.8 6.0 %collective-permute-start.7 = (bf16[512,128]{1,0:T(8,128)(2,1)S(1)}, bf16[512,128]{1,0:T(8,128)(2,1)S(1)}, u32[]{:S(2)}, u32[]{:S(2)}) collective-permute-start(bf16[512,128]{1,0:T(8,128)(2,1)S(1)} %bitcast.163), channel_id=1, source_target_pairs={{0,2},{2,4},{4,6},{6,7},{7,5},{5,3},{3,1},{1,0},{8,10},{10,12},{12... | collective-permute-start | bytes 393224 | tf_op jit(solution)/shard_map/ppermute | solution.py:34
  166.4 5.9 %collective-permute-start.11 = (bf16[512,128]{1,0:T(8,128)(2,1)S(1)}, bf16[512,128]{1,0:T(8,128)(2,1)S(1)}, u32[]{:S(2)}, u32[]{:S(2)}) collective-permute-start(bf16[512,128]{1,0:T(8,128)(2,1)S(1)} %bitcast.164), channel_id=1, source_target_pairs={{0,1},{2,0},{4,2},{6,4},{7,6},{5,7},{3,5},{1,3},{8,9},{10,8},{12,1... | collective-permute-start | bytes 393224 | tf_op jit(solution)/shard_map/ppermute | solution.py:38
  170.7 5.1 %collective-permute-start.8 = (bf16[512,128]{1,0:T(8,128)(2,1)S(1)}, bf16[512,128]{1,0:T(8,128)(2,1)S(1)}, u32[]{:S(2)}, u32[]{:S(2)}) collective-permute-start(bf16[512,128]{1,0:T(8,128)(2,1)S(1)} %collective-permute-done.7.refs_1_), channel_id=1, source_target_pairs={{0,2},{2,4},{4,6},{6,7},{7,5},{5,3},{3,1},{1,0},{8,10},{10,12},{12... | collective-permute-start | bytes 393224 | tf_op jit(solution)/shard_map/ppermute | solution.py:34
  172.3 5.1 %collective-permute-start.12 = (bf16[512,128]{1,0:T(8,128)(2,1)S(1)}, bf16[512,128]{1,0:T(8,128)(2,1)S(1)}, u32[]{:S(2)}, u32[]{:S(2)}) collective-permute-start(bf16[512,128]{1,0:T(8,128)(2,1)S(1)} %collective-permute-done.11.refs_5_), channel_id=1, source_target_pairs={{0,1},{2,0},{4,2},{6,4},{7,6},{5,7},{3,5},{1,3},{8,9},{10,8},{12,1... | collective-permute-start | bytes 393224 | tf_op jit(solution)/shard_map/ppermute | solution.py:38
  175.9 5.0 %collective-permute-start.9 = (bf16[512,128]{1,0:T(8,128)(2,1)S(1)}, bf16[512,128]{1,0:T(8,128)(2,1)S(1)}, u32[]{:S(2)}, u32[]{:S(2)}) collective-permute-start(bf16[512,128]{1,0:T(8,128)(2,1)S(1)} %collective-permute-done.8.refs_2_), channel_id=1, source_target_pairs={{0,2},{2,4},{4,6},{6,7},{7,5},{5,3},{3,1},{1,0},{8,10},{10,12},{12... | collective-permute-start | bytes 393224 | tf_op jit(solution)/shard_map/ppermute | solution.py:34
  177.4 5.7 %collective-permute-start.13 = (bf16[512,128]{1,0:T(8,128)(2,1)S(1)}, bf16[512,128]{1,0:T(8,128)(2,1)S(1)}, u32[]{:S(2)}, u32[]{:S(2)}) collective-permute-start(bf16[512,128]{1,0:T(8,128)(2,1)S(1)} %collective-permute-done.12.refs_6_), channel_id=1, source_target_pairs={{0,1},{2,0},{4,2},{6,4},{7,6},{5,7},{3,5},{1,3},{8,9},{10,8},{12,1... | collective-permute-start | bytes 393224 | tf_op jit(solution)/shard_map/ppermute | solution.py:38
  180.8 5.0 %collective-permute-start.10 = (bf16[512,128]{1,0:T(8,128)(2,1)S(1)}, bf16[512,128]{1,0:T(8,128)(2,1)S(1)}, u32[]{:S(2)}, u32[]{:S(2)}) collective-permute-start(bf16[512,128]{1,0:T(8,128)(2,1)S(1)} %collective-permute-done.9.refs_3_), channel_id=1, source_target_pairs={{0,2},{2,4},{4,6},{6,7},{7,5},{5,3},{3,1},{1,0},{8,10},{10,12},{12... | collective-permute-start | bytes 393224 | tf_op jit(solution)/shard_map/ppermute | solution.py:34
  228.6 7.8 %collective-permute-start.29 = (bf16[512,384]{1,0:T(8,128)(2,1)S(1)}, bf16[512,384]{1,0:T(8,128)(2,1)S(1)}, u32[]{:S(2)}, u32[]{:S(2)}) collective-permute-start(bf16[512,384]{1,0:T(8,128)(2,1)S(1)} %get-tuple-element.23), channel_id=1, source_target_pairs={{0,2},{2,4},{4,6},{6,7},{7,5},{5,3},{3,1},{1,0},{8,10},{10,12},{12... | collective-permute-start | bytes 1179656 | tf_op jit(solution)/shard_map/ppermute | solution.py:61
  230.2 7.8 %collective-permute-start.36 = (bf16[512,384]{1,0:T(8,128)(2,1)S(1)}, bf16[512,384]{1,0:T(8,128)(2,1)S(1)}, u32[]{:S(2)}, u32[]{:S(2)}) collective-permute-start(bf16[512,384]{1,0:T(8,128)(2,1)S(1)} %get-tuple-element.24), channel_id=1, source_target_pairs={{0,1},{2,0},{4,2},{6,4},{7,6},{5,7},{3,5},{1,3},{8,9},{10,8},{12,1... | collective-permute-start | bytes 1179656 | tf_op jit(solution)/shard_map/ppermute | solution.py:63
  239.3 9.1 %collective-permute-start.30 = (bf16[512,384]{1,0:T(8,128)(2,1)S(1)}, bf16[512,384]{1,0:T(8,128)(2,1)S(1)}, u32[]{:S(2)}, u32[]{:S(2)}) collective-permute-start(bf16[512,384]{1,0:T(8,128)(2,1)S(1)} %get-tuple-element.21), channel_id=1, source_target_pairs={{0,2},{2,4},{4,6},{6,7},{7,5},{5,3},{3,1},{1,0},{8,10},{10,12},{12... | collective-permute-start | bytes 1179656 | tf_op jit(solution)/shard_map/ppermute | solution.py:61
  241.4 9.7 %collective-permute-start.37 = (bf16[512,384]{1,0:T(8,128)(2,1)S(1)}, bf16[512,384]{1,0:T(8,128)(2,1)S(1)}, u32[]{:S(2)}, u32[]{:S(2)}) collective-permute-start(bf16[512,384]{1,0:T(8,128)(2,1)S(1)} %get-tuple-element.22), channel_id=1, source_target_pairs={{0,1},{2,0},{4,2},{6,4},{7,6},{5,7},{3,5},{1,3},{8,9},{10,8},{12,1... | collective-permute-start | bytes 1179656 | tf_op jit(solution)/shard_map/ppermute | solution.py:63
  252.4 10.9 %collective-permute-start.31 = (bf16[512,384]{1,0:T(8,128)(2,1)S(1)}, bf16[512,384]{1,0:T(8,128)(2,1)S(1)}, u32[]{:S(2)}, u32[]{:S(2)}) collective-permute-start(bf16[512,384]{1,0:T(8,128)(2,1)S(1)} %get-tuple-element.19), channel_id=1, source_target_pairs={{0,2},{2,4},{4,6},{6,7},{7,5},{5,3},{3,1},{1,0},{8,10},{10,12},{12... | collective-permute-start | bytes 1179656 | tf_op jit(solution)/shard_map/ppermute | solution.py:61
  253.2 11.2 %collective-permute-start.38 = (bf16[512,384]{1,0:T(8,128)(2,1)S(1)}, bf16[512,384]{1,0:T(8,128)(2,1)S(1)}, u32[]{:S(2)}, u32[]{:S(2)}) collective-permute-start(bf16[512,384]{1,0:T(8,128)(2,1)S(1)} %get-tuple-element.20), channel_id=1, source_target_pairs={{0,1},{2,0},{4,2},{6,4},{7,6},{5,7},{3,5},{1,3},{8,9},{10,8},{12,1... | collective-permute-start | bytes 1179656 | tf_op jit(solution)/shard_map/ppermute | solution.py:63
  265.8 11.7 %collective-permute-start.32 = (bf16[512,384]{1,0:T(8,128)(2,1)S(1)}, bf16[512,384]{1,0:T(8,128)(2,1)S(1)}, u32[]{:S(2)}, u32[]{:S(2)}) collective-permute-start(bf16[512,384]{1,0:T(8,128)(2,1)S(1)} %get-tuple-element.17), channel_id=1, source_target_pairs={{0,2},{2,4},{4,6},{6,7},{7,5},{5,3},{3,1},{1,0},{8,10},{10,12},{12... | collective-permute-start | bytes 1179656 | tf_op jit(solution)/shard_map/ppermute | solution.py:61
  266.2 11.3 %collective-permute-start.39 = (bf16[512,384]{1,0:T(8,128)(2,1)S(1)}, bf16[512,384]{1,0:T(8,128)(2,1)S(1)}, u32[]{:S(2)}, u32[]{:S(2)}) collective-permute-start(bf16[512,384]{1,0:T(8,128)(2,1)S(1)} %get-tuple-element.18), channel_id=1, source_target_pairs={{0,1},{2,0},{4,2},{6,4},{7,6},{5,7},{3,5},{1,3},{8,9},{10,8},{12,1... | collective-permute-start | bytes 1179656 | tf_op jit(solution)/shard_map/ppermute | solution.py:63
  278.9 10.7 %collective-permute-start.33 = (bf16[512,384]{1,0:T(8,128)(2,1)S(1)}, bf16[512,384]{1,0:T(8,128)(2,1)S(1)}, u32[]{:S(2)}, u32[]{:S(2)}) collective-permute-start(bf16[512,384]{1,0:T(8,128)(2,1)S(1)} %get-tuple-element.15), channel_id=1, source_target_pairs={{0,2},{2,4},{4,6},{6,7},{7,5},{5,3},{3,1},{1,0},{8,10},{10,12},{12... | collective-permute-start | bytes 1179656 | tf_op jit(solution)/shard_map/ppermute | solution.py:61
  279.3 10.5 %collective-permute-start.40 = (bf16[512,384]{1,0:T(8,128)(2,1)S(1)}, bf16[512,384]{1,0:T(8,128)(2,1)S(1)}, u32[]{:S(2)}, u32[]{:S(2)}) collective-permute-start(bf16[512,384]{1,0:T(8,128)(2,1)S(1)} %get-tuple-element.16), channel_id=1, source_target_pairs={{0,1},{2,0},{4,2},{6,4},{7,6},{5,7},{3,5},{1,3},{8,9},{10,8},{12,1... | collective-permute-start | bytes 1179656 | tf_op jit(solution)/shard_map/ppermute | solution.py:63
  291.1 10.7 %collective-permute-start.34 = (bf16[512,384]{1,0:T(8,128)(2,1)S(1)}, bf16[512,384]{1,0:T(8,128)(2,1)S(1)}, u32[]{:S(2)}, u32[]{:S(2)}) collective-permute-start(bf16[512,384]{1,0:T(8,128)(2,1)S(1)} %get-tuple-element.13), channel_id=1, source_target_pairs={{0,2},{2,4},{4,6},{6,7},{7,5},{5,3},{3,1},{1,0},{8,10},{10,12},{12... | collective-permute-start | bytes 1179656 | tf_op jit(solution)/shard_map/ppermute | solution.py:61
  291.5 10.5 %collective-permute-start.41 = (bf16[512,384]{1,0:T(8,128)(2,1)S(1)}, bf16[512,384]{1,0:T(8,128)(2,1)}, u32[]{:S(2)}, u32[]{:S(2)}) collective-permute-start(bf16[512,384]{1,0:T(8,128)(2,1)S(1)} %get-tuple-element.14), channel_id=1, source_target_pairs={{0,1},{2,0},{4,2},{6,4},{7,6},{5,7},{3,5},{1,3},{8,9},{10,8},{12,1... | collective-permute-start | bytes 1179656 | tf_op jit(solution)/shard_map/ppermute | solution.py:63
  304.2 8.0 %collective-permute-start.35 = (bf16[512,384]{1,0:T(8,128)(2,1)}, bf16[512,384]{1,0:T(8,128)(2,1)S(1)}, u32[]{:S(2)}, u32[]{:S(2)}) collective-permute-start(bf16[512,384]{1,0:T(8,128)(2,1)} %get-tuple-element.11), channel_id=1, source_target_pairs={{0,2},{2,4},{4,6},{6,7},{7,5},{5,3},{3,1},{1,0},{8,10},{10,12},{12... | collective-permute-start | bytes 1179656 | tf_op jit(solution)/shard_map/ppermute | solution.py:61
  305.7 7.9 %collective-permute-start.42 = (bf16[512,384]{1,0:T(8,128)(2,1)S(1)}, bf16[512,384]{1,0:T(8,128)(2,1)}, u32[]{:S(2)}, u32[]{:S(2)}) collective-permute-start(bf16[512,384]{1,0:T(8,128)(2,1)S(1)} %get-tuple-element.12), channel_id=1, source_target_pairs={{0,1},{2,0},{4,2},{6,4},{7,6},{5,7},{3,5},{1,3},{8,9},{10,8},{12,1... | collective-permute-start | bytes 1179656 | tf_op jit(solution)/shard_map/ppermute | solution.py:63
  (23 other events, 363.4 us)
Sparse Core Ops, SparseCore 0:
  8.9 18.3 all-gather.2
  28.9 17.9 all-gather.4

commit v16 on v14

--- a/solution.py
+++ b/solution.py
@@ -297,8 +297,16 @@
     hidden_units = jax.nn.gelu(pre_act).astype(jnp.bfloat16)
     down_terms = jnp.dot(hidden_units, down_full, preferred_element_type=jnp.float32)
     if gather_weights:
-        mlp_out = ring_reduce_scatter(
-            down_terms.reshape(token_count, model_width), "tp", tp_count
+        split = share_width // 2
+        blocks = down_terms.reshape(token_count, tp_count, share_width)
+        ring_part = ring_reduce_scatter(
+            blocks[:, :, :split].reshape(token_count, tp_count * split), "tp", tp_count
+        )
+        offload_part = lax.psum_scatter(
+            blocks[:, :, split:].astype(jnp.bfloat16), "tp", scatter_dimension=1, tiled=True
+        ).reshape(token_count, share_width - split)
+        mlp_out = jnp.concatenate(
+            [ring_part, offload_part.astype(jnp.float32)], axis=1
         ).reshape(local_count, row_count, share_width)
     else:
         mlp_out = lax.psum_scatter(

time: 327 us -> 353 us (1.080)
  waiting for transfers between devices: 159 us -> 171 us
  local copies, waits for them, and re-layouts: 21.6 us -> 29.1 us
  between operations: 32.8 us -> 37.3 us
    ppermute x7, waiting for transfers between devices: 7.52 us -> 22.5 us  [ring_reduce_scatter(): lax.ppermute(backward.astype(jnp.bfloat16), axis_name, behind)]
    unnamed x59 -> x70, local copies, waits for them, and re-layouts: 10.3 us -> 16.5 us
    ppermute x7, waiting for transfers between devices: 50.8 us -> 46 us  [ring_reduce_scatter(): lax.ppermute(forward.astype(jnp.bfloat16), axis_name, ahead)]
  transfers between devices with their start and end apart: 45 -> 46, of which waited for: 25 -> 24; matrix products, arithmetic and copies ran while one was open for 13% -> 16% of each run, Pallas kernels for 7% -> 6%
where the time goes in v16:
time: 353 us; the launch traced here: 352 us
  waiting for transfers between devices  171 us (48%)
  starting transfers between devices  41 us (12%)
  between operations  37.3 us (11%)
  local copies, waits for them, and re-layouts  29.1 us (8%)
  matrix products  24.8 us (7%)
  Pallas kernels  22.9 us (6%)
  other arithmetic  21.2 us (6%)
  blocking collectives  4.54 us (1%)
    ppermute x12, waiting for transfers between devices, ring_gather(): forward = lax.ppermute(forward, axis_name, ahead)  80.6 us
    ppermute x7, waiting for transfers between devices, ring_reduce_scatter(): lax.ppermute(forward.astype(jnp.bfloat16), axis_name, ahead)  46 us
    pallas_call x1, Pallas kernels, grouped_out_proj(): pl.pallas_call(functools.partial(out_proj_kernel, group_count, tiles_per_...  22.9 us
    ppermute x7, waiting for transfers between devices, ring_reduce_scatter(): lax.ppermute(backward.astype(jnp.bfloat16), axis_name, behind)  22.5 us
    ppermute x12, starting transfers between devices, ring_gather(): forward = lax.ppermute(forward, axis_name, ahead)  21.7 us
    ppermute x9, waiting for transfers between devices, ring_gather(): backward = lax.ppermute(backward, axis_name, behind)  21.1 us
    unnamed x70, local copies, waits for them, and re-layouts  16.5 us
    dot_general x1, matrix products, local(): pre_act = jnp.dot(mlp_in, up_full, preferred_element_type=jnp.float32)  10 us
  transfers between devices with their start and end apart: 46, of which 24 were waited for; matrix products, arithmetic and copies ran while one was open for 16% of the time, Pallas kernels for 6%

profile of v16, /device:TPU:0, one launch (start us, length us, event | category | flops | bytes accessed | tf_op | source)
XLA Modules:
  0.0 351.9 jit_solution(3046275562638876686)
XLA Ops:
  7.4 3.1 collective-permute-start
  10.5 2.1 collective-permute-start.14
  14.4 14.5 %collective-permute-done = bf16[4,128,768]{2,1,0:T(8,128)(2,1)S(1)} collective-permute-done((bf16[4,128,768]{2,1,0:T(8,128)(2,1)}, bf16[4,128,768]{2,1,0:T(8,128)(2,1)S(1)}, u32[]{:S(2)}, u32[]{:S(2)}) %collective-permute-start) | collective-permute-done | bytes 786464 | tf_op jit(solution)/shard_map/ppermute | solution.py:34
  29.0 2.1 collective-permute-start.1
  31.4 30.5 %collective-permute-done.1 = bf16[4,128,768]{2,1,0:T(8,128)(2,1)} collective-permute-done((bf16[4,128,768]{2,1,0:T(8,128)(2,1)S(1)}, bf16[4,128,768]{2,1,0:T(8,128)(2,1)}, u32[]{:S(2)}, u32[]{:S(2)}) %collective-permute-start.1) | collective-permute-done | bytes 786464 | tf_op jit(solution)/shard_map/ppermute | solution.py:34
  61.9 1.8 collective-permute-start.2
  65.5 2.2 all_gather.12
  67.7 13.3 %collective-permute-done.2 = bf16[4,128,768]{2,1,0:T(8,128)(2,1)} collective-permute-done((bf16[4,128,768]{2,1,0:T(8,128)(2,1)}, bf16[4,128,768]{2,1,0:T(8,128)(2,1)}, u32[]{:S(2)}, u32[]{:S(2)}) %collective-permute-start.2) | collective-permute-done | bytes 786464 | tf_op jit(solution)/shard_map/ppermute | solution.py:34
  96.6 6.6 %copy.31 = bf16[6144,3,128]{0,2,1:T(8,128)(2,1)} copy(bf16[6144,3,128]{2,0,1:T(8,128)(2,1)} %param.22) | data formatting | bytes 9437184 | tf_op args[7]
  104.5 1.6 collective-permute-start.15
  113.6 8.5 %collective-permute-done.15.refs_10_ = bf16[128,3072]{1,0:T(8,128)(2,1)} collective-permute-done((bf16[128,3072]{1,0:T(8,128)(2,1)}, bf16[128,3072]{1,0:T(8,128)(2,1)}, u32[]{:S(2)}, u32[]{:S(2)}) %collective-permute-start.15) | collective-permute-done | bytes 786464 | tf_op jit(solution)/shard_map/ppermute | solution.py:34
  122.1 4.7 %collective-permute-done.6 = bf16[4,128,768]{2,1,0:T(8,128)(2,1)S(1)} collective-permute-done((bf16[4,128,768]{2,1,0:T(8,128)(2,1)}, bf16[4,128,768]{2,1,0:T(8,128)(2,1)S(1)}, u32[]{:S(2)}, u32[]{:S(2)}) %collective-permute-start.6) | collective-permute-done | bytes 786464 | tf_op jit(solution)/shard_map/ppermute | solution.py:38
  129.8 2.7 fusion.3
  132.5 5.8 %convolution_convert_fusion.1 = bf16[512,384]{1,0:T(8,128)(2,1)S(1)} fusion(bf16[512,6144]{1,0:T(8,128)(2,1)S(1)} %bitcast.167, bf16[6144,384]{0,1:T(8,128)(2,1)} %bitcast.168), kind=kOutput, calls=%fused_computation.27 | convolution fusion | flops 2416115712 | bytes 11403264 | tf_op jit(solution)/shard_map/dot_general | solution.py:243
  139.2 2.4 all_gather.13
  144.3 1.6 collective-permute-start.17
  147.5 16.3 %collective-permute-done.20.refs_15_ = bf16[128,3072]{1,0:T(8,128)(2,1)S(1)} collective-permute-done((bf16[128,3072]{1,0:T(8,128)(2,1)}, bf16[128,3072]{1,0:T(8,128)(2,1)S(1)}, u32[]{:S(2)}, u32[]{:S(2)}) %collective-permute-start.20) | collective-permute-done | bytes 786464 | tf_op jit(solution)/shard_map/ppermute | solution.py:38
  164.9 1.6 collective-permute-start.7
  167.0 3.9 %collective-permute-done.7.refs_1_ = bf16[512,128]{1,0:T(8,128)(2,1)S(1)} collective-permute-done((bf16[512,128]{1,0:T(8,128)(2,1)S(1)}, bf16[512,128]{1,0:T(8,128)(2,1)S(1)}, u32[]{:S(2)}, u32[]{:S(2)}) %collective-permute-start.7) | collective-permute-done | bytes 131104 | tf_op jit(solution)/shard_map/ppermute | solution.py:34
  172.9 3.1 collective-permute-done.8.refs_2_
  178.1 2.9 collective-permute-done.9.refs_3_
  182.7 3.3 collective-permute-done.10.refs_4_
  187.0 22.9 %shard_map.145 = (f32[512,6144]{1,0:T(8,128)}, f32[512,128]{1,0:T(8,128)}) custom-call(s32[1]{0:T(128)} %bitcast.span_ref, bf16[512,128]{1,0:T(8,128)(2,1)} %bitcast.180, bf16[512,128]{1,0:T(8,128)(2,1)} %copy-done.21, bf16[512,128]{1,0:T(8,128)(2,1)} %copy-done.23, bf16[512,128]{1,0:T(8,128)(2,1)} %copy-done.25, bf16[512,128]{1,0:T(8,128)(2,1)} %copy-done.27, ...), custom_call_target="tpu_custom_call" | custom-call | flops 6442450944 | bytes 32505856 | tf_op jit(solution)/shard_map/pallas_call | solution.py:134
  210.9 10.0 %fusion.27 = bf16[4,128,512]{2,1,0:T(8,128)(2,1)S(1)} fusion(bf16[6144,512]{1,0:T(8,128)(2,1)} %all-gather.3.cloned.1.call-done, f32[4,128,6144]{2,1,0:T(8,128)} %bitcast.173, f32[4,6144]{1,0:T(4,128)S(1)} %get-tuple-element.32, f32[4,6144]{1,0:T(4,128)S(1)} %get-tuple-element.31, f32[4,128]{1,0:T(4,128)S(1)} %bitcast.177), kind=kOutput, calls=%fused_computation.38 | convolution fusion | flops 3236167680 | bytes 19597312 | tf_op jit(solution)/shard_map/dot_general | solution.py:296
  221.0 6.4 %convolution_convert_fusion = bf16[4,128,6144]{2,1,0:T(8,128)(2,1)S(1)} fusion(bf16[4,128,512]{2,1,0:T(8,128)(2,1)S(1)} %fusion.27, bf16[512,6144]{1,0:T(8,128)(2,1)} %all-gather.5.cloned.1.call-done), kind=kOutput, calls=%fused_computation.7 | convolution fusion | flops 3224371200 | bytes 13107200 | tf_op jit(solution)/shard_map/dot_general | solution.py:298
  227.4 2.0 copy.45
  229.4 2.3 fusion.40
  231.7 2.0 copy.42
  235.1 2.6 copy.46
  237.7 1.6 copy-done.3
  239.6 1.8 collective-permute-start.29
  243.1 8.2 %collective-permute-done.29 = bf16[512,192]{1,0:T(8,128)(2,1)S(1)} collective-permute-done((bf16[512,192]{1,0:T(8,128)(2,1)S(1)}, bf16[512,192]{1,0:T(8,128)(2,1)S(1)}, u32[]{:S(2)}, u32[]{:S(2)}) %collective-permute-start.29) | collective-permute-done | bytes 196640 | tf_op jit(solution)/shard_map/ppermute | solution.py:61
  251.3 8.6 %collective-permute-done.36 = bf16[512,192]{1,0:T(8,128)(2,1)S(1)} collective-permute-done((bf16[512,192]{1,0:T(8,128)(2,1)S(1)}, bf16[512,192]{1,0:T(8,128)(2,1)S(1)}, u32[]{:S(2)}, u32[]{:S(2)}) %collective-permute-start.36) | collective-permute-done | bytes 196640 | tf_op jit(solution)/shard_map/ppermute | solution.py:63
  261.9 1.6 collective-permute-start.37
  264.7 6.8 %collective-permute-done.30 = bf16[512,192]{1,0:T(8,128)(2,1)S(1)} collective-permute-done((bf16[512,192]{1,0:T(8,128)(2,1)S(1)}, bf16[512,192]{1,0:T(8,128)(2,1)S(1)}, u32[]{:S(2)}, u32[]{:S(2)}) %collective-permute-start.30) | collective-permute-done | bytes 196640 | tf_op jit(solution)/shard_map/ppermute | solution.py:61
  271.5 7.0 %collective-permute-done.37 = bf16[512,192]{1,0:T(8,128)(2,1)S(1)} collective-permute-done((bf16[512,192]{1,0:T(8,128)(2,1)S(1)}, bf16[512,192]{1,0:T(8,128)(2,1)S(1)}, u32[]{:S(2)}, u32[]{:S(2)}) %collective-permute-start.37) | collective-permute-done | bytes 196640 | tf_op jit(solution)/shard_map/ppermute | solution.py:63
  283.3 7.8 %collective-permute-done.31 = bf16[512,192]{1,0:T(8,128)(2,1)S(1)} collective-permute-done((bf16[512,192]{1,0:T(8,128)(2,1)S(1)}, bf16[512,192]{1,0:T(8,128)(2,1)S(1)}, u32[]{:S(2)}, u32[]{:S(2)}) %collective-permute-start.31) | collective-permute-done | bytes 196640 | tf_op jit(solution)/shard_map/ppermute | solution.py:61
  292.7 2.5 collective-permute-start.39
  296.4 5.2 %collective-permute-done.32 = bf16[512,192]{1,0:T(8,128)(2,1)S(1)} collective-permute-done((bf16[512,192]{1,0:T(8,128)(2,1)S(1)}, bf16[512,192]{1,0:T(8,128)(2,1)S(1)}, u32[]{:S(2)}, u32[]{:S(2)}) %collective-permute-start.32) | collective-permute-done | bytes 196640 | tf_op jit(solution)/shard_map/ppermute | solution.py:61
  303.1 2.2 collective-permute-start.33
  306.6 10.1 %collective-permute-done.33 = bf16[512,192]{1,0:T(8,128)(2,1)S(1)} collective-permute-done((bf16[512,192]{1,0:T(8,128)(2,1)S(1)}, bf16[512,192]{1,0:T(8,128)(2,1)S(1)}, u32[]{:S(2)}, u32[]{:S(2)}) %collective-permute-start.33) | collective-permute-done | bytes 196640 | tf_op jit(solution)/shard_map/ppermute | solution.py:61
  316.7 4.6 %collective-permute-done.40 = bf16[512,192]{1,0:T(8,128)(2,1)S(1)} collective-permute-done((bf16[512,192]{1,0:T(8,128)(2,1)S(1)}, bf16[512,192]{1,0:T(8,128)(2,1)S(1)}, u32[]{:S(2)}, u32[]{:S(2)}) %collective-permute-start.40) | collective-permute-done | bytes 196640 | tf_op jit(solution)/shard_map/ppermute | solution.py:63
  323.1 1.8 collective-permute-start.41
  325.6 4.2 %collective-permute-done.34 = bf16[512,192]{1,0:T(8,128)(2,1)S(1)} collective-permute-done((bf16[512,192]{1,0:T(8,128)(2,1)S(1)}, bf16[512,192]{1,0:T(8,128)(2,1)S(1)}, u32[]{:S(2)}, u32[]{:S(2)}) %collective-permute-start.34) | collective-permute-done | bytes 196640 | tf_op jit(solution)/shard_map/ppermute | solution.py:61
  331.5 2.0 collective-permute-start.35
  334.2 3.7 %collective-permute-done.35 = bf16[512,192]{1,0:T(8,128)(2,1)S(1)} collective-permute-done((bf16[512,192]{1,0:T(8,128)(2,1)S(1)}, bf16[512,192]{1,0:T(8,128)(2,1)S(1)}, u32[]{:S(2)}, u32[]{:S(2)}) %collective-permute-start.35) | collective-permute-done | bytes 196640 | tf_op jit(solution)/shard_map/ppermute | solution.py:61
  337.9 2.0 collective-permute-done.42
  342.7 2.6 add_convert_fusion.2
  (175 shorter events, 47.2 us)
Async XLA Ops:
  6.6 204.4 %all-gather.3.cloned.1.call-start = ((), (), s32[]{:S(2)}) async-start(), calls=%async_computation.1 | async-start | bytes 9437184 | tf_op jit(solution)/shard_map/all_gather | solution.py:229
  7.3 83.5 %copy-start.10 = (s32[8]{0:T(128)S(1)}, s32[8]{0:T(128)}, u32[]{:S(2)}) copy-start(s32[8]{0:T(128)} %constant.291.clone) | copy-start | bytes 100
  7.3 213.7 %all-gather.5.cloned.1.call-start = ((), (), s32[]{:S(2)}) async-start(), calls=%async_computation.2 | async-start | bytes 9437184 | tf_op jit(solution)/shard_map/all_gather | solution.py:230
  7.4 21.6 %collective-permute-start = (bf16[4,128,768]{2,1,0:T(8,128)(2,1)}, bf16[4,128,768]{2,1,0:T(8,128)(2,1)S(1)}, u32[]{:S(2)}, u32[]{:S(2)}) collective-permute-start(bf16[4,128,768]{2,1,0:T(8,128)(2,1)} %param.15), channel_id=1, source_target_pairs={{0,2},{2,4},{4,6},{6,7},{7,5},{5,3},{3,1},{1,0},{8,10},{10,12},{12... | collective-permute-start | bytes 2359304 | tf_op jit(solution)/shard_map/ppermute | solution.py:34
  10.4 53.4 %collective-permute-start.4 = (bf16[4,128,768]{2,1,0:T(8,128)(2,1)}, bf16[4,128,768]{2,1,0:T(8,128)(2,1)}, u32[]{:S(2)}, u32[]{:S(2)}) collective-permute-start(bf16[4,128,768]{2,1,0:T(8,128)(2,1)} %param.15), channel_id=1, source_target_pairs={{0,1},{2,0},{4,2},{6,4},{7,6},{5,7},{3,5},{1,3},{8,9},{10,8},{12,1... | collective-permute-start | bytes 2359304 | tf_op jit(solution)/shard_map/ppermute | solution.py:38
  10.5 92.7 %copy-start.5 = (bf16[128,3072]{1,0:T(8,128)(2,1)}, bf16[128,3072]{1,0:T(8,128)(2,1)S(1)}, u32[]{:S(2)}) copy-start(bf16[128,3072]{1,0:T(8,128)(2,1)S(1)} %constant_dynamic-slice_fusion.2.refs_8_) | copy-start | bytes 2359300
  10.5 93.9 %collective-permute-start.14 = (bf16[128,3072]{1,0:T(8,128)(2,1)S(1)}, bf16[128,3072]{1,0:T(8,128)(2,1)}, u32[]{:S(2)}, u32[]{:S(2)}) collective-permute-start(bf16[128,3072]{1,0:T(8,128)(2,1)S(1)} %constant_dynamic-slice_fusion.2.refs_8_), channel_id=1, source_target_pairs={{0,2},{2,4},{4,6},{6,7},{7,5},{5,3},{3,1},{1,0},{8,10},{10,12},{12... | collective-permute-start | bytes 2359304 | tf_op jit(solution)/shard_map/ppermute | solution.py:34
  12.6 96.6 %collective-permute-start.18 = (bf16[128,3072]{1,0:T(8,128)(2,1)S(1)}, bf16[128,3072]{1,0:T(8,128)(2,1)}, u32[]{:S(2)}, u32[]{:S(2)}) collective-permute-start(bf16[128,3072]{1,0:T(8,128)(2,1)S(1)} %constant_dynamic-slice_fusion.2.refs_8_), channel_id=1, source_target_pairs={{0,1},{2,0},{4,2},{6,4},{7,6},{5,7},{3,5},{1,3},{8,9},{10,8},{12,1... | collective-permute-start | bytes 2359304 | tf_op jit(solution)/shard_map/ppermute | solution.py:38
  12.6 131.0 %collective-permute-start.21 = (bf16[128,3072]{1,0:T(8,128)(2,1)S(1)}, bf16[128,3072]{1,0:T(8,128)(2,1)}, u32[]{:S(2)}, u32[]{:S(2)}) collective-permute-start(bf16[128,3072]{1,0:T(8,128)(2,1)S(1)} %constant_dynamic-slice_fusion.2.refs_8_), channel_id=1, source_target_pairs={{0,8},{8,0},{1,9},{9,1},{2,10},{10,2},{3,11},{11,3},{4,12},{12,4},... | collective-permute-start | bytes 2359304 | tf_op jit(solution)/shard_map/ppermute | solution.py:227
  12.6 328.7 %reduce-scatter.2.cloned.1.call-start = ((), (), s32[]{:S(2)}) async-start(), calls=%async_computation.3 | async-start | bytes 3538944 | tf_op jit(solution)/shard_map/reduce_scatter | solution.py:305
  29.0 33.0 %collective-permute-start.1 = (bf16[4,128,768]{2,1,0:T(8,128)(2,1)S(1)}, bf16[4,128,768]{2,1,0:T(8,128)(2,1)}, u32[]{:S(2)}, u32[]{:S(2)}) collective-permute-start(bf16[4,128,768]{2,1,0:T(8,128)(2,1)S(1)} %collective-permute-done), channel_id=1, source_target_pairs={{0,2},{2,4},{4,6},{6,7},{7,5},{5,3},{3,1},{1,0},{8,10},{10,12},{12... | collective-permute-start | bytes 2359304 | tf_op jit(solution)/shard_map/ppermute | solution.py:34
  61.9 19.0 %collective-permute-start.2 = (bf16[4,128,768]{2,1,0:T(8,128)(2,1)}, bf16[4,128,768]{2,1,0:T(8,128)(2,1)}, u32[]{:S(2)}, u32[]{:S(2)}) collective-permute-start(bf16[4,128,768]{2,1,0:T(8,128)(2,1)} %collective-permute-done.1), channel_id=1, source_target_pairs={{0,2},{2,4},{4,6},{6,7},{7,5},{5,3},{3,1},{1,0},{8,10},{10,12},{12... | collective-permute-start | bytes 2359304 | tf_op jit(solution)/shard_map/ppermute | solution.py:34
  63.8 42.3 %collective-permute-start.5 = (bf16[4,128,768]{2,1,0:T(8,128)(2,1)}, bf16[4,128,768]{2,1,0:T(8,128)(2,1)}, u32[]{:S(2)}, u32[]{:S(2)}) collective-permute-start(bf16[4,128,768]{2,1,0:T(8,128)(2,1)} %collective-permute-done.4), channel_id=1, source_target_pairs={{0,1},{2,0},{4,2},{6,4},{7,6},{5,7},{3,5},{1,3},{8,9},{10,8},{12,1... | collective-permute-start | bytes 2359304 | tf_op jit(solution)/shard_map/ppermute | solution.py:38
  81.0 28.3 %collective-permute-start.3 = (bf16[4,128,768]{2,1,0:T(8,128)(2,1)}, bf16[4,128,768]{2,1,0:T(8,128)(2,1)}, u32[]{:S(2)}, u32[]{:S(2)}) collective-permute-start(bf16[4,128,768]{2,1,0:T(8,128)(2,1)} %collective-permute-done.2), channel_id=1, source_target_pairs={{0,2},{2,4},{4,6},{6,7},{7,5},{5,3},{3,1},{1,0},{8,10},{10,12},{12... | collective-permute-start | bytes 2359304 | tf_op jit(solution)/shard_map/ppermute | solution.py:34
  104.5 17.6 %collective-permute-start.15 = (bf16[128,3072]{1,0:T(8,128)(2,1)}, bf16[128,3072]{1,0:T(8,128)(2,1)}, u32[]{:S(2)}, u32[]{:S(2)}) collective-permute-start(bf16[128,3072]{1,0:T(8,128)(2,1)} %collective-permute-done.14.refs_9_), channel_id=1, source_target_pairs={{0,2},{2,4},{4,6},{6,7},{7,5},{5,3},{3,1},{1,0},{8,10},{10,12},{12... | collective-permute-start | bytes 2359304 | tf_op jit(solution)/shard_map/ppermute | solution.py:34
  106.1 20.7 %collective-permute-start.6 = (bf16[4,128,768]{2,1,0:T(8,128)(2,1)}, bf16[4,128,768]{2,1,0:T(8,128)(2,1)S(1)}, u32[]{:S(2)}, u32[]{:S(2)}) collective-permute-start(bf16[4,128,768]{2,1,0:T(8,128)(2,1)} %collective-permute-done.5), channel_id=1, source_target_pairs={{0,1},{2,0},{4,2},{6,4},{7,6},{5,7},{3,5},{1,3},{8,9},{10,8},{12,1... | collective-permute-start | bytes 2359304 | tf_op jit(solution)/shard_map/ppermute | solution.py:38
  109.2 35.1 %collective-permute-start.22 = (bf16[128,3072]{1,0:T(8,128)(2,1)}, bf16[128,3072]{1,0:T(8,128)(2,1)}, u32[]{:S(2)}, u32[]{:S(2)}) collective-permute-start(bf16[128,3072]{1,0:T(8,128)(2,1)} %collective-permute-done.14.refs_9_), channel_id=1, source_target_pairs={{0,8},{8,0},{1,9},{9,1},{2,10},{10,2},{3,11},{11,3},{4,12},{12,4},... | collective-permute-start | bytes 2359304 | tf_op jit(solution)/shard_map/ppermute | solution.py:227
  109.3 34.5 %collective-permute-start.19 = (bf16[128,3072]{1,0:T(8,128)(2,1)}, bf16[128,3072]{1,0:T(8,128)(2,1)}, u32[]{:S(2)}, u32[]{:S(2)}) collective-permute-start(bf16[128,3072]{1,0:T(8,128)(2,1)} %collective-permute-done.18.refs_13_), channel_id=1, source_target_pairs={{0,1},{2,0},{4,2},{6,4},{7,6},{5,7},{3,5},{1,3},{8,9},{10,8},{12,1... | collective-permute-start | bytes 2359304 | tf_op jit(solution)/shard_map/ppermute | solution.py:38
  122.1 25.2 %collective-permute-start.26 = (bf16[128,3072]{1,0:T(8,128)(2,1)}, bf16[128,3072]{1,0:T(8,128)(2,1)}, u32[]{:S(2)}, u32[]{:S(2)}) collective-permute-start(bf16[128,3072]{1,0:T(8,128)(2,1)} %collective-permute-done.18.refs_13_), channel_id=1, source_target_pairs={{0,8},{8,0},{1,9},{9,1},{2,10},{10,2},{3,11},{11,3},{4,12},{12,4},... | collective-permute-start | bytes 2359304 | tf_op jit(solution)/shard_map/ppermute | solution.py:227
  126.8 17.5 %collective-permute-start.16 = (bf16[128,3072]{1,0:T(8,128)(2,1)}, bf16[128,3072]{1,0:T(8,128)(2,1)}, u32[]{:S(2)}, u32[]{:S(2)}) collective-permute-start(bf16[128,3072]{1,0:T(8,128)(2,1)} %collective-permute-done.15.refs_10_), channel_id=1, source_target_pairs={{0,2},{2,4},{4,6},{6,7},{7,5},{5,3},{3,1},{1,0},{8,10},{10,12},{12... | collective-permute-start | bytes 2359304 | tf_op jit(solution)/shard_map/ppermute | solution.py:34
  143.6 21.3 %collective-permute-start.23 = (bf16[128,3072]{1,0:T(8,128)(2,1)}, bf16[128,3072]{1,0:T(8,128)(2,1)S(1)}, u32[]{:S(2)}, u32[]{:S(2)}) collective-permute-start(bf16[128,3072]{1,0:T(8,128)(2,1)} %collective-permute-done.15.refs_10_), channel_id=1, source_target_pairs={{0,8},{8,0},{1,9},{9,1},{2,10},{10,2},{3,11},{11,3},{4,12},{12,4},... | collective-permute-start | bytes 2359304 | tf_op jit(solution)/shard_map/ppermute | solution.py:227
  143.8 20.0 %collective-permute-start.20 = (bf16[128,3072]{1,0:T(8,128)(2,1)}, bf16[128,3072]{1,0:T(8,128)(2,1)S(1)}, u32[]{:S(2)}, u32[]{:S(2)}) collective-permute-start(bf16[128,3072]{1,0:T(8,128)(2,1)} %collective-permute-done.19.refs_14_), channel_id=1, source_target_pairs={{0,1},{2,0},{4,2},{6,4},{7,6},{5,7},{3,5},{1,3},{8,9},{10,8},{12,1... | collective-permute-start | bytes 2359304 | tf_op jit(solution)/shard_map/ppermute | solution.py:38
  144.3 22.3 %collective-permute-start.27 = (bf16[128,3072]{1,0:T(8,128)(2,1)}, bf16[128,3072]{1,0:T(8,128)(2,1)S(1)}, u32[]{:S(2)}, u32[]{:S(2)}) collective-permute-start(bf16[128,3072]{1,0:T(8,128)(2,1)} %collective-permute-done.19.refs_14_), channel_id=1, source_target_pairs={{0,8},{8,0},{1,9},{9,1},{2,10},{10,2},{3,11},{11,3},{4,12},{12,4},... | collective-permute-start | bytes 2359304 | tf_op jit(solution)/shard_map/ppermute | solution.py:227
  144.3 20.1 %collective-permute-start.17 = (bf16[128,3072]{1,0:T(8,128)(2,1)}, bf16[128,3072]{1,0:T(8,128)(2,1)S(1)}, u32[]{:S(2)}, u32[]{:S(2)}) collective-permute-start(bf16[128,3072]{1,0:T(8,128)(2,1)} %collective-permute-done.16.refs_11_), channel_id=1, source_target_pairs={{0,2},{2,4},{4,6},{6,7},{7,5},{5,3},{3,1},{1,0},{8,10},{10,12},{12... | collective-permute-start | bytes 2359304 | tf_op jit(solution)/shard_map/ppermute | solution.py:34
  147.3 35.3 %collective-permute-start.24 = (bf16[128,3072]{1,0:T(8,128)(2,1)}, bf16[128,3072]{1,0:T(8,128)(2,1)S(1)}, u32[]{:S(2)}, u32[]{:S(2)}) collective-permute-start(bf16[128,3072]{1,0:T(8,128)(2,1)} %collective-permute-done.16.refs_11_), channel_id=1, source_target_pairs={{0,8},{8,0},{1,9},{9,1},{2,10},{10,2},{3,11},{11,3},{4,12},{12,4},... | collective-permute-start | bytes 2359304 | tf_op jit(solution)/shard_map/ppermute | solution.py:227
  163.8 18.8 %collective-permute-start.28 = (bf16[128,3072]{1,0:T(8,128)(2,1)S(1)}, bf16[128,3072]{1,0:T(8,128)(2,1)S(1)}, u32[]{:S(2)}, u32[]{:S(2)}) collective-permute-start(bf16[128,3072]{1,0:T(8,128)(2,1)S(1)} %collective-permute-done.20.refs_15_), channel_id=1, source_target_pairs={{0,8},{8,0},{1,9},{9,1},{2,10},{10,2},{3,11},{11,3},{4,12},{12,4},... | collective-permute-start | bytes 2359304 | tf_op jit(solution)/shard_map/ppermute | solution.py:227
  164.4 21.5 %collective-permute-start.25 = (bf16[128,3072]{1,0:T(8,128)(2,1)S(1)}, bf16[128,3072]{1,0:T(8,128)(2,1)S(1)}, u32[]{:S(2)}, u32[]{:S(2)}) collective-permute-start(bf16[128,3072]{1,0:T(8,128)(2,1)S(1)} %collective-permute-done.17.refs_12_), channel_id=1, source_target_pairs={{0,8},{8,0},{1,9},{9,1},{2,10},{10,2},{3,11},{11,3},{4,12},{12,4},... | collective-permute-start | bytes 2359304 | tf_op jit(solution)/shard_map/ppermute | solution.py:227
  164.9 6.0 %collective-permute-start.7 = (bf16[512,128]{1,0:T(8,128)(2,1)S(1)}, bf16[512,128]{1,0:T(8,128)(2,1)S(1)}, u32[]{:S(2)}, u32[]{:S(2)}) collective-permute-start(bf16[512,128]{1,0:T(8,128)(2,1)S(1)} %bitcast.178), channel_id=1, source_target_pairs={{0,2},{2,4},{4,6},{6,7},{7,5},{5,3},{3,1},{1,0},{8,10},{10,12},{12... | collective-permute-start | bytes 393224 | tf_op jit(solution)/shard_map/ppermute | solution.py:34
  166.6 5.9 %collective-permute-start.11 = (bf16[512,128]{1,0:T(8,128)(2,1)S(1)}, bf16[512,128]{1,0:T(8,128)(2,1)S(1)}, u32[]{:S(2)}, u32[]{:S(2)}) collective-permute-start(bf16[512,128]{1,0:T(8,128)(2,1)S(1)} %bitcast.179), channel_id=1, source_target_pairs={{0,1},{2,0},{4,2},{6,4},{7,6},{5,7},{3,5},{1,3},{8,9},{10,8},{12,1... | collective-permute-start | bytes 393224 | tf_op jit(solution)/shard_map/ppermute | solution.py:38
  170.9 5.1 %collective-permute-start.8 = (bf16[512,128]{1,0:T(8,128)(2,1)S(1)}, bf16[512,128]{1,0:T(8,128)(2,1)S(1)}, u32[]{:S(2)}, u32[]{:S(2)}) collective-permute-start(bf16[512,128]{1,0:T(8,128)(2,1)S(1)} %collective-permute-done.7.refs_1_), channel_id=1, source_target_pairs={{0,2},{2,4},{4,6},{6,7},{7,5},{5,3},{3,1},{1,0},{8,10},{10,12},{12... | collective-permute-start | bytes 393224 | tf_op jit(solution)/shard_map/ppermute | solution.py:34
  172.5 5.1 %collective-permute-start.12 = (bf16[512,128]{1,0:T(8,128)(2,1)S(1)}, bf16[512,128]{1,0:T(8,128)(2,1)S(1)}, u32[]{:S(2)}, u32[]{:S(2)}) collective-permute-start(bf16[512,128]{1,0:T(8,128)(2,1)S(1)} %collective-permute-done.11.refs_5_), channel_id=1, source_target_pairs={{0,1},{2,0},{4,2},{6,4},{7,6},{5,7},{3,5},{1,3},{8,9},{10,8},{12,1... | collective-permute-start | bytes 393224 | tf_op jit(solution)/shard_map/ppermute | solution.py:38
  176.0 5.0 %collective-permute-start.9 = (bf16[512,128]{1,0:T(8,128)(2,1)S(1)}, bf16[512,128]{1,0:T(8,128)(2,1)S(1)}, u32[]{:S(2)}, u32[]{:S(2)}) collective-permute-start(bf16[512,128]{1,0:T(8,128)(2,1)S(1)} %collective-permute-done.8.refs_2_), channel_id=1, source_target_pairs={{0,2},{2,4},{4,6},{6,7},{7,5},{5,3},{3,1},{1,0},{8,10},{10,12},{12... | collective-permute-start | bytes 393224 | tf_op jit(solution)/shard_map/ppermute | solution.py:34
  177.6 5.0 %collective-permute-start.13 = (bf16[512,128]{1,0:T(8,128)(2,1)S(1)}, bf16[512,128]{1,0:T(8,128)(2,1)S(1)}, u32[]{:S(2)}, u32[]{:S(2)}) collective-permute-start(bf16[512,128]{1,0:T(8,128)(2,1)S(1)} %collective-permute-done.12.refs_6_), channel_id=1, source_target_pairs={{0,1},{2,0},{4,2},{6,4},{7,6},{5,7},{3,5},{1,3},{8,9},{10,8},{12,1... | collective-permute-start | bytes 393224 | tf_op jit(solution)/shard_map/ppermute | solution.py:38
  181.0 5.0 %collective-permute-start.10 = (bf16[512,128]{1,0:T(8,128)(2,1)S(1)}, bf16[512,128]{1,0:T(8,128)(2,1)S(1)}, u32[]{:S(2)}, u32[]{:S(2)}) collective-permute-start(bf16[512,128]{1,0:T(8,128)(2,1)S(1)} %collective-permute-done.9.refs_3_), channel_id=1, source_target_pairs={{0,2},{2,4},{4,6},{6,7},{7,5},{5,3},{3,1},{1,0},{8,10},{10,12},{12... | collective-permute-start | bytes 393224 | tf_op jit(solution)/shard_map/ppermute | solution.py:34
  239.6 11.7 %collective-permute-start.29 = (bf16[512,192]{1,0:T(8,128)(2,1)S(1)}, bf16[512,192]{1,0:T(8,128)(2,1)S(1)}, u32[]{:S(2)}, u32[]{:S(2)}) collective-permute-start(bf16[512,192]{1,0:T(8,128)(2,1)S(1)} %get-tuple-element.25), channel_id=1, source_target_pairs={{0,2},{2,4},{4,6},{6,7},{7,5},{5,3},{3,1},{1,0},{8,10},{10,12},{12... | collective-permute-start | bytes 589832 | tf_op jit(solution)/shard_map/ppermute | solution.py:61
  241.4 18.5 %collective-permute-start.36 = (bf16[512,192]{1,0:T(8,128)(2,1)S(1)}, bf16[512,192]{1,0:T(8,128)(2,1)S(1)}, u32[]{:S(2)}, u32[]{:S(2)}) collective-permute-start(bf16[512,192]{1,0:T(8,128)(2,1)S(1)} %get-tuple-element.26), channel_id=1, source_target_pairs={{0,1},{2,0},{4,2},{6,4},{7,6},{5,7},{3,5},{1,3},{8,9},{10,8},{12,1... | collective-permute-start | bytes 589832 | tf_op jit(solution)/shard_map/ppermute | solution.py:63
  261.4 10.1 %collective-permute-start.30 = (bf16[512,192]{1,0:T(8,128)(2,1)S(1)}, bf16[512,192]{1,0:T(8,128)(2,1)S(1)}, u32[]{:S(2)}, u32[]{:S(2)}) collective-permute-start(bf16[512,192]{1,0:T(8,128)(2,1)S(1)} %get-tuple-element.23), channel_id=1, source_target_pairs={{0,2},{2,4},{4,6},{6,7},{7,5},{5,3},{3,1},{1,0},{8,10},{10,12},{12... | collective-permute-start | bytes 589832 | tf_op jit(solution)/shard_map/ppermute | solution.py:61
  261.9 16.6 %collective-permute-start.37 = (bf16[512,192]{1,0:T(8,128)(2,1)S(1)}, bf16[512,192]{1,0:T(8,128)(2,1)S(1)}, u32[]{:S(2)}, u32[]{:S(2)}) collective-permute-start(bf16[512,192]{1,0:T(8,128)(2,1)S(1)} %get-tuple-element.24), channel_id=1, source_target_pairs={{0,1},{2,0},{4,2},{6,4},{7,6},{5,7},{3,5},{1,3},{8,9},{10,8},{12,1... | collective-permute-start | bytes 589832 | tf_op jit(solution)/shard_map/ppermute | solution.py:63
  279.9 11.2 %collective-permute-start.31 = (bf16[512,192]{1,0:T(8,128)(2,1)S(1)}, bf16[512,192]{1,0:T(8,128)(2,1)S(1)}, u32[]{:S(2)}, u32[]{:S(2)}) collective-permute-start(bf16[512,192]{1,0:T(8,128)(2,1)S(1)} %get-tuple-element.21), channel_id=1, source_target_pairs={{0,2},{2,4},{4,6},{6,7},{7,5},{5,3},{3,1},{1,0},{8,10},{10,12},{12... | collective-permute-start | bytes 589832 | tf_op jit(solution)/shard_map/ppermute | solution.py:61
  280.7 10.5 %collective-permute-start.38 = (bf16[512,192]{1,0:T(8,128)(2,1)S(1)}, bf16[512,192]{1,0:T(8,128)(2,1)S(1)}, u32[]{:S(2)}, u32[]{:S(2)}) collective-permute-start(bf16[512,192]{1,0:T(8,128)(2,1)S(1)} %get-tuple-element.22), channel_id=1, source_target_pairs={{0,1},{2,0},{4,2},{6,4},{7,6},{5,7},{3,5},{1,3},{8,9},{10,8},{12,1... | collective-permute-start | bytes 589832 | tf_op jit(solution)/shard_map/ppermute | solution.py:63
  292.6 9.0 %collective-permute-start.32 = (bf16[512,192]{1,0:T(8,128)(2,1)S(1)}, bf16[512,192]{1,0:T(8,128)(2,1)S(1)}, u32[]{:S(2)}, u32[]{:S(2)}) collective-permute-start(bf16[512,192]{1,0:T(8,128)(2,1)S(1)} %get-tuple-element.19), channel_id=1, source_target_pairs={{0,2},{2,4},{4,6},{6,7},{7,5},{5,3},{3,1},{1,0},{8,10},{10,12},{12... | collective-permute-start | bytes 589832 | tf_op jit(solution)/shard_map/ppermute | solution.py:61
  292.7 9.0 %collective-permute-start.39 = (bf16[512,192]{1,0:T(8,128)(2,1)S(1)}, bf16[512,192]{1,0:T(8,128)(2,1)S(1)}, u32[]{:S(2)}, u32[]{:S(2)}) collective-permute-start(bf16[512,192]{1,0:T(8,128)(2,1)S(1)} %get-tuple-element.20), channel_id=1, source_target_pairs={{0,1},{2,0},{4,2},{6,4},{7,6},{5,7},{3,5},{1,3},{8,9},{10,8},{12,1... | collective-permute-start | bytes 589832 | tf_op jit(solution)/shard_map/ppermute | solution.py:63
  303.1 13.6 %collective-permute-start.33 = (bf16[512,192]{1,0:T(8,128)(2,1)S(1)}, bf16[512,192]{1,0:T(8,128)(2,1)S(1)}, u32[]{:S(2)}, u32[]{:S(2)}) collective-permute-start(bf16[512,192]{1,0:T(8,128)(2,1)S(1)} %get-tuple-element.17), channel_id=1, source_target_pairs={{0,2},{2,4},{4,6},{6,7},{7,5},{5,3},{3,1},{1,0},{8,10},{10,12},{12... | collective-permute-start | bytes 589832 | tf_op jit(solution)/shard_map/ppermute | solution.py:61
  305.3 16.0 %collective-permute-start.40 = (bf16[512,192]{1,0:T(8,128)(2,1)S(1)}, bf16[512,192]{1,0:T(8,128)(2,1)S(1)}, u32[]{:S(2)}, u32[]{:S(2)}) collective-permute-start(bf16[512,192]{1,0:T(8,128)(2,1)S(1)} %get-tuple-element.18), channel_id=1, source_target_pairs={{0,1},{2,0},{4,2},{6,4},{7,6},{5,7},{3,5},{1,3},{8,9},{10,8},{12,1... | collective-permute-start | bytes 589832 | tf_op jit(solution)/shard_map/ppermute | solution.py:63
  322.7 7.1 %collective-permute-start.34 = (bf16[512,192]{1,0:T(8,128)(2,1)S(1)}, bf16[512,192]{1,0:T(8,128)(2,1)S(1)}, u32[]{:S(2)}, u32[]{:S(2)}) collective-permute-start(bf16[512,192]{1,0:T(8,128)(2,1)S(1)} %get-tuple-element.15), channel_id=1, source_target_pairs={{0,2},{2,4},{4,6},{6,7},{7,5},{5,3},{3,1},{1,0},{8,10},{10,12},{12... | collective-permute-start | bytes 589832 | tf_op jit(solution)/shard_map/ppermute | solution.py:61
  323.1 6.9 %collective-permute-start.41 = (bf16[512,192]{1,0:T(8,128)(2,1)S(1)}, bf16[512,192]{1,0:T(8,128)(2,1)S(1)}, u32[]{:S(2)}, u32[]{:S(2)}) collective-permute-start(bf16[512,192]{1,0:T(8,128)(2,1)S(1)} %get-tuple-element.16), channel_id=1, source_target_pairs={{0,1},{2,0},{4,2},{6,4},{7,6},{5,7},{3,5},{1,3},{8,9},{10,8},{12,1... | collective-permute-start | bytes 589832 | tf_op jit(solution)/shard_map/ppermute | solution.py:63
  331.5 6.4 %collective-permute-start.35 = (bf16[512,192]{1,0:T(8,128)(2,1)S(1)}, bf16[512,192]{1,0:T(8,128)(2,1)S(1)}, u32[]{:S(2)}, u32[]{:S(2)}) collective-permute-start(bf16[512,192]{1,0:T(8,128)(2,1)S(1)} %get-tuple-element.13), channel_id=1, source_target_pairs={{0,2},{2,4},{4,6},{6,7},{7,5},{5,3},{3,1},{1,0},{8,10},{10,12},{12... | collective-permute-start | bytes 589832 | tf_op jit(solution)/shard_map/ppermute | solution.py:61
  333.5 6.4 %collective-permute-start.42 = (bf16[512,192]{1,0:T(8,128)(2,1)S(1)}, bf16[512,192]{1,0:T(8,128)(2,1)S(1)}, u32[]{:S(2)}, u32[]{:S(2)}) collective-permute-start(bf16[512,192]{1,0:T(8,128)(2,1)S(1)} %get-tuple-element.14), channel_id=1, source_target_pairs={{0,1},{2,0},{4,2},{6,4},{7,6},{5,7},{3,5},{1,3},{8,9},{10,8},{12,1... | collective-permute-start | bytes 589832 | tf_op jit(solution)/shard_map/ppermute | solution.py:63
  (28 other events, 411.3 us)
Sparse Core Ops, SparseCore 0:
  8.9 18.3 all-gather.2
  28.8 17.9 all-gather.4
  233.9 91.1 reduce-scatter.1

commit v17 on v15

--- a/solution.py
+++ b/solution.py
@@ -104,7 +104,7 @@
 
 
 def grouped_out_proj(
-    span_index, att_blocks, mine_blocks, other_blocks, hidden, scale, tile_width=1024
+    span_index, att_blocks, mine_blocks, other_halves, hidden, scale, tile_width=1024
 ):
     group_count = len(att_blocks)
     token_count, head_width = att_blocks[0].shape
@@ -116,9 +116,12 @@
     mine_spec = pl.BlockSpec(
         (head_width, tile_width), lambda n, s: (0, jnp.minimum(n, tiles_per_half - 1))
     )
-    other_spec = pl.BlockSpec(
-        (head_width, tile_width), lambda n, s: (0, jnp.maximum(n - tiles_per_half, 0))
-    )
+    def other_spec(group):
+        return pl.BlockSpec(
+            (None, None, head_width, tile_width),
+            lambda n, s: (1 - s[0], group, 0, jnp.maximum(n - tiles_per_half, 0)),
+        )
+
 
     def column(n, s):
         return ((n // tiles_per_half + s[0]) % 2) * tiles_per_half + n % tiles_per_half
@@ -140,7 +143,8 @@
         grid_spec=pltpu.PrefetchScalarGridSpec(
             num_scalar_prefetch=1,
             grid=(tile_count,),
-            in_specs=[att_spec] * group_count + [mine_spec] * group_count + [other_spec] * group_count
+            in_specs=[att_spec] * group_count + [mine_spec] * group_count
+            + [other_spec(g) for g in range(group_count)]
             + [hidden_spec, scale_spec],
             out_specs=[out_spec, squares_spec],
         ),
@@ -149,7 +153,7 @@
         jnp.reshape(span_index, (1,)).astype(jnp.int32),
         *att_blocks,
         *mine_blocks,
-        *other_blocks,
+        *([other_halves] * group_count),
         hidden,
         scale,
     )
@@ -224,7 +228,7 @@
         column_part = model_width // span_count
         w_out_part = lax.dynamic_slice_in_dim(w_out, span_index * column_part, column_part, 1)
         mine_blocks = ring_gather(w_out_part, "tp", tp_count)
-        other_blocks = [lax.ppermute(b, "span", [(0, 1), (1, 0)]) for b in mine_blocks]
+        both_halves = lax.all_gather(jnp.stack(mine_blocks), "span", axis=0)
     up_full, down_full = (
         lax.all_gather(w_up, "span", axis=1, tiled=True),
         lax.all_gather(w_down, "span", axis=0, tiled=True),
@@ -269,7 +273,7 @@
             span_index,
             att_blocks,
             mine_blocks,
-            other_blocks,
+            both_halves,
             gathered_narrow.reshape(token_count, model_width),
             mod_rows[:, 2],
         )

time: 326 us -> 354 us (1.086)
  waiting for transfers between devices: 159 us -> 180 us
  local copies, waits for them, and re-layouts: 21.6 us -> 30.3 us
    ppermute x12, waiting for transfers between devices: 78.7 us -> 116 us  [ring_gather(): forward = lax.ppermute(forward, axis_name, ahead)]
    ppermute x9, waiting for transfers between devices: 21.1 us -> 5.02 us  [ring_gather(): backward = lax.ppermute(backward, axis_name, behind)]
    unnamed x59 -> x72, local copies, waits for them, and re-layouts: 10.3 us -> 19.3 us
  transfers between devices with their start and end apart: 45 -> 38, of which waited for: 25 -> 26; matrix products, arithmetic and copies ran while one was open for 13% -> 14% of each run, Pallas kernels for 7% -> 6%
where the time goes in v17:
time: 354 us; the launch traced here: 353 us
  waiting for transfers between devices  180 us (51%)
  starting transfers between devices  39.5 us (11%)
  between operations  32.3 us (9%)
  local copies, waits for them, and re-layouts  30.3 us (9%)
  matrix products  24.8 us (7%)
  Pallas kernels  22.2 us (6%)
  other arithmetic  19.1 us (5%)
  blocking collectives  4.92 us (1%)
    ppermute x12, waiting for transfers between devices, ring_gather(): forward = lax.ppermute(forward, axis_name, ahead)  116 us
    ppermute x7, waiting for transfers between devices, ring_reduce_scatter(): lax.ppermute(forward.astype(jnp.bfloat16), axis_name, ahead)  47.8 us
    pallas_call x1, Pallas kernels, grouped_out_proj(): pl.pallas_call(functools.partial(out_proj_kernel, group_count, tiles_per_...  22.2 us
    unnamed x72, local copies, waits for them, and re-layouts  19.3 us
    ppermute x12, starting transfers between devices, ring_gather(): forward = lax.ppermute(forward, axis_name, ahead)  18.6 us
    dot_general x1, matrix products, local(): pre_act = jnp.dot(mlp_in, up_full, preferred_element_type=jnp.float32)  10 us
    ppermute x7, waiting for transfers between devices, ring_reduce_scatter(): lax.ppermute(backward.astype(jnp.bfloat16), axis_name, behind)  9.92 us
    ppermute x7, starting transfers between devices, ring_reduce_scatter(): lax.ppermute(forward.astype(jnp.bfloat16), axis_name, ahead)  8.89 us
  transfers between devices with their start and end apart: 38, of which 26 were waited for; matrix products, arithmetic and copies ran while one was open for 14% of the time, Pallas kernels for 6%

profile of v17, /device:TPU:0, one launch (start us, length us, event | category | flops | bytes accessed | tf_op | source)
XLA Modules:
  0.0 352.8 jit_solution(17409921741285004899)
XLA Ops:
  6.5 2.3 bitcast_dynamic-update-slice_fusion.7
  8.8 3.0 collective-permute-start.14
  11.8 17.5 %collective-permute-done.14.refs_9_ = bf16[128,3072]{1,0:T(8,128)(2,1)S(1)} collective-permute-done((bf16[128,3072]{1,0:T(8,128)(2,1)S(1)}, bf16[128,3072]{1,0:T(8,128)(2,1)S(1)}, u32[]{:S(2)}, u32[]{:S(2)}) %collective-permute-start.14) | collective-permute-done | bytes 786464 | tf_op jit(solution)/shard_map/ppermute | solution.py:34
  29.3 1.8 collective-permute-start.15
  31.3 16.7 %collective-permute-done.15.refs_10_ = bf16[128,3072]{1,0:T(8,128)(2,1)S(1)} collective-permute-done((bf16[128,3072]{1,0:T(8,128)(2,1)S(1)}, bf16[128,3072]{1,0:T(8,128)(2,1)S(1)}, u32[]{:S(2)}, u32[]{:S(2)}) %collective-permute-start.15) | collective-permute-done | bytes 786464 | tf_op jit(solution)/shard_map/ppermute | solution.py:34
  48.0 1.5 collective-permute-start.16
  51.0 14.8 %collective-permute-done.16.refs_11_ = bf16[128,3072]{1,0:T(8,128)(2,1)S(1)} collective-permute-done((bf16[128,3072]{1,0:T(8,128)(2,1)S(1)}, bf16[128,3072]{1,0:T(8,128)(2,1)S(1)}, u32[]{:S(2)}, u32[]{:S(2)}) %collective-permute-start.16) | collective-permute-done | bytes 786464 | tf_op jit(solution)/shard_map/ppermute | solution.py:34
  65.8 1.4 collective-permute-start.17
  69.8 12.9 %collective-permute-done.17.refs_12_ = bf16[128,3072]{1,0:T(8,128)(2,1)S(1)} collective-permute-done((bf16[128,3072]{1,0:T(8,128)(2,1)S(1)}, bf16[128,3072]{1,0:T(8,128)(2,1)S(1)}, u32[]{:S(2)}, u32[]{:S(2)}) %collective-permute-start.17) | collective-permute-done | bytes 786464 | tf_op jit(solution)/shard_map/ppermute | solution.py:34
  92.2 14.1 %collective-permute-done = bf16[4,128,768]{2,1,0:T(8,128)(2,1)S(1)} collective-permute-done((bf16[4,128,768]{2,1,0:T(8,128)(2,1)}, bf16[4,128,768]{2,1,0:T(8,128)(2,1)S(1)}, u32[]{:S(2)}, u32[]{:S(2)}) %collective-permute-start) | collective-permute-done | bytes 786464 | tf_op jit(solution)/shard_map/ppermute | solution.py:34
  107.8 16.0 %collective-permute-done.1 = bf16[4,128,768]{2,1,0:T(8,128)(2,1)} collective-permute-done((bf16[4,128,768]{2,1,0:T(8,128)(2,1)S(1)}, bf16[4,128,768]{2,1,0:T(8,128)(2,1)}, u32[]{:S(2)}, u32[]{:S(2)}) %collective-permute-start.1) | collective-permute-done | bytes 786464 | tf_op jit(solution)/shard_map/ppermute | solution.py:34
  127.3 2.6 all_gather.18
  129.9 11.6 %collective-permute-done.2 = bf16[4,128,768]{2,1,0:T(8,128)(2,1)} collective-permute-done((bf16[4,128,768]{2,1,0:T(8,128)(2,1)}, bf16[4,128,768]{2,1,0:T(8,128)(2,1)}, u32[]{:S(2)}, u32[]{:S(2)}) %collective-permute-start.2) | collective-permute-done | bytes 786464 | tf_op jit(solution)/shard_map/ppermute | solution.py:34
  156.9 6.7 %copy.30 = bf16[6144,3,128]{0,2,1:T(8,128)(2,1)} copy(bf16[6144,3,128]{2,0,1:T(8,128)(2,1)} %param.22) | data formatting | bytes 9437184 | tf_op args[7]
  171.9 5.0 %collective-permute-done.6 = bf16[4,128,768]{2,1,0:T(8,128)(2,1)S(1)} collective-permute-done((bf16[4,128,768]{2,1,0:T(8,128)(2,1)}, bf16[4,128,768]{2,1,0:T(8,128)(2,1)S(1)}, u32[]{:S(2)}, u32[]{:S(2)}) %collective-permute-start.6) | collective-permute-done | bytes 786464 | tf_op jit(solution)/shard_map/ppermute | solution.py:38
  178.4 2.7 fusion.3
  181.1 5.8 %convolution_convert_fusion.1 = bf16[512,384]{1,0:T(8,128)(2,1)S(1)} fusion(bf16[512,6144]{1,0:T(8,128)(2,1)S(1)} %bitcast.177, bf16[6144,384]{0,1:T(8,128)(2,1)} %bitcast.178), kind=kOutput, calls=%fused_computation.27 | convolution fusion | flops 2416115712 | bytes 11403264 | tf_op jit(solution)/shard_map/dot_general | solution.py:247
  187.7 2.4 all_gather.19
  193.9 1.6 collective-permute-start.7
  196.0 3.5 collective-permute-done.7.refs_1_
  199.5 1.6 collective-permute-start.8
  201.6 2.9 collective-permute-done.8.refs_2_
  204.5 1.6 collective-permute-start.9
  206.5 3.3 collective-permute-done.9.refs_3_
  209.9 1.6 collective-permute-start.10
  212.1 2.7 collective-permute-done.10.refs_4_
  215.5 22.2 %shard_map.145 = (f32[512,6144]{1,0:T(8,128)}, f32[512,128]{1,0:T(8,128)}) custom-call(s32[1]{0:T(128)} %bitcast.span_ref, bf16[512,128]{1,0:T(8,128)(2,1)} %bitcast.187, bf16[512,128]{1,0:T(8,128)(2,1)} %copy-done.16, bf16[512,128]{1,0:T(8,128)(2,1)} %copy-done.18, bf16[512,128]{1,0:T(8,128)(2,1)} %copy-done.20, bf16[512,128]{1,0:T(8,128)(2,1)} %copy-done.22, ...), custom_call_target="tpu_custom_call" | custom-call | flops 6442450944 | bytes 32505856 | tf_op jit(solution)/shard_map/pallas_call | solution.py:137
  238.8 10.0 %fusion.27 = bf16[4,128,512]{2,1,0:T(8,128)(2,1)S(1)} fusion(bf16[6144,512]{1,0:T(8,128)(2,1)} %all-gather.5.cloned.1.call-done, f32[4,128,6144]{2,1,0:T(8,128)} %bitcast.183, f32[4,6144]{1,0:T(4,128)S(1)} %copy-done.24, f32[4,6144]{1,0:T(4,128)S(1)} %get-tuple-element.31, f32[4,128]{1,0:T(4,128)S(1)} %bitcast.190), kind=kOutput, calls=%fused_computation.38 | convolution fusion | flops 3236167680 | bytes 19597312 | tf_op jit(solution)/shard_map/dot_general | solution.py:300
  248.9 6.4 %convolution_convert_fusion = bf16[4,128,6144]{2,1,0:T(8,128)(2,1)S(1)} fusion(bf16[4,128,512]{2,1,0:T(8,128)(2,1)S(1)} %fusion.27, bf16[512,6144]{1,0:T(8,128)(2,1)} %all-gather.7.cloned.1.call-done), kind=kOutput, calls=%fused_computation.7 | convolution fusion | flops 3224371200 | bytes 13107200 | tf_op jit(solution)/shard_map/dot_general | solution.py:302
  255.3 2.6 copy-done.3
  258.1 1.6 collective-permute-start.21
  261.5 4.4 %collective-permute-done.21 = bf16[512,384]{1,0:T(8,128)(2,1)S(1)} collective-permute-done((bf16[512,384]{1,0:T(8,128)(2,1)S(1)}, bf16[512,384]{1,0:T(8,128)(2,1)S(1)}, u32[]{:S(2)}, u32[]{:S(2)}) %collective-permute-start.21) | collective-permute-done | bytes 393248 | tf_op jit(solution)/shard_map/ppermute | solution.py:61
  265.9 1.6 collective-permute-done.28
  267.5 1.3 add_convert_fusion.18
  268.8 1.7 collective-permute-start.22
  272.1 5.2 %collective-permute-done.22 = bf16[512,384]{1,0:T(8,128)(2,1)S(1)} collective-permute-done((bf16[512,384]{1,0:T(8,128)(2,1)S(1)}, bf16[512,384]{1,0:T(8,128)(2,1)S(1)}, u32[]{:S(2)}, u32[]{:S(2)}) %collective-permute-start.22) | collective-permute-done | bytes 393248 | tf_op jit(solution)/shard_map/ppermute | solution.py:61
  277.3 3.5 collective-permute-done.29
  280.7 1.3 add_convert_fusion.17
  282.1 2.8 collective-permute-start.23
  285.5 8.4 %collective-permute-done.23 = bf16[512,384]{1,0:T(8,128)(2,1)S(1)} collective-permute-done((bf16[512,384]{1,0:T(8,128)(2,1)S(1)}, bf16[512,384]{1,0:T(8,128)(2,1)S(1)}, u32[]{:S(2)}, u32[]{:S(2)}) %collective-permute-start.23) | collective-permute-done | bytes 393248 | tf_op jit(solution)/shard_map/ppermute | solution.py:61
  293.9 2.7 collective-permute-done.30
  300.0 9.1 %collective-permute-done.24 = bf16[512,384]{1,0:T(8,128)(2,1)S(1)} collective-permute-done((bf16[512,384]{1,0:T(8,128)(2,1)S(1)}, bf16[512,384]{1,0:T(8,128)(2,1)S(1)}, u32[]{:S(2)}, u32[]{:S(2)}) %collective-permute-start.24) | collective-permute-done | bytes 393248 | tf_op jit(solution)/shard_map/ppermute | solution.py:61
  311.7 1.7 collective-permute-start.32
  313.4 8.0 %collective-permute-done.25 = bf16[512,384]{1,0:T(8,128)(2,1)S(1)} collective-permute-done((bf16[512,384]{1,0:T(8,128)(2,1)S(1)}, bf16[512,384]{1,0:T(8,128)(2,1)S(1)}, u32[]{:S(2)}, u32[]{:S(2)}) %collective-permute-start.25) | collective-permute-done | bytes 393248 | tf_op jit(solution)/shard_map/ppermute | solution.py:61
  323.4 1.7 collective-permute-start.33
  325.0 7.0 %collective-permute-done.26 = bf16[512,384]{1,0:T(8,128)(2,1)S(1)} collective-permute-done((bf16[512,384]{1,0:T(8,128)(2,1)S(1)}, bf16[512,384]{1,0:T(8,128)(2,1)S(1)}, u32[]{:S(2)}, u32[]{:S(2)}) %collective-permute-start.26) | collective-permute-done | bytes 393248 | tf_op jit(solution)/shard_map/ppermute | solution.py:61
  335.7 5.7 %collective-permute-done.27 = bf16[512,384]{1,0:T(8,128)(2,1)S(1)} collective-permute-done((bf16[512,384]{1,0:T(8,128)(2,1)S(1)}, bf16[512,384]{1,0:T(8,128)(2,1)S(1)}, u32[]{:S(2)}, u32[]{:S(2)}) %collective-permute-start.27) | collective-permute-done | bytes 393248 | tf_op jit(solution)/shard_map/ppermute | solution.py:61
  343.6 2.6 add_convert_fusion.2
  (159 shorter events, 51.3 us)
Async XLA Ops:
  6.5 84.6 %copy-start = (bf16[4,6,6144]{2,0,1:T(4,128)(2,1)S(1)}, bf16[4,6,6144]{2,0,1:T(4,128)(2,1)}, u32[]{:S(2)}) copy-start(bf16[4,6,6144]{2,0,1:T(4,128)(2,1)} %param.21) | copy-start | bytes 884740
  6.5 208.3 %all-gather.9.cloned.1.call-start = ((), (), s32[]{:S(2)}) async-start(), calls=%async_computation.2 | async-start | bytes 18874368 | tf_op jit(solution)/shard_map/all_gather | solution.py:231
  8.8 78.7 %copy-start.4 = (bf16[128,3072]{1,0:T(8,128)(2,1)}, bf16[128,3072]{1,0:T(8,128)(2,1)S(1)}, u32[]{:S(2)}) copy-start(bf16[128,3072]{1,0:T(8,128)(2,1)S(1)} %get-tuple-element.10.refs_8_) | copy-start | bytes 2359300
  8.8 20.5 %collective-permute-start.14 = (bf16[128,3072]{1,0:T(8,128)(2,1)S(1)}, bf16[128,3072]{1,0:T(8,128)(2,1)S(1)}, u32[]{:S(2)}, u32[]{:S(2)}) collective-permute-start(bf16[128,3072]{1,0:T(8,128)(2,1)S(1)} %get-tuple-element.10.refs_8_), channel_id=1, source_target_pairs={{0,2},{2,4},{4,6},{6,7},{7,5},{5,3},{3,1},{1,0},{8,10},{10,12},{12... | collective-permute-start | bytes 2359304 | tf_op jit(solution)/shard_map/ppermute | solution.py:34
  29.3 58.2 %copy-start.5 = (bf16[128,3072]{1,0:T(8,128)(2,1)}, bf16[128,3072]{1,0:T(8,128)(2,1)S(1)}, u32[]{:S(2)}) copy-start(bf16[128,3072]{1,0:T(8,128)(2,1)S(1)} %collective-permute-done.14.refs_9_) | copy-start | bytes 2359300
  29.3 18.7 %collective-permute-start.15 = (bf16[128,3072]{1,0:T(8,128)(2,1)S(1)}, bf16[128,3072]{1,0:T(8,128)(2,1)S(1)}, u32[]{:S(2)}, u32[]{:S(2)}) collective-permute-start(bf16[128,3072]{1,0:T(8,128)(2,1)S(1)} %collective-permute-done.14.refs_9_), channel_id=1, source_target_pairs={{0,2},{2,4},{4,6},{6,7},{7,5},{5,3},{3,1},{1,0},{8,10},{10,12},{12... | collective-permute-start | bytes 2359304 | tf_op jit(solution)/shard_map/ppermute | solution.py:34
  31.1 18.4 %collective-permute-start.18 = (bf16[128,3072]{1,0:T(8,128)(2,1)S(1)}, bf16[128,3072]{1,0:T(8,128)(2,1)S(1)}, u32[]{:S(2)}, u32[]{:S(2)}) collective-permute-start(bf16[128,3072]{1,0:T(8,128)(2,1)S(1)} %get-tuple-element.10.refs_8_), channel_id=1, source_target_pairs={{0,1},{2,0},{4,2},{6,4},{7,6},{5,7},{3,5},{1,3},{8,9},{10,8},{12,1... | collective-permute-start | bytes 2359304 | tf_op jit(solution)/shard_map/ppermute | solution.py:38
  48.0 39.5 %copy-start.6 = (bf16[128,3072]{1,0:T(8,128)(2,1)}, bf16[128,3072]{1,0:T(8,128)(2,1)S(1)}, u32[]{:S(2)}) copy-start(bf16[128,3072]{1,0:T(8,128)(2,1)S(1)} %collective-permute-done.15.refs_10_) | copy-start | bytes 2359300
  48.0 17.8 %collective-permute-start.16 = (bf16[128,3072]{1,0:T(8,128)(2,1)S(1)}, bf16[128,3072]{1,0:T(8,128)(2,1)S(1)}, u32[]{:S(2)}, u32[]{:S(2)}) collective-permute-start(bf16[128,3072]{1,0:T(8,128)(2,1)S(1)} %collective-permute-done.15.refs_10_), channel_id=1, source_target_pairs={{0,2},{2,4},{4,6},{6,7},{7,5},{5,3},{3,1},{1,0},{8,10},{10,12},{12... | collective-permute-start | bytes 2359304 | tf_op jit(solution)/shard_map/ppermute | solution.py:34
  49.5 38.0 %copy-start.7 = (bf16[128,3072]{1,0:T(8,128)(2,1)}, bf16[128,3072]{1,0:T(8,128)(2,1)S(1)}, u32[]{:S(2)}) copy-start(bf16[128,3072]{1,0:T(8,128)(2,1)S(1)} %collective-permute-done.18.refs_13_) | copy-start | bytes 2359300
  49.5 18.7 %collective-permute-start.19 = (bf16[128,3072]{1,0:T(8,128)(2,1)S(1)}, bf16[128,3072]{1,0:T(8,128)(2,1)S(1)}, u32[]{:S(2)}, u32[]{:S(2)}) collective-permute-start(bf16[128,3072]{1,0:T(8,128)(2,1)S(1)} %collective-permute-done.18.refs_13_), channel_id=1, source_target_pairs={{0,1},{2,0},{4,2},{6,4},{7,6},{5,7},{3,5},{1,3},{8,9},{10,8},{12,1... | collective-permute-start | bytes 2359304 | tf_op jit(solution)/shard_map/ppermute | solution.py:38
  65.8 16.9 %collective-permute-start.17 = (bf16[128,3072]{1,0:T(8,128)(2,1)S(1)}, bf16[128,3072]{1,0:T(8,128)(2,1)S(1)}, u32[]{:S(2)}, u32[]{:S(2)}) collective-permute-start(bf16[128,3072]{1,0:T(8,128)(2,1)S(1)} %collective-permute-done.16.refs_11_), channel_id=1, source_target_pairs={{0,2},{2,4},{4,6},{6,7},{7,5},{5,3},{3,1},{1,0},{8,10},{10,12},{12... | collective-permute-start | bytes 2359304 | tf_op jit(solution)/shard_map/ppermute | solution.py:34
  68.2 17.5 %collective-permute-start.20 = (bf16[128,3072]{1,0:T(8,128)(2,1)S(1)}, bf16[128,3072]{1,0:T(8,128)(2,1)S(1)}, u32[]{:S(2)}, u32[]{:S(2)}) collective-permute-start(bf16[128,3072]{1,0:T(8,128)(2,1)S(1)} %collective-permute-done.19.refs_14_), channel_id=1, source_target_pairs={{0,1},{2,0},{4,2},{6,4},{7,6},{5,7},{3,5},{1,3},{8,9},{10,8},{12,1... | collective-permute-start | bytes 2359304 | tf_op jit(solution)/shard_map/ppermute | solution.py:38
  87.5 38.5 %copy-start.28 = (s32[8]{0:T(128)S(1)}, s32[8]{0:T(128)}, u32[]{:S(2)}) copy-start(s32[8]{0:T(128)} %constant.288.clone) | copy-start | bytes 100
  87.5 63.4 %copy-start.23 = (s32[8]{0:T(128)S(1)}, s32[8]{0:T(128)}, u32[]{:S(2)}) copy-start(s32[8]{0:T(128)} %constant.289.clone) | copy-start | bytes 100
  87.6 151.2 %all-gather.5.cloned.1.call-start = ((), (), s32[]{:S(2)}) async-start(), calls=%async_computation | async-start | bytes 9437184 | tf_op jit(solution)/shard_map/all_gather | solution.py:233
  87.6 39.7 %copy-start.14 = (bf16[4,128,2,128]{3,2,1,0:T(2,128)(2,1)S(1)}, bf16[4,128,2,128]{3,2,1,0:T(2,128)(2,1)}, u32[]{:S(2)}) copy-start(bf16[4,128,2,128]{3,2,1,0:T(2,128)(2,1)} %param.20) | copy-start | bytes 786436
  88.3 160.6 %all-gather.7.cloned.1.call-start = ((), (), s32[]{:S(2)}) async-start(), calls=%async_computation.1 | async-start | bytes 9437184 | tf_op jit(solution)/shard_map/all_gather | solution.py:234
  88.4 18.0 %collective-permute-start = (bf16[4,128,768]{2,1,0:T(8,128)(2,1)}, bf16[4,128,768]{2,1,0:T(8,128)(2,1)S(1)}, u32[]{:S(2)}, u32[]{:S(2)}) collective-permute-start(bf16[4,128,768]{2,1,0:T(8,128)(2,1)} %param.15), channel_id=1, source_target_pairs={{0,2},{2,4},{4,6},{6,7},{7,5},{5,3},{3,1},{1,0},{8,10},{10,12},{12... | collective-permute-start | bytes 2359304 | tf_op jit(solution)/shard_map/ppermute | solution.py:34
  89.5 35.5 %collective-permute-start.4 = (bf16[4,128,768]{2,1,0:T(8,128)(2,1)}, bf16[4,128,768]{2,1,0:T(8,128)(2,1)S(1)}, u32[]{:S(2)}, u32[]{:S(2)}) collective-permute-start(bf16[4,128,768]{2,1,0:T(8,128)(2,1)} %param.15), channel_id=1, source_target_pairs={{0,1},{2,0},{4,2},{6,4},{7,6},{5,7},{3,5},{1,3},{8,9},{10,8},{12,1... | collective-permute-start | bytes 2359304 | tf_op jit(solution)/shard_map/ppermute | solution.py:38
  106.3 50.6 %copy-start.13 = (bf16[4,128,768]{2,1,0:T(8,128)(2,1)}, bf16[4,128,768]{2,1,0:T(8,128)(2,1)S(1)}, u32[]{:S(2)}) copy-start(bf16[4,128,768]{2,1,0:T(8,128)(2,1)S(1)} %collective-permute-done) | copy-start | bytes 2359300
  106.3 17.5 %collective-permute-start.1 = (bf16[4,128,768]{2,1,0:T(8,128)(2,1)S(1)}, bf16[4,128,768]{2,1,0:T(8,128)(2,1)}, u32[]{:S(2)}, u32[]{:S(2)}) collective-permute-start(bf16[4,128,768]{2,1,0:T(8,128)(2,1)S(1)} %collective-permute-done), channel_id=1, source_target_pairs={{0,2},{2,4},{4,6},{6,7},{7,5},{5,3},{3,1},{1,0},{8,10},{10,12},{12... | collective-permute-start | bytes 2359304 | tf_op jit(solution)/shard_map/ppermute | solution.py:34
  123.8 17.7 %collective-permute-start.2 = (bf16[4,128,768]{2,1,0:T(8,128)(2,1)}, bf16[4,128,768]{2,1,0:T(8,128)(2,1)}, u32[]{:S(2)}, u32[]{:S(2)}) collective-permute-start(bf16[4,128,768]{2,1,0:T(8,128)(2,1)} %collective-permute-done.1), channel_id=1, source_target_pairs={{0,2},{2,4},{4,6},{6,7},{7,5},{5,3},{3,1},{1,0},{8,10},{10,12},{12... | collective-permute-start | bytes 2359304 | tf_op jit(solution)/shard_map/ppermute | solution.py:34
  125.0 39.6 %collective-permute-start.5 = (bf16[4,128,768]{2,1,0:T(8,128)(2,1)S(1)}, bf16[4,128,768]{2,1,0:T(8,128)(2,1)}, u32[]{:S(2)}, u32[]{:S(2)}) collective-permute-start(bf16[4,128,768]{2,1,0:T(8,128)(2,1)S(1)} %collective-permute-done.4), channel_id=1, source_target_pairs={{0,1},{2,0},{4,2},{6,4},{7,6},{5,7},{3,5},{1,3},{8,9},{10,8},{12,1... | collective-permute-start | bytes 2359304 | tf_op jit(solution)/shard_map/ppermute | solution.py:38
  141.5 27.8 %collective-permute-start.3 = (bf16[4,128,768]{2,1,0:T(8,128)(2,1)}, bf16[4,128,768]{2,1,0:T(8,128)(2,1)}, u32[]{:S(2)}, u32[]{:S(2)}) collective-permute-start(bf16[4,128,768]{2,1,0:T(8,128)(2,1)} %collective-permute-done.2), channel_id=1, source_target_pairs={{0,2},{2,4},{4,6},{6,7},{7,5},{5,3},{3,1},{1,0},{8,10},{10,12},{12... | collective-permute-start | bytes 2359304 | tf_op jit(solution)/shard_map/ppermute | solution.py:34
  164.7 12.3 %collective-permute-start.6 = (bf16[4,128,768]{2,1,0:T(8,128)(2,1)}, bf16[4,128,768]{2,1,0:T(8,128)(2,1)S(1)}, u32[]{:S(2)}, u32[]{:S(2)}) collective-permute-start(bf16[4,128,768]{2,1,0:T(8,128)(2,1)} %collective-permute-done.5), channel_id=1, source_target_pairs={{0,1},{2,0},{4,2},{6,4},{7,6},{5,7},{3,5},{1,3},{8,9},{10,8},{12,1... | collective-permute-start | bytes 2359304 | tf_op jit(solution)/shard_map/ppermute | solution.py:38
  193.9 5.6 %collective-permute-start.7 = (bf16[512,128]{1,0:T(8,128)(2,1)S(1)}, bf16[512,128]{1,0:T(8,128)(2,1)S(1)}, u32[]{:S(2)}, u32[]{:S(2)}) collective-permute-start(bf16[512,128]{1,0:T(8,128)(2,1)S(1)} %bitcast.185), channel_id=1, source_target_pairs={{0,2},{2,4},{4,6},{6,7},{7,5},{5,3},{3,1},{1,0},{8,10},{10,12},{12... | collective-permute-start | bytes 393224 | tf_op jit(solution)/shard_map/ppermute | solution.py:34
  195.6 5.5 %collective-permute-start.11 = (bf16[512,128]{1,0:T(8,128)(2,1)S(1)}, bf16[512,128]{1,0:T(8,128)(2,1)S(1)}, u32[]{:S(2)}, u32[]{:S(2)}) collective-permute-start(bf16[512,128]{1,0:T(8,128)(2,1)S(1)} %bitcast.186), channel_id=1, source_target_pairs={{0,1},{2,0},{4,2},{6,4},{7,6},{5,7},{3,5},{1,3},{8,9},{10,8},{12,1... | collective-permute-start | bytes 393224 | tf_op jit(solution)/shard_map/ppermute | solution.py:38
  199.5 5.0 %collective-permute-start.8 = (bf16[512,128]{1,0:T(8,128)(2,1)S(1)}, bf16[512,128]{1,0:T(8,128)(2,1)S(1)}, u32[]{:S(2)}, u32[]{:S(2)}) collective-permute-start(bf16[512,128]{1,0:T(8,128)(2,1)S(1)} %collective-permute-done.7.refs_1_), channel_id=1, source_target_pairs={{0,2},{2,4},{4,6},{6,7},{7,5},{5,3},{3,1},{1,0},{8,10},{10,12},{12... | collective-permute-start | bytes 393224 | tf_op jit(solution)/shard_map/ppermute | solution.py:34
  201.1 5.0 %collective-permute-start.12 = (bf16[512,128]{1,0:T(8,128)(2,1)S(1)}, bf16[512,128]{1,0:T(8,128)(2,1)S(1)}, u32[]{:S(2)}, u32[]{:S(2)}) collective-permute-start(bf16[512,128]{1,0:T(8,128)(2,1)S(1)} %collective-permute-done.11.refs_5_), channel_id=1, source_target_pairs={{0,1},{2,0},{4,2},{6,4},{7,6},{5,7},{3,5},{1,3},{8,9},{10,8},{12,1... | collective-permute-start | bytes 393224 | tf_op jit(solution)/shard_map/ppermute | solution.py:38
  204.5 5.4 %collective-permute-start.9 = (bf16[512,128]{1,0:T(8,128)(2,1)S(1)}, bf16[512,128]{1,0:T(8,128)(2,1)S(1)}, u32[]{:S(2)}, u32[]{:S(2)}) collective-permute-start(bf16[512,128]{1,0:T(8,128)(2,1)S(1)} %collective-permute-done.8.refs_2_), channel_id=1, source_target_pairs={{0,2},{2,4},{4,6},{6,7},{7,5},{5,3},{3,1},{1,0},{8,10},{10,12},{12... | collective-permute-start | bytes 393224 | tf_op jit(solution)/shard_map/ppermute | solution.py:34
  206.1 6.0 %collective-permute-start.13 = (bf16[512,128]{1,0:T(8,128)(2,1)S(1)}, bf16[512,128]{1,0:T(8,128)(2,1)S(1)}, u32[]{:S(2)}, u32[]{:S(2)}) collective-permute-start(bf16[512,128]{1,0:T(8,128)(2,1)S(1)} %collective-permute-done.12.refs_6_), channel_id=1, source_target_pairs={{0,1},{2,0},{4,2},{6,4},{7,6},{5,7},{3,5},{1,3},{8,9},{10,8},{12,1... | collective-permute-start | bytes 393224 | tf_op jit(solution)/shard_map/ppermute | solution.py:38
  209.9 5.0 %collective-permute-start.10 = (bf16[512,128]{1,0:T(8,128)(2,1)S(1)}, bf16[512,128]{1,0:T(8,128)(2,1)S(1)}, u32[]{:S(2)}, u32[]{:S(2)}) collective-permute-start(bf16[512,128]{1,0:T(8,128)(2,1)S(1)} %collective-permute-done.9.refs_3_), channel_id=1, source_target_pairs={{0,2},{2,4},{4,6},{6,7},{7,5},{5,3},{3,1},{1,0},{8,10},{10,12},{12... | collective-permute-start | bytes 393224 | tf_op jit(solution)/shard_map/ppermute | solution.py:34
  215.5 23.3 %copy-start.24 = (f32[4,6144]{1,0:T(4,128)S(1)}, f32[4,6144]{1,0:T(4,128)}, u32[]{:S(2)}) copy-start(f32[4,6144]{1,0:T(4,128)} %get-tuple-element.32) | copy-start | bytes 294916
  258.1 7.8 %collective-permute-start.21 = (bf16[512,384]{1,0:T(8,128)(2,1)S(1)}, bf16[512,384]{1,0:T(8,128)(2,1)S(1)}, u32[]{:S(2)}, u32[]{:S(2)}) collective-permute-start(bf16[512,384]{1,0:T(8,128)(2,1)S(1)} %get-tuple-element.25), channel_id=1, source_target_pairs={{0,2},{2,4},{4,6},{6,7},{7,5},{5,3},{3,1},{1,0},{8,10},{10,12},{12... | collective-permute-start | bytes 1179656 | tf_op jit(solution)/shard_map/ppermute | solution.py:61
  259.7 7.8 %collective-permute-start.28 = (bf16[512,384]{1,0:T(8,128)(2,1)S(1)}, bf16[512,384]{1,0:T(8,128)(2,1)S(1)}, u32[]{:S(2)}, u32[]{:S(2)}) collective-permute-start(bf16[512,384]{1,0:T(8,128)(2,1)S(1)} %get-tuple-element.26), channel_id=1, source_target_pairs={{0,1},{2,0},{4,2},{6,4},{7,6},{5,7},{3,5},{1,3},{8,9},{10,8},{12,1... | collective-permute-start | bytes 1179656 | tf_op jit(solution)/shard_map/ppermute | solution.py:63
  268.8 8.5 %collective-permute-start.22 = (bf16[512,384]{1,0:T(8,128)(2,1)S(1)}, bf16[512,384]{1,0:T(8,128)(2,1)S(1)}, u32[]{:S(2)}, u32[]{:S(2)}) collective-permute-start(bf16[512,384]{1,0:T(8,128)(2,1)S(1)} %get-tuple-element.23), channel_id=1, source_target_pairs={{0,2},{2,4},{4,6},{6,7},{7,5},{5,3},{3,1},{1,0},{8,10},{10,12},{12... | collective-permute-start | bytes 1179656 | tf_op jit(solution)/shard_map/ppermute | solution.py:61
  270.5 10.3 %collective-permute-start.29 = (bf16[512,384]{1,0:T(8,128)(2,1)S(1)}, bf16[512,384]{1,0:T(8,128)(2,1)S(1)}, u32[]{:S(2)}, u32[]{:S(2)}) collective-permute-start(bf16[512,384]{1,0:T(8,128)(2,1)S(1)} %get-tuple-element.24), channel_id=1, source_target_pairs={{0,1},{2,0},{4,2},{6,4},{7,6},{5,7},{3,5},{1,3},{8,9},{10,8},{12,1... | collective-permute-start | bytes 1179656 | tf_op jit(solution)/shard_map/ppermute | solution.py:63
  282.1 11.9 %collective-permute-start.23 = (bf16[512,384]{1,0:T(8,128)(2,1)S(1)}, bf16[512,384]{1,0:T(8,128)(2,1)S(1)}, u32[]{:S(2)}, u32[]{:S(2)}) collective-permute-start(bf16[512,384]{1,0:T(8,128)(2,1)S(1)} %get-tuple-element.21), channel_id=1, source_target_pairs={{0,2},{2,4},{4,6},{6,7},{7,5},{5,3},{3,1},{1,0},{8,10},{10,12},{12... | collective-permute-start | bytes 1179656 | tf_op jit(solution)/shard_map/ppermute | solution.py:61
  284.9 11.8 %collective-permute-start.30 = (bf16[512,384]{1,0:T(8,128)(2,1)S(1)}, bf16[512,384]{1,0:T(8,128)(2,1)S(1)}, u32[]{:S(2)}, u32[]{:S(2)}) collective-permute-start(bf16[512,384]{1,0:T(8,128)(2,1)S(1)} %get-tuple-element.22), channel_id=1, source_target_pairs={{0,1},{2,0},{4,2},{6,4},{7,6},{5,7},{3,5},{1,3},{8,9},{10,8},{12,1... | collective-permute-start | bytes 1179656 | tf_op jit(solution)/shard_map/ppermute | solution.py:63
  298.0 11.2 %collective-permute-start.24 = (bf16[512,384]{1,0:T(8,128)(2,1)S(1)}, bf16[512,384]{1,0:T(8,128)(2,1)S(1)}, u32[]{:S(2)}, u32[]{:S(2)}) collective-permute-start(bf16[512,384]{1,0:T(8,128)(2,1)S(1)} %get-tuple-element.19), channel_id=1, source_target_pairs={{0,2},{2,4},{4,6},{6,7},{7,5},{5,3},{3,1},{1,0},{8,10},{10,12},{12... | collective-permute-start | bytes 1179656 | tf_op jit(solution)/shard_map/ppermute | solution.py:61
  299.1 10.8 %collective-permute-start.31 = (bf16[512,384]{1,0:T(8,128)(2,1)S(1)}, bf16[512,384]{1,0:T(8,128)(2,1)S(1)}, u32[]{:S(2)}, u32[]{:S(2)}) collective-permute-start(bf16[512,384]{1,0:T(8,128)(2,1)S(1)} %get-tuple-element.20), channel_id=1, source_target_pairs={{0,1},{2,0},{4,2},{6,4},{7,6},{5,7},{3,5},{1,3},{8,9},{10,8},{12,1... | collective-permute-start | bytes 1179656 | tf_op jit(solution)/shard_map/ppermute | solution.py:63
  311.3 10.0 %collective-permute-start.25 = (bf16[512,384]{1,0:T(8,128)(2,1)S(1)}, bf16[512,384]{1,0:T(8,128)(2,1)S(1)}, u32[]{:S(2)}, u32[]{:S(2)}) collective-permute-start(bf16[512,384]{1,0:T(8,128)(2,1)S(1)} %get-tuple-element.17), channel_id=1, source_target_pairs={{0,2},{2,4},{4,6},{6,7},{7,5},{5,3},{3,1},{1,0},{8,10},{10,12},{12... | collective-permute-start | bytes 1179656 | tf_op jit(solution)/shard_map/ppermute | solution.py:61
  311.7 10.0 %collective-permute-start.32 = (bf16[512,384]{1,0:T(8,128)(2,1)S(1)}, bf16[512,384]{1,0:T(8,128)(2,1)S(1)}, u32[]{:S(2)}, u32[]{:S(2)}) collective-permute-start(bf16[512,384]{1,0:T(8,128)(2,1)S(1)} %get-tuple-element.18), channel_id=1, source_target_pairs={{0,1},{2,0},{4,2},{6,4},{7,6},{5,7},{3,5},{1,3},{8,9},{10,8},{12,1... | collective-permute-start | bytes 1179656 | tf_op jit(solution)/shard_map/ppermute | solution.py:63
  322.9 9.1 %collective-permute-start.26 = (bf16[512,384]{1,0:T(8,128)(2,1)S(1)}, bf16[512,384]{1,0:T(8,128)(2,1)S(1)}, u32[]{:S(2)}, u32[]{:S(2)}) collective-permute-start(bf16[512,384]{1,0:T(8,128)(2,1)S(1)} %get-tuple-element.15), channel_id=1, source_target_pairs={{0,2},{2,4},{4,6},{6,7},{7,5},{5,3},{3,1},{1,0},{8,10},{10,12},{12... | collective-permute-start | bytes 1179656 | tf_op jit(solution)/shard_map/ppermute | solution.py:61
  323.4 8.9 %collective-permute-start.33 = (bf16[512,384]{1,0:T(8,128)(2,1)S(1)}, bf16[512,384]{1,0:T(8,128)(2,1)S(1)}, u32[]{:S(2)}, u32[]{:S(2)}) collective-permute-start(bf16[512,384]{1,0:T(8,128)(2,1)S(1)} %get-tuple-element.16), channel_id=1, source_target_pairs={{0,1},{2,0},{4,2},{6,4},{7,6},{5,7},{3,5},{1,3},{8,9},{10,8},{12,1... | collective-permute-start | bytes 1179656 | tf_op jit(solution)/shard_map/ppermute | solution.py:63
  333.6 7.8 %collective-permute-start.27 = (bf16[512,384]{1,0:T(8,128)(2,1)S(1)}, bf16[512,384]{1,0:T(8,128)(2,1)S(1)}, u32[]{:S(2)}, u32[]{:S(2)}) collective-permute-start(bf16[512,384]{1,0:T(8,128)(2,1)S(1)} %get-tuple-element.13), channel_id=1, source_target_pairs={{0,2},{2,4},{4,6},{6,7},{7,5},{5,3},{3,1},{1,0},{8,10},{10,12},{12... | collective-permute-start | bytes 1179656 | tf_op jit(solution)/shard_map/ppermute | solution.py:61
  334.4 7.8 %collective-permute-start.34 = (bf16[512,384]{1,0:T(8,128)(2,1)S(1)}, bf16[512,384]{1,0:T(8,128)(2,1)S(1)}, u32[]{:S(2)}, u32[]{:S(2)}) collective-permute-start(bf16[512,384]{1,0:T(8,128)(2,1)S(1)} %get-tuple-element.14), channel_id=1, source_target_pairs={{0,1},{2,0},{4,2},{6,4},{7,6},{5,7},{3,5},{1,3},{8,9},{10,8},{12,1... | collective-permute-start | bytes 1179656 | tf_op jit(solution)/shard_map/ppermute | solution.py:63
  (19 other events, 180.2 us)
Sparse Core Ops, SparseCore 0:
  87.6 25.6 all-gather.8
  114.9 17.1 all-gather.4
  133.7 17.9 all-gather.6

commit v18 on v15

--- a/solution.py
+++ b/solution.py
@@ -225,10 +225,15 @@
         w_out_part = lax.dynamic_slice_in_dim(w_out, span_index * column_part, column_part, 1)
         mine_blocks = ring_gather(w_out_part, "tp", tp_count)
         other_blocks = [lax.ppermute(b, "span", [(0, 1), (1, 0)]) for b in mine_blocks]
-    up_full, down_full = (
-        lax.all_gather(w_up, "span", axis=1, tiled=True),
-        lax.all_gather(w_down, "span", axis=0, tiled=True),
-    )
+    if gather_weights:
+        swap = [(0, 1), (1, 0)]
+        up_full = jnp.concatenate([w_up, lax.ppermute(w_up, "span", swap)], axis=1)
+        down_full = jnp.concatenate([w_down, lax.ppermute(w_down, "span", swap)], axis=0)
+    else:
+        up_full, down_full = (
+            lax.all_gather(w_up, "span", axis=1, tiled=True),
+            lax.all_gather(w_down, "span", axis=0, tiled=True),
+        )
     mod_table = modulation.reshape(modulation.shape[0], -1)
     picker = (jnp.arange(mod_table.shape[0], dtype=jnp.int32)[None, :] == levels[:, None]).astype(
         jnp.bfloat16

time: 326 us -> 326 us (level)
  between operations: 32.8 us -> 18.4 us
  waiting for transfers between devices: 159 us -> 170 us
    ppermute x12, waiting for transfers between devices: 78.7 us -> 89.3 us  [ring_gather(): forward = lax.ppermute(forward, axis_name, ahead)]
    dot_general x1 -> x0, matrix products: 10 us -> none  [local(): pre_act = jnp.dot(mlp_in, up_full, preferred_element_type=jnp.float32)]
    dot_general x1, matrix products: 6.6 us -> 15.5 us  [local(): jnp.dot(hidden_units, down_full, preferred_element_type=jnp.float32)]
    unnamed x59 -> x51, local copies, waits for them, and re-layouts: 10.3 us -> 9.02 us
  transfers between devices with their start and end apart: 45 -> 45, of which waited for: 25 -> 25; matrix products, arithmetic and copies ran while one was open for 13% -> 12% of each run, Pallas kernels for 7% -> 7%
where the time goes in v18:
time: 326 us; the launch traced here: 325 us
  waiting for transfers between devices  170 us (52%)
  starting transfers between devices  40.6 us (12%)
  matrix products  24.8 us (8%)
  local copies, waits for them, and re-layouts  23.2 us (7%)
  other arithmetic  22 us (7%)
  Pallas kernels  21.6 us (7%)
  between operations  18.4 us (6%)
  blocking collectives  4.36 us (1%)
    ppermute x12, waiting for transfers between devices, ring_gather(): forward = lax.ppermute(forward, axis_name, ahead)  89.3 us
    ppermute x7, waiting for transfers between devices, ring_reduce_scatter(): lax.ppermute(forward.astype(jnp.bfloat16), axis_name, ahead)  51.9 us
    ppermute x9, waiting for transfers between devices, ring_gather(): backward = lax.ppermute(backward, axis_name, behind)  22.3 us
    pallas_call x1, Pallas kernels, grouped_out_proj(): pl.pallas_call(functools.partial(out_proj_kernel, group_count, tiles_per_...  21.6 us
    ppermute x12, starting transfers between devices, ring_gather(): forward = lax.ppermute(forward, axis_name, ahead)  21.3 us
    dot_general x1, matrix products, local(): jnp.dot(hidden_units, down_full, preferred_element_type=jnp.float32)  15.5 us
    unnamed x51, local copies, waits for them, and re-layouts  9.02 us
    ppermute x7, starting transfers between devices, ring_reduce_scatter(): lax.ppermute(backward.astype(jnp.bfloat16), axis_name, behind)  8.95 us
  transfers between devices with their start and end apart: 45, of which 25 were waited for; matrix products, arithmetic and copies ran while one was open for 12% of the time, Pallas kernels for 7%

profile of v18, /device:TPU:0, one launch (start us, length us, event | category | flops | bytes accessed | tf_op | source)
XLA Modules:
  0.0 325.0 jit_solution(17314738926885593539)
XLA Ops:
  0.0 3.0 collective-permute-start
  3.1 2.1 collective-permute-start.14
  7.9 13.7 %collective-permute-done = bf16[4,128,768]{2,1,0:T(8,128)(2,1)} collective-permute-done((bf16[4,128,768]{2,1,0:T(8,128)(2,1)}, bf16[4,128,768]{2,1,0:T(8,128)(2,1)}, u32[]{:S(2)}, u32[]{:S(2)}) %collective-permute-start) | collective-permute-done | bytes 786464 | tf_op jit(solution)/shard_map/ppermute | solution.py:34
  21.7 2.1 collective-permute-start.1
  25.5 29.0 %collective-permute-done.1 = bf16[4,128,768]{2,1,0:T(8,128)(2,1)S(1)} collective-permute-done((bf16[4,128,768]{2,1,0:T(8,128)(2,1)}, bf16[4,128,768]{2,1,0:T(8,128)(2,1)S(1)}, u32[]{:S(2)}, u32[]{:S(2)}) %collective-permute-start.1) | collective-permute-done | bytes 786464 | tf_op jit(solution)/shard_map/ppermute | solution.py:34
  54.4 1.8 collective-permute-start.2
  60.1 2.2 all_gather.6
  62.4 10.9 %collective-permute-done.2 = bf16[4,128,768]{2,1,0:T(8,128)(2,1)} collective-permute-done((bf16[4,128,768]{2,1,0:T(8,128)(2,1)S(1)}, bf16[4,128,768]{2,1,0:T(8,128)(2,1)}, u32[]{:S(2)}, u32[]{:S(2)}) %collective-permute-start.2) | collective-permute-done | bytes 786464 | tf_op jit(solution)/shard_map/ppermute | solution.py:34
  73.3 1.5 collective-permute-start.3
  82.5 1.9 fusion.50
  89.4 6.7 %copy.30 = bf16[6144,3,128]{0,2,1:T(8,128)(2,1)} copy(bf16[6144,3,128]{2,0,1:T(8,128)(2,1)} %param.22) | data formatting | bytes 9437184 | tf_op args[7]
  97.1 1.6 collective-permute-start.15
  107.3 7.4 %collective-permute-done.15.refs_10_ = bf16[128,3072]{1,0:T(8,128)(2,1)} collective-permute-done((bf16[128,3072]{1,0:T(8,128)(2,1)}, bf16[128,3072]{1,0:T(8,128)(2,1)}, u32[]{:S(2)}, u32[]{:S(2)}) %collective-permute-start.15) | collective-permute-done | bytes 786464 | tf_op jit(solution)/shard_map/ppermute | solution.py:34
  114.7 4.7 %collective-permute-done.6 = bf16[4,128,768]{2,1,0:T(8,128)(2,1)S(1)} collective-permute-done((bf16[4,128,768]{2,1,0:T(8,128)(2,1)}, bf16[4,128,768]{2,1,0:T(8,128)(2,1)S(1)}, u32[]{:S(2)}, u32[]{:S(2)}) %collective-permute-start.6) | collective-permute-done | bytes 786464 | tf_op jit(solution)/shard_map/ppermute | solution.py:38
  119.5 1.6 collective-permute-start.16
  122.5 2.7 fusion.3
  125.2 5.8 %convolution_convert_fusion.1 = bf16[512,384]{1,0:T(8,128)(2,1)S(1)} fusion(bf16[512,6144]{1,0:T(8,128)(2,1)S(1)} %bitcast.153, bf16[6144,384]{0,1:T(8,128)(2,1)} %bitcast.154), kind=kOutput, calls=%fused_computation.31 | convolution fusion | flops 2416115712 | bytes 11403264 | tf_op jit(solution)/shard_map/dot_general | solution.py:248
  131.8 2.2 all_gather.7
  137.3 17.5 %collective-permute-done.20.refs_15_ = bf16[128,3072]{1,0:T(8,128)(2,1)S(1)} collective-permute-done((bf16[128,3072]{1,0:T(8,128)(2,1)}, bf16[128,3072]{1,0:T(8,128)(2,1)S(1)}, u32[]{:S(2)}, u32[]{:S(2)}) %collective-permute-start.20) | collective-permute-done | bytes 786464 | tf_op jit(solution)/shard_map/ppermute | solution.py:38
  154.8 1.5 collective-permute-start.17
  158.2 15.7 %collective-permute-done.17.refs_12_ = bf16[128,3072]{1,0:T(8,128)(2,1)S(1)} collective-permute-done((bf16[128,3072]{1,0:T(8,128)(2,1)}, bf16[128,3072]{1,0:T(8,128)(2,1)S(1)}, u32[]{:S(2)}, u32[]{:S(2)}) %collective-permute-start.17) | collective-permute-done | bytes 786464 | tf_op jit(solution)/shard_map/ppermute | solution.py:34
  174.5 1.6 collective-permute-start.7
  176.6 3.8 %collective-permute-done.7.refs_1_ = bf16[512,128]{1,0:T(8,128)(2,1)S(1)} collective-permute-done((bf16[512,128]{1,0:T(8,128)(2,1)S(1)}, bf16[512,128]{1,0:T(8,128)(2,1)S(1)}, u32[]{:S(2)}, u32[]{:S(2)}) %collective-permute-start.7) | collective-permute-done | bytes 131104 | tf_op jit(solution)/shard_map/ppermute | solution.py:34
  180.4 1.5 collective-permute-start.8
  182.5 3.1 collective-permute-done.8.refs_2_
  185.6 1.5 collective-permute-start.9
  187.6 2.9 collective-permute-done.9.refs_3_
  190.5 1.5 collective-permute-start.10
  192.8 2.7 collective-permute-done.10.refs_4_
  196.5 21.6 %shard_map.145 = (f32[512,6144]{1,0:T(8,128)}, f32[512,128]{1,0:T(8,128)}) custom-call(s32[1]{0:T(128)} %bitcast.span_ref, bf16[512,128]{1,0:T(8,128)(2,1)} %bitcast.166, bf16[512,128]{1,0:T(8,128)(2,1)} %copy-done.15, bf16[512,128]{1,0:T(8,128)(2,1)} %copy-done.17, bf16[512,128]{1,0:T(8,128)(2,1)} %copy-done.19, bf16[512,128]{1,0:T(8,128)(2,1)} %copy-done.21, ...), custom_call_target="tpu_custom_call" | custom-call | flops 6442450944 | bytes 32505856 | tf_op jit(solution)/shard_map/pallas_call | solution.py:134
  219.2 15.5 %convolution_convert_fusion = bf16[4,128,6144]{2,1,0:T(8,128)(2,1)} fusion(bf16[256,6144]{1,0:T(8,128)(2,1)} %collective-permute-done.30, bf16[256,6144]{1,0:T(8,128)(2,1)} %param.25, bf16[6144,256]{1,0:T(8,128)(2,1)} %collective-permute-done.29, bf16[6144,256]{1,0:T(8,128)(2,1)} %param.24, f32[4,128,6144]{2,1,0:T(8,128)} %bitcast.159, ...), kind=kOutput, calls=%fused_computation.7 | convolution fusion | flops 6485704704 | bytes 31655936 | tf_op jit(solution)/shard_map/dot_general | solution.py:303
  236.0 1.6 collective-permute-start.31
  239.3 4.5 %collective-permute-done.31 = bf16[512,384]{1,0:T(8,128)(2,1)S(1)} collective-permute-done((bf16[512,384]{1,0:T(8,128)(2,1)S(1)}, bf16[512,384]{1,0:T(8,128)(2,1)S(1)}, u32[]{:S(2)}, u32[]{:S(2)}) %collective-permute-start.31) | collective-permute-done | bytes 393248 | tf_op jit(solution)/shard_map/ppermute | solution.py:61
  243.8 2.0 collective-permute-done.38
  250.4 6.1 %collective-permute-done.32 = bf16[512,384]{1,0:T(8,128)(2,1)S(1)} collective-permute-done((bf16[512,384]{1,0:T(8,128)(2,1)S(1)}, bf16[512,384]{1,0:T(8,128)(2,1)S(1)}, u32[]{:S(2)}, u32[]{:S(2)}) %collective-permute-start.32) | collective-permute-done | bytes 393248 | tf_op jit(solution)/shard_map/ppermute | solution.py:61
  259.4 1.6 collective-permute-start.40
  261.6 8.3 %collective-permute-done.33 = bf16[512,384]{1,0:T(8,128)(2,1)S(1)} collective-permute-done((bf16[512,384]{1,0:T(8,128)(2,1)S(1)}, bf16[512,384]{1,0:T(8,128)(2,1)S(1)}, u32[]{:S(2)}, u32[]{:S(2)}) %collective-permute-start.33) | collective-permute-done | bytes 393248 | tf_op jit(solution)/shard_map/ppermute | solution.py:61
  272.0 2.0 collective-permute-start.41
  274.0 9.5 %collective-permute-done.34 = bf16[512,384]{1,0:T(8,128)(2,1)S(1)} collective-permute-done((bf16[512,384]{1,0:T(8,128)(2,1)S(1)}, bf16[512,384]{1,0:T(8,128)(2,1)S(1)}, u32[]{:S(2)}, u32[]{:S(2)}) %collective-permute-start.34) | collective-permute-done | bytes 393248 | tf_op jit(solution)/shard_map/ppermute | solution.py:61
  285.2 1.8 collective-permute-start.42
  287.1 8.8 %collective-permute-done.35 = bf16[512,384]{1,0:T(8,128)(2,1)S(1)} collective-permute-done((bf16[512,384]{1,0:T(8,128)(2,1)S(1)}, bf16[512,384]{1,0:T(8,128)(2,1)S(1)}, u32[]{:S(2)}, u32[]{:S(2)}) %collective-permute-start.35) | collective-permute-done | bytes 393248 | tf_op jit(solution)/shard_map/ppermute | solution.py:61
  299.4 8.8 %collective-permute-done.36 = bf16[512,384]{1,0:T(8,128)(2,1)S(1)} collective-permute-done((bf16[512,384]{1,0:T(8,128)(2,1)S(1)}, bf16[512,384]{1,0:T(8,128)(2,1)S(1)}, u32[]{:S(2)}, u32[]{:S(2)}) %collective-permute-start.36) | collective-permute-done | bytes 393248 | tf_op jit(solution)/shard_map/ppermute | solution.py:61
  309.0 2.2 add_convert_fusion.13
  311.2 1.7 collective-permute-start.37
  313.2 6.0 %collective-permute-done.37 = bf16[512,384]{1,0:T(8,128)(2,1)S(1)} collective-permute-done((bf16[512,384]{1,0:T(8,128)(2,1)}, bf16[512,384]{1,0:T(8,128)(2,1)S(1)}, u32[]{:S(2)}, u32[]{:S(2)}) %collective-permute-start.37) | collective-permute-done | bytes 393248 | tf_op jit(solution)/shard_map/ppermute | solution.py:61
  319.2 1.6 collective-permute-done.44
  320.8 1.4 convert_add_fusion.1
  322.3 2.6 add_convert_fusion.2
  (148 shorter events, 44.6 us)
Async XLA Ops:
  0.0 21.6 %collective-permute-start = (bf16[4,128,768]{2,1,0:T(8,128)(2,1)}, bf16[4,128,768]{2,1,0:T(8,128)(2,1)}, u32[]{:S(2)}, u32[]{:S(2)}) collective-permute-start(bf16[4,128,768]{2,1,0:T(8,128)(2,1)} %param.15), channel_id=1, source_target_pairs={{0,2},{2,4},{4,6},{6,7},{7,5},{5,3},{3,1},{1,0},{8,10},{10,12},{12... | collective-permute-start | bytes 2359304 | tf_op jit(solution)/shard_map/ppermute | solution.py:34
  3.0 53.3 %collective-permute-start.4 = (bf16[4,128,768]{2,1,0:T(8,128)(2,1)}, bf16[4,128,768]{2,1,0:T(8,128)(2,1)}, u32[]{:S(2)}, u32[]{:S(2)}) collective-permute-start(bf16[4,128,768]{2,1,0:T(8,128)(2,1)} %param.15), channel_id=1, source_target_pairs={{0,1},{2,0},{4,2},{6,4},{7,6},{5,7},{3,5},{1,3},{8,9},{10,8},{12,1... | collective-permute-start | bytes 2359304 | tf_op jit(solution)/shard_map/ppermute | solution.py:38
  3.1 93.0 %copy-start.4 = (bf16[128,3072]{1,0:T(8,128)(2,1)}, bf16[128,3072]{1,0:T(8,128)(2,1)S(1)}, u32[]{:S(2)}) copy-start(bf16[128,3072]{1,0:T(8,128)(2,1)S(1)} %constant_dynamic-slice_fusion.2.refs_8_) | copy-start | bytes 2359300
  3.1 94.0 %collective-permute-start.14 = (bf16[128,3072]{1,0:T(8,128)(2,1)S(1)}, bf16[128,3072]{1,0:T(8,128)(2,1)}, u32[]{:S(2)}, u32[]{:S(2)}) collective-permute-start(bf16[128,3072]{1,0:T(8,128)(2,1)S(1)} %constant_dynamic-slice_fusion.2.refs_8_), channel_id=1, source_target_pairs={{0,2},{2,4},{4,6},{6,7},{7,5},{5,3},{3,1},{1,0},{8,10},{10,12},{12... | collective-permute-start | bytes 2359304 | tf_op jit(solution)/shard_map/ppermute | solution.py:34
  5.2 97.8 %collective-permute-start.18 = (bf16[128,3072]{1,0:T(8,128)(2,1)S(1)}, bf16[128,3072]{1,0:T(8,128)(2,1)}, u32[]{:S(2)}, u32[]{:S(2)}) collective-permute-start(bf16[128,3072]{1,0:T(8,128)(2,1)S(1)} %constant_dynamic-slice_fusion.2.refs_8_), channel_id=1, source_target_pairs={{0,1},{2,0},{4,2},{6,4},{7,6},{5,7},{3,5},{1,3},{8,9},{10,8},{12,1... | collective-permute-start | bytes 2359304 | tf_op jit(solution)/shard_map/ppermute | solution.py:38
  5.2 128.9 %collective-permute-start.21 = (bf16[128,3072]{1,0:T(8,128)(2,1)S(1)}, bf16[128,3072]{1,0:T(8,128)(2,1)}, u32[]{:S(2)}, u32[]{:S(2)}) collective-permute-start(bf16[128,3072]{1,0:T(8,128)(2,1)S(1)} %constant_dynamic-slice_fusion.2.refs_8_), channel_id=1, source_target_pairs={{0,8},{8,0},{1,9},{9,1},{2,10},{10,2},{3,11},{11,3},{4,12},{12,4},... | collective-permute-start | bytes 2359304 | tf_op jit(solution)/shard_map/ppermute | solution.py:227
  21.7 32.8 %collective-permute-start.1 = (bf16[4,128,768]{2,1,0:T(8,128)(2,1)}, bf16[4,128,768]{2,1,0:T(8,128)(2,1)S(1)}, u32[]{:S(2)}, u32[]{:S(2)}) collective-permute-start(bf16[4,128,768]{2,1,0:T(8,128)(2,1)} %collective-permute-done), channel_id=1, source_target_pairs={{0,2},{2,4},{4,6},{6,7},{7,5},{5,3},{3,1},{1,0},{8,10},{10,12},{12... | collective-permute-start | bytes 2359304 | tf_op jit(solution)/shard_map/ppermute | solution.py:34
  54.4 34.9 %copy-start.5 = (bf16[4,128,768]{2,1,0:T(8,128)(2,1)}, bf16[4,128,768]{2,1,0:T(8,128)(2,1)S(1)}, u32[]{:S(2)}) copy-start(bf16[4,128,768]{2,1,0:T(8,128)(2,1)S(1)} %collective-permute-done.1) | copy-start | bytes 2359300
  54.4 18.8 %collective-permute-start.2 = (bf16[4,128,768]{2,1,0:T(8,128)(2,1)S(1)}, bf16[4,128,768]{2,1,0:T(8,128)(2,1)}, u32[]{:S(2)}, u32[]{:S(2)}) collective-permute-start(bf16[4,128,768]{2,1,0:T(8,128)(2,1)S(1)} %collective-permute-done.1), channel_id=1, source_target_pairs={{0,2},{2,4},{4,6},{6,7},{7,5},{5,3},{3,1},{1,0},{8,10},{10,12},{12... | collective-permute-start | bytes 2359304 | tf_op jit(solution)/shard_map/ppermute | solution.py:34
  56.3 42.5 %collective-permute-start.5 = (bf16[4,128,768]{2,1,0:T(8,128)(2,1)}, bf16[4,128,768]{2,1,0:T(8,128)(2,1)}, u32[]{:S(2)}, u32[]{:S(2)}) collective-permute-start(bf16[4,128,768]{2,1,0:T(8,128)(2,1)} %collective-permute-done.4), channel_id=1, source_target_pairs={{0,1},{2,0},{4,2},{6,4},{7,6},{5,7},{3,5},{1,3},{8,9},{10,8},{12,1... | collective-permute-start | bytes 2359304 | tf_op jit(solution)/shard_map/ppermute | solution.py:38
  73.3 29.8 %collective-permute-start.3 = (bf16[4,128,768]{2,1,0:T(8,128)(2,1)}, bf16[4,128,768]{2,1,0:T(8,128)(2,1)}, u32[]{:S(2)}, u32[]{:S(2)}) collective-permute-start(bf16[4,128,768]{2,1,0:T(8,128)(2,1)} %collective-permute-done.2), channel_id=1, source_target_pairs={{0,2},{2,4},{4,6},{6,7},{7,5},{5,3},{3,1},{1,0},{8,10},{10,12},{12... | collective-permute-start | bytes 2359304 | tf_op jit(solution)/shard_map/ppermute | solution.py:34
  97.1 17.6 %collective-permute-start.15 = (bf16[128,3072]{1,0:T(8,128)(2,1)}, bf16[128,3072]{1,0:T(8,128)(2,1)}, u32[]{:S(2)}, u32[]{:S(2)}) collective-permute-start(bf16[128,3072]{1,0:T(8,128)(2,1)} %collective-permute-done.14.refs_9_), channel_id=1, source_target_pairs={{0,2},{2,4},{4,6},{6,7},{7,5},{5,3},{3,1},{1,0},{8,10},{10,12},{12... | collective-permute-start | bytes 2359304 | tf_op jit(solution)/shard_map/ppermute | solution.py:34
  98.8 20.7 %collective-permute-start.6 = (bf16[4,128,768]{2,1,0:T(8,128)(2,1)}, bf16[4,128,768]{2,1,0:T(8,128)(2,1)S(1)}, u32[]{:S(2)}, u32[]{:S(2)}) collective-permute-start(bf16[4,128,768]{2,1,0:T(8,128)(2,1)} %collective-permute-done.5), channel_id=1, source_target_pairs={{0,1},{2,0},{4,2},{6,4},{7,6},{5,7},{3,5},{1,3},{8,9},{10,8},{12,1... | collective-permute-start | bytes 2359304 | tf_op jit(solution)/shard_map/ppermute | solution.py:38
  102.9 31.7 %collective-permute-start.22 = (bf16[128,3072]{1,0:T(8,128)(2,1)}, bf16[128,3072]{1,0:T(8,128)(2,1)}, u32[]{:S(2)}, u32[]{:S(2)}) collective-permute-start(bf16[128,3072]{1,0:T(8,128)(2,1)} %collective-permute-done.14.refs_9_), channel_id=1, source_target_pairs={{0,8},{8,0},{1,9},{9,1},{2,10},{10,2},{3,11},{11,3},{4,12},{12,4},... | collective-permute-start | bytes 2359304 | tf_op jit(solution)/shard_map/ppermute | solution.py:227
  103.0 31.2 %collective-permute-start.19 = (bf16[128,3072]{1,0:T(8,128)(2,1)}, bf16[128,3072]{1,0:T(8,128)(2,1)}, u32[]{:S(2)}, u32[]{:S(2)}) collective-permute-start(bf16[128,3072]{1,0:T(8,128)(2,1)} %collective-permute-done.18.refs_13_), channel_id=1, source_target_pairs={{0,1},{2,0},{4,2},{6,4},{7,6},{5,7},{3,5},{1,3},{8,9},{10,8},{12,1... | collective-permute-start | bytes 2359304 | tf_op jit(solution)/shard_map/ppermute | solution.py:38
  114.7 20.1 %collective-permute-start.26 = (bf16[128,3072]{1,0:T(8,128)(2,1)}, bf16[128,3072]{1,0:T(8,128)(2,1)}, u32[]{:S(2)}, u32[]{:S(2)}) collective-permute-start(bf16[128,3072]{1,0:T(8,128)(2,1)} %collective-permute-done.18.refs_13_), channel_id=1, source_target_pairs={{0,8},{8,0},{1,9},{9,1},{2,10},{10,2},{3,11},{11,3},{4,12},{12,4},... | collective-permute-start | bytes 2359304 | tf_op jit(solution)/shard_map/ppermute | solution.py:227
  119.5 15.9 %collective-permute-start.16 = (bf16[128,3072]{1,0:T(8,128)(2,1)}, bf16[128,3072]{1,0:T(8,128)(2,1)}, u32[]{:S(2)}, u32[]{:S(2)}) collective-permute-start(bf16[128,3072]{1,0:T(8,128)(2,1)} %collective-permute-done.15.refs_10_), channel_id=1, source_target_pairs={{0,2},{2,4},{4,6},{6,7},{7,5},{5,3},{3,1},{1,0},{8,10},{10,12},{12... | collective-permute-start | bytes 2359304 | tf_op jit(solution)/shard_map/ppermute | solution.py:34
  134.1 85.1 %collective-permute-start.29 = (bf16[6144,256]{1,0:T(8,128)(2,1)}, bf16[6144,256]{1,0:T(8,128)(2,1)}, u32[]{:S(2)}, u32[]{:S(2)}) collective-permute-start(bf16[6144,256]{1,0:T(8,128)(2,1)} %param.24), channel_id=1, source_target_pairs={{0,8},{8,0},{1,9},{9,1},{2,10},{10,2},{3,11},{11,3},{4,12},{12,4},... | collective-permute-start | bytes 9437192 | tf_op jit(solution)/shard_map/ppermute | solution.py:230
  134.3 84.9 %collective-permute-start.30 = (bf16[256,6144]{1,0:T(8,128)(2,1)}, bf16[256,6144]{1,0:T(8,128)(2,1)}, u32[]{:S(2)}, u32[]{:S(2)}) collective-permute-start(bf16[256,6144]{1,0:T(8,128)(2,1)} %param.25), channel_id=1, source_target_pairs={{0,8},{8,0},{1,9},{9,1},{2,10},{10,2},{3,11},{11,3},{4,12},{12,4},... | collective-permute-start | bytes 9437192 | tf_op jit(solution)/shard_map/ppermute | solution.py:231
  134.7 21.7 %collective-permute-start.23 = (bf16[128,3072]{1,0:T(8,128)(2,1)}, bf16[128,3072]{1,0:T(8,128)(2,1)S(1)}, u32[]{:S(2)}, u32[]{:S(2)}) collective-permute-start(bf16[128,3072]{1,0:T(8,128)(2,1)} %collective-permute-done.15.refs_10_), channel_id=1, source_target_pairs={{0,8},{8,0},{1,9},{9,1},{2,10},{10,2},{3,11},{11,3},{4,12},{12,4},... | collective-permute-start | bytes 2359304 | tf_op jit(solution)/shard_map/ppermute | solution.py:227
  134.8 20.0 %collective-permute-start.20 = (bf16[128,3072]{1,0:T(8,128)(2,1)}, bf16[128,3072]{1,0:T(8,128)(2,1)S(1)}, u32[]{:S(2)}, u32[]{:S(2)}) collective-permute-start(bf16[128,3072]{1,0:T(8,128)(2,1)} %collective-permute-done.19.refs_14_), channel_id=1, source_target_pairs={{0,1},{2,0},{4,2},{6,4},{7,6},{5,7},{3,5},{1,3},{8,9},{10,8},{12,1... | collective-permute-start | bytes 2359304 | tf_op jit(solution)/shard_map/ppermute | solution.py:38
  135.4 21.0 %collective-permute-start.27 = (bf16[128,3072]{1,0:T(8,128)(2,1)}, bf16[128,3072]{1,0:T(8,128)(2,1)S(1)}, u32[]{:S(2)}, u32[]{:S(2)}) collective-permute-start(bf16[128,3072]{1,0:T(8,128)(2,1)} %collective-permute-done.19.refs_14_), channel_id=1, source_target_pairs={{0,8},{8,0},{1,9},{9,1},{2,10},{10,2},{3,11},{11,3},{4,12},{12,4},... | collective-permute-start | bytes 2359304 | tf_op jit(solution)/shard_map/ppermute | solution.py:227
  154.8 19.1 %collective-permute-start.17 = (bf16[128,3072]{1,0:T(8,128)(2,1)}, bf16[128,3072]{1,0:T(8,128)(2,1)S(1)}, u32[]{:S(2)}, u32[]{:S(2)}) collective-permute-start(bf16[128,3072]{1,0:T(8,128)(2,1)} %collective-permute-done.16.refs_11_), channel_id=1, source_target_pairs={{0,2},{2,4},{4,6},{6,7},{7,5},{5,3},{3,1},{1,0},{8,10},{10,12},{12... | collective-permute-start | bytes 2359304 | tf_op jit(solution)/shard_map/ppermute | solution.py:34
  156.4 18.1 %collective-permute-start.24 = (bf16[128,3072]{1,0:T(8,128)(2,1)}, bf16[128,3072]{1,0:T(8,128)(2,1)S(1)}, u32[]{:S(2)}, u32[]{:S(2)}) collective-permute-start(bf16[128,3072]{1,0:T(8,128)(2,1)} %collective-permute-done.16.refs_11_), channel_id=1, source_target_pairs={{0,8},{8,0},{1,9},{9,1},{2,10},{10,2},{3,11},{11,3},{4,12},{12,4},... | collective-permute-start | bytes 2359304 | tf_op jit(solution)/shard_map/ppermute | solution.py:227
  156.4 19.6 %collective-permute-start.28 = (bf16[128,3072]{1,0:T(8,128)(2,1)S(1)}, bf16[128,3072]{1,0:T(8,128)(2,1)S(1)}, u32[]{:S(2)}, u32[]{:S(2)}) collective-permute-start(bf16[128,3072]{1,0:T(8,128)(2,1)S(1)} %collective-permute-done.20.refs_15_), channel_id=1, source_target_pairs={{0,8},{8,0},{1,9},{9,1},{2,10},{10,2},{3,11},{11,3},{4,12},{12,4},... | collective-permute-start | bytes 2359304 | tf_op jit(solution)/shard_map/ppermute | solution.py:227
  174.0 21.5 %collective-permute-start.25 = (bf16[128,3072]{1,0:T(8,128)(2,1)S(1)}, bf16[128,3072]{1,0:T(8,128)(2,1)S(1)}, u32[]{:S(2)}, u32[]{:S(2)}) collective-permute-start(bf16[128,3072]{1,0:T(8,128)(2,1)S(1)} %collective-permute-done.17.refs_12_), channel_id=1, source_target_pairs={{0,8},{8,0},{1,9},{9,1},{2,10},{10,2},{3,11},{11,3},{4,12},{12,4},... | collective-permute-start | bytes 2359304 | tf_op jit(solution)/shard_map/ppermute | solution.py:227
  174.5 6.0 %collective-permute-start.7 = (bf16[512,128]{1,0:T(8,128)(2,1)S(1)}, bf16[512,128]{1,0:T(8,128)(2,1)S(1)}, u32[]{:S(2)}, u32[]{:S(2)}) collective-permute-start(bf16[512,128]{1,0:T(8,128)(2,1)S(1)} %bitcast.164), channel_id=1, source_target_pairs={{0,2},{2,4},{4,6},{6,7},{7,5},{5,3},{3,1},{1,0},{8,10},{10,12},{12... | collective-permute-start | bytes 393224 | tf_op jit(solution)/shard_map/ppermute | solution.py:34
  176.0 5.9 %collective-permute-start.11 = (bf16[512,128]{1,0:T(8,128)(2,1)S(1)}, bf16[512,128]{1,0:T(8,128)(2,1)S(1)}, u32[]{:S(2)}, u32[]{:S(2)}) collective-permute-start(bf16[512,128]{1,0:T(8,128)(2,1)S(1)} %bitcast.165), channel_id=1, source_target_pairs={{0,1},{2,0},{4,2},{6,4},{7,6},{5,7},{3,5},{1,3},{8,9},{10,8},{12,1... | collective-permute-start | bytes 393224 | tf_op jit(solution)/shard_map/ppermute | solution.py:38
  180.4 5.1 %collective-permute-start.8 = (bf16[512,128]{1,0:T(8,128)(2,1)S(1)}, bf16[512,128]{1,0:T(8,128)(2,1)S(1)}, u32[]{:S(2)}, u32[]{:S(2)}) collective-permute-start(bf16[512,128]{1,0:T(8,128)(2,1)S(1)} %collective-permute-done.7.refs_1_), channel_id=1, source_target_pairs={{0,2},{2,4},{4,6},{6,7},{7,5},{5,3},{3,1},{1,0},{8,10},{10,12},{12... | collective-permute-start | bytes 393224 | tf_op jit(solution)/shard_map/ppermute | solution.py:34
  181.9 5.1 %collective-permute-start.12 = (bf16[512,128]{1,0:T(8,128)(2,1)S(1)}, bf16[512,128]{1,0:T(8,128)(2,1)S(1)}, u32[]{:S(2)}, u32[]{:S(2)}) collective-permute-start(bf16[512,128]{1,0:T(8,128)(2,1)S(1)} %collective-permute-done.11.refs_5_), channel_id=1, source_target_pairs={{0,1},{2,0},{4,2},{6,4},{7,6},{5,7},{3,5},{1,3},{8,9},{10,8},{12,1... | collective-permute-start | bytes 393224 | tf_op jit(solution)/shard_map/ppermute | solution.py:38
  185.6 5.0 %collective-permute-start.9 = (bf16[512,128]{1,0:T(8,128)(2,1)S(1)}, bf16[512,128]{1,0:T(8,128)(2,1)S(1)}, u32[]{:S(2)}, u32[]{:S(2)}) collective-permute-start(bf16[512,128]{1,0:T(8,128)(2,1)S(1)} %collective-permute-done.8.refs_2_), channel_id=1, source_target_pairs={{0,2},{2,4},{4,6},{6,7},{7,5},{5,3},{3,1},{1,0},{8,10},{10,12},{12... | collective-permute-start | bytes 393224 | tf_op jit(solution)/shard_map/ppermute | solution.py:34
  187.1 5.7 %collective-permute-start.13 = (bf16[512,128]{1,0:T(8,128)(2,1)S(1)}, bf16[512,128]{1,0:T(8,128)(2,1)S(1)}, u32[]{:S(2)}, u32[]{:S(2)}) collective-permute-start(bf16[512,128]{1,0:T(8,128)(2,1)S(1)} %collective-permute-done.12.refs_6_), channel_id=1, source_target_pairs={{0,1},{2,0},{4,2},{6,4},{7,6},{5,7},{3,5},{1,3},{8,9},{10,8},{12,1... | collective-permute-start | bytes 393224 | tf_op jit(solution)/shard_map/ppermute | solution.py:38
  190.5 5.0 %collective-permute-start.10 = (bf16[512,128]{1,0:T(8,128)(2,1)S(1)}, bf16[512,128]{1,0:T(8,128)(2,1)S(1)}, u32[]{:S(2)}, u32[]{:S(2)}) collective-permute-start(bf16[512,128]{1,0:T(8,128)(2,1)S(1)} %collective-permute-done.9.refs_3_), channel_id=1, source_target_pairs={{0,2},{2,4},{4,6},{6,7},{7,5},{5,3},{3,1},{1,0},{8,10},{10,12},{12... | collective-permute-start | bytes 393224 | tf_op jit(solution)/shard_map/ppermute | solution.py:34
  236.0 7.8 %collective-permute-start.31 = (bf16[512,384]{1,0:T(8,128)(2,1)S(1)}, bf16[512,384]{1,0:T(8,128)(2,1)S(1)}, u32[]{:S(2)}, u32[]{:S(2)}) collective-permute-start(bf16[512,384]{1,0:T(8,128)(2,1)S(1)} %get-tuple-element.23), channel_id=1, source_target_pairs={{0,2},{2,4},{4,6},{6,7},{7,5},{5,3},{3,1},{1,0},{8,10},{10,12},{12... | collective-permute-start | bytes 1179656 | tf_op jit(solution)/shard_map/ppermute | solution.py:61
  237.5 8.2 %collective-permute-start.38 = (bf16[512,384]{1,0:T(8,128)(2,1)S(1)}, bf16[512,384]{1,0:T(8,128)(2,1)S(1)}, u32[]{:S(2)}, u32[]{:S(2)}) collective-permute-start(bf16[512,384]{1,0:T(8,128)(2,1)S(1)} %get-tuple-element.24), channel_id=1, source_target_pairs={{0,1},{2,0},{4,2},{6,4},{7,6},{5,7},{3,5},{1,3},{8,9},{10,8},{12,1... | collective-permute-start | bytes 1179656 | tf_op jit(solution)/shard_map/ppermute | solution.py:63
  247.1 9.4 %collective-permute-start.32 = (bf16[512,384]{1,0:T(8,128)(2,1)S(1)}, bf16[512,384]{1,0:T(8,128)(2,1)S(1)}, u32[]{:S(2)}, u32[]{:S(2)}) collective-permute-start(bf16[512,384]{1,0:T(8,128)(2,1)S(1)} %get-tuple-element.21), channel_id=1, source_target_pairs={{0,2},{2,4},{4,6},{6,7},{7,5},{5,3},{3,1},{1,0},{8,10},{10,12},{12... | collective-permute-start | bytes 1179656 | tf_op jit(solution)/shard_map/ppermute | solution.py:61
  247.8 9.8 %collective-permute-start.39 = (bf16[512,384]{1,0:T(8,128)(2,1)S(1)}, bf16[512,384]{1,0:T(8,128)(2,1)S(1)}, u32[]{:S(2)}, u32[]{:S(2)}) collective-permute-start(bf16[512,384]{1,0:T(8,128)(2,1)S(1)} %get-tuple-element.22), channel_id=1, source_target_pairs={{0,1},{2,0},{4,2},{6,4},{7,6},{5,7},{3,5},{1,3},{8,9},{10,8},{12,1... | collective-permute-start | bytes 1179656 | tf_op jit(solution)/shard_map/ppermute | solution.py:63
  258.9 11.0 %collective-permute-start.33 = (bf16[512,384]{1,0:T(8,128)(2,1)S(1)}, bf16[512,384]{1,0:T(8,128)(2,1)S(1)}, u32[]{:S(2)}, u32[]{:S(2)}) collective-permute-start(bf16[512,384]{1,0:T(8,128)(2,1)S(1)} %get-tuple-element.19), channel_id=1, source_target_pairs={{0,2},{2,4},{4,6},{6,7},{7,5},{5,3},{3,1},{1,0},{8,10},{10,12},{12... | collective-permute-start | bytes 1179656 | tf_op jit(solution)/shard_map/ppermute | solution.py:61
  259.4 11.3 %collective-permute-start.40 = (bf16[512,384]{1,0:T(8,128)(2,1)S(1)}, bf16[512,384]{1,0:T(8,128)(2,1)S(1)}, u32[]{:S(2)}, u32[]{:S(2)}) collective-permute-start(bf16[512,384]{1,0:T(8,128)(2,1)S(1)} %get-tuple-element.20), channel_id=1, source_target_pairs={{0,1},{2,0},{4,2},{6,4},{7,6},{5,7},{3,5},{1,3},{8,9},{10,8},{12,1... | collective-permute-start | bytes 1179656 | tf_op jit(solution)/shard_map/ppermute | solution.py:63
  272.0 11.6 %collective-permute-start.34 = (bf16[512,384]{1,0:T(8,128)(2,1)S(1)}, bf16[512,384]{1,0:T(8,128)(2,1)S(1)}, u32[]{:S(2)}, u32[]{:S(2)}) collective-permute-start(bf16[512,384]{1,0:T(8,128)(2,1)S(1)} %get-tuple-element.17), channel_id=1, source_target_pairs={{0,2},{2,4},{4,6},{6,7},{7,5},{5,3},{3,1},{1,0},{8,10},{10,12},{12... | collective-permute-start | bytes 1179656 | tf_op jit(solution)/shard_map/ppermute | solution.py:61
  272.0 11.6 %collective-permute-start.41 = (bf16[512,384]{1,0:T(8,128)(2,1)S(1)}, bf16[512,384]{1,0:T(8,128)(2,1)S(1)}, u32[]{:S(2)}, u32[]{:S(2)}) collective-permute-start(bf16[512,384]{1,0:T(8,128)(2,1)S(1)} %get-tuple-element.18), channel_id=1, source_target_pairs={{0,1},{2,0},{4,2},{6,4},{7,6},{5,7},{3,5},{1,3},{8,9},{10,8},{12,1... | collective-permute-start | bytes 1179656 | tf_op jit(solution)/shard_map/ppermute | solution.py:63
  285.0 10.9 %collective-permute-start.35 = (bf16[512,384]{1,0:T(8,128)(2,1)S(1)}, bf16[512,384]{1,0:T(8,128)(2,1)S(1)}, u32[]{:S(2)}, u32[]{:S(2)}) collective-permute-start(bf16[512,384]{1,0:T(8,128)(2,1)S(1)} %get-tuple-element.15), channel_id=1, source_target_pairs={{0,2},{2,4},{4,6},{6,7},{7,5},{5,3},{3,1},{1,0},{8,10},{10,12},{12... | collective-permute-start | bytes 1179656 | tf_op jit(solution)/shard_map/ppermute | solution.py:61
  285.2 10.7 %collective-permute-start.42 = (bf16[512,384]{1,0:T(8,128)(2,1)S(1)}, bf16[512,384]{1,0:T(8,128)(2,1)S(1)}, u32[]{:S(2)}, u32[]{:S(2)}) collective-permute-start(bf16[512,384]{1,0:T(8,128)(2,1)S(1)} %get-tuple-element.16), channel_id=1, source_target_pairs={{0,1},{2,0},{4,2},{6,4},{7,6},{5,7},{3,5},{1,3},{8,9},{10,8},{12,1... | collective-permute-start | bytes 1179656 | tf_op jit(solution)/shard_map/ppermute | solution.py:63
  297.3 10.9 %collective-permute-start.36 = (bf16[512,384]{1,0:T(8,128)(2,1)S(1)}, bf16[512,384]{1,0:T(8,128)(2,1)S(1)}, u32[]{:S(2)}, u32[]{:S(2)}) collective-permute-start(bf16[512,384]{1,0:T(8,128)(2,1)S(1)} %get-tuple-element.13), channel_id=1, source_target_pairs={{0,2},{2,4},{4,6},{6,7},{7,5},{5,3},{3,1},{1,0},{8,10},{10,12},{12... | collective-permute-start | bytes 1179656 | tf_op jit(solution)/shard_map/ppermute | solution.py:61
  298.0 11.0 %collective-permute-start.43 = (bf16[512,384]{1,0:T(8,128)(2,1)S(1)}, bf16[512,384]{1,0:T(8,128)(2,1)}, u32[]{:S(2)}, u32[]{:S(2)}) collective-permute-start(bf16[512,384]{1,0:T(8,128)(2,1)S(1)} %get-tuple-element.14), channel_id=1, source_target_pairs={{0,1},{2,0},{4,2},{6,4},{7,6},{5,7},{3,5},{1,3},{8,9},{10,8},{12,1... | collective-permute-start | bytes 1179656 | tf_op jit(solution)/shard_map/ppermute | solution.py:63
  299.4 25.6 %copy-start.1 = (bf16[128,6144]{1,0:T(8,128)(2,1)S(1)}, bf16[128,6144]{1,0:T(8,128)(2,1)}, u32[]{:S(2)}) copy-start(bf16[128,6144]{1,0:T(8,128)(2,1)} %param.23) | copy-start | bytes 4718596
  311.2 8.0 %collective-permute-start.37 = (bf16[512,384]{1,0:T(8,128)(2,1)}, bf16[512,384]{1,0:T(8,128)(2,1)S(1)}, u32[]{:S(2)}, u32[]{:S(2)}) collective-permute-start(bf16[512,384]{1,0:T(8,128)(2,1)} %get-tuple-element.11), channel_id=1, source_target_pairs={{0,2},{2,4},{4,6},{6,7},{7,5},{5,3},{3,1},{1,0},{8,10},{10,12},{12... | collective-permute-start | bytes 1179656 | tf_op jit(solution)/shard_map/ppermute | solution.py:61
  312.9 7.9 %collective-permute-start.44 = (bf16[512,384]{1,0:T(8,128)(2,1)S(1)}, bf16[512,384]{1,0:T(8,128)(2,1)}, u32[]{:S(2)}, u32[]{:S(2)}) collective-permute-start(bf16[512,384]{1,0:T(8,128)(2,1)S(1)} %get-tuple-element.12), channel_id=1, source_target_pairs={{0,1},{2,0},{4,2},{6,4},{7,6},{5,7},{3,5},{1,3},{8,9},{10,8},{12,1... | collective-permute-start | bytes 1179656 | tf_op jit(solution)/shard_map/ppermute | solution.py:63
  (19 other events, 200.5 us)

commit v19 on v18

--- a/solution.py
+++ b/solution.py
@@ -229,6 +229,10 @@
         swap = [(0, 1), (1, 0)]
         up_full = jnp.concatenate([w_up, lax.ppermute(w_up, "span", swap)], axis=1)
         down_full = jnp.concatenate([w_down, lax.ppermute(w_down, "span", swap)], axis=0)
+        gathered_narrow, up_full, down_full = lax.optimization_barrier(
+            (gathered_narrow, up_full, down_full)
+        )
+        gathered = gathered_narrow.astype(jnp.float32)
     else:
         up_full, down_full = (
             lax.all_gather(w_up, "span", axis=1, tiled=True),

time: 326 us -> 367 us (1.13)
  waiting for transfers between devices: 170 us -> 197 us
  other arithmetic: 22 us -> 34.8 us
    ppermute x9, waiting for transfers between devices: 22.3 us -> 69.2 us  [ring_gather(): backward = lax.ppermute(backward, axis_name, behind)]
    ppermute x12, waiting for transfers between devices: 89.3 us -> 71.6 us  [ring_gather(): forward = lax.ppermute(forward, axis_name, ahead)]
    concatenate x0 -> x2, other arithmetic: none -> 11.2 us  [the longest x1 6.26 us: local(): jnp.concatenate([w_down, lax.ppermute(w_down, 'span', swap)], axis=0)]
    dot_general x0 -> x1, matrix products: none -> 10 us  [local(): pre_act = jnp.dot(mlp_in, up_full, preferred_element_type=jnp.float32)]
    dot_general x1, matrix products: 15.5 us -> 6.6 us  [local(): jnp.dot(hidden_units, down_full, preferred_element_type=jnp.float32)]
    dynamic_update_slice x8, local copies, waits for them, and re-layouts: 7.58 us -> 3.07 us  [local(): lax.dynamic_update_slice_in_dim(gathered, piece, owner * share_width, 2)]
    ppermute x7, waiting for transfers between devices: 51.9 us -> 47.5 us  [ring_reduce_scatter(): lax.ppermute(forward.astype(jnp.bfloat16), axis_name, ahead)]
    ppermute x7, starting transfers between devices: 5.53 us -> 9.45 us  [ring_reduce_scatter(): lax.ppermute(forward.astype(jnp.bfloat16), axis_name, ahead)]
  transfers between devices with their start and end apart: 45 -> 45, of which waited for: 25 -> 26; matrix products, arithmetic and copies ran while one was open for 12% -> 13% of each run, Pallas kernels for 7% -> 0%
where the time goes in v19:
time: 367 us; the launch traced here: 366 us
  waiting for transfers between devices  197 us (54%)
  starting transfers between devices  44.1 us (12%)
  other arithmetic  34.8 us (9%)
  matrix products  25.7 us (7%)
  Pallas kernels  21.6 us (6%)
  local copies, waits for them, and re-layouts  19.9 us (5%)
  between operations  18.2 us (5%)
  blocking collectives  4.68 us (1%)
    ppermute x12, waiting for transfers between devices, ring_gather(): forward = lax.ppermute(forward, axis_name, ahead)  71.6 us
    ppermute x9, waiting for transfers between devices, ring_gather(): backward = lax.ppermute(backward, axis_name, behind)  69.2 us
    ppermute x7, waiting for transfers between devices, ring_reduce_scatter(): lax.ppermute(forward.astype(jnp.bfloat16), axis_name, ahead)  47.5 us
    pallas_call x1, Pallas kernels, grouped_out_proj(): pl.pallas_call(functools.partial(out_proj_kernel, group_count, tiles_per_...  21.6 us
    ppermute x12, starting transfers between devices, ring_gather(): forward = lax.ppermute(forward, axis_name, ahead)  21.6 us
    dot_general x1, matrix products, local(): pre_act = jnp.dot(mlp_in, up_full, preferred_element_type=jnp.float32)  10 us
    unnamed x57, local copies, waits for them, and re-layouts  9.69 us
    ppermute x7, starting transfers between devices, ring_reduce_scatter(): lax.ppermute(forward.astype(jnp.bfloat16), axis_name, ahead)  9.45 us
  transfers between devices with their start and end apart: 45, of which 26 were waited for; matrix products, arithmetic and copies ran while one was open for 13% of the time, Pallas kernels for 0%

profile of v19, /device:TPU:0, one launch (start us, length us, event | category | flops | bytes accessed | tf_op | source)
XLA Modules:
  0.0 365.6 jit_solution(4268982948643741265)
XLA Ops:
  0.0 3.0 collective-permute-start
  4.5 2.0 collective-permute-start.16
  7.9 13.6 %collective-permute-done = bf16[4,128,768]{2,1,0:T(8,128)(2,1)S(1)} collective-permute-done((bf16[4,128,768]{2,1,0:T(8,128)(2,1)}, bf16[4,128,768]{2,1,0:T(8,128)(2,1)S(1)}, u32[]{:S(2)}, u32[]{:S(2)}) %collective-permute-start) | collective-permute-done | bytes 786464 | tf_op jit(solution)/shard_map/ppermute | solution.py:34
  21.5 2.1 collective-permute-start.1
  25.1 29.3 %collective-permute-done.1 = bf16[4,128,768]{2,1,0:T(8,128)(2,1)S(1)} collective-permute-done((bf16[4,128,768]{2,1,0:T(8,128)(2,1)S(1)}, bf16[4,128,768]{2,1,0:T(8,128)(2,1)S(1)}, u32[]{:S(2)}, u32[]{:S(2)}) %collective-permute-start.1) | collective-permute-done | bytes 786464 | tf_op jit(solution)/shard_map/ppermute | solution.py:34
  54.4 1.8 collective-permute-start.2
  57.9 15.3 %collective-permute-done.2 = bf16[4,128,768]{2,1,0:T(8,128)(2,1)} collective-permute-done((bf16[4,128,768]{2,1,0:T(8,128)(2,1)S(1)}, bf16[4,128,768]{2,1,0:T(8,128)(2,1)}, u32[]{:S(2)}, u32[]{:S(2)}) %collective-permute-start.2) | collective-permute-done | bytes 786464 | tf_op jit(solution)/shard_map/ppermute | solution.py:34
  84.8 1.9 fusion.42
  91.6 6.7 %copy.30 = bf16[6144,3,128]{0,2,1:T(8,128)(2,1)} copy(bf16[6144,3,128]{2,0,1:T(8,128)(2,1)} %param.22) | data formatting | bytes 9437184 | tf_op args[7]
  98.5 2.3 all_gather.6
  106.7 14.6 %collective-permute-done.5 = bf16[4,128,768]{2,1,0:T(8,128)(2,1)S(1)} collective-permute-done((bf16[4,128,768]{2,1,0:T(8,128)(2,1)S(1)}, bf16[4,128,768]{2,1,0:T(8,128)(2,1)S(1)}, u32[]{:S(2)}, u32[]{:S(2)}) %collective-permute-start.5) | collective-permute-done | bytes 786464 | tf_op jit(solution)/shard_map/ppermute | solution.py:38
  121.3 1.6 collective-permute-start.17
  123.0 14.5 %collective-permute-done.20.refs_13_ = bf16[128,3072]{1,0:T(8,128)(2,1)} collective-permute-done((bf16[128,3072]{1,0:T(8,128)(2,1)}, bf16[128,3072]{1,0:T(8,128)(2,1)}, u32[]{:S(2)}, u32[]{:S(2)}) %collective-permute-start.20) | collective-permute-done | bytes 786464 | tf_op jit(solution)/shard_map/ppermute | solution.py:38
  138.0 4.9 %pad_maximum_fusion = bf16[6144,512]{1,0:T(8,128)(2,1)} fusion(bf16[6144,256]{1,0:T(8,128)(2,1)} %collective-permute-done.7, bf16[6144,256]{1,0:T(8,128)(2,1)S(1)} %copy-done.4), kind=kLoop, calls=%fused_computation.9 | loop fusion | flops 12582912 | bytes 12582912 | tf_op jit(solution)/shard_map/concatenate | solution.py:230
  144.4 6.3 %pad_maximum_fusion.1 = bf16[512,6144]{1,0:T(8,128)(2,1)} fusion(bf16[256,6144]{1,0:T(8,128)(2,1)} %collective-permute-done.8, bf16[256,6144]{1,0:T(8,128)(2,1)} %param.25), kind=kLoop, calls=%fused_computation.10 | loop fusion | flops 12582912 | bytes 12582912 | tf_op jit(solution)/shard_map/concatenate | solution.py:231
  150.6 23.8 %collective-permute-done.6 = bf16[4,128,768]{2,1,0:T(8,128)(2,1)S(1)} collective-permute-done((bf16[4,128,768]{2,1,0:T(8,128)(2,1)S(1)}, bf16[4,128,768]{2,1,0:T(8,128)(2,1)S(1)}, u32[]{:S(2)}, u32[]{:S(2)}) %collective-permute-start.6) | collective-permute-done | bytes 786464 | tf_op jit(solution)/shard_map/ppermute | solution.py:38
  177.5 5.3 %fusion.3 = bf16[4,128,6144]{2,1,0:T(8,128)(2,1)} fusion(bf16[4,128,6144]{2,1,0:T(8,128)(2,1)S(1)} %constant_dynamic-update-slice_fusion, f32[4,6144]{1,0:T(4,128)S(1)} %get-tuple-element.38, f32[4,6144]{1,0:T(4,128)S(1)} %get-tuple-element.39, f32[4,128]{1,0:T(4,128)S(1)} %add_rsqrt_fusion), kind=kLoop, calls=%fused_computation.5 | loop fusion | flops 15728640 | bytes 12781568 | tf_op jit(solution)/shard_map/convert_element_type | solution.py:248
  182.8 5.6 %convolution_convert_fusion.1 = bf16[512,384]{1,0:T(8,128)(2,1)S(1)} fusion(bf16[512,6144]{1,0:T(8,128)(2,1)} %bitcast.152, bf16[6144,384]{0,1:T(8,128)(2,1)S(1)} %bitcast.155), kind=kOutput, calls=%fused_computation.29 | convolution fusion | flops 2416115712 | bytes 11403264 | tf_op jit(solution)/shard_map/dot_general | solution.py:252
  189.0 2.4 all_gather.7
  194.3 1.6 collective-permute-start.19
  197.5 16.3 %collective-permute-done.22.refs_15_ = bf16[128,3072]{1,0:T(8,128)(2,1)S(1)} collective-permute-done((bf16[128,3072]{1,0:T(8,128)(2,1)}, bf16[128,3072]{1,0:T(8,128)(2,1)S(1)}, u32[]{:S(2)}, u32[]{:S(2)}) %collective-permute-start.22) | collective-permute-done | bytes 786464 | tf_op jit(solution)/shard_map/ppermute | solution.py:38
  215.0 1.6 collective-permute-start.9
  217.1 3.9 %collective-permute-done.9.refs_1_ = bf16[512,128]{1,0:T(8,128)(2,1)S(1)} collective-permute-done((bf16[512,128]{1,0:T(8,128)(2,1)S(1)}, bf16[512,128]{1,0:T(8,128)(2,1)S(1)}, u32[]{:S(2)}, u32[]{:S(2)}) %collective-permute-start.9) | collective-permute-done | bytes 131104 | tf_op jit(solution)/shard_map/ppermute | solution.py:34
  221.0 1.6 collective-permute-start.10
  223.0 3.1 collective-permute-done.10.refs_2_
  226.1 1.6 collective-permute-start.11
  228.1 2.9 collective-permute-done.11.refs_3_
  231.1 1.6 collective-permute-start.12
  233.4 2.7 collective-permute-done.12.refs_4_
  236.3 21.6 %shard_map.145 = (f32[512,6144]{1,0:T(8,128)}, f32[512,128]{1,0:T(8,128)}) custom-call(s32[1]{0:T(128)} %bitcast.span_ref, bf16[512,128]{1,0:T(8,128)(2,1)} %bitcast.167, bf16[512,128]{1,0:T(8,128)(2,1)} %copy-done.17, bf16[512,128]{1,0:T(8,128)(2,1)} %copy-done.19, bf16[512,128]{1,0:T(8,128)(2,1)} %copy-done.21, ...), custom_call_target="tpu_custom_call" | custom-call | flops 6442450944 | bytes 32505856 | tf_op jit(solution)/shard_map/pallas_call | solution.py:134
  259.0 10.0 %fusion.27 = bf16[4,128,512]{2,1,0:T(8,128)(2,1)S(1)} fusion(bf16[6144,512]{1,0:T(8,128)(2,1)} %pad_maximum_fusion, f32[4,128,6144]{2,1,0:T(8,128)} %bitcast.160, f32[4,6144]{1,0:T(4,128)S(1)} %copy-done.12, f32[4,6144]{1,0:T(4,128)S(1)} %get-tuple-element.35, f32[4,128]{1,0:T(4,128)S(1)} %bitcast.164), kind=kOutput, calls=%fused_computation.40 | convolution fusion | flops 3236167680 | bytes 19597312 | tf_op jit(solution)/shard_map/dot_general | solution.py:305
  269.0 6.6 %convolution_convert_fusion = bf16[4,128,6144]{2,1,0:T(8,128)(2,1)S(1)} fusion(bf16[4,128,512]{2,1,0:T(8,128)(2,1)S(1)} %fusion.27, bf16[512,6144]{1,0:T(8,128)(2,1)} %pad_maximum_fusion.1), kind=kOutput, calls=%fused_computation.7 | convolution fusion | flops 3224371200 | bytes 13107200 | tf_op jit(solution)/shard_map/dot_general | solution.py:307
  275.6 2.6 copy-done.3
  278.3 1.6 collective-permute-start.31
  281.7 4.5 %collective-permute-done.31 = bf16[512,384]{1,0:T(8,128)(2,1)S(1)} collective-permute-done((bf16[512,384]{1,0:T(8,128)(2,1)S(1)}, bf16[512,384]{1,0:T(8,128)(2,1)S(1)}, u32[]{:S(2)}, u32[]{:S(2)}) %collective-permute-start.31) | collective-permute-done | bytes 393248 | tf_op jit(solution)/shard_map/ppermute | solution.py:61
  286.2 1.6 collective-permute-done.38
  289.0 1.6 collective-permute-start.32
  292.4 4.9 %collective-permute-done.32 = bf16[512,384]{1,0:T(8,128)(2,1)S(1)} collective-permute-done((bf16[512,384]{1,0:T(8,128)(2,1)S(1)}, bf16[512,384]{1,0:T(8,128)(2,1)S(1)}, u32[]{:S(2)}, u32[]{:S(2)}) %collective-permute-start.32) | collective-permute-done | bytes 393248 | tf_op jit(solution)/shard_map/ppermute | solution.py:61
  297.3 1.9 collective-permute-done.39
  300.5 3.2 collective-permute-start.33
  304.3 7.5 %collective-permute-done.33 = bf16[512,384]{1,0:T(8,128)(2,1)S(1)} collective-permute-done((bf16[512,384]{1,0:T(8,128)(2,1)S(1)}, bf16[512,384]{1,0:T(8,128)(2,1)S(1)}, u32[]{:S(2)}, u32[]{:S(2)}) %collective-permute-start.33) | collective-permute-done | bytes 393248 | tf_op jit(solution)/shard_map/ppermute | solution.py:61
  311.9 2.8 collective-permute-done.40
  318.1 9.8 %collective-permute-done.34 = bf16[512,384]{1,0:T(8,128)(2,1)S(1)} collective-permute-done((bf16[512,384]{1,0:T(8,128)(2,1)S(1)}, bf16[512,384]{1,0:T(8,128)(2,1)S(1)}, u32[]{:S(2)}, u32[]{:S(2)}) %collective-permute-start.34) | collective-permute-done | bytes 393248 | tf_op jit(solution)/shard_map/ppermute | solution.py:61
  330.2 1.6 collective-permute-start.42
  331.8 8.4 %collective-permute-done.35 = bf16[512,384]{1,0:T(8,128)(2,1)S(1)} collective-permute-done((bf16[512,384]{1,0:T(8,128)(2,1)S(1)}, bf16[512,384]{1,0:T(8,128)(2,1)S(1)}, u32[]{:S(2)}, u32[]{:S(2)}) %collective-permute-start.35) | collective-permute-done | bytes 393248 | tf_op jit(solution)/shard_map/ppermute | solution.py:61
  343.9 7.4 %collective-permute-done.36 = bf16[512,384]{1,0:T(8,128)(2,1)S(1)} collective-permute-done((bf16[512,384]{1,0:T(8,128)(2,1)S(1)}, bf16[512,384]{1,0:T(8,128)(2,1)S(1)}, u32[]{:S(2)}, u32[]{:S(2)}) %collective-permute-start.36) | collective-permute-done | bytes 393248 | tf_op jit(solution)/shard_map/ppermute | solution.py:61
  355.8 5.0 %collective-permute-done.37 = bf16[512,384]{1,0:T(8,128)(2,1)S(1)} collective-permute-done((bf16[512,384]{1,0:T(8,128)(2,1)S(1)}, bf16[512,384]{1,0:T(8,128)(2,1)S(1)}, u32[]{:S(2)}, u32[]{:S(2)}) %collective-permute-start.37) | collective-permute-done | bytes 393248 | tf_op jit(solution)/shard_map/ppermute | solution.py:61
  362.9 2.6 add_convert_fusion.2
  (158 shorter events, 48.2 us)
Async XLA Ops:
  0.0 21.5 %collective-permute-start = (bf16[4,128,768]{2,1,0:T(8,128)(2,1)}, bf16[4,128,768]{2,1,0:T(8,128)(2,1)S(1)}, u32[]{:S(2)}, u32[]{:S(2)}) collective-permute-start(bf16[4,128,768]{2,1,0:T(8,128)(2,1)} %param.15), channel_id=1, source_target_pairs={{0,2},{2,4},{4,6},{6,7},{7,5},{5,3},{3,1},{1,0},{8,10},{10,12},{12... | collective-permute-start | bytes 2359304 | tf_op jit(solution)/shard_map/ppermute | solution.py:34
  3.0 97.8 %collective-permute-start.4 = (bf16[4,128,768]{2,1,0:T(8,128)(2,1)}, bf16[4,128,768]{2,1,0:T(8,128)(2,1)S(1)}, u32[]{:S(2)}, u32[]{:S(2)}) collective-permute-start(bf16[4,128,768]{2,1,0:T(8,128)(2,1)} %param.15), channel_id=1, source_target_pairs={{0,1},{2,0},{4,2},{6,4},{7,6},{5,7},{3,5},{1,3},{8,9},{10,8},{12,1... | collective-permute-start | bytes 2359304 | tf_op jit(solution)/shard_map/ppermute | solution.py:38
  3.0 134.4 %collective-permute-start.7 = (bf16[6144,256]{1,0:T(8,128)(2,1)}, bf16[6144,256]{1,0:T(8,128)(2,1)}, u32[]{:S(2)}, u32[]{:S(2)}) collective-permute-start(bf16[6144,256]{1,0:T(8,128)(2,1)} %param.24), channel_id=1, source_target_pairs={{0,8},{8,0},{1,9},{9,1},{2,10},{10,2},{3,11},{11,3},{4,12},{12,4},... | collective-permute-start | bytes 9437192 | tf_op jit(solution)/shard_map/ppermute | solution.py:230
  3.0 139.9 %collective-permute-start.8 = (bf16[256,6144]{1,0:T(8,128)(2,1)}, bf16[256,6144]{1,0:T(8,128)(2,1)}, u32[]{:S(2)}, u32[]{:S(2)}) collective-permute-start(bf16[256,6144]{1,0:T(8,128)(2,1)} %param.25), channel_id=1, source_target_pairs={{0,8},{8,0},{1,9},{9,1},{2,10},{10,2},{3,11},{11,3},{4,12},{12,4},... | collective-permute-start | bytes 9437192 | tf_op jit(solution)/shard_map/ppermute | solution.py:231
  4.5 93.8 %copy-start.11 = (bf16[4,128,2,128]{3,2,1,0:T(2,128)(2,1)S(1)}, bf16[4,128,2,128]{3,2,1,0:T(2,128)(2,1)}, u32[]{:S(2)}) copy-start(bf16[4,128,2,128]{3,2,1,0:T(2,128)(2,1)} %param.20) | copy-start | bytes 786436
  4.5 102.1 %collective-permute-start.16 = (bf16[128,3072]{1,0:T(8,128)(2,1)}, bf16[128,3072]{1,0:T(8,128)(2,1)}, u32[]{:S(2)}, u32[]{:S(2)}) collective-permute-start(bf16[128,3072]{1,0:T(8,128)(2,1)} %constant_dynamic-slice_fusion.2.refs_8_), channel_id=1, source_target_pairs={{0,2},{2,4},{4,6},{6,7},{7,5},{5,3},{3,1},{1,0},{8,10},{10,12},{12... | collective-permute-start | bytes 2359304 | tf_op jit(solution)/shard_map/ppermute | solution.py:34
  7.9 90.5 %copy-start.5 = (f32[4,6,6144]{2,0,1:T(4,128)}, f32[4,6,6144]{2,0,1:T(4,128)S(1)}, u32[]{:S(2)}) copy-start(f32[4,6,6144]{2,0,1:T(4,128)S(1)} %fusion.31) | copy-start | bytes 1769476
  21.5 70.0 %copy-start.7 = (bf16[4,128,768]{2,1,0:T(8,128)(2,1)}, bf16[4,128,768]{2,1,0:T(8,128)(2,1)S(1)}, u32[]{:S(2)}) copy-start(bf16[4,128,768]{2,1,0:T(8,128)(2,1)S(1)} %collective-permute-done) | copy-start | bytes 2359300
  21.5 32.9 %collective-permute-start.1 = (bf16[4,128,768]{2,1,0:T(8,128)(2,1)S(1)}, bf16[4,128,768]{2,1,0:T(8,128)(2,1)S(1)}, u32[]{:S(2)}, u32[]{:S(2)}) collective-permute-start(bf16[4,128,768]{2,1,0:T(8,128)(2,1)S(1)} %collective-permute-done), channel_id=1, source_target_pairs={{0,2},{2,4},{4,6},{6,7},{7,5},{5,3},{3,1},{1,0},{8,10},{10,12},{12... | collective-permute-start | bytes 2359304 | tf_op jit(solution)/shard_map/ppermute | solution.py:34
  54.4 18.8 %collective-permute-start.2 = (bf16[4,128,768]{2,1,0:T(8,128)(2,1)S(1)}, bf16[4,128,768]{2,1,0:T(8,128)(2,1)}, u32[]{:S(2)}, u32[]{:S(2)}) collective-permute-start(bf16[4,128,768]{2,1,0:T(8,128)(2,1)S(1)} %collective-permute-done.1), channel_id=1, source_target_pairs={{0,2},{2,4},{4,6},{6,7},{7,5},{5,3},{3,1},{1,0},{8,10},{10,12},{12... | collective-permute-start | bytes 2359304 | tf_op jit(solution)/shard_map/ppermute | solution.py:34
  73.3 29.1 %collective-permute-start.3 = (bf16[4,128,768]{2,1,0:T(8,128)(2,1)}, bf16[4,128,768]{2,1,0:T(8,128)(2,1)}, u32[]{:S(2)}, u32[]{:S(2)}) collective-permute-start(bf16[4,128,768]{2,1,0:T(8,128)(2,1)} %collective-permute-done.2), channel_id=1, source_target_pairs={{0,2},{2,4},{4,6},{6,7},{7,5},{5,3},{3,1},{1,0},{8,10},{10,12},{12... | collective-permute-start | bytes 2359304 | tf_op jit(solution)/shard_map/ppermute | solution.py:34
  100.8 20.4 %collective-permute-start.5 = (bf16[4,128,768]{2,1,0:T(8,128)(2,1)S(1)}, bf16[4,128,768]{2,1,0:T(8,128)(2,1)S(1)}, u32[]{:S(2)}, u32[]{:S(2)}) collective-permute-start(bf16[4,128,768]{2,1,0:T(8,128)(2,1)S(1)} %collective-permute-done.4), channel_id=1, source_target_pairs={{0,1},{2,0},{4,2},{6,4},{7,6},{5,7},{3,5},{1,3},{8,9},{10,8},{12,1... | collective-permute-start | bytes 2359304 | tf_op jit(solution)/shard_map/ppermute | solution.py:38
  102.3 35.1 %collective-permute-start.20 = (bf16[128,3072]{1,0:T(8,128)(2,1)}, bf16[128,3072]{1,0:T(8,128)(2,1)}, u32[]{:S(2)}, u32[]{:S(2)}) collective-permute-start(bf16[128,3072]{1,0:T(8,128)(2,1)} %constant_dynamic-slice_fusion.2.refs_8_), channel_id=1, source_target_pairs={{0,1},{2,0},{4,2},{6,4},{7,6},{5,7},{3,5},{1,3},{8,9},{10,8},{12,1... | collective-permute-start | bytes 2359304 | tf_op jit(solution)/shard_map/ppermute | solution.py:38
  106.7 86.9 %collective-permute-start.23 = (bf16[128,3072]{1,0:T(8,128)(2,1)}, bf16[128,3072]{1,0:T(8,128)(2,1)}, u32[]{:S(2)}, u32[]{:S(2)}) collective-permute-start(bf16[128,3072]{1,0:T(8,128)(2,1)} %constant_dynamic-slice_fusion.2.refs_8_), channel_id=1, source_target_pairs={{0,8},{8,0},{1,9},{9,1},{2,10},{10,2},{3,11},{11,3},{4,12},{12,4},... | collective-permute-start | bytes 2359304 | tf_op jit(solution)/shard_map/ppermute | solution.py:227
  121.3 29.3 %collective-permute-start.17 = (bf16[128,3072]{1,0:T(8,128)(2,1)}, bf16[128,3072]{1,0:T(8,128)(2,1)}, u32[]{:S(2)}, u32[]{:S(2)}) collective-permute-start(bf16[128,3072]{1,0:T(8,128)(2,1)} %collective-permute-done.16.refs_9_), channel_id=1, source_target_pairs={{0,2},{2,4},{4,6},{6,7},{7,5},{5,3},{3,1},{1,0},{8,10},{10,12},{12... | collective-permute-start | bytes 2359304 | tf_op jit(solution)/shard_map/ppermute | solution.py:34
  137.4 56.8 %collective-permute-start.24 = (bf16[128,3072]{1,0:T(8,128)(2,1)}, bf16[128,3072]{1,0:T(8,128)(2,1)}, u32[]{:S(2)}, u32[]{:S(2)}) collective-permute-start(bf16[128,3072]{1,0:T(8,128)(2,1)} %collective-permute-done.16.refs_9_), channel_id=1, source_target_pairs={{0,8},{8,0},{1,9},{9,1},{2,10},{10,2},{3,11},{11,3},{4,12},{12,4},... | collective-permute-start | bytes 2359304 | tf_op jit(solution)/shard_map/ppermute | solution.py:227
  137.4 56.3 %collective-permute-start.21 = (bf16[128,3072]{1,0:T(8,128)(2,1)}, bf16[128,3072]{1,0:T(8,128)(2,1)}, u32[]{:S(2)}, u32[]{:S(2)}) collective-permute-start(bf16[128,3072]{1,0:T(8,128)(2,1)} %collective-permute-done.20.refs_13_), channel_id=1, source_target_pairs={{0,1},{2,0},{4,2},{6,4},{7,6},{5,7},{3,5},{1,3},{8,9},{10,8},{12,1... | collective-permute-start | bytes 2359304 | tf_op jit(solution)/shard_map/ppermute | solution.py:38
  142.9 31.5 %collective-permute-start.6 = (bf16[4,128,768]{2,1,0:T(8,128)(2,1)S(1)}, bf16[4,128,768]{2,1,0:T(8,128)(2,1)S(1)}, u32[]{:S(2)}, u32[]{:S(2)}) collective-permute-start(bf16[4,128,768]{2,1,0:T(8,128)(2,1)S(1)} %collective-permute-done.5), channel_id=1, source_target_pairs={{0,1},{2,0},{4,2},{6,4},{7,6},{5,7},{3,5},{1,3},{8,9},{10,8},{12,1... | collective-permute-start | bytes 2359304 | tf_op jit(solution)/shard_map/ppermute | solution.py:38
  150.6 46.6 %collective-permute-start.28 = (bf16[128,3072]{1,0:T(8,128)(2,1)}, bf16[128,3072]{1,0:T(8,128)(2,1)}, u32[]{:S(2)}, u32[]{:S(2)}) collective-permute-start(bf16[128,3072]{1,0:T(8,128)(2,1)} %collective-permute-done.20.refs_13_), channel_id=1, source_target_pairs={{0,8},{8,0},{1,9},{9,1},{2,10},{10,2},{3,11},{11,3},{4,12},{12,4},... | collective-permute-start | bytes 2359304 | tf_op jit(solution)/shard_map/ppermute | solution.py:227
  174.5 19.9 %collective-permute-start.18 = (bf16[128,3072]{1,0:T(8,128)(2,1)}, bf16[128,3072]{1,0:T(8,128)(2,1)}, u32[]{:S(2)}, u32[]{:S(2)}) collective-permute-start(bf16[128,3072]{1,0:T(8,128)(2,1)} %collective-permute-done.17.refs_10_), channel_id=1, source_target_pairs={{0,2},{2,4},{4,6},{6,7},{7,5},{5,3},{3,1},{1,0},{8,10},{10,12},{12... | collective-permute-start | bytes 2359304 | tf_op jit(solution)/shard_map/ppermute | solution.py:34
  193.6 21.4 %collective-permute-start.25 = (bf16[128,3072]{1,0:T(8,128)(2,1)}, bf16[128,3072]{1,0:T(8,128)(2,1)S(1)}, u32[]{:S(2)}, u32[]{:S(2)}) collective-permute-start(bf16[128,3072]{1,0:T(8,128)(2,1)} %collective-permute-done.17.refs_10_), channel_id=1, source_target_pairs={{0,8},{8,0},{1,9},{9,1},{2,10},{10,2},{3,11},{11,3},{4,12},{12,4},... | collective-permute-start | bytes 2359304 | tf_op jit(solution)/shard_map/ppermute | solution.py:227
  193.8 20.0 %collective-permute-start.22 = (bf16[128,3072]{1,0:T(8,128)(2,1)}, bf16[128,3072]{1,0:T(8,128)(2,1)S(1)}, u32[]{:S(2)}, u32[]{:S(2)}) collective-permute-start(bf16[128,3072]{1,0:T(8,128)(2,1)} %collective-permute-done.21.refs_14_), channel_id=1, source_target_pairs={{0,1},{2,0},{4,2},{6,4},{7,6},{5,7},{3,5},{1,3},{8,9},{10,8},{12,1... | collective-permute-start | bytes 2359304 | tf_op jit(solution)/shard_map/ppermute | solution.py:38
  194.2 22.4 %collective-permute-start.29 = (bf16[128,3072]{1,0:T(8,128)(2,1)}, bf16[128,3072]{1,0:T(8,128)(2,1)S(1)}, u32[]{:S(2)}, u32[]{:S(2)}) collective-permute-start(bf16[128,3072]{1,0:T(8,128)(2,1)} %collective-permute-done.21.refs_14_), channel_id=1, source_target_pairs={{0,8},{8,0},{1,9},{9,1},{2,10},{10,2},{3,11},{11,3},{4,12},{12,4},... | collective-permute-start | bytes 2359304 | tf_op jit(solution)/shard_map/ppermute | solution.py:227
  194.3 20.2 %collective-permute-start.19 = (bf16[128,3072]{1,0:T(8,128)(2,1)}, bf16[128,3072]{1,0:T(8,128)(2,1)}, u32[]{:S(2)}, u32[]{:S(2)}) collective-permute-start(bf16[128,3072]{1,0:T(8,128)(2,1)} %collective-permute-done.18.refs_11_), channel_id=1, source_target_pairs={{0,2},{2,4},{4,6},{6,7},{7,5},{5,3},{3,1},{1,0},{8,10},{10,12},{12... | collective-permute-start | bytes 2359304 | tf_op jit(solution)/shard_map/ppermute | solution.py:34
  197.3 36.1 %collective-permute-start.26 = (bf16[128,3072]{1,0:T(8,128)(2,1)}, bf16[128,3072]{1,0:T(8,128)(2,1)}, u32[]{:S(2)}, u32[]{:S(2)}) collective-permute-start(bf16[128,3072]{1,0:T(8,128)(2,1)} %collective-permute-done.18.refs_11_), channel_id=1, source_target_pairs={{0,8},{8,0},{1,9},{9,1},{2,10},{10,2},{3,11},{11,3},{4,12},{12,4},... | collective-permute-start | bytes 2359304 | tf_op jit(solution)/shard_map/ppermute | solution.py:227
  213.8 19.6 %collective-permute-start.30 = (bf16[128,3072]{1,0:T(8,128)(2,1)S(1)}, bf16[128,3072]{1,0:T(8,128)(2,1)}, u32[]{:S(2)}, u32[]{:S(2)}) collective-permute-start(bf16[128,3072]{1,0:T(8,128)(2,1)S(1)} %collective-permute-done.22.refs_15_), channel_id=1, source_target_pairs={{0,8},{8,0},{1,9},{9,1},{2,10},{10,2},{3,11},{11,3},{4,12},{12,4},... | collective-permute-start | bytes 2359304 | tf_op jit(solution)/shard_map/ppermute | solution.py:227
  214.5 21.6 %collective-permute-start.27 = (bf16[128,3072]{1,0:T(8,128)(2,1)}, bf16[128,3072]{1,0:T(8,128)(2,1)}, u32[]{:S(2)}, u32[]{:S(2)}) collective-permute-start(bf16[128,3072]{1,0:T(8,128)(2,1)} %collective-permute-done.19.refs_12_), channel_id=1, source_target_pairs={{0,8},{8,0},{1,9},{9,1},{2,10},{10,2},{3,11},{11,3},{4,12},{12,4},... | collective-permute-start | bytes 2359304 | tf_op jit(solution)/shard_map/ppermute | solution.py:227
  215.0 6.0 %collective-permute-start.9 = (bf16[512,128]{1,0:T(8,128)(2,1)S(1)}, bf16[512,128]{1,0:T(8,128)(2,1)S(1)}, u32[]{:S(2)}, u32[]{:S(2)}) collective-permute-start(bf16[512,128]{1,0:T(8,128)(2,1)S(1)} %bitcast.165), channel_id=1, source_target_pairs={{0,2},{2,4},{4,6},{6,7},{7,5},{5,3},{3,1},{1,0},{8,10},{10,12},{12... | collective-permute-start | bytes 393224 | tf_op jit(solution)/shard_map/ppermute | solution.py:34
  216.7 5.9 %collective-permute-start.13 = (bf16[512,128]{1,0:T(8,128)(2,1)S(1)}, bf16[512,128]{1,0:T(8,128)(2,1)S(1)}, u32[]{:S(2)}, u32[]{:S(2)}) collective-permute-start(bf16[512,128]{1,0:T(8,128)(2,1)S(1)} %bitcast.166), channel_id=1, source_target_pairs={{0,1},{2,0},{4,2},{6,4},{7,6},{5,7},{3,5},{1,3},{8,9},{10,8},{12,1... | collective-permute-start | bytes 393224 | tf_op jit(solution)/shard_map/ppermute | solution.py:38
  221.0 5.1 %collective-permute-start.10 = (bf16[512,128]{1,0:T(8,128)(2,1)S(1)}, bf16[512,128]{1,0:T(8,128)(2,1)S(1)}, u32[]{:S(2)}, u32[]{:S(2)}) collective-permute-start(bf16[512,128]{1,0:T(8,128)(2,1)S(1)} %collective-permute-done.9.refs_1_), channel_id=1, source_target_pairs={{0,2},{2,4},{4,6},{6,7},{7,5},{5,3},{3,1},{1,0},{8,10},{10,12},{12... | collective-permute-start | bytes 393224 | tf_op jit(solution)/shard_map/ppermute | solution.py:34
  222.6 5.1 %collective-permute-start.14 = (bf16[512,128]{1,0:T(8,128)(2,1)S(1)}, bf16[512,128]{1,0:T(8,128)(2,1)S(1)}, u32[]{:S(2)}, u32[]{:S(2)}) collective-permute-start(bf16[512,128]{1,0:T(8,128)(2,1)S(1)} %collective-permute-done.13.refs_5_), channel_id=1, source_target_pairs={{0,1},{2,0},{4,2},{6,4},{7,6},{5,7},{3,5},{1,3},{8,9},{10,8},{12,1... | collective-permute-start | bytes 393224 | tf_op jit(solution)/shard_map/ppermute | solution.py:38
  226.1 5.0 %collective-permute-start.11 = (bf16[512,128]{1,0:T(8,128)(2,1)S(1)}, bf16[512,128]{1,0:T(8,128)(2,1)S(1)}, u32[]{:S(2)}, u32[]{:S(2)}) collective-permute-start(bf16[512,128]{1,0:T(8,128)(2,1)S(1)} %collective-permute-done.10.refs_2_), channel_id=1, source_target_pairs={{0,2},{2,4},{4,6},{6,7},{7,5},{5,3},{3,1},{1,0},{8,10},{10,12},{12... | collective-permute-start | bytes 393224 | tf_op jit(solution)/shard_map/ppermute | solution.py:34
  227.7 5.7 %collective-permute-start.15 = (bf16[512,128]{1,0:T(8,128)(2,1)S(1)}, bf16[512,128]{1,0:T(8,128)(2,1)S(1)}, u32[]{:S(2)}, u32[]{:S(2)}) collective-permute-start(bf16[512,128]{1,0:T(8,128)(2,1)S(1)} %collective-permute-done.14.refs_6_), channel_id=1, source_target_pairs={{0,1},{2,0},{4,2},{6,4},{7,6},{5,7},{3,5},{1,3},{8,9},{10,8},{12,1... | collective-permute-start | bytes 393224 | tf_op jit(solution)/shard_map/ppermute | solution.py:38
  231.1 5.1 %collective-permute-start.12 = (bf16[512,128]{1,0:T(8,128)(2,1)S(1)}, bf16[512,128]{1,0:T(8,128)(2,1)}, u32[]{:S(2)}, u32[]{:S(2)}) collective-permute-start(bf16[512,128]{1,0:T(8,128)(2,1)S(1)} %collective-permute-done.11.refs_3_), channel_id=1, source_target_pairs={{0,2},{2,4},{4,6},{6,7},{7,5},{5,3},{3,1},{1,0},{8,10},{10,12},{12... | collective-permute-start | bytes 393224 | tf_op jit(solution)/shard_map/ppermute | solution.py:34
  278.3 7.8 %collective-permute-start.31 = (bf16[512,384]{1,0:T(8,128)(2,1)S(1)}, bf16[512,384]{1,0:T(8,128)(2,1)S(1)}, u32[]{:S(2)}, u32[]{:S(2)}) collective-permute-start(bf16[512,384]{1,0:T(8,128)(2,1)S(1)} %get-tuple-element.29), channel_id=1, source_target_pairs={{0,2},{2,4},{4,6},{6,7},{7,5},{5,3},{3,1},{1,0},{8,10},{10,12},{12... | collective-permute-start | bytes 1179656 | tf_op jit(solution)/shard_map/ppermute | solution.py:61
  280.0 7.8 %collective-permute-start.38 = (bf16[512,384]{1,0:T(8,128)(2,1)S(1)}, bf16[512,384]{1,0:T(8,128)(2,1)S(1)}, u32[]{:S(2)}, u32[]{:S(2)}) collective-permute-start(bf16[512,384]{1,0:T(8,128)(2,1)S(1)} %get-tuple-element.30), channel_id=1, source_target_pairs={{0,1},{2,0},{4,2},{6,4},{7,6},{5,7},{3,5},{1,3},{8,9},{10,8},{12,1... | collective-permute-start | bytes 1179656 | tf_op jit(solution)/shard_map/ppermute | solution.py:63
  289.0 8.2 %collective-permute-start.32 = (bf16[512,384]{1,0:T(8,128)(2,1)S(1)}, bf16[512,384]{1,0:T(8,128)(2,1)S(1)}, u32[]{:S(2)}, u32[]{:S(2)}) collective-permute-start(bf16[512,384]{1,0:T(8,128)(2,1)S(1)} %get-tuple-element.27), channel_id=1, source_target_pairs={{0,2},{2,4},{4,6},{6,7},{7,5},{5,3},{3,1},{1,0},{8,10},{10,12},{12... | collective-permute-start | bytes 1179656 | tf_op jit(solution)/shard_map/ppermute | solution.py:61
  290.7 8.5 %collective-permute-start.39 = (bf16[512,384]{1,0:T(8,128)(2,1)S(1)}, bf16[512,384]{1,0:T(8,128)(2,1)S(1)}, u32[]{:S(2)}, u32[]{:S(2)}) collective-permute-start(bf16[512,384]{1,0:T(8,128)(2,1)S(1)} %get-tuple-element.28), channel_id=1, source_target_pairs={{0,1},{2,0},{4,2},{6,4},{7,6},{5,7},{3,5},{1,3},{8,9},{10,8},{12,1... | collective-permute-start | bytes 1179656 | tf_op jit(solution)/shard_map/ppermute | solution.py:63
  300.5 11.3 %collective-permute-start.33 = (bf16[512,384]{1,0:T(8,128)(2,1)S(1)}, bf16[512,384]{1,0:T(8,128)(2,1)S(1)}, u32[]{:S(2)}, u32[]{:S(2)}) collective-permute-start(bf16[512,384]{1,0:T(8,128)(2,1)S(1)} %get-tuple-element.25), channel_id=1, source_target_pairs={{0,2},{2,4},{4,6},{6,7},{7,5},{5,3},{3,1},{1,0},{8,10},{10,12},{12... | collective-permute-start | bytes 1179656 | tf_op jit(solution)/shard_map/ppermute | solution.py:61
  303.7 11.0 %collective-permute-start.40 = (bf16[512,384]{1,0:T(8,128)(2,1)S(1)}, bf16[512,384]{1,0:T(8,128)(2,1)S(1)}, u32[]{:S(2)}, u32[]{:S(2)}) collective-permute-start(bf16[512,384]{1,0:T(8,128)(2,1)S(1)} %get-tuple-element.26), channel_id=1, source_target_pairs={{0,1},{2,0},{4,2},{6,4},{7,6},{5,7},{3,5},{1,3},{8,9},{10,8},{12,1... | collective-permute-start | bytes 1179656 | tf_op jit(solution)/shard_map/ppermute | solution.py:63
  316.0 11.9 %collective-permute-start.34 = (bf16[512,384]{1,0:T(8,128)(2,1)S(1)}, bf16[512,384]{1,0:T(8,128)(2,1)S(1)}, u32[]{:S(2)}, u32[]{:S(2)}) collective-permute-start(bf16[512,384]{1,0:T(8,128)(2,1)S(1)} %get-tuple-element.23), channel_id=1, source_target_pairs={{0,2},{2,4},{4,6},{6,7},{7,5},{5,3},{3,1},{1,0},{8,10},{10,12},{12... | collective-permute-start | bytes 1179656 | tf_op jit(solution)/shard_map/ppermute | solution.py:61
  317.2 11.2 %collective-permute-start.41 = (bf16[512,384]{1,0:T(8,128)(2,1)S(1)}, bf16[512,384]{1,0:T(8,128)(2,1)S(1)}, u32[]{:S(2)}, u32[]{:S(2)}) collective-permute-start(bf16[512,384]{1,0:T(8,128)(2,1)S(1)} %get-tuple-element.24), channel_id=1, source_target_pairs={{0,1},{2,0},{4,2},{6,4},{7,6},{5,7},{3,5},{1,3},{8,9},{10,8},{12,1... | collective-permute-start | bytes 1179656 | tf_op jit(solution)/shard_map/ppermute | solution.py:63
  329.7 10.5 %collective-permute-start.35 = (bf16[512,384]{1,0:T(8,128)(2,1)S(1)}, bf16[512,384]{1,0:T(8,128)(2,1)S(1)}, u32[]{:S(2)}, u32[]{:S(2)}) collective-permute-start(bf16[512,384]{1,0:T(8,128)(2,1)S(1)} %get-tuple-element.21), channel_id=1, source_target_pairs={{0,2},{2,4},{4,6},{6,7},{7,5},{5,3},{3,1},{1,0},{8,10},{10,12},{12... | collective-permute-start | bytes 1179656 | tf_op jit(solution)/shard_map/ppermute | solution.py:61
  330.2 10.3 %collective-permute-start.42 = (bf16[512,384]{1,0:T(8,128)(2,1)S(1)}, bf16[512,384]{1,0:T(8,128)(2,1)S(1)}, u32[]{:S(2)}, u32[]{:S(2)}) collective-permute-start(bf16[512,384]{1,0:T(8,128)(2,1)S(1)} %get-tuple-element.22), channel_id=1, source_target_pairs={{0,1},{2,0},{4,2},{6,4},{7,6},{5,7},{3,5},{1,3},{8,9},{10,8},{12,1... | collective-permute-start | bytes 1179656 | tf_op jit(solution)/shard_map/ppermute | solution.py:63
  341.8 9.5 %collective-permute-start.36 = (bf16[512,384]{1,0:T(8,128)(2,1)S(1)}, bf16[512,384]{1,0:T(8,128)(2,1)S(1)}, u32[]{:S(2)}, u32[]{:S(2)}) collective-permute-start(bf16[512,384]{1,0:T(8,128)(2,1)S(1)} %get-tuple-element.19), channel_id=1, source_target_pairs={{0,2},{2,4},{4,6},{6,7},{7,5},{5,3},{3,1},{1,0},{8,10},{10,12},{12... | collective-permute-start | bytes 1179656 | tf_op jit(solution)/shard_map/ppermute | solution.py:61
  342.4 9.3 %collective-permute-start.43 = (bf16[512,384]{1,0:T(8,128)(2,1)S(1)}, bf16[512,384]{1,0:T(8,128)(2,1)S(1)}, u32[]{:S(2)}, u32[]{:S(2)}) collective-permute-start(bf16[512,384]{1,0:T(8,128)(2,1)S(1)} %get-tuple-element.20), channel_id=1, source_target_pairs={{0,1},{2,0},{4,2},{6,4},{7,6},{5,7},{3,5},{1,3},{8,9},{10,8},{12,1... | collective-permute-start | bytes 1179656 | tf_op jit(solution)/shard_map/ppermute | solution.py:63
  353.1 7.8 %collective-permute-start.37 = (bf16[512,384]{1,0:T(8,128)(2,1)S(1)}, bf16[512,384]{1,0:T(8,128)(2,1)S(1)}, u32[]{:S(2)}, u32[]{:S(2)}) collective-permute-start(bf16[512,384]{1,0:T(8,128)(2,1)S(1)} %get-tuple-element.17), channel_id=1, source_target_pairs={{0,2},{2,4},{4,6},{6,7},{7,5},{5,3},{3,1},{1,0},{8,10},{10,12},{12... | collective-permute-start | bytes 1179656 | tf_op jit(solution)/shard_map/ppermute | solution.py:61
  353.8 7.8 %collective-permute-start.44 = (bf16[512,384]{1,0:T(8,128)(2,1)S(1)}, bf16[512,384]{1,0:T(8,128)(2,1)S(1)}, u32[]{:S(2)}, u32[]{:S(2)}) collective-permute-start(bf16[512,384]{1,0:T(8,128)(2,1)S(1)} %get-tuple-element.18), channel_id=1, source_target_pairs={{0,1},{2,0},{4,2},{6,4},{7,6},{5,7},{3,5},{1,3},{8,9},{10,8},{12,1... | collective-permute-start | bytes 1179656 | tf_op jit(solution)/shard_map/ppermute | solution.py:63
  (22 other events, 303.2 us)

commit v20 on v18

--- a/solution.py
+++ b/solution.py
@@ -227,8 +227,7 @@
         other_blocks = [lax.ppermute(b, "span", [(0, 1), (1, 0)]) for b in mine_blocks]
     if gather_weights:
         swap = [(0, 1), (1, 0)]
-        up_full = jnp.concatenate([w_up, lax.ppermute(w_up, "span", swap)], axis=1)
-        down_full = jnp.concatenate([w_down, lax.ppermute(w_down, "span", swap)], axis=0)
+        up_full = down_full = None
     else:
         up_full, down_full = (
             lax.all_gather(w_up, "span", axis=1, tiled=True),
@@ -270,6 +269,11 @@
     )(queries, cache_seen, fresh_seen)
     if gather_weights:
         att_blocks = ring_gather(attended.reshape(token_count, per_device), "tp", tp_count)
+        last_block, up_late, down_late = lax.optimization_barrier((att_blocks[-1], w_up, w_down))
+        att_blocks[-1] = last_block
+        swap = [(0, 1), (1, 0)]
+        up_full = jnp.concatenate([up_late, lax.ppermute(up_late, "span", swap)], axis=1)
+        down_full = jnp.concatenate([down_late, lax.ppermute(down_late, "span", swap)], axis=0)
         residual_rows, square_sums = grouped_out_proj(
             span_index,
             att_blocks,

time: 326 us -> 354 us (1.086)
  waiting for transfers between devices: 170 us -> 196 us
    ppermute x9, waiting for transfers between devices: 22.3 us -> 35.9 us  [ring_gather(): backward = lax.ppermute(backward, axis_name, behind)]
    ppermute x12, waiting for transfers between devices: 89.3 us -> 102 us  [ring_gather(): forward = lax.ppermute(forward, axis_name, ahead)]
    ppermute x7, starting transfers between devices: 5.53 us -> 9.35 us  [ring_reduce_scatter(): lax.ppermute(forward.astype(jnp.bfloat16), axis_name, ahead)]
    unnamed x51 -> x49, local copies, waits for them, and re-layouts: 9.02 us -> 8.12 us
  transfers between devices with their start and end apart: 45 -> 45, of which waited for: 25 -> 29; matrix products, arithmetic and copies ran while one was open for 12% -> 11% of each run, Pallas kernels for 7% -> 6%
where the time goes in v20:
time: 354 us; the launch traced here: 353 us
  waiting for transfers between devices  196 us (55%)
  starting transfers between devices  42.5 us (12%)
  matrix products  24.8 us (7%)
  local copies, waits for them, and re-layouts  22.3 us (6%)
  other arithmetic  22.1 us (6%)
  Pallas kernels  21.6 us (6%)
  between operations  18.9 us (5%)
  blocking collectives  4.54 us (1%)
    ppermute x12, waiting for transfers between devices, ring_gather(): forward = lax.ppermute(forward, axis_name, ahead)  102 us
    ppermute x7, waiting for transfers between devices, ring_reduce_scatter(): lax.ppermute(forward.astype(jnp.bfloat16), axis_name, ahead)  49.5 us
    ppermute x9, waiting for transfers between devices, ring_gather(): backward = lax.ppermute(backward, axis_name, behind)  35.9 us
    pallas_call x1, Pallas kernels, grouped_out_proj(): pl.pallas_call(functools.partial(out_proj_kernel, group_count, tiles_per_...  21.6 us
    ppermute x12, starting transfers between devices, ring_gather(): forward = lax.ppermute(forward, axis_name, ahead)  21.2 us
    dot_general x1, matrix products, local(): jnp.dot(hidden_units, down_full, preferred_element_type=jnp.float32)  15.5 us
    ppermute x7, starting transfers between devices, ring_reduce_scatter(): lax.ppermute(forward.astype(jnp.bfloat16), axis_name, ahead)  9.35 us
    convert_element_type x6, other arithmetic, ring_reduce_scatter(): forward.astype(jnp.bfloat16)  8.73 us
  transfers between devices with their start and end apart: 45, of which 29 were waited for; matrix products, arithmetic and copies ran while one was open for 11% of the time, Pallas kernels for 6%

profile of v20, /device:TPU:0, one launch (start us, length us, event | category | flops | bytes accessed | tf_op | source)
XLA Modules:
  0.0 353.0 jit_solution(8174500690978527869)
XLA Ops:
  0.0 3.0 collective-permute-start
  3.1 2.1 collective-permute-start.14
  7.9 13.7 %collective-permute-done = bf16[4,128,768]{2,1,0:T(8,128)(2,1)} collective-permute-done((bf16[4,128,768]{2,1,0:T(8,128)(2,1)}, bf16[4,128,768]{2,1,0:T(8,128)(2,1)}, u32[]{:S(2)}, u32[]{:S(2)}) %collective-permute-start) | collective-permute-done | bytes 786464 | tf_op jit(solution)/shard_map/ppermute | solution.py:34
  21.7 2.1 collective-permute-start.1
  25.5 29.0 %collective-permute-done.1 = bf16[4,128,768]{2,1,0:T(8,128)(2,1)S(1)} collective-permute-done((bf16[4,128,768]{2,1,0:T(8,128)(2,1)}, bf16[4,128,768]{2,1,0:T(8,128)(2,1)S(1)}, u32[]{:S(2)}, u32[]{:S(2)}) %collective-permute-start.1) | collective-permute-done | bytes 786464 | tf_op jit(solution)/shard_map/ppermute | solution.py:34
  54.4 1.8 collective-permute-start.2
  60.2 2.2 all_gather.6
  62.4 10.8 %collective-permute-done.2 = bf16[4,128,768]{2,1,0:T(8,128)(2,1)} collective-permute-done((bf16[4,128,768]{2,1,0:T(8,128)(2,1)S(1)}, bf16[4,128,768]{2,1,0:T(8,128)(2,1)}, u32[]{:S(2)}, u32[]{:S(2)}) %collective-permute-start.2) | collective-permute-done | bytes 786464 | tf_op jit(solution)/shard_map/ppermute | solution.py:34
  73.3 1.5 collective-permute-start.3
  82.9 1.9 fusion.50
  89.9 6.7 %copy.30 = bf16[6144,3,128]{0,2,1:T(8,128)(2,1)} copy(bf16[6144,3,128]{2,0,1:T(8,128)(2,1)} %param.22) | data formatting | bytes 9437184 | tf_op args[7]
  105.7 9.4 %collective-permute-done.6 = bf16[4,128,768]{2,1,0:T(8,128)(2,1)S(1)} collective-permute-done((bf16[4,128,768]{2,1,0:T(8,128)(2,1)}, bf16[4,128,768]{2,1,0:T(8,128)(2,1)S(1)}, u32[]{:S(2)}, u32[]{:S(2)}) %collective-permute-start.6) | collective-permute-done | bytes 786464 | tf_op jit(solution)/shard_map/ppermute | solution.py:38
  116.5 2.7 fusion.3
  119.2 5.8 %convolution_convert_fusion.1 = bf16[512,384]{1,0:T(8,128)(2,1)S(1)} fusion(bf16[512,6144]{1,0:T(8,128)(2,1)S(1)} %bitcast.153, bf16[6144,384]{0,1:T(8,128)(2,1)} %bitcast.154), kind=kOutput, calls=%fused_computation.31 | convolution fusion | flops 2416115712 | bytes 11403264 | tf_op jit(solution)/shard_map/dot_general | solution.py:247
  125.7 2.4 all_gather.7
  134.3 3.4 collective-permute-done.11.refs_5_
  139.7 4.4 %collective-permute-done.12.refs_6_ = bf16[512,128]{1,0:T(8,128)(2,1)S(1)} collective-permute-done((bf16[512,128]{1,0:T(8,128)(2,1)S(1)}, bf16[512,128]{1,0:T(8,128)(2,1)S(1)}, u32[]{:S(2)}, u32[]{:S(2)}) %collective-permute-start.12) | collective-permute-done | bytes 131104 | tf_op jit(solution)/shard_map/ppermute | solution.py:38
  145.0 17.1 %collective-permute-done.13.refs_7_ = bf16[512,128]{1,0:T(8,128)(2,1)} collective-permute-done((bf16[512,128]{1,0:T(8,128)(2,1)S(1)}, bf16[512,128]{1,0:T(8,128)(2,1)}, u32[]{:S(2)}, u32[]{:S(2)}) %collective-permute-start.13) | collective-permute-done | bytes 131104 | tf_op jit(solution)/shard_map/ppermute | solution.py:38
  162.8 1.6 collective-permute-start.16
  165.2 17.5 %collective-permute-done.16.refs_11_ = bf16[128,3072]{1,0:T(8,128)(2,1)S(1)} collective-permute-done((bf16[128,3072]{1,0:T(8,128)(2,1)S(1)}, bf16[128,3072]{1,0:T(8,128)(2,1)S(1)}, u32[]{:S(2)}, u32[]{:S(2)}) %collective-permute-start.16) | collective-permute-done | bytes 786464 | tf_op jit(solution)/shard_map/ppermute | solution.py:34
  182.7 1.4 collective-permute-done.20.refs_15_
  184.1 1.6 collective-permute-start.17
  186.3 16.7 %collective-permute-done.17.refs_12_ = bf16[128,3072]{1,0:T(8,128)(2,1)} collective-permute-done((bf16[128,3072]{1,0:T(8,128)(2,1)S(1)}, bf16[128,3072]{1,0:T(8,128)(2,1)}, u32[]{:S(2)}, u32[]{:S(2)}) %collective-permute-start.17) | collective-permute-done | bytes 786464 | tf_op jit(solution)/shard_map/ppermute | solution.py:34
  203.0 1.6 collective-permute-start.7
  204.6 4.3 %collective-permute-done.7.refs_1_ = bf16[512,128]{1,0:T(8,128)(2,1)S(1)} collective-permute-done((bf16[512,128]{1,0:T(8,128)(2,1)S(1)}, bf16[512,128]{1,0:T(8,128)(2,1)S(1)}, u32[]{:S(2)}, u32[]{:S(2)}) %collective-permute-start.7) | collective-permute-done | bytes 131104 | tf_op jit(solution)/shard_map/ppermute | solution.py:34
  208.9 1.6 collective-permute-start.8
  210.5 3.5 %collective-permute-done.8.refs_2_ = bf16[512,128]{1,0:T(8,128)(2,1)S(1)} collective-permute-done((bf16[512,128]{1,0:T(8,128)(2,1)S(1)}, bf16[512,128]{1,0:T(8,128)(2,1)S(1)}, u32[]{:S(2)}, u32[]{:S(2)}) %collective-permute-start.8) | collective-permute-done | bytes 131104 | tf_op jit(solution)/shard_map/ppermute | solution.py:34
  214.1 1.6 collective-permute-start.9
  215.6 3.5 collective-permute-done.9.refs_3_
  219.1 1.6 collective-permute-start.10
  221.3 3.1 collective-permute-done.10.refs_4_
  224.5 21.6 %shard_map.145 = (f32[512,6144]{1,0:T(8,128)}, f32[512,128]{1,0:T(8,128)}) custom-call(s32[1]{0:T(128)} %bitcast.span_ref, bf16[512,128]{1,0:T(8,128)(2,1)} %bitcast.166, bf16[512,128]{1,0:T(8,128)(2,1)} %copy-done.19, bf16[512,128]{1,0:T(8,128)(2,1)} %copy-done.20, bf16[512,128]{1,0:T(8,128)(2,1)} %collective-permute-done.9.refs_3_, ...), custom_call_target="tpu_custom_call" | custom-call | flops 6442450944 | bytes 32505856 | tf_op jit(solution)/shard_map/pallas_call | solution.py:134
  247.2 15.5 %convolution_convert_fusion = bf16[4,128,6144]{2,1,0:T(8,128)(2,1)} fusion(bf16[256,6144]{1,0:T(8,128)(2,1)} %collective-permute-done.30, bf16[256,6144]{1,0:T(8,128)(2,1)} %param.25, bf16[6144,256]{1,0:T(8,128)(2,1)} %collective-permute-done.29, bf16[6144,256]{1,0:T(8,128)(2,1)} %param.24, f32[4,128,6144]{2,1,0:T(8,128)} %bitcast.159, ...), kind=kOutput, calls=%fused_computation.7 | convolution fusion | flops 6485704704 | bytes 31655936 | tf_op jit(solution)/shard_map/dot_general | solution.py:307
  264.0 1.6 collective-permute-start.31
  267.2 4.6 %collective-permute-done.31 = bf16[512,384]{1,0:T(8,128)(2,1)S(1)} collective-permute-done((bf16[512,384]{1,0:T(8,128)(2,1)S(1)}, bf16[512,384]{1,0:T(8,128)(2,1)S(1)}, u32[]{:S(2)}, u32[]{:S(2)}) %collective-permute-start.31) | collective-permute-done | bytes 393248 | tf_op jit(solution)/shard_map/ppermute | solution.py:61
  271.8 1.6 collective-permute-done.38
  274.7 1.6 collective-permute-start.32
  278.1 4.9 %collective-permute-done.32 = bf16[512,384]{1,0:T(8,128)(2,1)S(1)} collective-permute-done((bf16[512,384]{1,0:T(8,128)(2,1)S(1)}, bf16[512,384]{1,0:T(8,128)(2,1)S(1)}, u32[]{:S(2)}, u32[]{:S(2)}) %collective-permute-start.32) | collective-permute-done | bytes 393248 | tf_op jit(solution)/shard_map/ppermute | solution.py:61
  283.0 2.0 collective-permute-done.39
  286.3 2.5 collective-permute-start.33
  289.5 7.3 %collective-permute-done.33 = bf16[512,384]{1,0:T(8,128)(2,1)S(1)} collective-permute-done((bf16[512,384]{1,0:T(8,128)(2,1)S(1)}, bf16[512,384]{1,0:T(8,128)(2,1)S(1)}, u32[]{:S(2)}, u32[]{:S(2)}) %collective-permute-start.33) | collective-permute-done | bytes 393248 | tf_op jit(solution)/shard_map/ppermute | solution.py:61
  296.8 2.8 collective-permute-done.40
  303.0 9.9 %collective-permute-done.34 = bf16[512,384]{1,0:T(8,128)(2,1)S(1)} collective-permute-done((bf16[512,384]{1,0:T(8,128)(2,1)S(1)}, bf16[512,384]{1,0:T(8,128)(2,1)S(1)}, u32[]{:S(2)}, u32[]{:S(2)}) %collective-permute-start.34) | collective-permute-done | bytes 393248 | tf_op jit(solution)/shard_map/ppermute | solution.py:61
  317.1 8.5 %collective-permute-done.35 = bf16[512,384]{1,0:T(8,128)(2,1)S(1)} collective-permute-done((bf16[512,384]{1,0:T(8,128)(2,1)S(1)}, bf16[512,384]{1,0:T(8,128)(2,1)S(1)}, u32[]{:S(2)}, u32[]{:S(2)}) %collective-permute-start.35) | collective-permute-done | bytes 393248 | tf_op jit(solution)/shard_map/ppermute | solution.py:61
  329.4 8.3 %collective-permute-done.36 = bf16[512,384]{1,0:T(8,128)(2,1)S(1)} collective-permute-done((bf16[512,384]{1,0:T(8,128)(2,1)S(1)}, bf16[512,384]{1,0:T(8,128)(2,1)S(1)}, u32[]{:S(2)}, u32[]{:S(2)}) %collective-permute-start.36) | collective-permute-done | bytes 393248 | tf_op jit(solution)/shard_map/ppermute | solution.py:61
  338.2 2.2 add_convert_fusion.13
  342.4 6.0 %collective-permute-done.37 = bf16[512,384]{1,0:T(8,128)(2,1)S(1)} collective-permute-done((bf16[512,384]{1,0:T(8,128)(2,1)}, bf16[512,384]{1,0:T(8,128)(2,1)S(1)}, u32[]{:S(2)}, u32[]{:S(2)}) %collective-permute-start.37) | collective-permute-done | bytes 393248 | tf_op jit(solution)/shard_map/ppermute | solution.py:61
  350.4 2.6 add_convert_fusion.2
  (146 shorter events, 51.0 us)
Async XLA Ops:
  0.0 21.6 %collective-permute-start = (bf16[4,128,768]{2,1,0:T(8,128)(2,1)}, bf16[4,128,768]{2,1,0:T(8,128)(2,1)}, u32[]{:S(2)}, u32[]{:S(2)}) collective-permute-start(bf16[4,128,768]{2,1,0:T(8,128)(2,1)} %param.15), channel_id=1, source_target_pairs={{0,2},{2,4},{4,6},{6,7},{7,5},{5,3},{3,1},{1,0},{8,10},{10,12},{12... | collective-permute-start | bytes 2359304 | tf_op jit(solution)/shard_map/ppermute | solution.py:34
  3.0 53.3 %collective-permute-start.4 = (bf16[4,128,768]{2,1,0:T(8,128)(2,1)}, bf16[4,128,768]{2,1,0:T(8,128)(2,1)}, u32[]{:S(2)}, u32[]{:S(2)}) collective-permute-start(bf16[4,128,768]{2,1,0:T(8,128)(2,1)} %param.15), channel_id=1, source_target_pairs={{0,1},{2,0},{4,2},{6,4},{7,6},{5,7},{3,5},{1,3},{8,9},{10,8},{12,1... | collective-permute-start | bytes 2359304 | tf_op jit(solution)/shard_map/ppermute | solution.py:38
  3.1 129.9 %copy-start.4 = (bf16[128,3072]{1,0:T(8,128)(2,1)}, bf16[128,3072]{1,0:T(8,128)(2,1)S(1)}, u32[]{:S(2)}) copy-start(bf16[128,3072]{1,0:T(8,128)(2,1)S(1)} %constant_dynamic-slice_fusion.2.refs_8_) | copy-start | bytes 2359300
  3.1 129.9 %collective-permute-start.14 = (bf16[128,3072]{1,0:T(8,128)(2,1)S(1)}, bf16[128,3072]{1,0:T(8,128)(2,1)}, u32[]{:S(2)}, u32[]{:S(2)}) collective-permute-start(bf16[128,3072]{1,0:T(8,128)(2,1)S(1)} %constant_dynamic-slice_fusion.2.refs_8_), channel_id=1, source_target_pairs={{0,2},{2,4},{4,6},{6,7},{7,5},{5,3},{3,1},{1,0},{8,10},{10,12},{12... | collective-permute-start | bytes 2359304 | tf_op jit(solution)/shard_map/ppermute | solution.py:34
  5.2 133.4 %collective-permute-start.18 = (bf16[128,3072]{1,0:T(8,128)(2,1)S(1)}, bf16[128,3072]{1,0:T(8,128)(2,1)}, u32[]{:S(2)}, u32[]{:S(2)}) collective-permute-start(bf16[128,3072]{1,0:T(8,128)(2,1)S(1)} %constant_dynamic-slice_fusion.2.refs_8_), channel_id=1, source_target_pairs={{0,1},{2,0},{4,2},{6,4},{7,6},{5,7},{3,5},{1,3},{8,9},{10,8},{12,1... | collective-permute-start | bytes 2359304 | tf_op jit(solution)/shard_map/ppermute | solution.py:38
  21.7 32.8 %collective-permute-start.1 = (bf16[4,128,768]{2,1,0:T(8,128)(2,1)}, bf16[4,128,768]{2,1,0:T(8,128)(2,1)S(1)}, u32[]{:S(2)}, u32[]{:S(2)}) collective-permute-start(bf16[4,128,768]{2,1,0:T(8,128)(2,1)} %collective-permute-done), channel_id=1, source_target_pairs={{0,2},{2,4},{4,6},{6,7},{7,5},{5,3},{3,1},{1,0},{8,10},{10,12},{12... | collective-permute-start | bytes 2359304 | tf_op jit(solution)/shard_map/ppermute | solution.py:34
  54.4 18.8 %collective-permute-start.2 = (bf16[4,128,768]{2,1,0:T(8,128)(2,1)S(1)}, bf16[4,128,768]{2,1,0:T(8,128)(2,1)}, u32[]{:S(2)}, u32[]{:S(2)}) collective-permute-start(bf16[4,128,768]{2,1,0:T(8,128)(2,1)S(1)} %collective-permute-done.1), channel_id=1, source_target_pairs={{0,2},{2,4},{4,6},{6,7},{7,5},{5,3},{3,1},{1,0},{8,10},{10,12},{12... | collective-permute-start | bytes 2359304 | tf_op jit(solution)/shard_map/ppermute | solution.py:34
  56.3 41.3 %collective-permute-start.5 = (bf16[4,128,768]{2,1,0:T(8,128)(2,1)}, bf16[4,128,768]{2,1,0:T(8,128)(2,1)}, u32[]{:S(2)}, u32[]{:S(2)}) collective-permute-start(bf16[4,128,768]{2,1,0:T(8,128)(2,1)} %collective-permute-done.4), channel_id=1, source_target_pairs={{0,1},{2,0},{4,2},{6,4},{7,6},{5,7},{3,5},{1,3},{8,9},{10,8},{12,1... | collective-permute-start | bytes 2359304 | tf_op jit(solution)/shard_map/ppermute | solution.py:38
  73.3 28.7 %collective-permute-start.3 = (bf16[4,128,768]{2,1,0:T(8,128)(2,1)}, bf16[4,128,768]{2,1,0:T(8,128)(2,1)}, u32[]{:S(2)}, u32[]{:S(2)}) collective-permute-start(bf16[4,128,768]{2,1,0:T(8,128)(2,1)} %collective-permute-done.2), channel_id=1, source_target_pairs={{0,2},{2,4},{4,6},{6,7},{7,5},{5,3},{3,1},{1,0},{8,10},{10,12},{12... | collective-permute-start | bytes 2359304 | tf_op jit(solution)/shard_map/ppermute | solution.py:34
  97.6 17.5 %collective-permute-start.6 = (bf16[4,128,768]{2,1,0:T(8,128)(2,1)}, bf16[4,128,768]{2,1,0:T(8,128)(2,1)S(1)}, u32[]{:S(2)}, u32[]{:S(2)}) collective-permute-start(bf16[4,128,768]{2,1,0:T(8,128)(2,1)} %collective-permute-done.5), channel_id=1, source_target_pairs={{0,1},{2,0},{4,2},{6,4},{7,6},{5,7},{3,5},{1,3},{8,9},{10,8},{12,1... | collective-permute-start | bytes 2359304 | tf_op jit(solution)/shard_map/ppermute | solution.py:38
  132.1 5.6 %collective-permute-start.11 = (bf16[512,128]{1,0:T(8,128)(2,1)S(1)}, bf16[512,128]{1,0:T(8,128)(2,1)S(1)}, u32[]{:S(2)}, u32[]{:S(2)}) collective-permute-start(bf16[512,128]{1,0:T(8,128)(2,1)S(1)} %bitcast.164), channel_id=1, source_target_pairs={{0,1},{2,0},{4,2},{6,4},{7,6},{5,7},{3,5},{1,3},{8,9},{10,8},{12,1... | collective-permute-start | bytes 393224 | tf_op jit(solution)/shard_map/ppermute | solution.py:38
  133.0 29.1 %collective-permute-start.21 = (bf16[128,3072]{1,0:T(8,128)(2,1)S(1)}, bf16[128,3072]{1,0:T(8,128)(2,1)S(1)}, u32[]{:S(2)}, u32[]{:S(2)}) collective-permute-start(bf16[128,3072]{1,0:T(8,128)(2,1)S(1)} %constant_dynamic-slice_fusion.2.refs_8_), channel_id=1, source_target_pairs={{0,8},{8,0},{1,9},{9,1},{2,10},{10,2},{3,11},{11,3},{4,12},{12,4},... | collective-permute-start | bytes 2359304 | tf_op jit(solution)/shard_map/ppermute | solution.py:227
  133.0 29.6 %collective-permute-start.15 = (bf16[128,3072]{1,0:T(8,128)(2,1)}, bf16[128,3072]{1,0:T(8,128)(2,1)S(1)}, u32[]{:S(2)}, u32[]{:S(2)}) collective-permute-start(bf16[128,3072]{1,0:T(8,128)(2,1)} %collective-permute-done.14.refs_9_), channel_id=1, source_target_pairs={{0,2},{2,4},{4,6},{6,7},{7,5},{5,3},{3,1},{1,0},{8,10},{10,12},{12... | collective-permute-start | bytes 2359304 | tf_op jit(solution)/shard_map/ppermute | solution.py:34
  137.7 86.7 %copy-start.17 = (bf16[512,128]{1,0:T(8,128)(2,1)}, bf16[512,128]{1,0:T(8,128)(2,1)S(1)}, u32[]{:S(2)}) copy-start(bf16[512,128]{1,0:T(8,128)(2,1)S(1)} %collective-permute-done.11.refs_5_) | copy-start | bytes 393220
  137.7 6.4 %collective-permute-start.12 = (bf16[512,128]{1,0:T(8,128)(2,1)S(1)}, bf16[512,128]{1,0:T(8,128)(2,1)S(1)}, u32[]{:S(2)}, u32[]{:S(2)}) collective-permute-start(bf16[512,128]{1,0:T(8,128)(2,1)S(1)} %collective-permute-done.11.refs_5_), channel_id=1, source_target_pairs={{0,1},{2,0},{4,2},{6,4},{7,6},{5,7},{3,5},{1,3},{8,9},{10,8},{12,1... | collective-permute-start | bytes 393224 | tf_op jit(solution)/shard_map/ppermute | solution.py:38
  138.6 24.2 %collective-permute-start.19 = (bf16[128,3072]{1,0:T(8,128)(2,1)}, bf16[128,3072]{1,0:T(8,128)(2,1)S(1)}, u32[]{:S(2)}, u32[]{:S(2)}) collective-permute-start(bf16[128,3072]{1,0:T(8,128)(2,1)} %collective-permute-done.18.refs_13_), channel_id=1, source_target_pairs={{0,1},{2,0},{4,2},{6,4},{7,6},{5,7},{3,5},{1,3},{8,9},{10,8},{12,1... | collective-permute-start | bytes 2359304 | tf_op jit(solution)/shard_map/ppermute | solution.py:38
  139.7 24.7 %collective-permute-start.22 = (bf16[128,3072]{1,0:T(8,128)(2,1)}, bf16[128,3072]{1,0:T(8,128)(2,1)S(1)}, u32[]{:S(2)}, u32[]{:S(2)}) collective-permute-start(bf16[128,3072]{1,0:T(8,128)(2,1)} %collective-permute-done.14.refs_9_), channel_id=1, source_target_pairs={{0,8},{8,0},{1,9},{9,1},{2,10},{10,2},{3,11},{11,3},{4,12},{12,4},... | collective-permute-start | bytes 2359304 | tf_op jit(solution)/shard_map/ppermute | solution.py:227
  144.1 80.3 %copy-start.18 = (bf16[512,128]{1,0:T(8,128)(2,1)}, bf16[512,128]{1,0:T(8,128)(2,1)S(1)}, u32[]{:S(2)}) copy-start(bf16[512,128]{1,0:T(8,128)(2,1)S(1)} %collective-permute-done.12.refs_6_) | copy-start | bytes 393220
  144.1 18.0 %collective-permute-start.13 = (bf16[512,128]{1,0:T(8,128)(2,1)S(1)}, bf16[512,128]{1,0:T(8,128)(2,1)}, u32[]{:S(2)}, u32[]{:S(2)}) collective-permute-start(bf16[512,128]{1,0:T(8,128)(2,1)S(1)} %collective-permute-done.12.refs_6_), channel_id=1, source_target_pairs={{0,1},{2,0},{4,2},{6,4},{7,6},{5,7},{3,5},{1,3},{8,9},{10,8},{12,1... | collective-permute-start | bytes 393224 | tf_op jit(solution)/shard_map/ppermute | solution.py:38
  162.2 2.9 collective-permute-start.26
  162.2 85.0 %collective-permute-start.29 = (bf16[6144,256]{1,0:T(8,128)(2,1)}, bf16[6144,256]{1,0:T(8,128)(2,1)}, u32[]{:S(2)}, u32[]{:S(2)}) collective-permute-start(bf16[6144,256]{1,0:T(8,128)(2,1)} %param.24), channel_id=1, source_target_pairs={{0,8},{8,0},{1,9},{9,1},{2,10},{10,2},{3,11},{11,3},{4,12},{12,4},... | collective-permute-start | bytes 9437192 | tf_op jit(solution)/shard_map/ppermute | solution.py:275
  162.7 84.5 %collective-permute-start.30 = (bf16[256,6144]{1,0:T(8,128)(2,1)}, bf16[256,6144]{1,0:T(8,128)(2,1)}, u32[]{:S(2)}, u32[]{:S(2)}) collective-permute-start(bf16[256,6144]{1,0:T(8,128)(2,1)} %param.25), channel_id=1, source_target_pairs={{0,8},{8,0},{1,9},{9,1},{2,10},{10,2},{3,11},{11,3},{4,12},{12,4},... | collective-permute-start | bytes 9437192 | tf_op jit(solution)/shard_map/ppermute | solution.py:276
  162.8 19.9 %collective-permute-start.16 = (bf16[128,3072]{1,0:T(8,128)(2,1)S(1)}, bf16[128,3072]{1,0:T(8,128)(2,1)S(1)}, u32[]{:S(2)}, u32[]{:S(2)}) collective-permute-start(bf16[128,3072]{1,0:T(8,128)(2,1)S(1)} %collective-permute-done.15.refs_10_), channel_id=1, source_target_pairs={{0,2},{2,4},{4,6},{6,7},{7,5},{5,3},{3,1},{1,0},{8,10},{10,12},{12... | collective-permute-start | bytes 2359304 | tf_op jit(solution)/shard_map/ppermute | solution.py:34
  164.4 19.7 %collective-permute-start.20 = (bf16[128,3072]{1,0:T(8,128)(2,1)S(1)}, bf16[128,3072]{1,0:T(8,128)(2,1)}, u32[]{:S(2)}, u32[]{:S(2)}) collective-permute-start(bf16[128,3072]{1,0:T(8,128)(2,1)S(1)} %collective-permute-done.19.refs_14_), channel_id=1, source_target_pairs={{0,1},{2,0},{4,2},{6,4},{7,6},{5,7},{3,5},{1,3},{8,9},{10,8},{12,1... | collective-permute-start | bytes 2359304 | tf_op jit(solution)/shard_map/ppermute | solution.py:38
  165.0 20.6 %collective-permute-start.23 = (bf16[128,3072]{1,0:T(8,128)(2,1)S(1)}, bf16[128,3072]{1,0:T(8,128)(2,1)S(1)}, u32[]{:S(2)}, u32[]{:S(2)}) collective-permute-start(bf16[128,3072]{1,0:T(8,128)(2,1)S(1)} %collective-permute-done.15.refs_10_), channel_id=1, source_target_pairs={{0,8},{8,0},{1,9},{9,1},{2,10},{10,2},{3,11},{11,3},{4,12},{12,4},... | collective-permute-start | bytes 2359304 | tf_op jit(solution)/shard_map/ppermute | solution.py:227
  182.7 3.1 collective-permute-start.27
  184.1 18.9 %collective-permute-start.17 = (bf16[128,3072]{1,0:T(8,128)(2,1)S(1)}, bf16[128,3072]{1,0:T(8,128)(2,1)}, u32[]{:S(2)}, u32[]{:S(2)}) collective-permute-start(bf16[128,3072]{1,0:T(8,128)(2,1)S(1)} %collective-permute-done.16.refs_11_), channel_id=1, source_target_pairs={{0,2},{2,4},{4,6},{6,7},{7,5},{5,3},{3,1},{1,0},{8,10},{10,12},{12... | collective-permute-start | bytes 2359304 | tf_op jit(solution)/shard_map/ppermute | solution.py:34
  185.7 17.3 %collective-permute-start.24 = (bf16[128,3072]{1,0:T(8,128)(2,1)S(1)}, bf16[128,3072]{1,0:T(8,128)(2,1)S(1)}, u32[]{:S(2)}, u32[]{:S(2)}) collective-permute-start(bf16[128,3072]{1,0:T(8,128)(2,1)S(1)} %collective-permute-done.16.refs_11_), channel_id=1, source_target_pairs={{0,8},{8,0},{1,9},{9,1},{2,10},{10,2},{3,11},{11,3},{4,12},{12,4},... | collective-permute-start | bytes 2359304 | tf_op jit(solution)/shard_map/ppermute | solution.py:227
  185.8 35.6 %collective-permute-start.28 = (bf16[128,3072]{1,0:T(8,128)(2,1)}, bf16[128,3072]{1,0:T(8,128)(2,1)}, u32[]{:S(2)}, u32[]{:S(2)}) collective-permute-start(bf16[128,3072]{1,0:T(8,128)(2,1)} %collective-permute-done.20.refs_15_), channel_id=1, source_target_pairs={{0,8},{8,0},{1,9},{9,1},{2,10},{10,2},{3,11},{11,3},{4,12},{12,4},... | collective-permute-start | bytes 2359304 | tf_op jit(solution)/shard_map/ppermute | solution.py:227
  203.0 21.5 %collective-permute-start.25 = (bf16[128,3072]{1,0:T(8,128)(2,1)}, bf16[128,3072]{1,0:T(8,128)(2,1)}, u32[]{:S(2)}, u32[]{:S(2)}) collective-permute-start(bf16[128,3072]{1,0:T(8,128)(2,1)} %collective-permute-done.17.refs_12_), channel_id=1, source_target_pairs={{0,8},{8,0},{1,9},{9,1},{2,10},{10,2},{3,11},{11,3},{4,12},{12,4},... | collective-permute-start | bytes 2359304 | tf_op jit(solution)/shard_map/ppermute | solution.py:227
  203.0 5.9 %collective-permute-start.7 = (bf16[512,128]{1,0:T(8,128)(2,1)S(1)}, bf16[512,128]{1,0:T(8,128)(2,1)S(1)}, u32[]{:S(2)}, u32[]{:S(2)}) collective-permute-start(bf16[512,128]{1,0:T(8,128)(2,1)S(1)} %bitcast.165), channel_id=1, source_target_pairs={{0,2},{2,4},{4,6},{6,7},{7,5},{5,3},{3,1},{1,0},{8,10},{10,12},{12... | collective-permute-start | bytes 393224 | tf_op jit(solution)/shard_map/ppermute | solution.py:34
  208.9 5.1 %collective-permute-start.8 = (bf16[512,128]{1,0:T(8,128)(2,1)S(1)}, bf16[512,128]{1,0:T(8,128)(2,1)S(1)}, u32[]{:S(2)}, u32[]{:S(2)}) collective-permute-start(bf16[512,128]{1,0:T(8,128)(2,1)S(1)} %collective-permute-done.7.refs_1_), channel_id=1, source_target_pairs={{0,2},{2,4},{4,6},{6,7},{7,5},{5,3},{3,1},{1,0},{8,10},{10,12},{12... | collective-permute-start | bytes 393224 | tf_op jit(solution)/shard_map/ppermute | solution.py:34
  214.1 5.1 %collective-permute-start.9 = (bf16[512,128]{1,0:T(8,128)(2,1)S(1)}, bf16[512,128]{1,0:T(8,128)(2,1)}, u32[]{:S(2)}, u32[]{:S(2)}) collective-permute-start(bf16[512,128]{1,0:T(8,128)(2,1)S(1)} %collective-permute-done.8.refs_2_), channel_id=1, source_target_pairs={{0,2},{2,4},{4,6},{6,7},{7,5},{5,3},{3,1},{1,0},{8,10},{10,12},{12... | collective-permute-start | bytes 393224 | tf_op jit(solution)/shard_map/ppermute | solution.py:34
  219.1 5.3 %collective-permute-start.10 = (bf16[512,128]{1,0:T(8,128)(2,1)}, bf16[512,128]{1,0:T(8,128)(2,1)}, u32[]{:S(2)}, u32[]{:S(2)}) collective-permute-start(bf16[512,128]{1,0:T(8,128)(2,1)} %collective-permute-done.9.refs_3_), channel_id=1, source_target_pairs={{0,2},{2,4},{4,6},{6,7},{7,5},{5,3},{3,1},{1,0},{8,10},{10,12},{12... | collective-permute-start | bytes 393224 | tf_op jit(solution)/shard_map/ppermute | solution.py:34
  264.0 7.8 %collective-permute-start.31 = (bf16[512,384]{1,0:T(8,128)(2,1)S(1)}, bf16[512,384]{1,0:T(8,128)(2,1)S(1)}, u32[]{:S(2)}, u32[]{:S(2)}) collective-permute-start(bf16[512,384]{1,0:T(8,128)(2,1)S(1)} %get-tuple-element.29), channel_id=1, source_target_pairs={{0,2},{2,4},{4,6},{6,7},{7,5},{5,3},{3,1},{1,0},{8,10},{10,12},{12... | collective-permute-start | bytes 1179656 | tf_op jit(solution)/shard_map/ppermute | solution.py:61
  265.6 7.8 %collective-permute-start.38 = (bf16[512,384]{1,0:T(8,128)(2,1)S(1)}, bf16[512,384]{1,0:T(8,128)(2,1)S(1)}, u32[]{:S(2)}, u32[]{:S(2)}) collective-permute-start(bf16[512,384]{1,0:T(8,128)(2,1)S(1)} %get-tuple-element.30), channel_id=1, source_target_pairs={{0,1},{2,0},{4,2},{6,4},{7,6},{5,7},{3,5},{1,3},{8,9},{10,8},{12,1... | collective-permute-start | bytes 1179656 | tf_op jit(solution)/shard_map/ppermute | solution.py:63
  274.7 8.3 %collective-permute-start.32 = (bf16[512,384]{1,0:T(8,128)(2,1)S(1)}, bf16[512,384]{1,0:T(8,128)(2,1)S(1)}, u32[]{:S(2)}, u32[]{:S(2)}) collective-permute-start(bf16[512,384]{1,0:T(8,128)(2,1)S(1)} %get-tuple-element.27), channel_id=1, source_target_pairs={{0,2},{2,4},{4,6},{6,7},{7,5},{5,3},{3,1},{1,0},{8,10},{10,12},{12... | collective-permute-start | bytes 1179656 | tf_op jit(solution)/shard_map/ppermute | solution.py:61
  276.3 8.7 %collective-permute-start.39 = (bf16[512,384]{1,0:T(8,128)(2,1)S(1)}, bf16[512,384]{1,0:T(8,128)(2,1)S(1)}, u32[]{:S(2)}, u32[]{:S(2)}) collective-permute-start(bf16[512,384]{1,0:T(8,128)(2,1)S(1)} %get-tuple-element.28), channel_id=1, source_target_pairs={{0,1},{2,0},{4,2},{6,4},{7,6},{5,7},{3,5},{1,3},{8,9},{10,8},{12,1... | collective-permute-start | bytes 1179656 | tf_op jit(solution)/shard_map/ppermute | solution.py:63
  286.3 10.5 %collective-permute-start.33 = (bf16[512,384]{1,0:T(8,128)(2,1)S(1)}, bf16[512,384]{1,0:T(8,128)(2,1)S(1)}, u32[]{:S(2)}, u32[]{:S(2)}) collective-permute-start(bf16[512,384]{1,0:T(8,128)(2,1)S(1)} %get-tuple-element.25), channel_id=1, source_target_pairs={{0,2},{2,4},{4,6},{6,7},{7,5},{5,3},{3,1},{1,0},{8,10},{10,12},{12... | collective-permute-start | bytes 1179656 | tf_op jit(solution)/shard_map/ppermute | solution.py:61
  288.8 10.8 %collective-permute-start.40 = (bf16[512,384]{1,0:T(8,128)(2,1)S(1)}, bf16[512,384]{1,0:T(8,128)(2,1)S(1)}, u32[]{:S(2)}, u32[]{:S(2)}) collective-permute-start(bf16[512,384]{1,0:T(8,128)(2,1)S(1)} %get-tuple-element.26), channel_id=1, source_target_pairs={{0,1},{2,0},{4,2},{6,4},{7,6},{5,7},{3,5},{1,3},{8,9},{10,8},{12,1... | collective-permute-start | bytes 1179656 | tf_op jit(solution)/shard_map/ppermute | solution.py:63
  300.9 12.0 %collective-permute-start.34 = (bf16[512,384]{1,0:T(8,128)(2,1)S(1)}, bf16[512,384]{1,0:T(8,128)(2,1)S(1)}, u32[]{:S(2)}, u32[]{:S(2)}) collective-permute-start(bf16[512,384]{1,0:T(8,128)(2,1)S(1)} %get-tuple-element.23), channel_id=1, source_target_pairs={{0,2},{2,4},{4,6},{6,7},{7,5},{5,3},{3,1},{1,0},{8,10},{10,12},{12... | collective-permute-start | bytes 1179656 | tf_op jit(solution)/shard_map/ppermute | solution.py:61
  302.3 11.4 %collective-permute-start.41 = (bf16[512,384]{1,0:T(8,128)(2,1)S(1)}, bf16[512,384]{1,0:T(8,128)(2,1)S(1)}, u32[]{:S(2)}, u32[]{:S(2)}) collective-permute-start(bf16[512,384]{1,0:T(8,128)(2,1)S(1)} %get-tuple-element.24), channel_id=1, source_target_pairs={{0,1},{2,0},{4,2},{6,4},{7,6},{5,7},{3,5},{1,3},{8,9},{10,8},{12,1... | collective-permute-start | bytes 1179656 | tf_op jit(solution)/shard_map/ppermute | solution.py:63
  315.0 10.6 %collective-permute-start.35 = (bf16[512,384]{1,0:T(8,128)(2,1)S(1)}, bf16[512,384]{1,0:T(8,128)(2,1)S(1)}, u32[]{:S(2)}, u32[]{:S(2)}) collective-permute-start(bf16[512,384]{1,0:T(8,128)(2,1)S(1)} %get-tuple-element.21), channel_id=1, source_target_pairs={{0,2},{2,4},{4,6},{6,7},{7,5},{5,3},{3,1},{1,0},{8,10},{10,12},{12... | collective-permute-start | bytes 1179656 | tf_op jit(solution)/shard_map/ppermute | solution.py:61
  315.9 10.1 %collective-permute-start.42 = (bf16[512,384]{1,0:T(8,128)(2,1)S(1)}, bf16[512,384]{1,0:T(8,128)(2,1)S(1)}, u32[]{:S(2)}, u32[]{:S(2)}) collective-permute-start(bf16[512,384]{1,0:T(8,128)(2,1)S(1)} %get-tuple-element.22), channel_id=1, source_target_pairs={{0,1},{2,0},{4,2},{6,4},{7,6},{5,7},{3,5},{1,3},{8,9},{10,8},{12,1... | collective-permute-start | bytes 1179656 | tf_op jit(solution)/shard_map/ppermute | solution.py:63
  327.3 10.3 %collective-permute-start.36 = (bf16[512,384]{1,0:T(8,128)(2,1)S(1)}, bf16[512,384]{1,0:T(8,128)(2,1)S(1)}, u32[]{:S(2)}, u32[]{:S(2)}) collective-permute-start(bf16[512,384]{1,0:T(8,128)(2,1)S(1)} %get-tuple-element.19), channel_id=1, source_target_pairs={{0,2},{2,4},{4,6},{6,7},{7,5},{5,3},{3,1},{1,0},{8,10},{10,12},{12... | collective-permute-start | bytes 1179656 | tf_op jit(solution)/shard_map/ppermute | solution.py:61
  328.0 10.1 %collective-permute-start.43 = (bf16[512,384]{1,0:T(8,128)(2,1)S(1)}, bf16[512,384]{1,0:T(8,128)(2,1)}, u32[]{:S(2)}, u32[]{:S(2)}) collective-permute-start(bf16[512,384]{1,0:T(8,128)(2,1)S(1)} %get-tuple-element.20), channel_id=1, source_target_pairs={{0,1},{2,0},{4,2},{6,4},{7,6},{5,7},{3,5},{1,3},{8,9},{10,8},{12,1... | collective-permute-start | bytes 1179656 | tf_op jit(solution)/shard_map/ppermute | solution.py:63
  340.3 8.0 %collective-permute-start.37 = (bf16[512,384]{1,0:T(8,128)(2,1)}, bf16[512,384]{1,0:T(8,128)(2,1)S(1)}, u32[]{:S(2)}, u32[]{:S(2)}) collective-permute-start(bf16[512,384]{1,0:T(8,128)(2,1)} %get-tuple-element.17), channel_id=1, source_target_pairs={{0,2},{2,4},{4,6},{6,7},{7,5},{5,3},{3,1},{1,0},{8,10},{10,12},{12... | collective-permute-start | bytes 1179656 | tf_op jit(solution)/shard_map/ppermute | solution.py:61
  341.0 7.9 %collective-permute-start.44 = (bf16[512,384]{1,0:T(8,128)(2,1)S(1)}, bf16[512,384]{1,0:T(8,128)(2,1)}, u32[]{:S(2)}, u32[]{:S(2)}) collective-permute-start(bf16[512,384]{1,0:T(8,128)(2,1)S(1)} %get-tuple-element.18), channel_id=1, source_target_pairs={{0,1},{2,0},{4,2},{6,4},{7,6},{5,7},{3,5},{1,3},{8,9},{10,8},{12,1... | collective-permute-start | bytes 1179656 | tf_op jit(solution)/shard_map/ppermute | solution.py:63
  (18 other events, 455.1 us)

commit v21 on v7

--- a/solution.py
+++ b/solution.py
@@ -65,62 +65,82 @@
     return jnp.concatenate([forward, backward], axis=1)
 
 
-def out_proj_kernel(group_count, tiles_per_half, span_ref, *refs):
+def out_proj_kernel(group_count, row_count, span_ref, *refs):
     att_refs = refs[:group_count]
-    mine_refs = refs[group_count:2 * group_count]
-    other_refs = refs[2 * group_count:3 * group_count]
-    out_ref = refs[3 * group_count]
+    w_refs = refs[group_count:2 * group_count]
+    hidden_ref, scale_ref = refs[2 * group_count:2 * group_count + 2]
+    out_ref, squares_ref = refs[-2:]
     tile = pl.program_id(0)
-
-    def accumulate(w_refs):
-        total = None
-        for group in range(group_count):
-            term = jnp.dot(att_refs[group][...], w_refs[group][...], preferred_element_type=jnp.float32)
-            term = term.astype(jnp.bfloat16).astype(jnp.float32)
-            total = term if total is None else total + term
-        out_ref[...] = total
-
-    @pl.when(tile < tiles_per_half)
+    total = None
+    for group in range(group_count):
+        term = jnp.dot(att_refs[group][...], w_refs[group][...], preferred_element_type=jnp.float32)
+        term = term.astype(jnp.bfloat16).astype(jnp.float32)
+        total = term if total is None else total + term
+    for span in range(scale_ref.shape[0]):
+        rows = slice(span * row_count, (span + 1) * row_count)
+        out_ref[rows, :] = (
+            hidden_ref[rows, :].astype(jnp.float32) + scale_ref[span:span + 1, :] * total[rows, :]
+        )
+    result = out_ref[...]
+    partial = jnp.broadcast_to(jnp.sum(result * result, axis=1, keepdims=True), squares_ref.shape)
+
+    @pl.when(tile == 0)
     def _():
-        accumulate(mine_refs)
-
-    @pl.when(tile >= tiles_per_half)
+        squares_ref[...] = partial
+
+    @pl.when(tile > 0)
     def _():
-        accumulate(other_refs)
-
-
-def grouped_out_proj(span_index, att_blocks, mine_blocks, other_blocks, tile_width=512):
+        squares_ref[...] += partial
+
+
+def grouped_out_half(span_index, half, att_blocks, w_blocks, hidden, scale, earlier=None, tile_width=1024):
     group_count = len(att_blocks)
     token_count, head_width = att_blocks[0].shape
-    half_width = mine_blocks[0].shape[1]
+    half_width = w_blocks[0].shape[1]
+    span_rows = scale.shape[0]
     tile_width = min(tile_width, half_width)
-    tiles_per_half = half_width // tile_width
+    tiles = half_width // tile_width
+
+    def column(n, s):
+        return ((half + s[0]) % 2) * tiles + n
+
     att_spec = pl.BlockSpec((token_count, head_width), lambda n, s: (0, 0))
-    mine_spec = pl.BlockSpec(
-        (head_width, tile_width), lambda n, s: (0, jnp.minimum(n, tiles_per_half - 1))
-    )
-    other_spec = pl.BlockSpec(
-        (head_width, tile_width), lambda n, s: (0, jnp.maximum(n - tiles_per_half, 0))
-    )
-    out_spec = pl.BlockSpec(
-        (token_count, tile_width),
-        lambda n, s: (0, ((n // tiles_per_half + s[0]) % 2) * tiles_per_half + n % tiles_per_half),
-    )
-    flops = 2 * token_count * head_width * group_count * half_width * 2
-    moved = 2 * (group_count * token_count * head_width + 2 * group_count * head_width * half_width)
+    w_spec = pl.BlockSpec((head_width, tile_width), lambda n, s: (0, n))
+    tile_spec = pl.BlockSpec((token_count, tile_width), lambda n, s: (0, column(n, s)))
+    scale_spec = pl.BlockSpec((span_rows, tile_width), lambda n, s: (0, column(n, s)))
+    squares_spec = pl.BlockSpec((token_count, 128), lambda n, s: (0, 0))
+    in_specs = [att_spec] * group_count + [w_spec] * group_count + [tile_spec, scale_spec]
+    operands = [jnp.reshape(span_index, (1,)).astype(jnp.int32), *att_blocks, *w_blocks, hidden, scale]
+    aliases = {}
+    if earlier is not None:
+        in_specs.append(pl.BlockSpec(memory_space=pl.ANY))
+        aliases = {len(operands): 0}
+        operands.append(earlier)
+    flops = 2 * token_count * head_width * group_count * half_width
+    moved = 2 * (group_count * token_count * head_width + group_count * head_width * half_width)
+    moved += token_count * half_width * (4 + 2)
+    body = functools.partial(out_proj_kernel, group_count, token_count // span_rows)
+    if earlier is not None:
+        plain = body
+
+        def body(span_ref, *refs):
+            plain(span_ref, *refs[:2 * group_count + 2], *refs[2 * group_count + 3:])
+
     return pl.pallas_call(
-        functools.partial(out_proj_kernel, group_count, tiles_per_half),
-        out_shape=jax.ShapeDtypeStruct((token_count, 2 * half_width), jnp.float32),
+        body,
+        out_shape=(
+            jax.ShapeDtypeStruct((token_count, 2 * half_width), jnp.float32),
+            jax.ShapeDtypeStruct((token_count, 128), jnp.float32),
+        ),
         grid_spec=pltpu.PrefetchScalarGridSpec(
             num_scalar_prefetch=1,
-            grid=(2 * tiles_per_half,),
-            in_specs=[att_spec] * group_count + [mine_spec] * group_count + [other_spec] * group_count,
-            out_specs=out_spec,
+            grid=(tiles,),
+            in_specs=in_specs,
+            out_specs=[tile_spec, squares_spec],
         ),
-        cost_estimate=pl.CostEstimate(
-            flops=flops, bytes_accessed=moved + token_count * 2 * half_width * 4, transcendentals=0
-        ),
-    )(jnp.reshape(span_index, (1,)).astype(jnp.int32), *att_blocks, *mine_blocks, *other_blocks)
+        input_output_aliases=aliases,
+        cost_estimate=pl.CostEstimate(flops=flops, bytes_accessed=moved, transcendentals=0),
+    )(*operands)
 
 
 def select_row(source, target):
@@ -183,6 +203,7 @@
         for step, piece in zip(steps, ring_gather(hidden_in, "tp", tp_count)):
             owner = owners[(position - step + tp_count) % tp_count]
             gathered = lax.dynamic_update_slice_in_dim(gathered, piece, owner * share_width, 2)
+        gathered_narrow = gathered
         gathered = gathered.astype(jnp.float32)
     else:
         gathered = lax.all_gather(hidden_in, "tp", axis=2, tiled=True).astype(jnp.float32)
@@ -231,11 +252,18 @@
     )(queries, cache_seen, fresh_seen)
     if gather_weights:
         att_blocks = ring_gather(attended.reshape(token_count, per_device), "tp", tp_count)
-        attn_out = grouped_out_proj(span_index, att_blocks, mine_blocks, other_blocks)
-        attn_out = attn_out.reshape(local_count, row_count, model_width)
-        residual_full = gathered + mod_rows[:, 2][:, None] * attn_out
+        hidden_rows = gathered_narrow.reshape(token_count, model_width)
+        first, first_squares = grouped_out_half(
+            span_index, 0, att_blocks, mine_blocks, hidden_rows, mod_rows[:, 2]
+        )
+        residual_rows, second_squares = grouped_out_half(
+            span_index, 1, att_blocks, other_blocks, hidden_rows, mod_rows[:, 2], earlier=first
+        )
+        square_sums = first_squares[:, 0] + second_squares[:, 0]
+        residual_full = residual_rows.reshape(local_count, row_count, model_width)
+        inverse = lax.rsqrt(square_sums.reshape(local_count, row_count, 1) / model_width + EPSILON)
         mlp_in = (
-            normalize(residual_full) * mod_rows[:, 4][:, None] + mod_rows[:, 3][:, None]
+            residual_full * inverse * mod_rows[:, 4][:, None] + mod_rows[:, 3][:, None]
         ).astype(jnp.bfloat16)
     else:
         partial_value = jnp.dot(

time: 334 us -> 321 us (0.961)
  other arithmetic: 31.7 us -> 19.4 us
  waiting for transfers between devices: 158 us -> 148 us
  Pallas kernels: 20.4 us -> 24.8 us
    reduce_sum x2 -> x1, other arithmetic: 14.7 us -> 1.31 us  [normalize(): jnp.mean(values * values, axis=-1, keepdims=True) + EPSILON]
    ppermute x12, waiting for transfers between devices: 79.3 us -> 73 us  [ring_gather(): forward = lax.ppermute(forward, axis_name, ahead)]
    ppermute x7, waiting for transfers between devices: 51.2 us -> 46.6 us  [ring_reduce_scatter(): lax.ppermute(forward.astype(jnp.bfloat16), axis_name, ahead)]
    pallas_call x1 -> x2, Pallas kernels: 20.4 us -> 24.8 us  [grouped_out_half(): pl.pallas_call(body, out_shape=(jax.ShapeDtypeStruct((token_count, 2 * ha...]
    unnamed x55 -> x65, local copies, waits for them, and re-layouts: 10.5 us -> 12.5 us
  transfers between devices with their start and end apart: 45 -> 45, of which waited for: 24 -> 24; matrix products, arithmetic and copies ran while one was open for 17% -> 14% of each run, Pallas kernels for 6% -> 8%
where the time goes in v21:
time: 321 us; the launch traced here: 320 us
  waiting for transfers between devices  148 us (46%)
  starting transfers between devices  40.9 us (13%)
  between operations  33.3 us (10%)
  matrix products  25 us (8%)
  Pallas kernels  24.8 us (8%)
  local copies, waits for them, and re-layouts  23.8 us (7%)
  other arithmetic  19.4 us (6%)
  blocking collectives  4.54 us (1%)
    ppermute x12, waiting for transfers between devices, ring_gather(): forward = lax.ppermute(forward, axis_name, ahead)  73 us
    ppermute x7, waiting for transfers between devices, ring_reduce_scatter(): lax.ppermute(forward.astype(jnp.bfloat16), axis_name, ahead)  46.6 us
    pallas_call x2, Pallas kernels, grouped_out_half(): pl.pallas_call(body, out_shape=(jax.ShapeDtypeStruct((token_count, 2 * ha...  24.8 us
    ppermute x9, waiting for transfers between devices, ring_gather(): backward = lax.ppermute(backward, axis_name, behind)  21.8 us
    ppermute x12, starting transfers between devices, ring_gather(): forward = lax.ppermute(forward, axis_name, ahead)  21.1 us
    unnamed x65, local copies, waits for them, and re-layouts  12.5 us
    dot_general x1, matrix products, local(): pre_act = jnp.dot(mlp_in, up_full, preferred_element_type=jnp.float32)  10 us
    convert_element_type x6, other arithmetic, ring_reduce_scatter(): forward.astype(jnp.bfloat16)  8.11 us
  transfers between devices with their start and end apart: 45, of which 24 were waited for; matrix products, arithmetic and copies ran while one was open for 14% of the time, Pallas kernels for 8%

profile of v21, /device:TPU:0, one launch (start us, length us, event | category | flops | bytes accessed | tf_op | source)
XLA Modules:
  0.0 320.3 jit_solution(6574808480868708606)
XLA Ops:
  7.4 3.1 collective-permute-start
  10.5 2.1 collective-permute-start.15
  14.4 14.7 %collective-permute-done = bf16[4,128,768]{2,1,0:T(8,128)(2,1)} collective-permute-done((bf16[4,128,768]{2,1,0:T(8,128)(2,1)}, bf16[4,128,768]{2,1,0:T(8,128)(2,1)}, u32[]{:S(2)}, u32[]{:S(2)}) %collective-permute-start) | collective-permute-done | bytes 786464 | tf_op jit(solution)/shard_map/ppermute | solution.py:34
  29.1 2.1 collective-permute-start.1
  31.5 30.3 %collective-permute-done.1 = bf16[4,128,768]{2,1,0:T(8,128)(2,1)S(1)} collective-permute-done((bf16[4,128,768]{2,1,0:T(8,128)(2,1)}, bf16[4,128,768]{2,1,0:T(8,128)(2,1)S(1)}, u32[]{:S(2)}, u32[]{:S(2)}) %collective-permute-start.1) | collective-permute-done | bytes 786464 | tf_op jit(solution)/shard_map/ppermute | solution.py:34
  61.8 1.8 collective-permute-start.2
  64.0 1.8 collective-permute-start.17
  67.3 2.2 all_gather.12
  69.5 12.9 %collective-permute-done.2 = bf16[4,128,768]{2,1,0:T(8,128)(2,1)} collective-permute-done((bf16[4,128,768]{2,1,0:T(8,128)(2,1)S(1)}, bf16[4,128,768]{2,1,0:T(8,128)(2,1)}, u32[]{:S(2)}, u32[]{:S(2)}) %collective-permute-start.2) | collective-permute-done | bytes 786464 | tf_op jit(solution)/shard_map/ppermute | solution.py:34
  82.4 1.8 collective-permute-start.3
  99.3 6.7 %copy.31 = bf16[6144,3,128]{0,2,1:T(8,128)(2,1)} copy(bf16[6144,3,128]{2,0,1:T(8,128)(2,1)} %param.22) | data formatting | bytes 9437184 | tf_op args[7]
  107.3 1.7 collective-permute-start.6
  113.1 3.0 collective-permute-done.3
  119.9 8.1 %collective-permute-done.25.refs_14_ = bf16[128,3072]{1,0:T(8,128)(2,1)} collective-permute-done((bf16[128,3072]{1,0:T(8,128)(2,1)}, bf16[128,3072]{1,0:T(8,128)(2,1)}, u32[]{:S(2)}, u32[]{:S(2)}) %collective-permute-start.25) | collective-permute-done | bytes 786464 | tf_op jit(solution)/shard_map/ppermute | solution.py:38
  127.9 13.8 %collective-permute-done.6 = bf16[4,128,768]{2,1,0:T(8,128)(2,1)S(1)} collective-permute-done((bf16[4,128,768]{2,1,0:T(8,128)(2,1)}, bf16[4,128,768]{2,1,0:T(8,128)(2,1)S(1)}, u32[]{:S(2)}, u32[]{:S(2)}) %collective-permute-start.6) | collective-permute-done | bytes 786464 | tf_op jit(solution)/shard_map/ppermute | solution.py:38
  141.9 1.8 collective-permute-start.21
  145.1 2.7 fusion.3
  147.9 5.8 %convolution_convert_fusion.1 = bf16[512,384]{1,0:T(8,128)(2,1)S(1)} fusion(bf16[512,6144]{1,0:T(8,128)(2,1)S(1)} %bitcast.155, bf16[6144,384]{0,1:T(8,128)(2,1)} %bitcast.156), kind=kOutput, calls=%fused_computation.27 | convolution fusion | flops 2416115712 | bytes 11403264 | tf_op jit(solution)/shard_map/dot_general | solution.py:230
  154.5 2.4 all_gather.13
  160.7 1.6 collective-permute-start.7
  162.8 3.5 %collective-permute-done.7.refs_1_ = bf16[512,128]{1,0:T(8,128)(2,1)S(1)} collective-permute-done((bf16[512,128]{1,0:T(8,128)(2,1)S(1)}, bf16[512,128]{1,0:T(8,128)(2,1)S(1)}, u32[]{:S(2)}, u32[]{:S(2)}) %collective-permute-start.7) | collective-permute-done | bytes 131104 | tf_op jit(solution)/shard_map/ppermute | solution.py:34
  166.3 1.6 collective-permute-start.8
  168.3 2.9 collective-permute-done.8.refs_2_
  171.3 1.6 collective-permute-start.9
  173.3 3.3 %collective-permute-done.9.refs_3_ = bf16[512,128]{1,0:T(8,128)(2,1)S(1)} collective-permute-done((bf16[512,128]{1,0:T(8,128)(2,1)S(1)}, bf16[512,128]{1,0:T(8,128)(2,1)S(1)}, u32[]{:S(2)}, u32[]{:S(2)}) %collective-permute-start.9) | collective-permute-done | bytes 131104 | tf_op jit(solution)/shard_map/ppermute | solution.py:34
  176.7 1.6 collective-permute-start.10
  179.3 2.3 collective-permute-done.10.refs_4_
  182.9 12.4 %shard_map.145 = (f32[512,6144]{1,0:T(8,128)}, f32[512,128]{1,0:T(8,128)}) custom-call(s32[1]{0:T(128)} %bitcast.span_ref, bf16[512,128]{1,0:T(8,128)(2,1)} %bitcast.161, bf16[512,128]{1,0:T(8,128)(2,1)} %copy-done.11, bf16[512,128]{1,0:T(8,128)(2,1)} %copy-done.13, bf16[512,128]{1,0:T(8,128)(2,1)} %copy-done.15, bf16[512,128]{1,0:T(8,128)(2,1)} %copy-done.17, ...), custom_call_target="tpu_custom_call" | custom-call | flops 3221225472 | bytes 16777216 | tf_op jit(solution)/shard_map/pallas_call | solution.py:129
  196.8 12.4 %shard_map.146 = (f32[512,6144]{1,0:T(8,128)}, f32[512,128]{1,0:T(8,128)}) custom-call(s32[1]{0:T(128)} %bitcast.span_ref, bf16[512,128]{1,0:T(8,128)(2,1)} %bitcast.162, bf16[512,128]{1,0:T(8,128)(2,1)} %copy-done.11, bf16[512,128]{1,0:T(8,128)(2,1)} %copy-done.13, bf16[512,128]{1,0:T(8,128)(2,1)} %copy-done.15, ...), custom_call_target="tpu_custom_call", output_to_operand_aliasing={{0}: (19, {})} | custom-call | flops 3221225472 | bytes 16777216 | tf_op jit(solution)/shard_map/pallas_call | solution.py:129
  210.3 10.0 %fusion.27 = bf16[4,128,512]{2,1,0:T(8,128)(2,1)S(1)} fusion(bf16[6144,512]{1,0:T(8,128)(2,1)} %all-gather.3.cloned.1.call-done, f32[4,128,6144]{2,1,0:T(8,128)} %bitcast.144, f32[4,6144]{1,0:T(4,128)S(1)} %copy-done.24, f32[4,6144]{1,0:T(4,128)S(1)} %copy-done.23, f32[4,128]{1,0:T(4,128)S(1)} %bitcast.167), kind=kOutput, calls=%fused_computation.38 | convolution fusion | flops 3236167680 | bytes 19597312 | tf_op jit(solution)/shard_map/dot_general | solution.py:283
  220.3 6.6 %convolution_convert_fusion = bf16[4,128,6144]{2,1,0:T(8,128)(2,1)S(1)} fusion(bf16[4,128,512]{2,1,0:T(8,128)(2,1)S(1)} %fusion.27, bf16[512,6144]{1,0:T(8,128)(2,1)} %all-gather.5.cloned.1.call-done), kind=kOutput, calls=%fused_computation.7 | convolution fusion | flops 3224371200 | bytes 13107200 | tf_op jit(solution)/shard_map/dot_general | solution.py:285
  227.0 2.6 copy-done.3
  229.7 1.6 collective-permute-start.29
  232.9 7.8 %collective-permute-done.29 = bf16[512,384]{1,0:T(8,128)(2,1)S(1)} collective-permute-done((bf16[512,384]{1,0:T(8,128)(2,1)S(1)}, bf16[512,384]{1,0:T(8,128)(2,1)S(1)}, u32[]{:S(2)}, u32[]{:S(2)}) %collective-permute-start.29) | collective-permute-done | bytes 393248 | tf_op jit(solution)/shard_map/ppermute | solution.py:61
  243.2 1.9 collective-permute-start.30
  246.8 6.4 %collective-permute-done.30 = bf16[512,384]{1,0:T(8,128)(2,1)S(1)} collective-permute-done((bf16[512,384]{1,0:T(8,128)(2,1)S(1)}, bf16[512,384]{1,0:T(8,128)(2,1)S(1)}, u32[]{:S(2)}, u32[]{:S(2)}) %collective-permute-start.30) | collective-permute-done | bytes 393248 | tf_op jit(solution)/shard_map/ppermute | solution.py:61
  255.8 1.6 collective-permute-start.31
  258.4 5.9 %collective-permute-done.31 = bf16[512,384]{1,0:T(8,128)(2,1)S(1)} collective-permute-done((bf16[512,384]{1,0:T(8,128)(2,1)S(1)}, bf16[512,384]{1,0:T(8,128)(2,1)S(1)}, u32[]{:S(2)}, u32[]{:S(2)}) %collective-permute-start.31) | collective-permute-done | bytes 393248 | tf_op jit(solution)/shard_map/ppermute | solution.py:61
  269.0 5.8 %collective-permute-done.32 = bf16[512,384]{1,0:T(8,128)(2,1)S(1)} collective-permute-done((bf16[512,384]{1,0:T(8,128)(2,1)S(1)}, bf16[512,384]{1,0:T(8,128)(2,1)S(1)}, u32[]{:S(2)}, u32[]{:S(2)}) %collective-permute-start.32) | collective-permute-done | bytes 393248 | tf_op jit(solution)/shard_map/ppermute | solution.py:61
  277.7 1.5 collective-permute-start.40
  279.1 7.1 %collective-permute-done.33 = bf16[512,384]{1,0:T(8,128)(2,1)S(1)} collective-permute-done((bf16[512,384]{1,0:T(8,128)(2,1)S(1)}, bf16[512,384]{1,0:T(8,128)(2,1)S(1)}, u32[]{:S(2)}, u32[]{:S(2)}) %collective-permute-start.33) | collective-permute-done | bytes 393248 | tf_op jit(solution)/shard_map/ppermute | solution.py:61
  289.0 1.4 collective-permute-start.41
  290.4 8.0 %collective-permute-done.34 = bf16[512,384]{1,0:T(8,128)(2,1)S(1)} collective-permute-done((bf16[512,384]{1,0:T(8,128)(2,1)S(1)}, bf16[512,384]{1,0:T(8,128)(2,1)S(1)}, u32[]{:S(2)}, u32[]{:S(2)}) %collective-permute-start.34) | collective-permute-done | bytes 393248 | tf_op jit(solution)/shard_map/ppermute | solution.py:61
  299.4 1.6 add_convert_fusion.13
  301.4 1.7 collective-permute-start.42
  303.0 5.7 %collective-permute-done.35 = bf16[512,384]{1,0:T(8,128)(2,1)S(1)} collective-permute-done((bf16[512,384]{1,0:T(8,128)(2,1)S(1)}, bf16[512,384]{1,0:T(8,128)(2,1)S(1)}, u32[]{:S(2)}, u32[]{:S(2)}) %collective-permute-start.35) | collective-permute-done | bytes 393248 | tf_op jit(solution)/shard_map/ppermute | solution.py:61
  309.3 1.4 convert_add_fusion.1
  310.8 2.6 add_convert_fusion.2
  (166 shorter events, 44.1 us)
Async XLA Ops:
  6.5 86.9 %copy-start.22 = (s32[8]{0:T(128)S(1)}, s32[8]{0:T(128)}, u32[]{:S(2)}) copy-start(s32[8]{0:T(128)} %constant.289.clone) | copy-start | bytes 100
  6.6 60.6 %copy-start.20 = (bf16[4,128,2,128]{3,2,1,0:T(2,128)(2,1)S(1)}, bf16[4,128,2,128]{3,2,1,0:T(2,128)(2,1)}, u32[]{:S(2)}) copy-start(bf16[4,128,2,128]{3,2,1,0:T(2,128)(2,1)} %param.20) | copy-start | bytes 786436
  6.6 203.7 %all-gather.3.cloned.1.call-start = ((), (), s32[]{:S(2)}) async-start(), calls=%async_computation | async-start | bytes 9437184 | tf_op jit(solution)/shard_map/all_gather | solution.py:216
  7.3 213.0 %all-gather.5.cloned.1.call-start = ((), (), s32[]{:S(2)}) async-start(), calls=%async_computation.1 | async-start | bytes 9437184 | tf_op jit(solution)/shard_map/all_gather | solution.py:217
  7.4 21.7 %collective-permute-start = (bf16[4,128,768]{2,1,0:T(8,128)(2,1)}, bf16[4,128,768]{2,1,0:T(8,128)(2,1)}, u32[]{:S(2)}, u32[]{:S(2)}) collective-permute-start(bf16[4,128,768]{2,1,0:T(8,128)(2,1)} %param.15), channel_id=1, source_target_pairs={{0,2},{2,4},{4,6},{6,7},{7,5},{5,3},{3,1},{1,0},{8,10},{10,12},{12... | collective-permute-start | bytes 2359304 | tf_op jit(solution)/shard_map/ppermute | solution.py:34
  10.4 53.3 %collective-permute-start.4 = (bf16[4,128,768]{2,1,0:T(8,128)(2,1)}, bf16[4,128,768]{2,1,0:T(8,128)(2,1)}, u32[]{:S(2)}, u32[]{:S(2)}) collective-permute-start(bf16[4,128,768]{2,1,0:T(8,128)(2,1)} %param.15), channel_id=1, source_target_pairs={{0,1},{2,0},{4,2},{6,4},{7,6},{5,7},{3,5},{1,3},{8,9},{10,8},{12,1... | collective-permute-start | bytes 2359304 | tf_op jit(solution)/shard_map/ppermute | solution.py:38
  10.5 95.5 %copy-start.4 = (bf16[128,3072]{1,0:T(8,128)(2,1)}, bf16[128,3072]{1,0:T(8,128)(2,1)S(1)}, u32[]{:S(2)}) copy-start(bf16[128,3072]{1,0:T(8,128)(2,1)S(1)} %constant_dynamic-slice_fusion.2.refs_8_) | copy-start | bytes 2359300
  10.5 53.4 %collective-permute-start.15 = (bf16[128,3072]{1,0:T(8,128)(2,1)S(1)}, bf16[128,3072]{1,0:T(8,128)(2,1)}, u32[]{:S(2)}, u32[]{:S(2)}) collective-permute-start(bf16[128,3072]{1,0:T(8,128)(2,1)S(1)} %constant_dynamic-slice_fusion.2.refs_8_), channel_id=1, source_target_pairs={{0,2},{2,4},{4,6},{6,7},{7,5},{5,3},{3,1},{1,0},{8,10},{10,12},{12... | collective-permute-start | bytes 2359304 | tf_op jit(solution)/shard_map/ppermute | solution.py:34
  12.6 94.5 %collective-permute-start.23 = (bf16[128,3072]{1,0:T(8,128)(2,1)S(1)}, bf16[128,3072]{1,0:T(8,128)(2,1)}, u32[]{:S(2)}, u32[]{:S(2)}) collective-permute-start(bf16[128,3072]{1,0:T(8,128)(2,1)S(1)} %constant_dynamic-slice_fusion.2.refs_8_), channel_id=1, source_target_pairs={{0,1},{2,0},{4,2},{6,4},{7,6},{5,7},{3,5},{1,3},{8,9},{10,8},{12,1... | collective-permute-start | bytes 2359304 | tf_op jit(solution)/shard_map/ppermute | solution.py:38
  12.6 148.1 %collective-permute-start.14 = (bf16[128,3072]{1,0:T(8,128)(2,1)S(1)}, bf16[128,3072]{1,0:T(8,128)(2,1)}, u32[]{:S(2)}, u32[]{:S(2)}) collective-permute-start(bf16[128,3072]{1,0:T(8,128)(2,1)S(1)} %constant_dynamic-slice_fusion.2.refs_8_), channel_id=1, source_target_pairs={{0,8},{8,0},{1,9},{9,1},{2,10},{10,2},{3,11},{11,3},{4,12},{12,4},... | collective-permute-start | bytes 2359304 | tf_op jit(solution)/shard_map/ppermute | solution.py:214
  29.1 32.8 %collective-permute-start.1 = (bf16[4,128,768]{2,1,0:T(8,128)(2,1)}, bf16[4,128,768]{2,1,0:T(8,128)(2,1)S(1)}, u32[]{:S(2)}, u32[]{:S(2)}) collective-permute-start(bf16[4,128,768]{2,1,0:T(8,128)(2,1)} %collective-permute-done), channel_id=1, source_target_pairs={{0,2},{2,4},{4,6},{6,7},{7,5},{5,3},{3,1},{1,0},{8,10},{10,12},{12... | collective-permute-start | bytes 2359304 | tf_op jit(solution)/shard_map/ppermute | solution.py:34
  61.8 20.6 %collective-permute-start.2 = (bf16[4,128,768]{2,1,0:T(8,128)(2,1)S(1)}, bf16[4,128,768]{2,1,0:T(8,128)(2,1)}, u32[]{:S(2)}, u32[]{:S(2)}) collective-permute-start(bf16[4,128,768]{2,1,0:T(8,128)(2,1)S(1)} %collective-permute-done.1), channel_id=1, source_target_pairs={{0,2},{2,4},{4,6},{6,7},{7,5},{5,3},{3,1},{1,0},{8,10},{10,12},{12... | collective-permute-start | bytes 2359304 | tf_op jit(solution)/shard_map/ppermute | solution.py:34
  63.7 43.6 %collective-permute-start.5 = (bf16[4,128,768]{2,1,0:T(8,128)(2,1)}, bf16[4,128,768]{2,1,0:T(8,128)(2,1)}, u32[]{:S(2)}, u32[]{:S(2)}) collective-permute-start(bf16[4,128,768]{2,1,0:T(8,128)(2,1)} %collective-permute-done.4), channel_id=1, source_target_pairs={{0,1},{2,0},{4,2},{6,4},{7,6},{5,7},{3,5},{1,3},{8,9},{10,8},{12,1... | collective-permute-start | bytes 2359304 | tf_op jit(solution)/shard_map/ppermute | solution.py:38
  64.0 45.1 %collective-permute-start.17 = (bf16[128,3072]{1,0:T(8,128)(2,1)}, bf16[128,3072]{1,0:T(8,128)(2,1)}, u32[]{:S(2)}, u32[]{:S(2)}) collective-permute-start(bf16[128,3072]{1,0:T(8,128)(2,1)} %collective-permute-done.15.refs_9_), channel_id=1, source_target_pairs={{0,2},{2,4},{4,6},{6,7},{7,5},{5,3},{3,1},{1,0},{8,10},{10,12},{12... | collective-permute-start | bytes 2359304 | tf_op jit(solution)/shard_map/ppermute | solution.py:34
  82.4 33.7 %collective-permute-start.3 = (bf16[4,128,768]{2,1,0:T(8,128)(2,1)}, bf16[4,128,768]{2,1,0:T(8,128)(2,1)}, u32[]{:S(2)}, u32[]{:S(2)}) collective-permute-start(bf16[4,128,768]{2,1,0:T(8,128)(2,1)} %collective-permute-done.2), channel_id=1, source_target_pairs={{0,2},{2,4},{4,6},{6,7},{7,5},{5,3},{3,1},{1,0},{8,10},{10,12},{12... | collective-permute-start | bytes 2359304 | tf_op jit(solution)/shard_map/ppermute | solution.py:34
  107.1 20.8 %collective-permute-start.25 = (bf16[128,3072]{1,0:T(8,128)(2,1)}, bf16[128,3072]{1,0:T(8,128)(2,1)}, u32[]{:S(2)}, u32[]{:S(2)}) collective-permute-start(bf16[128,3072]{1,0:T(8,128)(2,1)} %collective-permute-done.23.refs_13_), channel_id=1, source_target_pairs={{0,1},{2,0},{4,2},{6,4},{7,6},{5,7},{3,5},{1,3},{8,9},{10,8},{12,1... | collective-permute-start | bytes 2359304 | tf_op jit(solution)/shard_map/ppermute | solution.py:38
  107.3 34.3 %collective-permute-start.6 = (bf16[4,128,768]{2,1,0:T(8,128)(2,1)}, bf16[4,128,768]{2,1,0:T(8,128)(2,1)S(1)}, u32[]{:S(2)}, u32[]{:S(2)}) collective-permute-start(bf16[4,128,768]{2,1,0:T(8,128)(2,1)} %collective-permute-done.5), channel_id=1, source_target_pairs={{0,1},{2,0},{4,2},{6,4},{7,6},{5,7},{3,5},{1,3},{8,9},{10,8},{12,1... | collective-permute-start | bytes 2359304 | tf_op jit(solution)/shard_map/ppermute | solution.py:38
  109.1 32.8 %collective-permute-start.19 = (bf16[128,3072]{1,0:T(8,128)(2,1)}, bf16[128,3072]{1,0:T(8,128)(2,1)}, u32[]{:S(2)}, u32[]{:S(2)}) collective-permute-start(bf16[128,3072]{1,0:T(8,128)(2,1)} %collective-permute-done.17.refs_10_), channel_id=1, source_target_pairs={{0,2},{2,4},{4,6},{6,7},{7,5},{5,3},{3,1},{1,0},{8,10},{10,12},{12... | collective-permute-start | bytes 2359304 | tf_op jit(solution)/shard_map/ppermute | solution.py:34
  116.1 46.2 %collective-permute-start.16 = (bf16[128,3072]{1,0:T(8,128)(2,1)}, bf16[128,3072]{1,0:T(8,128)(2,1)}, u32[]{:S(2)}, u32[]{:S(2)}) collective-permute-start(bf16[128,3072]{1,0:T(8,128)(2,1)} %collective-permute-done.15.refs_9_), channel_id=1, source_target_pairs={{0,8},{8,0},{1,9},{9,1},{2,10},{10,2},{3,11},{11,3},{4,12},{12,4},... | collective-permute-start | bytes 2359304 | tf_op jit(solution)/shard_map/ppermute | solution.py:214
  127.9 50.3 %collective-permute-start.24 = (bf16[128,3072]{1,0:T(8,128)(2,1)}, bf16[128,3072]{1,0:T(8,128)(2,1)}, u32[]{:S(2)}, u32[]{:S(2)}) collective-permute-start(bf16[128,3072]{1,0:T(8,128)(2,1)} %collective-permute-done.23.refs_13_), channel_id=1, source_target_pairs={{0,8},{8,0},{1,9},{9,1},{2,10},{10,2},{3,11},{11,3},{4,12},{12,4},... | collective-permute-start | bytes 2359304 | tf_op jit(solution)/shard_map/ppermute | solution.py:214
  141.7 36.6 %collective-permute-start.27 = (bf16[128,3072]{1,0:T(8,128)(2,1)}, bf16[128,3072]{1,0:T(8,128)(2,1)}, u32[]{:S(2)}, u32[]{:S(2)}) collective-permute-start(bf16[128,3072]{1,0:T(8,128)(2,1)} %collective-permute-done.25.refs_14_), channel_id=1, source_target_pairs={{0,1},{2,0},{4,2},{6,4},{7,6},{5,7},{3,5},{1,3},{8,9},{10,8},{12,1... | collective-permute-start | bytes 2359304 | tf_op jit(solution)/shard_map/ppermute | solution.py:38
  141.9 36.8 %collective-permute-start.21 = (bf16[128,3072]{1,0:T(8,128)(2,1)}, bf16[128,3072]{1,0:T(8,128)(2,1)}, u32[]{:S(2)}, u32[]{:S(2)}) collective-permute-start(bf16[128,3072]{1,0:T(8,128)(2,1)} %collective-permute-done.19.refs_11_), channel_id=1, source_target_pairs={{0,2},{2,4},{4,6},{6,7},{7,5},{5,3},{3,1},{1,0},{8,10},{10,12},{12... | collective-permute-start | bytes 2359304 | tf_op jit(solution)/shard_map/ppermute | solution.py:34
  160.7 5.6 %collective-permute-start.7 = (bf16[512,128]{1,0:T(8,128)(2,1)S(1)}, bf16[512,128]{1,0:T(8,128)(2,1)S(1)}, u32[]{:S(2)}, u32[]{:S(2)}) collective-permute-start(bf16[512,128]{1,0:T(8,128)(2,1)S(1)} %bitcast.159), channel_id=1, source_target_pairs={{0,2},{2,4},{4,6},{6,7},{7,5},{5,3},{3,1},{1,0},{8,10},{10,12},{12... | collective-permute-start | bytes 393224 | tf_op jit(solution)/shard_map/ppermute | solution.py:34
  162.4 5.5 %collective-permute-start.11 = (bf16[512,128]{1,0:T(8,128)(2,1)S(1)}, bf16[512,128]{1,0:T(8,128)(2,1)S(1)}, u32[]{:S(2)}, u32[]{:S(2)}) collective-permute-start(bf16[512,128]{1,0:T(8,128)(2,1)S(1)} %bitcast.160), channel_id=1, source_target_pairs={{0,1},{2,0},{4,2},{6,4},{7,6},{5,7},{3,5},{1,3},{8,9},{10,8},{12,1... | collective-permute-start | bytes 393224 | tf_op jit(solution)/shard_map/ppermute | solution.py:38
  166.3 5.0 %collective-permute-start.8 = (bf16[512,128]{1,0:T(8,128)(2,1)S(1)}, bf16[512,128]{1,0:T(8,128)(2,1)S(1)}, u32[]{:S(2)}, u32[]{:S(2)}) collective-permute-start(bf16[512,128]{1,0:T(8,128)(2,1)S(1)} %collective-permute-done.7.refs_1_), channel_id=1, source_target_pairs={{0,2},{2,4},{4,6},{6,7},{7,5},{5,3},{3,1},{1,0},{8,10},{10,12},{12... | collective-permute-start | bytes 393224 | tf_op jit(solution)/shard_map/ppermute | solution.py:34
  167.9 5.0 %collective-permute-start.12 = (bf16[512,128]{1,0:T(8,128)(2,1)S(1)}, bf16[512,128]{1,0:T(8,128)(2,1)S(1)}, u32[]{:S(2)}, u32[]{:S(2)}) collective-permute-start(bf16[512,128]{1,0:T(8,128)(2,1)S(1)} %collective-permute-done.11.refs_5_), channel_id=1, source_target_pairs={{0,1},{2,0},{4,2},{6,4},{7,6},{5,7},{3,5},{1,3},{8,9},{10,8},{12,1... | collective-permute-start | bytes 393224 | tf_op jit(solution)/shard_map/ppermute | solution.py:38
  171.3 5.4 %collective-permute-start.9 = (bf16[512,128]{1,0:T(8,128)(2,1)S(1)}, bf16[512,128]{1,0:T(8,128)(2,1)S(1)}, u32[]{:S(2)}, u32[]{:S(2)}) collective-permute-start(bf16[512,128]{1,0:T(8,128)(2,1)S(1)} %collective-permute-done.8.refs_2_), channel_id=1, source_target_pairs={{0,2},{2,4},{4,6},{6,7},{7,5},{5,3},{3,1},{1,0},{8,10},{10,12},{12... | collective-permute-start | bytes 393224 | tf_op jit(solution)/shard_map/ppermute | solution.py:34
  172.9 6.0 %collective-permute-start.13 = (bf16[512,128]{1,0:T(8,128)(2,1)S(1)}, bf16[512,128]{1,0:T(8,128)(2,1)S(1)}, u32[]{:S(2)}, u32[]{:S(2)}) collective-permute-start(bf16[512,128]{1,0:T(8,128)(2,1)S(1)} %collective-permute-done.12.refs_6_), channel_id=1, source_target_pairs={{0,1},{2,0},{4,2},{6,4},{7,6},{5,7},{3,5},{1,3},{8,9},{10,8},{12,1... | collective-permute-start | bytes 393224 | tf_op jit(solution)/shard_map/ppermute | solution.py:38
  176.7 5.0 %collective-permute-start.10 = (bf16[512,128]{1,0:T(8,128)(2,1)S(1)}, bf16[512,128]{1,0:T(8,128)(2,1)S(1)}, u32[]{:S(2)}, u32[]{:S(2)}) collective-permute-start(bf16[512,128]{1,0:T(8,128)(2,1)S(1)} %collective-permute-done.9.refs_3_), channel_id=1, source_target_pairs={{0,2},{2,4},{4,6},{6,7},{7,5},{5,3},{3,1},{1,0},{8,10},{10,12},{12... | collective-permute-start | bytes 393224 | tf_op jit(solution)/shard_map/ppermute | solution.py:34
  178.2 17.1 %collective-permute-start.18 = (bf16[128,3072]{1,0:T(8,128)(2,1)}, bf16[128,3072]{1,0:T(8,128)(2,1)S(1)}, u32[]{:S(2)}, u32[]{:S(2)}) collective-permute-start(bf16[128,3072]{1,0:T(8,128)(2,1)} %collective-permute-done.17.refs_10_), channel_id=1, source_target_pairs={{0,8},{8,0},{1,9},{9,1},{2,10},{10,2},{3,11},{11,3},{4,12},{12,4},... | collective-permute-start | bytes 2359304 | tf_op jit(solution)/shard_map/ppermute | solution.py:214
  178.2 17.1 %collective-permute-start.26 = (bf16[128,3072]{1,0:T(8,128)(2,1)}, bf16[128,3072]{1,0:T(8,128)(2,1)S(1)}, u32[]{:S(2)}, u32[]{:S(2)}) collective-permute-start(bf16[128,3072]{1,0:T(8,128)(2,1)} %collective-permute-done.25.refs_14_), channel_id=1, source_target_pairs={{0,8},{8,0},{1,9},{9,1},{2,10},{10,2},{3,11},{11,3},{4,12},{12,4},... | collective-permute-start | bytes 2359304 | tf_op jit(solution)/shard_map/ppermute | solution.py:214
  178.8 16.6 %collective-permute-start.20 = (bf16[128,3072]{1,0:T(8,128)(2,1)}, bf16[128,3072]{1,0:T(8,128)(2,1)S(1)}, u32[]{:S(2)}, u32[]{:S(2)}) collective-permute-start(bf16[128,3072]{1,0:T(8,128)(2,1)} %collective-permute-done.19.refs_11_), channel_id=1, source_target_pairs={{0,8},{8,0},{1,9},{9,1},{2,10},{10,2},{3,11},{11,3},{4,12},{12,4},... | collective-permute-start | bytes 2359304 | tf_op jit(solution)/shard_map/ppermute | solution.py:214
  178.8 16.5 %collective-permute-start.28 = (bf16[128,3072]{1,0:T(8,128)(2,1)}, bf16[128,3072]{1,0:T(8,128)(2,1)}, u32[]{:S(2)}, u32[]{:S(2)}) collective-permute-start(bf16[128,3072]{1,0:T(8,128)(2,1)} %collective-permute-done.27.refs_15_), channel_id=1, source_target_pairs={{0,8},{8,0},{1,9},{9,1},{2,10},{10,2},{3,11},{11,3},{4,12},{12,4},... | collective-permute-start | bytes 2359304 | tf_op jit(solution)/shard_map/ppermute | solution.py:214
  181.6 13.8 %collective-permute-start.22 = (bf16[128,3072]{1,0:T(8,128)(2,1)}, bf16[128,3072]{1,0:T(8,128)(2,1)}, u32[]{:S(2)}, u32[]{:S(2)}) collective-permute-start(bf16[128,3072]{1,0:T(8,128)(2,1)} %collective-permute-done.21.refs_12_), channel_id=1, source_target_pairs={{0,8},{8,0},{1,9},{9,1},{2,10},{10,2},{3,11},{11,3},{4,12},{12,4},... | collective-permute-start | bytes 2359304 | tf_op jit(solution)/shard_map/ppermute | solution.py:214
  229.7 10.9 %collective-permute-start.29 = (bf16[512,384]{1,0:T(8,128)(2,1)S(1)}, bf16[512,384]{1,0:T(8,128)(2,1)S(1)}, u32[]{:S(2)}, u32[]{:S(2)}) collective-permute-start(bf16[512,384]{1,0:T(8,128)(2,1)S(1)} %get-tuple-element.27), channel_id=1, source_target_pairs={{0,2},{2,4},{4,6},{6,7},{7,5},{5,3},{3,1},{1,0},{8,10},{10,12},{12... | collective-permute-start | bytes 1179656 | tf_op jit(solution)/shard_map/ppermute | solution.py:61
  231.2 10.6 %collective-permute-start.36 = (bf16[512,384]{1,0:T(8,128)(2,1)S(1)}, bf16[512,384]{1,0:T(8,128)(2,1)S(1)}, u32[]{:S(2)}, u32[]{:S(2)}) collective-permute-start(bf16[512,384]{1,0:T(8,128)(2,1)S(1)} %get-tuple-element.28), channel_id=1, source_target_pairs={{0,1},{2,0},{4,2},{6,4},{7,6},{5,7},{3,5},{1,3},{8,9},{10,8},{12,1... | collective-permute-start | bytes 1179656 | tf_op jit(solution)/shard_map/ppermute | solution.py:63
  243.2 10.0 %collective-permute-start.30 = (bf16[512,384]{1,0:T(8,128)(2,1)S(1)}, bf16[512,384]{1,0:T(8,128)(2,1)S(1)}, u32[]{:S(2)}, u32[]{:S(2)}) collective-permute-start(bf16[512,384]{1,0:T(8,128)(2,1)S(1)} %get-tuple-element.25), channel_id=1, source_target_pairs={{0,2},{2,4},{4,6},{6,7},{7,5},{5,3},{3,1},{1,0},{8,10},{10,12},{12... | collective-permute-start | bytes 1179656 | tf_op jit(solution)/shard_map/ppermute | solution.py:61
  245.0 9.4 %collective-permute-start.37 = (bf16[512,384]{1,0:T(8,128)(2,1)S(1)}, bf16[512,384]{1,0:T(8,128)(2,1)S(1)}, u32[]{:S(2)}, u32[]{:S(2)}) collective-permute-start(bf16[512,384]{1,0:T(8,128)(2,1)S(1)} %get-tuple-element.26), channel_id=1, source_target_pairs={{0,1},{2,0},{4,2},{6,4},{7,6},{5,7},{3,5},{1,3},{8,9},{10,8},{12,1... | collective-permute-start | bytes 1179656 | tf_op jit(solution)/shard_map/ppermute | solution.py:63
  255.8 8.6 %collective-permute-start.31 = (bf16[512,384]{1,0:T(8,128)(2,1)S(1)}, bf16[512,384]{1,0:T(8,128)(2,1)S(1)}, u32[]{:S(2)}, u32[]{:S(2)}) collective-permute-start(bf16[512,384]{1,0:T(8,128)(2,1)S(1)} %get-tuple-element.23), channel_id=1, source_target_pairs={{0,2},{2,4},{4,6},{6,7},{7,5},{5,3},{3,1},{1,0},{8,10},{10,12},{12... | collective-permute-start | bytes 1179656 | tf_op jit(solution)/shard_map/ppermute | solution.py:61
  257.4 8.2 %collective-permute-start.38 = (bf16[512,384]{1,0:T(8,128)(2,1)S(1)}, bf16[512,384]{1,0:T(8,128)(2,1)S(1)}, u32[]{:S(2)}, u32[]{:S(2)}) collective-permute-start(bf16[512,384]{1,0:T(8,128)(2,1)S(1)} %get-tuple-element.24), channel_id=1, source_target_pairs={{0,1},{2,0},{4,2},{6,4},{7,6},{5,7},{3,5},{1,3},{8,9},{10,8},{12,1... | collective-permute-start | bytes 1179656 | tf_op jit(solution)/shard_map/ppermute | solution.py:63
  266.9 7.8 %collective-permute-start.32 = (bf16[512,384]{1,0:T(8,128)(2,1)S(1)}, bf16[512,384]{1,0:T(8,128)(2,1)S(1)}, u32[]{:S(2)}, u32[]{:S(2)}) collective-permute-start(bf16[512,384]{1,0:T(8,128)(2,1)S(1)} %get-tuple-element.21), channel_id=1, source_target_pairs={{0,2},{2,4},{4,6},{6,7},{7,5},{5,3},{3,1},{1,0},{8,10},{10,12},{12... | collective-permute-start | bytes 1179656 | tf_op jit(solution)/shard_map/ppermute | solution.py:61
  267.7 8.0 %collective-permute-start.39 = (bf16[512,384]{1,0:T(8,128)(2,1)S(1)}, bf16[512,384]{1,0:T(8,128)(2,1)S(1)}, u32[]{:S(2)}, u32[]{:S(2)}) collective-permute-start(bf16[512,384]{1,0:T(8,128)(2,1)S(1)} %get-tuple-element.22), channel_id=1, source_target_pairs={{0,1},{2,0},{4,2},{6,4},{7,6},{5,7},{3,5},{1,3},{8,9},{10,8},{12,1... | collective-permute-start | bytes 1179656 | tf_op jit(solution)/shard_map/ppermute | solution.py:63
  277.1 9.2 %collective-permute-start.33 = (bf16[512,384]{1,0:T(8,128)(2,1)S(1)}, bf16[512,384]{1,0:T(8,128)(2,1)S(1)}, u32[]{:S(2)}, u32[]{:S(2)}) collective-permute-start(bf16[512,384]{1,0:T(8,128)(2,1)S(1)} %get-tuple-element.19), channel_id=1, source_target_pairs={{0,2},{2,4},{4,6},{6,7},{7,5},{5,3},{3,1},{1,0},{8,10},{10,12},{12... | collective-permute-start | bytes 1179656 | tf_op jit(solution)/shard_map/ppermute | solution.py:61
  277.7 9.4 %collective-permute-start.40 = (bf16[512,384]{1,0:T(8,128)(2,1)S(1)}, bf16[512,384]{1,0:T(8,128)(2,1)S(1)}, u32[]{:S(2)}, u32[]{:S(2)}) collective-permute-start(bf16[512,384]{1,0:T(8,128)(2,1)S(1)} %get-tuple-element.20), channel_id=1, source_target_pairs={{0,1},{2,0},{4,2},{6,4},{7,6},{5,7},{3,5},{1,3},{8,9},{10,8},{12,1... | collective-permute-start | bytes 1179656 | tf_op jit(solution)/shard_map/ppermute | solution.py:63
  288.3 10.0 %collective-permute-start.34 = (bf16[512,384]{1,0:T(8,128)(2,1)S(1)}, bf16[512,384]{1,0:T(8,128)(2,1)S(1)}, u32[]{:S(2)}, u32[]{:S(2)}) collective-permute-start(bf16[512,384]{1,0:T(8,128)(2,1)S(1)} %get-tuple-element.17), channel_id=1, source_target_pairs={{0,2},{2,4},{4,6},{6,7},{7,5},{5,3},{3,1},{1,0},{8,10},{10,12},{12... | collective-permute-start | bytes 1179656 | tf_op jit(solution)/shard_map/ppermute | solution.py:61
  289.0 10.4 %collective-permute-start.41 = (bf16[512,384]{1,0:T(8,128)(2,1)S(1)}, bf16[512,384]{1,0:T(8,128)(2,1)}, u32[]{:S(2)}, u32[]{:S(2)}) collective-permute-start(bf16[512,384]{1,0:T(8,128)(2,1)S(1)} %get-tuple-element.18), channel_id=1, source_target_pairs={{0,1},{2,0},{4,2},{6,4},{7,6},{5,7},{3,5},{1,3},{8,9},{10,8},{12,1... | collective-permute-start | bytes 1179656 | tf_op jit(solution)/shard_map/ppermute | solution.py:63
  301.0 7.8 %collective-permute-start.35 = (bf16[512,384]{1,0:T(8,128)(2,1)S(1)}, bf16[512,384]{1,0:T(8,128)(2,1)S(1)}, u32[]{:S(2)}, u32[]{:S(2)}) collective-permute-start(bf16[512,384]{1,0:T(8,128)(2,1)S(1)} %get-tuple-element.15), channel_id=1, source_target_pairs={{0,2},{2,4},{4,6},{6,7},{7,5},{5,3},{3,1},{1,0},{8,10},{10,12},{12... | collective-permute-start | bytes 1179656 | tf_op jit(solution)/shard_map/ppermute | solution.py:61
  301.4 7.9 %collective-permute-start.42 = (bf16[512,384]{1,0:T(8,128)(2,1)S(1)}, bf16[512,384]{1,0:T(8,128)(2,1)}, u32[]{:S(2)}, u32[]{:S(2)}) collective-permute-start(bf16[512,384]{1,0:T(8,128)(2,1)S(1)} %get-tuple-element.16), channel_id=1, source_target_pairs={{0,1},{2,0},{4,2},{6,4},{7,6},{5,7},{3,5},{1,3},{8,9},{10,8},{12,1... | collective-permute-start | bytes 1179656 | tf_op jit(solution)/shard_map/ppermute | solution.py:63
  (26 other events, 321.3 us)
Sparse Core Ops, SparseCore 0:
  8.9 18.3 all-gather.2
  28.9 17.9 all-gather.4
